TPU v7x, 32 devices: a whole 2x2x4 slice. The times are simulated.
32 devices in a mesh: gx: 8 (over z, x), ka: 4 (over y, core).
Axes of the slice: x: 2, y: 2, z: 4, core: 2. Of those that a mesh axis runs over, the one named last changes fastest.
Arguments:
- direct_snapshots: bfloat16 [128, 32, 64, 128], P('ka', 'gx'), may hold values from -40 to 40
- adjoint_snapshots: bfloat16 [128, 32, 64, 128], P('ka', 'gx'), may hold values from -40 to 40
- quad_weight: float32 [32, 64], P('gx'), may hold values from 0.5 to 2
- mean_velocity: float32 [32, 64], P('gx'), may hold values from 0.2 to 1.2
- diffusivity: float32 [32, 64], P('gx'), may hold values from 0.05 to 0.5
Outputs:
- hankel_gram: float32 [8192, 128], P(('ka', 'gx'))
- reduced_operator: float32 [8192, 128], P(('ka', 'gx'))
- hankel_norm: float32 [128], P('ka')
All inputs are finite; a program needn't handle non-finite values.
Results may differ from a plain program's by a relative error of at most 0.0071.
Values may be sent and summed in bfloat16 or wider, within the bound.
No kernel may reach another device: no remote copies, remote signals or barrier semaphores. Data moves between devices by JAX's collectives and lax.ppermute only.
A program may use at most 64 MiB of HBM per device.

v0:
```python
import math

import jax
import jax.numpy as jnp
from jax import lax
from jax.sharding import PartitionSpec as P

epsilon = 1e-06


def padded_2(cells, sides, width):
    for axis, dim in sides:
        count = lax.axis_size(axis)
        ends = count - 1
        head = lax.slice_in_dim(cells, 0, width, axis=dim)
        tail = lax.slice_in_dim(cells, cells.shape[dim] - width, cells.shape[dim], axis=dim)
        cells = jnp.concatenate(
            [
                lax.ppermute(tail, axis, [(i, (i + 1) % count) for i in range(ends)]),
                cells,
                lax.ppermute(head, axis, [((i + 1) % count, i) for i in range(ends)]),
            ],
            axis=dim,
        )
    return cells


def dft_tables(count):
    wave_index = jnp.arange(count, dtype=jnp.int32) - count // 2
    angle_index = jnp.arange(count, dtype=jnp.int32)
    residues = wave_index[:, None] * angle_index[None, :] % count
    phases = 2.0 * math.pi * residues.astype(jnp.float32) / count
    scaling = 1.0 / math.sqrt(count)
    return (
        (jnp.cos(phases) * scaling).astype(jnp.bfloat16),
        (jnp.sin(phases) * scaling).astype(jnp.bfloat16),
    )


def combine_parts(cos_part, sin_part, half):
    real_part = cos_part[..., :half] + sin_part[..., half:]
    imag_part = cos_part[..., half:] - sin_part[..., :half]
    return jnp.concatenate([real_part, imag_part], axis=-1).astype(jnp.bfloat16)


def complex_blocks(product, half):
    upper_rows = product[..., :half, :]
    lower_rows = product[..., half:, :]
    pieces = []
    for offset in (0, 2 * half):
        pieces.append(
            upper_rows[..., offset : offset + half]
            + lower_rows[..., offset + half : offset + 2 * half]
        )
        pieces.append(
            upper_rows[..., offset + half : offset + 2 * half]
            - lower_rows[..., offset : offset + half]
        )
    return jnp.concatenate(pieces, axis=-1)


def local(direct_snapshots, adjoint_snapshots, quad_weight, mean_velocity, diffusivity):
    local_angles, axial_cells, radial_cells, columns = direct_snapshots.shape
    snap_count = columns // 2
    total_angles = local_angles * lax.axis_size("ka")
    cos_table, sin_table = dft_tables(total_angles)
    first_wave = lax.axis_index("ka") * local_angles
    moved_direct, moved_adjoint = (
        lax.all_to_all(direct_snapshots, "ka", split_axis=2, concat_axis=0, tiled=True),
        lax.all_to_all(adjoint_snapshots, "ka", split_axis=2, concat_axis=0, tiled=True),
    )

    def transform_all(snapshots):
        flattened = snapshots.reshape(total_angles, -1)
        cos_part = jnp.dot(cos_table, flattened, preferred_element_type=jnp.float32).reshape(
            snapshots.shape
        )
        sin_part = jnp.dot(sin_table, flattened, preferred_element_type=jnp.float32).reshape(
            snapshots.shape
        )
        return combine_parts(cos_part, sin_part, snap_count)

    direct_modes, adjoint_modes = (
        lax.all_to_all(transform_all(moved_direct), "ka", split_axis=0, concat_axis=2, tiled=True),
        lax.all_to_all(transform_all(moved_adjoint), "ka", split_axis=0, concat_axis=2, tiled=True),
    )
    padded = padded_2(direct_modes, (("gx", 1),), 1)
    field_f32 = direct_modes.astype(jnp.float32)
    forward = padded[:, 2:].astype(jnp.float32)
    behind = padded[:, :-2].astype(jnp.float32)
    radial_pad = jnp.pad(field_f32, ((0, 0), (0, 0), (1, 1), (0, 0)))
    outward = radial_pad[:, :, 2:]
    inward = radial_pad[:, :, :-2]
    radius = 0.25 + (jnp.arange(radial_cells, dtype=jnp.float32) + 0.5) / radial_cells
    wavenumber = (
        first_wave + jnp.arange(local_angles, dtype=jnp.int32) - total_angles // 2
    ).astype(jnp.float32) / total_angles
    azimuthal = (wavenumber[:, None] / radius[None, :]) ** 2
    velocity = mean_velocity[None, :, :, None]
    diffusion = diffusivity[None, :, :, None]
    image = (
        -velocity * (forward - behind) * 0.5
        + diffusion
        * (
            forward
            + behind
            + outward
            + inward
            - 4.0 * field_f32
            - azimuthal[:, None, :, None] * field_f32
        )
    ).astype(jnp.bfloat16)
    norm_factor = 1.0 / math.sqrt(axial_cells * lax.axis_size("gx") * radial_cells)
    plane_weight = quad_weight * norm_factor
    weighted = (adjoint_modes.astype(jnp.float32) * plane_weight[None, :, :, None]).astype(
        jnp.bfloat16
    )
    right_side = jnp.concatenate([direct_modes, image], axis=-1)
    product = jnp.einsum(
        "kpa,kpb->kab",
        weighted.reshape(local_angles, -1, columns),
        right_side.reshape(local_angles, -1, 2 * columns),
        preferred_element_type=jnp.float32,
    )
    gram_terms = complex_blocks(product, snap_count).reshape(local_angles * snap_count, 2 * columns)
    row_count = gram_terms.shape[0] // lax.axis_size("gx")
    row_index = lax.axis_index("gx") * row_count + jnp.arange(row_count, dtype=jnp.int32)
    owner = row_index // snap_count
    selector = (owner[:, None] == jnp.arange(local_angles, dtype=jnp.int32)[None, :]).astype(
        jnp.float32
    )
    own_rows = lax.psum_scatter(gram_terms, "gx", scatter_dimension=0, tiled=True)
    row_energy = jnp.sum(own_rows[:, :columns] ** 2, axis=1)
    energy = lax.psum(jnp.sum(selector * row_energy[:, None], axis=0), "gx")
    mean_sq = energy / (2.0 * snap_count * snap_count)
    row_scale = jnp.sum(selector * lax.rsqrt(mean_sq + epsilon)[None, :], axis=1)
    hankel_gram = own_rows[:, :columns] * row_scale[:, None]
    reduced_operator = own_rows[:, columns:] * row_scale[:, None]
    hankel_norm = jnp.sqrt(mean_sq)
    return (hankel_gram, reduced_operator, hankel_norm)


def solution(mesh):
    placed = (
        P("ka", "gx", None, None),
        P("ka", "gx", None, None),
        P("gx", None),
        P("gx", None),
        P("gx", None),
    )
    return jax.shard_map(
        local,
        mesh=mesh,
        in_specs=placed,
        out_specs=(P(("ka", "gx"), None), P(("ka", "gx"), None), P("ka")),
        check_vma=False,
    )
```

profile of v0, /device:TPU:0, one launch (start us, length us, event | category | flops | bytes accessed | tf_op | source)
XLA Modules:
  0.0 245.9 jit_solution(12957159092731298327)
XLA Ops:
  7.2 4.3 %copy.51 = bf16[32,4,64,128]{3,0,1,2:T(8,128)(2,1)} copy(bf16[32,4,64,128]{3,2,1,0:T(8,128)(2,1)} %param.5) | data formatting | bytes 4194304 | tf_op args[0]
  11.5 4.2 %all-to-all-start.2 = ((bf16[32,4,64,128]{3,0,1,2:T(8,128)(2,1)}), bf16[32,4,64,128]{3,0,1,2:T(8,128)(2,1)S(1)}, u32[]{:S(2)}, u32[]{:S(2)}) async-start(bf16[32,4,64,128]{3,0,1,2:T(8,128)(2,1)} %copy.51), calls=%async_computation.2 | async-start | bytes 4194304 | tf_op jit(solution)/shard_map/all_to_all | solution.py:69
  15.7 4.2 %copy.46 = bf16[32,4,64,128]{3,0,1,2:T(8,128)(2,1)} copy(bf16[32,4,64,128]{3,2,1,0:T(8,128)(2,1)} %param.6) | data formatting | bytes 4194304 | tf_op args[1]
  19.9 21.5 %all-to-all-done.2 = bf16[32,4,64,128]{3,0,1,2:T(8,128)(2,1)S(1)} async-done(((bf16[32,4,64,128]{3,0,1,2:T(8,128)(2,1)}), bf16[32,4,64,128]{3,0,1,2:T(8,128)(2,1)S(1)}, u32[]{:S(2)}, u32[]{:S(2)}) %all-to-all-start.2) | async-done | bytes 2097184 | tf_op jit(solution)/shard_map/all_to_all | solution.py:69
  41.4 4.5 %all-to-all-start = ((bf16[32,4,64,128]{3,0,1,2:T(8,128)(2,1)}), bf16[32,4,64,128]{3,0,1,2:T(8,128)(2,1)}, u32[]{:S(2)}, u32[]{:S(2)}) async-start(bf16[32,4,64,128]{3,0,1,2:T(8,128)(2,1)} %copy.46), calls=%async_computation | async-start | bytes 4194304 | tf_op jit(solution)/shard_map/all_to_all | solution.py:70
  45.9 2.7 %copy.63 = bf16[32,4,4,16,128]{4,3,1,0,2:T(8,128)(2,1)} copy(bf16[32,4,4,16,128]{4,0,1,3,2:T(8,128)(2,1)S(1)} %bitcast.57) | data formatting | bytes 4194304 | tf_op jit(solution)/shard_map/all_to_all | solution.py:69
  48.5 4.2 %reshape.108 = bf16[128,8192]{1,0:T(8,128)(2,1)} reshape(bf16[4,32,4,16,128]{4,3,2,1,0:T(8,128)(2,1)} %bitcast.59) | data formatting | bytes 4194304 | tf_op jit(solution)/shard_map/reshape | solution.py:74
  52.8 3.2 %copy.53 = bf16[8192,128]{1,0:T(8,128)(2,1)S(1)} copy(bf16[8192,128]{0,1:T(8,128)(2,1)} %bitcast.60) | data formatting | bytes 4194304 | tf_op jit(solution)/shard_map/dot_general | solution.py:75
  56.0 1.0 fusion.26
  57.0 1.0 fusion.30
  58.0 1.0 fusion.15
  59.1 0.1 pad_maximum_fusion.3
  59.2 3.0 %copy.54 = bf16[128,4,16,128]{3,2,1,0:T(8,128)(2,1)} copy(bf16[128,4,16,128]{0,3,2,1:T(8,128)(2,1)S(1)} %pad_maximum_fusion.3) | data formatting | bytes 4194304 | tf_op jit(solution)/shard_map/concatenate | solution.py:43
  62.2 9.4 %all-to-all-done = bf16[32,4,64,128]{3,0,1,2:T(8,128)(2,1)} async-done(((bf16[32,4,64,128]{3,0,1,2:T(8,128)(2,1)}), bf16[32,4,64,128]{3,0,1,2:T(8,128)(2,1)}, u32[]{:S(2)}, u32[]{:S(2)}) %all-to-all-start) | async-done | bytes 2097184 | tf_op jit(solution)/shard_map/all_to_all | solution.py:70
  71.6 4.6 %all-to-all-start.3 = ((bf16[128,4,16,128]{3,2,1,0:T(8,128)(2,1)}), bf16[128,4,16,128]{3,2,1,0:T(8,128)(2,1)}, u32[]{:S(2)}, u32[]{:S(2)}) async-start(bf16[128,4,16,128]{3,2,1,0:T(8,128)(2,1)} %copy.54), calls=%async_computation.3 | async-start | bytes 4194304 | tf_op jit(solution)/shard_map/all_to_all | solution.py:84
  76.3 2.9 %copy.64 = bf16[32,4,4,16,128]{4,3,1,0,2:T(8,128)(2,1)S(1)} copy(bf16[32,4,4,16,128]{4,0,1,3,2:T(8,128)(2,1)} %bitcast.2) | data formatting | bytes 4194304 | tf_op jit(solution)/shard_map/all_to_all | solution.py:70
  79.2 2.3 reshape.107
  81.5 3.2 %copy.48 = bf16[8192,128]{1,0:T(8,128)(2,1)S(1)} copy(bf16[8192,128]{0,1:T(8,128)(2,1)} %bitcast.62) | data formatting | bytes 4194304 | tf_op jit(solution)/shard_map/dot_general | solution.py:75
  84.7 1.0 fusion.28
  85.7 1.0 fusion.32
  86.8 1.0 fusion.17
  87.8 0.1 pad_maximum_fusion.2
  87.9 3.0 %copy.49 = bf16[128,4,16,128]{3,2,1,0:T(8,128)(2,1)} copy(bf16[128,4,16,128]{0,3,2,1:T(8,128)(2,1)S(1)} %pad_maximum_fusion.2) | data formatting | bytes 4194304 | tf_op jit(solution)/shard_map/concatenate | solution.py:43
  91.0 10.8 %all-to-all-done.3 = bf16[128,4,16,128]{3,2,1,0:T(8,128)(2,1)} async-done(((bf16[128,4,16,128]{3,2,1,0:T(8,128)(2,1)}), bf16[128,4,16,128]{3,2,1,0:T(8,128)(2,1)}, u32[]{:S(2)}, u32[]{:S(2)}) %all-to-all-start.3) | async-done | bytes 2097184 | tf_op jit(solution)/shard_map/all_to_all | solution.py:84
  101.8 4.5 %all-to-all-start.1 = ((bf16[128,4,16,128]{3,2,1,0:T(8,128)(2,1)}), bf16[128,4,16,128]{3,2,1,0:T(8,128)(2,1)}, u32[]{:S(2)}, u32[]{:S(2)}) async-start(bf16[128,4,16,128]{3,2,1,0:T(8,128)(2,1)} %copy.49), calls=%async_computation.1 | async-start | bytes 4194304 | tf_op jit(solution)/shard_map/all_to_all | solution.py:85
  106.4 0.1 mul.139
  106.5 0.1 divide_multiply_fusion
  106.6 2.2 copy.55
  108.7 1.1 fusion.55
  109.9 4.2 %collective-permute-start.1 = (bf16[32,1,64,128]{3,2,1,0:T(8,128)(2,1)}, bf16[32,1,64,128]{3,2,1,0:T(8,128)(2,1)S(1)}, u32[]{:S(2)}, u32[]{:S(2)}) collective-permute-start(bf16[32,1,64,128]{3,2,1,0:T(8,128)(2,1)} %get-tuple-element.12), channel_id=1, source_target_pairs={{0,4},{4,8},{8,12},{12,16},{16,20},{20,24},{24,28},{1,5},{5,9},{9,... | collective-permute-start | bytes 1572872 | tf_op jit(solution)/shard_map/ppermute | solution.py:19
  114.1 1.5 collective-permute-start
  115.6 2.6 %bitcast_convert_fusion = f32[32,4,64,128]{3,2,1,0:T(8,128)} fusion(bf16[32,4,4,16,128]{4,3,2,1,0:T(8,128)(2,1)S(1)} %copy.55), kind=kLoop, calls=%fused_computation.74 | loop fusion | flops 1048576 | bytes 6291456 | tf_op jit(solution)/shard_map/convert_element_type | solution.py:88
  118.2 13.9 %all-to-all-done.1 = bf16[128,4,16,128]{3,2,1,0:T(8,128)(2,1)} async-done(((bf16[128,4,16,128]{3,2,1,0:T(8,128)(2,1)}), bf16[128,4,16,128]{3,2,1,0:T(8,128)(2,1)}, u32[]{:S(2)}, u32[]{:S(2)}) %all-to-all-start.1) | async-done | bytes 2097184 | tf_op jit(solution)/shard_map/all_to_all | solution.py:85
  132.1 2.1 convert_bitcast_fusion
  134.1 0.6 copy.50
  134.8 0.6 fusion.13
  135.4 1.9 collective-permute-done.1
  137.4 4.4 %fusion.6 = bf16[32,4,64,128]{3,2,1,0:T(8,128)(2,1)S(1)} fusion(f32[32,4,64,128]{3,2,1,0:T(8,128)S(1)} %copy-done, bf16[32,4,64,128]{3,2,1,0:T(8,128)(2,1)S(1)} %bitcast.50, bf16[32,1,64,128]{3,2,1,0:T(8,128)(2,1)S(1)} %collective-permute-done.1, bf16[32,1,64,128]{3,2,1,0:T(8,128)(2,1)S(1)} %collective-permute-done, f32[32,64]{1,0:T(8,128)S(1)} %divide_multiply_fusion, ...), kind=kLoop, calls=%fused_computation.10 | loop fusion | flops 17825792 | bytes 9447424 | tf_op jit(solution)/shard_map/convert_element_type | solution.py:112
  141.8 1.1 fusion.9
  142.9 1.1 slice_add_fusion.3
  144.1 2.2 pad_maximum_fusion.4
  146.3 70.1 %reduce-scatter.2.cloned.1.call-done = f32[256,256]{1,0:T(8,128)} async-done(((f32[2048,256]{1,0:T(8,128)}), f32[256,256]{1,0:T(8,128)}) %reduce-scatter.2.cloned.1.call-update) | async-done | bytes 262160 | tf_op jit(solution)/shard_map/reduce_scatter | solution.py:132
  216.4 1.0 multiply_reduce_fusion
  217.4 0.1 select_reduce_fusion.1
  217.5 19.1 %psum.7 = f32[32]{0:T(128)S(1)} all-reduce(f32[32]{0:T(128)S(1)} %select_reduce_fusion.1), channel_id=1, replica_groups=mesh['gx'=8,'ka'=4] {'gx'}, use_global_device_ids=true, to_apply=%region_3.4 | all-reduce | flops 32 | bytes 256 | tf_op jit(solution)/shard_map/psum | solution.py:134
  236.7 0.5 multiply_sqrt_fusion
  237.2 0.1 select_reduce_fusion
  237.3 1.8 slice_multiply_fusion
  (17 shorter events, 0.1 us)
Async XLA Ops:
  11.5 29.9 %all-to-all-start.2 = ((bf16[32,4,64,128]{3,0,1,2:T(8,128)(2,1)}), bf16[32,4,64,128]{3,0,1,2:T(8,128)(2,1)S(1)}, u32[]{:S(2)}, u32[]{:S(2)}) async-start(bf16[32,4,64,128]{3,0,1,2:T(8,128)(2,1)} %copy.51), calls=%async_computation.2 | async-start | bytes 4194304 | tf_op jit(solution)/shard_map/all_to_all | solution.py:69
  41.4 30.2 %all-to-all-start = ((bf16[32,4,64,128]{3,0,1,2:T(8,128)(2,1)}), bf16[32,4,64,128]{3,0,1,2:T(8,128)(2,1)}, u32[]{:S(2)}, u32[]{:S(2)}) async-start(bf16[32,4,64,128]{3,0,1,2:T(8,128)(2,1)} %copy.46), calls=%async_computation | async-start | bytes 4194304 | tf_op jit(solution)/shard_map/all_to_all | solution.py:70
  71.6 30.2 %all-to-all-start.3 = ((bf16[128,4,16,128]{3,2,1,0:T(8,128)(2,1)}), bf16[128,4,16,128]{3,2,1,0:T(8,128)(2,1)}, u32[]{:S(2)}, u32[]{:S(2)}) async-start(bf16[128,4,16,128]{3,2,1,0:T(8,128)(2,1)} %copy.54), calls=%async_computation.3 | async-start | bytes 4194304 | tf_op jit(solution)/shard_map/all_to_all | solution.py:84
  91.0 15.4 %copy-start.2 = (f32[4,64]{1,0:T(4,128)S(1)}, f32[4,64]{1,0:T(4,128)}, u32[]{:S(2)}) copy-start(f32[4,64]{1,0:T(4,128)} %param.7) | copy-start | bytes 3076
  91.0 15.5 %copy-start.3 = (f32[4,64]{1,0:T(4,128)S(1)}, f32[4,64]{1,0:T(4,128)}, u32[]{:S(2)}) copy-start(f32[4,64]{1,0:T(4,128)} %param.8) | copy-start | bytes 3076
  101.8 30.2 %all-to-all-start.1 = ((bf16[128,4,16,128]{3,2,1,0:T(8,128)(2,1)}), bf16[128,4,16,128]{3,2,1,0:T(8,128)(2,1)}, u32[]{:S(2)}, u32[]{:S(2)}) async-start(bf16[128,4,16,128]{3,2,1,0:T(8,128)(2,1)} %copy.49), calls=%async_computation.1 | async-start | bytes 4194304 | tf_op jit(solution)/shard_map/all_to_all | solution.py:85
  106.3 110.1 %reduce-scatter.2.cloned.1.call-start = ((), (), s32[]{:S(2)}) async-start(), calls=%async_computation.5 | async-start | bytes 2359296 | tf_op jit(solution)/shard_map/reduce_scatter | solution.py:132
  109.9 27.5 %collective-permute-start.1 = (bf16[32,1,64,128]{3,2,1,0:T(8,128)(2,1)}, bf16[32,1,64,128]{3,2,1,0:T(8,128)(2,1)S(1)}, u32[]{:S(2)}, u32[]{:S(2)}) collective-permute-start(bf16[32,1,64,128]{3,2,1,0:T(8,128)(2,1)} %get-tuple-element.12), channel_id=1, source_target_pairs={{0,4},{4,8},{8,12},{12,16},{16,20},{20,24},{24,28},{1,5},{5,9},{9,... | collective-permute-start | bytes 1572872 | tf_op jit(solution)/shard_map/ppermute | solution.py:19
  114.1 23.3 %collective-permute-start = (bf16[32,1,64,128]{3,2,1,0:T(8,128)(2,1)}, bf16[32,1,64,128]{3,2,1,0:T(8,128)(2,1)S(1)}, u32[]{:S(2)}, u32[]{:S(2)}) collective-permute-start(bf16[32,1,64,128]{3,2,1,0:T(8,128)(2,1)} %get-tuple-element.11), channel_id=1, source_target_pairs={{4,0},{8,4},{12,8},{16,12},{20,16},{24,20},{28,24},{5,1},{9,5},{13... | collective-permute-start | bytes 1572872 | tf_op jit(solution)/shard_map/ppermute | solution.py:21
  134.8 2.6 %copy-start = (f32[32,4,64,128]{3,2,1,0:T(8,128)S(1)}, f32[32,4,64,128]{3,2,1,0:T(8,128)}, u32[]{:S(2)}) copy-start(f32[32,4,64,128]{3,2,1,0:T(8,128)} %bitcast_convert_fusion) | copy-start | bytes 12582916
  134.8 2.6 %copy-start.1 = (f32[4,64]{1,0:T(4,128)S(1)}, f32[4,64]{1,0:T(4,128)}, u32[]{:S(2)}) copy-start(f32[4,64]{1,0:T(4,128)} %param.9) | copy-start | bytes 3076
Sparse Core Ops, SparseCore 0:
  146.4 69.9 reduce-scatter.1
where the time goes:
time: 247 us; the launch traced here: 246 us
  waiting for transfers between devices  128 us (52%)
  local copies, waits for them, and re-layouts  37.2 us (15%)
  starting transfers between devices  23.6 us (10%)
  blocking collectives  19.1 us (8%)
  other arithmetic  19 us (8%)
  between operations  14.3 us (6%)
  matrix products  5.14 us (2%)
    reduce_scatter x1, waiting for transfers between devices, local(): lax.psum_scatter(gram_terms, 'gx', scatter_dimension=0, tiled=True)  70.1 us
    all_to_all x1, waiting for transfers between devices, local(): lax.all_to_all(direct_snapshots, 'ka', split_axis=2, concat_axis=0, tiled...  21.5 us
    psum x1, blocking collectives, local(): energy = lax.psum(jnp.sum(selector * row_energy[:, None], axis=0), 'gx')  19.1 us
    all_to_all x1, waiting for transfers between devices, local(): lax.all_to_all(transform_all(moved_adjoint), 'ka', split_axis=0, concat_a...  13.9 us
    all_to_all x1, waiting for transfers between devices, local(): lax.all_to_all(transform_all(moved_direct), 'ka', split_axis=0, concat_ax...  10.8 us
    all_to_all x1, waiting for transfers between devices, local(): lax.all_to_all(adjoint_snapshots, 'ka', split_axis=2, concat_axis=0, tile...  9.43 us
    unnamed x10, local copies, waits for them, and re-layouts  8.55 us
    reshape x2, local copies, waits for them, and re-layouts, transform_all(): flattened = snapshots.reshape(total_angles, -1)  6.53 us
  transfers between devices with their start and end apart: 7, of which 6 were waited for; matrix products, arithmetic and copies ran while one was open for 18% of the time, Pallas kernels for 0%

commit v1 on v0

--- a/solution.py
+++ b/solution.py
@@ -140,6 +140,119 @@
     return (hankel_gram, reduced_operator, hankel_norm)
 
 
+def permuted_tables(count, wave_index):
+    angle_index = jnp.arange(count, dtype=jnp.int32)
+    residues = wave_index[:, None] * angle_index[None, :] % count
+    phases = 2.0 * math.pi * residues.astype(jnp.float32) / count
+    scaling = 1.0 / math.sqrt(count)
+    return (
+        (jnp.cos(phases) * scaling).astype(jnp.bfloat16),
+        (jnp.sin(phases) * scaling).astype(jnp.bfloat16),
+    )
+
+
+def by_wavenumber(direct_snapshots, adjoint_snapshots, quad_weight, mean_velocity, diffusivity):
+    local_angles, axial_cells, radial_cells, columns = direct_snapshots.shape
+    snap_count = columns // 2
+    band_count = lax.axis_size("ka")
+    axial_count = lax.axis_size("gx")
+    total_angles = local_angles * band_count
+    devices = band_count * axial_count
+    waves_here = total_angles // devices
+    points = axial_cells * radial_cells
+    band = points // band_count
+    band_index = lax.axis_index("ka")
+    axial_index = lax.axis_index("gx")
+
+    row = jnp.arange(total_angles, dtype=jnp.int32)
+    chunk = row // waves_here
+    owner = (chunk % band_count) * axial_count + chunk // band_count
+    wave_index = owner * waves_here + row % waves_here - total_angles // 2
+    cos_table, sin_table = permuted_tables(total_angles, wave_index)
+
+    fields = jnp.stack([mean_velocity, diffusivity])
+    fields = lax.all_gather(fields, "gx", axis=1, tiled=True)
+
+    def gather_angles(snapshots):
+        flat = snapshots.reshape(local_angles, points, columns)
+        return lax.all_to_all(flat, "ka", split_axis=1, concat_axis=0, tiled=True)
+
+    def transform_all(moved):
+        flattened = moved.reshape(total_angles, -1)
+        cos_part = jnp.dot(cos_table, flattened, preferred_element_type=jnp.float32).reshape(
+            moved.shape
+        )
+        sin_part = jnp.dot(sin_table, flattened, preferred_element_type=jnp.float32).reshape(
+            moved.shape
+        )
+        return combine_parts(cos_part, sin_part, snap_count)
+
+    def scatter_waves(modes):
+        return lax.all_to_all(modes, ("gx", "ka"), split_axis=0, concat_axis=1, tiled=True)
+
+    direct_modes = scatter_waves(transform_all(gather_angles(direct_snapshots)))
+    norm_factor = 1.0 / math.sqrt(axial_cells * axial_count * radial_cells)
+    plane_weight = (quad_weight * norm_factor).reshape(points)
+    band_weight = lax.dynamic_slice_in_dim(plane_weight, band_index * band, band)
+    adjoint_modes = transform_all(gather_angles(adjoint_snapshots))
+    weighted = (adjoint_modes.astype(jnp.float32) * band_weight[None, :, None]).astype(jnp.bfloat16)
+    weighted = scatter_waves(weighted)
+
+    all_axial = axial_cells * axial_count
+    field = direct_modes.reshape(waves_here, all_axial, radial_cells, columns)
+    field_f32 = field.astype(jnp.float32)
+    padded = jnp.pad(field_f32, ((0, 0), (1, 1), (1, 1), (0, 0)))
+    forward = padded[:, 2:, 1:-1]
+    behind = padded[:, :-2, 1:-1]
+    outward = padded[:, 1:-1, 2:]
+    inward = padded[:, 1:-1, :-2]
+    radius = 0.25 + (jnp.arange(radial_cells, dtype=jnp.float32) + 0.5) / radial_cells
+    first_wave = (band_index * axial_count + axial_index) * waves_here
+    wavenumber = (
+        first_wave + jnp.arange(waves_here, dtype=jnp.int32) - total_angles // 2
+    ).astype(jnp.float32) / total_angles
+    azimuthal = (wavenumber[:, None] / radius[None, :]) ** 2
+    velocity = fields[0][None, :, :, None]
+    diffusion = fields[1][None, :, :, None]
+    image = (
+        -velocity * (forward - behind) * 0.5
+        + diffusion
+        * (
+            forward
+            + behind
+            + outward
+            + inward
+            - 4.0 * field_f32
+            - azimuthal[:, None, :, None] * field_f32
+        )
+    ).astype(jnp.bfloat16)
+    right_side = jnp.concatenate([field, image], axis=-1)
+    product = jnp.einsum(
+        "kpa,kpb->kab",
+        weighted,
+        right_side.reshape(waves_here, -1, 2 * columns),
+        preferred_element_type=jnp.float32,
+    )
+    gram_terms = complex_blocks(product, snap_count)
+    energy = jnp.sum(gram_terms[..., :columns] ** 2, axis=(1, 2))
+    mean_sq = energy / (2.0 * snap_count * snap_count)
+    scales = lax.rsqrt(mean_sq + epsilon)
+    hankel_gram = (gram_terms[..., :columns] * scales[:, None, None]).reshape(-1, columns)
+    reduced_operator = (gram_terms[..., columns:] * scales[:, None, None]).reshape(-1, columns)
+    hankel_norm = lax.all_gather(jnp.sqrt(mean_sq), "gx", tiled=True)
+    return (hankel_gram, reduced_operator, hankel_norm)
+
+
+def dispatch(direct_snapshots, *rest):
+    local_angles, axial_cells, radial_cells, _ = direct_snapshots.shape
+    band_count = lax.axis_size("ka")
+    devices = band_count * lax.axis_size("gx")
+    whole_waves = (local_angles * band_count) % devices == 0
+    even_bands = (axial_cells * radial_cells) % band_count == 0
+    body = by_wavenumber if whole_waves and even_bands else local
+    return body(direct_snapshots, *rest)
+
+
 def solution(mesh):
     placed = (
         P("ka", "gx", None, None),
@@ -149,7 +262,7 @@
         P("gx", None),
     )
     return jax.shard_map(
-        local,
+        dispatch,
         mesh=mesh,
         in_specs=placed,
         out_specs=(P(("ka", "gx"), None), P(("ka", "gx"), None), P("ka")),

time: 247 us -> 226 us (0.915)
  blocking collectives: 19.1 us -> 87.4 us
  waiting for transfers between devices: 128 us -> 67.1 us
  between operations: 14.3 us -> 1.53 us
  other arithmetic: 19 us -> 9.44 us
  starting transfers between devices: 23.6 us -> 18.8 us
    reduce_scatter x1 -> x0, waiting for transfers between devices: 70.1 us -> none  [local(): lax.psum_scatter(gram_terms, 'gx', scatter_dimension=0, tiled=True)]
    all_gather x0 -> x1, blocking collectives: none -> 67.3 us  [by_wavenumber(): fields = lax.all_gather(fields, 'gx', axis=1, tiled=True)]
    unnamed x0 -> x1, blocking collectives: none -> 20 us
    psum x1 -> x0, blocking collectives: 19.1 us -> none  [local(): energy = lax.psum(jnp.sum(selector * row_energy[:, None], axis=0), 'gx')]
    all_to_all x4, waiting for transfers between devices: 55.6 us -> 67.1 us  [the longest x2 33.6 us: scatter_waves(): lax.all_to_all(modes, ('gx', 'ka'), split_axis=0, concat_axis=1, tiled=True)]
    unnamed x10 -> x16, local copies, waits for them, and re-layouts: 8.55 us -> 16.4 us
    reshape x2 -> x1, local copies, waits for them, and re-layouts: 6.53 us -> 0.08 us  [by_wavenumber(): plane_weight = (quad_weight * norm_factor).reshape(points)]
    ppermute x2 -> x0, starting transfers between devices: 5.72 us -> none  [the longest x1 4.2 us: padded_2(): lax.ppermute(tail, axis, [(i, (i + 1) % count) for i in range(ends)])]
  transfers between devices with their start and end apart: 7 -> 4, of which waited for: 6 -> 3; matrix products, arithmetic and copies ran while one was open for 18% -> 16% of each run, Pallas kernels for 0% -> 0%
where the time goes in v1:
time: 226 us; the launch traced here: 225 us
  blocking collectives  87.4 us (39%)
  waiting for transfers between devices  67.1 us (30%)
  local copies, waits for them, and re-layouts  35.8 us (16%)
  starting transfers between devices  18.8 us (8%)
  other arithmetic  9.44 us (4%)
  matrix products  4.96 us (2%)
    all_gather x1, blocking collectives, by_wavenumber(): fields = lax.all_gather(fields, 'gx', axis=1, tiled=True)  67.3 us
    all_to_all x2, waiting for transfers between devices, scatter_waves(): lax.all_to_all(modes, ('gx', 'ka'), split_axis=0, concat_axis=1, tiled=True)  33.6 us
    all_to_all x2, waiting for transfers between devices, gather_angles(): return lax.all_to_all(flat, 'ka', split_axis=1, concat_axis=0, tiled=True)  33.5 us
    unnamed x1, blocking collectives  20 us
    unnamed x16, local copies, waits for them, and re-layouts  16.4 us
    all_to_all x2, starting transfers between devices, scatter_waves(): lax.all_to_all(modes, ('gx', 'ka'), split_axis=0, concat_axis=1, tiled=True)  10.1 us
    all_to_all x2, starting transfers between devices, gather_angles(): return lax.all_to_all(flat, 'ka', split_axis=1, concat_axis=0, tiled=True)  8.68 us
    dot_general x2, local copies, waits for them, and re-layouts, transform_all(): jnp.dot(cos_table, flattened, preferred_element_type=jnp.float32)  6.43 us
  transfers between devices with their start and end apart: 4, of which 3 were waited for; matrix products, arithmetic and copies ran while one was open for 16% of the time, Pallas kernels for 0%

profile of v1, /device:TPU:0, one launch (start us, length us, event | category | flops | bytes accessed | tf_op | source)
XLA Modules:
  0.0 225.0 jit_solution(7960492328090820535)
XLA Ops:
  0.6 4.3 %copy.30 = bf16[32,4,64,128]{3,0,2,1:T(8,128)(2,1)} copy(bf16[32,4,64,128]{3,2,1,0:T(8,128)(2,1)} %param.6) | data formatting | bytes 4194304 | tf_op args[1]
  4.9 4.2 %all-to-all-start = ((bf16[32,256,128]{2,0,1:T(8,128)(2,1)}), bf16[32,256,128]{2,0,1:T(8,128)(2,1)S(1)}, u32[]{:S(2)}, u32[]{:S(2)}) async-start(bf16[32,256,128]{2,0,1:T(8,128)(2,1)} %bitcast.66), calls=%async_computation | async-start | bytes 4194304 | tf_op jit(solution)/shard_map/all_to_all | solution.py:178
  9.1 4.3 %copy.36 = bf16[32,4,64,128]{3,0,2,1:T(8,128)(2,1)} copy(bf16[32,4,64,128]{3,2,1,0:T(8,128)(2,1)} %param.5) | data formatting | bytes 4194304 | tf_op args[0]
  13.4 21.4 %all-to-all-done = bf16[32,256,128]{2,0,1:T(8,128)(2,1)S(1)} async-done(((bf16[32,256,128]{2,0,1:T(8,128)(2,1)}), bf16[32,256,128]{2,0,1:T(8,128)(2,1)S(1)}, u32[]{:S(2)}, u32[]{:S(2)}) %all-to-all-start) | async-done | bytes 2097184 | tf_op jit(solution)/shard_map/all_to_all | solution.py:178
  34.8 4.4 %all-to-all-start.2 = ((bf16[32,256,128]{2,0,1:T(8,128)(2,1)}), bf16[32,256,128]{2,0,1:T(8,128)(2,1)}, u32[]{:S(2)}, u32[]{:S(2)}) async-start(bf16[32,256,128]{2,0,1:T(8,128)(2,1)} %bitcast.11), calls=%async_computation.2 | async-start | bytes 4194304 | tf_op jit(solution)/shard_map/all_to_all | solution.py:178
  39.3 0.1 reshape.152
  39.4 0.1 dynamic_slice.3
  39.5 0.8 copy.32
  40.3 3.1 %copy.51 = bf16[16,8,64,128]{3,1,2,0:T(8,128)(2,1)} copy(bf16[16,8,64,128]{3,2,1,0:T(8,128)(2,1)S(1)} %bitcast.67) | data formatting | bytes 4194304
  43.4 3.2 %copy.33 = bf16[8192,128]{1,0:T(8,128)(2,1)S(1)} copy(bf16[8192,128]{0,1:T(8,128)(2,1)} %bitcast.68) | data formatting | bytes 4194304 | tf_op jit(solution)/shard_map/dot_general | solution.py:182
  46.6 1.0 fusion.22
  47.6 1.0 fusion.26
  48.6 1.0 fusion.10
  49.7 0.5 multiply_convert_fusion
  50.1 2.8 %copy.34 = bf16[128,64,128]{2,1,0:T(8,128)(2,1)} copy(bf16[128,64,128]{0,2,1:T(8,128)(2,1)S(1)} %multiply_convert_fusion) | data formatting | bytes 4194304 | tf_op jit(solution)/shard_map/convert_element_type | solution.py:198
  53.0 12.1 %all-to-all-done.2 = bf16[32,256,128]{2,0,1:T(8,128)(2,1)} async-done(((bf16[32,256,128]{2,0,1:T(8,128)(2,1)}), bf16[32,256,128]{2,0,1:T(8,128)(2,1)}, u32[]{:S(2)}, u32[]{:S(2)}) %all-to-all-start.2) | async-done | bytes 2097184 | tf_op jit(solution)/shard_map/all_to_all | solution.py:178
  65.0 6.0 %all-to-all-start.1 = ((bf16[128,64,128]{2,1,0:T(8,128)(2,1)}), bf16[128,64,128]{2,1,0:T(8,128)(2,1)}, u32[]{:S(2)}, u32[]{:S(2)}) async-start(bf16[128,64,128]{2,1,0:T(8,128)(2,1)} %copy.34), calls=%async_computation.1 | async-start | bytes 4194304 | tf_op jit(solution)/shard_map/all_to_all | solution.py:191
  71.0 2.4 %copy.38 = bf16[4,32,64,128]{3,2,1,0:T(8,128)(2,1)S(1)} copy(bf16[4,32,64,128]{3,1,2,0:T(8,128)(2,1)} %bitcast.14) | data formatting | bytes 4194304 | tf_op jit(solution)/shard_map/all_to_all | solution.py:178
  73.4 3.1 %copy.50 = bf16[16,8,64,128]{3,1,2,0:T(8,128)(2,1)} copy(bf16[16,8,64,128]{3,2,1,0:T(8,128)(2,1)S(1)} %bitcast.69) | data formatting | bytes 4194304
  76.6 3.2 %copy.39 = bf16[8192,128]{1,0:T(8,128)(2,1)S(1)} copy(bf16[8192,128]{0,1:T(8,128)(2,1)} %bitcast.70) | data formatting | bytes 4194304 | tf_op jit(solution)/shard_map/dot_general | solution.py:182
  79.8 1.0 fusion.20
  80.8 1.0 fusion.24
  81.8 1.0 fusion.8
  82.8 0.1 pad_maximum_fusion.1
  83.0 0.0 copy-start.4
  83.0 0.0 copy-start.2
  83.0 0.0 copy-start.3
  83.0 2.9 %copy.40 = bf16[128,64,128]{2,1,0:T(8,128)(2,1)} copy(bf16[128,64,128]{0,2,1:T(8,128)(2,1)S(1)} %pad_maximum_fusion.1) | data formatting | bytes 4194304 | tf_op jit(solution)/shard_map/concatenate | solution.py:43
  86.0 33.6 %all-to-all-done.1 = bf16[128,64,128]{2,1,0:T(8,128)(2,1)} async-done(((bf16[128,64,128]{2,1,0:T(8,128)(2,1)}), bf16[128,64,128]{2,1,0:T(8,128)(2,1)}, u32[]{:S(2)}, u32[]{:S(2)}) %all-to-all-start.1) | async-done | bytes 2097184 | tf_op jit(solution)/shard_map/all_to_all | solution.py:191
  119.6 4.1 %all-to-all-start.3 = ((bf16[128,64,128]{2,1,0:T(8,128)(2,1)}), bf16[128,64,128]{2,1,0:T(8,128)(2,1)S(1)}, u32[]{:S(2)}, u32[]{:S(2)}) async-start(bf16[128,64,128]{2,1,0:T(8,128)(2,1)} %copy.40), calls=%async_computation.3 | async-start | bytes 4194304 | tf_op jit(solution)/shard_map/all_to_all | solution.py:191
  123.7 0.6 dynamic-slice
  125.0 67.3 %all_gather.6 = f32[2,32,64]{2,0,1:T(2,128)S(1)} all-gather(f32[2,4,64]{2,0,1:T(2,128)S(1)} %pad_maximum_fusion.2), channel_id=1, replica_groups=mesh['gx'=8,'ka'=4] {'gx'}, dimensions={1}, use_global_device_ids=true | all-gather | bytes 18432 | tf_op jit(solution)/shard_map/all_gather | solution.py:174
  192.4 0.1 divide_multiply_fusion
  192.5 3.1 %copy.35 = bf16[4,32,64,128]{3,2,1,0:T(8,128)(2,1)} copy(bf16[4,32,64,128]{3,2,0,1:T(8,128)(2,1)} %bitcast.9) | data formatting | bytes 4194304 | tf_op jit(solution)/shard_map/all_to_all | solution.py:191
  195.6 0.0 all-to-all-done.3
  195.6 0.5 convert_element_type.47
  196.1 3.9 %fusion.6 = bf16[4,32,64,128]{3,2,0,1:T(8,128)(2,1)S(1)} fusion(f32[4,32,64,128]{3,2,0,1:T(8,128)S(1)} %convert_element_type.47, f32[4,64]{1,0:T(4,128)S(1)} %divide_multiply_fusion, f32[32,64]{1,0:T(8,128)S(1)} %bitcast.76, f32[32,64]{1,0:T(8,128)S(1)} %bitcast.75), kind=kLoop, calls=%fused_computation.10 | loop fusion | flops 13631488 | bytes 6308864 | tf_op jit(solution)/shard_map/convert_element_type | solution.py:228
  200.0 0.9 pad_maximum_fusion
  200.9 0.6 copy.41
  201.5 1.0 copy-done
  202.5 1.0 fusion.52
  203.4 0.2 slice_add_fusion.2
  203.6 0.2 fusion.11
  203.8 0.1 sqrt_dynamic-update-slice_fusion
  203.9 0.1 mul.180
  204.0 0.1 mul.181
  204.1 20.0 %all-reduce.1 = f32[32]{0:T(128)} all-reduce(f32[32]{0:T(128)S(1)} %get-tuple-element.15), channel_id=1, replica_groups=mesh['gx'=8,'ka'=4] {'gx'}, use_global_device_ids=true, to_apply=%add.1 | all-reduce | flops 32 | bytes 256
  224.1 0.9 maximum_multiply_fusion.2
  (13 shorter events, 0.1 us)
Async XLA Ops:
  4.9 29.9 %all-to-all-start = ((bf16[32,256,128]{2,0,1:T(8,128)(2,1)}), bf16[32,256,128]{2,0,1:T(8,128)(2,1)S(1)}, u32[]{:S(2)}, u32[]{:S(2)}) async-start(bf16[32,256,128]{2,0,1:T(8,128)(2,1)} %bitcast.66), calls=%async_computation | async-start | bytes 4194304 | tf_op jit(solution)/shard_map/all_to_all | solution.py:178
  9.1 30.2 %copy-start.1 = (f32[4,64]{1,0:T(4,128)S(1)}, f32[4,64]{1,0:T(4,128)}, u32[]{:S(2)}) copy-start(f32[4,64]{1,0:T(4,128)} %param.7) | copy-start | bytes 3076
  34.8 30.2 %all-to-all-start.2 = ((bf16[32,256,128]{2,0,1:T(8,128)(2,1)}), bf16[32,256,128]{2,0,1:T(8,128)(2,1)}, u32[]{:S(2)}, u32[]{:S(2)}) async-start(bf16[32,256,128]{2,0,1:T(8,128)(2,1)} %bitcast.11), calls=%async_computation.2 | async-start | bytes 4194304 | tf_op jit(solution)/shard_map/all_to_all | solution.py:178
  65.0 54.6 %all-to-all-start.1 = ((bf16[128,64,128]{2,1,0:T(8,128)(2,1)}), bf16[128,64,128]{2,1,0:T(8,128)(2,1)}, u32[]{:S(2)}, u32[]{:S(2)}) async-start(bf16[128,64,128]{2,1,0:T(8,128)(2,1)} %copy.34), calls=%async_computation.1 | async-start | bytes 4194304 | tf_op jit(solution)/shard_map/all_to_all | solution.py:191
  83.0 40.7 %copy-start.4 = (u32[32]{0:T(128)S(1)}, u32[32]{0:T(128)}, u32[]{:S(2)}) copy-start(u32[32]{0:T(128)} %constant.119) | copy-start | bytes 388
  83.0 42.0 %copy-start.2 = (f32[4,64]{1,0:T(4,128)S(1)}, f32[4,64]{1,0:T(4,128)}, u32[]{:S(2)}) copy-start(f32[4,64]{1,0:T(4,128)} %param.9) | copy-start | bytes 3076
  83.0 42.0 %copy-start.3 = (f32[4,64]{1,0:T(4,128)S(1)}, f32[4,64]{1,0:T(4,128)}, u32[]{:S(2)}) copy-start(f32[4,64]{1,0:T(4,128)} %param.8) | copy-start | bytes 3076
  119.6 76.0 %all-to-all-start.3 = ((bf16[128,64,128]{2,1,0:T(8,128)(2,1)}), bf16[128,64,128]{2,1,0:T(8,128)(2,1)S(1)}, u32[]{:S(2)}, u32[]{:S(2)}) async-start(bf16[128,64,128]{2,1,0:T(8,128)(2,1)} %copy.40), calls=%async_computation.3 | async-start | bytes 4194304 | tf_op jit(solution)/shard_map/all_to_all | solution.py:191
  200.9 1.6 copy-start

commit v2 on v1

--- a/solution.py
+++ b/solution.py
@@ -140,6 +140,12 @@
     return (hankel_gram, reduced_operator, hankel_norm)
 
 
+def gather_small(values, axis):
+    count = lax.axis_size(axis)
+    copies = jnp.broadcast_to(values[None], (count,) + values.shape)
+    return lax.all_to_all(copies, axis, split_axis=0, concat_axis=0, tiled=True)
+
+
 def permuted_tables(count, wave_index):
     angle_index = jnp.arange(count, dtype=jnp.int32)
     residues = wave_index[:, None] * angle_index[None, :] % count
@@ -170,8 +176,8 @@
     wave_index = owner * waves_here + row % waves_here - total_angles // 2
     cos_table, sin_table = permuted_tables(total_angles, wave_index)
 
-    fields = jnp.stack([mean_velocity, diffusivity])
-    fields = lax.all_gather(fields, "gx", axis=1, tiled=True)
+    fields = gather_small(jnp.stack([mean_velocity, diffusivity]), "gx")
+    fields = jnp.moveaxis(fields, 0, 1).reshape(2, axial_count * axial_cells, radial_cells)
 
     def gather_angles(snapshots):
         flat = snapshots.reshape(local_angles, points, columns)
@@ -239,7 +245,7 @@
     scales = lax.rsqrt(mean_sq + epsilon)
     hankel_gram = (gram_terms[..., :columns] * scales[:, None, None]).reshape(-1, columns)
     reduced_operator = (gram_terms[..., columns:] * scales[:, None, None]).reshape(-1, columns)
-    hankel_norm = lax.all_gather(jnp.sqrt(mean_sq), "gx", tiled=True)
+    hankel_norm = gather_small(jnp.sqrt(mean_sq), "gx").reshape(-1)
     return (hankel_gram, reduced_operator, hankel_norm)
 
 

time: 226 us -> 202 us (0.89)
  blocking collectives: 87.4 us -> 0 us
  waiting for transfers between devices: 67.1 us -> 119 us
  starting transfers between devices: 18.8 us -> 26.5 us
  local copies, waits for them, and re-layouts: 35.8 us -> 38.2 us
    all_gather x1 -> x0, blocking collectives: 67.3 us -> none  [by_wavenumber(): fields = lax.all_gather(fields, 'gx', axis=1, tiled=True)]
    all_to_all x2, waiting for transfers between devices: 33.6 us -> 77.9 us  [scatter_waves(): lax.all_to_all(modes, ('gx', 'ka'), split_axis=0, concat_axis=1, tiled=True)]
    unnamed x1 -> x0, blocking collectives: 20 us -> none
    all_to_all x0 -> x2, starting transfers between devices: none -> 10.8 us  [gather_small(): return lax.all_to_all(copies, axis, split_axis=0, concat_axis=0, tiled=True)]
    all_to_all x0 -> x2, waiting for transfers between devices: none -> 7.91 us  [gather_small(): return lax.all_to_all(copies, axis, split_axis=0, concat_axis=0, tiled=True)]
    all_to_all x2, starting transfers between devices: 10.1 us -> 7.64 us  [scatter_waves(): lax.all_to_all(modes, ('gx', 'ka'), split_axis=0, concat_axis=1, tiled=True)]
    unnamed x16 -> x10, local copies, waits for them, and re-layouts: 16.4 us -> 16.6 us
  transfers between devices with their start and end apart: 4 -> 6, of which waited for: 3 -> 6; matrix products, arithmetic and copies ran while one was open for 16% -> 21% of each run, Pallas kernels for 0% -> 0%
where the time goes in v2:
time: 202 us; the launch traced here: 201 us
  waiting for transfers between devices  119 us (59%)
  local copies, waits for them, and re-layouts  38.2 us (19%)
  starting transfers between devices  26.5 us (13%)
  other arithmetic  11.4 us (6%)
  matrix products  4.97 us (2%)
    all_to_all x2, waiting for transfers between devices, scatter_waves(): lax.all_to_all(modes, ('gx', 'ka'), split_axis=0, concat_axis=1, tiled=True)  77.9 us
    all_to_all x2, waiting for transfers between devices, gather_angles(): return lax.all_to_all(flat, 'ka', split_axis=1, concat_axis=0, tiled=True)  33.4 us
    unnamed x10, local copies, waits for them, and re-layouts  16.6 us
    all_to_all x2, starting transfers between devices, gather_small(): return lax.all_to_all(copies, axis, split_axis=0, concat_axis=0, tiled=True)  10.8 us
    all_to_all x2, starting transfers between devices, gather_angles(): return lax.all_to_all(flat, 'ka', split_axis=1, concat_axis=0, tiled=True)  8.06 us
    all_to_all x2, waiting for transfers between devices, gather_small(): return lax.all_to_all(copies, axis, split_axis=0, concat_axis=0, tiled=True)  7.91 us
    all_to_all x2, starting transfers between devices, scatter_waves(): lax.all_to_all(modes, ('gx', 'ka'), split_axis=0, concat_axis=1, tiled=True)  7.64 us
    dot_general x2, local copies, waits for them, and re-layouts, transform_all(): jnp.dot(cos_table, flattened, preferred_element_type=jnp.float32)  6.43 us
  transfers between devices with their start and end apart: 6, of which 6 were waited for; matrix products, arithmetic and copies ran while one was open for 21% of the time, Pallas kernels for 0%

profile of v2, /device:TPU:0, one launch (start us, length us, event | category | flops | bytes accessed | tf_op | source)
XLA Modules:
  0.0 201.2 jit_solution(8823420122211340814)
XLA Ops:
  0.6 0.7 pad_maximum_fusion.2
  1.3 0.7 reshape.188
  2.0 7.3 %all-to-all-start.4 = ((f32[8,1,512]{2,1,0:T(1,128)}), f32[8,1,512]{2,1,0:T(1,128)S(1)}, u32[]{:S(2)}, u32[]{:S(2)}) async-start(f32[8,1,512]{2,1,0:T(1,128)} %reshape.188), calls=%async_computation.4 | async-start | bytes 32768 | tf_op jit(solution)/shard_map/all_to_all | solution.py:146
  9.3 4.3 %copy.29 = bf16[32,4,64,128]{3,0,2,1:T(8,128)(2,1)} copy(bf16[32,4,64,128]{3,2,1,0:T(8,128)(2,1)} %param.6) | data formatting | bytes 4194304 | tf_op args[1]
  13.6 2.3 %all-to-all-done.4 = f32[8,1,512]{2,1,0:T(1,128)S(1)} async-done(((f32[8,1,512]{2,1,0:T(1,128)}), f32[8,1,512]{2,1,0:T(1,128)S(1)}, u32[]{:S(2)}, u32[]{:S(2)}) %all-to-all-start.4) | async-done | bytes 16416 | tf_op jit(solution)/shard_map/all_to_all | solution.py:146
  15.9 3.6 %all-to-all-start = ((bf16[32,256,128]{2,0,1:T(8,128)(2,1)}), bf16[32,256,128]{2,0,1:T(8,128)(2,1)S(1)}, u32[]{:S(2)}, u32[]{:S(2)}) async-start(bf16[32,256,128]{2,0,1:T(8,128)(2,1)} %bitcast.66), calls=%async_computation | async-start | bytes 4194304 | tf_op jit(solution)/shard_map/all_to_all | solution.py:184
  19.5 4.3 %copy.35 = bf16[32,4,64,128]{3,0,2,1:T(8,128)(2,1)} copy(bf16[32,4,64,128]{3,2,1,0:T(8,128)(2,1)} %param.5) | data formatting | bytes 4194304 | tf_op args[0]
  23.8 21.4 %all-to-all-done = bf16[32,256,128]{2,0,1:T(8,128)(2,1)S(1)} async-done(((bf16[32,256,128]{2,0,1:T(8,128)(2,1)}), bf16[32,256,128]{2,0,1:T(8,128)(2,1)S(1)}, u32[]{:S(2)}, u32[]{:S(2)}) %all-to-all-start) | async-done | bytes 2097184 | tf_op jit(solution)/shard_map/all_to_all | solution.py:184
  45.2 4.5 %all-to-all-start.2 = ((bf16[32,256,128]{2,0,1:T(8,128)(2,1)}), bf16[32,256,128]{2,0,1:T(8,128)(2,1)}, u32[]{:S(2)}, u32[]{:S(2)}) async-start(bf16[32,256,128]{2,0,1:T(8,128)(2,1)} %bitcast.11), calls=%async_computation.2 | async-start | bytes 4194304 | tf_op jit(solution)/shard_map/all_to_all | solution.py:184
  49.8 0.8 copy.31
  50.6 3.1 %copy.50 = bf16[16,8,64,128]{3,1,2,0:T(8,128)(2,1)} copy(bf16[16,8,64,128]{3,2,1,0:T(8,128)(2,1)S(1)} %bitcast.67) | data formatting | bytes 4194304
  53.7 3.2 %copy.32 = bf16[8192,128]{1,0:T(8,128)(2,1)S(1)} copy(bf16[8192,128]{0,1:T(8,128)(2,1)} %bitcast.68) | data formatting | bytes 4194304 | tf_op jit(solution)/shard_map/dot_general | solution.py:188
  57.0 1.0 fusion.22
  58.0 1.0 fusion.26
  59.0 1.0 fusion.10
  60.0 0.5 multiply_convert_fusion
  60.5 2.8 %copy.33 = bf16[128,64,128]{2,1,0:T(8,128)(2,1)} copy(bf16[128,64,128]{0,2,1:T(8,128)(2,1)S(1)} %multiply_convert_fusion) | data formatting | bytes 4194304 | tf_op jit(solution)/shard_map/convert_element_type | solution.py:204
  63.3 12.0 %all-to-all-done.2 = bf16[32,256,128]{2,0,1:T(8,128)(2,1)} async-done(((bf16[32,256,128]{2,0,1:T(8,128)(2,1)}), bf16[32,256,128]{2,0,1:T(8,128)(2,1)}, u32[]{:S(2)}, u32[]{:S(2)}) %all-to-all-start.2) | async-done | bytes 2097184 | tf_op jit(solution)/shard_map/all_to_all | solution.py:184
  75.4 3.7 %all-to-all-start.1 = ((bf16[128,64,128]{2,1,0:T(8,128)(2,1)}), bf16[128,64,128]{2,1,0:T(8,128)(2,1)}, u32[]{:S(2)}, u32[]{:S(2)}) async-start(bf16[128,64,128]{2,1,0:T(8,128)(2,1)} %copy.33), calls=%async_computation.1 | async-start | bytes 4194304 | tf_op jit(solution)/shard_map/all_to_all | solution.py:197
  79.0 2.4 %copy.37 = bf16[4,32,64,128]{3,2,1,0:T(8,128)(2,1)S(1)} copy(bf16[4,32,64,128]{3,1,2,0:T(8,128)(2,1)} %bitcast.14) | data formatting | bytes 4194304 | tf_op jit(solution)/shard_map/all_to_all | solution.py:184
  81.4 3.1 %copy.49 = bf16[16,8,64,128]{3,1,2,0:T(8,128)(2,1)} copy(bf16[16,8,64,128]{3,2,1,0:T(8,128)(2,1)S(1)} %bitcast.69) | data formatting | bytes 4194304
  84.6 3.2 %copy.38 = bf16[8192,128]{1,0:T(8,128)(2,1)S(1)} copy(bf16[8192,128]{0,1:T(8,128)(2,1)} %bitcast.70) | data formatting | bytes 4194304 | tf_op jit(solution)/shard_map/dot_general | solution.py:188
  87.8 1.0 fusion.20
  88.8 1.0 fusion.24
  89.8 1.0 fusion.8
  90.8 0.1 pad_maximum_fusion.1
  91.0 2.9 %copy.39 = bf16[128,64,128]{2,1,0:T(8,128)(2,1)} copy(bf16[128,64,128]{0,2,1:T(8,128)(2,1)S(1)} %pad_maximum_fusion.1) | data formatting | bytes 4194304 | tf_op jit(solution)/shard_map/concatenate | solution.py:43
  93.9 33.7 %all-to-all-done.1 = bf16[128,64,128]{2,1,0:T(8,128)(2,1)} async-done(((bf16[128,64,128]{2,1,0:T(8,128)(2,1)}), bf16[128,64,128]{2,1,0:T(8,128)(2,1)}, u32[]{:S(2)}, u32[]{:S(2)}) %all-to-all-start.1) | async-done | bytes 2097184 | tf_op jit(solution)/shard_map/all_to_all | solution.py:197
  127.6 4.0 %all-to-all-start.3 = ((bf16[128,64,128]{2,1,0:T(8,128)(2,1)}), bf16[128,64,128]{2,1,0:T(8,128)(2,1)S(1)}, u32[]{:S(2)}, u32[]{:S(2)}) async-start(bf16[128,64,128]{2,1,0:T(8,128)(2,1)} %copy.39), calls=%async_computation.3 | async-start | bytes 4194304 | tf_op jit(solution)/shard_map/all_to_all | solution.py:197
  131.7 0.5 broadcast.244
  132.2 0.7 reduce.4
  133.0 3.1 %copy.34 = bf16[4,32,64,128]{3,2,1,0:T(8,128)(2,1)} copy(bf16[4,32,64,128]{3,2,0,1:T(8,128)(2,1)} %bitcast.9) | data formatting | bytes 4194304 | tf_op jit(solution)/shard_map/all_to_all | solution.py:197
  136.1 44.2 %all-to-all-done.3 = bf16[128,64,128]{2,1,0:T(8,128)(2,1)S(1)} async-done(((bf16[128,64,128]{2,1,0:T(8,128)(2,1)}), bf16[128,64,128]{2,1,0:T(8,128)(2,1)S(1)}, u32[]{:S(2)}, u32[]{:S(2)}) %all-to-all-start.3) | async-done | bytes 2097184 | tf_op jit(solution)/shard_map/all_to_all | solution.py:197
  180.3 0.5 convert_element_type.47
  180.8 3.9 %fusion.6 = bf16[4,32,64,128]{3,2,0,1:T(8,128)(2,1)S(1)} fusion(f32[4,32,64,128]{3,2,0,1:T(8,128)S(1)} %convert_element_type.47, f32[4,64]{1,0:T(4,128)S(1)} %divide_multiply_fusion, f32[32,64]{1,0:T(8,128)S(1)} %bitcast.77, f32[32,64]{1,0:T(8,128)S(1)} %bitcast.76), kind=kLoop, calls=%fused_computation.10 | loop fusion | flops 13631488 | bytes 6308864 | tf_op jit(solution)/shard_map/convert_element_type | solution.py:234
  184.8 0.9 pad_maximum_fusion
  185.6 0.6 copy.40
  186.2 1.0 copy-done
  187.2 1.0 fusion.52
  188.2 0.2 slice_add_fusion.2
  188.4 0.2 fusion.11
  188.8 0.6 broadcast_in_dim.5
  189.4 3.6 %all-to-all-start.5 = ((f32[8,1,4]{2,1,0:T(1,128)}), f32[8,1,4]{2,1,0:T(1,128)S(1)}, u32[]{:S(2)}, u32[]{:S(2)}) async-start(f32[8,1,4]{2,1,0:T(1,128)} %broadcast_in_dim.5), calls=%async_computation.5 | async-start | bytes 8192 | tf_op jit(solution)/shard_map/all_to_all | solution.py:146
  192.9 0.9 maximum_multiply_fusion.2
  193.8 5.6 %all-to-all-done.5 = f32[8,1,4]{2,1,0:T(1,128)S(1)} async-done(((f32[8,1,4]{2,1,0:T(1,128)}), f32[8,1,4]{2,1,0:T(1,128)S(1)}, u32[]{:S(2)}, u32[]{:S(2)}) %all-to-all-start.5) | async-done | bytes 160 | tf_op jit(solution)/shard_map/all_to_all | solution.py:146
  199.4 0.5 broadcast.243
  199.9 0.7 reduce.3
  200.6 0.6 reshape.176
  (16 shorter events, 0.5 us)
Async XLA Ops:
  2.0 13.8 %all-to-all-start.4 = ((f32[8,1,512]{2,1,0:T(1,128)}), f32[8,1,512]{2,1,0:T(1,128)S(1)}, u32[]{:S(2)}, u32[]{:S(2)}) async-start(f32[8,1,512]{2,1,0:T(1,128)} %reshape.188), calls=%async_computation.4 | async-start | bytes 32768 | tf_op jit(solution)/shard_map/all_to_all | solution.py:146
  15.9 29.3 %all-to-all-start = ((bf16[32,256,128]{2,0,1:T(8,128)(2,1)}), bf16[32,256,128]{2,0,1:T(8,128)(2,1)S(1)}, u32[]{:S(2)}, u32[]{:S(2)}) async-start(bf16[32,256,128]{2,0,1:T(8,128)(2,1)} %bitcast.66), calls=%async_computation | async-start | bytes 4194304 | tf_op jit(solution)/shard_map/all_to_all | solution.py:184
  19.5 30.1 %copy-start.1 = (f32[4,64]{1,0:T(4,128)S(1)}, f32[4,64]{1,0:T(4,128)}, u32[]{:S(2)}) copy-start(f32[4,64]{1,0:T(4,128)} %param.7) | copy-start | bytes 3076
  45.2 30.2 %all-to-all-start.2 = ((bf16[32,256,128]{2,0,1:T(8,128)(2,1)}), bf16[32,256,128]{2,0,1:T(8,128)(2,1)}, u32[]{:S(2)}, u32[]{:S(2)}) async-start(bf16[32,256,128]{2,0,1:T(8,128)(2,1)} %bitcast.11), calls=%async_computation.2 | async-start | bytes 4194304 | tf_op jit(solution)/shard_map/all_to_all | solution.py:184
  75.4 52.2 %all-to-all-start.1 = ((bf16[128,64,128]{2,1,0:T(8,128)(2,1)}), bf16[128,64,128]{2,1,0:T(8,128)(2,1)}, u32[]{:S(2)}, u32[]{:S(2)}) async-start(bf16[128,64,128]{2,1,0:T(8,128)(2,1)} %copy.33), calls=%async_computation.1 | async-start | bytes 4194304 | tf_op jit(solution)/shard_map/all_to_all | solution.py:197
  127.6 52.8 %all-to-all-start.3 = ((bf16[128,64,128]{2,1,0:T(8,128)(2,1)}), bf16[128,64,128]{2,1,0:T(8,128)(2,1)S(1)}, u32[]{:S(2)}, u32[]{:S(2)}) async-start(bf16[128,64,128]{2,1,0:T(8,128)(2,1)} %copy.39), calls=%async_computation.3 | async-start | bytes 4194304 | tf_op jit(solution)/shard_map/all_to_all | solution.py:197
  185.6 1.6 copy-start
  189.4 10.0 %all-to-all-start.5 = ((f32[8,1,4]{2,1,0:T(1,128)}), f32[8,1,4]{2,1,0:T(1,128)S(1)}, u32[]{:S(2)}, u32[]{:S(2)}) async-start(f32[8,1,4]{2,1,0:T(1,128)} %broadcast_in_dim.5), calls=%async_computation.5 | async-start | bytes 8192 | tf_op jit(solution)/shard_map/all_to_all | solution.py:146

commit v3 on v2

--- a/solution.py
+++ b/solution.py
@@ -157,31 +157,33 @@
     )
 
 
-def by_wavenumber(direct_snapshots, adjoint_snapshots, quad_weight, mean_velocity, diffusivity):
+def by_band(direct_snapshots, adjoint_snapshots, quad_weight, mean_velocity, diffusivity):
     local_angles, axial_cells, radial_cells, columns = direct_snapshots.shape
     snap_count = columns // 2
     band_count = lax.axis_size("ka")
     axial_count = lax.axis_size("gx")
     total_angles = local_angles * band_count
-    devices = band_count * axial_count
-    waves_here = total_angles // devices
-    points = axial_cells * radial_cells
-    band = points // band_count
+    chunk_waves = total_angles // axial_count
+    waves_here = chunk_waves // band_count
+    band = radial_cells // band_count
     band_index = lax.axis_index("ka")
     axial_index = lax.axis_index("gx")
+    all_axial = axial_cells * axial_count
 
     row = jnp.arange(total_angles, dtype=jnp.int32)
-    chunk = row // waves_here
-    owner = (chunk % band_count) * axial_count + chunk // band_count
+    sub = (row % chunk_waves) // waves_here
+    owner = sub * axial_count + row // chunk_waves
     wave_index = owner * waves_here + row % waves_here - total_angles // 2
     cos_table, sin_table = permuted_tables(total_angles, wave_index)
 
     fields = gather_small(jnp.stack([mean_velocity, diffusivity]), "gx")
-    fields = jnp.moveaxis(fields, 0, 1).reshape(2, axial_count * axial_cells, radial_cells)
+    fields = jnp.moveaxis(fields, 0, 1).reshape(2, all_axial, radial_cells)
+    fields = lax.dynamic_slice_in_dim(fields, band_index * band, band, axis=2)
 
     def gather_angles(snapshots):
-        flat = snapshots.reshape(local_angles, points, columns)
-        return lax.all_to_all(flat, "ka", split_axis=1, concat_axis=0, tiled=True)
+        split = snapshots.reshape(local_angles, axial_cells, band_count, band, columns)
+        moved = lax.all_to_all(split, "ka", split_axis=2, concat_axis=0, tiled=True)
+        return moved.reshape(total_angles, axial_cells, band, columns)
 
     def transform_all(moved):
         flattened = moved.reshape(total_angles, -1)
@@ -193,30 +195,34 @@
         )
         return combine_parts(cos_part, sin_part, snap_count)
 
-    def scatter_waves(modes):
-        return lax.all_to_all(modes, ("gx", "ka"), split_axis=0, concat_axis=1, tiled=True)
-
-    direct_modes = scatter_waves(transform_all(gather_angles(direct_snapshots)))
-    norm_factor = 1.0 / math.sqrt(axial_cells * axial_count * radial_cells)
-    plane_weight = (quad_weight * norm_factor).reshape(points)
-    band_weight = lax.dynamic_slice_in_dim(plane_weight, band_index * band, band)
+    def gather_axial(modes):
+        return lax.all_to_all(modes, "gx", split_axis=0, concat_axis=1, tiled=True)
+
+    field = gather_axial(transform_all(gather_angles(direct_snapshots)))
+    norm_factor = 1.0 / math.sqrt(all_axial * radial_cells)
+    plane_weight = lax.dynamic_slice_in_dim(quad_weight * norm_factor, band_index * band, band, axis=1)
     adjoint_modes = transform_all(gather_angles(adjoint_snapshots))
-    weighted = (adjoint_modes.astype(jnp.float32) * band_weight[None, :, None]).astype(jnp.bfloat16)
-    weighted = scatter_waves(weighted)
-
-    all_axial = axial_cells * axial_count
-    field = direct_modes.reshape(waves_here, all_axial, radial_cells, columns)
+    weighted = (adjoint_modes.astype(jnp.float32) * plane_weight[None, :, :, None]).astype(
+        jnp.bfloat16
+    )
+    weighted = gather_axial(weighted)
+
     field_f32 = field.astype(jnp.float32)
-    padded = jnp.pad(field_f32, ((0, 0), (1, 1), (1, 1), (0, 0)))
-    forward = padded[:, 2:, 1:-1]
-    behind = padded[:, :-2, 1:-1]
-    outward = padded[:, 1:-1, 2:]
-    inward = padded[:, 1:-1, :-2]
-    radius = 0.25 + (jnp.arange(radial_cells, dtype=jnp.float32) + 0.5) / radial_cells
-    first_wave = (band_index * axial_count + axial_index) * waves_here
-    wavenumber = (
-        first_wave + jnp.arange(waves_here, dtype=jnp.int32) - total_angles // 2
-    ).astype(jnp.float32) / total_angles
+    radial_halo = padded_2(field, (("ka", 2),), 1).astype(jnp.float32)
+    outward = radial_halo[:, :, 2:]
+    inward = radial_halo[:, :, :-2]
+    axial_pad = jnp.pad(field_f32, ((0, 0), (1, 1), (0, 0), (0, 0)))
+    forward = axial_pad[:, 2:]
+    behind = axial_pad[:, :-2]
+    radial_index = (band_index * band + jnp.arange(band, dtype=jnp.int32)).astype(jnp.float32)
+    radius = 0.25 + (radial_index + 0.5) / radial_cells
+    local_row = jnp.arange(chunk_waves, dtype=jnp.int32)
+    local_wave = (
+        ((local_row // waves_here) * axial_count + axial_index) * waves_here
+        + local_row % waves_here
+        - total_angles // 2
+    )
+    wavenumber = local_wave.astype(jnp.float32) / total_angles
     azimuthal = (wavenumber[:, None] / radius[None, :]) ** 2
     velocity = fields[0][None, :, :, None]
     diffusion = fields[1][None, :, :, None]
@@ -235,11 +241,12 @@
     right_side = jnp.concatenate([field, image], axis=-1)
     product = jnp.einsum(
         "kpa,kpb->kab",
-        weighted,
-        right_side.reshape(waves_here, -1, 2 * columns),
+        weighted.reshape(chunk_waves, -1, columns),
+        right_side.reshape(chunk_waves, -1, 2 * columns),
         preferred_element_type=jnp.float32,
     )
-    gram_terms = complex_blocks(product, snap_count)
+    partial = complex_blocks(product, snap_count).reshape(band_count, waves_here, snap_count, 2 * columns)
+    gram_terms = jnp.sum(lax.all_to_all(partial, "ka", split_axis=0, concat_axis=0, tiled=True), axis=0)
     energy = jnp.sum(gram_terms[..., :columns] ** 2, axis=(1, 2))
     mean_sq = energy / (2.0 * snap_count * snap_count)
     scales = lax.rsqrt(mean_sq + epsilon)
@@ -250,12 +257,13 @@
 
 
 def dispatch(direct_snapshots, *rest):
-    local_angles, axial_cells, radial_cells, _ = direct_snapshots.shape
+    local_angles, _, radial_cells, _ = direct_snapshots.shape
     band_count = lax.axis_size("ka")
-    devices = band_count * lax.axis_size("gx")
-    whole_waves = (local_angles * band_count) % devices == 0
-    even_bands = (axial_cells * radial_cells) % band_count == 0
-    body = by_wavenumber if whole_waves and even_bands else local
+    axial_count = lax.axis_size("gx")
+    total_angles = local_angles * band_count
+    whole_waves = total_angles % (axial_count * band_count) == 0
+    even_bands = radial_cells % band_count == 0
+    body = by_band if whole_waves and even_bands else local
     return body(direct_snapshots, *rest)
 
 

time: 202 us -> 221 us (1.094)
  blocking collectives: 0 us -> 16.9 us
  starting transfers between devices: 26.5 us -> 30.4 us
  local copies, waits for them, and re-layouts: 38.2 us -> 34.4 us
  other arithmetic: 11.4 us -> 14.4 us
    all_to_all x0 -> x1, blocking collectives: none -> 16.9 us  [by_band(): lax.all_to_all(partial, 'ka', split_axis=0, concat_axis=0, tiled=True)]
    unnamed x10 -> x6, local copies, waits for them, and re-layouts: 16.6 us -> 1.2 us
    reshape x2 -> x3, local copies, waits for them, and re-layouts: 0.67 us -> 7.68 us  [the longest x2 7.09 us: gather_angles(): snapshots.reshape(local_angles, axial_cells, band_count, band, columns)]
    another operation x0 -> x2, local copies, waits for them, and re-layouts: none -> 6.52 us  [transform_all(): flattened = moved.reshape(total_angles, -1)]
    convert_element_type x3 -> x4, other arithmetic: 4.86 us -> 7.87 us  [the longest x1 3.26 us: by_band(): image = (-velocity * (forward - behind) * 0.5 + diffusion * (forward + be...]
    ppermute x0 -> x2, starting transfers between devices: none -> 2.78 us  [the longest x1 1.47 us: padded_2(): lax.ppermute(head, axis, [((i + 1) % count, i) for i in range(ends)])]
    all_to_all x4, waiting for transfers between devices: 111 us -> 109 us  [the longest x2 72.6 us: gather_axial(): return lax.all_to_all(modes, 'gx', split_axis=0, concat_axis=1, tiled=True)]
    all_to_all x3 -> x2, local copies, waits for them, and re-layouts: 6.35 us -> 4.23 us  [gather_axial(): return lax.all_to_all(modes, 'gx', split_axis=0, concat_axis=1, tiled=True)]
  transfers between devices with their start and end apart: 6 -> 8, of which waited for: 6 -> 6; matrix products, arithmetic and copies ran while one was open for 21% -> 19% of each run, Pallas kernels for 0% -> 0%
where the time goes in v3:
time: 221 us; the launch traced here: 219 us
  waiting for transfers between devices  117 us (53%)
  local copies, waits for them, and re-layouts  34.4 us (16%)
  starting transfers between devices  30.4 us (14%)
  blocking collectives  16.9 us (8%)
  other arithmetic  14.4 us (7%)
  matrix products  5.12 us (2%)
    all_to_all x2, waiting for transfers between devices, gather_axial(): return lax.all_to_all(modes, 'gx', split_axis=0, concat_axis=1, tiled=True)  72.6 us
    all_to_all x2, waiting for transfers between devices, gather_angles(): moved = lax.all_to_all(split, 'ka', split_axis=2, concat_axis=0, tiled=True)  36.1 us
    all_to_all x1, blocking collectives, by_band(): lax.all_to_all(partial, 'ka', split_axis=0, concat_axis=0, tiled=True)  16.9 us
    all_to_all x2, starting transfers between devices, gather_small(): return lax.all_to_all(copies, axis, split_axis=0, concat_axis=0, tiled=True)  10.9 us
    all_to_all x2, waiting for transfers between devices, gather_small(): return lax.all_to_all(copies, axis, split_axis=0, concat_axis=0, tiled=True)  8.7 us
    all_to_all x2, starting transfers between devices, gather_axial(): return lax.all_to_all(modes, 'gx', split_axis=0, concat_axis=1, tiled=True)  8.68 us
    all_to_all x2, starting transfers between devices, gather_angles(): moved = lax.all_to_all(split, 'ka', split_axis=2, concat_axis=0, tiled=True)  8.06 us
    reshape x2, local copies, waits for them, and re-layouts, gather_angles(): snapshots.reshape(local_angles, axial_cells, band_count, band, columns)  7.09 us
  transfers between devices with their start and end apart: 8, of which 6 were waited for; matrix products, arithmetic and copies ran while one was open for 19% of the time, Pallas kernels for 0%

profile of v3, /device:TPU:0, one launch (start us, length us, event | category | flops | bytes accessed | tf_op | source)
XLA Modules:
  0.0 219.5 jit_solution(15952264026283520068)
XLA Ops:
  0.6 0.7 pad_maximum_fusion.2
  1.3 0.7 reshape.200
  2.0 7.3 %all-to-all-start.4 = ((f32[8,1,512]{2,1,0:T(1,128)}), f32[8,1,512]{2,1,0:T(1,128)S(1)}, u32[]{:S(2)}, u32[]{:S(2)}) async-start(f32[8,1,512]{2,1,0:T(1,128)} %reshape.200), calls=%async_computation.4 | async-start | bytes 32768 | tf_op jit(solution)/shard_map/all_to_all | solution.py:146
  9.3 3.6 %copy.36 = bf16[32,4,4,16,128]{4,3,1,0,2:T(8,128)(2,1)} copy(bf16[32,4,4,16,128]{4,3,2,1,0:T(8,128)(2,1)} %bitcast.71) | data formatting | bytes 4194304 | tf_op jit(solution)/shard_map/reshape | solution.py:184
  12.8 3.0 %all-to-all-done.4 = f32[8,1,512]{2,1,0:T(1,128)S(1)} async-done(((f32[8,1,512]{2,1,0:T(1,128)}), f32[8,1,512]{2,1,0:T(1,128)S(1)}, u32[]{:S(2)}, u32[]{:S(2)}) %all-to-all-start.4) | async-done | bytes 16416 | tf_op jit(solution)/shard_map/all_to_all | solution.py:146
  15.9 3.6 %all-to-all-start.2 = ((bf16[32,4,4,16,128]{4,3,1,0,2:T(8,128)(2,1)}), bf16[32,4,4,16,128]{4,3,1,0,2:T(8,128)(2,1)S(1)}, u32[]{:S(2)}, u32[]{:S(2)}) async-start(bf16[32,4,4,16,128]{4,3,1,0,2:T(8,128)(2,1)} %copy.36), calls=%async_computation.2 | async-start | bytes 4194304 | tf_op jit(solution)/shard_map/all_to_all | solution.py:185
  19.5 3.5 %copy.32 = bf16[32,4,4,16,128]{4,3,1,0,2:T(8,128)(2,1)} copy(bf16[32,4,4,16,128]{4,3,2,1,0:T(8,128)(2,1)} %bitcast.72) | data formatting | bytes 4194304 | tf_op jit(solution)/shard_map/reshape | solution.py:184
  23.0 22.1 %all-to-all-done.2 = bf16[32,4,4,16,128]{4,3,1,0,2:T(8,128)(2,1)S(1)} async-done(((bf16[32,4,4,16,128]{4,3,1,0,2:T(8,128)(2,1)}), bf16[32,4,4,16,128]{4,3,1,0,2:T(8,128)(2,1)S(1)}, u32[]{:S(2)}, u32[]{:S(2)}) %all-to-all-start.2) | async-done | bytes 2097184 | tf_op jit(solution)/shard_map/all_to_all | solution.py:185
  45.2 4.5 %all-to-all-start = ((bf16[32,4,4,16,128]{4,3,1,0,2:T(8,128)(2,1)}), bf16[32,4,4,16,128]{4,3,1,0,2:T(8,128)(2,1)}, u32[]{:S(2)}, u32[]{:S(2)}) async-start(bf16[32,4,4,16,128]{4,3,1,0,2:T(8,128)(2,1)} %copy.32), calls=%async_computation | async-start | bytes 4194304 | tf_op jit(solution)/shard_map/all_to_all | solution.py:185
  49.6 2.3 %reshape_reshape.7 = bf16[128,8192]{1,0:T(8,128)(2,1)} reshape(bf16[4,32,4,1,16,128]{5,4,2,1,0,3:T(8,128)(2,1)S(1)} %bitcast.66) | data formatting | bytes 4194304 | tf_op jit(solution)/shard_map/reshape;reshape | solution.py:189
  51.9 3.2 %copy.37 = bf16[8192,128]{1,0:T(8,128)(2,1)S(1)} copy(bf16[8192,128]{0,1:T(8,128)(2,1)} %bitcast.67) | data formatting | bytes 4194304 | tf_op jit(solution)/shard_map/dot_general | solution.py:190
  55.2 1.0 fusion.21
  56.2 1.0 fusion.25
  57.2 1.0 fusion.10
  58.3 3.1 %copy.38 = bf16[128,4,16,128]{3,2,1,0:T(8,128)(2,1)} copy(bf16[128,4,16,128]{0,3,2,1:T(8,128)(2,1)S(1)} %pad_maximum_fusion) | data formatting | bytes 4194304 | tf_op jit(solution)/shard_map/concatenate | solution.py:43
  61.4 14.0 %all-to-all-done = bf16[32,4,4,16,128]{4,3,1,0,2:T(8,128)(2,1)} async-done(((bf16[32,4,4,16,128]{4,3,1,0,2:T(8,128)(2,1)}), bf16[32,4,4,16,128]{4,3,1,0,2:T(8,128)(2,1)}, u32[]{:S(2)}, u32[]{:S(2)}) %all-to-all-start) | async-done | bytes 2097184 | tf_op jit(solution)/shard_map/all_to_all | solution.py:185
  75.4 4.3 %all-to-all-start.3 = ((bf16[128,4,16,128]{3,2,1,0:T(8,128)(2,1)}), bf16[128,4,16,128]{3,2,1,0:T(8,128)(2,1)}, u32[]{:S(2)}, u32[]{:S(2)}) async-start(bf16[128,4,16,128]{3,2,1,0:T(8,128)(2,1)} %copy.38), calls=%async_computation.3 | async-start | bytes 4194304 | tf_op jit(solution)/shard_map/all_to_all | solution.py:199
  79.8 4.2 %reshape_reshape.6 = bf16[128,8192]{1,0:T(8,128)(2,1)} reshape(bf16[4,32,4,1,16,128]{5,4,2,1,0,3:T(8,128)(2,1)} %bitcast.4) | data formatting | bytes 4194304 | tf_op jit(solution)/shard_map/reshape;reshape | solution.py:189
  84.0 3.2 %copy.33 = bf16[8192,128]{1,0:T(8,128)(2,1)S(1)} copy(bf16[8192,128]{0,1:T(8,128)(2,1)} %bitcast.68) | data formatting | bytes 4194304 | tf_op jit(solution)/shard_map/dot_general | solution.py:190
  87.3 1.0 fusion.23
  88.3 1.0 fusion.27
  89.3 1.0 fusion.12
  90.3 0.5 multiply_convert_fusion
  90.8 3.0 %copy.34 = bf16[128,4,16,128]{3,2,1,0:T(8,128)(2,1)} copy(bf16[128,4,16,128]{0,3,2,1:T(8,128)(2,1)S(1)} %multiply_convert_fusion) | data formatting | bytes 4194304 | tf_op jit(solution)/shard_map/convert_element_type | solution.py:205
  93.8 34.3 %all-to-all-done.3 = bf16[128,4,16,128]{3,2,1,0:T(8,128)(2,1)} async-done(((bf16[128,4,16,128]{3,2,1,0:T(8,128)(2,1)}), bf16[128,4,16,128]{3,2,1,0:T(8,128)(2,1)}, u32[]{:S(2)}, u32[]{:S(2)}) %all-to-all-start.3) | async-done | bytes 2097184 | tf_op jit(solution)/shard_map/all_to_all | solution.py:199
  128.0 4.3 %all-to-all-start.1 = ((bf16[128,4,16,128]{3,2,1,0:T(8,128)(2,1)}), bf16[128,4,16,128]{3,2,1,0:T(8,128)(2,1)}, u32[]{:S(2)}, u32[]{:S(2)}) async-start(bf16[128,4,16,128]{3,2,1,0:T(8,128)(2,1)} %copy.34), calls=%async_computation.1 | async-start | bytes 4194304 | tf_op jit(solution)/shard_map/all_to_all | solution.py:199
  132.4 2.2 copy.39
  134.6 0.6 fusion.62
  135.2 1.3 collective-permute-start
  136.5 1.5 collective-permute-start.1
  138.0 0.5 broadcast.325
  138.5 0.7 reduce.4
  139.4 2.4 %convert_element_type.57 = f32[16,32,16,128]{3,2,1,0:T(8,128)} convert(bf16[16,32,16,128]{3,2,1,0:T(8,128)(2,1)S(1)} %bitcast.59) | non-fusion elementwise | flops 1048576 | bytes 6291456 | tf_op jit(solution)/shard_map/convert_element_type | solution.py:210
  141.8 38.4 %all-to-all-done.1 = bf16[128,4,16,128]{3,2,1,0:T(8,128)(2,1)} async-done(((bf16[128,4,16,128]{3,2,1,0:T(8,128)(2,1)}), bf16[128,4,16,128]{3,2,1,0:T(8,128)(2,1)}, u32[]{:S(2)}, u32[]{:S(2)}) %all-to-all-start.1) | async-done | bytes 2097184 | tf_op jit(solution)/shard_map/all_to_all | solution.py:199
  180.2 2.1 copy.35
  182.3 1.7 maximum_convert_fusion
  184.4 3.3 %fusion.4 = bf16[16,32,16,128]{3,2,1,0:T(8,128)(2,1)S(1)} fusion(f32[16,32,18,128]{3,2,1,0:T(8,128)S(1)} %maximum_convert_fusion, f32[16,32,16,128]{3,2,1,0:T(8,128)S(1)} %copy-done, f32[16,16]{1,0:T(8,128)S(1)} %divide_multiply_fusion, f32[32,16]{1,0:T(8,128)S(1)} %get-tuple-element.16, f32[32,16]{1,0:T(8,128)S(1)} %get-tuple-element.15), kind=kLoop, calls=%fused_computation.7 | loop fusion | flops 13631488 | bytes 14685184 | tf_op jit(solution)/shard_map/convert_element_type | solution.py:240
  187.7 1.1 fusion.5
  188.8 0.6 slice_add_fusion.5
  189.5 0.5 pad_maximum_fusion.1
  189.9 16.9 %all_to_all.79 = f32[4,4,64,256]{3,2,1,0:T(8,128)S(1)} all-to-all(f32[4,4,64,256]{3,2,1,0:T(8,128)S(1)} %bitcast.69), channel_id=1, replica_groups=mesh['gx'=8,'ka'=4] {'ka'}, dimensions={0} | all-to-all | bytes 2097152 | tf_op jit(solution)/shard_map/all_to_all | solution.py:249
  207.0 0.6 broadcast_in_dim.5
  207.6 3.6 %all-to-all-start.6 = ((f32[8,1,4]{2,1,0:T(1,128)}), f32[8,1,4]{2,1,0:T(1,128)S(1)}, u32[]{:S(2)}, u32[]{:S(2)}) async-start(f32[8,1,4]{2,1,0:T(1,128)} %broadcast_in_dim.5), calls=%async_computation.6 | async-start | bytes 8192 | tf_op jit(solution)/shard_map/all_to_all | solution.py:146
  211.3 0.8 slice_multiply_fusion
  212.0 5.7 %all-to-all-done.6 = f32[8,1,4]{2,1,0:T(1,128)S(1)} async-done(((f32[8,1,4]{2,1,0:T(1,128)}), f32[8,1,4]{2,1,0:T(1,128)S(1)}, u32[]{:S(2)}, u32[]{:S(2)}) %all-to-all-start.6) | async-done | bytes 160 | tf_op jit(solution)/shard_map/all_to_all | solution.py:146
  217.7 0.5 broadcast.324
  218.2 0.7 reduce.3
  218.9 0.6 reshape.188
  (19 shorter events, 1.1 us)
Async XLA Ops:
  2.0 13.8 %all-to-all-start.4 = ((f32[8,1,512]{2,1,0:T(1,128)}), f32[8,1,512]{2,1,0:T(1,128)S(1)}, u32[]{:S(2)}, u32[]{:S(2)}) async-start(f32[8,1,512]{2,1,0:T(1,128)} %reshape.200), calls=%async_computation.4 | async-start | bytes 32768 | tf_op jit(solution)/shard_map/all_to_all | solution.py:146
  15.9 29.3 %all-to-all-start.2 = ((bf16[32,4,4,16,128]{4,3,1,0,2:T(8,128)(2,1)}), bf16[32,4,4,16,128]{4,3,1,0,2:T(8,128)(2,1)S(1)}, u32[]{:S(2)}, u32[]{:S(2)}) async-start(bf16[32,4,4,16,128]{4,3,1,0,2:T(8,128)(2,1)} %copy.36), calls=%async_computation.2 | async-start | bytes 4194304 | tf_op jit(solution)/shard_map/all_to_all | solution.py:185
  45.2 30.2 %all-to-all-start = ((bf16[32,4,4,16,128]{4,3,1,0,2:T(8,128)(2,1)}), bf16[32,4,4,16,128]{4,3,1,0,2:T(8,128)(2,1)}, u32[]{:S(2)}, u32[]{:S(2)}) async-start(bf16[32,4,4,16,128]{4,3,1,0,2:T(8,128)(2,1)} %copy.32), calls=%async_computation | async-start | bytes 4194304 | tf_op jit(solution)/shard_map/all_to_all | solution.py:185
  61.4 18.3 %copy-start.1 = (f32[4,64]{1,0:T(4,128)S(1)}, f32[4,64]{1,0:T(4,128)}, u32[]{:S(2)}) copy-start(f32[4,64]{1,0:T(4,128)} %param.7) | copy-start | bytes 3076
  75.4 52.7 %all-to-all-start.3 = ((bf16[128,4,16,128]{3,2,1,0:T(8,128)(2,1)}), bf16[128,4,16,128]{3,2,1,0:T(8,128)(2,1)}, u32[]{:S(2)}, u32[]{:S(2)}) async-start(bf16[128,4,16,128]{3,2,1,0:T(8,128)(2,1)} %copy.38), calls=%async_computation.3 | async-start | bytes 4194304 | tf_op jit(solution)/shard_map/all_to_all | solution.py:199
  128.0 52.2 %all-to-all-start.1 = ((bf16[128,4,16,128]{3,2,1,0:T(8,128)(2,1)}), bf16[128,4,16,128]{3,2,1,0:T(8,128)(2,1)}, u32[]{:S(2)}, u32[]{:S(2)}) async-start(bf16[128,4,16,128]{3,2,1,0:T(8,128)(2,1)} %copy.34), calls=%async_computation.1 | async-start | bytes 4194304 | tf_op jit(solution)/shard_map/all_to_all | solution.py:199
  135.2 47.1 %collective-permute-start = (bf16[16,32,1,128]{3,2,1,0:T(2,128)(2,1)S(1)}, bf16[16,32,1,128]{3,2,1,0:T(2,128)(2,1)S(1)}, u32[]{:S(2)}, u32[]{:S(2)}) collective-permute-start(bf16[16,32,1,128]{3,2,1,0:T(2,128)(2,1)S(1)} %get-tuple-element.11), channel_id=1, source_target_pairs={{0,1},{1,2},{2,3},{4,5},{5,6},{6,7},{8,9},{9,10},{10,11},{12,13},{... | collective-permute-start | bytes 393224 | tf_op jit(solution)/shard_map/ppermute | solution.py:19
  136.5 45.8 %collective-permute-start.1 = (bf16[16,32,1,128]{3,2,1,0:T(2,128)(2,1)S(1)}, bf16[16,32,1,128]{3,2,1,0:T(2,128)(2,1)S(1)}, u32[]{:S(2)}, u32[]{:S(2)}) collective-permute-start(bf16[16,32,1,128]{3,2,1,0:T(2,128)(2,1)S(1)} %get-tuple-element.12), channel_id=1, source_target_pairs={{1,0},{2,1},{3,2},{5,4},{6,5},{7,6},{9,8},{10,9},{11,10},{13,12},{... | collective-permute-start | bytes 393224 | tf_op jit(solution)/shard_map/ppermute | solution.py:21
  182.2 2.2 copy-start
  207.6 10.1 %all-to-all-start.6 = ((f32[8,1,4]{2,1,0:T(1,128)}), f32[8,1,4]{2,1,0:T(1,128)S(1)}, u32[]{:S(2)}, u32[]{:S(2)}) async-start(f32[8,1,4]{2,1,0:T(1,128)} %broadcast_in_dim.5), calls=%async_computation.6 | async-start | bytes 8192 | tf_op jit(solution)/shard_map/all_to_all | solution.py:146

commit v4 on v0

--- a/solution.py
+++ b/solution.py
@@ -23,6 +23,12 @@
             axis=dim,
         )
     return cells
+
+
+def gather_small(values, axis):
+    count = lax.axis_size(axis)
+    copies = jnp.broadcast_to(values[None], (count,) + values.shape)
+    return lax.all_to_all(copies, axis, split_axis=0, concat_axis=0, tiled=True)
 
 
 def dft_tables(count):
@@ -129,9 +135,11 @@
     selector = (owner[:, None] == jnp.arange(local_angles, dtype=jnp.int32)[None, :]).astype(
         jnp.float32
     )
-    own_rows = lax.psum_scatter(gram_terms, "gx", scatter_dimension=0, tiled=True)
+    shares = gram_terms.astype(jnp.bfloat16).reshape(lax.axis_size("gx"), row_count, 2 * columns)
+    shares = lax.all_to_all(shares, "gx", split_axis=0, concat_axis=0, tiled=True)
+    own_rows = jnp.sum(shares.astype(jnp.float32), axis=0)
     row_energy = jnp.sum(own_rows[:, :columns] ** 2, axis=1)
-    energy = lax.psum(jnp.sum(selector * row_energy[:, None], axis=0), "gx")
+    energy = jnp.sum(gather_small(jnp.sum(selector * row_energy[:, None], axis=0), "gx"), axis=0)
     mean_sq = energy / (2.0 * snap_count * snap_count)
     row_scale = jnp.sum(selector * lax.rsqrt(mean_sq + epsilon)[None, :], axis=1)
     hankel_gram = own_rows[:, :columns] * row_scale[:, None]

time: 247 us -> 184 us (0.74)
  waiting for transfers between devices: 128 us -> 83.8 us
  between operations: 14.3 us -> 0.87 us
  blocking collectives: 19.1 us -> 9.9 us
  starting transfers between devices: 23.6 us -> 29.9 us
    reduce_scatter x1 -> x0, waiting for transfers between devices: 70.1 us -> none  [local(): lax.psum_scatter(gram_terms, 'gx', scatter_dimension=0, tiled=True)]
    all_to_all x0 -> x1, waiting for transfers between devices: none -> 26 us  [local(): lax.all_to_all(shares, 'gx', split_axis=0, concat_axis=0, tiled=True)]
    psum x1 -> x0, blocking collectives: 19.1 us -> none  [local(): energy = lax.psum(jnp.sum(selector * row_energy[:, None], axis=0), 'gx')]
    all_to_all x0 -> x1, blocking collectives: none -> 9.9 us  [gather_small(): return lax.all_to_all(copies, axis, split_axis=0, concat_axis=0, tiled=True)]
    all_to_all x0 -> x1, starting transfers between devices: none -> 6.64 us  [local(): lax.all_to_all(shares, 'gx', split_axis=0, concat_axis=0, tiled=True)]
  transfers between devices with their start and end apart: 7 -> 7, of which waited for: 6 -> 6; matrix products, arithmetic and copies ran while one was open for 18% -> 24% of each run, Pallas kernels for 0% -> 0%
where the time goes in v4:
time: 184 us
  waiting for transfers between devices  83.8 us (46%)
  local copies, waits for them, and re-layouts  37.2 us (20%)
  starting transfers between devices  29.9 us (16%)
  other arithmetic  16.7 us (9%)
  blocking collectives  9.9 us (5%)
  matrix products  5.13 us (3%)
    all_to_all x1, waiting for transfers between devices, local(): lax.all_to_all(shares, 'gx', split_axis=0, concat_axis=0, tiled=True)  26 us
    all_to_all x1, waiting for transfers between devices, local(): lax.all_to_all(direct_snapshots, 'ka', split_axis=2, concat_axis=0, tiled...  21.4 us
    all_to_all x1, waiting for transfers between devices, local(): lax.all_to_all(transform_all(moved_adjoint), 'ka', split_axis=0, concat_a...  14.2 us
    all_to_all x1, waiting for transfers between devices, local(): lax.all_to_all(transform_all(moved_direct), 'ka', split_axis=0, concat_ax...  10.9 us
    all_to_all x1, blocking collectives, gather_small(): return lax.all_to_all(copies, axis, split_axis=0, concat_axis=0, tiled=True)  9.9 us
    all_to_all x1, waiting for transfers between devices, local(): lax.all_to_all(adjoint_snapshots, 'ka', split_axis=2, concat_axis=0, tile...  9.44 us
    unnamed x10, local copies, waits for them, and re-layouts  8.56 us
    all_to_all x1, starting transfers between devices, local(): lax.all_to_all(shares, 'gx', split_axis=0, concat_axis=0, tiled=True)  6.64 us
  transfers between devices with their start and end apart: 7, of which 6 were waited for; matrix products, arithmetic and copies ran while one was open for 24% of the time, Pallas kernels for 0%

profile of v4, /device:TPU:0, one launch (start us, length us, event | category | flops | bytes accessed | tf_op | source)
XLA Modules:
  0.0 183.5 jit_solution(15534416840451435407)
XLA Ops:
  0.6 4.3 %copy.63 = bf16[32,4,64,128]{3,0,1,2:T(8,128)(2,1)} copy(bf16[32,4,64,128]{3,2,1,0:T(8,128)(2,1)} %param.5) | data formatting | bytes 4194304 | tf_op args[0]
  4.9 4.2 %all-to-all-start.2 = ((bf16[32,4,64,128]{3,0,1,2:T(8,128)(2,1)}), bf16[32,4,64,128]{3,0,1,2:T(8,128)(2,1)S(1)}, u32[]{:S(2)}, u32[]{:S(2)}) async-start(bf16[32,4,64,128]{3,0,1,2:T(8,128)(2,1)} %copy.63), calls=%async_computation.2 | async-start | bytes 4194304 | tf_op jit(solution)/shard_map/all_to_all | solution.py:75
  9.2 4.3 %copy.58 = bf16[32,4,64,128]{3,0,1,2:T(8,128)(2,1)} copy(bf16[32,4,64,128]{3,2,1,0:T(8,128)(2,1)} %param.6) | data formatting | bytes 4194304 | tf_op args[1]
  13.4 21.4 %all-to-all-done.2 = bf16[32,4,64,128]{3,0,1,2:T(8,128)(2,1)S(1)} async-done(((bf16[32,4,64,128]{3,0,1,2:T(8,128)(2,1)}), bf16[32,4,64,128]{3,0,1,2:T(8,128)(2,1)S(1)}, u32[]{:S(2)}, u32[]{:S(2)}) %all-to-all-start.2) | async-done | bytes 2097184 | tf_op jit(solution)/shard_map/all_to_all | solution.py:75
  34.9 4.4 %all-to-all-start = ((bf16[32,4,64,128]{3,0,1,2:T(8,128)(2,1)}), bf16[32,4,64,128]{3,0,1,2:T(8,128)(2,1)}, u32[]{:S(2)}, u32[]{:S(2)}) async-start(bf16[32,4,64,128]{3,0,1,2:T(8,128)(2,1)} %copy.58), calls=%async_computation | async-start | bytes 4194304 | tf_op jit(solution)/shard_map/all_to_all | solution.py:76
  39.3 2.7 %copy.76 = bf16[32,4,4,16,128]{4,3,1,0,2:T(8,128)(2,1)} copy(bf16[32,4,4,16,128]{4,0,1,3,2:T(8,128)(2,1)S(1)} %bitcast.57) | data formatting | bytes 4194304 | tf_op jit(solution)/shard_map/all_to_all | solution.py:75
  42.0 4.2 %reshape.119 = bf16[128,8192]{1,0:T(8,128)(2,1)} reshape(bf16[4,32,4,16,128]{4,3,2,1,0:T(8,128)(2,1)} %bitcast.59) | data formatting | bytes 4194304 | tf_op jit(solution)/shard_map/reshape | solution.py:80
  46.2 3.2 %copy.65 = bf16[8192,128]{1,0:T(8,128)(2,1)S(1)} copy(bf16[8192,128]{0,1:T(8,128)(2,1)} %bitcast.60) | data formatting | bytes 4194304 | tf_op jit(solution)/shard_map/dot_general | solution.py:81
  49.4 1.0 fusion.30
  50.5 1.0 fusion.34
  51.5 1.0 fusion.15
  52.5 0.1 pad_maximum_fusion.3
  52.6 3.0 %copy.66 = bf16[128,4,16,128]{3,2,1,0:T(8,128)(2,1)} copy(bf16[128,4,16,128]{0,3,2,1:T(8,128)(2,1)S(1)} %pad_maximum_fusion.3) | data formatting | bytes 4194304 | tf_op jit(solution)/shard_map/concatenate | solution.py:49
  55.6 9.4 %all-to-all-done = bf16[32,4,64,128]{3,0,1,2:T(8,128)(2,1)} async-done(((bf16[32,4,64,128]{3,0,1,2:T(8,128)(2,1)}), bf16[32,4,64,128]{3,0,1,2:T(8,128)(2,1)}, u32[]{:S(2)}, u32[]{:S(2)}) %all-to-all-start) | async-done | bytes 2097184 | tf_op jit(solution)/shard_map/all_to_all | solution.py:76
  65.1 4.6 %all-to-all-start.3 = ((bf16[128,4,16,128]{3,2,1,0:T(8,128)(2,1)}), bf16[128,4,16,128]{3,2,1,0:T(8,128)(2,1)}, u32[]{:S(2)}, u32[]{:S(2)}) async-start(bf16[128,4,16,128]{3,2,1,0:T(8,128)(2,1)} %copy.66), calls=%async_computation.3 | async-start | bytes 4194304 | tf_op jit(solution)/shard_map/all_to_all | solution.py:90
  69.7 2.9 %copy.77 = bf16[32,4,4,16,128]{4,3,1,0,2:T(8,128)(2,1)S(1)} copy(bf16[32,4,4,16,128]{4,0,1,3,2:T(8,128)(2,1)} %bitcast.2) | data formatting | bytes 4194304 | tf_op jit(solution)/shard_map/all_to_all | solution.py:76
  72.7 2.3 %reshape.118 = bf16[128,8192]{1,0:T(8,128)(2,1)} reshape(bf16[4,32,4,16,128]{4,3,2,1,0:T(8,128)(2,1)S(1)} %bitcast.61) | data formatting | bytes 4194304 | tf_op jit(solution)/shard_map/reshape | solution.py:80
  75.0 3.2 %copy.60 = bf16[8192,128]{1,0:T(8,128)(2,1)S(1)} copy(bf16[8192,128]{0,1:T(8,128)(2,1)} %bitcast.62) | data formatting | bytes 4194304 | tf_op jit(solution)/shard_map/dot_general | solution.py:81
  78.2 1.0 fusion.32
  79.2 1.0 fusion.36
  80.2 1.0 fusion.17
  81.2 0.1 pad_maximum_fusion.2
  81.4 3.0 %copy.61 = bf16[128,4,16,128]{3,2,1,0:T(8,128)(2,1)} copy(bf16[128,4,16,128]{0,3,2,1:T(8,128)(2,1)S(1)} %pad_maximum_fusion.2) | data formatting | bytes 4194304 | tf_op jit(solution)/shard_map/concatenate | solution.py:49
  84.4 10.9 %all-to-all-done.3 = bf16[128,4,16,128]{3,2,1,0:T(8,128)(2,1)} async-done(((bf16[128,4,16,128]{3,2,1,0:T(8,128)(2,1)}), bf16[128,4,16,128]{3,2,1,0:T(8,128)(2,1)}, u32[]{:S(2)}, u32[]{:S(2)}) %all-to-all-start.3) | async-done | bytes 2097184 | tf_op jit(solution)/shard_map/all_to_all | solution.py:90
  95.3 4.5 %all-to-all-start.1 = ((bf16[128,4,16,128]{3,2,1,0:T(8,128)(2,1)}), bf16[128,4,16,128]{3,2,1,0:T(8,128)(2,1)}, u32[]{:S(2)}, u32[]{:S(2)}) async-start(bf16[128,4,16,128]{3,2,1,0:T(8,128)(2,1)} %copy.61), calls=%async_computation.1 | async-start | bytes 4194304 | tf_op jit(solution)/shard_map/all_to_all | solution.py:91
  100.0 2.2 %copy.67 = bf16[32,4,4,16,128]{4,3,2,1,0:T(8,128)(2,1)S(1)} copy(bf16[32,4,4,16,128]{4,3,1,0,2:T(8,128)(2,1)} %bitcast.18) | data formatting | bytes 4194304 | tf_op jit(solution)/shard_map/all_to_all | solution.py:90
  102.1 1.1 fusion.59
  103.3 4.2 %collective-permute-start.1 = (bf16[32,1,64,128]{3,2,1,0:T(8,128)(2,1)}, bf16[32,1,64,128]{3,2,1,0:T(8,128)(2,1)S(1)}, u32[]{:S(2)}, u32[]{:S(2)}) collective-permute-start(bf16[32,1,64,128]{3,2,1,0:T(8,128)(2,1)} %get-tuple-element.12), channel_id=1, source_target_pairs={{0,4},{4,8},{8,12},{12,16},{16,20},{20,24},{24,28},{1,5},{5,9},{9,... | collective-permute-start | bytes 1572872 | tf_op jit(solution)/shard_map/ppermute | solution.py:19
  107.5 1.3 collective-permute-start
  108.8 2.6 %bitcast_convert_fusion = f32[32,4,64,128]{3,2,1,0:T(8,128)} fusion(bf16[32,4,4,16,128]{4,3,2,1,0:T(8,128)(2,1)S(1)} %copy.67), kind=kLoop, calls=%fused_computation.79 | loop fusion | flops 1048576 | bytes 6291456 | tf_op jit(solution)/shard_map/convert_element_type | solution.py:94
  111.3 14.2 %all-to-all-done.1 = bf16[128,4,16,128]{3,2,1,0:T(8,128)(2,1)} async-done(((bf16[128,4,16,128]{3,2,1,0:T(8,128)(2,1)}), bf16[128,4,16,128]{3,2,1,0:T(8,128)(2,1)}, u32[]{:S(2)}, u32[]{:S(2)}) %all-to-all-start.1) | async-done | bytes 2097184 | tf_op jit(solution)/shard_map/all_to_all | solution.py:91
  125.5 2.1 %convert_bitcast_fusion = f32[32,4,4,16,128]{4,3,1,0,2:T(8,128)S(1)} fusion(bf16[4,32,4,16,128]{4,3,2,1,0:T(8,128)(2,1)} %bitcast.25), kind=kLoop, calls=%fused_computation.17 | loop fusion | flops 1048576 | bytes 6291456 | tf_op jit(solution)/shard_map/convert_element_type | solution.py:121
  127.6 0.6 copy.62
  128.3 0.6 fusion.13
  128.9 1.9 %collective-permute-done.1 = bf16[32,1,64,128]{3,2,1,0:T(8,128)(2,1)S(1)} collective-permute-done((bf16[32,1,64,128]{3,2,1,0:T(8,128)(2,1)}, bf16[32,1,64,128]{3,2,1,0:T(8,128)(2,1)S(1)}, u32[]{:S(2)}, u32[]{:S(2)}) %collective-permute-start.1) | collective-permute-done | bytes 524320 | tf_op jit(solution)/shard_map/ppermute | solution.py:19
  130.8 4.4 %fusion.6 = bf16[32,4,64,128]{3,2,1,0:T(8,128)(2,1)S(1)} fusion(f32[32,4,64,128]{3,2,1,0:T(8,128)S(1)} %copy-done, bf16[32,4,64,128]{3,2,1,0:T(8,128)(2,1)S(1)} %bitcast.51, bf16[32,1,64,128]{3,2,1,0:T(8,128)(2,1)S(1)} %collective-permute-done.1, bf16[32,1,64,128]{3,2,1,0:T(8,128)(2,1)S(1)} %collective-permute-done, f32[32,64]{1,0:T(8,128)S(1)} %divide_multiply_fusion, ...), kind=kLoop, calls=%fused_computation.10 | loop fusion | flops 17825792 | bytes 9447424 | tf_op jit(solution)/shard_map/convert_element_type | solution.py:118
  135.2 1.1 fusion.9
  136.3 1.2 fusion.21
  137.5 1.7 pad_maximum_fusion.4
  139.2 6.6 %all-to-all-start.4 = ((bf16[8,256,256]{2,1,0:T(8,128)(2,1)}), bf16[8,256,256]{2,1,0:T(8,128)(2,1)S(1)}, u32[]{:S(2)}, u32[]{:S(2)}) async-start(bf16[8,256,256]{2,1,0:T(8,128)(2,1)} %bitcast.23), calls=%async_computation.4 | async-start | bytes 2097152 | tf_op jit(solution)/shard_map/all_to_all | solution.py:139
  145.8 26.0 %all-to-all-done.4 = bf16[8,256,256]{2,1,0:T(8,128)(2,1)S(1)} async-done(((bf16[8,256,256]{2,1,0:T(8,128)(2,1)}), bf16[8,256,256]{2,1,0:T(8,128)(2,1)S(1)}, u32[]{:S(2)}, u32[]{:S(2)}) %all-to-all-start.4) | async-done | bytes 1048608 | tf_op jit(solution)/shard_map/all_to_all | solution.py:139
  171.8 0.1 convert_reduce_fusion
  171.9 0.1 multiply_reduce_fusion
  172.0 0.1 select_reduce_fusion.1
  172.2 9.9 %all_to_all.68 = f32[8,1,32]{2,1,0:T(1,128)S(1)} all-to-all(f32[8,1,32]{2,1,0:T(1,128)S(1)} %broadcast_in_dim.2), channel_id=1, replica_groups=mesh['gx'=8,'ka'=4] {'gx'}, dimensions={0} | all-to-all | bytes 2048 | tf_op jit(solution)/shard_map/all_to_all | solution.py:31
  182.1 0.5 multiply_sqrt_fusion
  182.6 0.1 select_reduce_fusion
  182.7 0.8 slice_multiply_fusion
  (19 shorter events, 0.2 us)
Async XLA Ops:
  4.9 29.9 %all-to-all-start.2 = ((bf16[32,4,64,128]{3,0,1,2:T(8,128)(2,1)}), bf16[32,4,64,128]{3,0,1,2:T(8,128)(2,1)S(1)}, u32[]{:S(2)}, u32[]{:S(2)}) async-start(bf16[32,4,64,128]{3,0,1,2:T(8,128)(2,1)} %copy.63), calls=%async_computation.2 | async-start | bytes 4194304 | tf_op jit(solution)/shard_map/all_to_all | solution.py:75
  34.9 30.2 %all-to-all-start = ((bf16[32,4,64,128]{3,0,1,2:T(8,128)(2,1)}), bf16[32,4,64,128]{3,0,1,2:T(8,128)(2,1)}, u32[]{:S(2)}, u32[]{:S(2)}) async-start(bf16[32,4,64,128]{3,0,1,2:T(8,128)(2,1)} %copy.58), calls=%async_computation | async-start | bytes 4194304 | tf_op jit(solution)/shard_map/all_to_all | solution.py:76
  65.1 30.2 %all-to-all-start.3 = ((bf16[128,4,16,128]{3,2,1,0:T(8,128)(2,1)}), bf16[128,4,16,128]{3,2,1,0:T(8,128)(2,1)}, u32[]{:S(2)}, u32[]{:S(2)}) async-start(bf16[128,4,16,128]{3,2,1,0:T(8,128)(2,1)} %copy.66), calls=%async_computation.3 | async-start | bytes 4194304 | tf_op jit(solution)/shard_map/all_to_all | solution.py:90
  84.4 15.3 %copy-start.2 = (f32[4,64]{1,0:T(4,128)S(1)}, f32[4,64]{1,0:T(4,128)}, u32[]{:S(2)}) copy-start(f32[4,64]{1,0:T(4,128)} %param.7) | copy-start | bytes 3076
  84.4 15.4 %copy-start.3 = (f32[4,64]{1,0:T(4,128)S(1)}, f32[4,64]{1,0:T(4,128)}, u32[]{:S(2)}) copy-start(f32[4,64]{1,0:T(4,128)} %param.8) | copy-start | bytes 3076
  95.3 30.2 %all-to-all-start.1 = ((bf16[128,4,16,128]{3,2,1,0:T(8,128)(2,1)}), bf16[128,4,16,128]{3,2,1,0:T(8,128)(2,1)}, u32[]{:S(2)}, u32[]{:S(2)}) async-start(bf16[128,4,16,128]{3,2,1,0:T(8,128)(2,1)} %copy.61), calls=%async_computation.1 | async-start | bytes 4194304 | tf_op jit(solution)/shard_map/all_to_all | solution.py:91
  103.3 27.5 %collective-permute-start.1 = (bf16[32,1,64,128]{3,2,1,0:T(8,128)(2,1)}, bf16[32,1,64,128]{3,2,1,0:T(8,128)(2,1)S(1)}, u32[]{:S(2)}, u32[]{:S(2)}) collective-permute-start(bf16[32,1,64,128]{3,2,1,0:T(8,128)(2,1)} %get-tuple-element.12), channel_id=1, source_target_pairs={{0,4},{4,8},{8,12},{12,16},{16,20},{20,24},{24,28},{1,5},{5,9},{9,... | collective-permute-start | bytes 1572872 | tf_op jit(solution)/shard_map/ppermute | solution.py:19
  107.5 23.3 %collective-permute-start = (bf16[32,1,64,128]{3,2,1,0:T(8,128)(2,1)}, bf16[32,1,64,128]{3,2,1,0:T(8,128)(2,1)S(1)}, u32[]{:S(2)}, u32[]{:S(2)}) collective-permute-start(bf16[32,1,64,128]{3,2,1,0:T(8,128)(2,1)} %get-tuple-element.11), channel_id=1, source_target_pairs={{4,0},{8,4},{12,8},{16,12},{20,16},{24,20},{28,24},{5,1},{9,5},{13... | collective-permute-start | bytes 1572872 | tf_op jit(solution)/shard_map/ppermute | solution.py:21
  128.2 2.5 %copy-start = (f32[32,4,64,128]{3,2,1,0:T(8,128)S(1)}, f32[32,4,64,128]{3,2,1,0:T(8,128)}, u32[]{:S(2)}) copy-start(f32[32,4,64,128]{3,2,1,0:T(8,128)} %bitcast_convert_fusion) | copy-start | bytes 12582916
  128.3 2.5 %copy-start.1 = (f32[4,64]{1,0:T(4,128)S(1)}, f32[4,64]{1,0:T(4,128)}, u32[]{:S(2)}) copy-start(f32[4,64]{1,0:T(4,128)} %param.9) | copy-start | bytes 3076
  139.2 32.6 %all-to-all-start.4 = ((bf16[8,256,256]{2,1,0:T(8,128)(2,1)}), bf16[8,256,256]{2,1,0:T(8,128)(2,1)S(1)}, u32[]{:S(2)}, u32[]{:S(2)}) async-start(bf16[8,256,256]{2,1,0:T(8,128)(2,1)} %bitcast.23), calls=%async_computation.4 | async-start | bytes 2097152 | tf_op jit(solution)/shard_map/all_to_all | solution.py:139

commit v5 on v4

--- a/solution.py
+++ b/solution.py
@@ -31,6 +31,42 @@
     return lax.all_to_all(copies, axis, split_axis=0, concat_axis=0, tiled=True)
 
 
+def exchange(cells, axis, split_axis):
+    count = lax.axis_size(axis)
+    here = lax.axis_index(axis)
+    width = cells.shape[split_axis] // count
+    pieces = []
+    for shift in range(count):
+        piece = lax.dynamic_slice_in_dim(cells, ((here + shift) % count) * width, width, axis=split_axis)
+        if shift:
+            piece = lax.ppermute(piece, axis, [(j, (j + shift) % count) for j in range(count)])
+        pieces.append(piece)
+    return pieces
+
+
+def in_source_order(pieces, axis, concat_axis):
+    count = len(pieces)
+    here = lax.axis_index(axis)
+    stacked = jnp.stack(pieces)
+    ordered = [lax.dynamic_index_in_dim(stacked, (here - source) % count, 0, keepdims=False) for source in range(count)]
+    return jnp.concatenate(ordered, axis=concat_axis)
+
+
+def shifted_tables(count, local_angles, axis):
+    here = lax.axis_index(axis)
+    blocks = count // local_angles
+    wave_index = jnp.arange(count, dtype=jnp.int32) - count // 2
+    position = jnp.arange(count, dtype=jnp.int32)
+    angle_index = ((here - position // local_angles) % blocks) * local_angles + position % local_angles
+    residues = wave_index[:, None] * angle_index[None, :] % count
+    phases = 2.0 * math.pi * residues.astype(jnp.float32) / count
+    scaling = 1.0 / math.sqrt(count)
+    return (
+        (jnp.cos(phases) * scaling).astype(jnp.bfloat16),
+        (jnp.sin(phases) * scaling).astype(jnp.bfloat16),
+    )
+
+
 def dft_tables(count):
     wave_index = jnp.arange(count, dtype=jnp.int32) - count // 2
     angle_index = jnp.arange(count, dtype=jnp.int32)
@@ -69,11 +105,11 @@
     local_angles, axial_cells, radial_cells, columns = direct_snapshots.shape
     snap_count = columns // 2
     total_angles = local_angles * lax.axis_size("ka")
-    cos_table, sin_table = dft_tables(total_angles)
+    cos_table, sin_table = shifted_tables(total_angles, local_angles, "ka")
     first_wave = lax.axis_index("ka") * local_angles
     moved_direct, moved_adjoint = (
-        lax.all_to_all(direct_snapshots, "ka", split_axis=2, concat_axis=0, tiled=True),
-        lax.all_to_all(adjoint_snapshots, "ka", split_axis=2, concat_axis=0, tiled=True),
+        jnp.concatenate(exchange(direct_snapshots, "ka", 2), axis=0),
+        jnp.concatenate(exchange(adjoint_snapshots, "ka", 2), axis=0),
     )
 
     def transform_all(snapshots):
@@ -87,8 +123,8 @@
         return combine_parts(cos_part, sin_part, snap_count)
 
     direct_modes, adjoint_modes = (
-        lax.all_to_all(transform_all(moved_direct), "ka", split_axis=0, concat_axis=2, tiled=True),
-        lax.all_to_all(transform_all(moved_adjoint), "ka", split_axis=0, concat_axis=2, tiled=True),
+        in_source_order(exchange(transform_all(moved_direct), "ka", 0), "ka", 2),
+        in_source_order(exchange(transform_all(moved_adjoint), "ka", 0), "ka", 2),
     )
     padded = padded_2(direct_modes, (("gx", 1),), 1)
     field_f32 = direct_modes.astype(jnp.float32)

time: 184 us -> 187 us (1.016)
  other arithmetic: 16.7 us -> 37.3 us
  waiting for transfers between devices: 83.8 us -> 73.4 us
  starting transfers between devices: 29.9 us -> 22 us
  matrix products: 5.13 us -> 8.9 us
  local copies, waits for them, and re-layouts: 37.2 us -> 33.5 us
    all_to_all x4 -> x0, waiting for transfers between devices: 55.9 us -> none  [the longest x1 21.4 us: local(): lax.all_to_all(direct_snapshots, 'ka', split_axis=2, concat_axis=0, tiled...]
    ppermute x0 -> x12, waiting for transfers between devices: none -> 33.5 us  [exchange(): lax.ppermute(piece, axis, [(j, (j + shift) % count) for j in range(count)])]
    dynamic_slice x0 -> x10, local copies, waits for them, and re-layouts: none -> 25.4 us  [exchange(): lax.dynamic_slice_in_dim(cells, (here + shift) % count * width, width, ax...]
    all_to_all x4 -> x0, starting transfers between devices: 17.8 us -> none  [the longest x1 4.63 us: local(): lax.all_to_all(transform_all(moved_direct), 'ka', split_axis=0, concat_ax...]
    concatenate x2, other arithmetic: 0.28 us -> 10.6 us  [combine_parts(): return jnp.concatenate([real_part, imag_part], axis=-1).astype(jnp.bfloat16)]
    ppermute x0 -> x12, starting transfers between devices: none -> 10.1 us  [exchange(): lax.ppermute(piece, axis, [(j, (j + shift) % count) for j in range(count)])]
    ppermute x1, waiting for transfers between devices: 1.89 us -> 11.1 us  [padded_2(): lax.ppermute(tail, axis, [(i, (i + 1) % count) for i in range(ends)])]
    unnamed x10 -> x8, local copies, waits for them, and re-layouts: 8.56 us -> 0.02 us
  transfers between devices with their start and end apart: 7 -> 15, of which waited for: 6 -> 8; matrix products, arithmetic and copies ran while one was open for 24% -> 25% of each run, Pallas kernels for 0% -> 0%
where the time goes in v5:
time: 187 us; the launch traced here: 186 us
  waiting for transfers between devices  73.4 us (39%)
  other arithmetic  37.3 us (20%)
  local copies, waits for them, and re-layouts  33.5 us (18%)
  starting transfers between devices  22 us (12%)
  blocking collectives  9.9 us (5%)
  matrix products  8.9 us (5%)
    ppermute x12, waiting for transfers between devices, exchange(): lax.ppermute(piece, axis, [(j, (j + shift) % count) for j in range(count)])  33.5 us
    all_to_all x1, waiting for transfers between devices, local(): lax.all_to_all(shares, 'gx', split_axis=0, concat_axis=0, tiled=True)  25.9 us
    dynamic_slice x10, local copies, waits for them, and re-layouts, exchange(): lax.dynamic_slice_in_dim(cells, (here + shift) % count * width, width, ax...  25.4 us
    ppermute x1, waiting for transfers between devices, padded_2(): lax.ppermute(tail, axis, [(i, (i + 1) % count) for i in range(ends)])  11.1 us
    concatenate x2, other arithmetic, combine_parts(): return jnp.concatenate([real_part, imag_part], axis=-1).astype(jnp.bfloat16)  10.6 us
    ppermute x12, starting transfers between devices, exchange(): lax.ppermute(piece, axis, [(j, (j + shift) % count) for j in range(count)])  10.1 us
    all_to_all x1, blocking collectives, gather_small(): return lax.all_to_all(copies, axis, split_axis=0, concat_axis=0, tiled=True)  9.9 us
    reshape x2, local copies, waits for them, and re-layouts, transform_all(): flattened = snapshots.reshape(total_angles, -1)  6.97 us
  transfers between devices with their start and end apart: 15, of which 8 were waited for; matrix products, arithmetic and copies ran while one was open for 25% of the time, Pallas kernels for 0%

profile of v5, /device:TPU:0, one launch (start us, length us, event | category | flops | bytes accessed | tf_op | source)
XLA Modules:
  0.0 185.9 jit_solution(8416963658968330869)
XLA Ops:
  0.7 3.3 %constant_dynamic-slice_fusion.7 = (bf16[32,4,16,128]{3,2,1,0:T(8,128)(2,1)S(1)}, bf16[32,4,16,128]{3,2,1,0:T(8,128)(2,1)}, bf16[32,4,16,128]{3,2,1,0:T(8,128)(2,1)S(1)}, bf16[32,4,16,128]{3,2,1,0:T(8,128)(2,1)}) fusion(bf16[32,4,64,128]{3,2,1,0:T(8,128)(2,1)} %param.6, s32[]{:T(128)S(6)} %select_n.161, s32[]{:T(128)S(6)} %select_n.163, s32[]{:T(128)S(6)} %select_n.167, ...), kind=kLoop, calls=%fused_computation.119 | loop fusion | bytes 4194320 | tf_op jit(solution)/shard_map/dynamic_slice | solution.py:40
  4.5 2.5 %collective-permute-start.1 = (bf16[32,4,16,128]{3,2,1,0:T(8,128)(2,1)}, bf16[32,4,16,128]{3,2,1,0:T(8,128)(2,1)S(1)}, u32[]{:S(2)}, u32[]{:S(2)}) collective-permute-start(bf16[32,4,16,128]{3,2,1,0:T(8,128)(2,1)} %get-tuple-element.22), channel_id=1, source_target_pairs={{0,2},{1,3},{2,0},{3,1},{4,6},{5,7},{6,4},{7,5},{8,10},{9,11},{10,... | collective-permute-start | bytes 1572872 | tf_op jit(solution)/shard_map/ppermute | solution.py:42
  7.0 1.4 collective-permute-start.2
  8.4 1.6 constant_dynamic-slice_fusion.3
  10.7 7.6 %collective-permute-done = bf16[32,4,16,128]{3,2,1,0:T(8,128)(2,1)S(1)} collective-permute-done((bf16[32,4,16,128]{3,2,1,0:T(8,128)(2,1)}, bf16[32,4,16,128]{3,2,1,0:T(8,128)(2,1)S(1)}, u32[]{:S(2)}, u32[]{:S(2)}) %collective-permute-start) | collective-permute-done | bytes 524320 | tf_op jit(solution)/shard_map/ppermute | solution.py:42
  18.3 1.7 collective-permute-done.1
  19.9 10.8 %collective-permute-done.2 = bf16[32,4,16,128]{3,2,1,0:T(8,128)(2,1)} collective-permute-done((bf16[32,4,16,128]{3,2,1,0:T(8,128)(2,1)S(1)}, bf16[32,4,16,128]{3,2,1,0:T(8,128)(2,1)}, u32[]{:S(2)}, u32[]{:S(2)}) %collective-permute-start.2) | collective-permute-done | bytes 524320 | tf_op jit(solution)/shard_map/ppermute | solution.py:42
  30.7 2.6 %pad_maximum_fusion.9 = bf16[128,4,16,128]{3,2,1,0:T(8,128)(2,1)} fusion(bf16[32,4,16,128]{3,2,1,0:T(8,128)(2,1)} %collective-permute-done.2, bf16[32,4,16,128]{3,2,1,0:T(8,128)(2,1)S(1)} %collective-permute-done.1, bf16[32,4,16,128]{3,2,1,0:T(8,128)(2,1)S(1)} %collective-permute-done, bf16[32,4,16,128]{3,2,1,0:T(8,128)(2,1)S(1)} %get-tuple-element.19), kind=kLoop, calls=%fused_computation.57 | loop fusion | flops 3145728 | bytes 4194304 | tf_op jit(solution)/shard_map/concatenate | solution.py:112
  33.4 3.5 %copy.73 = bf16[128,4,16,128]{0,3,2,1:T(8,128)(2,1)S(1)} copy(bf16[128,4,16,128]{3,2,1,0:T(8,128)(2,1)} %pad_maximum_fusion.9) | data formatting | bytes 4194304 | tf_op jit(solution)/shard_map/reshape | solution.py:116
  36.9 3.0 %fusion.28 = f32[128,4,16,128]{0,3,2,1:T(8,128)} fusion(bf16[128,4,16,128]{0,3,2,1:T(8,128)(2,1)S(1)} %copy.73, s32[128]{0:T(128)S(1)} %get-tuple-element.43, s32[128]{0:T(128)S(1)} %get-tuple-element.44), kind=kOutput, calls=%fused_computation.67 | convolution fusion | flops 268697600 | bytes 6292480 | tf_op jit(solution)/shard_map/dot_general | solution.py:120
  39.8 3.0 %fusion.30 = f32[128,4,16,128]{0,3,2,1:T(8,128)} fusion(bf16[128,4,16,128]{0,3,2,1:T(8,128)(2,1)S(1)} %copy.73, s32[128]{0:T(128)S(1)} %get-tuple-element.43, s32[128]{0:T(128)S(1)} %get-tuple-element.44), kind=kOutput, calls=%fused_computation.69 | convolution fusion | flops 268697600 | bytes 6292480 | tf_op jit(solution)/shard_map/dot_general | solution.py:117
  42.8 9.8 %collective-permute-done.8 = bf16[32,4,16,128]{3,2,1,0:T(8,128)(2,1)} collective-permute-done((bf16[32,4,16,128]{3,2,1,0:T(8,128)(2,1)S(1)}, bf16[32,4,16,128]{3,2,1,0:T(8,128)(2,1)}, u32[]{:S(2)}, u32[]{:S(2)}) %collective-permute-start.8) | collective-permute-done | bytes 524320 | tf_op jit(solution)/shard_map/ppermute | solution.py:42
  52.6 3.0 %pad_maximum_fusion.12 = bf16[128,4,16,128]{3,2,1,0:T(8,128)(2,1)} fusion(bf16[32,4,16,128]{3,2,1,0:T(8,128)(2,1)} %collective-permute-done.8, bf16[32,4,16,128]{3,2,1,0:T(8,128)(2,1)} %collective-permute-done.7, bf16[32,4,16,128]{3,2,1,0:T(8,128)(2,1)} %collective-permute-done.6, bf16[32,4,16,128]{3,2,1,0:T(8,128)(2,1)S(1)} %get-tuple-element.35), kind=kLoop, calls=%fused_computation.60 | loop fusion | flops 3145728 | bytes 4194304 | tf_op jit(solution)/shard_map/concatenate | solution.py:111
  55.6 3.5 %copy.74 = bf16[128,4,16,128]{0,3,2,1:T(8,128)(2,1)S(1)} copy(bf16[128,4,16,128]{3,2,1,0:T(8,128)(2,1)} %pad_maximum_fusion.12) | data formatting | bytes 4194304 | tf_op jit(solution)/shard_map/reshape | solution.py:116
  59.1 1.0 fusion.26
  60.1 1.0 fusion.24
  61.2 1.0 fusion.20
  62.2 5.1 %fusion.11 = (bf16[32,4,16,128]{0,3,2,1:T(8,128)(2,1)S(1)}, bf16[32,4,16,128]{0,3,2,1:T(8,128)(2,1)}, bf16[32,4,16,128]{0,3,2,1:T(8,128)(2,1)}, bf16[32,4,16,128]{0,3,2,1:T(8,128)(2,1)}) fusion(s32[]{:T(128)S(6)} %select_n.168, bf16[128,4,16,64]{0,3,2,1:T(8,128)(2,1)S(1)} %get-tuple-element.6, bf16[128,4,16,64]{0,3,2,1:T(8,128)(2,1)S(1)} %get-tuple-element.5, ...), kind=kLoop, calls=%fused_computation.33 | loop fusion | flops 4194304 | bytes 4194320 | tf_op jit(solution)/shard_map/concatenate | solution.py:85
  67.3 2.8 %copy.65 = bf16[32,4,16,128]{3,2,1,0:T(8,128)(2,1)} copy(bf16[32,4,16,128]{0,3,2,1:T(8,128)(2,1)} %get-tuple-element.32) | data formatting | bytes 1048576 | tf_op jit(solution)/shard_map/dynamic_slice | solution.py:40
  70.3 2.9 %copy.66 = bf16[32,4,16,128]{3,2,1,0:T(8,128)(2,1)} copy(bf16[32,4,16,128]{0,3,2,1:T(8,128)(2,1)} %get-tuple-element.33) | data formatting | bytes 1048576 | tf_op jit(solution)/shard_map/dynamic_slice | solution.py:40
  73.1 2.3 %collective-permute-start.10 = (bf16[32,4,16,128]{3,2,1,0:T(8,128)(2,1)}, bf16[32,4,16,128]{3,2,1,0:T(8,128)(2,1)}, u32[]{:S(2)}, u32[]{:S(2)}) collective-permute-start(bf16[32,4,16,128]{3,2,1,0:T(8,128)(2,1)} %copy.66), channel_id=1, source_target_pairs={{0,2},{1,3},{2,0},{3,1},{4,6},{5,7},{6,4},{7,5},{8,10},{9,11},{10,... | collective-permute-start | bytes 1572872 | tf_op jit(solution)/shard_map/ppermute | solution.py:42
  75.4 2.8 %copy.67 = bf16[32,4,16,128]{3,2,1,0:T(8,128)(2,1)} copy(bf16[32,4,16,128]{0,3,2,1:T(8,128)(2,1)} %get-tuple-element.34) | data formatting | bytes 1048576 | tf_op jit(solution)/shard_map/dynamic_slice | solution.py:40
  78.3 4.5 %fusion.22 = (bf16[128,4,16,64]{0,3,2,1:T(8,128)(2,1)S(1)}, bf16[128,4,16,64]{0,3,2,1:T(8,128)(2,1)S(1)}) fusion(f32[128,4,16,128]{0,3,2,1:T(8,128)} %fusion.28, f32[128,4,16,128]{0,3,2,1:T(8,128)} %fusion.30), kind=kLoop, calls=%fused_computation.54 | loop fusion | flops 2097152 | bytes 10485760 | tf_op jit(solution)/shard_map/convert.8
  82.8 5.5 %fusion.15 = (bf16[32,4,16,128]{0,3,2,1:T(8,128)(2,1)}, bf16[32,4,16,128]{0,3,2,1:T(8,128)(2,1)}, bf16[32,4,16,128]{0,3,2,1:T(8,128)(2,1)}, bf16[32,4,16,128]{0,3,2,1:T(8,128)(2,1)}) fusion(s32[]{:T(128)S(6)} %select_n.168, bf16[128,4,16,64]{0,3,2,1:T(8,128)(2,1)S(1)} %get-tuple-element.4, bf16[128,4,16,64]{0,3,2,1:T(8,128)(2,1)S(1)} %get-tuple-element.3, ...), kind=kLoop, calls=%fused_computation.37 | loop fusion | flops 4194304 | bytes 4194320 | tf_op jit(solution)/shard_map/concatenate | solution.py:85
  88.3 2.9 %copy.60 = bf16[32,4,16,128]{3,2,1,0:T(8,128)(2,1)} copy(bf16[32,4,16,128]{0,3,2,1:T(8,128)(2,1)} %get-tuple-element.16) | data formatting | bytes 1048576 | tf_op jit(solution)/shard_map/dynamic_slice | solution.py:40
  91.7 2.9 %copy.61 = bf16[32,4,16,128]{3,2,1,0:T(8,128)(2,1)} copy(bf16[32,4,16,128]{0,3,2,1:T(8,128)(2,1)} %get-tuple-element.17) | data formatting | bytes 1048576 | tf_op jit(solution)/shard_map/dynamic_slice | solution.py:40
  94.5 0.8 collective-permute-start.4
  95.4 2.9 %copy.62 = bf16[32,4,16,128]{3,2,1,0:T(8,128)(2,1)} copy(bf16[32,4,16,128]{0,3,2,1:T(8,128)(2,1)} %get-tuple-element.18) | data formatting | bytes 1048576 | tf_op jit(solution)/shard_map/dynamic_slice | solution.py:40
  98.3 2.2 %copy.59 = bf16[32,4,16,128]{3,2,1,0:T(8,128)(2,1)S(1)} copy(bf16[32,4,16,128]{0,3,2,1:T(8,128)(2,1)} %get-tuple-element.15) | data formatting | bytes 1048576 | tf_op jit(solution)/shard_map/dynamic_slice | solution.py:40
  100.5 1.1 copy.64
  101.6 1.5 collective-permute-start.5
  103.2 1.6 pad_maximum_fusion.13
  105.2 0.8 pad_maximum_fusion.14
  106.1 1.3 collective-permute-start.12
  107.4 4.8 %collective-permute-start.13 = (bf16[32,1,64,128]{3,2,1,0:T(8,128)(2,1)S(1)}, bf16[32,1,64,128]{3,2,1,0:T(8,128)(2,1)S(1)}, u32[]{:S(2)}, u32[]{:S(2)}) collective-permute-start(bf16[32,1,64,128]{3,2,1,0:T(8,128)(2,1)S(1)} %get-tuple-element.24), channel_id=1, source_target_pairs={{0,4},{4,8},{8,12},{12,16},{16,20},{20,24},{24,28},{1,5},{5,9},{9,... | collective-permute-start | bytes 1572872 | tf_op jit(solution)/shard_map/ppermute | solution.py:19
  112.2 3.7 %collective-permute-done.5 = bf16[32,4,16,128]{3,2,1,0:T(8,128)(2,1)S(1)} collective-permute-done((bf16[32,4,16,128]{3,2,1,0:T(8,128)(2,1)}, bf16[32,4,16,128]{3,2,1,0:T(8,128)(2,1)S(1)}, u32[]{:S(2)}, u32[]{:S(2)}) %collective-permute-start.5) | collective-permute-done | bytes 524320 | tf_op jit(solution)/shard_map/ppermute | solution.py:42
  115.9 1.5 pad_maximum_fusion.10
  118.1 2.8 %collective-permute-done.12 = bf16[32,1,64,128]{3,2,1,0:T(8,128)(2,1)S(1)} collective-permute-done((bf16[32,1,64,128]{3,2,1,0:T(8,128)(2,1)S(1)}, bf16[32,1,64,128]{3,2,1,0:T(8,128)(2,1)S(1)}, u32[]{:S(2)}, u32[]{:S(2)}) %collective-permute-start.12) | collective-permute-done | bytes 524320 | tf_op jit(solution)/shard_map/ppermute | solution.py:21
  120.9 11.1 %collective-permute-done.13 = bf16[32,1,64,128]{3,2,1,0:T(8,128)(2,1)S(1)} collective-permute-done((bf16[32,1,64,128]{3,2,1,0:T(8,128)(2,1)S(1)}, bf16[32,1,64,128]{3,2,1,0:T(8,128)(2,1)S(1)}, u32[]{:S(2)}, u32[]{:S(2)}) %collective-permute-start.13) | collective-permute-done | bytes 524320 | tf_op jit(solution)/shard_map/ppermute | solution.py:19
  132.0 5.9 %fusion.6 = bf16[32,4,64,128]{3,2,1,0:T(8,128)(2,1)S(1)} fusion(f32[32,4,64,128]{3,2,1,0:T(8,128)S(1)} %get-tuple-element.26, bf16[32,1,64,128]{3,2,1,0:T(8,128)(2,1)S(1)} %collective-permute-done.13, bf16[32,4,16,128]{3,2,1,0:T(8,128)(2,1)S(1)} %get-tuple-element.28, bf16[32,4,16,128]{3,2,1,0:T(8,128)(2,1)S(1)} %get-tuple-element.29, ...), kind=kLoop, calls=%fused_computation.10 | loop fusion | flops 34603008 | bytes 9447424 | tf_op jit(solution)/shard_map/convert_element_type | solution.py:154
  138.0 0.7 pad_maximum_fusion
  138.7 0.9 fusion.18
  139.6 1.2 fusion.36
  140.8 1.7 pad_maximum_fusion.15
  142.5 5.8 %all-to-all-start = ((bf16[8,256,256]{2,1,0:T(8,128)(2,1)}), bf16[8,256,256]{2,1,0:T(8,128)(2,1)S(1)}, u32[]{:S(2)}, u32[]{:S(2)}) async-start(bf16[8,256,256]{2,1,0:T(8,128)(2,1)} %bitcast.34), calls=%async_computation | async-start | bytes 2097152 | tf_op jit(solution)/shard_map/all_to_all | solution.py:175
  148.3 25.9 %all-to-all-done = bf16[8,256,256]{2,1,0:T(8,128)(2,1)S(1)} async-done(((bf16[8,256,256]{2,1,0:T(8,128)(2,1)}), bf16[8,256,256]{2,1,0:T(8,128)(2,1)S(1)}, u32[]{:S(2)}, u32[]{:S(2)}) %all-to-all-start) | async-done | bytes 1048608 | tf_op jit(solution)/shard_map/all_to_all | solution.py:175
  174.6 9.9 %all_to_all.11 = f32[8,1,32]{2,1,0:T(1,128)S(1)} all-to-all(f32[8,1,32]{2,1,0:T(1,128)S(1)} %broadcast_in_dim.2), channel_id=1, replica_groups=mesh['gx'=8,'ka'=4] {'gx'}, dimensions={0} | all-to-all | bytes 2048 | tf_op jit(solution)/shard_map/all_to_all | solution.py:31
  185.1 0.8 slice_multiply_fusion
  (41 shorter events, 3.9 us)
Async XLA Ops:
  0.7 7.8 %copy-start = (bf16[32,4,64,128]{3,2,1,0:T(8,128)(2,1)S(1)}, bf16[32,4,64,128]{3,2,1,0:T(8,128)(2,1)}, u32[]{:S(2)}) copy-start(bf16[32,4,64,128]{3,2,1,0:T(8,128)(2,1)} %param.5) | copy-start | bytes 6291460
  4.0 14.3 %collective-permute-start = (bf16[32,4,16,128]{3,2,1,0:T(8,128)(2,1)}, bf16[32,4,16,128]{3,2,1,0:T(8,128)(2,1)S(1)}, u32[]{:S(2)}, u32[]{:S(2)}) collective-permute-start(bf16[32,4,16,128]{3,2,1,0:T(8,128)(2,1)} %get-tuple-element.20), channel_id=1, source_target_pairs={{0,1},{1,2},{2,3},{3,0},{4,5},{5,6},{6,7},{7,4},{8,9},{9,10},{10,1... | collective-permute-start | bytes 1572872 | tf_op jit(solution)/shard_map/ppermute | solution.py:42
  4.5 15.5 %collective-permute-start.1 = (bf16[32,4,16,128]{3,2,1,0:T(8,128)(2,1)}, bf16[32,4,16,128]{3,2,1,0:T(8,128)(2,1)S(1)}, u32[]{:S(2)}, u32[]{:S(2)}) collective-permute-start(bf16[32,4,16,128]{3,2,1,0:T(8,128)(2,1)} %get-tuple-element.22), channel_id=1, source_target_pairs={{0,2},{1,3},{2,0},{3,1},{4,6},{5,7},{6,4},{7,5},{8,10},{9,11},{10,... | collective-permute-start | bytes 1572872 | tf_op jit(solution)/shard_map/ppermute | solution.py:42
  7.0 3.5 %copy-start.2 = (f32[4,64]{1,0:T(4,128)S(1)}, f32[4,64]{1,0:T(4,128)}, u32[]{:S(2)}) copy-start(f32[4,64]{1,0:T(4,128)} %param.8) | copy-start | bytes 3076
  7.0 3.5 %copy-start.3 = (f32[4,64]{1,0:T(4,128)S(1)}, f32[4,64]{1,0:T(4,128)}, u32[]{:S(2)}) copy-start(f32[4,64]{1,0:T(4,128)} %param.7) | copy-start | bytes 3076
  7.0 23.7 %collective-permute-start.2 = (bf16[32,4,16,128]{3,2,1,0:T(8,128)(2,1)S(1)}, bf16[32,4,16,128]{3,2,1,0:T(8,128)(2,1)}, u32[]{:S(2)}, u32[]{:S(2)}) collective-permute-start(bf16[32,4,16,128]{3,2,1,0:T(8,128)(2,1)S(1)} %get-tuple-element.21), channel_id=1, source_target_pairs={{0,3},{1,0},{2,1},{3,2},{4,7},{5,4},{6,5},{7,6},{8,11},{9,8},{10,9... | collective-permute-start | bytes 1572872 | tf_op jit(solution)/shard_map/ppermute | solution.py:42
  10.1 32.7 %collective-permute-start.6 = (bf16[32,4,16,128]{3,2,1,0:T(8,128)(2,1)}, bf16[32,4,16,128]{3,2,1,0:T(8,128)(2,1)}, u32[]{:S(2)}, u32[]{:S(2)}) collective-permute-start(bf16[32,4,16,128]{3,2,1,0:T(8,128)(2,1)} %get-tuple-element.36), channel_id=1, source_target_pairs={{0,1},{1,2},{2,3},{3,0},{4,5},{5,6},{6,7},{7,4},{8,9},{9,10},{10,1... | collective-permute-start | bytes 1572872 | tf_op jit(solution)/shard_map/ppermute | solution.py:42
  10.1 32.7 %collective-permute-start.7 = (bf16[32,4,16,128]{3,2,1,0:T(8,128)(2,1)}, bf16[32,4,16,128]{3,2,1,0:T(8,128)(2,1)}, u32[]{:S(2)}, u32[]{:S(2)}) collective-permute-start(bf16[32,4,16,128]{3,2,1,0:T(8,128)(2,1)} %get-tuple-element.38), channel_id=1, source_target_pairs={{0,2},{1,3},{2,0},{3,1},{4,6},{5,7},{6,4},{7,5},{8,10},{9,11},{10,... | collective-permute-start | bytes 1572872 | tf_op jit(solution)/shard_map/ppermute | solution.py:42
  18.3 34.4 %collective-permute-start.8 = (bf16[32,4,16,128]{3,2,1,0:T(8,128)(2,1)S(1)}, bf16[32,4,16,128]{3,2,1,0:T(8,128)(2,1)}, u32[]{:S(2)}, u32[]{:S(2)}) collective-permute-start(bf16[32,4,16,128]{3,2,1,0:T(8,128)(2,1)S(1)} %get-tuple-element.37), channel_id=1, source_target_pairs={{0,3},{1,0},{2,1},{3,2},{4,7},{5,4},{6,5},{7,6},{8,11},{9,8},{10,9... | collective-permute-start | bytes 1572872 | tf_op jit(solution)/shard_map/ppermute | solution.py:42
  70.2 31.5 %collective-permute-start.9 = (bf16[32,4,16,128]{3,2,1,0:T(8,128)(2,1)}, bf16[32,4,16,128]{3,2,1,0:T(8,128)(2,1)}, u32[]{:S(2)}, u32[]{:S(2)}) collective-permute-start(bf16[32,4,16,128]{3,2,1,0:T(8,128)(2,1)} %copy.65), channel_id=1, source_target_pairs={{0,1},{1,2},{2,3},{3,0},{4,5},{5,6},{6,7},{7,4},{8,9},{9,10},{10,1... | collective-permute-start | bytes 1572872 | tf_op jit(solution)/shard_map/ppermute | solution.py:42
  73.1 30.0 %collective-permute-start.10 = (bf16[32,4,16,128]{3,2,1,0:T(8,128)(2,1)}, bf16[32,4,16,128]{3,2,1,0:T(8,128)(2,1)}, u32[]{:S(2)}, u32[]{:S(2)}) collective-permute-start(bf16[32,4,16,128]{3,2,1,0:T(8,128)(2,1)} %copy.66), channel_id=1, source_target_pairs={{0,2},{1,3},{2,0},{3,1},{4,6},{5,7},{6,4},{7,5},{8,10},{9,11},{10,... | collective-permute-start | bytes 1572872 | tf_op jit(solution)/shard_map/ppermute | solution.py:42
  78.3 24.9 %collective-permute-start.11 = (bf16[32,4,16,128]{3,2,1,0:T(8,128)(2,1)}, bf16[32,4,16,128]{3,2,1,0:T(8,128)(2,1)}, u32[]{:S(2)}, u32[]{:S(2)}) collective-permute-start(bf16[32,4,16,128]{3,2,1,0:T(8,128)(2,1)} %copy.67), channel_id=1, source_target_pairs={{0,3},{1,0},{2,1},{3,2},{4,7},{5,4},{6,5},{7,6},{8,11},{9,8},{10,9... | collective-permute-start | bytes 1572872 | tf_op jit(solution)/shard_map/ppermute | solution.py:42
  91.2 21.0 %collective-permute-start.3 = (bf16[32,4,16,128]{3,2,1,0:T(8,128)(2,1)}, bf16[32,4,16,128]{3,2,1,0:T(8,128)(2,1)}, u32[]{:S(2)}, u32[]{:S(2)}) collective-permute-start(bf16[32,4,16,128]{3,2,1,0:T(8,128)(2,1)} %copy.60), channel_id=1, source_target_pairs={{0,1},{1,2},{2,3},{3,0},{4,5},{5,6},{6,7},{7,4},{8,9},{9,10},{10,1... | collective-permute-start | bytes 1572872 | tf_op jit(solution)/shard_map/ppermute | solution.py:42
  94.5 17.7 %collective-permute-start.4 = (bf16[32,4,16,128]{3,2,1,0:T(8,128)(2,1)}, bf16[32,4,16,128]{3,2,1,0:T(8,128)(2,1)}, u32[]{:S(2)}, u32[]{:S(2)}) collective-permute-start(bf16[32,4,16,128]{3,2,1,0:T(8,128)(2,1)} %copy.61), channel_id=1, source_target_pairs={{0,2},{1,3},{2,0},{3,1},{4,6},{5,7},{6,4},{7,5},{8,10},{9,11},{10,... | collective-permute-start | bytes 1572872 | tf_op jit(solution)/shard_map/ppermute | solution.py:42
  101.6 14.3 %collective-permute-start.5 = (bf16[32,4,16,128]{3,2,1,0:T(8,128)(2,1)}, bf16[32,4,16,128]{3,2,1,0:T(8,128)(2,1)S(1)}, u32[]{:S(2)}, u32[]{:S(2)}) collective-permute-start(bf16[32,4,16,128]{3,2,1,0:T(8,128)(2,1)} %copy.62), channel_id=1, source_target_pairs={{0,3},{1,0},{2,1},{3,2},{4,7},{5,4},{6,5},{7,6},{8,11},{9,8},{10,9... | collective-permute-start | bytes 1572872 | tf_op jit(solution)/shard_map/ppermute | solution.py:42
  106.1 14.8 %collective-permute-start.12 = (bf16[32,1,64,128]{3,2,1,0:T(8,128)(2,1)S(1)}, bf16[32,1,64,128]{3,2,1,0:T(8,128)(2,1)S(1)}, u32[]{:S(2)}, u32[]{:S(2)}) collective-permute-start(bf16[32,1,64,128]{3,2,1,0:T(8,128)(2,1)S(1)} %get-tuple-element.23), channel_id=1, source_target_pairs={{4,0},{8,4},{12,8},{16,12},{20,16},{24,20},{28,24},{5,1},{9,5},{13... | collective-permute-start | bytes 1572872 | tf_op jit(solution)/shard_map/ppermute | solution.py:21
  107.4 24.6 %collective-permute-start.13 = (bf16[32,1,64,128]{3,2,1,0:T(8,128)(2,1)S(1)}, bf16[32,1,64,128]{3,2,1,0:T(8,128)(2,1)S(1)}, u32[]{:S(2)}, u32[]{:S(2)}) collective-permute-start(bf16[32,1,64,128]{3,2,1,0:T(8,128)(2,1)S(1)} %get-tuple-element.24), channel_id=1, source_target_pairs={{0,4},{4,8},{8,12},{12,16},{16,20},{20,24},{24,28},{1,5},{5,9},{9,... | collective-permute-start | bytes 1572872 | tf_op jit(solution)/shard_map/ppermute | solution.py:19
  117.8 14.2 %copy-start.1 = (f32[4,64]{1,0:T(4,128)S(1)}, f32[4,64]{1,0:T(4,128)}, u32[]{:S(2)}) copy-start(f32[4,64]{1,0:T(4,128)} %param.9) | copy-start | bytes 3076
  142.5 31.7 %all-to-all-start = ((bf16[8,256,256]{2,1,0:T(8,128)(2,1)}), bf16[8,256,256]{2,1,0:T(8,128)(2,1)S(1)}, u32[]{:S(2)}, u32[]{:S(2)}) async-start(bf16[8,256,256]{2,1,0:T(8,128)(2,1)} %bitcast.34), calls=%async_computation | async-start | bytes 2097152 | tf_op jit(solution)/shard_map/all_to_all | solution.py:175

commit v6 on v5

--- a/solution.py
+++ b/solution.py
@@ -1,8 +1,11 @@
+import functools
 import math
 
 import jax
 import jax.numpy as jnp
 from jax import lax
+from jax.experimental import pallas as pl
+from jax.experimental.pallas import tpu as pltpu
 from jax.sharding import PartitionSpec as P
 
 epsilon = 1e-06
@@ -67,6 +70,63 @@
     )
 
 
+def dft_kernel(*refs, count, weighted):
+    table_ref = refs[0]
+    piece_refs = refs[1:1 + count]
+    rest = refs[1 + count:]
+    out_ref = rest[-1]
+    width = piece_refs[0].shape[1]
+    lane = lax.broadcasted_iota(jnp.int32, (1, width), 1) % 128
+    low = lane < 64
+    rows = []
+    for piece_ref in piece_refs:
+        x = piece_ref[...].astype(jnp.float32)
+        swapped = jnp.where(low, pltpu.roll(x, width - 64, 1), -pltpu.roll(x, 64, 1))
+        rows.append(x)
+        rows.append(swapped)
+    stacked = jnp.concatenate(rows, axis=0).astype(jnp.bfloat16)
+    acc = jnp.dot(table_ref[...], stacked, preferred_element_type=jnp.float32)
+    modes = acc.astype(jnp.bfloat16)
+    if weighted:
+        modes = (modes.astype(jnp.float32) * rest[0][...]).astype(jnp.bfloat16)
+    out_ref[...] = modes
+
+def dft(table, pieces, weight=None):
+    count = len(pieces)
+    angles, total = pieces[0].shape
+    waves = table.shape[0]
+    block = math.gcd(total, 1024)
+    grid = (total // block,)
+    in_specs = [pl.BlockSpec((waves, table.shape[1]), lambda j: (0, 0))]
+    in_specs += [pl.BlockSpec((angles, block), lambda j: (0, j)) for _ in pieces]
+    args = [table, *pieces]
+    if weight is not None:
+        in_specs.append(pl.BlockSpec((1, block), lambda j: (0, j)))
+        args.append(weight)
+    return pl.pallas_call(
+        functools.partial(dft_kernel, count=count, weighted=weight is not None),
+        grid=grid,
+        in_specs=in_specs,
+        out_specs=pl.BlockSpec((waves, block), lambda j: (0, j)),
+        out_shape=jax.ShapeDtypeStruct((waves, total), jnp.bfloat16),
+    )(*args)
+
+
+def piece_tables(count, local_angles, axis):
+    here = lax.axis_index(axis)
+    blocks = count // local_angles
+    wave_index = jnp.arange(count, dtype=jnp.int32) - count // 2
+    scaling = 1.0 / math.sqrt(count)
+    columns = []
+    for shift in range(blocks):
+        angle_index = ((here - shift) % blocks) * local_angles + jnp.arange(local_angles, dtype=jnp.int32)
+        residues = wave_index[:, None] * angle_index[None, :] % count
+        phases = 2.0 * math.pi * residues.astype(jnp.float32) / count
+        columns.append((jnp.cos(phases) * scaling).astype(jnp.bfloat16))
+        columns.append((jnp.sin(phases) * scaling).astype(jnp.bfloat16))
+    return jnp.concatenate(columns, axis=1)
+
+
 def dft_tables(count):
     wave_index = jnp.arange(count, dtype=jnp.int32) - count // 2
     angle_index = jnp.arange(count, dtype=jnp.int32)
@@ -105,26 +165,25 @@
     local_angles, axial_cells, radial_cells, columns = direct_snapshots.shape
     snap_count = columns // 2
     total_angles = local_angles * lax.axis_size("ka")
-    cos_table, sin_table = shifted_tables(total_angles, local_angles, "ka")
+    table = piece_tables(total_angles, local_angles, "ka")
     first_wave = lax.axis_index("ka") * local_angles
-    moved_direct, moved_adjoint = (
-        jnp.concatenate(exchange(direct_snapshots, "ka", 2), axis=0),
-        jnp.concatenate(exchange(adjoint_snapshots, "ka", 2), axis=0),
-    )
-
-    def transform_all(snapshots):
-        flattened = snapshots.reshape(total_angles, -1)
-        cos_part = jnp.dot(cos_table, flattened, preferred_element_type=jnp.float32).reshape(
-            snapshots.shape
-        )
-        sin_part = jnp.dot(sin_table, flattened, preferred_element_type=jnp.float32).reshape(
-            snapshots.shape
-        )
-        return combine_parts(cos_part, sin_part, snap_count)
-
-    direct_modes, adjoint_modes = (
-        in_source_order(exchange(transform_all(moved_direct), "ka", 0), "ka", 2),
-        in_source_order(exchange(transform_all(moved_adjoint), "ka", 0), "ka", 2),
+    band_count = lax.axis_size("ka")
+    band = radial_cells // band_count
+    lanes = axial_cells * band * columns
+    norm_factor = 1.0 / math.sqrt(axial_cells * lax.axis_size("gx") * radial_cells)
+    band_weight = lax.dynamic_slice_in_dim(
+        quad_weight * norm_factor, lax.axis_index("ka") * band, band, axis=1
+    )
+    lane_weight = jnp.broadcast_to(band_weight[:, :, None], (axial_cells, band, columns)).reshape(1, lanes)
+
+    def transform_all(snapshots, weight=None):
+        pieces = [piece.reshape(local_angles, lanes) for piece in exchange(snapshots, "ka", 2)]
+        modes = dft(table, pieces, weight)
+        return modes.reshape(total_angles, axial_cells, band, columns)
+
+    direct_modes = in_source_order(exchange(transform_all(direct_snapshots), "ka", 0), "ka", 2)
+    weighted = in_source_order(
+        exchange(transform_all(adjoint_snapshots, lane_weight), "ka", 0), "ka", 2
     )
     padded = padded_2(direct_modes, (("gx", 1),), 1)
     field_f32 = direct_modes.astype(jnp.float32)
@@ -152,11 +211,6 @@
             - azimuthal[:, None, :, None] * field_f32
         )
     ).astype(jnp.bfloat16)
-    norm_factor = 1.0 / math.sqrt(axial_cells * lax.axis_size("gx") * radial_cells)
-    plane_weight = quad_weight * norm_factor
-    weighted = (adjoint_modes.astype(jnp.float32) * plane_weight[None, :, :, None]).astype(
-        jnp.bfloat16
-    )
     right_side = jnp.concatenate([direct_modes, image], axis=-1)
     product = jnp.einsum(
         "kpa,kpb->kab",

time: 187 us -> 161 us (0.86)
  other arithmetic: 37.3 us -> 15.3 us
  Pallas kernels: 0 us -> 14.1 us
  matrix products: 8.9 us -> 0.9 us
  local copies, waits for them, and re-layouts: 33.5 us -> 25.9 us
  waiting for transfers between devices: 73.4 us -> 67.4 us
  starting transfers between devices: 22 us -> 25 us
    dynamic_slice x10 -> x2, local copies, waits for them, and re-layouts: 25.4 us -> 4.54 us  [exchange(): lax.dynamic_slice_in_dim(cells, (here + shift) % count * width, width, ax...]
    unnamed x8 -> x18, local copies, waits for them, and re-layouts: 0.02 us -> 16.6 us
    concatenate x4 -> x0, other arithmetic: 16.3 us -> none  [the longest x2 10.6 us: combine_parts(): return jnp.concatenate([real_part, imag_part], axis=-1).astype(jnp.bfloat16)]
    pallas_call x0 -> x2, Pallas kernels: none -> 14.1 us  [dft(): pl.pallas_call(functools.partial(dft_kernel, count=count, weighted=weight...]
    dot_general x4 -> x0, matrix products: 7.97 us -> none  [the longest x2 3.99 us: transform_all(): jnp.dot(cos_table, flattened, preferred_element_type=jnp.float32)]
    reshape x2 -> x0, local copies, waits for them, and re-layouts: 6.97 us -> none  [transform_all(): flattened = snapshots.reshape(total_angles, -1)]
    another operation x3 -> x1, other arithmetic: 6.72 us -> 1.17 us
    ppermute x1, waiting for transfers between devices: 11.1 us -> 7.14 us  [padded_2(): lax.ppermute(tail, axis, [(i, (i + 1) % count) for i in range(ends)])]
  transfers between devices with their start and end apart: 15 -> 15, of which waited for: 8 -> 9; matrix products, arithmetic and copies ran while one was open for 25% -> 17% of each run, Pallas kernels for 0% -> 9%
where the time goes in v6:
time: 161 us; the launch traced here: 159 us
  waiting for transfers between devices  67.4 us (42%)
  local copies, waits for them, and re-layouts  25.9 us (16%)
  starting transfers between devices  25 us (16%)
  other arithmetic  15.3 us (10%)
  Pallas kernels  14.1 us (9%)
  blocking collectives  9.9 us (6%)
    ppermute x12, waiting for transfers between devices, exchange(): lax.ppermute(piece, axis, [(j, (j + shift) % count) for j in range(count)])  34.2 us
    all_to_all x1, waiting for transfers between devices, local(): lax.all_to_all(shares, 'gx', split_axis=0, concat_axis=0, tiled=True)  26 us
    unnamed x18, local copies, waits for them, and re-layouts  16.6 us
    pallas_call x2, Pallas kernels, dft(): pl.pallas_call(functools.partial(dft_kernel, count=count, weighted=weight...  14.1 us
    ppermute x12, starting transfers between devices, exchange(): lax.ppermute(piece, axis, [(j, (j + shift) % count) for j in range(count)])  13.1 us
    all_to_all x1, blocking collectives, gather_small(): return lax.all_to_all(copies, axis, split_axis=0, concat_axis=0, tiled=True)  9.9 us
    ppermute x1, waiting for transfers between devices, padded_2(): lax.ppermute(tail, axis, [(i, (i + 1) % count) for i in range(ends)])  7.14 us
    convert_element_type x1, other arithmetic, local(): image = (-velocity * (forward - behind) * 0.5 + diffusion * (forward + be...  5.9 us
  transfers between devices with their start and end apart: 15, of which 9 were waited for; matrix products, arithmetic and copies ran while one was open for 17% of the time, Pallas kernels for 9%

profile of v6, /device:TPU:0, one launch (start us, length us, event | category | flops | bytes accessed | tf_op | source)
XLA Modules:
  0.0 159.4 jit_solution(12066143040622175152)
XLA Ops:
  0.7 3.1 %constant_dynamic-slice_fusion.3 = (bf16[32,4,16,128]{3,2,1,0:T(8,128)(2,1)}, bf16[32,4,16,128]{3,2,1,0:T(8,128)(2,1)}, bf16[32,4,16,128]{3,2,1,0:T(8,128)(2,1)S(1)}, bf16[32,4,16,128]{3,2,1,0:T(8,128)(2,1)}) fusion(bf16[32,4,64,128]{3,2,1,0:T(8,128)(2,1)} %param.5, s32[]{:T(128)S(6)} %select_n.166, s32[]{:T(128)S(6)} %select_n.162, s32[]{:T(128)S(6)} %select_n.160, ...), kind=kLoop, calls=%fused_computation.100 | loop fusion | bytes 4194320 | tf_op jit(solution)/shard_map/dynamic_slice | solution.py:43
  3.8 2.4 %collective-permute-start.8 = (bf16[32,4,16,128]{3,2,1,0:T(8,128)(2,1)}, bf16[32,4,16,128]{3,2,1,0:T(8,128)(2,1)}, u32[]{:S(2)}, u32[]{:S(2)}) collective-permute-start(bf16[32,4,16,128]{3,2,1,0:T(8,128)(2,1)} %get-tuple-element.19), channel_id=1, source_target_pairs={{0,3},{1,0},{2,1},{3,2},{4,7},{5,4},{6,5},{7,6},{8,11},{9,8},{10,9... | collective-permute-start | bytes 1572872 | tf_op jit(solution)/shard_map/ppermute | solution.py:45
  6.2 0.6 collective-permute-start.7
  7.0 1.5 constant_dynamic-slice_fusion.11
  8.4 1.6 %collective-permute-start.2 = (bf16[32,4,16,128]{3,2,1,0:T(8,128)(2,1)}, bf16[32,4,16,128]{3,2,1,0:T(8,128)(2,1)S(1)}, u32[]{:S(2)}, u32[]{:S(2)}) collective-permute-start(bf16[32,4,16,128]{3,2,1,0:T(8,128)(2,1)} %get-tuple-element.31), channel_id=1, source_target_pairs={{0,3},{1,0},{2,1},{3,2},{4,7},{5,4},{6,5},{7,6},{8,11},{9,8},{10,9... | collective-permute-start | bytes 1572872 | tf_op jit(solution)/shard_map/ppermute | solution.py:45
  10.0 1.4 collective-permute-start.1
  13.0 1.1 copy.40
  14.2 1.1 copy.44
  15.3 0.8 concatenate.23.refs_0_
  16.1 2.6 %collective-permute-done.8 = bf16[32,4,16,128]{3,2,1,0:T(8,128)(2,1)} collective-permute-done((bf16[32,4,16,128]{3,2,1,0:T(8,128)(2,1)}, bf16[32,4,16,128]{3,2,1,0:T(8,128)(2,1)}, u32[]{:S(2)}, u32[]{:S(2)}) %collective-permute-start.8) | collective-permute-done | bytes 524320 | tf_op jit(solution)/shard_map/ppermute | solution.py:45
  18.7 1.2 collective-permute-start
  20.0 2.2 %copy.37 = bf16[4,8,64,128]{3,1,2,0:T(8,128)(2,1)} copy(bf16[4,8,64,128]{3,2,1,0:T(8,128)(2,1)} %bitcast.46) | data formatting | bytes 1048576
  22.1 9.0 %collective-permute-done.7 = bf16[32,4,16,128]{3,2,1,0:T(8,128)(2,1)} collective-permute-done((bf16[32,4,16,128]{3,2,1,0:T(8,128)(2,1)}, bf16[32,4,16,128]{3,2,1,0:T(8,128)(2,1)}, u32[]{:S(2)}, u32[]{:S(2)}) %collective-permute-start.7) | collective-permute-done | bytes 524320 | tf_op jit(solution)/shard_map/ppermute | solution.py:45
  31.1 2.2 %copy.38 = bf16[4,8,64,128]{3,1,2,0:T(8,128)(2,1)} copy(bf16[4,8,64,128]{3,2,1,0:T(8,128)(2,1)} %bitcast.43) | data formatting | bytes 1048576
  33.3 2.2 %copy.39 = bf16[4,8,64,128]{3,1,2,0:T(8,128)(2,1)} copy(bf16[4,8,64,128]{3,2,1,0:T(8,128)(2,1)} %bitcast.40) | data formatting | bytes 1048576
  35.5 7.0 %shard_map.77 = bf16[128,8192]{1,0:T(8,128)(2,1)} custom-call(bf16[128,256]{1,0:T(8,128)(2,1)} %concatenate.23.refs_0_, bf16[32,8192]{1,0:T(8,128)(2,1)} %bitcast.88, bf16[32,8192]{1,0:T(8,128)(2,1)} %bitcast.94, bf16[32,8192]{1,0:T(8,128)(2,1)} %bitcast.92, bf16[32,8192]{1,0:T(8,128)(2,1)} %bitcast.90), custom_call_target="tpu_custom_call" | custom-call | tf_op jit(solution)/shard_map/pallas_call | solution.py:106
  42.4 2.2 %copy.28 = bf16[16,8,64,128]{3,2,1,0:T(8,128)(2,1)S(1)} copy(bf16[16,8,64,128]{3,1,2,0:T(8,128)(2,1)} %bitcast.84) | data formatting | bytes 4194304
  44.6 1.4 dynamic-slice_bitcast_fusion.4
  46.0 1.4 collective-permute-start.10
  47.4 1.4 collective-permute-start.11
  49.0 1.2 copy.41
  50.2 3.2 %collective-permute-done.1 = bf16[32,4,16,128]{3,2,1,0:T(8,128)(2,1)S(1)} collective-permute-done((bf16[32,4,16,128]{3,2,1,0:T(8,128)(2,1)}, bf16[32,4,16,128]{3,2,1,0:T(8,128)(2,1)S(1)}, u32[]{:S(2)}, u32[]{:S(2)}) %collective-permute-start.1) | collective-permute-done | bytes 524320 | tf_op jit(solution)/shard_map/ppermute | solution.py:45
  53.4 1.1 copy.42
  54.6 1.1 copy.43
  55.7 0.7 broadcast_in_dim.4
  56.4 7.1 %shard_map.76 = bf16[128,8192]{1,0:T(8,128)(2,1)} custom-call(bf16[128,256]{1,0:T(8,128)(2,1)} %concatenate.23.refs_0_, bf16[32,8192]{1,0:T(8,128)(2,1)} %bitcast.87, bf16[32,8192]{1,0:T(8,128)(2,1)} %bitcast.93, bf16[32,8192]{1,0:T(8,128)(2,1)} %bitcast.91, bf16[32,8192]{1,0:T(8,128)(2,1)} %bitcast.89, f32[1,8192]{1,0:T(1,128)} %bitcast.102), custom_call_target="tpu_custom_call" | custom-call | tf_op jit(solution)/shard_map/pallas_call | solution.py:106
  63.5 2.2 %copy.23 = bf16[16,8,64,128]{3,2,1,0:T(8,128)(2,1)S(1)} copy(bf16[16,8,64,128]{3,1,2,0:T(8,128)(2,1)} %bitcast.82) | data formatting | bytes 4194304
  65.7 0.4 dynamic-slice_bitcast_fusion.9
  66.2 1.4 collective-permute-start.4
  67.6 1.4 collective-permute-start.5
  69.0 5.8 %collective-permute-done.11 = bf16[32,4,16,128]{3,2,1,0:T(8,128)(2,1)} collective-permute-done((bf16[32,4,16,128]{3,2,1,0:T(8,128)(2,1)S(1)}, bf16[32,4,16,128]{3,2,1,0:T(8,128)(2,1)}, u32[]{:S(2)}, u32[]{:S(2)}) %collective-permute-start.11) | collective-permute-done | bytes 524320 | tf_op jit(solution)/shard_map/ppermute | solution.py:45
  74.8 1.5 pad_maximum_fusion.11
  76.7 0.8 pad_maximum_fusion.12
  77.6 1.3 collective-permute-start.12
  78.9 4.8 %collective-permute-start.13 = (bf16[32,1,64,128]{3,2,1,0:T(8,128)(2,1)S(1)}, bf16[32,1,64,128]{3,2,1,0:T(8,128)(2,1)S(1)}, u32[]{:S(2)}, u32[]{:S(2)}) collective-permute-start(bf16[32,1,64,128]{3,2,1,0:T(8,128)(2,1)S(1)} %get-tuple-element.8), channel_id=1, source_target_pairs={{0,4},{4,8},{8,12},{12,16},{16,20},{20,24},{24,28},{1,5},{5,9},{9,... | collective-permute-start | bytes 1572872 | tf_op jit(solution)/shard_map/ppermute | solution.py:22
  83.6 3.1 %collective-permute-done.3 = bf16[32,4,16,128]{3,2,1,0:T(8,128)(2,1)S(1)} collective-permute-done((bf16[32,4,16,128]{3,2,1,0:T(8,128)(2,1)S(1)}, bf16[32,4,16,128]{3,2,1,0:T(8,128)(2,1)S(1)}, u32[]{:S(2)}, u32[]{:S(2)}) %collective-permute-start.3) | collective-permute-done | bytes 524320 | tf_op jit(solution)/shard_map/ppermute | solution.py:45
  87.1 10.1 %collective-permute-done.5 = bf16[32,4,16,128]{3,2,1,0:T(8,128)(2,1)S(1)} collective-permute-done((bf16[32,4,16,128]{3,2,1,0:T(8,128)(2,1)S(1)}, bf16[32,4,16,128]{3,2,1,0:T(8,128)(2,1)S(1)}, u32[]{:S(2)}, u32[]{:S(2)}) %collective-permute-start.5) | collective-permute-done | bytes 524320 | tf_op jit(solution)/shard_map/ppermute | solution.py:45
  98.3 7.1 %collective-permute-done.13 = bf16[32,1,64,128]{3,2,1,0:T(8,128)(2,1)S(1)} collective-permute-done((bf16[32,1,64,128]{3,2,1,0:T(8,128)(2,1)S(1)}, bf16[32,1,64,128]{3,2,1,0:T(8,128)(2,1)S(1)}, u32[]{:S(2)}, u32[]{:S(2)}) %collective-permute-start.13) | collective-permute-done | bytes 524320 | tf_op jit(solution)/shard_map/ppermute | solution.py:22
  105.4 5.9 %fusion.6 = bf16[32,4,64,128]{3,2,1,0:T(8,128)(2,1)S(1)} fusion(f32[32,4,64,128]{3,2,1,0:T(8,128)S(1)} %get-tuple-element.10, bf16[32,1,64,128]{3,2,1,0:T(8,128)(2,1)S(1)} %collective-permute-done.13, bf16[32,4,16,128]{3,2,1,0:T(8,128)(2,1)S(1)} %get-tuple-element.12, bf16[32,4,16,128]{3,2,1,0:T(8,128)(2,1)S(1)} %get-tuple-element.13, ...), kind=kLoop, calls=%fused_computation.10 | loop fusion | flops 34603008 | bytes 9447424 | tf_op jit(solution)/shard_map/convert_element_type | solution.py:213
  111.3 0.7 pad_maximum_fusion
  112.1 0.9 fusion.23
  113.0 1.2 fusion.12
  114.1 1.7 %pad_maximum_fusion.13 = bf16[32,64,256]{2,1,0:T(8,128)(2,1)} fusion(bf16[32,64,64]{2,1,0:T(8,128)(2,1)S(1)} %get-tuple-element.6, bf16[32,64,64]{2,1,0:T(8,128)(2,1)S(1)} %get-tuple-element.5, bf16[32,64,64]{2,1,0:T(8,128)(2,1)S(1)} %get-tuple-element.4, bf16[32,64,64]{2,1,0:T(8,128)(2,1)S(1)} %get-tuple-element.3), kind=kLoop, calls=%fused_computation.35 | loop fusion | flops 4194304 | bytes 2097152 | tf_op jit(solution)/shard_map/concatenate | solution.py:161
  115.8 5.8 %all-to-all-start = ((bf16[8,256,256]{2,1,0:T(8,128)(2,1)}), bf16[8,256,256]{2,1,0:T(8,128)(2,1)S(1)}, u32[]{:S(2)}, u32[]{:S(2)}) async-start(bf16[8,256,256]{2,1,0:T(8,128)(2,1)} %bitcast.19), calls=%async_computation | async-start | bytes 2097152 | tf_op jit(solution)/shard_map/all_to_all | solution.py:229
  121.6 26.0 %all-to-all-done = bf16[8,256,256]{2,1,0:T(8,128)(2,1)S(1)} async-done(((bf16[8,256,256]{2,1,0:T(8,128)(2,1)}), bf16[8,256,256]{2,1,0:T(8,128)(2,1)S(1)}, u32[]{:S(2)}, u32[]{:S(2)}) %all-to-all-start) | async-done | bytes 1048608 | tf_op jit(solution)/shard_map/all_to_all | solution.py:229
  148.1 9.9 %all_to_all.11 = f32[8,1,32]{2,1,0:T(1,128)S(1)} all-to-all(f32[8,1,32]{2,1,0:T(1,128)S(1)} %broadcast_in_dim.5), channel_id=1, replica_groups=mesh['gx'=8,'ka'=4] {'gx'}, dimensions={0} | all-to-all | bytes 2048 | tf_op jit(solution)/shard_map/all_to_all | solution.py:34
  158.0 0.5 multiply_sqrt_fusion
  158.6 0.8 slice_multiply_fusion
  (48 shorter events, 4.2 us)
Async XLA Ops:
  0.6 6.4 %copy-start = (bf16[32,4,64,128]{3,2,1,0:T(8,128)(2,1)S(1)}, bf16[32,4,64,128]{3,2,1,0:T(8,128)(2,1)}, u32[]{:S(2)}) copy-start(bf16[32,4,64,128]{3,2,1,0:T(8,128)(2,1)} %param.6) | copy-start | bytes 6291460
  3.8 10.4 %copy-start.2 = (f32[4,64]{1,0:T(4,128)S(1)}, f32[4,64]{1,0:T(4,128)}, u32[]{:S(2)}) copy-start(f32[4,64]{1,0:T(4,128)} %param.8) | copy-start | bytes 3076
  3.8 12.3 %copy-start.3 = (f32[4,64]{1,0:T(4,128)S(1)}, f32[4,64]{1,0:T(4,128)}, u32[]{:S(2)}) copy-start(f32[4,64]{1,0:T(4,128)} %param.7) | copy-start | bytes 3076
  3.8 14.9 %collective-permute-start.8 = (bf16[32,4,16,128]{3,2,1,0:T(8,128)(2,1)}, bf16[32,4,16,128]{3,2,1,0:T(8,128)(2,1)}, u32[]{:S(2)}, u32[]{:S(2)}) collective-permute-start(bf16[32,4,16,128]{3,2,1,0:T(8,128)(2,1)} %get-tuple-element.19), channel_id=1, source_target_pairs={{0,3},{1,0},{2,1},{3,2},{4,7},{5,4},{6,5},{7,6},{8,11},{9,8},{10,9... | collective-permute-start | bytes 1572872 | tf_op jit(solution)/shard_map/ppermute | solution.py:45
  6.2 24.9 %collective-permute-start.7 = (bf16[32,4,16,128]{3,2,1,0:T(8,128)(2,1)}, bf16[32,4,16,128]{3,2,1,0:T(8,128)(2,1)}, u32[]{:S(2)}, u32[]{:S(2)}) collective-permute-start(bf16[32,4,16,128]{3,2,1,0:T(8,128)(2,1)} %get-tuple-element.22), channel_id=1, source_target_pairs={{0,2},{1,3},{2,0},{3,1},{4,6},{5,7},{6,4},{7,5},{8,10},{9,11},{10,... | collective-permute-start | bytes 1572872 | tf_op jit(solution)/shard_map/ppermute | solution.py:45
  6.8 26.4 %collective-permute-start.6 = (bf16[32,4,16,128]{3,2,1,0:T(8,128)(2,1)}, bf16[32,4,16,128]{3,2,1,0:T(8,128)(2,1)}, u32[]{:S(2)}, u32[]{:S(2)}) collective-permute-start(bf16[32,4,16,128]{3,2,1,0:T(8,128)(2,1)} %get-tuple-element.20), channel_id=1, source_target_pairs={{0,1},{1,2},{2,3},{3,0},{4,5},{5,6},{6,7},{7,4},{8,9},{9,10},{10,1... | collective-permute-start | bytes 1572872 | tf_op jit(solution)/shard_map/ppermute | solution.py:45
  8.4 39.0 %collective-permute-start.2 = (bf16[32,4,16,128]{3,2,1,0:T(8,128)(2,1)}, bf16[32,4,16,128]{3,2,1,0:T(8,128)(2,1)S(1)}, u32[]{:S(2)}, u32[]{:S(2)}) collective-permute-start(bf16[32,4,16,128]{3,2,1,0:T(8,128)(2,1)} %get-tuple-element.31), channel_id=1, source_target_pairs={{0,3},{1,0},{2,1},{3,2},{4,7},{5,4},{6,5},{7,6},{8,11},{9,8},{10,9... | collective-permute-start | bytes 1572872 | tf_op jit(solution)/shard_map/ppermute | solution.py:45
  10.0 43.4 %collective-permute-start.1 = (bf16[32,4,16,128]{3,2,1,0:T(8,128)(2,1)}, bf16[32,4,16,128]{3,2,1,0:T(8,128)(2,1)S(1)}, u32[]{:S(2)}, u32[]{:S(2)}) collective-permute-start(bf16[32,4,16,128]{3,2,1,0:T(8,128)(2,1)} %get-tuple-element.34), channel_id=1, source_target_pairs={{0,2},{1,3},{2,0},{3,1},{4,6},{5,7},{6,4},{7,5},{8,10},{9,11},{10,... | collective-permute-start | bytes 1572872 | tf_op jit(solution)/shard_map/ppermute | solution.py:45
  18.7 35.8 %collective-permute-start = (bf16[32,4,16,128]{3,2,1,0:T(8,128)(2,1)}, bf16[32,4,16,128]{3,2,1,0:T(8,128)(2,1)S(1)}, u32[]{:S(2)}, u32[]{:S(2)}) collective-permute-start(bf16[32,4,16,128]{3,2,1,0:T(8,128)(2,1)} %get-tuple-element.32), channel_id=1, source_target_pairs={{0,1},{1,2},{2,3},{3,0},{4,5},{5,6},{6,7},{7,4},{8,9},{9,10},{10,1... | collective-permute-start | bytes 1572872 | tf_op jit(solution)/shard_map/ppermute | solution.py:45
  46.0 21.5 %collective-permute-start.9 = (bf16[32,4,16,128]{3,2,1,0:T(8,128)(2,1)}, bf16[32,4,16,128]{3,2,1,0:T(8,128)(2,1)S(1)}, u32[]{:S(2)}, u32[]{:S(2)}) collective-permute-start(bf16[32,4,16,128]{3,2,1,0:T(8,128)(2,1)} %get-tuple-element.18), channel_id=1, source_target_pairs={{0,1},{1,2},{2,3},{3,0},{4,5},{5,6},{6,7},{7,4},{8,9},{9,10},{10,1... | collective-permute-start | bytes 1572872 | tf_op jit(solution)/shard_map/ppermute | solution.py:45
  46.0 22.9 %collective-permute-start.10 = (bf16[32,4,16,128]{3,2,1,0:T(8,128)(2,1)}, bf16[32,4,16,128]{3,2,1,0:T(8,128)(2,1)}, u32[]{:S(2)}, u32[]{:S(2)}) collective-permute-start(bf16[32,4,16,128]{3,2,1,0:T(8,128)(2,1)} %get-tuple-element.17), channel_id=1, source_target_pairs={{0,2},{1,3},{2,0},{3,1},{4,6},{5,7},{6,4},{7,5},{8,10},{9,11},{10,... | collective-permute-start | bytes 1572872 | tf_op jit(solution)/shard_map/ppermute | solution.py:45
  47.4 27.3 %collective-permute-start.11 = (bf16[32,4,16,128]{3,2,1,0:T(8,128)(2,1)S(1)}, bf16[32,4,16,128]{3,2,1,0:T(8,128)(2,1)}, u32[]{:S(2)}, u32[]{:S(2)}) collective-permute-start(bf16[32,4,16,128]{3,2,1,0:T(8,128)(2,1)S(1)} %get-tuple-element.16), channel_id=1, source_target_pairs={{0,3},{1,0},{2,1},{3,2},{4,7},{5,4},{6,5},{7,6},{8,11},{9,8},{10,9... | collective-permute-start | bytes 1572872 | tf_op jit(solution)/shard_map/ppermute | solution.py:45
  66.1 20.7 %collective-permute-start.3 = (bf16[32,4,16,128]{3,2,1,0:T(8,128)(2,1)S(1)}, bf16[32,4,16,128]{3,2,1,0:T(8,128)(2,1)S(1)}, u32[]{:S(2)}, u32[]{:S(2)}) collective-permute-start(bf16[32,4,16,128]{3,2,1,0:T(8,128)(2,1)S(1)} %get-tuple-element.30), channel_id=1, source_target_pairs={{0,1},{1,2},{2,3},{3,0},{4,5},{5,6},{6,7},{7,4},{8,9},{9,10},{10,1... | collective-permute-start | bytes 1572872 | tf_op jit(solution)/shard_map/ppermute | solution.py:45
  66.2 21.0 %collective-permute-start.4 = (bf16[32,4,16,128]{3,2,1,0:T(8,128)(2,1)S(1)}, bf16[32,4,16,128]{3,2,1,0:T(8,128)(2,1)S(1)}, u32[]{:S(2)}, u32[]{:S(2)}) collective-permute-start(bf16[32,4,16,128]{3,2,1,0:T(8,128)(2,1)S(1)} %get-tuple-element.29), channel_id=1, source_target_pairs={{0,2},{1,3},{2,0},{3,1},{4,6},{5,7},{6,4},{7,5},{8,10},{9,11},{10,... | collective-permute-start | bytes 1572872 | tf_op jit(solution)/shard_map/ppermute | solution.py:45
  67.6 29.7 %collective-permute-start.5 = (bf16[32,4,16,128]{3,2,1,0:T(8,128)(2,1)S(1)}, bf16[32,4,16,128]{3,2,1,0:T(8,128)(2,1)S(1)}, u32[]{:S(2)}, u32[]{:S(2)}) collective-permute-start(bf16[32,4,16,128]{3,2,1,0:T(8,128)(2,1)S(1)} %get-tuple-element.28), channel_id=1, source_target_pairs={{0,3},{1,0},{2,1},{3,2},{4,7},{5,4},{6,5},{7,6},{8,11},{9,8},{10,9... | collective-permute-start | bytes 1572872 | tf_op jit(solution)/shard_map/ppermute | solution.py:45
  77.6 20.7 %collective-permute-start.12 = (bf16[32,1,64,128]{3,2,1,0:T(8,128)(2,1)S(1)}, bf16[32,1,64,128]{3,2,1,0:T(8,128)(2,1)S(1)}, u32[]{:S(2)}, u32[]{:S(2)}) collective-permute-start(bf16[32,1,64,128]{3,2,1,0:T(8,128)(2,1)S(1)} %get-tuple-element.7), channel_id=1, source_target_pairs={{4,0},{8,4},{12,8},{16,12},{20,16},{24,20},{28,24},{5,1},{9,5},{13... | collective-permute-start | bytes 1572872 | tf_op jit(solution)/shard_map/ppermute | solution.py:24
  78.9 26.5 %collective-permute-start.13 = (bf16[32,1,64,128]{3,2,1,0:T(8,128)(2,1)S(1)}, bf16[32,1,64,128]{3,2,1,0:T(8,128)(2,1)S(1)}, u32[]{:S(2)}, u32[]{:S(2)}) collective-permute-start(bf16[32,1,64,128]{3,2,1,0:T(8,128)(2,1)S(1)} %get-tuple-element.8), channel_id=1, source_target_pairs={{0,4},{4,8},{8,12},{12,16},{16,20},{20,24},{24,28},{1,5},{5,9},{9,... | collective-permute-start | bytes 1572872 | tf_op jit(solution)/shard_map/ppermute | solution.py:22
  97.5 7.9 %copy-start.1 = (f32[4,64]{1,0:T(4,128)S(1)}, f32[4,64]{1,0:T(4,128)}, u32[]{:S(2)}) copy-start(f32[4,64]{1,0:T(4,128)} %param.9) | copy-start | bytes 3076
  115.8 31.8 %all-to-all-start = ((bf16[8,256,256]{2,1,0:T(8,128)(2,1)}), bf16[8,256,256]{2,1,0:T(8,128)(2,1)S(1)}, u32[]{:S(2)}, u32[]{:S(2)}) async-start(bf16[8,256,256]{2,1,0:T(8,128)(2,1)} %bitcast.19), calls=%async_computation | async-start | bytes 2097152 | tf_op jit(solution)/shard_map/all_to_all | solution.py:229

commit v7 on v6

--- a/solution.py
+++ b/solution.py
@@ -34,13 +34,15 @@
     return lax.all_to_all(copies, axis, split_axis=0, concat_axis=0, tiled=True)
 
 
-def exchange(cells, axis, split_axis):
+def exchange(cells, axis, split_axis, offset=0, width=None):
     count = lax.axis_size(axis)
     here = lax.axis_index(axis)
-    width = cells.shape[split_axis] // count
+    stride = cells.shape[split_axis] // count
+    width = stride if width is None else width
     pieces = []
     for shift in range(count):
-        piece = lax.dynamic_slice_in_dim(cells, ((here + shift) % count) * width, width, axis=split_axis)
+        start = ((here + shift) % count) * stride + offset
+        piece = lax.dynamic_slice_in_dim(cells, start, width, axis=split_axis)
         if shift:
             piece = lax.ppermute(piece, axis, [(j, (j + shift) % count) for j in range(count)])
         pieces.append(piece)
@@ -112,10 +114,10 @@
     )(*args)
 
 
-def piece_tables(count, local_angles, axis):
+def piece_tables(count, local_angles, axis, wave_order):
     here = lax.axis_index(axis)
     blocks = count // local_angles
-    wave_index = jnp.arange(count, dtype=jnp.int32) - count // 2
+    wave_index = wave_order - count // 2
     scaling = 1.0 / math.sqrt(count)
     columns = []
     for shift in range(blocks):
@@ -164,13 +166,27 @@
 def local(direct_snapshots, adjoint_snapshots, quad_weight, mean_velocity, diffusivity):
     local_angles, axial_cells, radial_cells, columns = direct_snapshots.shape
     snap_count = columns // 2
-    total_angles = local_angles * lax.axis_size("ka")
-    table = piece_tables(total_angles, local_angles, "ka")
+    band_count = lax.axis_size("ka")
+    axial_count = lax.axis_size("gx")
+    total_angles = local_angles * band_count
+    owned = local_angles // axial_count
+    halves = 2 if local_angles % axial_count == 0 and owned % 2 == 0 else 1
+    half_waves = local_angles // halves
+    position = jnp.arange(local_angles, dtype=jnp.int32)
+    if halves == 1:
+        local_order = position
+    else:
+        part = owned // halves
+        within = position % half_waves
+        local_order = (within // part) * owned + (position // half_waves) * part + within % part
+    wave_order = (
+        jnp.arange(band_count, dtype=jnp.int32)[:, None] * local_angles + local_order[None, :]
+    ).reshape(total_angles)
+    table = piece_tables(total_angles, local_angles, "ka", wave_order)
     first_wave = lax.axis_index("ka") * local_angles
-    band_count = lax.axis_size("ka")
     band = radial_cells // band_count
     lanes = axial_cells * band * columns
-    norm_factor = 1.0 / math.sqrt(axial_cells * lax.axis_size("gx") * radial_cells)
+    norm_factor = 1.0 / math.sqrt(axial_cells * axial_count * radial_cells)
     band_weight = lax.dynamic_slice_in_dim(
         quad_weight * norm_factor, lax.axis_index("ka") * band, band, axis=1
     )
@@ -181,53 +197,58 @@
         modes = dft(table, pieces, weight)
         return modes.reshape(total_angles, axial_cells, band, columns)
 
-    direct_modes = in_source_order(exchange(transform_all(direct_snapshots), "ka", 0), "ka", 2)
-    weighted = in_source_order(
-        exchange(transform_all(adjoint_snapshots, lane_weight), "ka", 0), "ka", 2
-    )
-    padded = padded_2(direct_modes, (("gx", 1),), 1)
-    field_f32 = direct_modes.astype(jnp.float32)
-    forward = padded[:, 2:].astype(jnp.float32)
-    behind = padded[:, :-2].astype(jnp.float32)
-    radial_pad = jnp.pad(field_f32, ((0, 0), (0, 0), (1, 1), (0, 0)))
-    outward = radial_pad[:, :, 2:]
-    inward = radial_pad[:, :, :-2]
+    direct_all = transform_all(direct_snapshots)
+    weighted_all = transform_all(adjoint_snapshots, lane_weight)
     radius = 0.25 + (jnp.arange(radial_cells, dtype=jnp.float32) + 0.5) / radial_cells
-    wavenumber = (
-        first_wave + jnp.arange(local_angles, dtype=jnp.int32) - total_angles // 2
-    ).astype(jnp.float32) / total_angles
-    azimuthal = (wavenumber[:, None] / radius[None, :]) ** 2
     velocity = mean_velocity[None, :, :, None]
     diffusion = diffusivity[None, :, :, None]
-    image = (
-        -velocity * (forward - behind) * 0.5
-        + diffusion
-        * (
-            forward
-            + behind
-            + outward
-            + inward
-            - 4.0 * field_f32
-            - azimuthal[:, None, :, None] * field_f32
-        )
-    ).astype(jnp.bfloat16)
-    right_side = jnp.concatenate([direct_modes, image], axis=-1)
-    product = jnp.einsum(
-        "kpa,kpb->kab",
-        weighted.reshape(local_angles, -1, columns),
-        right_side.reshape(local_angles, -1, 2 * columns),
-        preferred_element_type=jnp.float32,
-    )
-    gram_terms = complex_blocks(product, snap_count).reshape(local_angles * snap_count, 2 * columns)
-    row_count = gram_terms.shape[0] // lax.axis_size("gx")
+    row_count = local_angles * snap_count // axial_count
+    half_rows = row_count // halves
+    own_parts = []
+    for half in range(halves):
+        offset = half * half_waves
+        direct_modes = in_source_order(exchange(direct_all, "ka", 0, offset, half_waves), "ka", 2)
+        weighted = in_source_order(exchange(weighted_all, "ka", 0, offset, half_waves), "ka", 2)
+        padded = padded_2(direct_modes, (("gx", 1),), 1)
+        field_f32 = direct_modes.astype(jnp.float32)
+        forward = padded[:, 2:].astype(jnp.float32)
+        behind = padded[:, :-2].astype(jnp.float32)
+        radial_pad = jnp.pad(field_f32, ((0, 0), (0, 0), (1, 1), (0, 0)))
+        outward = radial_pad[:, :, 2:]
+        inward = radial_pad[:, :, :-2]
+        wavenumber = (
+            first_wave + local_order[offset : offset + half_waves] - total_angles // 2
+        ).astype(jnp.float32) / total_angles
+        azimuthal = (wavenumber[:, None] / radius[None, :]) ** 2
+        image = (
+            -velocity * (forward - behind) * 0.5
+            + diffusion
+            * (
+                forward
+                + behind
+                + outward
+                + inward
+                - 4.0 * field_f32
+                - azimuthal[:, None, :, None] * field_f32
+            )
+        ).astype(jnp.bfloat16)
+        right_side = jnp.concatenate([direct_modes, image], axis=-1)
+        product = jnp.einsum(
+            "kpa,kpb->kab",
+            weighted.reshape(half_waves, -1, columns),
+            right_side.reshape(half_waves, -1, 2 * columns),
+            preferred_element_type=jnp.float32,
+        )
+        gram_terms = complex_blocks(product, snap_count).reshape(half_waves * snap_count, 2 * columns)
+        shares = gram_terms.astype(jnp.bfloat16).reshape(axial_count, half_rows, 2 * columns)
+        shares = lax.all_to_all(shares, "gx", split_axis=0, concat_axis=0, tiled=True)
+        own_parts.append(jnp.sum(shares.astype(jnp.float32), axis=0))
+    own_rows = jnp.concatenate(own_parts, axis=0)
     row_index = lax.axis_index("gx") * row_count + jnp.arange(row_count, dtype=jnp.int32)
     owner = row_index // snap_count
     selector = (owner[:, None] == jnp.arange(local_angles, dtype=jnp.int32)[None, :]).astype(
         jnp.float32
     )
-    shares = gram_terms.astype(jnp.bfloat16).reshape(lax.axis_size("gx"), row_count, 2 * columns)
-    shares = lax.all_to_all(shares, "gx", split_axis=0, concat_axis=0, tiled=True)
-    own_rows = jnp.sum(shares.astype(jnp.float32), axis=0)
     row_energy = jnp.sum(own_rows[:, :columns] ** 2, axis=1)
     energy = jnp.sum(gather_small(jnp.sum(selector * row_energy[:, None], axis=0), "gx"), axis=0)
     mean_sq = energy / (2.0 * snap_count * snap_count)

time: 161 us -> 172 us (1.068)
  starting transfers between devices: 25 us -> 41.8 us
  waiting for transfers between devices: 67.4 us -> 59 us
  other arithmetic: 15.3 us -> 18.1 us
    ppermute x12 -> x18, starting transfers between devices: 13.1 us -> 19.5 us  [exchange(): lax.ppermute(piece, axis, [(j, (j + shift) % count) for j in range(count)])]
    ppermute x1 -> x2, starting transfers between devices: 4.76 us -> 10.2 us  [padded_2(): lax.ppermute(tail, axis, [(i, (i + 1) % count) for i in range(ends)])]
    all_to_all x1 -> x2, waiting for transfers between devices: 26 us -> 21.4 us  [local(): lax.all_to_all(shares, 'gx', split_axis=0, concat_axis=0, tiled=True)]
    all_to_all x1 -> x2, starting transfers between devices: 5.78 us -> 9.43 us  [local(): lax.all_to_all(shares, 'gx', split_axis=0, concat_axis=0, tiled=True)]
    ppermute x12 -> x18, waiting for transfers between devices: 34.2 us -> 30.9 us  [exchange(): lax.ppermute(piece, axis, [(j, (j + shift) % count) for j in range(count)])]
    convert_element_type x1 -> x2, other arithmetic: 5.9 us -> 6.9 us  [local(): image = (-velocity * (forward - behind) * 0.5 + diffusion * (forward + be...]
    unnamed x18 -> x30, local copies, waits for them, and re-layouts: 16.6 us -> 15.7 us
    ppermute x1 -> x2, waiting for transfers between devices: 7.14 us -> 6.69 us  [padded_2(): lax.ppermute(tail, axis, [(i, (i + 1) % count) for i in range(ends)])]
  transfers between devices with their start and end apart: 15 -> 24, of which waited for: 9 -> 7; matrix products, arithmetic and copies ran while one was open for 17% -> 23% of each run, Pallas kernels for 9% -> 8%
where the time goes in v7:
time: 172 us; the launch traced here: 171 us
  waiting for transfers between devices  59 us (34%)
  starting transfers between devices  41.8 us (24%)
  local copies, waits for them, and re-layouts  25.6 us (15%)
  other arithmetic  18.1 us (11%)
  Pallas kernels  13.9 us (8%)
  blocking collectives  9.9 us (6%)
    ppermute x18, waiting for transfers between devices, exchange(): lax.ppermute(piece, axis, [(j, (j + shift) % count) for j in range(count)])  30.9 us
    all_to_all x2, waiting for transfers between devices, local(): lax.all_to_all(shares, 'gx', split_axis=0, concat_axis=0, tiled=True)  21.4 us
    ppermute x18, starting transfers between devices, exchange(): lax.ppermute(piece, axis, [(j, (j + shift) % count) for j in range(count)])  19.5 us
    unnamed x30, local copies, waits for them, and re-layouts  15.7 us
    pallas_call x2, Pallas kernels, dft(): pl.pallas_call(functools.partial(dft_kernel, count=count, weighted=weight...  13.9 us
    ppermute x2, starting transfers between devices, padded_2(): lax.ppermute(tail, axis, [(i, (i + 1) % count) for i in range(ends)])  10.2 us
    all_to_all x1, blocking collectives, gather_small(): return lax.all_to_all(copies, axis, split_axis=0, concat_axis=0, tiled=True)  9.9 us
    all_to_all x2, starting transfers between devices, local(): lax.all_to_all(shares, 'gx', split_axis=0, concat_axis=0, tiled=True)  9.43 us
  transfers between devices with their start and end apart: 24, of which 7 were waited for; matrix products, arithmetic and copies ran while one was open for 23% of the time, Pallas kernels for 8%

profile of v7, /device:TPU:0, one launch (start us, length us, event | category | flops | bytes accessed | tf_op | source)
XLA Modules:
  0.0 170.5 jit_solution(8133147338133551253)
XLA Ops:
  0.7 3.1 %constant_dynamic-slice_fusion.9 = (bf16[32,4,16,128]{3,2,1,0:T(8,128)(2,1)}, bf16[32,4,16,128]{3,2,1,0:T(8,128)(2,1)}, bf16[32,4,16,128]{3,2,1,0:T(8,128)(2,1)S(1)}, bf16[32,4,16,128]{3,2,1,0:T(8,128)(2,1)}) fusion(bf16[32,4,64,128]{3,2,1,0:T(8,128)(2,1)} %param.5, s32[]{:T(128)S(6)} %select_n.300, s32[]{:T(128)S(6)} %select_n.296, s32[]{:T(128)S(6)} %select_n.294, ...), kind=kLoop, calls=%fused_computation.155 | loop fusion | bytes 4194320 | tf_op jit(solution)/shard_map/dynamic_slice | solution.py:45
  3.8 2.4 %collective-permute-start.8 = (bf16[32,4,16,128]{3,2,1,0:T(8,128)(2,1)}, bf16[32,4,16,128]{3,2,1,0:T(8,128)(2,1)}, u32[]{:S(2)}, u32[]{:S(2)}) collective-permute-start(bf16[32,4,16,128]{3,2,1,0:T(8,128)(2,1)} %get-tuple-element.27), channel_id=1, source_target_pairs={{0,3},{1,0},{2,1},{3,2},{4,7},{5,4},{6,5},{7,6},{8,11},{9,8},{10,9... | collective-permute-start | bytes 1572872 | tf_op jit(solution)/shard_map/ppermute | solution.py:47
  7.0 1.5 constant_dynamic-slice_fusion.17
  8.5 1.5 collective-permute-start.2
  10.0 1.5 collective-permute-start.1
  13.3 5.4 %collective-permute-done.8 = bf16[32,4,16,128]{3,2,1,0:T(8,128)(2,1)} collective-permute-done((bf16[32,4,16,128]{3,2,1,0:T(8,128)(2,1)}, bf16[32,4,16,128]{3,2,1,0:T(8,128)(2,1)}, u32[]{:S(2)}, u32[]{:S(2)}) %collective-permute-start.8) | collective-permute-done | bytes 524320 | tf_op jit(solution)/shard_map/ppermute | solution.py:47
  18.8 1.1 collective-permute-start
  20.0 1.1 copy.45
  21.1 0.8 concatenate.46.refs_0_
  21.9 2.2 %copy.42 = bf16[4,8,64,128]{3,1,2,0:T(8,128)(2,1)} copy(bf16[4,8,64,128]{3,2,1,0:T(8,128)(2,1)} %bitcast.65) | data formatting | bytes 1048576
  24.1 6.9 %collective-permute-done.7 = bf16[32,4,16,128]{3,2,1,0:T(8,128)(2,1)S(1)} collective-permute-done((bf16[32,4,16,128]{3,2,1,0:T(8,128)(2,1)}, bf16[32,4,16,128]{3,2,1,0:T(8,128)(2,1)S(1)}, u32[]{:S(2)}, u32[]{:S(2)}) %collective-permute-start.7) | collective-permute-done | bytes 524320 | tf_op jit(solution)/shard_map/ppermute | solution.py:47
  31.0 1.1 copy.43
  32.1 1.2 copy.44
  33.3 6.9 %shard_map.77 = bf16[128,8192]{1,0:T(8,128)(2,1)} custom-call(bf16[128,256]{1,0:T(8,128)(2,1)} %concatenate.46.refs_0_, bf16[32,8192]{1,0:T(8,128)(2,1)} %bitcast.121, bf16[32,8192]{1,0:T(8,128)(2,1)} %bitcast.128, bf16[32,8192]{1,0:T(8,128)(2,1)} %bitcast.126, bf16[32,8192]{1,0:T(8,128)(2,1)} %bitcast.124), custom_call_target="tpu_custom_call" | custom-call | tf_op jit(solution)/shard_map/pallas_call | solution.py:108
  40.2 2.2 %copy.33 = bf16[16,8,64,128]{3,2,1,0:T(8,128)(2,1)S(1)} copy(bf16[16,8,64,128]{3,1,2,0:T(8,128)(2,1)} %bitcast.115) | data formatting | bytes 4194304
  42.4 1.1 dynamic-slice_bitcast_fusion.14
  43.6 1.4 collective-permute-start.10
  45.0 1.4 collective-permute-start.11
  46.4 1.1 copy.49
  47.6 1.1 copy.46
  48.8 4.7 %collective-permute-done.1 = bf16[32,4,16,128]{3,2,1,0:T(8,128)(2,1)S(1)} collective-permute-done((bf16[32,4,16,128]{3,2,1,0:T(8,128)(2,1)}, bf16[32,4,16,128]{3,2,1,0:T(8,128)(2,1)S(1)}, u32[]{:S(2)}, u32[]{:S(2)}) %collective-permute-start.1) | collective-permute-done | bytes 524320 | tf_op jit(solution)/shard_map/ppermute | solution.py:47
  53.5 1.1 copy.47
  54.6 2.2 %copy.48 = bf16[4,8,64,128]{3,1,2,0:T(8,128)(2,1)} copy(bf16[4,8,64,128]{3,2,1,0:T(8,128)(2,1)} %bitcast.44) | data formatting | bytes 1048576
  57.5 7.0 %shard_map.76 = bf16[128,8192]{1,0:T(8,128)(2,1)} custom-call(bf16[128,256]{1,0:T(8,128)(2,1)} %concatenate.46.refs_0_, bf16[32,8192]{1,0:T(8,128)(2,1)} %bitcast.122, bf16[32,8192]{1,0:T(8,128)(2,1)} %bitcast.127, bf16[32,8192]{1,0:T(8,128)(2,1)} %bitcast.125, bf16[32,8192]{1,0:T(8,128)(2,1)} %bitcast.123, f32[1,8192]{1,0:T(1,128)} %bitcast.142), custom_call_target="tpu_custom_call" | custom-call | tf_op jit(solution)/shard_map/pallas_call | solution.py:108
  64.5 2.2 %copy.28 = bf16[16,8,64,128]{3,2,1,0:T(8,128)(2,1)S(1)} copy(bf16[16,8,64,128]{3,1,2,0:T(8,128)(2,1)} %bitcast.112) | data formatting | bytes 4194304
  67.2 1.4 collective-permute-start.4
  69.1 1.4 collective-permute-start.18
  70.8 1.2 pad_maximum_fusion.20
  72.7 13.8 %collective-permute-done.17 = bf16[16,4,16,128]{3,2,1,0:T(8,128)(2,1)S(1)} collective-permute-done((bf16[16,4,16,128]{3,2,1,0:T(8,128)(2,1)S(1)}, bf16[16,4,16,128]{3,2,1,0:T(8,128)(2,1)S(1)}, u32[]{:S(2)}, u32[]{:S(2)}) %collective-permute-start.17) | collective-permute-done | bytes 262176 | tf_op jit(solution)/shard_map/ppermute | solution.py:47
  86.4 3.7 %collective-permute-start.14 = (bf16[16,4,16,128]{3,2,1,0:T(8,128)(2,1)S(1)}, bf16[16,4,16,128]{3,2,1,0:T(8,128)(2,1)S(1)}, u32[]{:S(2)}, u32[]{:S(2)}) collective-permute-start(bf16[16,4,16,128]{3,2,1,0:T(8,128)(2,1)S(1)} %get-tuple-element.18), channel_id=1, source_target_pairs={{0,1},{1,2},{2,3},{3,0},{4,5},{5,6},{6,7},{7,4},{8,9},{9,10},{10,1... | collective-permute-start | bytes 786440 | tf_op jit(solution)/shard_map/ppermute | solution.py:47
  90.1 2.1 %collective-permute-start.15 = (bf16[16,4,16,128]{3,2,1,0:T(8,128)(2,1)S(1)}, bf16[16,4,16,128]{3,2,1,0:T(8,128)(2,1)S(1)}, u32[]{:S(2)}, u32[]{:S(2)}) collective-permute-start(bf16[16,4,16,128]{3,2,1,0:T(8,128)(2,1)S(1)} %get-tuple-element.17), channel_id=1, source_target_pairs={{0,2},{1,3},{2,0},{3,1},{4,6},{5,7},{6,4},{7,5},{8,10},{9,11},{10,... | collective-permute-start | bytes 786440 | tf_op jit(solution)/shard_map/ppermute | solution.py:47
  92.7 1.3 collective-permute-start.12
  94.0 4.6 %collective-permute-start.13 = (bf16[16,1,64,128]{3,2,1,0:T(8,128)(2,1)S(1)}, bf16[16,1,64,128]{3,2,1,0:T(8,128)(2,1)S(1)}, u32[]{:S(2)}, u32[]{:S(2)}) collective-permute-start(bf16[16,1,64,128]{3,2,1,0:T(8,128)(2,1)S(1)} %get-tuple-element.36), channel_id=1, source_target_pairs={{0,4},{4,8},{8,12},{12,16},{16,20},{20,24},{24,28},{1,5},{5,9},{9,... | collective-permute-start | bytes 786440 | tf_op jit(solution)/shard_map/ppermute | solution.py:22
  99.4 0.8 fusion.42
  100.2 1.3 collective-permute-start.20
  101.5 5.7 %collective-permute-start.21 = (bf16[16,1,64,128]{3,2,1,0:T(8,128)(2,1)}, bf16[16,1,64,128]{3,2,1,0:T(8,128)(2,1)}, u32[]{:S(2)}, u32[]{:S(2)}) collective-permute-start(bf16[16,1,64,128]{3,2,1,0:T(8,128)(2,1)} %get-tuple-element.48), channel_id=1, source_target_pairs={{0,4},{4,8},{8,12},{12,16},{16,20},{20,24},{24,28},{1,5},{5,9},{9,... | collective-permute-start | bytes 786440 | tf_op jit(solution)/shard_map/ppermute | solution.py:22
  107.9 6.7 %collective-permute-done.13 = bf16[16,1,64,128]{3,2,1,0:T(8,128)(2,1)S(1)} collective-permute-done((bf16[16,1,64,128]{3,2,1,0:T(8,128)(2,1)S(1)}, bf16[16,1,64,128]{3,2,1,0:T(8,128)(2,1)S(1)}, u32[]{:S(2)}, u32[]{:S(2)}) %collective-permute-start.13) | collective-permute-done | bytes 262176 | tf_op jit(solution)/shard_map/ppermute | solution.py:22
  114.5 2.8 %fusion.6 = bf16[16,4,64,128]{3,2,1,0:T(8,128)(2,1)S(1)} fusion(f32[16,4,64,128]{3,2,1,0:T(8,128)S(1)} %get-tuple-element.38, bf16[16,1,64,128]{3,2,1,0:T(8,128)(2,1)S(1)} %collective-permute-done.13, bf16[16,4,16,128]{3,2,1,0:T(8,128)(2,1)S(1)} %get-tuple-element.40, bf16[16,4,16,128]{3,2,1,0:T(8,128)(2,1)S(1)} %get-tuple-element.41, ...), kind=kLoop, calls=%fused_computation.14 | loop fusion | flops 17301504 | bytes 4724736 | tf_op jit(solution)/shard_map/convert_element_type | solution.py:234
  118.8 1.2 pad_maximum_fusion.26
  120.0 5.8 %all-to-all-start = ((bf16[8,128,256]{2,1,0:T(8,128)(2,1)}), bf16[8,128,256]{2,1,0:T(8,128)(2,1)}, u32[]{:S(2)}, u32[]{:S(2)}) async-start(bf16[8,128,256]{2,1,0:T(8,128)(2,1)} %bitcast.118), calls=%async_computation | async-start | bytes 1048576 | tf_op jit(solution)/shard_map/all_to_all | solution.py:244
  125.9 4.1 %fusion.13 = bf16[16,4,64,128]{3,2,1,0:T(8,128)(2,1)S(1)} fusion(f32[16,4,64,128]{3,2,1,0:T(8,128)S(1)} %get-tuple-element.50, bf16[16,1,64,128]{3,2,1,0:T(8,128)(2,1)} %collective-permute-done.21, bf16[16,4,16,128]{3,2,1,0:T(8,128)(2,1)} %copy-done, bf16[16,4,16,128]{3,2,1,0:T(8,128)(2,1)} %copy-done.2, bf16[16,4,16,128]{3,2,1,0:T(8,128)(2,1)} %copy-done.4, ...), kind=kLoop, calls=%fused_computation.21 | loop fusion | flops 17301504 | bytes 4724736 | tf_op jit(solution)/shard_map/convert_element_type | solution.py:234
  131.5 1.2 pad_maximum_fusion.27
  132.6 7.9 %all-to-all-done = bf16[8,128,256]{2,1,0:T(8,128)(2,1)} async-done(((bf16[8,128,256]{2,1,0:T(8,128)(2,1)}), bf16[8,128,256]{2,1,0:T(8,128)(2,1)}, u32[]{:S(2)}, u32[]{:S(2)}) %all-to-all-start) | async-done | bytes 524320 | tf_op jit(solution)/shard_map/all_to_all | solution.py:244
  140.6 3.6 %all-to-all-start.1 = ((bf16[8,128,256]{2,1,0:T(8,128)(2,1)}), bf16[8,128,256]{2,1,0:T(8,128)(2,1)S(1)}, u32[]{:S(2)}, u32[]{:S(2)}) async-start(bf16[8,128,256]{2,1,0:T(8,128)(2,1)} %bitcast.38), calls=%async_computation.1 | async-start | bytes 1048576 | tf_op jit(solution)/shard_map/all_to_all | solution.py:244
  144.2 1.1 convert_reduce_fusion.1
  145.3 13.5 %all-to-all-done.1 = bf16[8,128,256]{2,1,0:T(8,128)(2,1)S(1)} async-done(((bf16[8,128,256]{2,1,0:T(8,128)(2,1)}), bf16[8,128,256]{2,1,0:T(8,128)(2,1)S(1)}, u32[]{:S(2)}, u32[]{:S(2)}) %all-to-all-start.1) | async-done | bytes 524320 | tf_op jit(solution)/shard_map/all_to_all | solution.py:244
  159.2 9.9 %all_to_all.16 = f32[8,1,32]{2,1,0:T(1,128)S(1)} all-to-all(f32[8,1,32]{2,1,0:T(1,128)S(1)} %broadcast_in_dim.5), channel_id=1, replica_groups=mesh['gx'=8,'ka'=4] {'gx'}, dimensions={0} | all-to-all | bytes 2048 | tf_op jit(solution)/shard_map/all_to_all | solution.py:34
  169.7 0.8 fusion.27
  (94 shorter events, 11.0 us)
Async XLA Ops:
  0.7 6.3 %copy-start.6 = (bf16[32,4,64,128]{3,2,1,0:T(8,128)(2,1)S(1)}, bf16[32,4,64,128]{3,2,1,0:T(8,128)(2,1)}, u32[]{:S(2)}) copy-start(bf16[32,4,64,128]{3,2,1,0:T(8,128)(2,1)} %param.6) | copy-start | bytes 6291460
  3.8 14.9 %collective-permute-start.8 = (bf16[32,4,16,128]{3,2,1,0:T(8,128)(2,1)}, bf16[32,4,16,128]{3,2,1,0:T(8,128)(2,1)}, u32[]{:S(2)}, u32[]{:S(2)}) collective-permute-start(bf16[32,4,16,128]{3,2,1,0:T(8,128)(2,1)} %get-tuple-element.27), channel_id=1, source_target_pairs={{0,3},{1,0},{2,1},{3,2},{4,7},{5,4},{6,5},{7,6},{8,11},{9,8},{10,9... | collective-permute-start | bytes 1572872 | tf_op jit(solution)/shard_map/ppermute | solution.py:47
  6.2 24.8 %collective-permute-start.7 = (bf16[32,4,16,128]{3,2,1,0:T(8,128)(2,1)}, bf16[32,4,16,128]{3,2,1,0:T(8,128)(2,1)S(1)}, u32[]{:S(2)}, u32[]{:S(2)}) collective-permute-start(bf16[32,4,16,128]{3,2,1,0:T(8,128)(2,1)} %get-tuple-element.30), channel_id=1, source_target_pairs={{0,2},{1,3},{2,0},{3,1},{4,6},{5,7},{6,4},{7,5},{8,10},{9,11},{10,... | collective-permute-start | bytes 1572872 | tf_op jit(solution)/shard_map/ppermute | solution.py:47
  6.8 25.3 %collective-permute-start.6 = (bf16[32,4,16,128]{3,2,1,0:T(8,128)(2,1)}, bf16[32,4,16,128]{3,2,1,0:T(8,128)(2,1)S(1)}, u32[]{:S(2)}, u32[]{:S(2)}) collective-permute-start(bf16[32,4,16,128]{3,2,1,0:T(8,128)(2,1)} %get-tuple-element.28), channel_id=1, source_target_pairs={{0,1},{1,2},{2,3},{3,0},{4,5},{5,6},{6,7},{7,4},{8,9},{9,10},{10,1... | collective-permute-start | bytes 1572872 | tf_op jit(solution)/shard_map/ppermute | solution.py:47
  8.5 36.5 %collective-permute-start.2 = (bf16[32,4,16,128]{3,2,1,0:T(8,128)(2,1)}, bf16[32,4,16,128]{3,2,1,0:T(8,128)(2,1)S(1)}, u32[]{:S(2)}, u32[]{:S(2)}) collective-permute-start(bf16[32,4,16,128]{3,2,1,0:T(8,128)(2,1)} %get-tuple-element.31), channel_id=1, source_target_pairs={{0,3},{1,0},{2,1},{3,2},{4,7},{5,4},{6,5},{7,6},{8,11},{9,8},{10,9... | collective-permute-start | bytes 1572872 | tf_op jit(solution)/shard_map/ppermute | solution.py:47
  10.0 43.5 %collective-permute-start.1 = (bf16[32,4,16,128]{3,2,1,0:T(8,128)(2,1)}, bf16[32,4,16,128]{3,2,1,0:T(8,128)(2,1)S(1)}, u32[]{:S(2)}, u32[]{:S(2)}) collective-permute-start(bf16[32,4,16,128]{3,2,1,0:T(8,128)(2,1)} %get-tuple-element.34), channel_id=1, source_target_pairs={{0,2},{1,3},{2,0},{3,1},{4,6},{5,7},{6,4},{7,5},{8,10},{9,11},{10,... | collective-permute-start | bytes 1572872 | tf_op jit(solution)/shard_map/ppermute | solution.py:47
  18.8 35.9 %collective-permute-start = (bf16[32,4,16,128]{3,2,1,0:T(8,128)(2,1)}, bf16[32,4,16,128]{3,2,1,0:T(8,128)(2,1)}, u32[]{:S(2)}, u32[]{:S(2)}) collective-permute-start(bf16[32,4,16,128]{3,2,1,0:T(8,128)(2,1)} %get-tuple-element.32), channel_id=1, source_target_pairs={{0,1},{1,2},{2,3},{3,0},{4,5},{5,6},{6,7},{7,4},{8,9},{9,10},{10,1... | collective-permute-start | bytes 1572872 | tf_op jit(solution)/shard_map/ppermute | solution.py:47
  42.4 4.0 %copy-start.8 = (f32[4,64]{1,0:T(4,128)S(1)}, f32[4,64]{1,0:T(4,128)}, u32[]{:S(2)}) copy-start(f32[4,64]{1,0:T(4,128)} %param.7) | copy-start | bytes 3076
  42.4 4.0 %copy-start.9 = (f32[4,64]{1,0:T(4,128)S(1)}, f32[4,64]{1,0:T(4,128)}, u32[]{:S(2)}) copy-start(f32[4,64]{1,0:T(4,128)} %param.8) | copy-start | bytes 3076
  43.6 25.1 %collective-permute-start.9 = (bf16[16,4,16,128]{3,2,1,0:T(8,128)(2,1)}, bf16[16,4,16,128]{3,2,1,0:T(8,128)(2,1)}, u32[]{:S(2)}, u32[]{:S(2)}) collective-permute-start(bf16[16,4,16,128]{3,2,1,0:T(8,128)(2,1)} %get-tuple-element.14), channel_id=1, source_target_pairs={{0,1},{1,2},{2,3},{3,0},{4,5},{5,6},{6,7},{7,4},{8,9},{9,10},{10,1... | collective-permute-start | bytes 786440 | tf_op jit(solution)/shard_map/ppermute | solution.py:47
  43.6 25.5 %collective-permute-start.10 = (bf16[16,4,16,128]{3,2,1,0:T(8,128)(2,1)S(1)}, bf16[16,4,16,128]{3,2,1,0:T(8,128)(2,1)}, u32[]{:S(2)}, u32[]{:S(2)}) collective-permute-start(bf16[16,4,16,128]{3,2,1,0:T(8,128)(2,1)S(1)} %get-tuple-element.13), channel_id=1, source_target_pairs={{0,2},{1,3},{2,0},{3,1},{4,6},{5,7},{6,4},{7,5},{8,10},{9,11},{10,... | collective-permute-start | bytes 786440 | tf_op jit(solution)/shard_map/ppermute | solution.py:47
  45.0 25.5 %collective-permute-start.11 = (bf16[16,4,16,128]{3,2,1,0:T(8,128)(2,1)S(1)}, bf16[16,4,16,128]{3,2,1,0:T(8,128)(2,1)}, u32[]{:S(2)}, u32[]{:S(2)}) collective-permute-start(bf16[16,4,16,128]{3,2,1,0:T(8,128)(2,1)S(1)} %get-tuple-element.12), channel_id=1, source_target_pairs={{0,3},{1,0},{2,1},{3,2},{4,7},{5,4},{6,5},{7,6},{8,11},{9,8},{10,9... | collective-permute-start | bytes 786440 | tf_op jit(solution)/shard_map/ppermute | solution.py:47
  67.2 25.5 %collective-permute-start.3 = (bf16[16,4,16,128]{3,2,1,0:T(8,128)(2,1)S(1)}, bf16[16,4,16,128]{3,2,1,0:T(8,128)(2,1)S(1)}, u32[]{:S(2)}, u32[]{:S(2)}) collective-permute-start(bf16[16,4,16,128]{3,2,1,0:T(8,128)(2,1)S(1)} %get-tuple-element.22), channel_id=1, source_target_pairs={{0,1},{1,2},{2,3},{3,0},{4,5},{5,6},{6,7},{7,4},{8,9},{9,10},{10,1... | collective-permute-start | bytes 786440 | tf_op jit(solution)/shard_map/ppermute | solution.py:47
  67.2 25.5 %collective-permute-start.4 = (bf16[16,4,16,128]{3,2,1,0:T(8,128)(2,1)S(1)}, bf16[16,4,16,128]{3,2,1,0:T(8,128)(2,1)S(1)}, u32[]{:S(2)}, u32[]{:S(2)}) collective-permute-start(bf16[16,4,16,128]{3,2,1,0:T(8,128)(2,1)S(1)} %get-tuple-element.21), channel_id=1, source_target_pairs={{0,2},{1,3},{2,0},{3,1},{4,6},{5,7},{6,4},{7,5},{8,10},{9,11},{10,... | collective-permute-start | bytes 786440 | tf_op jit(solution)/shard_map/ppermute | solution.py:47
  68.7 17.8 %collective-permute-start.17 = (bf16[16,4,16,128]{3,2,1,0:T(8,128)(2,1)S(1)}, bf16[16,4,16,128]{3,2,1,0:T(8,128)(2,1)S(1)}, u32[]{:S(2)}, u32[]{:S(2)}) collective-permute-start(bf16[16,4,16,128]{3,2,1,0:T(8,128)(2,1)S(1)} %get-tuple-element.10), channel_id=1, source_target_pairs={{0,1},{1,2},{2,3},{3,0},{4,5},{5,6},{6,7},{7,4},{8,9},{9,10},{10,1... | collective-permute-start | bytes 786440 | tf_op jit(solution)/shard_map/ppermute | solution.py:47
  69.1 17.4 %collective-permute-start.18 = (bf16[16,4,16,128]{3,2,1,0:T(8,128)(2,1)S(1)}, bf16[16,4,16,128]{3,2,1,0:T(8,128)(2,1)S(1)}, u32[]{:S(2)}, u32[]{:S(2)}) collective-permute-start(bf16[16,4,16,128]{3,2,1,0:T(8,128)(2,1)S(1)} %get-tuple-element.9), channel_id=1, source_target_pairs={{0,2},{1,3},{2,0},{3,1},{4,6},{5,7},{6,4},{7,5},{8,10},{9,11},{10,... | collective-permute-start | bytes 786440 | tf_op jit(solution)/shard_map/ppermute | solution.py:47
  70.5 19.7 %collective-permute-start.19 = (bf16[16,4,16,128]{3,2,1,0:T(8,128)(2,1)S(1)}, bf16[16,4,16,128]{3,2,1,0:T(8,128)(2,1)S(1)}, u32[]{:S(2)}, u32[]{:S(2)}) collective-permute-start(bf16[16,4,16,128]{3,2,1,0:T(8,128)(2,1)S(1)} %get-tuple-element.8), channel_id=1, source_target_pairs={{0,3},{1,0},{2,1},{3,2},{4,7},{5,4},{6,5},{7,6},{8,11},{9,8},{10,9... | collective-permute-start | bytes 786440 | tf_op jit(solution)/shard_map/ppermute | solution.py:47
  86.4 7.6 %collective-permute-start.5 = (bf16[16,4,16,128]{3,2,1,0:T(8,128)(2,1)S(1)}, bf16[16,4,16,128]{3,2,1,0:T(8,128)(2,1)S(1)}, u32[]{:S(2)}, u32[]{:S(2)}) collective-permute-start(bf16[16,4,16,128]{3,2,1,0:T(8,128)(2,1)S(1)} %get-tuple-element.20), channel_id=1, source_target_pairs={{0,3},{1,0},{2,1},{3,2},{4,7},{5,4},{6,5},{7,6},{8,11},{9,8},{10,9... | collective-permute-start | bytes 786440 | tf_op jit(solution)/shard_map/ppermute | solution.py:47
  86.4 13.8 %collective-permute-start.14 = (bf16[16,4,16,128]{3,2,1,0:T(8,128)(2,1)S(1)}, bf16[16,4,16,128]{3,2,1,0:T(8,128)(2,1)S(1)}, u32[]{:S(2)}, u32[]{:S(2)}) collective-permute-start(bf16[16,4,16,128]{3,2,1,0:T(8,128)(2,1)S(1)} %get-tuple-element.18), channel_id=1, source_target_pairs={{0,1},{1,2},{2,3},{3,0},{4,5},{5,6},{6,7},{7,4},{8,9},{9,10},{10,1... | collective-permute-start | bytes 786440 | tf_op jit(solution)/shard_map/ppermute | solution.py:47
  90.1 11.4 %collective-permute-start.15 = (bf16[16,4,16,128]{3,2,1,0:T(8,128)(2,1)S(1)}, bf16[16,4,16,128]{3,2,1,0:T(8,128)(2,1)S(1)}, u32[]{:S(2)}, u32[]{:S(2)}) collective-permute-start(bf16[16,4,16,128]{3,2,1,0:T(8,128)(2,1)S(1)} %get-tuple-element.17), channel_id=1, source_target_pairs={{0,2},{1,3},{2,0},{3,1},{4,6},{5,7},{6,4},{7,5},{8,10},{9,11},{10,... | collective-permute-start | bytes 786440 | tf_op jit(solution)/shard_map/ppermute | solution.py:47
  92.5 6.6 %copy-start = (bf16[16,4,16,128]{3,2,1,0:T(8,128)(2,1)}, bf16[16,4,16,128]{3,2,1,0:T(8,128)(2,1)S(1)}, u32[]{:S(2)}) copy-start(bf16[16,4,16,128]{3,2,1,0:T(8,128)(2,1)S(1)} %get-tuple-element.52) | copy-start | bytes 786436
  92.5 6.6 %copy-start.2 = (bf16[16,4,16,128]{3,2,1,0:T(8,128)(2,1)}, bf16[16,4,16,128]{3,2,1,0:T(8,128)(2,1)S(1)}, u32[]{:S(2)}) copy-start(bf16[16,4,16,128]{3,2,1,0:T(8,128)(2,1)S(1)} %get-tuple-element.53) | copy-start | bytes 786436
  92.6 6.6 %copy-start.4 = (bf16[16,4,16,128]{3,2,1,0:T(8,128)(2,1)}, bf16[16,4,16,128]{3,2,1,0:T(8,128)(2,1)S(1)}, u32[]{:S(2)}) copy-start(bf16[16,4,16,128]{3,2,1,0:T(8,128)(2,1)S(1)} %get-tuple-element.54) | copy-start | bytes 786436
  92.6 14.6 %collective-permute-start.16 = (bf16[16,4,16,128]{3,2,1,0:T(8,128)(2,1)S(1)}, bf16[16,4,16,128]{3,2,1,0:T(8,128)(2,1)S(1)}, u32[]{:S(2)}, u32[]{:S(2)}) collective-permute-start(bf16[16,4,16,128]{3,2,1,0:T(8,128)(2,1)S(1)} %get-tuple-element.16), channel_id=1, source_target_pairs={{0,3},{1,0},{2,1},{3,2},{4,7},{5,4},{6,5},{7,6},{8,11},{9,8},{10,9... | collective-permute-start | bytes 786440 | tf_op jit(solution)/shard_map/ppermute | solution.py:47
  92.7 15.1 %collective-permute-start.12 = (bf16[16,1,64,128]{3,2,1,0:T(8,128)(2,1)S(1)}, bf16[16,1,64,128]{3,2,1,0:T(8,128)(2,1)S(1)}, u32[]{:S(2)}, u32[]{:S(2)}) collective-permute-start(bf16[16,1,64,128]{3,2,1,0:T(8,128)(2,1)S(1)} %get-tuple-element.35), channel_id=1, source_target_pairs={{4,0},{8,4},{12,8},{16,12},{20,16},{24,20},{28,24},{5,1},{9,5},{13... | collective-permute-start | bytes 786440 | tf_op jit(solution)/shard_map/ppermute | solution.py:24
  94.0 20.5 %collective-permute-start.13 = (bf16[16,1,64,128]{3,2,1,0:T(8,128)(2,1)S(1)}, bf16[16,1,64,128]{3,2,1,0:T(8,128)(2,1)S(1)}, u32[]{:S(2)}, u32[]{:S(2)}) collective-permute-start(bf16[16,1,64,128]{3,2,1,0:T(8,128)(2,1)S(1)} %get-tuple-element.36), channel_id=1, source_target_pairs={{0,4},{4,8},{8,12},{12,16},{16,20},{20,24},{24,28},{1,5},{5,9},{9,... | collective-permute-start | bytes 786440 | tf_op jit(solution)/shard_map/ppermute | solution.py:22
  100.2 25.6 %collective-permute-start.20 = (bf16[16,1,64,128]{3,2,1,0:T(8,128)(2,1)}, bf16[16,1,64,128]{3,2,1,0:T(8,128)(2,1)}, u32[]{:S(2)}, u32[]{:S(2)}) collective-permute-start(bf16[16,1,64,128]{3,2,1,0:T(8,128)(2,1)} %get-tuple-element.47), channel_id=1, source_target_pairs={{4,0},{8,4},{12,8},{16,12},{20,16},{24,20},{28,24},{5,1},{9,5},{13... | collective-permute-start | bytes 786440 | tf_op jit(solution)/shard_map/ppermute | solution.py:24
  101.5 24.3 %collective-permute-start.21 = (bf16[16,1,64,128]{3,2,1,0:T(8,128)(2,1)}, bf16[16,1,64,128]{3,2,1,0:T(8,128)(2,1)}, u32[]{:S(2)}, u32[]{:S(2)}) collective-permute-start(bf16[16,1,64,128]{3,2,1,0:T(8,128)(2,1)} %get-tuple-element.48), channel_id=1, source_target_pairs={{0,4},{4,8},{8,12},{12,16},{16,20},{20,24},{24,28},{1,5},{5,9},{9,... | collective-permute-start | bytes 786440 | tf_op jit(solution)/shard_map/ppermute | solution.py:22
  107.5 7.0 %copy-start.7 = (f32[4,64]{1,0:T(4,128)S(1)}, f32[4,64]{1,0:T(4,128)}, u32[]{:S(2)}) copy-start(f32[4,64]{1,0:T(4,128)} %param.9) | copy-start | bytes 3076
  120.0 20.5 %all-to-all-start = ((bf16[8,128,256]{2,1,0:T(8,128)(2,1)}), bf16[8,128,256]{2,1,0:T(8,128)(2,1)}, u32[]{:S(2)}, u32[]{:S(2)}) async-start(bf16[8,128,256]{2,1,0:T(8,128)(2,1)} %bitcast.118), calls=%async_computation | async-start | bytes 1048576 | tf_op jit(solution)/shard_map/all_to_all | solution.py:244
  125.8 4.1 %copy-start.1 = (bf16[16,4,16,128]{3,2,1,0:T(8,128)(2,1)S(1)}, bf16[16,4,16,128]{3,2,1,0:T(8,128)(2,1)}, u32[]{:S(2)}) copy-start(bf16[16,4,16,128]{3,2,1,0:T(8,128)(2,1)} %copy-done) | copy-start | bytes 786436
  125.9 4.1 %copy-start.3 = (bf16[16,4,16,128]{3,2,1,0:T(8,128)(2,1)S(1)}, bf16[16,4,16,128]{3,2,1,0:T(8,128)(2,1)}, u32[]{:S(2)}) copy-start(bf16[16,4,16,128]{3,2,1,0:T(8,128)(2,1)} %copy-done.2) | copy-start | bytes 786436
  125.9 4.1 %copy-start.5 = (bf16[16,4,16,128]{3,2,1,0:T(8,128)(2,1)S(1)}, bf16[16,4,16,128]{3,2,1,0:T(8,128)(2,1)}, u32[]{:S(2)}) copy-start(bf16[16,4,16,128]{3,2,1,0:T(8,128)(2,1)} %copy-done.4) | copy-start | bytes 786436
  140.6 18.3 %all-to-all-start.1 = ((bf16[8,128,256]{2,1,0:T(8,128)(2,1)}), bf16[8,128,256]{2,1,0:T(8,128)(2,1)S(1)}, u32[]{:S(2)}, u32[]{:S(2)}) async-start(bf16[8,128,256]{2,1,0:T(8,128)(2,1)} %bitcast.38), calls=%async_computation.1 | async-start | bytes 1048576 | tf_op jit(solution)/shard_map/all_to_all | solution.py:244

commit v8 on v6

--- a/solution.py
+++ b/solution.py
@@ -78,9 +78,12 @@
     width = piece_refs[0].shape[1]
     lane = lax.broadcasted_iota(jnp.int32, (1, width), 1) % 128
     low = lane < 64
+    packed = piece_refs[0].shape[0] % 16 == 0
     rows = []
     for piece_ref in piece_refs:
-        x = piece_ref[...].astype(jnp.float32)
+        x = piece_ref[...]
+        if not packed:
+            x = x.astype(jnp.float32)
         swapped = jnp.where(low, pltpu.roll(x, width - 64, 1), -pltpu.roll(x, 64, 1))
         rows.append(x)
         rows.append(swapped)
@@ -95,7 +98,7 @@
     count = len(pieces)
     angles, total = pieces[0].shape
     waves = table.shape[0]
-    block = math.gcd(total, 1024)
+    block = math.gcd(total, 4096)
     grid = (total // block,)
     in_specs = [pl.BlockSpec((waves, table.shape[1]), lambda j: (0, 0))]
     in_specs += [pl.BlockSpec((angles, block), lambda j: (0, j)) for _ in pieces]

time: 161 us -> 160 us (level)
  waiting for transfers between devices: 67.4 us -> 74.5 us
  Pallas kernels: 14.1 us -> 7.09 us
    ppermute x12, waiting for transfers between devices: 34.2 us -> 41.4 us  [exchange(): lax.ppermute(piece, axis, [(j, (j + shift) % count) for j in range(count)])]
    pallas_call x2, Pallas kernels: 14.1 us -> 7.09 us  [dft(): pl.pallas_call(functools.partial(dft_kernel, count=count, weighted=weight...]
  transfers between devices with their start and end apart: 15 -> 15, of which waited for: 9 -> 10; matrix products, arithmetic and copies ran while one was open for 17% -> 17% of each run, Pallas kernels for 9% -> 4%
where the time goes in v8:
time: 160 us; the launch traced here: 159 us
  waiting for transfers between devices  74.5 us (47%)
  local copies, waits for them, and re-layouts  25.9 us (16%)
  starting transfers between devices  24.8 us (16%)
  other arithmetic  15.3 us (10%)
  blocking collectives  9.9 us (6%)
  Pallas kernels  7.09 us (4%)
    ppermute x12, waiting for transfers between devices, exchange(): lax.ppermute(piece, axis, [(j, (j + shift) % count) for j in range(count)])  41.4 us
    all_to_all x1, waiting for transfers between devices, local(): lax.all_to_all(shares, 'gx', split_axis=0, concat_axis=0, tiled=True)  26 us
    unnamed x18, local copies, waits for them, and re-layouts  16.6 us
    ppermute x12, starting transfers between devices, exchange(): lax.ppermute(piece, axis, [(j, (j + shift) % count) for j in range(count)])  13 us
    all_to_all x1, blocking collectives, gather_small(): return lax.all_to_all(copies, axis, split_axis=0, concat_axis=0, tiled=True)  9.9 us
    ppermute x1, waiting for transfers between devices, padded_2(): lax.ppermute(tail, axis, [(i, (i + 1) % count) for i in range(ends)])  7.14 us
    pallas_call x2, Pallas kernels, dft(): pl.pallas_call(functools.partial(dft_kernel, count=count, weighted=weight...  7.09 us
    convert_element_type x1, other arithmetic, local(): image = (-velocity * (forward - behind) * 0.5 + diffusion * (forward + be...  5.9 us
  transfers between devices with their start and end apart: 15, of which 10 were waited for; matrix products, arithmetic and copies ran while one was open for 17% of the time, Pallas kernels for 4%

profile of v8, /device:TPU:0, one launch (start us, length us, event | category | flops | bytes accessed | tf_op | source)
XLA Modules:
  0.0 159.4 jit_solution(7102583150445460164)
XLA Ops:
  0.7 3.1 %constant_dynamic-slice_fusion.3 = (bf16[32,4,16,128]{3,2,1,0:T(8,128)(2,1)}, bf16[32,4,16,128]{3,2,1,0:T(8,128)(2,1)}, bf16[32,4,16,128]{3,2,1,0:T(8,128)(2,1)S(1)}, bf16[32,4,16,128]{3,2,1,0:T(8,128)(2,1)}) fusion(bf16[32,4,64,128]{3,2,1,0:T(8,128)(2,1)} %param.5, s32[]{:T(128)S(6)} %select_n.166, s32[]{:T(128)S(6)} %select_n.162, s32[]{:T(128)S(6)} %select_n.160, ...), kind=kLoop, calls=%fused_computation.100 | loop fusion | bytes 4194320 | tf_op jit(solution)/shard_map/dynamic_slice | solution.py:43
  3.8 2.4 %collective-permute-start.8 = (bf16[32,4,16,128]{3,2,1,0:T(8,128)(2,1)}, bf16[32,4,16,128]{3,2,1,0:T(8,128)(2,1)}, u32[]{:S(2)}, u32[]{:S(2)}) collective-permute-start(bf16[32,4,16,128]{3,2,1,0:T(8,128)(2,1)} %get-tuple-element.19), channel_id=1, source_target_pairs={{0,3},{1,0},{2,1},{3,2},{4,7},{5,4},{6,5},{7,6},{8,11},{9,8},{10,9... | collective-permute-start | bytes 1572872 | tf_op jit(solution)/shard_map/ppermute | solution.py:45
  6.2 0.6 collective-permute-start.7
  7.0 1.5 constant_dynamic-slice_fusion.11
  8.4 1.6 %collective-permute-start.2 = (bf16[32,4,16,128]{3,2,1,0:T(8,128)(2,1)}, bf16[32,4,16,128]{3,2,1,0:T(8,128)(2,1)S(1)}, u32[]{:S(2)}, u32[]{:S(2)}) collective-permute-start(bf16[32,4,16,128]{3,2,1,0:T(8,128)(2,1)} %get-tuple-element.31), channel_id=1, source_target_pairs={{0,3},{1,0},{2,1},{3,2},{4,7},{5,4},{6,5},{7,6},{8,11},{9,8},{10,9... | collective-permute-start | bytes 1572872 | tf_op jit(solution)/shard_map/ppermute | solution.py:45
  10.0 1.4 collective-permute-start.1
  13.0 1.1 copy.40
  14.2 1.1 copy.44
  15.3 0.8 concatenate.23.refs_0_
  16.1 2.6 %collective-permute-done.8 = bf16[32,4,16,128]{3,2,1,0:T(8,128)(2,1)} collective-permute-done((bf16[32,4,16,128]{3,2,1,0:T(8,128)(2,1)}, bf16[32,4,16,128]{3,2,1,0:T(8,128)(2,1)}, u32[]{:S(2)}, u32[]{:S(2)}) %collective-permute-start.8) | collective-permute-done | bytes 524320 | tf_op jit(solution)/shard_map/ppermute | solution.py:45
  18.7 1.2 collective-permute-start
  20.0 2.2 %copy.37 = bf16[4,8,64,128]{3,1,2,0:T(8,128)(2,1)} copy(bf16[4,8,64,128]{3,2,1,0:T(8,128)(2,1)} %bitcast.46) | data formatting | bytes 1048576
  22.1 9.0 %collective-permute-done.7 = bf16[32,4,16,128]{3,2,1,0:T(8,128)(2,1)} collective-permute-done((bf16[32,4,16,128]{3,2,1,0:T(8,128)(2,1)}, bf16[32,4,16,128]{3,2,1,0:T(8,128)(2,1)}, u32[]{:S(2)}, u32[]{:S(2)}) %collective-permute-start.7) | collective-permute-done | bytes 524320 | tf_op jit(solution)/shard_map/ppermute | solution.py:45
  31.1 2.2 %copy.38 = bf16[4,8,64,128]{3,1,2,0:T(8,128)(2,1)} copy(bf16[4,8,64,128]{3,2,1,0:T(8,128)(2,1)} %bitcast.43) | data formatting | bytes 1048576
  33.3 2.2 %copy.39 = bf16[4,8,64,128]{3,1,2,0:T(8,128)(2,1)} copy(bf16[4,8,64,128]{3,2,1,0:T(8,128)(2,1)} %bitcast.40) | data formatting | bytes 1048576
  35.5 3.5 %shard_map.77 = bf16[128,8192]{1,0:T(8,128)(2,1)} custom-call(bf16[128,256]{1,0:T(8,128)(2,1)} %concatenate.23.refs_0_, bf16[32,8192]{1,0:T(8,128)(2,1)} %bitcast.88, bf16[32,8192]{1,0:T(8,128)(2,1)} %bitcast.94, bf16[32,8192]{1,0:T(8,128)(2,1)} %bitcast.92, bf16[32,8192]{1,0:T(8,128)(2,1)} %bitcast.90), custom_call_target="tpu_custom_call" | custom-call | tf_op jit(solution)/shard_map/pallas_call | solution.py:109
  38.9 2.2 %copy.28 = bf16[16,8,64,128]{3,2,1,0:T(8,128)(2,1)S(1)} copy(bf16[16,8,64,128]{3,1,2,0:T(8,128)(2,1)} %bitcast.84) | data formatting | bytes 4194304
  41.1 1.4 dynamic-slice_bitcast_fusion.4
  42.5 1.4 collective-permute-start.10
  43.9 1.4 collective-permute-start.11
  45.5 1.2 copy.41
  46.7 6.8 %collective-permute-done.1 = bf16[32,4,16,128]{3,2,1,0:T(8,128)(2,1)S(1)} collective-permute-done((bf16[32,4,16,128]{3,2,1,0:T(8,128)(2,1)}, bf16[32,4,16,128]{3,2,1,0:T(8,128)(2,1)S(1)}, u32[]{:S(2)}, u32[]{:S(2)}) %collective-permute-start.1) | collective-permute-done | bytes 524320 | tf_op jit(solution)/shard_map/ppermute | solution.py:45
  53.4 1.1 copy.42
  54.6 1.1 copy.43
  55.7 0.7 broadcast_in_dim.4
  56.4 3.6 %shard_map.76 = bf16[128,8192]{1,0:T(8,128)(2,1)} custom-call(bf16[128,256]{1,0:T(8,128)(2,1)} %concatenate.23.refs_0_, bf16[32,8192]{1,0:T(8,128)(2,1)} %bitcast.87, bf16[32,8192]{1,0:T(8,128)(2,1)} %bitcast.93, bf16[32,8192]{1,0:T(8,128)(2,1)} %bitcast.91, bf16[32,8192]{1,0:T(8,128)(2,1)} %bitcast.89, f32[1,8192]{1,0:T(1,128)} %bitcast.102), custom_call_target="tpu_custom_call" | custom-call | tf_op jit(solution)/shard_map/pallas_call | solution.py:109
  60.0 2.2 %copy.23 = bf16[16,8,64,128]{3,2,1,0:T(8,128)(2,1)S(1)} copy(bf16[16,8,64,128]{3,1,2,0:T(8,128)(2,1)} %bitcast.82) | data formatting | bytes 4194304
  62.2 0.4 dynamic-slice_bitcast_fusion.9
  62.7 1.4 collective-permute-start.4
  64.3 1.2 collective-permute-start.5
  65.5 9.2 %collective-permute-done.11 = bf16[32,4,16,128]{3,2,1,0:T(8,128)(2,1)} collective-permute-done((bf16[32,4,16,128]{3,2,1,0:T(8,128)(2,1)S(1)}, bf16[32,4,16,128]{3,2,1,0:T(8,128)(2,1)}, u32[]{:S(2)}, u32[]{:S(2)}) %collective-permute-start.11) | collective-permute-done | bytes 524320 | tf_op jit(solution)/shard_map/ppermute | solution.py:45
  74.8 1.5 pad_maximum_fusion.11
  76.7 0.8 pad_maximum_fusion.12
  77.6 1.3 collective-permute-start.12
  78.9 4.8 %collective-permute-start.13 = (bf16[32,1,64,128]{3,2,1,0:T(8,128)(2,1)S(1)}, bf16[32,1,64,128]{3,2,1,0:T(8,128)(2,1)S(1)}, u32[]{:S(2)}, u32[]{:S(2)}) collective-permute-start(bf16[32,1,64,128]{3,2,1,0:T(8,128)(2,1)S(1)} %get-tuple-element.8), channel_id=1, source_target_pairs={{0,4},{4,8},{8,12},{12,16},{16,20},{20,24},{24,28},{1,5},{5,9},{9,... | collective-permute-start | bytes 1572872 | tf_op jit(solution)/shard_map/ppermute | solution.py:22
  83.6 3.1 %collective-permute-done.3 = bf16[32,4,16,128]{3,2,1,0:T(8,128)(2,1)S(1)} collective-permute-done((bf16[32,4,16,128]{3,2,1,0:T(8,128)(2,1)S(1)}, bf16[32,4,16,128]{3,2,1,0:T(8,128)(2,1)S(1)}, u32[]{:S(2)}, u32[]{:S(2)}) %collective-permute-start.3) | collective-permute-done | bytes 524320 | tf_op jit(solution)/shard_map/ppermute | solution.py:45
  87.1 10.1 %collective-permute-done.5 = bf16[32,4,16,128]{3,2,1,0:T(8,128)(2,1)S(1)} collective-permute-done((bf16[32,4,16,128]{3,2,1,0:T(8,128)(2,1)S(1)}, bf16[32,4,16,128]{3,2,1,0:T(8,128)(2,1)S(1)}, u32[]{:S(2)}, u32[]{:S(2)}) %collective-permute-start.5) | collective-permute-done | bytes 524320 | tf_op jit(solution)/shard_map/ppermute | solution.py:45
  98.3 7.1 %collective-permute-done.13 = bf16[32,1,64,128]{3,2,1,0:T(8,128)(2,1)S(1)} collective-permute-done((bf16[32,1,64,128]{3,2,1,0:T(8,128)(2,1)S(1)}, bf16[32,1,64,128]{3,2,1,0:T(8,128)(2,1)S(1)}, u32[]{:S(2)}, u32[]{:S(2)}) %collective-permute-start.13) | collective-permute-done | bytes 524320 | tf_op jit(solution)/shard_map/ppermute | solution.py:22
  105.4 5.9 %fusion.6 = bf16[32,4,64,128]{3,2,1,0:T(8,128)(2,1)S(1)} fusion(f32[32,4,64,128]{3,2,1,0:T(8,128)S(1)} %get-tuple-element.10, bf16[32,1,64,128]{3,2,1,0:T(8,128)(2,1)S(1)} %collective-permute-done.13, bf16[32,4,16,128]{3,2,1,0:T(8,128)(2,1)S(1)} %get-tuple-element.12, bf16[32,4,16,128]{3,2,1,0:T(8,128)(2,1)S(1)} %get-tuple-element.13, ...), kind=kLoop, calls=%fused_computation.10 | loop fusion | flops 34603008 | bytes 9447424 | tf_op jit(solution)/shard_map/convert_element_type | solution.py:216
  111.3 0.7 pad_maximum_fusion
  112.1 0.9 fusion.23
  113.0 1.2 fusion.12
  114.1 1.7 %pad_maximum_fusion.13 = bf16[32,64,256]{2,1,0:T(8,128)(2,1)} fusion(bf16[32,64,64]{2,1,0:T(8,128)(2,1)S(1)} %get-tuple-element.6, bf16[32,64,64]{2,1,0:T(8,128)(2,1)S(1)} %get-tuple-element.5, bf16[32,64,64]{2,1,0:T(8,128)(2,1)S(1)} %get-tuple-element.4, bf16[32,64,64]{2,1,0:T(8,128)(2,1)S(1)} %get-tuple-element.3), kind=kLoop, calls=%fused_computation.35 | loop fusion | flops 4194304 | bytes 2097152 | tf_op jit(solution)/shard_map/concatenate | solution.py:164
  115.8 5.8 %all-to-all-start = ((bf16[8,256,256]{2,1,0:T(8,128)(2,1)}), bf16[8,256,256]{2,1,0:T(8,128)(2,1)S(1)}, u32[]{:S(2)}, u32[]{:S(2)}) async-start(bf16[8,256,256]{2,1,0:T(8,128)(2,1)} %bitcast.19), calls=%async_computation | async-start | bytes 2097152 | tf_op jit(solution)/shard_map/all_to_all | solution.py:232
  121.6 26.0 %all-to-all-done = bf16[8,256,256]{2,1,0:T(8,128)(2,1)S(1)} async-done(((bf16[8,256,256]{2,1,0:T(8,128)(2,1)}), bf16[8,256,256]{2,1,0:T(8,128)(2,1)S(1)}, u32[]{:S(2)}, u32[]{:S(2)}) %all-to-all-start) | async-done | bytes 1048608 | tf_op jit(solution)/shard_map/all_to_all | solution.py:232
  148.1 9.9 %all_to_all.11 = f32[8,1,32]{2,1,0:T(1,128)S(1)} all-to-all(f32[8,1,32]{2,1,0:T(1,128)S(1)} %broadcast_in_dim.5), channel_id=1, replica_groups=mesh['gx'=8,'ka'=4] {'gx'}, dimensions={0} | all-to-all | bytes 2048 | tf_op jit(solution)/shard_map/all_to_all | solution.py:34
  158.0 0.5 multiply_sqrt_fusion
  158.6 0.8 slice_multiply_fusion
  (48 shorter events, 4.4 us)
Async XLA Ops:
  0.6 6.4 %copy-start = (bf16[32,4,64,128]{3,2,1,0:T(8,128)(2,1)S(1)}, bf16[32,4,64,128]{3,2,1,0:T(8,128)(2,1)}, u32[]{:S(2)}) copy-start(bf16[32,4,64,128]{3,2,1,0:T(8,128)(2,1)} %param.6) | copy-start | bytes 6291460
  3.8 10.4 %copy-start.2 = (f32[4,64]{1,0:T(4,128)S(1)}, f32[4,64]{1,0:T(4,128)}, u32[]{:S(2)}) copy-start(f32[4,64]{1,0:T(4,128)} %param.8) | copy-start | bytes 3076
  3.8 12.3 %copy-start.3 = (f32[4,64]{1,0:T(4,128)S(1)}, f32[4,64]{1,0:T(4,128)}, u32[]{:S(2)}) copy-start(f32[4,64]{1,0:T(4,128)} %param.7) | copy-start | bytes 3076
  3.8 14.9 %collective-permute-start.8 = (bf16[32,4,16,128]{3,2,1,0:T(8,128)(2,1)}, bf16[32,4,16,128]{3,2,1,0:T(8,128)(2,1)}, u32[]{:S(2)}, u32[]{:S(2)}) collective-permute-start(bf16[32,4,16,128]{3,2,1,0:T(8,128)(2,1)} %get-tuple-element.19), channel_id=1, source_target_pairs={{0,3},{1,0},{2,1},{3,2},{4,7},{5,4},{6,5},{7,6},{8,11},{9,8},{10,9... | collective-permute-start | bytes 1572872 | tf_op jit(solution)/shard_map/ppermute | solution.py:45
  6.2 24.9 %collective-permute-start.7 = (bf16[32,4,16,128]{3,2,1,0:T(8,128)(2,1)}, bf16[32,4,16,128]{3,2,1,0:T(8,128)(2,1)}, u32[]{:S(2)}, u32[]{:S(2)}) collective-permute-start(bf16[32,4,16,128]{3,2,1,0:T(8,128)(2,1)} %get-tuple-element.22), channel_id=1, source_target_pairs={{0,2},{1,3},{2,0},{3,1},{4,6},{5,7},{6,4},{7,5},{8,10},{9,11},{10,... | collective-permute-start | bytes 1572872 | tf_op jit(solution)/shard_map/ppermute | solution.py:45
  6.8 26.4 %collective-permute-start.6 = (bf16[32,4,16,128]{3,2,1,0:T(8,128)(2,1)}, bf16[32,4,16,128]{3,2,1,0:T(8,128)(2,1)}, u32[]{:S(2)}, u32[]{:S(2)}) collective-permute-start(bf16[32,4,16,128]{3,2,1,0:T(8,128)(2,1)} %get-tuple-element.20), channel_id=1, source_target_pairs={{0,1},{1,2},{2,3},{3,0},{4,5},{5,6},{6,7},{7,4},{8,9},{9,10},{10,1... | collective-permute-start | bytes 1572872 | tf_op jit(solution)/shard_map/ppermute | solution.py:45
  8.4 35.5 %collective-permute-start.2 = (bf16[32,4,16,128]{3,2,1,0:T(8,128)(2,1)}, bf16[32,4,16,128]{3,2,1,0:T(8,128)(2,1)S(1)}, u32[]{:S(2)}, u32[]{:S(2)}) collective-permute-start(bf16[32,4,16,128]{3,2,1,0:T(8,128)(2,1)} %get-tuple-element.31), channel_id=1, source_target_pairs={{0,3},{1,0},{2,1},{3,2},{4,7},{5,4},{6,5},{7,6},{8,11},{9,8},{10,9... | collective-permute-start | bytes 1572872 | tf_op jit(solution)/shard_map/ppermute | solution.py:45
  10.0 43.4 %collective-permute-start.1 = (bf16[32,4,16,128]{3,2,1,0:T(8,128)(2,1)}, bf16[32,4,16,128]{3,2,1,0:T(8,128)(2,1)S(1)}, u32[]{:S(2)}, u32[]{:S(2)}) collective-permute-start(bf16[32,4,16,128]{3,2,1,0:T(8,128)(2,1)} %get-tuple-element.34), channel_id=1, source_target_pairs={{0,2},{1,3},{2,0},{3,1},{4,6},{5,7},{6,4},{7,5},{8,10},{9,11},{10,... | collective-permute-start | bytes 1572872 | tf_op jit(solution)/shard_map/ppermute | solution.py:45
  18.7 35.8 %collective-permute-start = (bf16[32,4,16,128]{3,2,1,0:T(8,128)(2,1)}, bf16[32,4,16,128]{3,2,1,0:T(8,128)(2,1)S(1)}, u32[]{:S(2)}, u32[]{:S(2)}) collective-permute-start(bf16[32,4,16,128]{3,2,1,0:T(8,128)(2,1)} %get-tuple-element.32), channel_id=1, source_target_pairs={{0,1},{1,2},{2,3},{3,0},{4,5},{5,6},{6,7},{7,4},{8,9},{9,10},{10,1... | collective-permute-start | bytes 1572872 | tf_op jit(solution)/shard_map/ppermute | solution.py:45
  42.5 21.8 %collective-permute-start.9 = (bf16[32,4,16,128]{3,2,1,0:T(8,128)(2,1)}, bf16[32,4,16,128]{3,2,1,0:T(8,128)(2,1)S(1)}, u32[]{:S(2)}, u32[]{:S(2)}) collective-permute-start(bf16[32,4,16,128]{3,2,1,0:T(8,128)(2,1)} %get-tuple-element.18), channel_id=1, source_target_pairs={{0,1},{1,2},{2,3},{3,0},{4,5},{5,6},{6,7},{7,4},{8,9},{9,10},{10,1... | collective-permute-start | bytes 1572872 | tf_op jit(solution)/shard_map/ppermute | solution.py:45
  42.5 23.0 %collective-permute-start.10 = (bf16[32,4,16,128]{3,2,1,0:T(8,128)(2,1)}, bf16[32,4,16,128]{3,2,1,0:T(8,128)(2,1)}, u32[]{:S(2)}, u32[]{:S(2)}) collective-permute-start(bf16[32,4,16,128]{3,2,1,0:T(8,128)(2,1)} %get-tuple-element.17), channel_id=1, source_target_pairs={{0,2},{1,3},{2,0},{3,1},{4,6},{5,7},{6,4},{7,5},{8,10},{9,11},{10,... | collective-permute-start | bytes 1572872 | tf_op jit(solution)/shard_map/ppermute | solution.py:45
  43.9 30.9 %collective-permute-start.11 = (bf16[32,4,16,128]{3,2,1,0:T(8,128)(2,1)S(1)}, bf16[32,4,16,128]{3,2,1,0:T(8,128)(2,1)}, u32[]{:S(2)}, u32[]{:S(2)}) collective-permute-start(bf16[32,4,16,128]{3,2,1,0:T(8,128)(2,1)S(1)} %get-tuple-element.16), channel_id=1, source_target_pairs={{0,3},{1,0},{2,1},{3,2},{4,7},{5,4},{6,5},{7,6},{8,11},{9,8},{10,9... | collective-permute-start | bytes 1572872 | tf_op jit(solution)/shard_map/ppermute | solution.py:45
  62.6 24.1 %collective-permute-start.3 = (bf16[32,4,16,128]{3,2,1,0:T(8,128)(2,1)S(1)}, bf16[32,4,16,128]{3,2,1,0:T(8,128)(2,1)S(1)}, u32[]{:S(2)}, u32[]{:S(2)}) collective-permute-start(bf16[32,4,16,128]{3,2,1,0:T(8,128)(2,1)S(1)} %get-tuple-element.30), channel_id=1, source_target_pairs={{0,1},{1,2},{2,3},{3,0},{4,5},{5,6},{6,7},{7,4},{8,9},{9,10},{10,1... | collective-permute-start | bytes 1572872 | tf_op jit(solution)/shard_map/ppermute | solution.py:45
  62.7 24.4 %collective-permute-start.4 = (bf16[32,4,16,128]{3,2,1,0:T(8,128)(2,1)S(1)}, bf16[32,4,16,128]{3,2,1,0:T(8,128)(2,1)S(1)}, u32[]{:S(2)}, u32[]{:S(2)}) collective-permute-start(bf16[32,4,16,128]{3,2,1,0:T(8,128)(2,1)S(1)} %get-tuple-element.29), channel_id=1, source_target_pairs={{0,2},{1,3},{2,0},{3,1},{4,6},{5,7},{6,4},{7,5},{8,10},{9,11},{10,... | collective-permute-start | bytes 1572872 | tf_op jit(solution)/shard_map/ppermute | solution.py:45
  64.3 32.9 %collective-permute-start.5 = (bf16[32,4,16,128]{3,2,1,0:T(8,128)(2,1)S(1)}, bf16[32,4,16,128]{3,2,1,0:T(8,128)(2,1)S(1)}, u32[]{:S(2)}, u32[]{:S(2)}) collective-permute-start(bf16[32,4,16,128]{3,2,1,0:T(8,128)(2,1)S(1)} %get-tuple-element.28), channel_id=1, source_target_pairs={{0,3},{1,0},{2,1},{3,2},{4,7},{5,4},{6,5},{7,6},{8,11},{9,8},{10,9... | collective-permute-start | bytes 1572872 | tf_op jit(solution)/shard_map/ppermute | solution.py:45
  77.6 20.7 %collective-permute-start.12 = (bf16[32,1,64,128]{3,2,1,0:T(8,128)(2,1)S(1)}, bf16[32,1,64,128]{3,2,1,0:T(8,128)(2,1)S(1)}, u32[]{:S(2)}, u32[]{:S(2)}) collective-permute-start(bf16[32,1,64,128]{3,2,1,0:T(8,128)(2,1)S(1)} %get-tuple-element.7), channel_id=1, source_target_pairs={{4,0},{8,4},{12,8},{16,12},{20,16},{24,20},{28,24},{5,1},{9,5},{13... | collective-permute-start | bytes 1572872 | tf_op jit(solution)/shard_map/ppermute | solution.py:24
  78.9 26.5 %collective-permute-start.13 = (bf16[32,1,64,128]{3,2,1,0:T(8,128)(2,1)S(1)}, bf16[32,1,64,128]{3,2,1,0:T(8,128)(2,1)S(1)}, u32[]{:S(2)}, u32[]{:S(2)}) collective-permute-start(bf16[32,1,64,128]{3,2,1,0:T(8,128)(2,1)S(1)} %get-tuple-element.8), channel_id=1, source_target_pairs={{0,4},{4,8},{8,12},{12,16},{16,20},{20,24},{24,28},{1,5},{5,9},{9,... | collective-permute-start | bytes 1572872 | tf_op jit(solution)/shard_map/ppermute | solution.py:22
  97.5 7.9 %copy-start.1 = (f32[4,64]{1,0:T(4,128)S(1)}, f32[4,64]{1,0:T(4,128)}, u32[]{:S(2)}) copy-start(f32[4,64]{1,0:T(4,128)} %param.9) | copy-start | bytes 3076
  115.8 31.8 %all-to-all-start = ((bf16[8,256,256]{2,1,0:T(8,128)(2,1)}), bf16[8,256,256]{2,1,0:T(8,128)(2,1)S(1)}, u32[]{:S(2)}, u32[]{:S(2)}) async-start(bf16[8,256,256]{2,1,0:T(8,128)(2,1)} %bitcast.19), calls=%async_computation | async-start | bytes 2097152 | tf_op jit(solution)/shard_map/all_to_all | solution.py:232

commit v9 on v8

--- a/solution.py
+++ b/solution.py
@@ -115,10 +115,12 @@
     )(*args)
 
 
-def piece_tables(count, local_angles, axis):
+def piece_tables(count, local_angles, axis, wave_order=None):
     here = lax.axis_index(axis)
     blocks = count // local_angles
-    wave_index = jnp.arange(count, dtype=jnp.int32) - count // 2
+    if wave_order is None:
+        wave_order = jnp.arange(count, dtype=jnp.int32)
+    wave_index = wave_order - count // 2
     scaling = 1.0 / math.sqrt(count)
     columns = []
     for shift in range(blocks):
@@ -241,6 +243,113 @@
     return (hankel_gram, reduced_operator, hankel_norm)
 
 
+def core_pairs(cells, partner_pairs):
+    return lax.ppermute(cells, "ka", partner_pairs)
+
+
+def by_chip(direct_snapshots, adjoint_snapshots, quad_weight, mean_velocity, diffusivity):
+    local_angles, axial_cells, radial_cells, columns = direct_snapshots.shape
+    snap_count = columns // 2
+    band_count = lax.axis_size("ka")
+    axial_count = lax.axis_size("gx")
+    total_angles = local_angles * band_count
+    band_index = lax.axis_index("ka")
+    core = band_index % 2
+    side = band_index // 2
+    band = radial_cells // band_count
+    lanes = axial_cells * band * columns
+    half = total_angles // 2
+    row = jnp.arange(total_angles, dtype=jnp.int32)
+    wave_order = (((row % half) // local_angles) * 2 + row // half) * local_angles + row % local_angles
+    table = piece_tables(total_angles, local_angles, "ka", wave_order)
+    norm_factor = 1.0 / math.sqrt(axial_cells * axial_count * radial_cells)
+    band_weight = lax.dynamic_slice_in_dim(quad_weight * norm_factor, band_index * band, band, axis=1)
+    lane_weight = jnp.broadcast_to(band_weight[:, :, None], (axial_cells, band, columns)).reshape(1, lanes)
+    across_cores = [(0, 1), (1, 0), (2, 3), (3, 2)]
+
+    def transform_all(snapshots, weight=None):
+        pieces = [piece.reshape(local_angles, lanes) for piece in exchange(snapshots, "ka", 2)]
+        modes = dft(table, pieces, weight).reshape(2, half, axial_cells, band, columns)
+        kept = lax.dynamic_index_in_dim(modes, core, 0, keepdims=False)
+        sent = lax.dynamic_index_in_dim(modes, 1 - core, 0, keepdims=False)
+        stacked = jnp.stack([kept, core_pairs(sent, across_cores)])
+        lower = lax.dynamic_index_in_dim(stacked, core, 0, keepdims=False)
+        upper = lax.dynamic_index_in_dim(stacked, 1 - core, 0, keepdims=False)
+        return jnp.concatenate([lower, upper], axis=2)
+
+    field = transform_all(direct_snapshots)
+    weighted = transform_all(adjoint_snapshots, lane_weight)
+    span = 2 * band
+    up_pairs = [(0, 2), (1, 3)]
+    down_pairs = [(2, 0), (3, 1)]
+    below = core_pairs(field[:, :, span - 1 :], up_pairs)
+    above = core_pairs(field[:, :, :1], down_pairs)
+    radial_halo = jnp.concatenate([below, field, above], axis=2).astype(jnp.float32)
+    outward = radial_halo[:, :, 2:]
+    inward = radial_halo[:, :, :-2]
+    padded = padded_2(field, (("gx", 1),), 1)
+    field_f32 = field.astype(jnp.float32)
+    forward = padded[:, 2:].astype(jnp.float32)
+    behind = padded[:, :-2].astype(jnp.float32)
+    first_radial = side * span
+    radial_index = (first_radial + jnp.arange(span, dtype=jnp.int32)).astype(jnp.float32)
+    radius = 0.25 + (radial_index + 0.5) / radial_cells
+    local_row = jnp.arange(half, dtype=jnp.int32)
+    wave = ((local_row // local_angles) * 2 + core) * local_angles + local_row % local_angles
+    wavenumber = (wave - total_angles // 2).astype(jnp.float32) / total_angles
+    azimuthal = (wavenumber[:, None] / radius[None, :]) ** 2
+    velocity = lax.dynamic_slice_in_dim(mean_velocity, first_radial, span, axis=1)[None, :, :, None]
+    diffusion = lax.dynamic_slice_in_dim(diffusivity, first_radial, span, axis=1)[None, :, :, None]
+    image = (
+        -velocity * (forward - behind) * 0.5
+        + diffusion
+        * (
+            forward
+            + behind
+            + outward
+            + inward
+            - 4.0 * field_f32
+            - azimuthal[:, None, :, None] * field_f32
+        )
+    ).astype(jnp.bfloat16)
+    right_side = jnp.concatenate([field, image], axis=-1)
+    product = jnp.einsum(
+        "kpa,kpb->kab",
+        weighted.reshape(half, -1, columns),
+        right_side.reshape(half, -1, 2 * columns),
+        preferred_element_type=jnp.float32,
+    )
+    gram_terms = complex_blocks(product, snap_count).reshape(2, local_angles * snap_count, 2 * columns)
+    mine = lax.dynamic_index_in_dim(gram_terms, side, 0, keepdims=False)
+    theirs = lax.dynamic_index_in_dim(gram_terms, 1 - side, 0, keepdims=False).astype(jnp.bfloat16)
+    across_sides = [(0, 2), (1, 3), (2, 0), (3, 1)]
+    summed = mine + core_pairs(theirs, across_sides).astype(jnp.float32)
+    row_count = local_angles * snap_count // axial_count
+    shares = summed.astype(jnp.bfloat16).reshape(axial_count, row_count, 2 * columns)
+    shares = lax.all_to_all(shares, "gx", split_axis=0, concat_axis=0, tiled=True)
+    own_rows = jnp.sum(shares.astype(jnp.float32), axis=0)
+    row_index = lax.axis_index("gx") * row_count + jnp.arange(row_count, dtype=jnp.int32)
+    owner = row_index // snap_count
+    selector = (owner[:, None] == jnp.arange(local_angles, dtype=jnp.int32)[None, :]).astype(
+        jnp.float32
+    )
+    row_energy = jnp.sum(own_rows[:, :columns] ** 2, axis=1)
+    energy = jnp.sum(gather_small(jnp.sum(selector * row_energy[:, None], axis=0), "gx"), axis=0)
+    mean_sq = energy / (2.0 * snap_count * snap_count)
+    row_scale = jnp.sum(selector * lax.rsqrt(mean_sq + epsilon)[None, :], axis=1)
+    hankel_gram = own_rows[:, :columns] * row_scale[:, None]
+    reduced_operator = own_rows[:, columns:] * row_scale[:, None]
+    hankel_norm = jnp.sqrt(mean_sq)
+    return (hankel_gram, reduced_operator, hankel_norm)
+
+
+def dispatch(direct_snapshots, *rest):
+    local_angles, _, radial_cells, _ = direct_snapshots.shape
+    fits = lax.axis_size("ka") == 4 and radial_cells % 4 == 0
+    body = by_chip if fits else local
+    return body(direct_snapshots, *rest)
+
+
 def solution(mesh):
     placed = (
         P("ka", "gx", None, None),
@@ -250,7 +359,7 @@
         P("gx", None),
     )
     return jax.shard_map(
-        local,
+        dispatch,
         mesh=mesh,
         in_specs=placed,
         out_specs=(P(("ka", "gx"), None), P(("ka", "gx"), None), P("ka")),

time: 160 us -> 190 us (1.19)
  other arithmetic: 15.3 us -> 28.5 us
  waiting for transfers between devices: 74.5 us -> 84.1 us
  matrix products: 0.9 us -> 4.55 us
  local copies, waits for them, and re-layouts: 25.9 us -> 29.3 us
    ppermute x0 -> x5, waiting for transfers between devices: none -> 28 us  [core_pairs(): return lax.ppermute(cells, 'ka', partner_pairs)]
    ppermute x12 -> x6, waiting for transfers between devices: 41.4 us -> 21.1 us  [exchange(): lax.ppermute(piece, axis, [(j, (j + shift) % count) for j in range(count)])]
    add x1 -> x2, other arithmetic: 0.01 us -> 9.76 us  [the longest x1 9.75 us: complex_blocks(): upper_rows[..., offset:offset + half]]
    ppermute x0 -> x5, starting transfers between devices: none -> 6.4 us  [core_pairs(): return lax.ppermute(cells, 'ka', partner_pairs)]
    ppermute x12 -> x6, starting transfers between devices: 13 us -> 7.42 us  [exchange(): lax.ppermute(piece, axis, [(j, (j + shift) % count) for j in range(count)])]
    dot_general x1, matrix products: 0.9 us -> 4.55 us  [by_chip(): jnp.einsum('kpa,kpb->kab', weighted.reshape(half, -1, columns), right_sid...]
    unnamed x18 -> x20, local copies, waits for them, and re-layouts: 16.6 us -> 19.6 us
    another operation x3 -> x0, other arithmetic: 2.9 us -> none  [the longest x2 1.72 us: in_source_order(): stacked = jnp.stack(pieces)]
  transfers between devices with their start and end apart: 15 -> 14, of which waited for: 10 -> 8; matrix products, arithmetic and copies ran while one was open for 17% -> 16% of each run, Pallas kernels for 4% -> 4%
where the time goes in v9:
time: 190 us
  waiting for transfers between devices  84.1 us (44%)
  local copies, waits for them, and re-layouts  29.3 us (15%)
  other arithmetic  28.5 us (15%)
  starting transfers between devices  25.5 us (13%)
  blocking collectives  9.63 us (5%)
  Pallas kernels  7.09 us (4%)
  matrix products  4.55 us (2%)
    ppermute x5, waiting for transfers between devices, core_pairs(): return lax.ppermute(cells, 'ka', partner_pairs)  28 us
    all_to_all x1, waiting for transfers between devices, by_chip(): lax.all_to_all(shares, 'gx', split_axis=0, concat_axis=0, tiled=True)  25.3 us
    ppermute x6, waiting for transfers between devices, exchange(): lax.ppermute(piece, axis, [(j, (j + shift) % count) for j in range(count)])  21.1 us
    unnamed x20, local copies, waits for them, and re-layouts  19.6 us
    add x1, other arithmetic, complex_blocks(): upper_rows[..., offset:offset + half]  9.75 us
    ppermute x1, waiting for transfers between devices, padded_2(): lax.ppermute(tail, axis, [(i, (i + 1) % count) for i in range(ends)])  9.73 us
    all_to_all x1, blocking collectives, gather_small(): return lax.all_to_all(copies, axis, split_axis=0, concat_axis=0, tiled=True)  9.63 us
    ppermute x6, starting transfers between devices, exchange(): lax.ppermute(piece, axis, [(j, (j + shift) % count) for j in range(count)])  7.42 us
  transfers between devices with their start and end apart: 14, of which 8 were waited for; matrix products, arithmetic and copies ran while one was open for 16% of the time, Pallas kernels for 4%

profile of v9, /device:TPU:0, one launch (start us, length us, event | category | flops | bytes accessed | tf_op | source)
XLA Modules:
  0.0 189.7 jit_solution(18332567747230579369)
XLA Ops:
  0.7 3.1 %constant_dynamic-slice_fusion.3 = (bf16[32,4,16,128]{3,2,1,0:T(8,128)(2,1)}, bf16[32,4,16,128]{3,2,1,0:T(8,128)(2,1)}, bf16[32,4,16,128]{3,2,1,0:T(8,128)(2,1)S(1)}, bf16[32,4,16,128]{3,2,1,0:T(8,128)(2,1)}) fusion(bf16[32,4,64,128]{3,2,1,0:T(8,128)(2,1)} %param.5, s32[]{:T(128)S(6)} %select_n.214, s32[]{:T(128)S(6)} %select_n.210, s32[]{:T(128)S(6)} %select_n.208, ...), kind=kLoop, calls=%fused_computation.109 | loop fusion | bytes 4194320 | tf_op jit(solution)/shard_map/dynamic_slice | solution.py:43
  3.8 2.4 %collective-permute-start.6 = (bf16[32,4,16,128]{3,2,1,0:T(8,128)(2,1)}, bf16[32,4,16,128]{3,2,1,0:T(8,128)(2,1)}, u32[]{:S(2)}, u32[]{:S(2)}) collective-permute-start(bf16[32,4,16,128]{3,2,1,0:T(8,128)(2,1)} %get-tuple-element.13), channel_id=1, source_target_pairs={{0,3},{1,0},{2,1},{3,2},{4,7},{5,4},{6,5},{7,6},{8,11},{9,8},{10,9... | collective-permute-start | bytes 1572872 | tf_op jit(solution)/shard_map/ppermute | solution.py:45
  6.2 0.6 collective-permute-start.5
  7.0 1.5 constant_dynamic-slice_fusion.9
  8.5 1.5 collective-permute-start.2
  10.0 1.5 collective-permute-start.1
  12.8 5.9 %collective-permute-done.6 = bf16[32,4,16,128]{3,2,1,0:T(8,128)(2,1)} collective-permute-done((bf16[32,4,16,128]{3,2,1,0:T(8,128)(2,1)}, bf16[32,4,16,128]{3,2,1,0:T(8,128)(2,1)}, u32[]{:S(2)}, u32[]{:S(2)}) %collective-permute-start.6) | collective-permute-done | bytes 524320 | tf_op jit(solution)/shard_map/ppermute | solution.py:45
  18.7 1.2 collective-permute-start
  20.2 1.1 copy.40
  21.4 0.8 concatenate.26.refs_0_
  22.1 2.2 %copy.37 = bf16[4,8,64,128]{3,1,2,0:T(8,128)(2,1)} copy(bf16[4,8,64,128]{3,2,1,0:T(8,128)(2,1)} %bitcast.41) | data formatting | bytes 1048576
  24.3 6.8 %collective-permute-done.5 = bf16[32,4,16,128]{3,2,1,0:T(8,128)(2,1)} collective-permute-done((bf16[32,4,16,128]{3,2,1,0:T(8,128)(2,1)}, bf16[32,4,16,128]{3,2,1,0:T(8,128)(2,1)}, u32[]{:S(2)}, u32[]{:S(2)}) %collective-permute-start.5) | collective-permute-done | bytes 524320 | tf_op jit(solution)/shard_map/ppermute | solution.py:45
  31.1 2.2 %copy.38 = bf16[4,8,64,128]{3,1,2,0:T(8,128)(2,1)} copy(bf16[4,8,64,128]{3,2,1,0:T(8,128)(2,1)} %bitcast.38) | data formatting | bytes 1048576
  33.3 2.2 %copy.39 = bf16[4,8,64,128]{3,1,2,0:T(8,128)(2,1)} copy(bf16[4,8,64,128]{3,2,1,0:T(8,128)(2,1)} %bitcast.35) | data formatting | bytes 1048576
  35.4 3.5 %shard_map.77 = bf16[128,8192]{1,0:T(8,128)(2,1)} custom-call(bf16[128,256]{1,0:T(8,128)(2,1)} %concatenate.26.refs_0_, bf16[32,8192]{1,0:T(8,128)(2,1)} %bitcast.84, bf16[32,8192]{1,0:T(8,128)(2,1)} %bitcast.91, bf16[32,8192]{1,0:T(8,128)(2,1)} %bitcast.89, bf16[32,8192]{1,0:T(8,128)(2,1)} %bitcast.87), custom_call_target="tpu_custom_call" | custom-call | tf_op jit(solution)/shard_map/pallas_call | solution.py:109
  38.9 2.2 %copy.28 = bf16[16,8,64,128]{3,2,1,0:T(8,128)(2,1)S(1)} copy(bf16[16,8,64,128]{3,1,2,0:T(8,128)(2,1)} %bitcast.81) | data formatting | bytes 4194304
  41.1 1.4 dynamic-slice_bitcast_fusion
  42.5 1.1 copy.44
  43.7 1.2 copy.41
  44.9 8.4 %collective-permute-done.1 = bf16[32,4,16,128]{3,2,1,0:T(8,128)(2,1)S(1)} collective-permute-done((bf16[32,4,16,128]{3,2,1,0:T(8,128)(2,1)}, bf16[32,4,16,128]{3,2,1,0:T(8,128)(2,1)S(1)}, u32[]{:S(2)}, u32[]{:S(2)}) %collective-permute-start.1) | collective-permute-done | bytes 524320 | tf_op jit(solution)/shard_map/ppermute | solution.py:45
  53.3 1.1 copy.42
  54.4 2.2 %copy.43 = bf16[4,8,64,128]{3,1,2,0:T(8,128)(2,1)} copy(bf16[4,8,64,128]{3,2,1,0:T(8,128)(2,1)} %bitcast.20) | data formatting | bytes 1048576
  56.6 0.7 broadcast_in_dim.4
  57.3 3.6 %shard_map.76 = bf16[128,8192]{1,0:T(8,128)(2,1)} custom-call(bf16[128,256]{1,0:T(8,128)(2,1)} %concatenate.26.refs_0_, bf16[32,8192]{1,0:T(8,128)(2,1)} %bitcast.85, bf16[32,8192]{1,0:T(8,128)(2,1)} %bitcast.90, bf16[32,8192]{1,0:T(8,128)(2,1)} %bitcast.88, bf16[32,8192]{1,0:T(8,128)(2,1)} %bitcast.86, f32[1,8192]{1,0:T(1,128)} %bitcast.95), custom_call_target="tpu_custom_call" | custom-call | tf_op jit(solution)/shard_map/pallas_call | solution.py:109
  60.9 2.2 %copy.23 = bf16[16,8,64,128]{3,2,1,0:T(8,128)(2,1)S(1)} copy(bf16[16,8,64,128]{3,1,2,0:T(8,128)(2,1)} %bitcast.80) | data formatting | bytes 4194304
  63.2 1.4 dynamic-slice_bitcast_fusion.1
  64.8 2.0 %fusion.12 = (bf16[64,4,16,128]{3,2,1,0:T(8,128)(2,1)S(1)}, bf16[64,4,16,128]{3,2,1,0:T(8,128)(2,1)S(1)}) fusion(s32[]{:T(128)S(6)} %select_n.218, bf16[1,64,4,16,128]{4,3,2,1,0:T(8,128)(2,1)S(1)} %get-tuple-element.12, bf16[1,64,4,16,128]{4,3,2,1,0:T(8,128)(2,1)} %bitcast.7, s32[]{:T(128)S(6)} %select_n.217), kind=kLoop, calls=%fused_computation.44 | loop fusion | flops 1048576 | bytes 4194312 | tf_op jit(solution)/shard_map/jit(dynamic_index_in_dim)/squeeze | solution.py:277
  67.1 1.3 collective-permute-start.8
  68.4 4.6 %collective-permute-start.9 = (bf16[64,1,32,128]{3,2,1,0:T(8,128)(2,1)S(1)}, bf16[64,1,32,128]{3,2,1,0:T(8,128)(2,1)S(1)}, u32[]{:S(2)}, u32[]{:S(2)}) collective-permute-start(bf16[64,1,32,128]{3,2,1,0:T(8,128)(2,1)S(1)} %get-tuple-element.8), channel_id=1, source_target_pairs={{0,4},{4,8},{8,12},{12,16},{16,20},{20,24},{24,28},{1,5},{5,9},{9,... | collective-permute-start | bytes 1572872 | tf_op jit(solution)/shard_map/ppermute | solution.py:22
  73.0 3.4 %collective-permute-start.10 = (bf16[64,4,1,128]{3,2,1,0:T(2,128)(2,1)S(1)}, bf16[64,4,1,128]{3,2,1,0:T(2,128)(2,1)S(1)}, u32[]{:S(2)}, u32[]{:S(2)}) collective-permute-start(bf16[64,4,1,128]{3,2,1,0:T(2,128)(2,1)S(1)} %slice.89), channel_id=1, source_target_pairs={{0,2},{1,3},{4,6},{5,7},{8,10},{9,11},{12,14},{13,15},{16,18},{17,... | collective-permute-start | bytes 196616 | tf_op jit(solution)/shard_map/ppermute | solution.py:247
  76.5 1.5 collective-permute-start.11
  77.9 0.8 fusion.18
  79.3 4.1 %collective-permute-done.11 = bf16[64,4,1,128]{3,2,1,0:T(2,128)(2,1)S(1)} collective-permute-done((bf16[64,4,1,128]{3,2,1,0:T(2,128)(2,1)S(1)}, bf16[64,4,1,128]{3,2,1,0:T(2,128)(2,1)S(1)}, u32[]{:S(2)}, u32[]{:S(2)}) %collective-permute-start.11) | collective-permute-done | bytes 65568 | tf_op jit(solution)/shard_map/ppermute | solution.py:247
  83.4 1.4 maximum_convert_fusion
  84.9 9.7 %collective-permute-done.9 = bf16[64,1,32,128]{3,2,1,0:T(8,128)(2,1)S(1)} collective-permute-done((bf16[64,1,32,128]{3,2,1,0:T(8,128)(2,1)S(1)}, bf16[64,1,32,128]{3,2,1,0:T(8,128)(2,1)S(1)}, u32[]{:S(2)}, u32[]{:S(2)}) %collective-permute-start.9) | collective-permute-done | bytes 524320 | tf_op jit(solution)/shard_map/ppermute | solution.py:22
  94.6 4.1 %fusion.3 = bf16[64,4,32,128]{3,2,1,0:T(8,128)(2,1)S(1)} fusion(f32[64,4,34,128]{3,2,1,0:T(8,128)S(1)} %maximum_convert_fusion, bf16[64,4,16,128]{3,2,1,0:T(8,128)(2,1)S(1)} %get-tuple-element.9, bf16[64,4,16,128]{3,2,1,0:T(8,128)(2,1)S(1)} %get-tuple-element.10, bf16[64,1,32,128]{3,2,1,0:T(8,128)(2,1)S(1)} %collective-permute-done.9, ...), kind=kLoop, calls=%fused_computation.7 | loop fusion | flops 30408704 | bytes 13640704 | tf_op jit(solution)/shard_map/convert_element_type | solution.py:314
  98.7 0.7 pad_maximum_fusion
  99.5 4.6 %fusion.41 = f32[64,128,256]{2,1,0:T(8,128)} fusion(bf16[64,128,128]{2,1,0:T(8,128)(2,1)S(1)} %bitcast.77, bf16[64,128,256]{2,1,0:T(8,128)(2,1)S(1)} %bitcast.74), kind=kOutput, calls=%fused_computation.159 | convolution fusion | flops 536870912 | bytes 14680064 | tf_op jit(solution)/shard_map/kpa,kpb->kab/dot_general | solution.py:316
  104.0 9.8 %slice_add_fusion.1 = (f32[64,64,64]{2,1,0:T(8,128)S(1)}, f32[64,64,64]{2,1,0:T(8,128)S(1)}, f32[64,64,64]{2,1,0:T(8,128)S(1)}, f32[64,64,64]{2,1,0:T(8,128)}) fusion(f32[64,128,256]{2,1,0:T(8,128)} %fusion.41), kind=kLoop, calls=%fused_computation.32 | loop fusion | flops 1048576 | bytes 12582912 | tf_op jit(solution)/shard_map/add | solution.py:159
  113.8 3.3 %pad_maximum_fusion.1 = f32[64,64,256]{2,1,0:T(8,128)S(1)} fusion(f32[64,64,64]{2,1,0:T(8,128)} %get-tuple-element.6, f32[64,64,64]{2,1,0:T(8,128)S(1)} %get-tuple-element.5, f32[64,64,64]{2,1,0:T(8,128)S(1)} %get-tuple-element.4, f32[64,64,64]{2,1,0:T(8,128)S(1)} %get-tuple-element.3), kind=kLoop, calls=%fused_computation.14 | loop fusion | flops 3145728 | bytes 8388608 | tf_op jit(solution)/shard_map/concatenate | solution.py:166
  117.1 1.9 %copy-done = f32[64,64,256]{2,1,0:T(8,128)} copy-done((f32[64,64,256]{2,1,0:T(8,128)}, f32[64,64,256]{2,1,0:T(8,128)S(1)}, u32[]{:S(2)}) %copy-start) | copy-done | bytes 4194328
  119.1 1.5 collective-permute-start.12
  120.6 23.7 %collective-permute-done.12 = bf16[2048,256]{1,0:T(8,128)(2,1)S(1)} collective-permute-done((bf16[2048,256]{1,0:T(8,128)(2,1)S(1)}, bf16[2048,256]{1,0:T(8,128)(2,1)S(1)}, u32[]{:S(2)}, u32[]{:S(2)}) %collective-permute-start.12) | collective-permute-done | bytes 1048608 | tf_op jit(solution)/shard_map/ppermute | solution.py:247
  144.3 2.8 %fusion.9 = bf16[2048,256]{1,0:T(8,128)(2,1)} fusion(bf16[2048,256]{1,0:T(8,128)(2,1)S(1)} %collective-permute-done.12, f32[2,2048,256]{2,1,0:T(8,128)} %bitcast.76, s32[]{:T(128)S(6)} %select_n.223), kind=kLoop, calls=%fused_computation.39 | loop fusion | flops 1572864 | bytes 4194308 | tf_op jit(solution)/shard_map/convert_element_type | solution.py:328
  147.1 5.8 %all-to-all-start = ((bf16[8,256,256]{2,1,0:T(8,128)(2,1)}), bf16[8,256,256]{2,1,0:T(8,128)(2,1)S(1)}, u32[]{:S(2)}, u32[]{:S(2)}) async-start(bf16[8,256,256]{2,1,0:T(8,128)(2,1)} %bitcast.14), calls=%async_computation | async-start | bytes 2097152 | tf_op jit(solution)/shard_map/all_to_all | solution.py:329
  152.9 25.3 %all-to-all-done = bf16[8,256,256]{2,1,0:T(8,128)(2,1)S(1)} async-done(((bf16[8,256,256]{2,1,0:T(8,128)(2,1)}), bf16[8,256,256]{2,1,0:T(8,128)(2,1)S(1)}, u32[]{:S(2)}, u32[]{:S(2)}) %all-to-all-start) | async-done | bytes 1048608 | tf_op jit(solution)/shard_map/all_to_all | solution.py:329
  178.6 9.6 %all_to_all.11 = f32[8,1,32]{2,1,0:T(1,128)S(1)} all-to-all(f32[8,1,32]{2,1,0:T(1,128)S(1)} %broadcast_in_dim.5), channel_id=1, replica_groups=mesh['gx'=8,'ka'=4] {'gx'}, dimensions={0} | all-to-all | bytes 2048 | tf_op jit(solution)/shard_map/all_to_all | solution.py:34
  188.9 0.8 slice_multiply_fusion
  (50 shorter events, 4.0 us)
Async XLA Ops:
  0.6 6.4 %copy-start.1 = (bf16[32,4,64,128]{3,2,1,0:T(8,128)(2,1)S(1)}, bf16[32,4,64,128]{3,2,1,0:T(8,128)(2,1)}, u32[]{:S(2)}) copy-start(bf16[32,4,64,128]{3,2,1,0:T(8,128)(2,1)} %param.6) | copy-start | bytes 6291460
  3.8 14.9 %collective-permute-start.6 = (bf16[32,4,16,128]{3,2,1,0:T(8,128)(2,1)}, bf16[32,4,16,128]{3,2,1,0:T(8,128)(2,1)}, u32[]{:S(2)}, u32[]{:S(2)}) collective-permute-start(bf16[32,4,16,128]{3,2,1,0:T(8,128)(2,1)} %get-tuple-element.13), channel_id=1, source_target_pairs={{0,3},{1,0},{2,1},{3,2},{4,7},{5,4},{6,5},{7,6},{8,11},{9,8},{10,9... | collective-permute-start | bytes 1572872 | tf_op jit(solution)/shard_map/ppermute | solution.py:45
  6.2 24.9 %collective-permute-start.5 = (bf16[32,4,16,128]{3,2,1,0:T(8,128)(2,1)}, bf16[32,4,16,128]{3,2,1,0:T(8,128)(2,1)}, u32[]{:S(2)}, u32[]{:S(2)}) collective-permute-start(bf16[32,4,16,128]{3,2,1,0:T(8,128)(2,1)} %get-tuple-element.16), channel_id=1, source_target_pairs={{0,2},{1,3},{2,0},{3,1},{4,6},{5,7},{6,4},{7,5},{8,10},{9,11},{10,... | collective-permute-start | bytes 1572872 | tf_op jit(solution)/shard_map/ppermute | solution.py:45
  6.8 26.5 %collective-permute-start.4 = (bf16[32,4,16,128]{3,2,1,0:T(8,128)(2,1)}, bf16[32,4,16,128]{3,2,1,0:T(8,128)(2,1)}, u32[]{:S(2)}, u32[]{:S(2)}) collective-permute-start(bf16[32,4,16,128]{3,2,1,0:T(8,128)(2,1)} %get-tuple-element.14), channel_id=1, source_target_pairs={{0,1},{1,2},{2,3},{3,0},{4,5},{5,6},{6,7},{7,4},{8,9},{9,10},{10,1... | collective-permute-start | bytes 1572872 | tf_op jit(solution)/shard_map/ppermute | solution.py:45
  8.5 35.2 %collective-permute-start.2 = (bf16[32,4,16,128]{3,2,1,0:T(8,128)(2,1)}, bf16[32,4,16,128]{3,2,1,0:T(8,128)(2,1)S(1)}, u32[]{:S(2)}, u32[]{:S(2)}) collective-permute-start(bf16[32,4,16,128]{3,2,1,0:T(8,128)(2,1)} %get-tuple-element.21), channel_id=1, source_target_pairs={{0,3},{1,0},{2,1},{3,2},{4,7},{5,4},{6,5},{7,6},{8,11},{9,8},{10,9... | collective-permute-start | bytes 1572872 | tf_op jit(solution)/shard_map/ppermute | solution.py:45
  10.0 43.3 %collective-permute-start.1 = (bf16[32,4,16,128]{3,2,1,0:T(8,128)(2,1)}, bf16[32,4,16,128]{3,2,1,0:T(8,128)(2,1)S(1)}, u32[]{:S(2)}, u32[]{:S(2)}) collective-permute-start(bf16[32,4,16,128]{3,2,1,0:T(8,128)(2,1)} %get-tuple-element.24), channel_id=1, source_target_pairs={{0,2},{1,3},{2,0},{3,1},{4,6},{5,7},{6,4},{7,5},{8,10},{9,11},{10,... | collective-permute-start | bytes 1572872 | tf_op jit(solution)/shard_map/ppermute | solution.py:45
  18.7 35.7 %collective-permute-start = (bf16[32,4,16,128]{3,2,1,0:T(8,128)(2,1)}, bf16[32,4,16,128]{3,2,1,0:T(8,128)(2,1)}, u32[]{:S(2)}, u32[]{:S(2)}) collective-permute-start(bf16[32,4,16,128]{3,2,1,0:T(8,128)(2,1)} %get-tuple-element.22), channel_id=1, source_target_pairs={{0,1},{1,2},{2,3},{3,0},{4,5},{5,6},{6,7},{7,4},{8,9},{9,10},{10,1... | collective-permute-start | bytes 1572872 | tf_op jit(solution)/shard_map/ppermute | solution.py:45
  38.9 3.6 %copy-start.4 = (f32[4,64]{1,0:T(4,128)S(1)}, f32[4,64]{1,0:T(4,128)}, u32[]{:S(2)}) copy-start(f32[4,64]{1,0:T(4,128)} %param.7) | copy-start | bytes 3076
  42.5 22.3 %collective-permute-start.7 = (bf16[64,4,16,128]{3,2,1,0:T(8,128)(2,1)}, bf16[64,4,16,128]{3,2,1,0:T(8,128)(2,1)}, u32[]{:S(2)}, u32[]{:S(2)}) collective-permute-start(bf16[64,4,16,128]{3,2,1,0:T(8,128)(2,1)} %get-tuple-element.11), channel_id=1, source_target_pairs={{0,1},{1,0},{2,3},{3,2},{4,5},{5,4},{6,7},{7,6},{8,9},{9,8},{10,11... | collective-permute-start | bytes 3145736 | tf_op jit(solution)/shard_map/ppermute | solution.py:247
  60.9 3.7 %copy-start.2 = (f32[4,64]{1,0:T(4,128)S(1)}, f32[4,64]{1,0:T(4,128)}, u32[]{:S(2)}) copy-start(f32[4,64]{1,0:T(4,128)} %param.9) | copy-start | bytes 3076
  60.9 3.7 %copy-start.3 = (f32[4,64]{1,0:T(4,128)S(1)}, f32[4,64]{1,0:T(4,128)}, u32[]{:S(2)}) copy-start(f32[4,64]{1,0:T(4,128)} %param.8) | copy-start | bytes 3076
  64.6 13.4 %collective-permute-start.3 = (bf16[64,4,16,128]{3,2,1,0:T(8,128)(2,1)}, bf16[64,4,16,128]{3,2,1,0:T(8,128)(2,1)S(1)}, u32[]{:S(2)}, u32[]{:S(2)}) collective-permute-start(bf16[64,4,16,128]{3,2,1,0:T(8,128)(2,1)} %get-tuple-element.19), channel_id=1, source_target_pairs={{0,1},{1,0},{2,3},{3,2},{4,5},{5,4},{6,7},{7,6},{8,9},{9,8},{10,11... | collective-permute-start | bytes 3145736 | tf_op jit(solution)/shard_map/ppermute | solution.py:247
  67.1 17.8 %collective-permute-start.8 = (bf16[64,1,32,128]{3,2,1,0:T(8,128)(2,1)S(1)}, bf16[64,1,32,128]{3,2,1,0:T(8,128)(2,1)S(1)}, u32[]{:S(2)}, u32[]{:S(2)}) collective-permute-start(bf16[64,1,32,128]{3,2,1,0:T(8,128)(2,1)S(1)} %get-tuple-element.7), channel_id=1, source_target_pairs={{4,0},{8,4},{12,8},{16,12},{20,16},{24,20},{28,24},{5,1},{9,5},{13... | collective-permute-start | bytes 1572872 | tf_op jit(solution)/shard_map/ppermute | solution.py:24
  68.4 26.2 %collective-permute-start.9 = (bf16[64,1,32,128]{3,2,1,0:T(8,128)(2,1)S(1)}, bf16[64,1,32,128]{3,2,1,0:T(8,128)(2,1)S(1)}, u32[]{:S(2)}, u32[]{:S(2)}) collective-permute-start(bf16[64,1,32,128]{3,2,1,0:T(8,128)(2,1)S(1)} %get-tuple-element.8), channel_id=1, source_target_pairs={{0,4},{4,8},{8,12},{12,16},{16,20},{20,24},{24,28},{1,5},{5,9},{9,... | collective-permute-start | bytes 1572872 | tf_op jit(solution)/shard_map/ppermute | solution.py:22
  73.0 6.3 %collective-permute-start.10 = (bf16[64,4,1,128]{3,2,1,0:T(2,128)(2,1)S(1)}, bf16[64,4,1,128]{3,2,1,0:T(2,128)(2,1)S(1)}, u32[]{:S(2)}, u32[]{:S(2)}) collective-permute-start(bf16[64,4,1,128]{3,2,1,0:T(2,128)(2,1)S(1)} %slice.89), channel_id=1, source_target_pairs={{0,2},{1,3},{4,6},{5,7},{8,10},{9,11},{12,14},{13,15},{16,18},{17,... | collective-permute-start | bytes 196616 | tf_op jit(solution)/shard_map/ppermute | solution.py:247
  76.5 7.0 %collective-permute-start.11 = (bf16[64,4,1,128]{3,2,1,0:T(2,128)(2,1)S(1)}, bf16[64,4,1,128]{3,2,1,0:T(2,128)(2,1)S(1)}, u32[]{:S(2)}, u32[]{:S(2)}) collective-permute-start(bf16[64,4,1,128]{3,2,1,0:T(2,128)(2,1)S(1)} %slice.90), channel_id=1, source_target_pairs={{2,0},{3,1},{6,4},{7,5},{10,8},{11,9},{14,12},{15,13},{18,16},{19,... | collective-permute-start | bytes 196616 | tf_op jit(solution)/shard_map/ppermute | solution.py:247
  117.0 1.9 %copy-start = (f32[64,64,256]{2,1,0:T(8,128)}, f32[64,64,256]{2,1,0:T(8,128)S(1)}, u32[]{:S(2)}) copy-start(f32[64,64,256]{2,1,0:T(8,128)S(1)} %pad_maximum_fusion.1) | copy-start | bytes 12582916
  119.1 25.2 %collective-permute-start.12 = (bf16[2048,256]{1,0:T(8,128)(2,1)S(1)}, bf16[2048,256]{1,0:T(8,128)(2,1)S(1)}, u32[]{:S(2)}, u32[]{:S(2)}) collective-permute-start(bf16[2048,256]{1,0:T(8,128)(2,1)S(1)} %fusion.10), channel_id=1, source_target_pairs={{0,2},{1,3},{2,0},{3,1},{4,6},{5,7},{6,4},{7,5},{8,10},{9,11},{10,... | collective-permute-start | bytes 3145736 | tf_op jit(solution)/shard_map/ppermute | solution.py:247
  147.1 31.1 %all-to-all-start = ((bf16[8,256,256]{2,1,0:T(8,128)(2,1)}), bf16[8,256,256]{2,1,0:T(8,128)(2,1)S(1)}, u32[]{:S(2)}, u32[]{:S(2)}) async-start(bf16[8,256,256]{2,1,0:T(8,128)(2,1)} %bitcast.14), calls=%async_computation | async-start | bytes 2097152 | tf_op jit(solution)/shard_map/all_to_all | solution.py:329

commit v10 on v7

--- a/solution.py
+++ b/solution.py
@@ -80,9 +80,12 @@
     width = piece_refs[0].shape[1]
     lane = lax.broadcasted_iota(jnp.int32, (1, width), 1) % 128
     low = lane < 64
+    packed = piece_refs[0].shape[0] % 16 == 0
     rows = []
     for piece_ref in piece_refs:
-        x = piece_ref[...].astype(jnp.float32)
+        x = piece_ref[...]
+        if not packed:
+            x = x.astype(jnp.float32)
         swapped = jnp.where(low, pltpu.roll(x, width - 64, 1), -pltpu.roll(x, 64, 1))
         rows.append(x)
         rows.append(swapped)
@@ -97,7 +100,7 @@
     count = len(pieces)
     angles, total = pieces[0].shape
     waves = table.shape[0]
-    block = math.gcd(total, 1024)
+    block = math.gcd(total, 4096)
     grid = (total // block,)
     in_specs = [pl.BlockSpec((waves, table.shape[1]), lambda j: (0, 0))]
     in_specs += [pl.BlockSpec((angles, block), lambda j: (0, j)) for _ in pieces]
@@ -241,6 +244,8 @@
         )
         gram_terms = complex_blocks(product, snap_count).reshape(half_waves * snap_count, 2 * columns)
         shares = gram_terms.astype(jnp.bfloat16).reshape(axial_count, half_rows, 2 * columns)
+        if half + 1 < halves:
+            shares, direct_all, weighted_all = lax.optimization_barrier((shares, direct_all, weighted_all))
         shares = lax.all_to_all(shares, "gx", split_axis=0, concat_axis=0, tiled=True)
         own_parts.append(jnp.sum(shares.astype(jnp.float32), axis=0))
     own_rows = jnp.concatenate(own_parts, axis=0)

time: 172 us -> 161 us (0.936)
  Pallas kernels: 13.9 us -> 7.14 us
    pallas_call x2, Pallas kernels: 13.9 us -> 7.14 us  [dft(): pl.pallas_call(functools.partial(dft_kernel, count=count, weighted=weight...]
    all_to_all x2, waiting for transfers between devices: 21.4 us -> 14.7 us  [local(): lax.all_to_all(shares, 'gx', split_axis=0, concat_axis=0, tiled=True)]
    ppermute x2, waiting for transfers between devices: 6.69 us -> 10.8 us  [padded_2(): lax.ppermute(tail, axis, [(i, (i + 1) % count) for i in range(ends)])]
    ppermute x2, waiting for transfers between devices: 0.01 us -> 3.58 us  [padded_2(): lax.ppermute(head, axis, [((i + 1) % count, i) for i in range(ends)])]
    ppermute x18, waiting for transfers between devices: 30.9 us -> 28.3 us  [exchange(): lax.ppermute(piece, axis, [(j, (j + shift) % count) for j in range(count)])]
    all_to_all x2, starting transfers between devices: 9.43 us -> 11.3 us  [local(): lax.all_to_all(shares, 'gx', split_axis=0, concat_axis=0, tiled=True)]
    unnamed x30 -> x18, local copies, waits for them, and re-layouts: 15.7 us -> 15.6 us
  transfers between devices with their start and end apart: 24 -> 24, of which waited for: 7 -> 11; matrix products, arithmetic and copies ran while one was open for 23% -> 20% of each run, Pallas kernels for 8% -> 4%
where the time goes in v10:
time: 161 us; the launch traced here: 160 us
  waiting for transfers between devices  57.3 us (36%)
  starting transfers between devices  41.7 us (26%)
  local copies, waits for them, and re-layouts  25.6 us (16%)
  other arithmetic  16.7 us (10%)
  blocking collectives  9.9 us (6%)
  Pallas kernels  7.14 us (4%)
    ppermute x18, waiting for transfers between devices, exchange(): lax.ppermute(piece, axis, [(j, (j + shift) % count) for j in range(count)])  28.3 us
    ppermute x18, starting transfers between devices, exchange(): lax.ppermute(piece, axis, [(j, (j + shift) % count) for j in range(count)])  18.1 us
    unnamed x18, local copies, waits for them, and re-layouts  15.6 us
    all_to_all x2, waiting for transfers between devices, local(): lax.all_to_all(shares, 'gx', split_axis=0, concat_axis=0, tiled=True)  14.7 us
    all_to_all x2, starting transfers between devices, local(): lax.all_to_all(shares, 'gx', split_axis=0, concat_axis=0, tiled=True)  11.3 us
    ppermute x2, waiting for transfers between devices, padded_2(): lax.ppermute(tail, axis, [(i, (i + 1) % count) for i in range(ends)])  10.8 us
    all_to_all x1, blocking collectives, gather_small(): return lax.all_to_all(copies, axis, split_axis=0, concat_axis=0, tiled=True)  9.9 us
    ppermute x2, starting transfers between devices, padded_2(): lax.ppermute(tail, axis, [(i, (i + 1) % count) for i in range(ends)])  9.77 us
  transfers between devices with their start and end apart: 24, of which 11 were waited for; matrix products, arithmetic and copies ran while one was open for 20% of the time, Pallas kernels for 4%

profile of v10, /device:TPU:0, one launch (start us, length us, event | category | flops | bytes accessed | tf_op | source)
XLA Modules:
  0.0 160.4 jit_solution(13435807135720221406)
XLA Ops:
  0.7 3.1 %constant_dynamic-slice_fusion.9 = (bf16[32,4,16,128]{3,2,1,0:T(8,128)(2,1)}, bf16[32,4,16,128]{3,2,1,0:T(8,128)(2,1)}, bf16[32,4,16,128]{3,2,1,0:T(8,128)(2,1)S(1)}, bf16[32,4,16,128]{3,2,1,0:T(8,128)(2,1)}) fusion(bf16[32,4,64,128]{3,2,1,0:T(8,128)(2,1)} %param.5, s32[]{:T(128)S(6)} %select_n.300, s32[]{:T(128)S(6)} %select_n.296, s32[]{:T(128)S(6)} %select_n.294, ...), kind=kLoop, calls=%fused_computation.155 | loop fusion | bytes 4194320 | tf_op jit(solution)/shard_map/dynamic_slice | solution.py:45
  3.8 2.4 %collective-permute-start.8 = (bf16[32,4,16,128]{3,2,1,0:T(8,128)(2,1)}, bf16[32,4,16,128]{3,2,1,0:T(8,128)(2,1)S(1)}, u32[]{:S(2)}, u32[]{:S(2)}) collective-permute-start(bf16[32,4,16,128]{3,2,1,0:T(8,128)(2,1)} %get-tuple-element.29), channel_id=1, source_target_pairs={{0,3},{1,0},{2,1},{3,2},{4,7},{5,4},{6,5},{7,6},{8,11},{9,8},{10,9... | collective-permute-start | bytes 1572872 | tf_op jit(solution)/shard_map/ppermute | solution.py:47
  7.0 1.5 constant_dynamic-slice_fusion.17
  8.5 1.5 collective-permute-start.2
  10.0 1.5 collective-permute-start.1
  13.3 5.4 %collective-permute-done.8 = bf16[32,4,16,128]{3,2,1,0:T(8,128)(2,1)S(1)} collective-permute-done((bf16[32,4,16,128]{3,2,1,0:T(8,128)(2,1)}, bf16[32,4,16,128]{3,2,1,0:T(8,128)(2,1)S(1)}, u32[]{:S(2)}, u32[]{:S(2)}) %collective-permute-start.8) | collective-permute-done | bytes 524320 | tf_op jit(solution)/shard_map/ppermute | solution.py:47
  18.8 1.1 collective-permute-start
  19.9 1.2 copy.45
  21.9 1.1 copy.42
  23.0 8.0 %collective-permute-done.7 = bf16[32,4,16,128]{3,2,1,0:T(8,128)(2,1)S(1)} collective-permute-done((bf16[32,4,16,128]{3,2,1,0:T(8,128)(2,1)}, bf16[32,4,16,128]{3,2,1,0:T(8,128)(2,1)S(1)}, u32[]{:S(2)}, u32[]{:S(2)}) %collective-permute-start.7) | collective-permute-done | bytes 524320 | tf_op jit(solution)/shard_map/ppermute | solution.py:47
  31.0 1.2 copy.43
  32.2 1.1 copy.44
  33.3 3.5 %shard_map.77 = bf16[128,8192]{1,0:T(8,128)(2,1)} custom-call(bf16[128,256]{1,0:T(8,128)(2,1)} %concatenate.46.refs_0_, bf16[32,8192]{1,0:T(8,128)(2,1)} %bitcast.123, bf16[32,8192]{1,0:T(8,128)(2,1)} %bitcast.129, bf16[32,8192]{1,0:T(8,128)(2,1)} %bitcast.127, bf16[32,8192]{1,0:T(8,128)(2,1)} %bitcast.125), custom_call_target="tpu_custom_call" | custom-call | tf_op jit(solution)/shard_map/pallas_call | solution.py:111
  36.8 2.2 %copy.33 = bf16[16,8,64,128]{3,2,1,0:T(8,128)(2,1)S(1)} copy(bf16[16,8,64,128]{3,1,2,0:T(8,128)(2,1)} %bitcast.117) | data formatting | bytes 4194304
  40.0 1.4 collective-permute-start.10
  41.4 1.8 %collective-permute-start.11 = (bf16[16,4,16,128]{3,2,1,0:T(8,128)(2,1)}, bf16[16,4,16,128]{3,2,1,0:T(8,128)(2,1)}, u32[]{:S(2)}, u32[]{:S(2)}) collective-permute-start(bf16[16,4,16,128]{3,2,1,0:T(8,128)(2,1)} %get-tuple-element.26), channel_id=1, source_target_pairs={{0,3},{1,0},{2,1},{3,2},{4,7},{5,4},{6,5},{7,6},{8,11},{9,8},{10,9... | collective-permute-start | bytes 786440 | tf_op jit(solution)/shard_map/ppermute | solution.py:47
  43.1 1.1 copy.49
  44.4 2.2 %copy.46 = bf16[4,8,64,128]{3,1,2,0:T(8,128)(2,1)} copy(bf16[4,8,64,128]{3,2,1,0:T(8,128)(2,1)} %bitcast.50) | data formatting | bytes 1048576
  46.6 6.9 %collective-permute-done.1 = bf16[32,4,16,128]{3,2,1,0:T(8,128)(2,1)S(1)} collective-permute-done((bf16[32,4,16,128]{3,2,1,0:T(8,128)(2,1)}, bf16[32,4,16,128]{3,2,1,0:T(8,128)(2,1)S(1)}, u32[]{:S(2)}, u32[]{:S(2)}) %collective-permute-start.1) | collective-permute-done | bytes 524320 | tf_op jit(solution)/shard_map/ppermute | solution.py:47
  53.5 1.1 copy.47
  54.6 2.2 %copy.48 = bf16[4,8,64,128]{3,1,2,0:T(8,128)(2,1)} copy(bf16[4,8,64,128]{3,2,1,0:T(8,128)(2,1)} %bitcast.44) | data formatting | bytes 1048576
  57.5 3.7 %shard_map.76 = bf16[128,8192]{1,0:T(8,128)(2,1)} custom-call(bf16[128,256]{1,0:T(8,128)(2,1)} %concatenate.46.refs_0_, bf16[32,8192]{1,0:T(8,128)(2,1)} %bitcast.122, bf16[32,8192]{1,0:T(8,128)(2,1)} %bitcast.128, bf16[32,8192]{1,0:T(8,128)(2,1)} %bitcast.126, bf16[32,8192]{1,0:T(8,128)(2,1)} %bitcast.124, f32[1,8192]{1,0:T(1,128)} %bitcast.142), custom_call_target="tpu_custom_call" | custom-call | tf_op jit(solution)/shard_map/pallas_call | solution.py:111
  61.1 2.2 %copy.28 = bf16[16,8,64,128]{3,2,1,0:T(8,128)(2,1)S(1)} copy(bf16[16,8,64,128]{3,1,2,0:T(8,128)(2,1)} %bitcast.114) | data formatting | bytes 4194304
  63.6 1.4 collective-permute-start.4
  65.1 1.4 collective-permute-start.5
  66.4 1.2 pad_maximum_fusion.20
  68.3 1.3 collective-permute-start.12
  69.6 4.7 %collective-permute-start.13 = (bf16[16,1,64,128]{3,2,1,0:T(8,128)(2,1)S(1)}, bf16[16,1,64,128]{3,2,1,0:T(8,128)(2,1)S(1)}, u32[]{:S(2)}, u32[]{:S(2)}) collective-permute-start(bf16[16,1,64,128]{3,2,1,0:T(8,128)(2,1)S(1)} %get-tuple-element.54), channel_id=1, source_target_pairs={{0,4},{4,8},{8,12},{12,16},{16,20},{20,24},{24,28},{1,5},{5,9},{9,... | collective-permute-start | bytes 786440 | tf_op jit(solution)/shard_map/ppermute | solution.py:22
  74.4 2.3 %collective-permute-done.5 = bf16[16,4,16,128]{3,2,1,0:T(8,128)(2,1)S(1)} collective-permute-done((bf16[16,4,16,128]{3,2,1,0:T(8,128)(2,1)S(1)}, bf16[16,4,16,128]{3,2,1,0:T(8,128)(2,1)S(1)}, u32[]{:S(2)}, u32[]{:S(2)}) %collective-permute-start.5) | collective-permute-done | bytes 262176 | tf_op jit(solution)/shard_map/ppermute | solution.py:47
  77.6 5.5 %collective-permute-done.13 = bf16[16,1,64,128]{3,2,1,0:T(8,128)(2,1)S(1)} collective-permute-done((bf16[16,1,64,128]{3,2,1,0:T(8,128)(2,1)S(1)}, bf16[16,1,64,128]{3,2,1,0:T(8,128)(2,1)S(1)}, u32[]{:S(2)}, u32[]{:S(2)}) %collective-permute-start.13) | collective-permute-done | bytes 262176 | tf_op jit(solution)/shard_map/ppermute | solution.py:22
  83.1 2.8 %fusion.6 = bf16[16,4,64,128]{3,2,1,0:T(8,128)(2,1)S(1)} fusion(f32[16,4,64,128]{3,2,1,0:T(8,128)S(1)} %get-tuple-element.56, bf16[16,1,64,128]{3,2,1,0:T(8,128)(2,1)S(1)} %collective-permute-done.13, bf16[16,4,16,128]{3,2,1,0:T(8,128)(2,1)S(1)} %get-tuple-element.58, bf16[16,4,16,128]{3,2,1,0:T(8,128)(2,1)S(1)} %get-tuple-element.59, ...), kind=kLoop, calls=%fused_computation.14 | loop fusion | flops 17301504 | bytes 4724736 | tf_op jit(solution)/shard_map/convert_element_type | solution.py:237
  87.4 1.2 pad_maximum_fusion.26
  89.7 1.3 collective-permute-start.18
  91.0 1.4 collective-permute-start.19
  93.5 5.8 %all-to-all-start = ((bf16[8,128,256]{2,1,0:T(8,128)(2,1)}), bf16[8,128,256]{2,1,0:T(8,128)(2,1)S(1)}, u32[]{:S(2)}, u32[]{:S(2)}) async-start(bf16[8,128,256]{2,1,0:T(8,128)(2,1)} %bitcast.19), calls=%async_computation | async-start | bytes 1048576 | tf_op jit(solution)/shard_map/all_to_all | solution.py:249
  99.2 1.2 collective-permute-start.16
  100.4 3.0 %collective-permute-done.19 = bf16[16,4,16,128]{3,2,1,0:T(8,128)(2,1)} collective-permute-done((bf16[16,4,16,128]{3,2,1,0:T(8,128)(2,1)S(1)}, bf16[16,4,16,128]{3,2,1,0:T(8,128)(2,1)}, u32[]{:S(2)}, u32[]{:S(2)}) %collective-permute-start.19) | collective-permute-done | bytes 262176 | tf_op jit(solution)/shard_map/ppermute | solution.py:47
  103.4 1.1 pad_maximum_fusion.24
  105.2 1.3 collective-permute-start.20
  106.5 5.0 %collective-permute-start.21 = (bf16[16,1,64,128]{3,2,1,0:T(8,128)(2,1)S(1)}, bf16[16,1,64,128]{3,2,1,0:T(8,128)(2,1)S(1)}, u32[]{:S(2)}, u32[]{:S(2)}) collective-permute-start(bf16[16,1,64,128]{3,2,1,0:T(8,128)(2,1)S(1)} %get-tuple-element.42), channel_id=1, source_target_pairs={{0,4},{4,8},{8,12},{12,16},{16,20},{20,24},{24,28},{1,5},{5,9},{9,... | collective-permute-start | bytes 786440 | tf_op jit(solution)/shard_map/ppermute | solution.py:22
  111.5 2.6 %collective-permute-done.16 = bf16[16,4,16,128]{3,2,1,0:T(8,128)(2,1)S(1)} collective-permute-done((bf16[16,4,16,128]{3,2,1,0:T(8,128)(2,1)S(1)}, bf16[16,4,16,128]{3,2,1,0:T(8,128)(2,1)S(1)}, u32[]{:S(2)}, u32[]{:S(2)}) %collective-permute-start.16) | collective-permute-done | bytes 262176 | tf_op jit(solution)/shard_map/ppermute | solution.py:47
  114.6 3.2 %collective-permute-done.20 = bf16[16,1,64,128]{3,2,1,0:T(8,128)(2,1)S(1)} collective-permute-done((bf16[16,1,64,128]{3,2,1,0:T(8,128)(2,1)S(1)}, bf16[16,1,64,128]{3,2,1,0:T(8,128)(2,1)S(1)}, u32[]{:S(2)}, u32[]{:S(2)}) %collective-permute-start.20) | collective-permute-done | bytes 262176 | tf_op jit(solution)/shard_map/ppermute | solution.py:24
  117.8 5.2 %collective-permute-done.21 = bf16[16,1,64,128]{3,2,1,0:T(8,128)(2,1)S(1)} collective-permute-done((bf16[16,1,64,128]{3,2,1,0:T(8,128)(2,1)S(1)}, bf16[16,1,64,128]{3,2,1,0:T(8,128)(2,1)S(1)}, u32[]{:S(2)}, u32[]{:S(2)}) %collective-permute-start.21) | collective-permute-done | bytes 262176 | tf_op jit(solution)/shard_map/ppermute | solution.py:22
  123.1 2.8 %fusion.13 = bf16[16,4,64,128]{3,2,1,0:T(8,128)(2,1)S(1)} fusion(f32[16,4,64,128]{3,2,1,0:T(8,128)S(1)} %get-tuple-element.44, bf16[16,1,64,128]{3,2,1,0:T(8,128)(2,1)S(1)} %collective-permute-done.21, bf16[16,4,16,128]{3,2,1,0:T(8,128)(2,1)S(1)} %get-tuple-element.46, bf16[16,4,16,128]{3,2,1,0:T(8,128)(2,1)S(1)} %get-tuple-element.47, ...), kind=kLoop, calls=%fused_computation.21 | loop fusion | flops 17301504 | bytes 4724736 | tf_op jit(solution)/shard_map/convert_element_type | solution.py:237
  127.4 1.2 pad_maximum_fusion.27
  128.6 5.5 %all-to-all-start.1 = ((bf16[8,128,256]{2,1,0:T(8,128)(2,1)}), bf16[8,128,256]{2,1,0:T(8,128)(2,1)S(1)}, u32[]{:S(2)}, u32[]{:S(2)}) async-start(bf16[8,128,256]{2,1,0:T(8,128)(2,1)} %bitcast.38), calls=%async_computation.1 | async-start | bytes 1048576 | tf_op jit(solution)/shard_map/all_to_all | solution.py:249
  134.1 14.7 %all-to-all-done.1 = bf16[8,128,256]{2,1,0:T(8,128)(2,1)S(1)} async-done(((bf16[8,128,256]{2,1,0:T(8,128)(2,1)}), bf16[8,128,256]{2,1,0:T(8,128)(2,1)S(1)}, u32[]{:S(2)}, u32[]{:S(2)}) %all-to-all-start.1) | async-done | bytes 524320 | tf_op jit(solution)/shard_map/all_to_all | solution.py:249
  149.1 9.9 %all_to_all.16 = f32[8,1,32]{2,1,0:T(1,128)S(1)} all-to-all(f32[8,1,32]{2,1,0:T(1,128)S(1)} %broadcast_in_dim.5), channel_id=1, replica_groups=mesh['gx'=8,'ka'=4] {'gx'}, dimensions={0} | all-to-all | bytes 2048 | tf_op jit(solution)/shard_map/all_to_all | solution.py:34
  (84 shorter events, 14.9 us)
Async XLA Ops:
  0.7 6.3 %copy-start = (bf16[32,4,64,128]{3,2,1,0:T(8,128)(2,1)S(1)}, bf16[32,4,64,128]{3,2,1,0:T(8,128)(2,1)}, u32[]{:S(2)}) copy-start(bf16[32,4,64,128]{3,2,1,0:T(8,128)(2,1)} %param.6) | copy-start | bytes 6291460
  3.8 14.9 %collective-permute-start.8 = (bf16[32,4,16,128]{3,2,1,0:T(8,128)(2,1)}, bf16[32,4,16,128]{3,2,1,0:T(8,128)(2,1)S(1)}, u32[]{:S(2)}, u32[]{:S(2)}) collective-permute-start(bf16[32,4,16,128]{3,2,1,0:T(8,128)(2,1)} %get-tuple-element.29), channel_id=1, source_target_pairs={{0,3},{1,0},{2,1},{3,2},{4,7},{5,4},{6,5},{7,6},{8,11},{9,8},{10,9... | collective-permute-start | bytes 1572872 | tf_op jit(solution)/shard_map/ppermute | solution.py:47
  6.2 24.8 %collective-permute-start.7 = (bf16[32,4,16,128]{3,2,1,0:T(8,128)(2,1)}, bf16[32,4,16,128]{3,2,1,0:T(8,128)(2,1)S(1)}, u32[]{:S(2)}, u32[]{:S(2)}) collective-permute-start(bf16[32,4,16,128]{3,2,1,0:T(8,128)(2,1)} %get-tuple-element.32), channel_id=1, source_target_pairs={{0,2},{1,3},{2,0},{3,1},{4,6},{5,7},{6,4},{7,5},{8,10},{9,11},{10,... | collective-permute-start | bytes 1572872 | tf_op jit(solution)/shard_map/ppermute | solution.py:47
  6.8 25.4 %collective-permute-start.6 = (bf16[32,4,16,128]{3,2,1,0:T(8,128)(2,1)}, bf16[32,4,16,128]{3,2,1,0:T(8,128)(2,1)S(1)}, u32[]{:S(2)}, u32[]{:S(2)}) collective-permute-start(bf16[32,4,16,128]{3,2,1,0:T(8,128)(2,1)} %get-tuple-element.30), channel_id=1, source_target_pairs={{0,1},{1,2},{2,3},{3,0},{4,5},{5,6},{6,7},{7,4},{8,9},{9,10},{10,1... | collective-permute-start | bytes 1572872 | tf_op jit(solution)/shard_map/ppermute | solution.py:47
  8.5 32.9 %collective-permute-start.2 = (bf16[32,4,16,128]{3,2,1,0:T(8,128)(2,1)}, bf16[32,4,16,128]{3,2,1,0:T(8,128)(2,1)}, u32[]{:S(2)}, u32[]{:S(2)}) collective-permute-start(bf16[32,4,16,128]{3,2,1,0:T(8,128)(2,1)} %get-tuple-element.37), channel_id=1, source_target_pairs={{0,3},{1,0},{2,1},{3,2},{4,7},{5,4},{6,5},{7,6},{8,11},{9,8},{10,9... | collective-permute-start | bytes 1572872 | tf_op jit(solution)/shard_map/ppermute | solution.py:47
  10.0 43.5 %collective-permute-start.1 = (bf16[32,4,16,128]{3,2,1,0:T(8,128)(2,1)}, bf16[32,4,16,128]{3,2,1,0:T(8,128)(2,1)S(1)}, u32[]{:S(2)}, u32[]{:S(2)}) collective-permute-start(bf16[32,4,16,128]{3,2,1,0:T(8,128)(2,1)} %get-tuple-element.40), channel_id=1, source_target_pairs={{0,2},{1,3},{2,0},{3,1},{4,6},{5,7},{6,4},{7,5},{8,10},{9,11},{10,... | collective-permute-start | bytes 1572872 | tf_op jit(solution)/shard_map/ppermute | solution.py:47
  18.8 35.9 %collective-permute-start = (bf16[32,4,16,128]{3,2,1,0:T(8,128)(2,1)}, bf16[32,4,16,128]{3,2,1,0:T(8,128)(2,1)}, u32[]{:S(2)}, u32[]{:S(2)}) collective-permute-start(bf16[32,4,16,128]{3,2,1,0:T(8,128)(2,1)} %get-tuple-element.38), channel_id=1, source_target_pairs={{0,1},{1,2},{2,3},{3,0},{4,5},{5,6},{6,7},{7,4},{8,9},{9,10},{10,1... | collective-permute-start | bytes 1572872 | tf_op jit(solution)/shard_map/ppermute | solution.py:47
  39.0 4.2 %copy-start.2 = (f32[4,64]{1,0:T(4,128)S(1)}, f32[4,64]{1,0:T(4,128)}, u32[]{:S(2)}) copy-start(f32[4,64]{1,0:T(4,128)} %param.7) | copy-start | bytes 3076
  39.0 4.2 %copy-start.3 = (f32[4,64]{1,0:T(4,128)S(1)}, f32[4,64]{1,0:T(4,128)}, u32[]{:S(2)}) copy-start(f32[4,64]{1,0:T(4,128)} %param.8) | copy-start | bytes 3076
  40.0 25.1 %collective-permute-start.9 = (bf16[16,4,16,128]{3,2,1,0:T(8,128)(2,1)}, bf16[16,4,16,128]{3,2,1,0:T(8,128)(2,1)}, u32[]{:S(2)}, u32[]{:S(2)}) collective-permute-start(bf16[16,4,16,128]{3,2,1,0:T(8,128)(2,1)} %get-tuple-element.28), channel_id=1, source_target_pairs={{0,1},{1,2},{2,3},{3,0},{4,5},{5,6},{6,7},{7,4},{8,9},{9,10},{10,1... | collective-permute-start | bytes 786440 | tf_op jit(solution)/shard_map/ppermute | solution.py:47
  40.0 26.5 %collective-permute-start.10 = (bf16[16,4,16,128]{3,2,1,0:T(8,128)(2,1)}, bf16[16,4,16,128]{3,2,1,0:T(8,128)(2,1)}, u32[]{:S(2)}, u32[]{:S(2)}) collective-permute-start(bf16[16,4,16,128]{3,2,1,0:T(8,128)(2,1)} %get-tuple-element.27), channel_id=1, source_target_pairs={{0,2},{1,3},{2,0},{3,1},{4,6},{5,7},{6,4},{7,5},{8,10},{9,11},{10,... | collective-permute-start | bytes 786440 | tf_op jit(solution)/shard_map/ppermute | solution.py:47
  41.4 25.1 %collective-permute-start.11 = (bf16[16,4,16,128]{3,2,1,0:T(8,128)(2,1)}, bf16[16,4,16,128]{3,2,1,0:T(8,128)(2,1)}, u32[]{:S(2)}, u32[]{:S(2)}) collective-permute-start(bf16[16,4,16,128]{3,2,1,0:T(8,128)(2,1)} %get-tuple-element.26), channel_id=1, source_target_pairs={{0,3},{1,0},{2,1},{3,2},{4,7},{5,4},{6,5},{7,6},{8,11},{9,8},{10,9... | collective-permute-start | bytes 786440 | tf_op jit(solution)/shard_map/ppermute | solution.py:47
  63.6 10.8 %collective-permute-start.3 = (bf16[16,4,16,128]{3,2,1,0:T(8,128)(2,1)S(1)}, bf16[16,4,16,128]{3,2,1,0:T(8,128)(2,1)S(1)}, u32[]{:S(2)}, u32[]{:S(2)}) collective-permute-start(bf16[16,4,16,128]{3,2,1,0:T(8,128)(2,1)S(1)} %get-tuple-element.36), channel_id=1, source_target_pairs={{0,1},{1,2},{2,3},{3,0},{4,5},{5,6},{6,7},{7,4},{8,9},{9,10},{10,1... | collective-permute-start | bytes 786440 | tf_op jit(solution)/shard_map/ppermute | solution.py:47
  63.6 10.8 %collective-permute-start.4 = (bf16[16,4,16,128]{3,2,1,0:T(8,128)(2,1)S(1)}, bf16[16,4,16,128]{3,2,1,0:T(8,128)(2,1)S(1)}, u32[]{:S(2)}, u32[]{:S(2)}) collective-permute-start(bf16[16,4,16,128]{3,2,1,0:T(8,128)(2,1)S(1)} %get-tuple-element.35), channel_id=1, source_target_pairs={{0,2},{1,3},{2,0},{3,1},{4,6},{5,7},{6,4},{7,5},{8,10},{9,11},{10,... | collective-permute-start | bytes 786440 | tf_op jit(solution)/shard_map/ppermute | solution.py:47
  65.1 11.7 %collective-permute-start.5 = (bf16[16,4,16,128]{3,2,1,0:T(8,128)(2,1)S(1)}, bf16[16,4,16,128]{3,2,1,0:T(8,128)(2,1)S(1)}, u32[]{:S(2)}, u32[]{:S(2)}) collective-permute-start(bf16[16,4,16,128]{3,2,1,0:T(8,128)(2,1)S(1)} %get-tuple-element.34), channel_id=1, source_target_pairs={{0,3},{1,0},{2,1},{3,2},{4,7},{5,4},{6,5},{7,6},{8,11},{9,8},{10,9... | collective-permute-start | bytes 786440 | tf_op jit(solution)/shard_map/ppermute | solution.py:47
  68.3 9.2 %collective-permute-start.12 = (bf16[16,1,64,128]{3,2,1,0:T(8,128)(2,1)S(1)}, bf16[16,1,64,128]{3,2,1,0:T(8,128)(2,1)S(1)}, u32[]{:S(2)}, u32[]{:S(2)}) collective-permute-start(bf16[16,1,64,128]{3,2,1,0:T(8,128)(2,1)S(1)} %get-tuple-element.53), channel_id=1, source_target_pairs={{4,0},{8,4},{12,8},{16,12},{20,16},{24,20},{28,24},{5,1},{9,5},{13... | collective-permute-start | bytes 786440 | tf_op jit(solution)/shard_map/ppermute | solution.py:24
  69.6 13.5 %collective-permute-start.13 = (bf16[16,1,64,128]{3,2,1,0:T(8,128)(2,1)S(1)}, bf16[16,1,64,128]{3,2,1,0:T(8,128)(2,1)S(1)}, u32[]{:S(2)}, u32[]{:S(2)}) collective-permute-start(bf16[16,1,64,128]{3,2,1,0:T(8,128)(2,1)S(1)} %get-tuple-element.54), channel_id=1, source_target_pairs={{0,4},{4,8},{8,12},{12,16},{16,20},{20,24},{24,28},{1,5},{5,9},{9,... | collective-permute-start | bytes 786440 | tf_op jit(solution)/shard_map/ppermute | solution.py:22
  76.9 6.2 %copy-start.1 = (f32[4,64]{1,0:T(4,128)S(1)}, f32[4,64]{1,0:T(4,128)}, u32[]{:S(2)}) copy-start(f32[4,64]{1,0:T(4,128)} %param.9) | copy-start | bytes 3076
  89.6 9.6 %collective-permute-start.17 = (bf16[16,4,16,128]{3,2,1,0:T(8,128)(2,1)}, bf16[16,4,16,128]{3,2,1,0:T(8,128)(2,1)S(1)}, u32[]{:S(2)}, u32[]{:S(2)}) collective-permute-start(bf16[16,4,16,128]{3,2,1,0:T(8,128)(2,1)} %get-tuple-element.16), channel_id=1, source_target_pairs={{0,1},{1,2},{2,3},{3,0},{4,5},{5,6},{6,7},{7,4},{8,9},{9,10},{10,1... | collective-permute-start | bytes 786440 | tf_op jit(solution)/shard_map/ppermute | solution.py:47
  89.7 10.8 %collective-permute-start.18 = (bf16[16,4,16,128]{3,2,1,0:T(8,128)(2,1)}, bf16[16,4,16,128]{3,2,1,0:T(8,128)(2,1)S(1)}, u32[]{:S(2)}, u32[]{:S(2)}) collective-permute-start(bf16[16,4,16,128]{3,2,1,0:T(8,128)(2,1)} %get-tuple-element.15), channel_id=1, source_target_pairs={{0,2},{1,3},{2,0},{3,1},{4,6},{5,7},{6,4},{7,5},{8,10},{9,11},{10,... | collective-permute-start | bytes 786440 | tf_op jit(solution)/shard_map/ppermute | solution.py:47
  91.0 12.5 %collective-permute-start.19 = (bf16[16,4,16,128]{3,2,1,0:T(8,128)(2,1)S(1)}, bf16[16,4,16,128]{3,2,1,0:T(8,128)(2,1)}, u32[]{:S(2)}, u32[]{:S(2)}) collective-permute-start(bf16[16,4,16,128]{3,2,1,0:T(8,128)(2,1)S(1)} %get-tuple-element.14), channel_id=1, source_target_pairs={{0,3},{1,0},{2,1},{3,2},{4,7},{5,4},{6,5},{7,6},{8,11},{9,8},{10,9... | collective-permute-start | bytes 786440 | tf_op jit(solution)/shard_map/ppermute | solution.py:47
  92.6 18.9 %collective-permute-start.14 = (bf16[16,4,16,128]{3,2,1,0:T(8,128)(2,1)S(1)}, bf16[16,4,16,128]{3,2,1,0:T(8,128)(2,1)S(1)}, u32[]{:S(2)}, u32[]{:S(2)}) collective-permute-start(bf16[16,4,16,128]{3,2,1,0:T(8,128)(2,1)S(1)} %get-tuple-element.20), channel_id=1, source_target_pairs={{0,1},{1,2},{2,3},{3,0},{4,5},{5,6},{6,7},{7,4},{8,9},{9,10},{10,1... | collective-permute-start | bytes 786440 | tf_op jit(solution)/shard_map/ppermute | solution.py:47
  92.7 18.9 %collective-permute-start.15 = (bf16[16,4,16,128]{3,2,1,0:T(8,128)(2,1)S(1)}, bf16[16,4,16,128]{3,2,1,0:T(8,128)(2,1)S(1)}, u32[]{:S(2)}, u32[]{:S(2)}) collective-permute-start(bf16[16,4,16,128]{3,2,1,0:T(8,128)(2,1)S(1)} %get-tuple-element.19), channel_id=1, source_target_pairs={{0,2},{1,3},{2,0},{3,1},{4,6},{5,7},{6,4},{7,5},{8,10},{9,11},{10,... | collective-permute-start | bytes 786440 | tf_op jit(solution)/shard_map/ppermute | solution.py:47
  93.5 35.1 %all-to-all-start = ((bf16[8,128,256]{2,1,0:T(8,128)(2,1)}), bf16[8,128,256]{2,1,0:T(8,128)(2,1)S(1)}, u32[]{:S(2)}, u32[]{:S(2)}) async-start(bf16[8,128,256]{2,1,0:T(8,128)(2,1)} %bitcast.19), calls=%async_computation | async-start | bytes 1048576 | tf_op jit(solution)/shard_map/all_to_all | solution.py:249
  99.2 14.9 %collective-permute-start.16 = (bf16[16,4,16,128]{3,2,1,0:T(8,128)(2,1)S(1)}, bf16[16,4,16,128]{3,2,1,0:T(8,128)(2,1)S(1)}, u32[]{:S(2)}, u32[]{:S(2)}) collective-permute-start(bf16[16,4,16,128]{3,2,1,0:T(8,128)(2,1)S(1)} %get-tuple-element.18), channel_id=1, source_target_pairs={{0,3},{1,0},{2,1},{3,2},{4,7},{5,4},{6,5},{7,6},{8,11},{9,8},{10,9... | collective-permute-start | bytes 786440 | tf_op jit(solution)/shard_map/ppermute | solution.py:47
  105.2 12.6 %collective-permute-start.20 = (bf16[16,1,64,128]{3,2,1,0:T(8,128)(2,1)S(1)}, bf16[16,1,64,128]{3,2,1,0:T(8,128)(2,1)S(1)}, u32[]{:S(2)}, u32[]{:S(2)}) collective-permute-start(bf16[16,1,64,128]{3,2,1,0:T(8,128)(2,1)S(1)} %get-tuple-element.41), channel_id=1, source_target_pairs={{4,0},{8,4},{12,8},{16,12},{20,16},{24,20},{28,24},{5,1},{9,5},{13... | collective-permute-start | bytes 786440 | tf_op jit(solution)/shard_map/ppermute | solution.py:24
  106.5 16.6 %collective-permute-start.21 = (bf16[16,1,64,128]{3,2,1,0:T(8,128)(2,1)S(1)}, bf16[16,1,64,128]{3,2,1,0:T(8,128)(2,1)S(1)}, u32[]{:S(2)}, u32[]{:S(2)}) collective-permute-start(bf16[16,1,64,128]{3,2,1,0:T(8,128)(2,1)S(1)} %get-tuple-element.42), channel_id=1, source_target_pairs={{0,4},{4,8},{8,12},{12,16},{16,20},{20,24},{24,28},{1,5},{5,9},{9,... | collective-permute-start | bytes 786440 | tf_op jit(solution)/shard_map/ppermute | solution.py:22
  128.6 20.2 %all-to-all-start.1 = ((bf16[8,128,256]{2,1,0:T(8,128)(2,1)}), bf16[8,128,256]{2,1,0:T(8,128)(2,1)S(1)}, u32[]{:S(2)}, u32[]{:S(2)}) async-start(bf16[8,128,256]{2,1,0:T(8,128)(2,1)} %bitcast.38), calls=%async_computation.1 | async-start | bytes 1048576 | tf_op jit(solution)/shard_map/all_to_all | solution.py:249

commit v11 on v10

--- a/solution.py
+++ b/solution.py
@@ -212,6 +212,10 @@
         offset = half * half_waves
         direct_modes = in_source_order(exchange(direct_all, "ka", 0, offset, half_waves), "ka", 2)
         weighted = in_source_order(exchange(weighted_all, "ka", 0, offset, half_waves), "ka", 2)
+        if half + 1 < halves:
+            direct_modes, weighted, direct_all, weighted_all = lax.optimization_barrier(
+                (direct_modes, weighted, direct_all, weighted_all)
+            )
         padded = padded_2(direct_modes, (("gx", 1),), 1)
         field_f32 = direct_modes.astype(jnp.float32)
         forward = padded[:, 2:].astype(jnp.float32)
@@ -244,8 +248,6 @@
         )
         gram_terms = complex_blocks(product, snap_count).reshape(half_waves * snap_count, 2 * columns)
         shares = gram_terms.astype(jnp.bfloat16).reshape(axial_count, half_rows, 2 * columns)
-        if half + 1 < halves:
-            shares, direct_all, weighted_all = lax.optimization_barrier((shares, direct_all, weighted_all))
         shares = lax.all_to_all(shares, "gx", split_axis=0, concat_axis=0, tiled=True)
         own_parts.append(jnp.sum(shares.astype(jnp.float32), axis=0))
     own_rows = jnp.concatenate(own_parts, axis=0)

time: 161 us -> 168 us (1.043)
  waiting for transfers between devices: 57.3 us -> 65.5 us
  starting transfers between devices: 41.7 us -> 38.2 us
    ppermute x18, waiting for transfers between devices: 28.3 us -> 39.1 us  [exchange(): lax.ppermute(piece, axis, [(j, (j + shift) % count) for j in range(count)])]
    ppermute x2, waiting for transfers between devices: 3.58 us -> 0.01 us  [padded_2(): lax.ppermute(head, axis, [((i + 1) % count, i) for i in range(ends)])]
  transfers between devices with their start and end apart: 24 -> 24, of which waited for: 11 -> 11; matrix products, arithmetic and copies ran while one was open for 20% -> 24% of each run, Pallas kernels for 4% -> 4%
where the time goes in v11:
time: 168 us; the launch traced here: 167 us
  waiting for transfers between devices  65.5 us (39%)
  starting transfers between devices  38.2 us (23%)
  local copies, waits for them, and re-layouts  26.2 us (16%)
  other arithmetic  17.9 us (11%)
  blocking collectives  9.92 us (6%)
  Pallas kernels  7.23 us (4%)
    ppermute x18, waiting for transfers between devices, exchange(): lax.ppermute(piece, axis, [(j, (j + shift) % count) for j in range(count)])  39.1 us
    ppermute x18, starting transfers between devices, exchange(): lax.ppermute(piece, axis, [(j, (j + shift) % count) for j in range(count)])  16.9 us
    unnamed x18, local copies, waits for them, and re-layouts  15.6 us
    all_to_all x2, waiting for transfers between devices, local(): lax.all_to_all(shares, 'gx', split_axis=0, concat_axis=0, tiled=True)  15.3 us
    ppermute x2, waiting for transfers between devices, padded_2(): lax.ppermute(tail, axis, [(i, (i + 1) % count) for i in range(ends)])  11.1 us
    all_to_all x2, starting transfers between devices, local(): lax.all_to_all(shares, 'gx', split_axis=0, concat_axis=0, tiled=True)  10.2 us
    all_to_all x1, blocking collectives, gather_small(): return lax.all_to_all(copies, axis, split_axis=0, concat_axis=0, tiled=True)  9.92 us
    ppermute x2, starting transfers between devices, padded_2(): lax.ppermute(tail, axis, [(i, (i + 1) % count) for i in range(ends)])  8.42 us
  transfers between devices with their start and end apart: 24, of which 11 were waited for; matrix products, arithmetic and copies ran while one was open for 24% of the time, Pallas kernels for 4%

profile of v11, /device:TPU:0, one launch (start us, length us, event | category | flops | bytes accessed | tf_op | source)
XLA Modules:
  0.0 167.2 jit_solution(14907199279038939627)
XLA Ops:
  0.7 3.1 %constant_dynamic-slice_fusion.17 = (bf16[32,4,16,128]{3,2,1,0:T(8,128)(2,1)}, bf16[32,4,16,128]{3,2,1,0:T(8,128)(2,1)}, bf16[32,4,16,128]{3,2,1,0:T(8,128)(2,1)S(1)}, bf16[32,4,16,128]{3,2,1,0:T(8,128)(2,1)}) fusion(bf16[32,4,64,128]{3,2,1,0:T(8,128)(2,1)} %param.5, s32[]{:T(128)S(6)} %select_n.300, s32[]{:T(128)S(6)} %select_n.296, s32[]{:T(128)S(6)} %select_n.294, ...), kind=kLoop, calls=%fused_computation.157 | loop fusion | bytes 4194320 | tf_op jit(solution)/shard_map/dynamic_slice | solution.py:45
  4.2 2.5 %collective-permute-start.1 = (bf16[32,4,16,128]{3,2,1,0:T(8,128)(2,1)}, bf16[32,4,16,128]{3,2,1,0:T(8,128)(2,1)S(1)}, u32[]{:S(2)}, u32[]{:S(2)}) collective-permute-start(bf16[32,4,16,128]{3,2,1,0:T(8,128)(2,1)} %get-tuple-element.42), channel_id=1, source_target_pairs={{0,2},{1,3},{2,0},{3,1},{4,6},{5,7},{6,4},{7,5},{8,10},{9,11},{10,... | collective-permute-start | bytes 1572872 | tf_op jit(solution)/shard_map/ppermute | solution.py:47
  6.8 1.4 collective-permute-start.2
  8.2 1.5 constant_dynamic-slice_fusion.10
  11.9 1.1 copy.49
  13.8 4.2 %collective-permute-done = bf16[32,4,16,128]{3,2,1,0:T(8,128)(2,1)S(1)} collective-permute-done((bf16[32,4,16,128]{3,2,1,0:T(8,128)(2,1)}, bf16[32,4,16,128]{3,2,1,0:T(8,128)(2,1)S(1)}, u32[]{:S(2)}, u32[]{:S(2)}) %collective-permute-start) | collective-permute-done | bytes 524320 | tf_op jit(solution)/shard_map/ppermute | solution.py:47
  18.1 1.1 copy.48
  19.7 1.2 copy.47
  20.9 9.7 %collective-permute-done.2 = bf16[32,4,16,128]{3,2,1,0:T(8,128)(2,1)S(1)} collective-permute-done((bf16[32,4,16,128]{3,2,1,0:T(8,128)(2,1)}, bf16[32,4,16,128]{3,2,1,0:T(8,128)(2,1)S(1)}, u32[]{:S(2)}, u32[]{:S(2)}) %collective-permute-start.2) | collective-permute-done | bytes 524320 | tf_op jit(solution)/shard_map/ppermute | solution.py:47
  30.6 1.2 copy.46
  31.8 3.5 %shard_map.76 = bf16[128,8192]{1,0:T(8,128)(2,1)} custom-call(bf16[128,256]{1,0:T(8,128)(2,1)} %concatenate.46.refs_0_, bf16[32,8192]{1,0:T(8,128)(2,1)} %bitcast.124, bf16[32,8192]{1,0:T(8,128)(2,1)} %bitcast.126, bf16[32,8192]{1,0:T(8,128)(2,1)} %bitcast.128, bf16[32,8192]{1,0:T(8,128)(2,1)} %bitcast.130), custom_call_target="tpu_custom_call" | custom-call | tf_op jit(solution)/shard_map/pallas_call | solution.py:111
  35.3 2.2 %copy.28 = bf16[16,8,64,128]{3,2,1,0:T(8,128)(2,1)S(1)} copy(bf16[16,8,64,128]{3,1,2,0:T(8,128)(2,1)} %bitcast.116) | data formatting | bytes 4194304
  37.5 1.0 dynamic-slice_bitcast_fusion.19
  38.5 2.2 %collective-permute-start.5 = (bf16[16,4,16,128]{3,2,1,0:T(8,128)(2,1)}, bf16[16,4,16,128]{3,2,1,0:T(8,128)(2,1)}, u32[]{:S(2)}, u32[]{:S(2)}) collective-permute-start(bf16[16,4,16,128]{3,2,1,0:T(8,128)(2,1)} %get-tuple-element.36), channel_id=1, source_target_pairs={{0,3},{1,0},{2,1},{3,2},{4,7},{5,4},{6,5},{7,6},{8,11},{9,8},{10,9... | collective-permute-start | bytes 786440 | tf_op jit(solution)/shard_map/ppermute | solution.py:47
  40.7 1.1 copy.45
  42.1 2.2 %copy.44 = bf16[4,8,64,128]{3,1,2,0:T(8,128)(2,1)} copy(bf16[4,8,64,128]{3,2,1,0:T(8,128)(2,1)} %bitcast.59) | data formatting | bytes 1048576
  44.2 1.1 copy.43
  45.4 7.7 %collective-permute-done.8 = bf16[32,4,16,128]{3,2,1,0:T(8,128)(2,1)} collective-permute-done((bf16[32,4,16,128]{3,2,1,0:T(8,128)(2,1)}, bf16[32,4,16,128]{3,2,1,0:T(8,128)(2,1)}, u32[]{:S(2)}, u32[]{:S(2)}) %collective-permute-start.8) | collective-permute-done | bytes 524320 | tf_op jit(solution)/shard_map/ppermute | solution.py:47
  53.1 2.2 %copy.42 = bf16[4,8,64,128]{3,1,2,0:T(8,128)(2,1)} copy(bf16[4,8,64,128]{3,2,1,0:T(8,128)(2,1)} %bitcast.65) | data formatting | bytes 1048576
  56.0 3.7 %shard_map.77 = bf16[128,8192]{1,0:T(8,128)(2,1)} custom-call(bf16[128,256]{1,0:T(8,128)(2,1)} %concatenate.46.refs_0_, bf16[32,8192]{1,0:T(8,128)(2,1)} %bitcast.123, bf16[32,8192]{1,0:T(8,128)(2,1)} %bitcast.125, bf16[32,8192]{1,0:T(8,128)(2,1)} %bitcast.127, bf16[32,8192]{1,0:T(8,128)(2,1)} %bitcast.129, f32[1,8192]{1,0:T(1,128)} %bitcast.143), custom_call_target="tpu_custom_call" | custom-call | tf_op jit(solution)/shard_map/pallas_call | solution.py:111
  59.7 2.2 %copy.33 = bf16[16,8,64,128]{3,2,1,0:T(8,128)(2,1)S(1)} copy(bf16[16,8,64,128]{3,1,2,0:T(8,128)(2,1)} %bitcast.114) | data formatting | bytes 4194304
  62.1 2.0 %collective-permute-start.11 = (bf16[16,4,16,128]{3,2,1,0:T(8,128)(2,1)S(1)}, bf16[16,4,16,128]{3,2,1,0:T(8,128)(2,1)S(1)}, u32[]{:S(2)}, u32[]{:S(2)}) collective-permute-start(bf16[16,4,16,128]{3,2,1,0:T(8,128)(2,1)S(1)} %get-tuple-element.28), channel_id=1, source_target_pairs={{0,3},{1,0},{2,1},{3,2},{4,7},{5,4},{6,5},{7,6},{8,11},{9,8},{10,9... | collective-permute-start | bytes 786440 | tf_op jit(solution)/shard_map/ppermute | solution.py:47
  64.3 1.1 pad_maximum_fusion.12
  65.4 5.3 %collective-permute-done.11 = bf16[16,4,16,128]{3,2,1,0:T(8,128)(2,1)S(1)} collective-permute-done((bf16[16,4,16,128]{3,2,1,0:T(8,128)(2,1)S(1)}, bf16[16,4,16,128]{3,2,1,0:T(8,128)(2,1)S(1)}, u32[]{:S(2)}, u32[]{:S(2)}) %collective-permute-start.11) | collective-permute-done | bytes 262176 | tf_op jit(solution)/shard_map/ppermute | solution.py:47
  70.6 5.9 %collective-permute-done.10 = bf16[16,4,16,128]{3,2,1,0:T(8,128)(2,1)S(1)} collective-permute-done((bf16[16,4,16,128]{3,2,1,0:T(8,128)(2,1)S(1)}, bf16[16,4,16,128]{3,2,1,0:T(8,128)(2,1)S(1)}, u32[]{:S(2)}, u32[]{:S(2)}) %collective-permute-start.10) | collective-permute-done | bytes 262176 | tf_op jit(solution)/shard_map/ppermute | solution.py:47
  77.7 1.8 %collective-permute-start.18 = (bf16[16,4,16,128]{3,2,1,0:T(8,128)(2,1)S(1)}, bf16[16,4,16,128]{3,2,1,0:T(8,128)(2,1)S(1)}, u32[]{:S(2)}, u32[]{:S(2)}) collective-permute-start(bf16[16,4,16,128]{3,2,1,0:T(8,128)(2,1)S(1)} %get-tuple-element.21), channel_id=1, source_target_pairs={{0,2},{1,3},{2,0},{3,1},{4,6},{5,7},{6,4},{7,5},{8,10},{9,11},{10,... | collective-permute-start | bytes 786440 | tf_op jit(solution)/shard_map/ppermute | solution.py:47
  79.7 1.0 dynamic-slice_bitcast_fusion.9
  80.6 1.6 collective-permute-start.16
  83.1 3.6 %collective-permute-start.14 = (bf16[16,4,16,128]{3,2,1,0:T(8,128)(2,1)}, bf16[16,4,16,128]{3,2,1,0:T(8,128)(2,1)}, u32[]{:S(2)}, u32[]{:S(2)}) collective-permute-start(bf16[16,4,16,128]{3,2,1,0:T(8,128)(2,1)} %get-tuple-element.26), channel_id=1, source_target_pairs={{0,1},{1,2},{2,3},{3,0},{4,5},{5,6},{6,7},{7,4},{8,9},{9,10},{10,1... | collective-permute-start | bytes 786440 | tf_op jit(solution)/shard_map/ppermute | solution.py:47
  86.7 5.5 %collective-permute-done.18 = bf16[16,4,16,128]{3,2,1,0:T(8,128)(2,1)S(1)} collective-permute-done((bf16[16,4,16,128]{3,2,1,0:T(8,128)(2,1)S(1)}, bf16[16,4,16,128]{3,2,1,0:T(8,128)(2,1)S(1)}, u32[]{:S(2)}, u32[]{:S(2)}) %collective-permute-start.18) | collective-permute-done | bytes 262176 | tf_op jit(solution)/shard_map/ppermute | solution.py:47
  92.2 3.3 %collective-permute-start.13 = (bf16[16,1,64,128]{3,2,1,0:T(8,128)(2,1)S(1)}, bf16[16,1,64,128]{3,2,1,0:T(8,128)(2,1)S(1)}, u32[]{:S(2)}, u32[]{:S(2)}) collective-permute-start(bf16[16,1,64,128]{3,2,1,0:T(8,128)(2,1)S(1)} %get-tuple-element.44), channel_id=1, source_target_pairs={{0,4},{4,8},{8,12},{12,16},{16,20},{20,24},{24,28},{1,5},{5,9},{9,... | collective-permute-start | bytes 786440 | tf_op jit(solution)/shard_map/ppermute | solution.py:22
  95.5 1.3 collective-permute-start.12
  97.6 0.8 fusion.41
  98.4 11.1 %collective-permute-done.13 = bf16[16,1,64,128]{3,2,1,0:T(8,128)(2,1)S(1)} collective-permute-done((bf16[16,1,64,128]{3,2,1,0:T(8,128)(2,1)S(1)}, bf16[16,1,64,128]{3,2,1,0:T(8,128)(2,1)S(1)}, u32[]{:S(2)}, u32[]{:S(2)}) %collective-permute-start.13) | collective-permute-done | bytes 262176 | tf_op jit(solution)/shard_map/ppermute | solution.py:22
  109.5 5.1 %collective-permute-start.21 = (bf16[16,1,64,128]{3,2,1,0:T(8,128)(2,1)}, bf16[16,1,64,128]{3,2,1,0:T(8,128)(2,1)}, u32[]{:S(2)}, u32[]{:S(2)}) collective-permute-start(bf16[16,1,64,128]{3,2,1,0:T(8,128)(2,1)} %get-tuple-element.46), channel_id=1, source_target_pairs={{0,4},{4,8},{8,12},{12,16},{16,20},{20,24},{24,28},{1,5},{5,9},{9,... | collective-permute-start | bytes 786440 | tf_op jit(solution)/shard_map/ppermute | solution.py:22
  114.6 1.5 collective-permute-start.20
  116.1 2.0 %fusion.6 = bf16[16,4,64,128]{3,2,1,0:T(8,128)(2,1)S(1)} fusion(f32[16,4,64,128]{3,2,1,0:T(8,128)S(1)} %convert_element_type.100, bf16[16,4,64,128]{3,2,1,0:T(8,128)(2,1)S(1)} %pad_maximum_fusion.13, bf16[16,1,64,128]{3,2,1,0:T(8,128)(2,1)S(1)} %collective-permute-done.13, bf16[16,1,64,128]{3,2,1,0:T(8,128)(2,1)S(1)} %collective-permute-done.12, ...), kind=kLoop, calls=%fused_computation.14 | loop fusion | flops 8912896 | bytes 4724736 | tf_op jit(solution)/shard_map/convert_element_type | solution.py:241
  119.6 1.2 pad_maximum_fusion.20
  120.8 5.3 %all-to-all-start = ((bf16[8,128,256]{2,1,0:T(8,128)(2,1)}), bf16[8,128,256]{2,1,0:T(8,128)(2,1)}, u32[]{:S(2)}, u32[]{:S(2)}) async-start(bf16[8,128,256]{2,1,0:T(8,128)(2,1)} %bitcast.120), calls=%async_computation | async-start | bytes 1048576 | tf_op jit(solution)/shard_map/all_to_all | solution.py:251
  126.1 1.2 pad_maximum_fusion.16
  127.7 3.8 %fusion.13 = bf16[16,4,64,128]{3,2,1,0:T(8,128)(2,1)S(1)} fusion(f32[16,4,64,128]{3,2,1,0:T(8,128)S(1)} %get-tuple-element.48, bf16[16,1,64,128]{3,2,1,0:T(8,128)(2,1)} %collective-permute-done.21, bf16[16,4,16,128]{3,2,1,0:T(8,128)(2,1)S(1)} %get-tuple-element.50, bf16[16,4,16,128]{3,2,1,0:T(8,128)(2,1)S(1)} %get-tuple-element.51, ...), kind=kLoop, calls=%fused_computation.21 | loop fusion | flops 17301504 | bytes 4724736 | tf_op jit(solution)/shard_map/convert_element_type | solution.py:241
  133.1 1.2 pad_maximum_fusion.21
  134.2 6.1 %all-to-all-done = bf16[8,128,256]{2,1,0:T(8,128)(2,1)} async-done(((bf16[8,128,256]{2,1,0:T(8,128)(2,1)}), bf16[8,128,256]{2,1,0:T(8,128)(2,1)}, u32[]{:S(2)}, u32[]{:S(2)}) %all-to-all-start) | async-done | bytes 524320 | tf_op jit(solution)/shard_map/all_to_all | solution.py:251
  140.4 4.9 %all-to-all-start.1 = ((bf16[8,128,256]{2,1,0:T(8,128)(2,1)}), bf16[8,128,256]{2,1,0:T(8,128)(2,1)S(1)}, u32[]{:S(2)}, u32[]{:S(2)}) async-start(bf16[8,128,256]{2,1,0:T(8,128)(2,1)} %bitcast.38), calls=%async_computation.1 | async-start | bytes 1048576 | tf_op jit(solution)/shard_map/all_to_all | solution.py:251
  145.3 1.1 convert_reduce_fusion.1
  146.4 9.2 %all-to-all-done.1 = bf16[8,128,256]{2,1,0:T(8,128)(2,1)S(1)} async-done(((bf16[8,128,256]{2,1,0:T(8,128)(2,1)}), bf16[8,128,256]{2,1,0:T(8,128)(2,1)S(1)}, u32[]{:S(2)}, u32[]{:S(2)}) %all-to-all-start.1) | async-done | bytes 524320 | tf_op jit(solution)/shard_map/all_to_all | solution.py:251
  155.9 9.9 %all_to_all.16 = f32[8,1,32]{2,1,0:T(1,128)S(1)} all-to-all(f32[8,1,32]{2,1,0:T(1,128)S(1)} %broadcast_in_dim.5), channel_id=1, replica_groups=mesh['gx'=8,'ka'=4] {'gx'}, dimensions={0} | all-to-all | bytes 2048 | tf_op jit(solution)/shard_map/all_to_all | solution.py:34
  166.4 0.8 fusion.27
  (85 shorter events, 12.3 us)
Async XLA Ops:
  0.7 7.5 %copy-start = (bf16[32,4,64,128]{3,2,1,0:T(8,128)(2,1)S(1)}, bf16[32,4,64,128]{3,2,1,0:T(8,128)(2,1)}, u32[]{:S(2)}) copy-start(bf16[32,4,64,128]{3,2,1,0:T(8,128)(2,1)} %param.6) | copy-start | bytes 6291460
  3.8 14.3 %collective-permute-start = (bf16[32,4,16,128]{3,2,1,0:T(8,128)(2,1)}, bf16[32,4,16,128]{3,2,1,0:T(8,128)(2,1)S(1)}, u32[]{:S(2)}, u32[]{:S(2)}) collective-permute-start(bf16[32,4,16,128]{3,2,1,0:T(8,128)(2,1)} %get-tuple-element.40), channel_id=1, source_target_pairs={{0,1},{1,2},{2,3},{3,0},{4,5},{5,6},{6,7},{7,4},{8,9},{9,10},{10,1... | collective-permute-start | bytes 1572872 | tf_op jit(solution)/shard_map/ppermute | solution.py:47
  4.2 15.5 %collective-permute-start.1 = (bf16[32,4,16,128]{3,2,1,0:T(8,128)(2,1)}, bf16[32,4,16,128]{3,2,1,0:T(8,128)(2,1)S(1)}, u32[]{:S(2)}, u32[]{:S(2)}) collective-permute-start(bf16[32,4,16,128]{3,2,1,0:T(8,128)(2,1)} %get-tuple-element.42), channel_id=1, source_target_pairs={{0,2},{1,3},{2,0},{3,1},{4,6},{5,7},{6,4},{7,5},{8,10},{9,11},{10,... | collective-permute-start | bytes 1572872 | tf_op jit(solution)/shard_map/ppermute | solution.py:47
  6.8 23.8 %collective-permute-start.2 = (bf16[32,4,16,128]{3,2,1,0:T(8,128)(2,1)}, bf16[32,4,16,128]{3,2,1,0:T(8,128)(2,1)S(1)}, u32[]{:S(2)}, u32[]{:S(2)}) collective-permute-start(bf16[32,4,16,128]{3,2,1,0:T(8,128)(2,1)} %get-tuple-element.39), channel_id=1, source_target_pairs={{0,3},{1,0},{2,1},{3,2},{4,7},{5,4},{6,5},{7,6},{8,11},{9,8},{10,9... | collective-permute-start | bytes 1572872 | tf_op jit(solution)/shard_map/ppermute | solution.py:47
  9.7 4.1 %copy-start.2 = (f32[4,64]{1,0:T(4,128)S(1)}, f32[4,64]{1,0:T(4,128)}, u32[]{:S(2)}) copy-start(f32[4,64]{1,0:T(4,128)} %param.7) | copy-start | bytes 3076
  9.7 32.2 %collective-permute-start.6 = (bf16[32,4,16,128]{3,2,1,0:T(8,128)(2,1)}, bf16[32,4,16,128]{3,2,1,0:T(8,128)(2,1)}, u32[]{:S(2)}, u32[]{:S(2)}) collective-permute-start(bf16[32,4,16,128]{3,2,1,0:T(8,128)(2,1)} %get-tuple-element.32), channel_id=1, source_target_pairs={{0,1},{1,2},{2,3},{3,0},{4,5},{5,6},{6,7},{7,4},{8,9},{9,10},{10,1... | collective-permute-start | bytes 1572872 | tf_op jit(solution)/shard_map/ppermute | solution.py:47
  9.7 34.5 %collective-permute-start.7 = (bf16[32,4,16,128]{3,2,1,0:T(8,128)(2,1)}, bf16[32,4,16,128]{3,2,1,0:T(8,128)(2,1)S(1)}, u32[]{:S(2)}, u32[]{:S(2)}) collective-permute-start(bf16[32,4,16,128]{3,2,1,0:T(8,128)(2,1)} %get-tuple-element.34), channel_id=1, source_target_pairs={{0,2},{1,3},{2,0},{3,1},{4,6},{5,7},{6,4},{7,5},{8,10},{9,11},{10,... | collective-permute-start | bytes 1572872 | tf_op jit(solution)/shard_map/ppermute | solution.py:47
  18.0 35.0 %collective-permute-start.8 = (bf16[32,4,16,128]{3,2,1,0:T(8,128)(2,1)}, bf16[32,4,16,128]{3,2,1,0:T(8,128)(2,1)}, u32[]{:S(2)}, u32[]{:S(2)}) collective-permute-start(bf16[32,4,16,128]{3,2,1,0:T(8,128)(2,1)} %get-tuple-element.31), channel_id=1, source_target_pairs={{0,3},{1,0},{2,1},{3,2},{4,7},{5,4},{6,5},{7,6},{8,11},{9,8},{10,9... | collective-permute-start | bytes 1572872 | tf_op jit(solution)/shard_map/ppermute | solution.py:47
  37.5 4.4 %copy-start.3 = (f32[4,64]{1,0:T(4,128)S(1)}, f32[4,64]{1,0:T(4,128)}, u32[]{:S(2)}) copy-start(f32[4,64]{1,0:T(4,128)} %param.8) | copy-start | bytes 3076
  38.5 25.6 %collective-permute-start.5 = (bf16[16,4,16,128]{3,2,1,0:T(8,128)(2,1)}, bf16[16,4,16,128]{3,2,1,0:T(8,128)(2,1)}, u32[]{:S(2)}, u32[]{:S(2)}) collective-permute-start(bf16[16,4,16,128]{3,2,1,0:T(8,128)(2,1)} %get-tuple-element.36), channel_id=1, source_target_pairs={{0,3},{1,0},{2,1},{3,2},{4,7},{5,4},{6,5},{7,6},{8,11},{9,8},{10,9... | collective-permute-start | bytes 786440 | tf_op jit(solution)/shard_map/ppermute | solution.py:47
  41.9 22.4 %collective-permute-start.4 = (bf16[16,4,16,128]{3,2,1,0:T(8,128)(2,1)}, bf16[16,4,16,128]{3,2,1,0:T(8,128)(2,1)S(1)}, u32[]{:S(2)}, u32[]{:S(2)}) collective-permute-start(bf16[16,4,16,128]{3,2,1,0:T(8,128)(2,1)} %get-tuple-element.37), channel_id=1, source_target_pairs={{0,2},{1,3},{2,0},{3,1},{4,6},{5,7},{6,4},{7,5},{8,10},{9,11},{10,... | collective-permute-start | bytes 786440 | tf_op jit(solution)/shard_map/ppermute | solution.py:47
  41.9 22.4 %collective-permute-start.3 = (bf16[16,4,16,128]{3,2,1,0:T(8,128)(2,1)}, bf16[16,4,16,128]{3,2,1,0:T(8,128)(2,1)S(1)}, u32[]{:S(2)}, u32[]{:S(2)}) collective-permute-start(bf16[16,4,16,128]{3,2,1,0:T(8,128)(2,1)} %get-tuple-element.38), channel_id=1, source_target_pairs={{0,1},{1,2},{2,3},{3,0},{4,5},{5,6},{6,7},{7,4},{8,9},{9,10},{10,1... | collective-permute-start | bytes 786440 | tf_op jit(solution)/shard_map/ppermute | solution.py:47
  62.1 8.6 %collective-permute-start.11 = (bf16[16,4,16,128]{3,2,1,0:T(8,128)(2,1)S(1)}, bf16[16,4,16,128]{3,2,1,0:T(8,128)(2,1)S(1)}, u32[]{:S(2)}, u32[]{:S(2)}) collective-permute-start(bf16[16,4,16,128]{3,2,1,0:T(8,128)(2,1)S(1)} %get-tuple-element.28), channel_id=1, source_target_pairs={{0,3},{1,0},{2,1},{3,2},{4,7},{5,4},{6,5},{7,6},{8,11},{9,8},{10,9... | collective-permute-start | bytes 786440 | tf_op jit(solution)/shard_map/ppermute | solution.py:47
  64.0 12.6 %collective-permute-start.10 = (bf16[16,4,16,128]{3,2,1,0:T(8,128)(2,1)S(1)}, bf16[16,4,16,128]{3,2,1,0:T(8,128)(2,1)S(1)}, u32[]{:S(2)}, u32[]{:S(2)}) collective-permute-start(bf16[16,4,16,128]{3,2,1,0:T(8,128)(2,1)S(1)} %get-tuple-element.29), channel_id=1, source_target_pairs={{0,2},{1,3},{2,0},{3,1},{4,6},{5,7},{6,4},{7,5},{8,10},{9,11},{10,... | collective-permute-start | bytes 786440 | tf_op jit(solution)/shard_map/ppermute | solution.py:47
  64.1 12.5 %collective-permute-start.9 = (bf16[16,4,16,128]{3,2,1,0:T(8,128)(2,1)S(1)}, bf16[16,4,16,128]{3,2,1,0:T(8,128)(2,1)S(1)}, u32[]{:S(2)}, u32[]{:S(2)}) collective-permute-start(bf16[16,4,16,128]{3,2,1,0:T(8,128)(2,1)S(1)} %get-tuple-element.30), channel_id=1, source_target_pairs={{0,1},{1,2},{2,3},{3,0},{4,5},{5,6},{6,7},{7,4},{8,9},{9,10},{10,1... | collective-permute-start | bytes 786440 | tf_op jit(solution)/shard_map/ppermute | solution.py:47
  77.6 5.4 %collective-permute-start.19 = (bf16[16,4,16,128]{3,2,1,0:T(8,128)(2,1)S(1)}, bf16[16,4,16,128]{3,2,1,0:T(8,128)(2,1)S(1)}, u32[]{:S(2)}, u32[]{:S(2)}) collective-permute-start(bf16[16,4,16,128]{3,2,1,0:T(8,128)(2,1)S(1)} %get-tuple-element.20), channel_id=1, source_target_pairs={{0,3},{1,0},{2,1},{3,2},{4,7},{5,4},{6,5},{7,6},{8,11},{9,8},{10,9... | collective-permute-start | bytes 786440 | tf_op jit(solution)/shard_map/ppermute | solution.py:47
  77.7 14.5 %collective-permute-start.18 = (bf16[16,4,16,128]{3,2,1,0:T(8,128)(2,1)S(1)}, bf16[16,4,16,128]{3,2,1,0:T(8,128)(2,1)S(1)}, u32[]{:S(2)}, u32[]{:S(2)}) collective-permute-start(bf16[16,4,16,128]{3,2,1,0:T(8,128)(2,1)S(1)} %get-tuple-element.21), channel_id=1, source_target_pairs={{0,2},{1,3},{2,0},{3,1},{4,6},{5,7},{6,4},{7,5},{8,10},{9,11},{10,... | collective-permute-start | bytes 786440 | tf_op jit(solution)/shard_map/ppermute | solution.py:47
  79.5 16.0 %collective-permute-start.17 = (bf16[16,4,16,128]{3,2,1,0:T(8,128)(2,1)S(1)}, bf16[16,4,16,128]{3,2,1,0:T(8,128)(2,1)S(1)}, u32[]{:S(2)}, u32[]{:S(2)}) collective-permute-start(bf16[16,4,16,128]{3,2,1,0:T(8,128)(2,1)S(1)} %get-tuple-element.22), channel_id=1, source_target_pairs={{0,1},{1,2},{2,3},{3,0},{4,5},{5,6},{6,7},{7,4},{8,9},{9,10},{10,1... | collective-permute-start | bytes 786440 | tf_op jit(solution)/shard_map/ppermute | solution.py:47
  80.6 45.5 %collective-permute-start.16 = (bf16[16,4,16,128]{3,2,1,0:T(8,128)(2,1)}, bf16[16,4,16,128]{3,2,1,0:T(8,128)(2,1)}, u32[]{:S(2)}, u32[]{:S(2)}) collective-permute-start(bf16[16,4,16,128]{3,2,1,0:T(8,128)(2,1)} %get-tuple-element.24), channel_id=1, source_target_pairs={{0,3},{1,0},{2,1},{3,2},{4,7},{5,4},{6,5},{7,6},{8,11},{9,8},{10,9... | collective-permute-start | bytes 786440 | tf_op jit(solution)/shard_map/ppermute | solution.py:47
  82.2 43.9 %collective-permute-start.15 = (bf16[16,4,16,128]{3,2,1,0:T(8,128)(2,1)}, bf16[16,4,16,128]{3,2,1,0:T(8,128)(2,1)}, u32[]{:S(2)}, u32[]{:S(2)}) collective-permute-start(bf16[16,4,16,128]{3,2,1,0:T(8,128)(2,1)} %get-tuple-element.25), channel_id=1, source_target_pairs={{0,2},{1,3},{2,0},{3,1},{4,6},{5,7},{6,4},{7,5},{8,10},{9,11},{10,... | collective-permute-start | bytes 786440 | tf_op jit(solution)/shard_map/ppermute | solution.py:47
  83.1 43.1 %collective-permute-start.14 = (bf16[16,4,16,128]{3,2,1,0:T(8,128)(2,1)}, bf16[16,4,16,128]{3,2,1,0:T(8,128)(2,1)}, u32[]{:S(2)}, u32[]{:S(2)}) collective-permute-start(bf16[16,4,16,128]{3,2,1,0:T(8,128)(2,1)} %get-tuple-element.26), channel_id=1, source_target_pairs={{0,1},{1,2},{2,3},{3,0},{4,5},{5,6},{6,7},{7,4},{8,9},{9,10},{10,1... | collective-permute-start | bytes 786440 | tf_op jit(solution)/shard_map/ppermute | solution.py:47
  92.2 17.3 %collective-permute-start.13 = (bf16[16,1,64,128]{3,2,1,0:T(8,128)(2,1)S(1)}, bf16[16,1,64,128]{3,2,1,0:T(8,128)(2,1)S(1)}, u32[]{:S(2)}, u32[]{:S(2)}) collective-permute-start(bf16[16,1,64,128]{3,2,1,0:T(8,128)(2,1)S(1)} %get-tuple-element.44), channel_id=1, source_target_pairs={{0,4},{4,8},{8,12},{12,16},{16,20},{20,24},{24,28},{1,5},{5,9},{9,... | collective-permute-start | bytes 786440 | tf_op jit(solution)/shard_map/ppermute | solution.py:22
  95.5 19.1 %collective-permute-start.12 = (bf16[16,1,64,128]{3,2,1,0:T(8,128)(2,1)S(1)}, bf16[16,1,64,128]{3,2,1,0:T(8,128)(2,1)S(1)}, u32[]{:S(2)}, u32[]{:S(2)}) collective-permute-start(bf16[16,1,64,128]{3,2,1,0:T(8,128)(2,1)S(1)} %get-tuple-element.43), channel_id=1, source_target_pairs={{4,0},{8,4},{12,8},{16,12},{20,16},{24,20},{28,24},{5,1},{9,5},{13... | collective-permute-start | bytes 786440 | tf_op jit(solution)/shard_map/ppermute | solution.py:24
  97.2 18.9 %copy-start.1 = (f32[4,64]{1,0:T(4,128)S(1)}, f32[4,64]{1,0:T(4,128)}, u32[]{:S(2)}) copy-start(f32[4,64]{1,0:T(4,128)} %param.9) | copy-start | bytes 3076
  109.5 18.2 %collective-permute-start.21 = (bf16[16,1,64,128]{3,2,1,0:T(8,128)(2,1)}, bf16[16,1,64,128]{3,2,1,0:T(8,128)(2,1)}, u32[]{:S(2)}, u32[]{:S(2)}) collective-permute-start(bf16[16,1,64,128]{3,2,1,0:T(8,128)(2,1)} %get-tuple-element.46), channel_id=1, source_target_pairs={{0,4},{4,8},{8,12},{12,16},{16,20},{20,24},{24,28},{1,5},{5,9},{9,... | collective-permute-start | bytes 786440 | tf_op jit(solution)/shard_map/ppermute | solution.py:22
  114.6 13.1 %collective-permute-start.20 = (bf16[16,1,64,128]{3,2,1,0:T(8,128)(2,1)}, bf16[16,1,64,128]{3,2,1,0:T(8,128)(2,1)}, u32[]{:S(2)}, u32[]{:S(2)}) collective-permute-start(bf16[16,1,64,128]{3,2,1,0:T(8,128)(2,1)} %get-tuple-element.45), channel_id=1, source_target_pairs={{4,0},{8,4},{12,8},{16,12},{20,16},{24,20},{28,24},{5,1},{9,5},{13... | collective-permute-start | bytes 786440 | tf_op jit(solution)/shard_map/ppermute | solution.py:24
  120.8 19.6 %all-to-all-start = ((bf16[8,128,256]{2,1,0:T(8,128)(2,1)}), bf16[8,128,256]{2,1,0:T(8,128)(2,1)}, u32[]{:S(2)}, u32[]{:S(2)}) async-start(bf16[8,128,256]{2,1,0:T(8,128)(2,1)} %bitcast.120), calls=%async_computation | async-start | bytes 1048576 | tf_op jit(solution)/shard_map/all_to_all | solution.py:251
  140.4 15.2 %all-to-all-start.1 = ((bf16[8,128,256]{2,1,0:T(8,128)(2,1)}), bf16[8,128,256]{2,1,0:T(8,128)(2,1)S(1)}, u32[]{:S(2)}, u32[]{:S(2)}) async-start(bf16[8,128,256]{2,1,0:T(8,128)(2,1)} %bitcast.38), calls=%async_computation.1 | async-start | bytes 1048576 | tf_op jit(solution)/shard_map/all_to_all | solution.py:251

commit v12 on v8

--- a/solution.py
+++ b/solution.py
@@ -229,14 +229,24 @@
         jnp.float32
     )
     shares = gram_terms.astype(jnp.bfloat16).reshape(lax.axis_size("gx"), row_count, 2 * columns)
-    shares = lax.all_to_all(shares, "gx", split_axis=0, concat_axis=0, tiled=True)
-    own_rows = jnp.sum(shares.astype(jnp.float32), axis=0)
-    row_energy = jnp.sum(own_rows[:, :columns] ** 2, axis=1)
-    energy = jnp.sum(gather_small(jnp.sum(selector * row_energy[:, None], axis=0), "gx"), axis=0)
+
+    def reduce_rows(part):
+        part = lax.all_to_all(part, "gx", split_axis=0, concat_axis=0, tiled=True)
+        return jnp.sum(part.astype(jnp.float32), axis=0)
+
+    own_hankel = reduce_rows(shares[..., :columns])
+    row_energy = jnp.sum(own_hankel**2, axis=1)
+    energy = jnp.sum(selector * row_energy[:, None], axis=0)
+    axial_count = lax.axis_size("gx")
+    energy = energy + sum(
+        lax.ppermute(energy, "gx", [(j, (j + shift) % axial_count) for j in range(axial_count)])
+        for shift in range(1, axial_count)
+    )
+    own_operator = reduce_rows(shares[..., columns:])
     mean_sq = energy / (2.0 * snap_count * snap_count)
     row_scale = jnp.sum(selector * lax.rsqrt(mean_sq + epsilon)[None, :], axis=1)
-    hankel_gram = own_rows[:, :columns] * row_scale[:, None]
-    reduced_operator = own_rows[:, columns:] * row_scale[:, None]
+    hankel_gram = own_hankel * row_scale[:, None]
+    reduced_operator = own_operator * row_scale[:, None]
     hankel_norm = jnp.sqrt(mean_sq)
     return (hankel_gram, reduced_operator, hankel_norm)
 

time: 160 us -> 161 us (level)
  waiting for transfers between devices: 74.5 us -> 54.8 us
  blocking collectives: 9.9 us -> 20.3 us
  starting transfers between devices: 24.8 us -> 34.9 us
    all_to_all x1, waiting for transfers between devices: 26 us -> 4.19 us  [reduce_rows(): part = lax.all_to_all(part, 'gx', split_axis=0, concat_axis=0, tiled=True)]
    ppermute x0 -> x7, starting transfers between devices: none -> 12.2 us  [local(): lax.ppermute(energy, 'gx', [(j, (j + shift) % axial_count) for j in range...]
    all_to_all x1, blocking collectives: 9.9 us -> 20.3 us  [reduce_rows(): part = lax.all_to_all(part, 'gx', split_axis=0, concat_axis=0, tiled=True)]
    ppermute x0 -> x7, waiting for transfers between devices: none -> 2.23 us  [local(): lax.ppermute(energy, 'gx', [(j, (j + shift) % axial_count) for j in range...]
    all_to_all x1, starting transfers between devices: 5.78 us -> 3.64 us  [reduce_rows(): part = lax.all_to_all(part, 'gx', split_axis=0, concat_axis=0, tiled=True)]
  transfers between devices with their start and end apart: 15 -> 22, of which waited for: 10 -> 12; matrix products, arithmetic and copies ran while one was open for 17% -> 17% of each run, Pallas kernels for 4% -> 4%
where the time goes in v12:
time: 161 us; the launch traced here: 160 us
  waiting for transfers between devices  54.8 us (34%)
  starting transfers between devices  34.9 us (22%)
  local copies, waits for them, and re-layouts  27.1 us (17%)
  blocking collectives  20.3 us (13%)
  other arithmetic  14.3 us (9%)
  Pallas kernels  7.1 us (4%)
    ppermute x12, waiting for transfers between devices, exchange(): lax.ppermute(piece, axis, [(j, (j + shift) % count) for j in range(count)])  41.2 us
    all_to_all x1, blocking collectives, reduce_rows(): part = lax.all_to_all(part, 'gx', split_axis=0, concat_axis=0, tiled=True)  20.3 us
    unnamed x18, local copies, waits for them, and re-layouts  16.7 us
    ppermute x12, starting transfers between devices, exchange(): lax.ppermute(piece, axis, [(j, (j + shift) % count) for j in range(count)])  13 us
    ppermute x7, starting transfers between devices, local(): lax.ppermute(energy, 'gx', [(j, (j + shift) % axial_count) for j in range...  12.2 us
    ppermute x1, waiting for transfers between devices, padded_2(): lax.ppermute(tail, axis, [(i, (i + 1) % count) for i in range(ends)])  7.14 us
    pallas_call x2, Pallas kernels, dft(): pl.pallas_call(functools.partial(dft_kernel, count=count, weighted=weight...  7.1 us
    convert_element_type x1, other arithmetic, local(): image = (-velocity * (forward - behind) * 0.5 + diffusion * (forward + be...  5.9 us
  transfers between devices with their start and end apart: 22, of which 12 were waited for; matrix products, arithmetic and copies ran while one was open for 17% of the time, Pallas kernels for 4%

profile of v12, /device:TPU:0, one launch (start us, length us, event | category | flops | bytes accessed | tf_op | source)
XLA Modules:
  0.0 160.4 jit_solution(12405682203036885730)
XLA Ops:
  0.7 3.1 %constant_dynamic-slice_fusion.3 = (bf16[32,4,16,128]{3,2,1,0:T(8,128)(2,1)}, bf16[32,4,16,128]{3,2,1,0:T(8,128)(2,1)}, bf16[32,4,16,128]{3,2,1,0:T(8,128)(2,1)S(1)}, bf16[32,4,16,128]{3,2,1,0:T(8,128)(2,1)}) fusion(bf16[32,4,64,128]{3,2,1,0:T(8,128)(2,1)} %param.5, s32[]{:T(128)S(6)} %select_n.166, s32[]{:T(128)S(6)} %select_n.162, s32[]{:T(128)S(6)} %select_n.160, ...), kind=kLoop, calls=%fused_computation.101 | loop fusion | bytes 4194320 | tf_op jit(solution)/shard_map/dynamic_slice | solution.py:43
  3.8 2.4 %collective-permute-start.8 = (bf16[32,4,16,128]{3,2,1,0:T(8,128)(2,1)}, bf16[32,4,16,128]{3,2,1,0:T(8,128)(2,1)}, u32[]{:S(2)}, u32[]{:S(2)}) collective-permute-start(bf16[32,4,16,128]{3,2,1,0:T(8,128)(2,1)} %get-tuple-element.21), channel_id=1, source_target_pairs={{0,3},{1,0},{2,1},{3,2},{4,7},{5,4},{6,5},{7,6},{8,11},{9,8},{10,9... | collective-permute-start | bytes 1572872 | tf_op jit(solution)/shard_map/ppermute | solution.py:45
  7.0 1.5 constant_dynamic-slice_fusion.11
  8.5 1.6 collective-permute-start.2
  10.1 1.4 collective-permute-start.1
  13.0 1.2 copy.37
  14.2 1.2 copy.41
  16.2 2.6 %collective-permute-done.8 = bf16[32,4,16,128]{3,2,1,0:T(8,128)(2,1)} collective-permute-done((bf16[32,4,16,128]{3,2,1,0:T(8,128)(2,1)}, bf16[32,4,16,128]{3,2,1,0:T(8,128)(2,1)}, u32[]{:S(2)}, u32[]{:S(2)}) %collective-permute-start.8) | collective-permute-done | bytes 524320 | tf_op jit(solution)/shard_map/ppermute | solution.py:45
  18.7 1.2 collective-permute-start
  20.0 2.2 %copy.34 = bf16[4,8,64,128]{3,1,2,0:T(8,128)(2,1)} copy(bf16[4,8,64,128]{3,2,1,0:T(8,128)(2,1)} %bitcast.45) | data formatting | bytes 1048576
  22.2 8.9 %collective-permute-done.7 = bf16[32,4,16,128]{3,2,1,0:T(8,128)(2,1)} collective-permute-done((bf16[32,4,16,128]{3,2,1,0:T(8,128)(2,1)}, bf16[32,4,16,128]{3,2,1,0:T(8,128)(2,1)}, u32[]{:S(2)}, u32[]{:S(2)}) %collective-permute-start.7) | collective-permute-done | bytes 524320 | tf_op jit(solution)/shard_map/ppermute | solution.py:45
  31.1 2.2 %copy.35 = bf16[4,8,64,128]{3,1,2,0:T(8,128)(2,1)} copy(bf16[4,8,64,128]{3,2,1,0:T(8,128)(2,1)} %bitcast.42) | data formatting | bytes 1048576
  33.3 2.2 %copy.36 = bf16[4,8,64,128]{3,1,2,0:T(8,128)(2,1)} copy(bf16[4,8,64,128]{3,2,1,0:T(8,128)(2,1)} %bitcast.39) | data formatting | bytes 1048576
  35.5 3.5 %shard_map.77 = bf16[128,8192]{1,0:T(8,128)(2,1)} custom-call(bf16[128,256]{1,0:T(8,128)(2,1)} %concatenate.23.refs_0_, bf16[32,8192]{1,0:T(8,128)(2,1)} %bitcast.88, bf16[32,8192]{1,0:T(8,128)(2,1)} %bitcast.94, bf16[32,8192]{1,0:T(8,128)(2,1)} %bitcast.92, bf16[32,8192]{1,0:T(8,128)(2,1)} %bitcast.90), custom_call_target="tpu_custom_call" | custom-call | tf_op jit(solution)/shard_map/pallas_call | solution.py:109
  38.9 2.2 %copy.25 = bf16[16,8,64,128]{3,2,1,0:T(8,128)(2,1)S(1)} copy(bf16[16,8,64,128]{3,1,2,0:T(8,128)(2,1)} %bitcast.83) | data formatting | bytes 4194304
  41.1 1.5 dynamic-slice_bitcast_fusion.4
  42.6 1.4 collective-permute-start.10
  44.0 1.4 collective-permute-start.11
  45.6 1.2 copy.38
  46.7 6.7 %collective-permute-done.1 = bf16[32,4,16,128]{3,2,1,0:T(8,128)(2,1)S(1)} collective-permute-done((bf16[32,4,16,128]{3,2,1,0:T(8,128)(2,1)}, bf16[32,4,16,128]{3,2,1,0:T(8,128)(2,1)S(1)}, u32[]{:S(2)}, u32[]{:S(2)}) %collective-permute-start.1) | collective-permute-done | bytes 524320 | tf_op jit(solution)/shard_map/ppermute | solution.py:45
  53.5 1.2 copy.39
  54.6 1.1 copy.40
  56.4 3.6 %shard_map.76 = bf16[128,8192]{1,0:T(8,128)(2,1)} custom-call(bf16[128,256]{1,0:T(8,128)(2,1)} %concatenate.23.refs_0_, bf16[32,8192]{1,0:T(8,128)(2,1)} %bitcast.87, bf16[32,8192]{1,0:T(8,128)(2,1)} %bitcast.93, bf16[32,8192]{1,0:T(8,128)(2,1)} %bitcast.91, bf16[32,8192]{1,0:T(8,128)(2,1)} %bitcast.89, f32[1,8192]{1,0:T(1,128)} %bitcast.102), custom_call_target="tpu_custom_call" | custom-call | tf_op jit(solution)/shard_map/pallas_call | solution.py:109
  60.1 2.2 %copy.20 = bf16[16,8,64,128]{3,2,1,0:T(8,128)(2,1)S(1)} copy(bf16[16,8,64,128]{3,1,2,0:T(8,128)(2,1)} %bitcast.81) | data formatting | bytes 4194304
  62.8 1.4 collective-permute-start.4
  64.3 1.3 collective-permute-start.5
  65.6 9.2 %collective-permute-done.11 = bf16[32,4,16,128]{3,2,1,0:T(8,128)(2,1)} collective-permute-done((bf16[32,4,16,128]{3,2,1,0:T(8,128)(2,1)S(1)}, bf16[32,4,16,128]{3,2,1,0:T(8,128)(2,1)}, u32[]{:S(2)}, u32[]{:S(2)}) %collective-permute-start.11) | collective-permute-done | bytes 524320 | tf_op jit(solution)/shard_map/ppermute | solution.py:45
  74.8 1.5 pad_maximum_fusion.11
  77.6 1.3 collective-permute-start.12
  78.9 4.8 %collective-permute-start.13 = (bf16[32,1,64,128]{3,2,1,0:T(8,128)(2,1)S(1)}, bf16[32,1,64,128]{3,2,1,0:T(8,128)(2,1)S(1)}, u32[]{:S(2)}, u32[]{:S(2)}) collective-permute-start(bf16[32,1,64,128]{3,2,1,0:T(8,128)(2,1)S(1)} %get-tuple-element.10), channel_id=1, source_target_pairs={{0,4},{4,8},{8,12},{12,16},{16,20},{20,24},{24,28},{1,5},{5,9},{9,... | collective-permute-start | bytes 1572872 | tf_op jit(solution)/shard_map/ppermute | solution.py:22
  83.7 3.1 %collective-permute-done.3 = bf16[32,4,16,128]{3,2,1,0:T(8,128)(2,1)S(1)} collective-permute-done((bf16[32,4,16,128]{3,2,1,0:T(8,128)(2,1)S(1)}, bf16[32,4,16,128]{3,2,1,0:T(8,128)(2,1)S(1)}, u32[]{:S(2)}, u32[]{:S(2)}) %collective-permute-start.3) | collective-permute-done | bytes 524320 | tf_op jit(solution)/shard_map/ppermute | solution.py:45
  87.2 10.1 %collective-permute-done.5 = bf16[32,4,16,128]{3,2,1,0:T(8,128)(2,1)S(1)} collective-permute-done((bf16[32,4,16,128]{3,2,1,0:T(8,128)(2,1)S(1)}, bf16[32,4,16,128]{3,2,1,0:T(8,128)(2,1)S(1)}, u32[]{:S(2)}, u32[]{:S(2)}) %collective-permute-start.5) | collective-permute-done | bytes 524320 | tf_op jit(solution)/shard_map/ppermute | solution.py:45
  98.3 7.1 %collective-permute-done.13 = bf16[32,1,64,128]{3,2,1,0:T(8,128)(2,1)S(1)} collective-permute-done((bf16[32,1,64,128]{3,2,1,0:T(8,128)(2,1)S(1)}, bf16[32,1,64,128]{3,2,1,0:T(8,128)(2,1)S(1)}, u32[]{:S(2)}, u32[]{:S(2)}) %collective-permute-start.13) | collective-permute-done | bytes 524320 | tf_op jit(solution)/shard_map/ppermute | solution.py:22
  105.4 5.9 %fusion.6 = bf16[32,4,64,128]{3,2,1,0:T(8,128)(2,1)S(1)} fusion(f32[32,4,64,128]{3,2,1,0:T(8,128)S(1)} %get-tuple-element.12, bf16[32,1,64,128]{3,2,1,0:T(8,128)(2,1)S(1)} %collective-permute-done.13, bf16[32,4,16,128]{3,2,1,0:T(8,128)(2,1)S(1)} %get-tuple-element.14, bf16[32,4,16,128]{3,2,1,0:T(8,128)(2,1)S(1)} %get-tuple-element.15, ...), kind=kLoop, calls=%fused_computation.10 | loop fusion | flops 34603008 | bytes 9447424 | tf_op jit(solution)/shard_map/convert_element_type | solution.py:216
  113.0 1.2 fusion.12
  114.9 1.1 fusion.24
  116.0 20.3 %all_to_all.10 = bf16[8,256,128]{2,1,0:T(8,128)(2,1)S(1)} all-to-all(bf16[8,256,128]{2,1,0:T(8,128)(2,1)S(1)} %get-tuple-element.38), channel_id=1, replica_groups=mesh['gx'=8,'ka'=4] {'gx'}, dimensions={0} | all-to-all | bytes 1048576 | tf_op jit(solution)/shard_map/all_to_all | solution.py:234
  136.3 3.6 %all-to-all-start.1 = ((bf16[8,256,128]{2,1,0:T(8,128)(2,1)}), bf16[8,256,128]{2,1,0:T(8,128)(2,1)S(1)}, u32[]{:S(2)}, u32[]{:S(2)}) async-start(bf16[8,256,128]{2,1,0:T(8,128)(2,1)} %get-tuple-element.37), calls=%async_computation.1 | async-start | bytes 1048576 | tf_op jit(solution)/shard_map/all_to_all | solution.py:234
  140.3 2.1 %collective-permute-start.14 = (f32[32]{0:T(128)S(1)}, f32[32]{0:T(128)S(1)}, u32[]{:S(2)}, u32[]{:S(2)}) collective-permute-start(f32[32]{0:T(128)S(1)} %select_reduce_fusion.1), channel_id=1, source_target_pairs={{0,4},{4,8},{8,12},{12,16},{16,20},{20,24},{24,28},{28,0},{1,5},{5... | collective-permute-start | bytes 392 | tf_op jit(solution)/shard_map/ppermute | solution.py:242
  142.3 1.5 collective-permute-start.15
  143.8 2.4 %collective-permute-start.16 = (f32[32]{0:T(128)S(1)}, f32[32]{0:T(128)S(1)}, u32[]{:S(2)}, u32[]{:S(2)}) collective-permute-start(f32[32]{0:T(128)S(1)} %select_reduce_fusion.1), channel_id=1, source_target_pairs={{0,12},{4,16},{8,20},{12,24},{16,28},{20,0},{24,4},{28,8},{1,13},{... | collective-permute-start | bytes 392 | tf_op jit(solution)/shard_map/ppermute | solution.py:242
  146.2 1.5 collective-permute-start.17
  147.6 2.4 %collective-permute-start.18 = (f32[32]{0:T(128)S(1)}, f32[32]{0:T(128)S(1)}, u32[]{:S(2)}, u32[]{:S(2)}) collective-permute-start(f32[32]{0:T(128)S(1)} %select_reduce_fusion.1), channel_id=1, source_target_pairs={{0,20},{4,24},{8,28},{12,0},{16,4},{20,8},{24,12},{28,16},{1,21},{... | collective-permute-start | bytes 392 | tf_op jit(solution)/shard_map/ppermute | solution.py:242
  150.0 4.2 %all-to-all-done.1 = bf16[8,256,128]{2,1,0:T(8,128)(2,1)S(1)} async-done(((bf16[8,256,128]{2,1,0:T(8,128)(2,1)}), bf16[8,256,128]{2,1,0:T(8,128)(2,1)S(1)}, u32[]{:S(2)}, u32[]{:S(2)}) %all-to-all-start.1) | async-done | bytes 524320 | tf_op jit(solution)/shard_map/all_to_all | solution.py:234
  154.3 1.2 collective-permute-start.19
  155.4 1.3 collective-permute-start.20
  156.8 1.1 collective-permute-done.19
  157.9 1.1 collective-permute-done.20
  (63 shorter events, 11.4 us)
Async XLA Ops:
  0.6 6.4 %copy-start = (bf16[32,4,64,128]{3,2,1,0:T(8,128)(2,1)S(1)}, bf16[32,4,64,128]{3,2,1,0:T(8,128)(2,1)}, u32[]{:S(2)}) copy-start(bf16[32,4,64,128]{3,2,1,0:T(8,128)(2,1)} %param.6) | copy-start | bytes 6291460
  3.8 10.4 %copy-start.2 = (f32[4,64]{1,0:T(4,128)S(1)}, f32[4,64]{1,0:T(4,128)}, u32[]{:S(2)}) copy-start(f32[4,64]{1,0:T(4,128)} %param.8) | copy-start | bytes 3076
  3.8 12.4 %copy-start.3 = (f32[4,64]{1,0:T(4,128)S(1)}, f32[4,64]{1,0:T(4,128)}, u32[]{:S(2)}) copy-start(f32[4,64]{1,0:T(4,128)} %param.7) | copy-start | bytes 3076
  3.8 14.9 %collective-permute-start.8 = (bf16[32,4,16,128]{3,2,1,0:T(8,128)(2,1)}, bf16[32,4,16,128]{3,2,1,0:T(8,128)(2,1)}, u32[]{:S(2)}, u32[]{:S(2)}) collective-permute-start(bf16[32,4,16,128]{3,2,1,0:T(8,128)(2,1)} %get-tuple-element.21), channel_id=1, source_target_pairs={{0,3},{1,0},{2,1},{3,2},{4,7},{5,4},{6,5},{7,6},{8,11},{9,8},{10,9... | collective-permute-start | bytes 1572872 | tf_op jit(solution)/shard_map/ppermute | solution.py:45
  6.2 24.9 %collective-permute-start.7 = (bf16[32,4,16,128]{3,2,1,0:T(8,128)(2,1)}, bf16[32,4,16,128]{3,2,1,0:T(8,128)(2,1)}, u32[]{:S(2)}, u32[]{:S(2)}) collective-permute-start(bf16[32,4,16,128]{3,2,1,0:T(8,128)(2,1)} %get-tuple-element.24), channel_id=1, source_target_pairs={{0,2},{1,3},{2,0},{3,1},{4,6},{5,7},{6,4},{7,5},{8,10},{9,11},{10,... | collective-permute-start | bytes 1572872 | tf_op jit(solution)/shard_map/ppermute | solution.py:45
  6.8 26.4 %collective-permute-start.6 = (bf16[32,4,16,128]{3,2,1,0:T(8,128)(2,1)}, bf16[32,4,16,128]{3,2,1,0:T(8,128)(2,1)}, u32[]{:S(2)}, u32[]{:S(2)}) collective-permute-start(bf16[32,4,16,128]{3,2,1,0:T(8,128)(2,1)} %get-tuple-element.22), channel_id=1, source_target_pairs={{0,1},{1,2},{2,3},{3,0},{4,5},{5,6},{6,7},{7,4},{8,9},{9,10},{10,1... | collective-permute-start | bytes 1572872 | tf_op jit(solution)/shard_map/ppermute | solution.py:45
  8.5 35.5 %collective-permute-start.2 = (bf16[32,4,16,128]{3,2,1,0:T(8,128)(2,1)}, bf16[32,4,16,128]{3,2,1,0:T(8,128)(2,1)S(1)}, u32[]{:S(2)}, u32[]{:S(2)}) collective-permute-start(bf16[32,4,16,128]{3,2,1,0:T(8,128)(2,1)} %get-tuple-element.33), channel_id=1, source_target_pairs={{0,3},{1,0},{2,1},{3,2},{4,7},{5,4},{6,5},{7,6},{8,11},{9,8},{10,9... | collective-permute-start | bytes 1572872 | tf_op jit(solution)/shard_map/ppermute | solution.py:45
  10.1 43.4 %collective-permute-start.1 = (bf16[32,4,16,128]{3,2,1,0:T(8,128)(2,1)}, bf16[32,4,16,128]{3,2,1,0:T(8,128)(2,1)S(1)}, u32[]{:S(2)}, u32[]{:S(2)}) collective-permute-start(bf16[32,4,16,128]{3,2,1,0:T(8,128)(2,1)} %get-tuple-element.36), channel_id=1, source_target_pairs={{0,2},{1,3},{2,0},{3,1},{4,6},{5,7},{6,4},{7,5},{8,10},{9,11},{10,... | collective-permute-start | bytes 1572872 | tf_op jit(solution)/shard_map/ppermute | solution.py:45
  18.7 35.9 %collective-permute-start = (bf16[32,4,16,128]{3,2,1,0:T(8,128)(2,1)}, bf16[32,4,16,128]{3,2,1,0:T(8,128)(2,1)S(1)}, u32[]{:S(2)}, u32[]{:S(2)}) collective-permute-start(bf16[32,4,16,128]{3,2,1,0:T(8,128)(2,1)} %get-tuple-element.34), channel_id=1, source_target_pairs={{0,1},{1,2},{2,3},{3,0},{4,5},{5,6},{6,7},{7,4},{8,9},{9,10},{10,1... | collective-permute-start | bytes 1572872 | tf_op jit(solution)/shard_map/ppermute | solution.py:45
  42.6 21.7 %collective-permute-start.9 = (bf16[32,4,16,128]{3,2,1,0:T(8,128)(2,1)}, bf16[32,4,16,128]{3,2,1,0:T(8,128)(2,1)S(1)}, u32[]{:S(2)}, u32[]{:S(2)}) collective-permute-start(bf16[32,4,16,128]{3,2,1,0:T(8,128)(2,1)} %get-tuple-element.20), channel_id=1, source_target_pairs={{0,1},{1,2},{2,3},{3,0},{4,5},{5,6},{6,7},{7,4},{8,9},{9,10},{10,1... | collective-permute-start | bytes 1572872 | tf_op jit(solution)/shard_map/ppermute | solution.py:45
  42.6 23.0 %collective-permute-start.10 = (bf16[32,4,16,128]{3,2,1,0:T(8,128)(2,1)}, bf16[32,4,16,128]{3,2,1,0:T(8,128)(2,1)}, u32[]{:S(2)}, u32[]{:S(2)}) collective-permute-start(bf16[32,4,16,128]{3,2,1,0:T(8,128)(2,1)} %get-tuple-element.19), channel_id=1, source_target_pairs={{0,2},{1,3},{2,0},{3,1},{4,6},{5,7},{6,4},{7,5},{8,10},{9,11},{10,... | collective-permute-start | bytes 1572872 | tf_op jit(solution)/shard_map/ppermute | solution.py:45
  44.0 30.8 %collective-permute-start.11 = (bf16[32,4,16,128]{3,2,1,0:T(8,128)(2,1)S(1)}, bf16[32,4,16,128]{3,2,1,0:T(8,128)(2,1)}, u32[]{:S(2)}, u32[]{:S(2)}) collective-permute-start(bf16[32,4,16,128]{3,2,1,0:T(8,128)(2,1)S(1)} %get-tuple-element.18), channel_id=1, source_target_pairs={{0,3},{1,0},{2,1},{3,2},{4,7},{5,4},{6,5},{7,6},{8,11},{9,8},{10,9... | collective-permute-start | bytes 1572872 | tf_op jit(solution)/shard_map/ppermute | solution.py:45
  62.7 24.1 %collective-permute-start.3 = (bf16[32,4,16,128]{3,2,1,0:T(8,128)(2,1)S(1)}, bf16[32,4,16,128]{3,2,1,0:T(8,128)(2,1)S(1)}, u32[]{:S(2)}, u32[]{:S(2)}) collective-permute-start(bf16[32,4,16,128]{3,2,1,0:T(8,128)(2,1)S(1)} %get-tuple-element.32), channel_id=1, source_target_pairs={{0,1},{1,2},{2,3},{3,0},{4,5},{5,6},{6,7},{7,4},{8,9},{9,10},{10,1... | collective-permute-start | bytes 1572872 | tf_op jit(solution)/shard_map/ppermute | solution.py:45
  62.8 24.4 %collective-permute-start.4 = (bf16[32,4,16,128]{3,2,1,0:T(8,128)(2,1)S(1)}, bf16[32,4,16,128]{3,2,1,0:T(8,128)(2,1)S(1)}, u32[]{:S(2)}, u32[]{:S(2)}) collective-permute-start(bf16[32,4,16,128]{3,2,1,0:T(8,128)(2,1)S(1)} %get-tuple-element.31), channel_id=1, source_target_pairs={{0,2},{1,3},{2,0},{3,1},{4,6},{5,7},{6,4},{7,5},{8,10},{9,11},{10,... | collective-permute-start | bytes 1572872 | tf_op jit(solution)/shard_map/ppermute | solution.py:45
  64.3 32.9 %collective-permute-start.5 = (bf16[32,4,16,128]{3,2,1,0:T(8,128)(2,1)S(1)}, bf16[32,4,16,128]{3,2,1,0:T(8,128)(2,1)S(1)}, u32[]{:S(2)}, u32[]{:S(2)}) collective-permute-start(bf16[32,4,16,128]{3,2,1,0:T(8,128)(2,1)S(1)} %get-tuple-element.30), channel_id=1, source_target_pairs={{0,3},{1,0},{2,1},{3,2},{4,7},{5,4},{6,5},{7,6},{8,11},{9,8},{10,9... | collective-permute-start | bytes 1572872 | tf_op jit(solution)/shard_map/ppermute | solution.py:45
  77.6 20.7 %collective-permute-start.12 = (bf16[32,1,64,128]{3,2,1,0:T(8,128)(2,1)S(1)}, bf16[32,1,64,128]{3,2,1,0:T(8,128)(2,1)S(1)}, u32[]{:S(2)}, u32[]{:S(2)}) collective-permute-start(bf16[32,1,64,128]{3,2,1,0:T(8,128)(2,1)S(1)} %get-tuple-element.9), channel_id=1, source_target_pairs={{4,0},{8,4},{12,8},{16,12},{20,16},{24,20},{28,24},{5,1},{9,5},{13... | collective-permute-start | bytes 1572872 | tf_op jit(solution)/shard_map/ppermute | solution.py:24
  78.9 26.5 %collective-permute-start.13 = (bf16[32,1,64,128]{3,2,1,0:T(8,128)(2,1)S(1)}, bf16[32,1,64,128]{3,2,1,0:T(8,128)(2,1)S(1)}, u32[]{:S(2)}, u32[]{:S(2)}) collective-permute-start(bf16[32,1,64,128]{3,2,1,0:T(8,128)(2,1)S(1)} %get-tuple-element.10), channel_id=1, source_target_pairs={{0,4},{4,8},{8,12},{12,16},{16,20},{20,24},{24,28},{1,5},{5,9},{9,... | collective-permute-start | bytes 1572872 | tf_op jit(solution)/shard_map/ppermute | solution.py:22
  97.5 7.9 %copy-start.1 = (f32[4,64]{1,0:T(4,128)S(1)}, f32[4,64]{1,0:T(4,128)}, u32[]{:S(2)}) copy-start(f32[4,64]{1,0:T(4,128)} %param.9) | copy-start | bytes 3076
  136.3 17.9 %all-to-all-start.1 = ((bf16[8,256,128]{2,1,0:T(8,128)(2,1)}), bf16[8,256,128]{2,1,0:T(8,128)(2,1)S(1)}, u32[]{:S(2)}, u32[]{:S(2)}) async-start(bf16[8,256,128]{2,1,0:T(8,128)(2,1)} %get-tuple-element.37), calls=%async_computation.1 | async-start | bytes 1048576 | tf_op jit(solution)/shard_map/all_to_all | solution.py:234
  140.3 14.0 %collective-permute-start.14 = (f32[32]{0:T(128)S(1)}, f32[32]{0:T(128)S(1)}, u32[]{:S(2)}, u32[]{:S(2)}) collective-permute-start(f32[32]{0:T(128)S(1)} %select_reduce_fusion.1), channel_id=1, source_target_pairs={{0,4},{4,8},{8,12},{12,16},{16,20},{20,24},{24,28},{28,0},{1,5},{5... | collective-permute-start | bytes 392 | tf_op jit(solution)/shard_map/ppermute | solution.py:242
  142.3 13.1 %collective-permute-start.15 = (f32[32]{0:T(128)S(1)}, f32[32]{0:T(128)S(1)}, u32[]{:S(2)}, u32[]{:S(2)}) collective-permute-start(f32[32]{0:T(128)S(1)} %select_reduce_fusion.1), channel_id=1, source_target_pairs={{0,8},{4,12},{8,16},{12,20},{16,24},{20,28},{24,0},{28,4},{1,9},{5... | collective-permute-start | bytes 392 | tf_op jit(solution)/shard_map/ppermute | solution.py:242
  143.8 13.0 %collective-permute-start.16 = (f32[32]{0:T(128)S(1)}, f32[32]{0:T(128)S(1)}, u32[]{:S(2)}, u32[]{:S(2)}) collective-permute-start(f32[32]{0:T(128)S(1)} %select_reduce_fusion.1), channel_id=1, source_target_pairs={{0,12},{4,16},{8,20},{12,24},{16,28},{20,0},{24,4},{28,8},{1,13},{... | collective-permute-start | bytes 392 | tf_op jit(solution)/shard_map/ppermute | solution.py:242
  146.2 10.6 %collective-permute-start.17 = (f32[32]{0:T(128)S(1)}, f32[32]{0:T(128)S(1)}, u32[]{:S(2)}, u32[]{:S(2)}) collective-permute-start(f32[32]{0:T(128)S(1)} %select_reduce_fusion.1), channel_id=1, source_target_pairs={{0,16},{4,20},{8,24},{12,28},{16,0},{20,4},{24,8},{28,12},{1,17},{... | collective-permute-start | bytes 392 | tf_op jit(solution)/shard_map/ppermute | solution.py:242
  147.6 9.1 %collective-permute-start.18 = (f32[32]{0:T(128)S(1)}, f32[32]{0:T(128)S(1)}, u32[]{:S(2)}, u32[]{:S(2)}) collective-permute-start(f32[32]{0:T(128)S(1)} %select_reduce_fusion.1), channel_id=1, source_target_pairs={{0,20},{4,24},{8,28},{12,0},{16,4},{20,8},{24,12},{28,16},{1,21},{... | collective-permute-start | bytes 392 | tf_op jit(solution)/shard_map/ppermute | solution.py:242
  154.3 3.6 %collective-permute-start.19 = (f32[32]{0:T(128)S(1)}, f32[32]{0:T(128)S(1)}, u32[]{:S(2)}, u32[]{:S(2)}) collective-permute-start(f32[32]{0:T(128)S(1)} %select_reduce_fusion.1), channel_id=1, source_target_pairs={{0,24},{4,28},{8,0},{12,4},{16,8},{20,12},{24,16},{28,20},{1,25},{... | collective-permute-start | bytes 392 | tf_op jit(solution)/shard_map/ppermute | solution.py:242
  155.4 3.5 %collective-permute-start.20 = (f32[32]{0:T(128)S(1)}, f32[32]{0:T(128)S(1)}, u32[]{:S(2)}, u32[]{:S(2)}) collective-permute-start(f32[32]{0:T(128)S(1)} %select_reduce_fusion.1), channel_id=1, source_target_pairs={{0,28},{4,0},{8,4},{12,8},{16,12},{20,16},{24,20},{28,24},{1,29},{... | collective-permute-start | bytes 392 | tf_op jit(solution)/shard_map/ppermute | solution.py:242

commit v13 on v8

--- a/solution.py
+++ b/solution.py
@@ -229,8 +229,7 @@
         jnp.float32
     )
     shares = gram_terms.astype(jnp.bfloat16).reshape(lax.axis_size("gx"), row_count, 2 * columns)
-    shares = lax.all_to_all(shares, "gx", split_axis=0, concat_axis=0, tiled=True)
-    own_rows = jnp.sum(shares.astype(jnp.float32), axis=0)
+    own_rows = sum(piece.astype(jnp.float32) for piece in exchange(shares, "gx", 0))[0]
     row_energy = jnp.sum(own_rows[:, :columns] ** 2, axis=1)
     energy = jnp.sum(gather_small(jnp.sum(selector * row_energy[:, None], axis=0), "gx"), axis=0)
     mean_sq = energy / (2.0 * snap_count * snap_count)

time: 160 us -> 157 us (0.981)
  waiting for transfers between devices: 74.5 us -> 56.7 us
  blocking collectives: 9.9 us -> 18.4 us
  starting transfers between devices: 24.8 us -> 31.6 us
    all_to_all x1 -> x0, waiting for transfers between devices: 26 us -> none  [local(): lax.all_to_all(shares, 'gx', split_axis=0, concat_axis=0, tiled=True)]
    ppermute x12 -> x19, starting transfers between devices: 13 us -> 25.6 us  [exchange(): lax.ppermute(piece, axis, [(j, (j + shift) % count) for j in range(count)])]
    all_to_all x1, blocking collectives: 9.9 us -> 18.4 us  [gather_small(): return lax.all_to_all(copies, axis, split_axis=0, concat_axis=0, tiled=True)]
    ppermute x12 -> x19, waiting for transfers between devices: 41.4 us -> 49.6 us  [exchange(): lax.ppermute(piece, axis, [(j, (j + shift) % count) for j in range(count)])]
    all_to_all x1 -> x0, starting transfers between devices: 5.78 us -> none  [local(): lax.all_to_all(shares, 'gx', split_axis=0, concat_axis=0, tiled=True)]
    dynamic_slice x2 -> x3, local copies, waits for them, and re-layouts: 4.54 us -> 4.64 us  [exchange(): lax.dynamic_slice_in_dim(cells, (here + shift) % count * width, width, ax...]
  transfers between devices with their start and end apart: 15 -> 21, of which waited for: 10 -> 13; matrix products, arithmetic and copies ran while one was open for 17% -> 17% of each run, Pallas kernels for 4% -> 4%
where the time goes in v13:
time: 157 us; the launch traced here: 156 us
  waiting for transfers between devices  56.7 us (36%)
  starting transfers between devices  31.6 us (20%)
  local copies, waits for them, and re-layouts  26.1 us (17%)
  blocking collectives  18.4 us (12%)
  other arithmetic  14.3 us (9%)
  Pallas kernels  7.02 us (4%)
    ppermute x19, waiting for transfers between devices, exchange(): lax.ppermute(piece, axis, [(j, (j + shift) % count) for j in range(count)])  49.6 us
    ppermute x19, starting transfers between devices, exchange(): lax.ppermute(piece, axis, [(j, (j + shift) % count) for j in range(count)])  25.6 us
    all_to_all x1, blocking collectives, gather_small(): return lax.all_to_all(copies, axis, split_axis=0, concat_axis=0, tiled=True)  18.4 us
    unnamed x18, local copies, waits for them, and re-layouts  16.7 us
    ppermute x1, waiting for transfers between devices, padded_2(): lax.ppermute(tail, axis, [(i, (i + 1) % count) for i in range(ends)])  7.14 us
    pallas_call x2, Pallas kernels, dft(): pl.pallas_call(functools.partial(dft_kernel, count=count, weighted=weight...  7.02 us
    convert_element_type x1, other arithmetic, local(): image = (-velocity * (forward - behind) * 0.5 + diffusion * (forward + be...  5.9 us
    ppermute x1, starting transfers between devices, padded_2(): lax.ppermute(tail, axis, [(i, (i + 1) % count) for i in range(ends)])  4.76 us
  transfers between devices with their start and end apart: 21, of which 13 were waited for; matrix products, arithmetic and copies ran while one was open for 17% of the time, Pallas kernels for 4%

profile of v13, /device:TPU:0, one launch (start us, length us, event | category | flops | bytes accessed | tf_op | source)
XLA Modules:
  0.0 156.2 jit_solution(10622509268149035385)
XLA Ops:
  0.7 3.1 %constant_dynamic-slice_fusion.10 = (bf16[32,4,16,128]{3,2,1,0:T(8,128)(2,1)}, bf16[32,4,16,128]{3,2,1,0:T(8,128)(2,1)}, bf16[32,4,16,128]{3,2,1,0:T(8,128)(2,1)S(1)}, bf16[32,4,16,128]{3,2,1,0:T(8,128)(2,1)}) fusion(bf16[32,4,64,128]{3,2,1,0:T(8,128)(2,1)} %param.5, s32[]{:T(128)S(6)} %select_n.222, s32[]{:T(128)S(6)} %select_n.218, s32[]{:T(128)S(6)} %select_n.216, ...), kind=kLoop, calls=%fused_computation.107 | loop fusion | bytes 4194320 | tf_op jit(solution)/shard_map/dynamic_slice | solution.py:43
  3.8 2.4 %collective-permute-start.8 = (bf16[32,4,16,128]{3,2,1,0:T(8,128)(2,1)}, bf16[32,4,16,128]{3,2,1,0:T(8,128)(2,1)}, u32[]{:S(2)}, u32[]{:S(2)}) collective-permute-start(bf16[32,4,16,128]{3,2,1,0:T(8,128)(2,1)} %get-tuple-element.19), channel_id=1, source_target_pairs={{0,3},{1,0},{2,1},{3,2},{4,7},{5,4},{6,5},{7,6},{8,11},{9,8},{10,9... | collective-permute-start | bytes 1572872 | tf_op jit(solution)/shard_map/ppermute | solution.py:45
  7.0 1.5 constant_dynamic-slice_fusion.18
  8.5 1.6 %collective-permute-start.2 = (bf16[32,4,16,128]{3,2,1,0:T(8,128)(2,1)}, bf16[32,4,16,128]{3,2,1,0:T(8,128)(2,1)S(1)}, u32[]{:S(2)}, u32[]{:S(2)}) collective-permute-start(bf16[32,4,16,128]{3,2,1,0:T(8,128)(2,1)} %get-tuple-element.31), channel_id=1, source_target_pairs={{0,3},{1,0},{2,1},{3,2},{4,7},{5,4},{6,5},{7,6},{8,11},{9,8},{10,9... | collective-permute-start | bytes 1572872 | tf_op jit(solution)/shard_map/ppermute | solution.py:45
  10.1 1.4 collective-permute-start.1
  13.1 1.2 copy.40
  14.3 1.2 copy.44
  16.2 2.5 %collective-permute-done.8 = bf16[32,4,16,128]{3,2,1,0:T(8,128)(2,1)} collective-permute-done((bf16[32,4,16,128]{3,2,1,0:T(8,128)(2,1)}, bf16[32,4,16,128]{3,2,1,0:T(8,128)(2,1)}, u32[]{:S(2)}, u32[]{:S(2)}) %collective-permute-start.8) | collective-permute-done | bytes 524320 | tf_op jit(solution)/shard_map/ppermute | solution.py:45
  18.7 1.2 collective-permute-start
  20.0 2.2 %copy.37 = bf16[4,8,64,128]{3,1,2,0:T(8,128)(2,1)} copy(bf16[4,8,64,128]{3,2,1,0:T(8,128)(2,1)} %bitcast.47) | data formatting | bytes 1048576
  22.2 8.9 %collective-permute-done.7 = bf16[32,4,16,128]{3,2,1,0:T(8,128)(2,1)} collective-permute-done((bf16[32,4,16,128]{3,2,1,0:T(8,128)(2,1)}, bf16[32,4,16,128]{3,2,1,0:T(8,128)(2,1)}, u32[]{:S(2)}, u32[]{:S(2)}) %collective-permute-start.7) | collective-permute-done | bytes 524320 | tf_op jit(solution)/shard_map/ppermute | solution.py:45
  31.1 2.2 %copy.38 = bf16[4,8,64,128]{3,1,2,0:T(8,128)(2,1)} copy(bf16[4,8,64,128]{3,2,1,0:T(8,128)(2,1)} %bitcast.44) | data formatting | bytes 1048576
  33.3 2.2 %copy.39 = bf16[4,8,64,128]{3,1,2,0:T(8,128)(2,1)} copy(bf16[4,8,64,128]{3,2,1,0:T(8,128)(2,1)} %bitcast.41) | data formatting | bytes 1048576
  35.5 3.4 %shard_map.77 = bf16[128,8192]{1,0:T(8,128)(2,1)} custom-call(bf16[128,256]{1,0:T(8,128)(2,1)} %concatenate.23.refs_0_, bf16[32,8192]{1,0:T(8,128)(2,1)} %bitcast.92, bf16[32,8192]{1,0:T(8,128)(2,1)} %bitcast.98, bf16[32,8192]{1,0:T(8,128)(2,1)} %bitcast.96, bf16[32,8192]{1,0:T(8,128)(2,1)} %bitcast.94), custom_call_target="tpu_custom_call" | custom-call | tf_op jit(solution)/shard_map/pallas_call | solution.py:109
  38.9 2.2 %copy.28 = bf16[16,8,64,128]{3,2,1,0:T(8,128)(2,1)S(1)} copy(bf16[16,8,64,128]{3,1,2,0:T(8,128)(2,1)} %bitcast.86) | data formatting | bytes 4194304
  41.1 1.4 dynamic-slice_bitcast_fusion.4
  42.5 1.4 collective-permute-start.10
  43.9 1.4 collective-permute-start.11
  45.5 1.1 copy.41
  46.7 6.8 %collective-permute-done.1 = bf16[32,4,16,128]{3,2,1,0:T(8,128)(2,1)S(1)} collective-permute-done((bf16[32,4,16,128]{3,2,1,0:T(8,128)(2,1)}, bf16[32,4,16,128]{3,2,1,0:T(8,128)(2,1)S(1)}, u32[]{:S(2)}, u32[]{:S(2)}) %collective-permute-start.1) | collective-permute-done | bytes 524320 | tf_op jit(solution)/shard_map/ppermute | solution.py:45
  53.5 1.2 copy.42
  54.6 1.1 copy.43
  56.4 3.6 %shard_map.76 = bf16[128,8192]{1,0:T(8,128)(2,1)} custom-call(bf16[128,256]{1,0:T(8,128)(2,1)} %concatenate.23.refs_0_, bf16[32,8192]{1,0:T(8,128)(2,1)} %bitcast.91, bf16[32,8192]{1,0:T(8,128)(2,1)} %bitcast.97, bf16[32,8192]{1,0:T(8,128)(2,1)} %bitcast.95, bf16[32,8192]{1,0:T(8,128)(2,1)} %bitcast.93, f32[1,8192]{1,0:T(1,128)} %bitcast.106), custom_call_target="tpu_custom_call" | custom-call | tf_op jit(solution)/shard_map/pallas_call | solution.py:109
  60.0 2.2 %copy.23 = bf16[16,8,64,128]{3,2,1,0:T(8,128)(2,1)S(1)} copy(bf16[16,8,64,128]{3,1,2,0:T(8,128)(2,1)} %bitcast.84) | data formatting | bytes 4194304
  62.7 1.4 collective-permute-start.4
  64.3 1.2 collective-permute-start.5
  65.6 9.3 %collective-permute-done.11 = bf16[32,4,16,128]{3,2,1,0:T(8,128)(2,1)} collective-permute-done((bf16[32,4,16,128]{3,2,1,0:T(8,128)(2,1)S(1)}, bf16[32,4,16,128]{3,2,1,0:T(8,128)(2,1)}, u32[]{:S(2)}, u32[]{:S(2)}) %collective-permute-start.11) | collective-permute-done | bytes 524320 | tf_op jit(solution)/shard_map/ppermute | solution.py:45
  74.8 1.5 pad_maximum_fusion.11
  76.7 0.8 pad_maximum_fusion.12
  77.6 1.3 collective-permute-start.12
  78.9 4.8 %collective-permute-start.13 = (bf16[32,1,64,128]{3,2,1,0:T(8,128)(2,1)S(1)}, bf16[32,1,64,128]{3,2,1,0:T(8,128)(2,1)S(1)}, u32[]{:S(2)}, u32[]{:S(2)}) collective-permute-start(bf16[32,1,64,128]{3,2,1,0:T(8,128)(2,1)S(1)} %get-tuple-element.8), channel_id=1, source_target_pairs={{0,4},{4,8},{8,12},{12,16},{16,20},{20,24},{24,28},{1,5},{5,9},{9,... | collective-permute-start | bytes 1572872 | tf_op jit(solution)/shard_map/ppermute | solution.py:22
  83.7 3.1 %collective-permute-done.3 = bf16[32,4,16,128]{3,2,1,0:T(8,128)(2,1)S(1)} collective-permute-done((bf16[32,4,16,128]{3,2,1,0:T(8,128)(2,1)S(1)}, bf16[32,4,16,128]{3,2,1,0:T(8,128)(2,1)S(1)}, u32[]{:S(2)}, u32[]{:S(2)}) %collective-permute-start.3) | collective-permute-done | bytes 524320 | tf_op jit(solution)/shard_map/ppermute | solution.py:45
  87.2 10.1 %collective-permute-done.5 = bf16[32,4,16,128]{3,2,1,0:T(8,128)(2,1)S(1)} collective-permute-done((bf16[32,4,16,128]{3,2,1,0:T(8,128)(2,1)S(1)}, bf16[32,4,16,128]{3,2,1,0:T(8,128)(2,1)S(1)}, u32[]{:S(2)}, u32[]{:S(2)}) %collective-permute-start.5) | collective-permute-done | bytes 524320 | tf_op jit(solution)/shard_map/ppermute | solution.py:45
  98.3 7.1 %collective-permute-done.13 = bf16[32,1,64,128]{3,2,1,0:T(8,128)(2,1)S(1)} collective-permute-done((bf16[32,1,64,128]{3,2,1,0:T(8,128)(2,1)S(1)}, bf16[32,1,64,128]{3,2,1,0:T(8,128)(2,1)S(1)}, u32[]{:S(2)}, u32[]{:S(2)}) %collective-permute-start.13) | collective-permute-done | bytes 524320 | tf_op jit(solution)/shard_map/ppermute | solution.py:22
  105.4 5.9 %fusion.6 = bf16[32,4,64,128]{3,2,1,0:T(8,128)(2,1)S(1)} fusion(f32[32,4,64,128]{3,2,1,0:T(8,128)S(1)} %get-tuple-element.10, bf16[32,1,64,128]{3,2,1,0:T(8,128)(2,1)S(1)} %collective-permute-done.13, bf16[32,4,16,128]{3,2,1,0:T(8,128)(2,1)S(1)} %get-tuple-element.12, bf16[32,4,16,128]{3,2,1,0:T(8,128)(2,1)S(1)} %get-tuple-element.13, ...), kind=kLoop, calls=%fused_computation.10 | loop fusion | flops 34603008 | bytes 9447424 | tf_op jit(solution)/shard_map/convert_element_type | solution.py:216
  112.1 0.9 fusion.23
  113.0 1.2 fusion.12
  115.0 2.5 %collective-permute-start.14 = (bf16[1,256,256]{2,1,0:T(8,128)(2,1)S(1)}, bf16[1,256,256]{2,1,0:T(8,128)(2,1)S(1)}, u32[]{:S(2)}, u32[]{:S(2)}) collective-permute-start(bf16[1,256,256]{2,1,0:T(8,128)(2,1)S(1)} %get-tuple-element.35), channel_id=1, source_target_pairs={{0,4},{4,8},{8,12},{12,16},{16,20},{20,24},{24,28},{28,0},{1,5},{5... | collective-permute-start | bytes 393224 | tf_op jit(solution)/shard_map/ppermute | solution.py:45
  117.5 1.6 %collective-permute-start.15 = (bf16[1,256,256]{2,1,0:T(8,128)(2,1)S(1)}, bf16[1,256,256]{2,1,0:T(8,128)(2,1)S(1)}, u32[]{:S(2)}, u32[]{:S(2)}) collective-permute-start(bf16[1,256,256]{2,1,0:T(8,128)(2,1)S(1)} %get-tuple-element.41), channel_id=1, source_target_pairs={{0,8},{4,12},{8,16},{12,20},{16,24},{20,28},{24,0},{28,4},{1,9},{5... | collective-permute-start | bytes 393224 | tf_op jit(solution)/shard_map/ppermute | solution.py:45
  119.1 1.4 collective-permute-start.16
  120.4 1.4 collective-permute-start.17
  121.9 2.0 %collective-permute-start.18 = (bf16[1,256,256]{2,1,0:T(8,128)(2,1)S(1)}, bf16[1,256,256]{2,1,0:T(8,128)(2,1)S(1)}, u32[]{:S(2)}, u32[]{:S(2)}) collective-permute-start(bf16[1,256,256]{2,1,0:T(8,128)(2,1)S(1)} %get-tuple-element.38), channel_id=1, source_target_pairs={{0,20},{4,24},{8,28},{12,0},{16,4},{20,8},{24,12},{28,16},{1,21},{... | collective-permute-start | bytes 393224 | tf_op jit(solution)/shard_map/ppermute | solution.py:45
  124.2 2.7 %collective-permute-start.19 = (bf16[1,256,256]{2,1,0:T(8,128)(2,1)S(1)}, bf16[1,256,256]{2,1,0:T(8,128)(2,1)S(1)}, u32[]{:S(2)}, u32[]{:S(2)}) collective-permute-start(bf16[1,256,256]{2,1,0:T(8,128)(2,1)S(1)} %get-tuple-element.37), channel_id=1, source_target_pairs={{0,24},{4,28},{8,0},{12,4},{16,8},{20,12},{24,16},{28,20},{1,25},{... | collective-permute-start | bytes 393224 | tf_op jit(solution)/shard_map/ppermute | solution.py:45
  126.9 1.0 collective-permute-start.20
  127.9 6.7 %collective-permute-done.16 = bf16[1,256,256]{2,1,0:T(8,128)(2,1)S(1)} collective-permute-done((bf16[1,256,256]{2,1,0:T(8,128)(2,1)S(1)}, bf16[1,256,256]{2,1,0:T(8,128)(2,1)S(1)}, u32[]{:S(2)}, u32[]{:S(2)}) %collective-permute-start.16) | collective-permute-done | bytes 131104 | tf_op jit(solution)/shard_map/ppermute | solution.py:45
  134.6 1.3 collective-permute-done.17
  136.3 18.4 %all_to_all.6 = f32[8,1,32]{2,1,0:T(1,128)S(1)} all-to-all(f32[8,1,32]{2,1,0:T(1,128)S(1)} %broadcast_in_dim.5), channel_id=1, replica_groups=mesh['gx'=8,'ka'=4] {'gx'}, dimensions={0} | all-to-all | bytes 2048 | tf_op jit(solution)/shard_map/all_to_all | solution.py:34
  155.4 0.8 slice_multiply_fusion
  (61 shorter events, 9.3 us)
Async XLA Ops:
  0.6 6.4 %copy-start = (bf16[32,4,64,128]{3,2,1,0:T(8,128)(2,1)S(1)}, bf16[32,4,64,128]{3,2,1,0:T(8,128)(2,1)}, u32[]{:S(2)}) copy-start(bf16[32,4,64,128]{3,2,1,0:T(8,128)(2,1)} %param.6) | copy-start | bytes 6291460
  3.8 10.5 %copy-start.2 = (f32[4,64]{1,0:T(4,128)S(1)}, f32[4,64]{1,0:T(4,128)}, u32[]{:S(2)}) copy-start(f32[4,64]{1,0:T(4,128)} %param.8) | copy-start | bytes 3076
  3.8 12.4 %copy-start.3 = (f32[4,64]{1,0:T(4,128)S(1)}, f32[4,64]{1,0:T(4,128)}, u32[]{:S(2)}) copy-start(f32[4,64]{1,0:T(4,128)} %param.7) | copy-start | bytes 3076
  3.8 14.9 %collective-permute-start.8 = (bf16[32,4,16,128]{3,2,1,0:T(8,128)(2,1)}, bf16[32,4,16,128]{3,2,1,0:T(8,128)(2,1)}, u32[]{:S(2)}, u32[]{:S(2)}) collective-permute-start(bf16[32,4,16,128]{3,2,1,0:T(8,128)(2,1)} %get-tuple-element.19), channel_id=1, source_target_pairs={{0,3},{1,0},{2,1},{3,2},{4,7},{5,4},{6,5},{7,6},{8,11},{9,8},{10,9... | collective-permute-start | bytes 1572872 | tf_op jit(solution)/shard_map/ppermute | solution.py:45
  6.2 24.9 %collective-permute-start.7 = (bf16[32,4,16,128]{3,2,1,0:T(8,128)(2,1)}, bf16[32,4,16,128]{3,2,1,0:T(8,128)(2,1)}, u32[]{:S(2)}, u32[]{:S(2)}) collective-permute-start(bf16[32,4,16,128]{3,2,1,0:T(8,128)(2,1)} %get-tuple-element.22), channel_id=1, source_target_pairs={{0,2},{1,3},{2,0},{3,1},{4,6},{5,7},{6,4},{7,5},{8,10},{9,11},{10,... | collective-permute-start | bytes 1572872 | tf_op jit(solution)/shard_map/ppermute | solution.py:45
  6.8 26.4 %collective-permute-start.6 = (bf16[32,4,16,128]{3,2,1,0:T(8,128)(2,1)}, bf16[32,4,16,128]{3,2,1,0:T(8,128)(2,1)}, u32[]{:S(2)}, u32[]{:S(2)}) collective-permute-start(bf16[32,4,16,128]{3,2,1,0:T(8,128)(2,1)} %get-tuple-element.20), channel_id=1, source_target_pairs={{0,1},{1,2},{2,3},{3,0},{4,5},{5,6},{6,7},{7,4},{8,9},{9,10},{10,1... | collective-permute-start | bytes 1572872 | tf_op jit(solution)/shard_map/ppermute | solution.py:45
  8.5 35.5 %collective-permute-start.2 = (bf16[32,4,16,128]{3,2,1,0:T(8,128)(2,1)}, bf16[32,4,16,128]{3,2,1,0:T(8,128)(2,1)S(1)}, u32[]{:S(2)}, u32[]{:S(2)}) collective-permute-start(bf16[32,4,16,128]{3,2,1,0:T(8,128)(2,1)} %get-tuple-element.31), channel_id=1, source_target_pairs={{0,3},{1,0},{2,1},{3,2},{4,7},{5,4},{6,5},{7,6},{8,11},{9,8},{10,9... | collective-permute-start | bytes 1572872 | tf_op jit(solution)/shard_map/ppermute | solution.py:45
  10.1 43.4 %collective-permute-start.1 = (bf16[32,4,16,128]{3,2,1,0:T(8,128)(2,1)}, bf16[32,4,16,128]{3,2,1,0:T(8,128)(2,1)S(1)}, u32[]{:S(2)}, u32[]{:S(2)}) collective-permute-start(bf16[32,4,16,128]{3,2,1,0:T(8,128)(2,1)} %get-tuple-element.34), channel_id=1, source_target_pairs={{0,2},{1,3},{2,0},{3,1},{4,6},{5,7},{6,4},{7,5},{8,10},{9,11},{10,... | collective-permute-start | bytes 1572872 | tf_op jit(solution)/shard_map/ppermute | solution.py:45
  18.7 35.9 %collective-permute-start = (bf16[32,4,16,128]{3,2,1,0:T(8,128)(2,1)}, bf16[32,4,16,128]{3,2,1,0:T(8,128)(2,1)S(1)}, u32[]{:S(2)}, u32[]{:S(2)}) collective-permute-start(bf16[32,4,16,128]{3,2,1,0:T(8,128)(2,1)} %get-tuple-element.32), channel_id=1, source_target_pairs={{0,1},{1,2},{2,3},{3,0},{4,5},{5,6},{6,7},{7,4},{8,9},{9,10},{10,1... | collective-permute-start | bytes 1572872 | tf_op jit(solution)/shard_map/ppermute | solution.py:45
  42.5 21.8 %collective-permute-start.9 = (bf16[32,4,16,128]{3,2,1,0:T(8,128)(2,1)}, bf16[32,4,16,128]{3,2,1,0:T(8,128)(2,1)S(1)}, u32[]{:S(2)}, u32[]{:S(2)}) collective-permute-start(bf16[32,4,16,128]{3,2,1,0:T(8,128)(2,1)} %get-tuple-element.18), channel_id=1, source_target_pairs={{0,1},{1,2},{2,3},{3,0},{4,5},{5,6},{6,7},{7,4},{8,9},{9,10},{10,1... | collective-permute-start | bytes 1572872 | tf_op jit(solution)/shard_map/ppermute | solution.py:45
  42.5 23.0 %collective-permute-start.10 = (bf16[32,4,16,128]{3,2,1,0:T(8,128)(2,1)}, bf16[32,4,16,128]{3,2,1,0:T(8,128)(2,1)}, u32[]{:S(2)}, u32[]{:S(2)}) collective-permute-start(bf16[32,4,16,128]{3,2,1,0:T(8,128)(2,1)} %get-tuple-element.17), channel_id=1, source_target_pairs={{0,2},{1,3},{2,0},{3,1},{4,6},{5,7},{6,4},{7,5},{8,10},{9,11},{10,... | collective-permute-start | bytes 1572872 | tf_op jit(solution)/shard_map/ppermute | solution.py:45
  43.9 30.9 %collective-permute-start.11 = (bf16[32,4,16,128]{3,2,1,0:T(8,128)(2,1)S(1)}, bf16[32,4,16,128]{3,2,1,0:T(8,128)(2,1)}, u32[]{:S(2)}, u32[]{:S(2)}) collective-permute-start(bf16[32,4,16,128]{3,2,1,0:T(8,128)(2,1)S(1)} %get-tuple-element.16), channel_id=1, source_target_pairs={{0,3},{1,0},{2,1},{3,2},{4,7},{5,4},{6,5},{7,6},{8,11},{9,8},{10,9... | collective-permute-start | bytes 1572872 | tf_op jit(solution)/shard_map/ppermute | solution.py:45
  62.7 24.1 %collective-permute-start.3 = (bf16[32,4,16,128]{3,2,1,0:T(8,128)(2,1)S(1)}, bf16[32,4,16,128]{3,2,1,0:T(8,128)(2,1)S(1)}, u32[]{:S(2)}, u32[]{:S(2)}) collective-permute-start(bf16[32,4,16,128]{3,2,1,0:T(8,128)(2,1)S(1)} %get-tuple-element.30), channel_id=1, source_target_pairs={{0,1},{1,2},{2,3},{3,0},{4,5},{5,6},{6,7},{7,4},{8,9},{9,10},{10,1... | collective-permute-start | bytes 1572872 | tf_op jit(solution)/shard_map/ppermute | solution.py:45
  62.7 24.4 %collective-permute-start.4 = (bf16[32,4,16,128]{3,2,1,0:T(8,128)(2,1)S(1)}, bf16[32,4,16,128]{3,2,1,0:T(8,128)(2,1)S(1)}, u32[]{:S(2)}, u32[]{:S(2)}) collective-permute-start(bf16[32,4,16,128]{3,2,1,0:T(8,128)(2,1)S(1)} %get-tuple-element.29), channel_id=1, source_target_pairs={{0,2},{1,3},{2,0},{3,1},{4,6},{5,7},{6,4},{7,5},{8,10},{9,11},{10,... | collective-permute-start | bytes 1572872 | tf_op jit(solution)/shard_map/ppermute | solution.py:45
  64.3 32.9 %collective-permute-start.5 = (bf16[32,4,16,128]{3,2,1,0:T(8,128)(2,1)S(1)}, bf16[32,4,16,128]{3,2,1,0:T(8,128)(2,1)S(1)}, u32[]{:S(2)}, u32[]{:S(2)}) collective-permute-start(bf16[32,4,16,128]{3,2,1,0:T(8,128)(2,1)S(1)} %get-tuple-element.28), channel_id=1, source_target_pairs={{0,3},{1,0},{2,1},{3,2},{4,7},{5,4},{6,5},{7,6},{8,11},{9,8},{10,9... | collective-permute-start | bytes 1572872 | tf_op jit(solution)/shard_map/ppermute | solution.py:45
  77.6 20.7 %collective-permute-start.12 = (bf16[32,1,64,128]{3,2,1,0:T(8,128)(2,1)S(1)}, bf16[32,1,64,128]{3,2,1,0:T(8,128)(2,1)S(1)}, u32[]{:S(2)}, u32[]{:S(2)}) collective-permute-start(bf16[32,1,64,128]{3,2,1,0:T(8,128)(2,1)S(1)} %get-tuple-element.7), channel_id=1, source_target_pairs={{4,0},{8,4},{12,8},{16,12},{20,16},{24,20},{28,24},{5,1},{9,5},{13... | collective-permute-start | bytes 1572872 | tf_op jit(solution)/shard_map/ppermute | solution.py:24
  78.9 26.5 %collective-permute-start.13 = (bf16[32,1,64,128]{3,2,1,0:T(8,128)(2,1)S(1)}, bf16[32,1,64,128]{3,2,1,0:T(8,128)(2,1)S(1)}, u32[]{:S(2)}, u32[]{:S(2)}) collective-permute-start(bf16[32,1,64,128]{3,2,1,0:T(8,128)(2,1)S(1)} %get-tuple-element.8), channel_id=1, source_target_pairs={{0,4},{4,8},{8,12},{12,16},{16,20},{20,24},{24,28},{1,5},{5,9},{9,... | collective-permute-start | bytes 1572872 | tf_op jit(solution)/shard_map/ppermute | solution.py:22
  97.5 7.9 %copy-start.1 = (f32[4,64]{1,0:T(4,128)S(1)}, f32[4,64]{1,0:T(4,128)}, u32[]{:S(2)}) copy-start(f32[4,64]{1,0:T(4,128)} %param.9) | copy-start | bytes 3076
  115.0 9.2 %collective-permute-start.14 = (bf16[1,256,256]{2,1,0:T(8,128)(2,1)S(1)}, bf16[1,256,256]{2,1,0:T(8,128)(2,1)S(1)}, u32[]{:S(2)}, u32[]{:S(2)}) collective-permute-start(bf16[1,256,256]{2,1,0:T(8,128)(2,1)S(1)} %get-tuple-element.35), channel_id=1, source_target_pairs={{0,4},{4,8},{8,12},{12,16},{16,20},{20,24},{24,28},{28,0},{1,5},{5... | collective-permute-start | bytes 393224 | tf_op jit(solution)/shard_map/ppermute | solution.py:45
  117.5 9.3 %collective-permute-start.15 = (bf16[1,256,256]{2,1,0:T(8,128)(2,1)S(1)}, bf16[1,256,256]{2,1,0:T(8,128)(2,1)S(1)}, u32[]{:S(2)}, u32[]{:S(2)}) collective-permute-start(bf16[1,256,256]{2,1,0:T(8,128)(2,1)S(1)} %get-tuple-element.41), channel_id=1, source_target_pairs={{0,8},{4,12},{8,16},{12,20},{16,24},{20,28},{24,0},{28,4},{1,9},{5... | collective-permute-start | bytes 393224 | tf_op jit(solution)/shard_map/ppermute | solution.py:45
  119.1 15.5 %collective-permute-start.16 = (bf16[1,256,256]{2,1,0:T(8,128)(2,1)S(1)}, bf16[1,256,256]{2,1,0:T(8,128)(2,1)S(1)}, u32[]{:S(2)}, u32[]{:S(2)}) collective-permute-start(bf16[1,256,256]{2,1,0:T(8,128)(2,1)S(1)} %get-tuple-element.40), channel_id=1, source_target_pairs={{0,12},{4,16},{8,20},{12,24},{16,28},{20,0},{24,4},{28,8},{1,13},{... | collective-permute-start | bytes 393224 | tf_op jit(solution)/shard_map/ppermute | solution.py:45
  120.4 15.4 %collective-permute-start.17 = (bf16[1,256,256]{2,1,0:T(8,128)(2,1)S(1)}, bf16[1,256,256]{2,1,0:T(8,128)(2,1)S(1)}, u32[]{:S(2)}, u32[]{:S(2)}) collective-permute-start(bf16[1,256,256]{2,1,0:T(8,128)(2,1)S(1)} %get-tuple-element.39), channel_id=1, source_target_pairs={{0,16},{4,20},{8,24},{12,28},{16,0},{20,4},{24,8},{28,12},{1,17},{... | collective-permute-start | bytes 393224 | tf_op jit(solution)/shard_map/ppermute | solution.py:45
  121.9 14.0 %collective-permute-start.18 = (bf16[1,256,256]{2,1,0:T(8,128)(2,1)S(1)}, bf16[1,256,256]{2,1,0:T(8,128)(2,1)S(1)}, u32[]{:S(2)}, u32[]{:S(2)}) collective-permute-start(bf16[1,256,256]{2,1,0:T(8,128)(2,1)S(1)} %get-tuple-element.38), channel_id=1, source_target_pairs={{0,20},{4,24},{8,28},{12,0},{16,4},{20,8},{24,12},{28,16},{1,21},{... | collective-permute-start | bytes 393224 | tf_op jit(solution)/shard_map/ppermute | solution.py:45
  124.2 11.7 %collective-permute-start.19 = (bf16[1,256,256]{2,1,0:T(8,128)(2,1)S(1)}, bf16[1,256,256]{2,1,0:T(8,128)(2,1)S(1)}, u32[]{:S(2)}, u32[]{:S(2)}) collective-permute-start(bf16[1,256,256]{2,1,0:T(8,128)(2,1)S(1)} %get-tuple-element.37), channel_id=1, source_target_pairs={{0,24},{4,28},{8,0},{12,4},{16,8},{20,12},{24,16},{28,20},{1,25},{... | collective-permute-start | bytes 393224 | tf_op jit(solution)/shard_map/ppermute | solution.py:45
  126.9 9.1 %collective-permute-start.20 = (bf16[1,256,256]{2,1,0:T(8,128)(2,1)S(1)}, bf16[1,256,256]{2,1,0:T(8,128)(2,1)S(1)}, u32[]{:S(2)}, u32[]{:S(2)}) collective-permute-start(bf16[1,256,256]{2,1,0:T(8,128)(2,1)S(1)} %get-tuple-element.36), channel_id=1, source_target_pairs={{0,28},{4,0},{8,4},{12,8},{16,12},{20,16},{24,20},{28,24},{1,29},{... | collective-permute-start | bytes 393224 | tf_op jit(solution)/shard_map/ppermute | solution.py:45

commit v14 on v13

--- a/solution.py
+++ b/solution.py
@@ -231,7 +231,9 @@
     shares = gram_terms.astype(jnp.bfloat16).reshape(lax.axis_size("gx"), row_count, 2 * columns)
     own_rows = sum(piece.astype(jnp.float32) for piece in exchange(shares, "gx", 0))[0]
     row_energy = jnp.sum(own_rows[:, :columns] ** 2, axis=1)
-    energy = jnp.sum(gather_small(jnp.sum(selector * row_energy[:, None], axis=0), "gx"), axis=0)
+    partial_energy = jnp.sum(selector * row_energy[:, None], axis=0)
+    copies = jnp.broadcast_to(partial_energy, (lax.axis_size("gx"), local_angles))
+    energy = sum(exchange(copies, "gx", 0))[0]
     mean_sq = energy / (2.0 * snap_count * snap_count)
     row_scale = jnp.sum(selector * lax.rsqrt(mean_sq + epsilon)[None, :], axis=1)
     hankel_gram = own_rows[:, :columns] * row_scale[:, None]

time: 157 us -> 158 us (level)
  blocking collectives: 18.4 us -> 0 us
  starting transfers between devices: 31.6 us -> 49.7 us
  waiting for transfers between devices: 56.7 us -> 58.6 us
    all_to_all x1 -> x0, blocking collectives: 18.4 us -> none  [gather_small(): return lax.all_to_all(copies, axis, split_axis=0, concat_axis=0, tiled=True)]
    ppermute x19 -> x26, starting transfers between devices: 25.6 us -> 43.7 us  [exchange(): lax.ppermute(piece, axis, [(j, (j + shift) % count) for j in range(count)])]
    ppermute x19 -> x26, waiting for transfers between devices: 49.6 us -> 51.5 us  [exchange(): lax.ppermute(piece, axis, [(j, (j + shift) % count) for j in range(count)])]
  transfers between devices with their start and end apart: 21 -> 28, of which waited for: 13 -> 15; matrix products, arithmetic and copies ran while one was open for 17% -> 17% of each run, Pallas kernels for 4% -> 4%
where the time goes in v14:
time: 158 us
  waiting for transfers between devices  58.6 us (37%)
  starting transfers between devices  49.7 us (31%)
  local copies, waits for them, and re-layouts  26.1 us (17%)
  other arithmetic  14.3 us (9%)
  Pallas kernels  7.07 us (4%)
    ppermute x26, waiting for transfers between devices, exchange(): lax.ppermute(piece, axis, [(j, (j + shift) % count) for j in range(count)])  51.5 us
    ppermute x26, starting transfers between devices, exchange(): lax.ppermute(piece, axis, [(j, (j + shift) % count) for j in range(count)])  43.7 us
    unnamed x18, local copies, waits for them, and re-layouts  16.7 us
    ppermute x1, waiting for transfers between devices, padded_2(): lax.ppermute(tail, axis, [(i, (i + 1) % count) for i in range(ends)])  7.14 us
    pallas_call x2, Pallas kernels, dft(): pl.pallas_call(functools.partial(dft_kernel, count=count, weighted=weight...  7.07 us
    convert_element_type x1, other arithmetic, local(): image = (-velocity * (forward - behind) * 0.5 + diffusion * (forward + be...  5.9 us
    ppermute x1, starting transfers between devices, padded_2(): lax.ppermute(tail, axis, [(i, (i + 1) % count) for i in range(ends)])  4.76 us
    dynamic_slice x3, local copies, waits for them, and re-layouts, exchange(): lax.dynamic_slice_in_dim(cells, (here + shift) % count * width, width, ax...  4.65 us
  transfers between devices with their start and end apart: 28, of which 15 were waited for; matrix products, arithmetic and copies ran while one was open for 17% of the time, Pallas kernels for 4%

profile of v14, /device:TPU:0, one launch (start us, length us, event | category | flops | bytes accessed | tf_op | source)
XLA Modules:
  0.0 157.8 jit_solution(8150111486993952869)
XLA Ops:
  0.7 3.1 %constant_dynamic-slice_fusion.10 = (bf16[32,4,16,128]{3,2,1,0:T(8,128)(2,1)}, bf16[32,4,16,128]{3,2,1,0:T(8,128)(2,1)}, bf16[32,4,16,128]{3,2,1,0:T(8,128)(2,1)S(1)}, bf16[32,4,16,128]{3,2,1,0:T(8,128)(2,1)}) fusion(bf16[32,4,64,128]{3,2,1,0:T(8,128)(2,1)} %param.5, s32[]{:T(128)S(6)} %select_n.246, s32[]{:T(128)S(6)} %select_n.242, s32[]{:T(128)S(6)} %select_n.240, ...), kind=kLoop, calls=%fused_computation.107 | loop fusion | bytes 4194320 | tf_op jit(solution)/shard_map/dynamic_slice | solution.py:43
  3.8 2.4 %collective-permute-start.8 = (bf16[32,4,16,128]{3,2,1,0:T(8,128)(2,1)}, bf16[32,4,16,128]{3,2,1,0:T(8,128)(2,1)}, u32[]{:S(2)}, u32[]{:S(2)}) collective-permute-start(bf16[32,4,16,128]{3,2,1,0:T(8,128)(2,1)} %get-tuple-element.21), channel_id=1, source_target_pairs={{0,3},{1,0},{2,1},{3,2},{4,7},{5,4},{6,5},{7,6},{8,11},{9,8},{10,9... | collective-permute-start | bytes 1572872 | tf_op jit(solution)/shard_map/ppermute | solution.py:45
  7.0 1.5 constant_dynamic-slice_fusion.18
  8.5 1.6 %collective-permute-start.2 = (bf16[32,4,16,128]{3,2,1,0:T(8,128)(2,1)}, bf16[32,4,16,128]{3,2,1,0:T(8,128)(2,1)S(1)}, u32[]{:S(2)}, u32[]{:S(2)}) collective-permute-start(bf16[32,4,16,128]{3,2,1,0:T(8,128)(2,1)} %get-tuple-element.33), channel_id=1, source_target_pairs={{0,3},{1,0},{2,1},{3,2},{4,7},{5,4},{6,5},{7,6},{8,11},{9,8},{10,9... | collective-permute-start | bytes 1572872 | tf_op jit(solution)/shard_map/ppermute | solution.py:45
  10.1 1.4 collective-permute-start.1
  13.1 1.1 copy.37
  14.3 1.1 copy.41
  16.2 2.5 %collective-permute-done.8 = bf16[32,4,16,128]{3,2,1,0:T(8,128)(2,1)} collective-permute-done((bf16[32,4,16,128]{3,2,1,0:T(8,128)(2,1)}, bf16[32,4,16,128]{3,2,1,0:T(8,128)(2,1)}, u32[]{:S(2)}, u32[]{:S(2)}) %collective-permute-start.8) | collective-permute-done | bytes 524320 | tf_op jit(solution)/shard_map/ppermute | solution.py:45
  18.7 1.2 collective-permute-start
  20.0 2.2 %copy.34 = bf16[4,8,64,128]{3,1,2,0:T(8,128)(2,1)} copy(bf16[4,8,64,128]{3,2,1,0:T(8,128)(2,1)} %bitcast.49) | data formatting | bytes 1048576
  22.2 8.9 %collective-permute-done.7 = bf16[32,4,16,128]{3,2,1,0:T(8,128)(2,1)} collective-permute-done((bf16[32,4,16,128]{3,2,1,0:T(8,128)(2,1)}, bf16[32,4,16,128]{3,2,1,0:T(8,128)(2,1)}, u32[]{:S(2)}, u32[]{:S(2)}) %collective-permute-start.7) | collective-permute-done | bytes 524320 | tf_op jit(solution)/shard_map/ppermute | solution.py:45
  31.1 2.2 %copy.35 = bf16[4,8,64,128]{3,1,2,0:T(8,128)(2,1)} copy(bf16[4,8,64,128]{3,2,1,0:T(8,128)(2,1)} %bitcast.46) | data formatting | bytes 1048576
  33.3 2.2 %copy.36 = bf16[4,8,64,128]{3,1,2,0:T(8,128)(2,1)} copy(bf16[4,8,64,128]{3,2,1,0:T(8,128)(2,1)} %bitcast.43) | data formatting | bytes 1048576
  35.5 3.4 %shard_map.77 = bf16[128,8192]{1,0:T(8,128)(2,1)} custom-call(bf16[128,256]{1,0:T(8,128)(2,1)} %concatenate.23.refs_0_, bf16[32,8192]{1,0:T(8,128)(2,1)} %bitcast.98, bf16[32,8192]{1,0:T(8,128)(2,1)} %bitcast.104, bf16[32,8192]{1,0:T(8,128)(2,1)} %bitcast.102, bf16[32,8192]{1,0:T(8,128)(2,1)} %bitcast.100), custom_call_target="tpu_custom_call" | custom-call | tf_op jit(solution)/shard_map/pallas_call | solution.py:109
  38.9 2.2 %copy.25 = bf16[16,8,64,128]{3,2,1,0:T(8,128)(2,1)S(1)} copy(bf16[16,8,64,128]{3,1,2,0:T(8,128)(2,1)} %bitcast.92) | data formatting | bytes 4194304
  41.1 1.4 dynamic-slice_bitcast_fusion.4
  42.6 1.4 collective-permute-start.10
  43.9 1.4 collective-permute-start.11
  45.5 1.2 copy.38
  46.7 6.7 %collective-permute-done.1 = bf16[32,4,16,128]{3,2,1,0:T(8,128)(2,1)S(1)} collective-permute-done((bf16[32,4,16,128]{3,2,1,0:T(8,128)(2,1)}, bf16[32,4,16,128]{3,2,1,0:T(8,128)(2,1)S(1)}, u32[]{:S(2)}, u32[]{:S(2)}) %collective-permute-start.1) | collective-permute-done | bytes 524320 | tf_op jit(solution)/shard_map/ppermute | solution.py:45
  54.6 1.2 copy.40
  56.4 3.6 %shard_map.76 = bf16[128,8192]{1,0:T(8,128)(2,1)} custom-call(bf16[128,256]{1,0:T(8,128)(2,1)} %concatenate.23.refs_0_, bf16[32,8192]{1,0:T(8,128)(2,1)} %bitcast.97, bf16[32,8192]{1,0:T(8,128)(2,1)} %bitcast.103, bf16[32,8192]{1,0:T(8,128)(2,1)} %bitcast.101, bf16[32,8192]{1,0:T(8,128)(2,1)} %bitcast.99, f32[1,8192]{1,0:T(1,128)} %bitcast.112), custom_call_target="tpu_custom_call" | custom-call | tf_op jit(solution)/shard_map/pallas_call | solution.py:109
  60.0 2.2 %copy.20 = bf16[16,8,64,128]{3,2,1,0:T(8,128)(2,1)S(1)} copy(bf16[16,8,64,128]{3,1,2,0:T(8,128)(2,1)} %bitcast.90) | data formatting | bytes 4194304
  62.7 1.4 collective-permute-start.4
  64.3 1.2 collective-permute-start.5
  65.6 9.2 %collective-permute-done.11 = bf16[32,4,16,128]{3,2,1,0:T(8,128)(2,1)} collective-permute-done((bf16[32,4,16,128]{3,2,1,0:T(8,128)(2,1)S(1)}, bf16[32,4,16,128]{3,2,1,0:T(8,128)(2,1)}, u32[]{:S(2)}, u32[]{:S(2)}) %collective-permute-start.11) | collective-permute-done | bytes 524320 | tf_op jit(solution)/shard_map/ppermute | solution.py:45
  74.8 1.5 pad_maximum_fusion.11
  77.6 1.3 collective-permute-start.12
  78.9 4.8 %collective-permute-start.13 = (bf16[32,1,64,128]{3,2,1,0:T(8,128)(2,1)S(1)}, bf16[32,1,64,128]{3,2,1,0:T(8,128)(2,1)S(1)}, u32[]{:S(2)}, u32[]{:S(2)}) collective-permute-start(bf16[32,1,64,128]{3,2,1,0:T(8,128)(2,1)S(1)} %get-tuple-element.10), channel_id=1, source_target_pairs={{0,4},{4,8},{8,12},{12,16},{16,20},{20,24},{24,28},{1,5},{5,9},{9,... | collective-permute-start | bytes 1572872 | tf_op jit(solution)/shard_map/ppermute | solution.py:22
  83.7 3.1 %collective-permute-done.3 = bf16[32,4,16,128]{3,2,1,0:T(8,128)(2,1)S(1)} collective-permute-done((bf16[32,4,16,128]{3,2,1,0:T(8,128)(2,1)S(1)}, bf16[32,4,16,128]{3,2,1,0:T(8,128)(2,1)S(1)}, u32[]{:S(2)}, u32[]{:S(2)}) %collective-permute-start.3) | collective-permute-done | bytes 524320 | tf_op jit(solution)/shard_map/ppermute | solution.py:45
  87.2 10.1 %collective-permute-done.5 = bf16[32,4,16,128]{3,2,1,0:T(8,128)(2,1)S(1)} collective-permute-done((bf16[32,4,16,128]{3,2,1,0:T(8,128)(2,1)S(1)}, bf16[32,4,16,128]{3,2,1,0:T(8,128)(2,1)S(1)}, u32[]{:S(2)}, u32[]{:S(2)}) %collective-permute-start.5) | collective-permute-done | bytes 524320 | tf_op jit(solution)/shard_map/ppermute | solution.py:45
  98.3 7.1 %collective-permute-done.13 = bf16[32,1,64,128]{3,2,1,0:T(8,128)(2,1)S(1)} collective-permute-done((bf16[32,1,64,128]{3,2,1,0:T(8,128)(2,1)S(1)}, bf16[32,1,64,128]{3,2,1,0:T(8,128)(2,1)S(1)}, u32[]{:S(2)}, u32[]{:S(2)}) %collective-permute-start.13) | collective-permute-done | bytes 524320 | tf_op jit(solution)/shard_map/ppermute | solution.py:22
  105.4 5.9 %fusion.6 = bf16[32,4,64,128]{3,2,1,0:T(8,128)(2,1)S(1)} fusion(f32[32,4,64,128]{3,2,1,0:T(8,128)S(1)} %get-tuple-element.12, bf16[32,1,64,128]{3,2,1,0:T(8,128)(2,1)S(1)} %collective-permute-done.13, bf16[32,4,16,128]{3,2,1,0:T(8,128)(2,1)S(1)} %get-tuple-element.14, bf16[32,4,16,128]{3,2,1,0:T(8,128)(2,1)S(1)} %get-tuple-element.15, ...), kind=kLoop, calls=%fused_computation.10 | loop fusion | flops 34603008 | bytes 9447424 | tf_op jit(solution)/shard_map/convert_element_type | solution.py:216
  113.0 1.2 fusion.12
  115.0 2.5 %collective-permute-start.14 = (bf16[1,256,256]{2,1,0:T(8,128)(2,1)S(1)}, bf16[1,256,256]{2,1,0:T(8,128)(2,1)S(1)}, u32[]{:S(2)}, u32[]{:S(2)}) collective-permute-start(bf16[1,256,256]{2,1,0:T(8,128)(2,1)S(1)} %get-tuple-element.37), channel_id=1, source_target_pairs={{0,4},{4,8},{8,12},{12,16},{16,20},{20,24},{24,28},{28,0},{1,5},{5... | collective-permute-start | bytes 393224 | tf_op jit(solution)/shard_map/ppermute | solution.py:45
  117.5 1.6 collective-permute-start.15
  119.1 1.4 collective-permute-start.16
  120.4 1.4 collective-permute-start.17
  121.9 2.0 %collective-permute-start.18 = (bf16[1,256,256]{2,1,0:T(8,128)(2,1)S(1)}, bf16[1,256,256]{2,1,0:T(8,128)(2,1)S(1)}, u32[]{:S(2)}, u32[]{:S(2)}) collective-permute-start(bf16[1,256,256]{2,1,0:T(8,128)(2,1)S(1)} %get-tuple-element.40), channel_id=1, source_target_pairs={{0,20},{4,24},{8,28},{12,0},{16,4},{20,8},{24,12},{28,16},{1,21},{... | collective-permute-start | bytes 393224 | tf_op jit(solution)/shard_map/ppermute | solution.py:45
  124.2 2.7 %collective-permute-start.19 = (bf16[1,256,256]{2,1,0:T(8,128)(2,1)S(1)}, bf16[1,256,256]{2,1,0:T(8,128)(2,1)S(1)}, u32[]{:S(2)}, u32[]{:S(2)}) collective-permute-start(bf16[1,256,256]{2,1,0:T(8,128)(2,1)S(1)} %get-tuple-element.39), channel_id=1, source_target_pairs={{0,24},{4,28},{8,0},{12,4},{16,8},{20,12},{24,16},{28,20},{1,25},{... | collective-permute-start | bytes 393224 | tf_op jit(solution)/shard_map/ppermute | solution.py:45
  127.9 6.7 %collective-permute-done.16 = bf16[1,256,256]{2,1,0:T(8,128)(2,1)S(1)} collective-permute-done((bf16[1,256,256]{2,1,0:T(8,128)(2,1)S(1)}, bf16[1,256,256]{2,1,0:T(8,128)(2,1)S(1)}, u32[]{:S(2)}, u32[]{:S(2)}) %collective-permute-start.16) | collective-permute-done | bytes 131104 | tf_op jit(solution)/shard_map/ppermute | solution.py:45
  134.6 1.3 collective-permute-done.17
  136.3 4.3 %collective-permute-start.21 = (f32[1,32]{1,0:T(1,128)S(1)}, f32[1,32]{1,0:T(1,128)S(1)}, u32[]{:S(2)}, u32[]{:S(2)}) collective-permute-start(f32[1,32]{1,0:T(1,128)S(1)} %bitcast.113), channel_id=1, source_target_pairs={{0,4},{4,8},{8,12},{12,16},{16,20},{20,24},{24,28},{28,0},{1,5},{5... | collective-permute-start | bytes 392 | tf_op jit(solution)/shard_map/ppermute | solution.py:45
  140.6 6.1 %collective-permute-start.22 = (f32[1,32]{1,0:T(1,128)S(1)}, f32[1,32]{1,0:T(1,128)S(1)}, u32[]{:S(2)}, u32[]{:S(2)}) collective-permute-start(f32[1,32]{1,0:T(1,128)S(1)} %bitcast.114), channel_id=1, source_target_pairs={{0,8},{4,12},{8,16},{12,20},{16,24},{20,28},{24,0},{28,4},{1,9},{5... | collective-permute-start | bytes 392 | tf_op jit(solution)/shard_map/ppermute | solution.py:45
  146.7 2.1 %collective-permute-start.24 = (f32[1,32]{1,0:T(1,128)S(1)}, f32[1,32]{1,0:T(1,128)S(1)}, u32[]{:S(2)}, u32[]{:S(2)}) collective-permute-start(f32[1,32]{1,0:T(1,128)S(1)} %bitcast.116), channel_id=1, source_target_pairs={{0,16},{4,20},{8,24},{12,28},{16,0},{20,4},{24,8},{28,12},{1,17},{... | collective-permute-start | bytes 392 | tf_op jit(solution)/shard_map/ppermute | solution.py:45
  148.8 3.4 %collective-permute-start.25 = (f32[1,32]{1,0:T(1,128)S(1)}, f32[1,32]{1,0:T(1,128)S(1)}, u32[]{:S(2)}, u32[]{:S(2)}) collective-permute-start(f32[1,32]{1,0:T(1,128)S(1)} %bitcast.117), channel_id=1, source_target_pairs={{0,20},{4,24},{8,28},{12,0},{16,4},{20,8},{24,12},{28,16},{1,21},{... | collective-permute-start | bytes 392 | tf_op jit(solution)/shard_map/ppermute | solution.py:45
  152.8 1.5 collective-permute-start.27
  154.4 1.3 collective-permute-done.26
  (73 shorter events, 15.3 us)
Async XLA Ops:
  0.6 6.4 %copy-start = (bf16[32,4,64,128]{3,2,1,0:T(8,128)(2,1)S(1)}, bf16[32,4,64,128]{3,2,1,0:T(8,128)(2,1)}, u32[]{:S(2)}) copy-start(bf16[32,4,64,128]{3,2,1,0:T(8,128)(2,1)} %param.6) | copy-start | bytes 6291460
  3.8 10.5 %copy-start.2 = (f32[4,64]{1,0:T(4,128)S(1)}, f32[4,64]{1,0:T(4,128)}, u32[]{:S(2)}) copy-start(f32[4,64]{1,0:T(4,128)} %param.8) | copy-start | bytes 3076
  3.8 12.4 %copy-start.3 = (f32[4,64]{1,0:T(4,128)S(1)}, f32[4,64]{1,0:T(4,128)}, u32[]{:S(2)}) copy-start(f32[4,64]{1,0:T(4,128)} %param.7) | copy-start | bytes 3076
  3.8 14.9 %collective-permute-start.8 = (bf16[32,4,16,128]{3,2,1,0:T(8,128)(2,1)}, bf16[32,4,16,128]{3,2,1,0:T(8,128)(2,1)}, u32[]{:S(2)}, u32[]{:S(2)}) collective-permute-start(bf16[32,4,16,128]{3,2,1,0:T(8,128)(2,1)} %get-tuple-element.21), channel_id=1, source_target_pairs={{0,3},{1,0},{2,1},{3,2},{4,7},{5,4},{6,5},{7,6},{8,11},{9,8},{10,9... | collective-permute-start | bytes 1572872 | tf_op jit(solution)/shard_map/ppermute | solution.py:45
  6.2 24.9 %collective-permute-start.7 = (bf16[32,4,16,128]{3,2,1,0:T(8,128)(2,1)}, bf16[32,4,16,128]{3,2,1,0:T(8,128)(2,1)}, u32[]{:S(2)}, u32[]{:S(2)}) collective-permute-start(bf16[32,4,16,128]{3,2,1,0:T(8,128)(2,1)} %get-tuple-element.24), channel_id=1, source_target_pairs={{0,2},{1,3},{2,0},{3,1},{4,6},{5,7},{6,4},{7,5},{8,10},{9,11},{10,... | collective-permute-start | bytes 1572872 | tf_op jit(solution)/shard_map/ppermute | solution.py:45
  6.8 26.4 %collective-permute-start.6 = (bf16[32,4,16,128]{3,2,1,0:T(8,128)(2,1)}, bf16[32,4,16,128]{3,2,1,0:T(8,128)(2,1)}, u32[]{:S(2)}, u32[]{:S(2)}) collective-permute-start(bf16[32,4,16,128]{3,2,1,0:T(8,128)(2,1)} %get-tuple-element.22), channel_id=1, source_target_pairs={{0,1},{1,2},{2,3},{3,0},{4,5},{5,6},{6,7},{7,4},{8,9},{9,10},{10,1... | collective-permute-start | bytes 1572872 | tf_op jit(solution)/shard_map/ppermute | solution.py:45
  8.5 35.5 %collective-permute-start.2 = (bf16[32,4,16,128]{3,2,1,0:T(8,128)(2,1)}, bf16[32,4,16,128]{3,2,1,0:T(8,128)(2,1)S(1)}, u32[]{:S(2)}, u32[]{:S(2)}) collective-permute-start(bf16[32,4,16,128]{3,2,1,0:T(8,128)(2,1)} %get-tuple-element.33), channel_id=1, source_target_pairs={{0,3},{1,0},{2,1},{3,2},{4,7},{5,4},{6,5},{7,6},{8,11},{9,8},{10,9... | collective-permute-start | bytes 1572872 | tf_op jit(solution)/shard_map/ppermute | solution.py:45
  10.1 43.4 %collective-permute-start.1 = (bf16[32,4,16,128]{3,2,1,0:T(8,128)(2,1)}, bf16[32,4,16,128]{3,2,1,0:T(8,128)(2,1)S(1)}, u32[]{:S(2)}, u32[]{:S(2)}) collective-permute-start(bf16[32,4,16,128]{3,2,1,0:T(8,128)(2,1)} %get-tuple-element.36), channel_id=1, source_target_pairs={{0,2},{1,3},{2,0},{3,1},{4,6},{5,7},{6,4},{7,5},{8,10},{9,11},{10,... | collective-permute-start | bytes 1572872 | tf_op jit(solution)/shard_map/ppermute | solution.py:45
  18.7 35.9 %collective-permute-start = (bf16[32,4,16,128]{3,2,1,0:T(8,128)(2,1)}, bf16[32,4,16,128]{3,2,1,0:T(8,128)(2,1)S(1)}, u32[]{:S(2)}, u32[]{:S(2)}) collective-permute-start(bf16[32,4,16,128]{3,2,1,0:T(8,128)(2,1)} %get-tuple-element.34), channel_id=1, source_target_pairs={{0,1},{1,2},{2,3},{3,0},{4,5},{5,6},{6,7},{7,4},{8,9},{9,10},{10,1... | collective-permute-start | bytes 1572872 | tf_op jit(solution)/shard_map/ppermute | solution.py:45
  42.6 21.8 %collective-permute-start.9 = (bf16[32,4,16,128]{3,2,1,0:T(8,128)(2,1)}, bf16[32,4,16,128]{3,2,1,0:T(8,128)(2,1)S(1)}, u32[]{:S(2)}, u32[]{:S(2)}) collective-permute-start(bf16[32,4,16,128]{3,2,1,0:T(8,128)(2,1)} %get-tuple-element.20), channel_id=1, source_target_pairs={{0,1},{1,2},{2,3},{3,0},{4,5},{5,6},{6,7},{7,4},{8,9},{9,10},{10,1... | collective-permute-start | bytes 1572872 | tf_op jit(solution)/shard_map/ppermute | solution.py:45
  42.6 23.0 %collective-permute-start.10 = (bf16[32,4,16,128]{3,2,1,0:T(8,128)(2,1)}, bf16[32,4,16,128]{3,2,1,0:T(8,128)(2,1)}, u32[]{:S(2)}, u32[]{:S(2)}) collective-permute-start(bf16[32,4,16,128]{3,2,1,0:T(8,128)(2,1)} %get-tuple-element.19), channel_id=1, source_target_pairs={{0,2},{1,3},{2,0},{3,1},{4,6},{5,7},{6,4},{7,5},{8,10},{9,11},{10,... | collective-permute-start | bytes 1572872 | tf_op jit(solution)/shard_map/ppermute | solution.py:45
  43.9 30.8 %collective-permute-start.11 = (bf16[32,4,16,128]{3,2,1,0:T(8,128)(2,1)S(1)}, bf16[32,4,16,128]{3,2,1,0:T(8,128)(2,1)}, u32[]{:S(2)}, u32[]{:S(2)}) collective-permute-start(bf16[32,4,16,128]{3,2,1,0:T(8,128)(2,1)S(1)} %get-tuple-element.18), channel_id=1, source_target_pairs={{0,3},{1,0},{2,1},{3,2},{4,7},{5,4},{6,5},{7,6},{8,11},{9,8},{10,9... | collective-permute-start | bytes 1572872 | tf_op jit(solution)/shard_map/ppermute | solution.py:45
  62.7 24.1 %collective-permute-start.3 = (bf16[32,4,16,128]{3,2,1,0:T(8,128)(2,1)S(1)}, bf16[32,4,16,128]{3,2,1,0:T(8,128)(2,1)S(1)}, u32[]{:S(2)}, u32[]{:S(2)}) collective-permute-start(bf16[32,4,16,128]{3,2,1,0:T(8,128)(2,1)S(1)} %get-tuple-element.32), channel_id=1, source_target_pairs={{0,1},{1,2},{2,3},{3,0},{4,5},{5,6},{6,7},{7,4},{8,9},{9,10},{10,1... | collective-permute-start | bytes 1572872 | tf_op jit(solution)/shard_map/ppermute | solution.py:45
  62.7 24.4 %collective-permute-start.4 = (bf16[32,4,16,128]{3,2,1,0:T(8,128)(2,1)S(1)}, bf16[32,4,16,128]{3,2,1,0:T(8,128)(2,1)S(1)}, u32[]{:S(2)}, u32[]{:S(2)}) collective-permute-start(bf16[32,4,16,128]{3,2,1,0:T(8,128)(2,1)S(1)} %get-tuple-element.31), channel_id=1, source_target_pairs={{0,2},{1,3},{2,0},{3,1},{4,6},{5,7},{6,4},{7,5},{8,10},{9,11},{10,... | collective-permute-start | bytes 1572872 | tf_op jit(solution)/shard_map/ppermute | solution.py:45
  64.3 32.9 %collective-permute-start.5 = (bf16[32,4,16,128]{3,2,1,0:T(8,128)(2,1)S(1)}, bf16[32,4,16,128]{3,2,1,0:T(8,128)(2,1)S(1)}, u32[]{:S(2)}, u32[]{:S(2)}) collective-permute-start(bf16[32,4,16,128]{3,2,1,0:T(8,128)(2,1)S(1)} %get-tuple-element.30), channel_id=1, source_target_pairs={{0,3},{1,0},{2,1},{3,2},{4,7},{5,4},{6,5},{7,6},{8,11},{9,8},{10,9... | collective-permute-start | bytes 1572872 | tf_op jit(solution)/shard_map/ppermute | solution.py:45
  77.6 20.7 %collective-permute-start.12 = (bf16[32,1,64,128]{3,2,1,0:T(8,128)(2,1)S(1)}, bf16[32,1,64,128]{3,2,1,0:T(8,128)(2,1)S(1)}, u32[]{:S(2)}, u32[]{:S(2)}) collective-permute-start(bf16[32,1,64,128]{3,2,1,0:T(8,128)(2,1)S(1)} %get-tuple-element.9), channel_id=1, source_target_pairs={{4,0},{8,4},{12,8},{16,12},{20,16},{24,20},{28,24},{5,1},{9,5},{13... | collective-permute-start | bytes 1572872 | tf_op jit(solution)/shard_map/ppermute | solution.py:24
  78.9 26.5 %collective-permute-start.13 = (bf16[32,1,64,128]{3,2,1,0:T(8,128)(2,1)S(1)}, bf16[32,1,64,128]{3,2,1,0:T(8,128)(2,1)S(1)}, u32[]{:S(2)}, u32[]{:S(2)}) collective-permute-start(bf16[32,1,64,128]{3,2,1,0:T(8,128)(2,1)S(1)} %get-tuple-element.10), channel_id=1, source_target_pairs={{0,4},{4,8},{8,12},{12,16},{16,20},{20,24},{24,28},{1,5},{5,9},{9,... | collective-permute-start | bytes 1572872 | tf_op jit(solution)/shard_map/ppermute | solution.py:22
  97.5 7.9 %copy-start.1 = (f32[4,64]{1,0:T(4,128)S(1)}, f32[4,64]{1,0:T(4,128)}, u32[]{:S(2)}) copy-start(f32[4,64]{1,0:T(4,128)} %param.9) | copy-start | bytes 3076
  115.0 9.2 %collective-permute-start.14 = (bf16[1,256,256]{2,1,0:T(8,128)(2,1)S(1)}, bf16[1,256,256]{2,1,0:T(8,128)(2,1)S(1)}, u32[]{:S(2)}, u32[]{:S(2)}) collective-permute-start(bf16[1,256,256]{2,1,0:T(8,128)(2,1)S(1)} %get-tuple-element.37), channel_id=1, source_target_pairs={{0,4},{4,8},{8,12},{12,16},{16,20},{20,24},{24,28},{28,0},{1,5},{5... | collective-permute-start | bytes 393224 | tf_op jit(solution)/shard_map/ppermute | solution.py:45
  117.5 9.3 %collective-permute-start.15 = (bf16[1,256,256]{2,1,0:T(8,128)(2,1)S(1)}, bf16[1,256,256]{2,1,0:T(8,128)(2,1)S(1)}, u32[]{:S(2)}, u32[]{:S(2)}) collective-permute-start(bf16[1,256,256]{2,1,0:T(8,128)(2,1)S(1)} %get-tuple-element.43), channel_id=1, source_target_pairs={{0,8},{4,12},{8,16},{12,20},{16,24},{20,28},{24,0},{28,4},{1,9},{5... | collective-permute-start | bytes 393224 | tf_op jit(solution)/shard_map/ppermute | solution.py:45
  119.1 15.5 %collective-permute-start.16 = (bf16[1,256,256]{2,1,0:T(8,128)(2,1)S(1)}, bf16[1,256,256]{2,1,0:T(8,128)(2,1)S(1)}, u32[]{:S(2)}, u32[]{:S(2)}) collective-permute-start(bf16[1,256,256]{2,1,0:T(8,128)(2,1)S(1)} %get-tuple-element.42), channel_id=1, source_target_pairs={{0,12},{4,16},{8,20},{12,24},{16,28},{20,0},{24,4},{28,8},{1,13},{... | collective-permute-start | bytes 393224 | tf_op jit(solution)/shard_map/ppermute | solution.py:45
  120.4 15.4 %collective-permute-start.17 = (bf16[1,256,256]{2,1,0:T(8,128)(2,1)S(1)}, bf16[1,256,256]{2,1,0:T(8,128)(2,1)S(1)}, u32[]{:S(2)}, u32[]{:S(2)}) collective-permute-start(bf16[1,256,256]{2,1,0:T(8,128)(2,1)S(1)} %get-tuple-element.41), channel_id=1, source_target_pairs={{0,16},{4,20},{8,24},{12,28},{16,0},{20,4},{24,8},{28,12},{1,17},{... | collective-permute-start | bytes 393224 | tf_op jit(solution)/shard_map/ppermute | solution.py:45
  121.9 14.0 %collective-permute-start.18 = (bf16[1,256,256]{2,1,0:T(8,128)(2,1)S(1)}, bf16[1,256,256]{2,1,0:T(8,128)(2,1)S(1)}, u32[]{:S(2)}, u32[]{:S(2)}) collective-permute-start(bf16[1,256,256]{2,1,0:T(8,128)(2,1)S(1)} %get-tuple-element.40), channel_id=1, source_target_pairs={{0,20},{4,24},{8,28},{12,0},{16,4},{20,8},{24,12},{28,16},{1,21},{... | collective-permute-start | bytes 393224 | tf_op jit(solution)/shard_map/ppermute | solution.py:45
  124.2 11.7 %collective-permute-start.19 = (bf16[1,256,256]{2,1,0:T(8,128)(2,1)S(1)}, bf16[1,256,256]{2,1,0:T(8,128)(2,1)S(1)}, u32[]{:S(2)}, u32[]{:S(2)}) collective-permute-start(bf16[1,256,256]{2,1,0:T(8,128)(2,1)S(1)} %get-tuple-element.39), channel_id=1, source_target_pairs={{0,24},{4,28},{8,0},{12,4},{16,8},{20,12},{24,16},{28,20},{1,25},{... | collective-permute-start | bytes 393224 | tf_op jit(solution)/shard_map/ppermute | solution.py:45
  126.8 9.1 %collective-permute-start.20 = (bf16[1,256,256]{2,1,0:T(8,128)(2,1)S(1)}, bf16[1,256,256]{2,1,0:T(8,128)(2,1)S(1)}, u32[]{:S(2)}, u32[]{:S(2)}) collective-permute-start(bf16[1,256,256]{2,1,0:T(8,128)(2,1)S(1)} %get-tuple-element.38), channel_id=1, source_target_pairs={{0,28},{4,0},{8,4},{12,8},{16,12},{20,16},{24,20},{28,24},{1,29},{... | collective-permute-start | bytes 393224 | tf_op jit(solution)/shard_map/ppermute | solution.py:45
  136.3 15.9 %collective-permute-start.21 = (f32[1,32]{1,0:T(1,128)S(1)}, f32[1,32]{1,0:T(1,128)S(1)}, u32[]{:S(2)}, u32[]{:S(2)}) collective-permute-start(f32[1,32]{1,0:T(1,128)S(1)} %bitcast.113), channel_id=1, source_target_pairs={{0,4},{4,8},{8,12},{12,16},{16,20},{20,24},{24,28},{28,0},{1,5},{5... | collective-permute-start | bytes 392 | tf_op jit(solution)/shard_map/ppermute | solution.py:45
  140.6 12.3 %collective-permute-start.22 = (f32[1,32]{1,0:T(1,128)S(1)}, f32[1,32]{1,0:T(1,128)S(1)}, u32[]{:S(2)}, u32[]{:S(2)}) collective-permute-start(f32[1,32]{1,0:T(1,128)S(1)} %bitcast.114), channel_id=1, source_target_pairs={{0,8},{4,12},{8,16},{12,20},{16,24},{20,28},{24,0},{28,4},{1,9},{5... | collective-permute-start | bytes 392 | tf_op jit(solution)/shard_map/ppermute | solution.py:45
  146.6 7.7 %collective-permute-start.23 = (f32[1,32]{1,0:T(1,128)S(1)}, f32[1,32]{1,0:T(1,128)S(1)}, u32[]{:S(2)}, u32[]{:S(2)}) collective-permute-start(f32[1,32]{1,0:T(1,128)S(1)} %bitcast.115), channel_id=1, source_target_pairs={{0,12},{4,16},{8,20},{12,24},{16,28},{20,0},{24,4},{28,8},{1,13},{... | collective-permute-start | bytes 392 | tf_op jit(solution)/shard_map/ppermute | solution.py:45
  146.7 7.7 %collective-permute-start.24 = (f32[1,32]{1,0:T(1,128)S(1)}, f32[1,32]{1,0:T(1,128)S(1)}, u32[]{:S(2)}, u32[]{:S(2)}) collective-permute-start(f32[1,32]{1,0:T(1,128)S(1)} %bitcast.116), channel_id=1, source_target_pairs={{0,16},{4,20},{8,24},{12,28},{16,0},{20,4},{24,8},{28,12},{1,17},{... | collective-permute-start | bytes 392 | tf_op jit(solution)/shard_map/ppermute | solution.py:45
  148.8 5.6 %collective-permute-start.25 = (f32[1,32]{1,0:T(1,128)S(1)}, f32[1,32]{1,0:T(1,128)S(1)}, u32[]{:S(2)}, u32[]{:S(2)}) collective-permute-start(f32[1,32]{1,0:T(1,128)S(1)} %bitcast.117), channel_id=1, source_target_pairs={{0,20},{4,24},{8,28},{12,0},{16,4},{20,8},{24,12},{28,16},{1,21},{... | collective-permute-start | bytes 392 | tf_op jit(solution)/shard_map/ppermute | solution.py:45
  152.2 3.5 %collective-permute-start.26 = (f32[1,32]{1,0:T(1,128)S(1)}, f32[1,32]{1,0:T(1,128)S(1)}, u32[]{:S(2)}, u32[]{:S(2)}) collective-permute-start(f32[1,32]{1,0:T(1,128)S(1)} %bitcast.118), channel_id=1, source_target_pairs={{0,24},{4,28},{8,0},{12,4},{16,8},{20,12},{24,16},{28,20},{1,25},{... | collective-permute-start | bytes 392 | tf_op jit(solution)/shard_map/ppermute | solution.py:45
  152.8 3.5 %collective-permute-start.27 = (f32[1,32]{1,0:T(1,128)S(1)}, f32[1,32]{1,0:T(1,128)S(1)}, u32[]{:S(2)}, u32[]{:S(2)}) collective-permute-start(f32[1,32]{1,0:T(1,128)S(1)} %bitcast.119), channel_id=1, source_target_pairs={{0,28},{4,0},{8,4},{12,8},{16,12},{20,16},{24,20},{28,24},{1,29},{... | collective-permute-start | bytes 392 | tf_op jit(solution)/shard_map/ppermute | solution.py:45

commit v15 on v13

--- a/solution.py
+++ b/solution.py
@@ -185,9 +185,9 @@
         return modes.reshape(total_angles, axial_cells, band, columns)
 
     direct_modes = in_source_order(exchange(transform_all(direct_snapshots), "ka", 0), "ka", 2)
-    weighted = in_source_order(
-        exchange(transform_all(adjoint_snapshots, lane_weight), "ka", 0), "ka", 2
-    )
+    weighted_all = transform_all(adjoint_snapshots, lane_weight)
+    direct_modes, weighted_all = lax.optimization_barrier((direct_modes, weighted_all))
+    weighted = in_source_order(exchange(weighted_all, "ka", 0), "ka", 2)
     padded = padded_2(direct_modes, (("gx", 1),), 1)
     field_f32 = direct_modes.astype(jnp.float32)
     forward = padded[:, 2:].astype(jnp.float32)

time: 157 us -> 159 us (1.013)
  waiting for transfers between devices: 56.7 us -> 71.4 us
  blocking collectives: 18.4 us -> 11 us
  starting transfers between devices: 31.6 us -> 26.6 us
    ppermute x19, waiting for transfers between devices: 49.6 us -> 70.9 us  [exchange(): lax.ppermute(piece, axis, [(j, (j + shift) % count) for j in range(count)])]
    all_to_all x1, blocking collectives: 18.4 us -> 11 us  [gather_small(): return lax.all_to_all(copies, axis, split_axis=0, concat_axis=0, tiled=True)]
    ppermute x1, waiting for transfers between devices: 7.14 us -> 0.5 us  [padded_2(): lax.ppermute(tail, axis, [(i, (i + 1) % count) for i in range(ends)])]
    ppermute x19, starting transfers between devices: 25.6 us -> 21.6 us  [exchange(): lax.ppermute(piece, axis, [(j, (j + shift) % count) for j in range(count)])]
  transfers between devices with their start and end apart: 21 -> 21, of which waited for: 13 -> 12; matrix products, arithmetic and copies ran while one was open for 17% -> 15% of each run, Pallas kernels for 4% -> 4%
where the time goes in v15:
time: 159 us
  waiting for transfers between devices  71.4 us (45%)
  starting transfers between devices  26.6 us (17%)
  local copies, waits for them, and re-layouts  26.2 us (16%)
  other arithmetic  14.3 us (9%)
  blocking collectives  11 us (7%)
  Pallas kernels  7.09 us (4%)
    ppermute x19, waiting for transfers between devices, exchange(): lax.ppermute(piece, axis, [(j, (j + shift) % count) for j in range(count)])  70.9 us
    ppermute x19, starting transfers between devices, exchange(): lax.ppermute(piece, axis, [(j, (j + shift) % count) for j in range(count)])  21.6 us
    unnamed x18, local copies, waits for them, and re-layouts  15.7 us
    all_to_all x1, blocking collectives, gather_small(): return lax.all_to_all(copies, axis, split_axis=0, concat_axis=0, tiled=True)  11 us
    pallas_call x2, Pallas kernels, dft(): pl.pallas_call(functools.partial(dft_kernel, count=count, weighted=weight...  7.09 us
    dynamic_slice x3, local copies, waits for them, and re-layouts, exchange(): lax.dynamic_slice_in_dim(cells, (here + shift) % count * width, width, ax...  4.68 us
    convert_element_type x1, other arithmetic, local(): image = (-velocity * (forward - behind) * 0.5 + diffusion * (forward + be...  4.41 us
    ppermute x1, starting transfers between devices, padded_2(): lax.ppermute(tail, axis, [(i, (i + 1) % count) for i in range(ends)])  3.46 us
  transfers between devices with their start and end apart: 21, of which 12 were waited for; matrix products, arithmetic and copies ran while one was open for 15% of the time, Pallas kernels for 4%

profile of v15, /device:TPU:0, one launch (start us, length us, event | category | flops | bytes accessed | tf_op | source)
XLA Modules:
  0.0 158.5 jit_solution(4506726679631572064)
XLA Ops:
  0.7 3.1 %constant_dynamic-slice_fusion.18 = (bf16[32,4,16,128]{3,2,1,0:T(8,128)(2,1)}, bf16[32,4,16,128]{3,2,1,0:T(8,128)(2,1)}, bf16[32,4,16,128]{3,2,1,0:T(8,128)(2,1)S(1)}, bf16[32,4,16,128]{3,2,1,0:T(8,128)(2,1)}) fusion(bf16[32,4,64,128]{3,2,1,0:T(8,128)(2,1)} %param.5, s32[]{:T(128)S(6)} %select_n.222, s32[]{:T(128)S(6)} %select_n.218, s32[]{:T(128)S(6)} %select_n.216, ...), kind=kLoop, calls=%fused_computation.109 | loop fusion | bytes 4194320 | tf_op jit(solution)/shard_map/dynamic_slice | solution.py:43
  4.3 2.5 %collective-permute-start.1 = (bf16[32,4,16,128]{3,2,1,0:T(8,128)(2,1)}, bf16[32,4,16,128]{3,2,1,0:T(8,128)(2,1)S(1)}, u32[]{:S(2)}, u32[]{:S(2)}) collective-permute-start(bf16[32,4,16,128]{3,2,1,0:T(8,128)(2,1)} %get-tuple-element.36), channel_id=1, source_target_pairs={{0,2},{1,3},{2,0},{3,1},{4,6},{5,7},{6,4},{7,5},{8,10},{9,11},{10,... | collective-permute-start | bytes 1572872 | tf_op jit(solution)/shard_map/ppermute | solution.py:45
  6.8 1.4 collective-permute-start.2
  8.2 1.5 constant_dynamic-slice_fusion.11
  11.2 1.2 copy.44
  12.9 0.8 concatenate.23.refs_0_
  13.6 4.5 %collective-permute-done = bf16[32,4,16,128]{3,2,1,0:T(8,128)(2,1)} collective-permute-done((bf16[32,4,16,128]{3,2,1,0:T(8,128)(2,1)}, bf16[32,4,16,128]{3,2,1,0:T(8,128)(2,1)}, u32[]{:S(2)}, u32[]{:S(2)}) %collective-permute-start) | collective-permute-done | bytes 524320 | tf_op jit(solution)/shard_map/ppermute | solution.py:45
  18.2 2.2 %copy.43 = bf16[4,8,64,128]{3,1,2,0:T(8,128)(2,1)} copy(bf16[4,8,64,128]{3,2,1,0:T(8,128)(2,1)} %bitcast.26) | data formatting | bytes 1048576
  20.4 1.2 copy.42
  21.5 9.1 %collective-permute-done.2 = bf16[32,4,16,128]{3,2,1,0:T(8,128)(2,1)S(1)} collective-permute-done((bf16[32,4,16,128]{3,2,1,0:T(8,128)(2,1)}, bf16[32,4,16,128]{3,2,1,0:T(8,128)(2,1)S(1)}, u32[]{:S(2)}, u32[]{:S(2)}) %collective-permute-start.2) | collective-permute-done | bytes 524320 | tf_op jit(solution)/shard_map/ppermute | solution.py:45
  30.6 1.2 copy.41
  31.8 3.5 %shard_map.76 = bf16[128,8192]{1,0:T(8,128)(2,1)} custom-call(bf16[128,256]{1,0:T(8,128)(2,1)} %concatenate.23.refs_0_, bf16[32,8192]{1,0:T(8,128)(2,1)} %bitcast.91, bf16[32,8192]{1,0:T(8,128)(2,1)} %bitcast.94, bf16[32,8192]{1,0:T(8,128)(2,1)} %bitcast.96, bf16[32,8192]{1,0:T(8,128)(2,1)} %bitcast.98), custom_call_target="tpu_custom_call" | custom-call | tf_op jit(solution)/shard_map/pallas_call | solution.py:109
  35.2 2.2 %copy.23 = bf16[16,8,64,128]{3,2,1,0:T(8,128)(2,1)S(1)} copy(bf16[16,8,64,128]{3,1,2,0:T(8,128)(2,1)} %bitcast.86) | data formatting | bytes 4194304
  37.4 1.5 dynamic-slice_bitcast_fusion.9
  38.9 2.1 %collective-permute-start.5 = (bf16[32,4,16,128]{3,2,1,0:T(8,128)(2,1)}, bf16[32,4,16,128]{3,2,1,0:T(8,128)(2,1)S(1)}, u32[]{:S(2)}, u32[]{:S(2)}) collective-permute-start(bf16[32,4,16,128]{3,2,1,0:T(8,128)(2,1)} %get-tuple-element.30), channel_id=1, source_target_pairs={{0,3},{1,0},{2,1},{3,2},{4,7},{5,4},{6,5},{7,6},{8,11},{9,8},{10,9... | collective-permute-start | bytes 1572872 | tf_op jit(solution)/shard_map/ppermute | solution.py:45
  41.1 1.2 copy.40
  42.4 1.2 copy.39
  43.5 1.1 copy.38
  44.7 8.4 %collective-permute-done.8 = bf16[32,4,16,128]{3,2,1,0:T(8,128)(2,1)} collective-permute-done((bf16[32,4,16,128]{3,2,1,0:T(8,128)(2,1)}, bf16[32,4,16,128]{3,2,1,0:T(8,128)(2,1)}, u32[]{:S(2)}, u32[]{:S(2)}) %collective-permute-start.8) | collective-permute-done | bytes 524320 | tf_op jit(solution)/shard_map/ppermute | solution.py:45
  53.1 2.2 %copy.37 = bf16[4,8,64,128]{3,1,2,0:T(8,128)(2,1)} copy(bf16[4,8,64,128]{3,2,1,0:T(8,128)(2,1)} %bitcast.47) | data formatting | bytes 1048576
  55.3 0.7 broadcast_in_dim.4
  56.0 3.6 %shard_map.77 = bf16[128,8192]{1,0:T(8,128)(2,1)} custom-call(bf16[128,256]{1,0:T(8,128)(2,1)} %concatenate.23.refs_0_, bf16[32,8192]{1,0:T(8,128)(2,1)} %bitcast.92, bf16[32,8192]{1,0:T(8,128)(2,1)} %bitcast.93, bf16[32,8192]{1,0:T(8,128)(2,1)} %bitcast.95, bf16[32,8192]{1,0:T(8,128)(2,1)} %bitcast.97, f32[1,8192]{1,0:T(1,128)} %bitcast.104), custom_call_target="tpu_custom_call" | custom-call | tf_op jit(solution)/shard_map/pallas_call | solution.py:109
  59.6 2.2 %copy.28 = bf16[16,8,64,128]{3,2,1,0:T(8,128)(2,1)S(1)} copy(bf16[16,8,64,128]{3,1,2,0:T(8,128)(2,1)} %bitcast.84) | data formatting | bytes 4194304
  61.8 2.5 %collective-permute-done.5 = bf16[32,4,16,128]{3,2,1,0:T(8,128)(2,1)S(1)} collective-permute-done((bf16[32,4,16,128]{3,2,1,0:T(8,128)(2,1)}, bf16[32,4,16,128]{3,2,1,0:T(8,128)(2,1)S(1)}, u32[]{:S(2)}, u32[]{:S(2)}) %collective-permute-start.5) | collective-permute-done | bytes 524320 | tf_op jit(solution)/shard_map/ppermute | solution.py:45
  64.3 10.9 %collective-permute-done.4 = bf16[32,4,16,128]{3,2,1,0:T(8,128)(2,1)} collective-permute-done((bf16[32,4,16,128]{3,2,1,0:T(8,128)(2,1)}, bf16[32,4,16,128]{3,2,1,0:T(8,128)(2,1)}, u32[]{:S(2)}, u32[]{:S(2)}) %collective-permute-start.4) | collective-permute-done | bytes 524320 | tf_op jit(solution)/shard_map/ppermute | solution.py:45
  75.2 1.5 pad_maximum_fusion.3
  77.4 1.5 dynamic-slice_bitcast_fusion.4
  78.9 2.3 %collective-permute-start.10 = (bf16[32,4,16,128]{3,2,1,0:T(8,128)(2,1)}, bf16[32,4,16,128]{3,2,1,0:T(8,128)(2,1)}, u32[]{:S(2)}, u32[]{:S(2)}) collective-permute-start(bf16[32,4,16,128]{3,2,1,0:T(8,128)(2,1)} %get-tuple-element.19), channel_id=1, source_target_pairs={{0,2},{1,3},{2,0},{3,1},{4,6},{5,7},{6,4},{7,5},{8,10},{9,11},{10,... | collective-permute-start | bytes 1572872 | tf_op jit(solution)/shard_map/ppermute | solution.py:45
  81.6 3.5 %collective-permute-start.13 = (bf16[32,1,64,128]{3,2,1,0:T(8,128)(2,1)S(1)}, bf16[32,1,64,128]{3,2,1,0:T(8,128)(2,1)S(1)}, u32[]{:S(2)}, u32[]{:S(2)}) collective-permute-start(bf16[32,1,64,128]{3,2,1,0:T(8,128)(2,1)S(1)} %get-tuple-element.12), channel_id=1, source_target_pairs={{0,4},{4,8},{8,12},{12,16},{16,20},{20,24},{24,28},{1,5},{5,9},{9,... | collective-permute-start | bytes 1572872 | tf_op jit(solution)/shard_map/ppermute | solution.py:22
  85.0 1.5 collective-permute-start.12
  87.1 2.6 %collective-permute-done.11 = bf16[32,4,16,128]{3,2,1,0:T(8,128)(2,1)} collective-permute-done((bf16[32,4,16,128]{3,2,1,0:T(8,128)(2,1)}, bf16[32,4,16,128]{3,2,1,0:T(8,128)(2,1)}, u32[]{:S(2)}, u32[]{:S(2)}) %collective-permute-start.11) | collective-permute-done | bytes 524320 | tf_op jit(solution)/shard_map/ppermute | solution.py:45
  89.6 15.7 %collective-permute-done.10 = bf16[32,4,16,128]{3,2,1,0:T(8,128)(2,1)} collective-permute-done((bf16[32,4,16,128]{3,2,1,0:T(8,128)(2,1)}, bf16[32,4,16,128]{3,2,1,0:T(8,128)(2,1)}, u32[]{:S(2)}, u32[]{:S(2)}) %collective-permute-start.10) | collective-permute-done | bytes 524320 | tf_op jit(solution)/shard_map/ppermute | solution.py:45
  105.4 1.6 %pad_maximum_fusion.5 = bf16[4,32,4,16,128]{4,3,2,1,0:T(8,128)(2,1)S(1)} fusion(bf16[1,32,4,16,128]{4,3,2,1,0:T(8,128)(2,1)} %bitcast.12, bf16[1,32,4,16,128]{4,3,2,1,0:T(8,128)(2,1)} %bitcast.11, bf16[1,32,4,16,128]{4,3,2,1,0:T(8,128)(2,1)} %bitcast.10, bf16[1,32,4,16,128]{4,3,2,1,0:T(8,128)(2,1)S(1)} %get-tuple-element.17), kind=kLoop, calls=%fused_computation.18 | loop fusion | flops 3145728 | bytes 4194304 | tf_op jit(solution)/shard_map/stack | solution.py:53
  107.9 4.4 %fusion.6 = bf16[32,4,64,128]{3,2,1,0:T(8,128)(2,1)S(1)} fusion(f32[32,4,64,128]{3,2,1,0:T(8,128)S(1)} %convert_element_type.101, bf16[32,4,64,128]{3,2,1,0:T(8,128)(2,1)S(1)} %pad_maximum_fusion.4, bf16[32,1,64,128]{3,2,1,0:T(8,128)(2,1)S(1)} %collective-permute-done.13, bf16[32,1,64,128]{3,2,1,0:T(8,128)(2,1)S(1)} %collective-permute-done.12, ...), kind=kLoop, calls=%fused_computation.10 | loop fusion | flops 17825792 | bytes 9447424 | tf_op jit(solution)/shard_map/convert_element_type | solution.py:216
  112.4 0.9 pad_maximum_fusion
  113.5 0.9 fusion.22
  114.5 1.2 fusion.12
  115.7 0.7 pad_maximum_fusion.7
  116.5 4.5 %collective-permute-start.20 = (bf16[1,256,256]{2,1,0:T(8,128)(2,1)S(1)}, bf16[1,256,256]{2,1,0:T(8,128)(2,1)S(1)}, u32[]{:S(2)}, u32[]{:S(2)}) collective-permute-start(bf16[1,256,256]{2,1,0:T(8,128)(2,1)S(1)} %get-tuple-element.38), channel_id=1, source_target_pairs={{0,28},{4,0},{8,4},{12,8},{16,12},{20,16},{24,20},{28,24},{1,29},{... | collective-permute-start | bytes 393224 | tf_op jit(solution)/shard_map/ppermute | solution.py:45
  121.0 1.5 collective-permute-start.19
  122.9 3.5 %collective-permute-start.17 = (bf16[1,256,256]{2,1,0:T(8,128)(2,1)S(1)}, bf16[1,256,256]{2,1,0:T(8,128)(2,1)S(1)}, u32[]{:S(2)}, u32[]{:S(2)}) collective-permute-start(bf16[1,256,256]{2,1,0:T(8,128)(2,1)S(1)} %get-tuple-element.41), channel_id=1, source_target_pairs={{0,16},{4,20},{8,24},{12,28},{16,0},{20,4},{24,8},{28,12},{1,17},{... | collective-permute-start | bytes 393224 | tf_op jit(solution)/shard_map/ppermute | solution.py:45
  126.4 0.9 collective-permute-start.15
  127.7 1.2 collective-permute-start.14
  128.9 1.7 %collective-permute-done.18 = bf16[1,256,256]{2,1,0:T(8,128)(2,1)S(1)} collective-permute-done((bf16[1,256,256]{2,1,0:T(8,128)(2,1)S(1)}, bf16[1,256,256]{2,1,0:T(8,128)(2,1)S(1)}, u32[]{:S(2)}, u32[]{:S(2)}) %collective-permute-start.18) | collective-permute-done | bytes 131104 | tf_op jit(solution)/shard_map/ppermute | solution.py:45
  130.5 13.8 %collective-permute-done.17 = bf16[1,256,256]{2,1,0:T(8,128)(2,1)S(1)} collective-permute-done((bf16[1,256,256]{2,1,0:T(8,128)(2,1)S(1)}, bf16[1,256,256]{2,1,0:T(8,128)(2,1)S(1)}, u32[]{:S(2)}, u32[]{:S(2)}) %collective-permute-start.17) | collective-permute-done | bytes 131104 | tf_op jit(solution)/shard_map/ppermute | solution.py:45
  144.3 1.3 collective-permute-done.16
  146.1 11.0 %all_to_all.6 = f32[8,1,32]{2,1,0:T(1,128)S(1)} all-to-all(f32[8,1,32]{2,1,0:T(1,128)S(1)} %broadcast_in_dim.5), channel_id=1, replica_groups=mesh['gx'=8,'ka'=4] {'gx'}, dimensions={0} | all-to-all | bytes 2048 | tf_op jit(solution)/shard_map/all_to_all | solution.py:34
  157.7 0.8 slice_multiply_fusion
  (62 shorter events, 7.3 us)
Async XLA Ops:
  0.7 7.5 %copy-start = (bf16[32,4,64,128]{3,2,1,0:T(8,128)(2,1)S(1)}, bf16[32,4,64,128]{3,2,1,0:T(8,128)(2,1)}, u32[]{:S(2)}) copy-start(bf16[32,4,64,128]{3,2,1,0:T(8,128)(2,1)} %param.6) | copy-start | bytes 6291460
  3.8 14.4 %collective-permute-start = (bf16[32,4,16,128]{3,2,1,0:T(8,128)(2,1)}, bf16[32,4,16,128]{3,2,1,0:T(8,128)(2,1)}, u32[]{:S(2)}, u32[]{:S(2)}) collective-permute-start(bf16[32,4,16,128]{3,2,1,0:T(8,128)(2,1)} %get-tuple-element.34), channel_id=1, source_target_pairs={{0,1},{1,2},{2,3},{3,0},{4,5},{5,6},{6,7},{7,4},{8,9},{9,10},{10,1... | collective-permute-start | bytes 1572872 | tf_op jit(solution)/shard_map/ppermute | solution.py:45
  4.3 16.1 %collective-permute-start.1 = (bf16[32,4,16,128]{3,2,1,0:T(8,128)(2,1)}, bf16[32,4,16,128]{3,2,1,0:T(8,128)(2,1)S(1)}, u32[]{:S(2)}, u32[]{:S(2)}) collective-permute-start(bf16[32,4,16,128]{3,2,1,0:T(8,128)(2,1)} %get-tuple-element.36), channel_id=1, source_target_pairs={{0,2},{1,3},{2,0},{3,1},{4,6},{5,7},{6,4},{7,5},{8,10},{9,11},{10,... | collective-permute-start | bytes 1572872 | tf_op jit(solution)/shard_map/ppermute | solution.py:45
  6.8 23.8 %collective-permute-start.2 = (bf16[32,4,16,128]{3,2,1,0:T(8,128)(2,1)}, bf16[32,4,16,128]{3,2,1,0:T(8,128)(2,1)S(1)}, u32[]{:S(2)}, u32[]{:S(2)}) collective-permute-start(bf16[32,4,16,128]{3,2,1,0:T(8,128)(2,1)} %get-tuple-element.33), channel_id=1, source_target_pairs={{0,3},{1,0},{2,1},{3,2},{4,7},{5,4},{6,5},{7,6},{8,11},{9,8},{10,9... | collective-permute-start | bytes 1572872 | tf_op jit(solution)/shard_map/ppermute | solution.py:45
  9.7 31.3 %collective-permute-start.6 = (bf16[32,4,16,128]{3,2,1,0:T(8,128)(2,1)}, bf16[32,4,16,128]{3,2,1,0:T(8,128)(2,1)S(1)}, u32[]{:S(2)}, u32[]{:S(2)}) collective-permute-start(bf16[32,4,16,128]{3,2,1,0:T(8,128)(2,1)} %get-tuple-element.22), channel_id=1, source_target_pairs={{0,1},{1,2},{2,3},{3,0},{4,5},{5,6},{6,7},{7,4},{8,9},{9,10},{10,1... | collective-permute-start | bytes 1572872 | tf_op jit(solution)/shard_map/ppermute | solution.py:45
  9.7 33.8 %collective-permute-start.7 = (bf16[32,4,16,128]{3,2,1,0:T(8,128)(2,1)}, bf16[32,4,16,128]{3,2,1,0:T(8,128)(2,1)S(1)}, u32[]{:S(2)}, u32[]{:S(2)}) collective-permute-start(bf16[32,4,16,128]{3,2,1,0:T(8,128)(2,1)} %get-tuple-element.24), channel_id=1, source_target_pairs={{0,2},{1,3},{2,0},{3,1},{4,6},{5,7},{6,4},{7,5},{8,10},{9,11},{10,... | collective-permute-start | bytes 1572872 | tf_op jit(solution)/shard_map/ppermute | solution.py:45
  18.2 34.9 %collective-permute-start.8 = (bf16[32,4,16,128]{3,2,1,0:T(8,128)(2,1)}, bf16[32,4,16,128]{3,2,1,0:T(8,128)(2,1)}, u32[]{:S(2)}, u32[]{:S(2)}) collective-permute-start(bf16[32,4,16,128]{3,2,1,0:T(8,128)(2,1)} %get-tuple-element.21), channel_id=1, source_target_pairs={{0,3},{1,0},{2,1},{3,2},{4,7},{5,4},{6,5},{7,6},{8,11},{9,8},{10,9... | collective-permute-start | bytes 1572872 | tf_op jit(solution)/shard_map/ppermute | solution.py:45
  37.4 4.9 %copy-start.2 = (f32[4,64]{1,0:T(4,128)S(1)}, f32[4,64]{1,0:T(4,128)}, u32[]{:S(2)}) copy-start(f32[4,64]{1,0:T(4,128)} %param.7) | copy-start | bytes 3076
  38.9 25.4 %collective-permute-start.5 = (bf16[32,4,16,128]{3,2,1,0:T(8,128)(2,1)}, bf16[32,4,16,128]{3,2,1,0:T(8,128)(2,1)S(1)}, u32[]{:S(2)}, u32[]{:S(2)}) collective-permute-start(bf16[32,4,16,128]{3,2,1,0:T(8,128)(2,1)} %get-tuple-element.30), channel_id=1, source_target_pairs={{0,3},{1,0},{2,1},{3,2},{4,7},{5,4},{6,5},{7,6},{8,11},{9,8},{10,9... | collective-permute-start | bytes 1572872 | tf_op jit(solution)/shard_map/ppermute | solution.py:45
  41.0 34.2 %collective-permute-start.4 = (bf16[32,4,16,128]{3,2,1,0:T(8,128)(2,1)}, bf16[32,4,16,128]{3,2,1,0:T(8,128)(2,1)}, u32[]{:S(2)}, u32[]{:S(2)}) collective-permute-start(bf16[32,4,16,128]{3,2,1,0:T(8,128)(2,1)} %get-tuple-element.31), channel_id=1, source_target_pairs={{0,2},{1,3},{2,0},{3,1},{4,6},{5,7},{6,4},{7,5},{8,10},{9,11},{10,... | collective-permute-start | bytes 1572872 | tf_op jit(solution)/shard_map/ppermute | solution.py:45
  41.0 34.2 %collective-permute-start.3 = (bf16[32,4,16,128]{3,2,1,0:T(8,128)(2,1)S(1)}, bf16[32,4,16,128]{3,2,1,0:T(8,128)(2,1)}, u32[]{:S(2)}, u32[]{:S(2)}) collective-permute-start(bf16[32,4,16,128]{3,2,1,0:T(8,128)(2,1)S(1)} %get-tuple-element.32), channel_id=1, source_target_pairs={{0,1},{1,2},{2,3},{3,0},{4,5},{5,6},{6,7},{7,4},{8,9},{9,10},{10,1... | collective-permute-start | bytes 1572872 | tf_op jit(solution)/shard_map/ppermute | solution.py:45
  77.4 4.1 %copy-start.3 = (f32[4,64]{1,0:T(4,128)S(1)}, f32[4,64]{1,0:T(4,128)}, u32[]{:S(2)}) copy-start(f32[4,64]{1,0:T(4,128)} %param.8) | copy-start | bytes 3076
  78.9 10.7 %collective-permute-start.11 = (bf16[32,4,16,128]{3,2,1,0:T(8,128)(2,1)}, bf16[32,4,16,128]{3,2,1,0:T(8,128)(2,1)}, u32[]{:S(2)}, u32[]{:S(2)}) collective-permute-start(bf16[32,4,16,128]{3,2,1,0:T(8,128)(2,1)} %get-tuple-element.18), channel_id=1, source_target_pairs={{0,3},{1,0},{2,1},{3,2},{4,7},{5,4},{6,5},{7,6},{8,11},{9,8},{10,9... | collective-permute-start | bytes 1572872 | tf_op jit(solution)/shard_map/ppermute | solution.py:45
  78.9 26.4 %collective-permute-start.10 = (bf16[32,4,16,128]{3,2,1,0:T(8,128)(2,1)}, bf16[32,4,16,128]{3,2,1,0:T(8,128)(2,1)}, u32[]{:S(2)}, u32[]{:S(2)}) collective-permute-start(bf16[32,4,16,128]{3,2,1,0:T(8,128)(2,1)} %get-tuple-element.19), channel_id=1, source_target_pairs={{0,2},{1,3},{2,0},{3,1},{4,6},{5,7},{6,4},{7,5},{8,10},{9,11},{10,... | collective-permute-start | bytes 1572872 | tf_op jit(solution)/shard_map/ppermute | solution.py:45
  81.2 24.1 %collective-permute-start.9 = (bf16[32,4,16,128]{3,2,1,0:T(8,128)(2,1)S(1)}, bf16[32,4,16,128]{3,2,1,0:T(8,128)(2,1)}, u32[]{:S(2)}, u32[]{:S(2)}) collective-permute-start(bf16[32,4,16,128]{3,2,1,0:T(8,128)(2,1)S(1)} %get-tuple-element.20), channel_id=1, source_target_pairs={{0,1},{1,2},{2,3},{3,0},{4,5},{5,6},{6,7},{7,4},{8,9},{9,10},{10,1... | collective-permute-start | bytes 1572872 | tf_op jit(solution)/shard_map/ppermute | solution.py:45
  81.6 26.4 %collective-permute-start.13 = (bf16[32,1,64,128]{3,2,1,0:T(8,128)(2,1)S(1)}, bf16[32,1,64,128]{3,2,1,0:T(8,128)(2,1)S(1)}, u32[]{:S(2)}, u32[]{:S(2)}) collective-permute-start(bf16[32,1,64,128]{3,2,1,0:T(8,128)(2,1)S(1)} %get-tuple-element.12), channel_id=1, source_target_pairs={{0,4},{4,8},{8,12},{12,16},{16,20},{20,24},{24,28},{1,5},{5,9},{9,... | collective-permute-start | bytes 1572872 | tf_op jit(solution)/shard_map/ppermute | solution.py:22
  85.0 22.9 %collective-permute-start.12 = (bf16[32,1,64,128]{3,2,1,0:T(8,128)(2,1)S(1)}, bf16[32,1,64,128]{3,2,1,0:T(8,128)(2,1)S(1)}, u32[]{:S(2)}, u32[]{:S(2)}) collective-permute-start(bf16[32,1,64,128]{3,2,1,0:T(8,128)(2,1)S(1)} %get-tuple-element.11), channel_id=1, source_target_pairs={{4,0},{8,4},{12,8},{16,12},{20,16},{24,20},{28,24},{5,1},{9,5},{13... | collective-permute-start | bytes 1572872 | tf_op jit(solution)/shard_map/ppermute | solution.py:24
  107.0 1.0 copy-start.1
  116.5 9.9 %collective-permute-start.20 = (bf16[1,256,256]{2,1,0:T(8,128)(2,1)S(1)}, bf16[1,256,256]{2,1,0:T(8,128)(2,1)S(1)}, u32[]{:S(2)}, u32[]{:S(2)}) collective-permute-start(bf16[1,256,256]{2,1,0:T(8,128)(2,1)S(1)} %get-tuple-element.38), channel_id=1, source_target_pairs={{0,28},{4,0},{8,4},{12,8},{16,12},{20,16},{24,20},{28,24},{1,29},{... | collective-permute-start | bytes 393224 | tf_op jit(solution)/shard_map/ppermute | solution.py:45
  121.0 6.7 %collective-permute-start.19 = (bf16[1,256,256]{2,1,0:T(8,128)(2,1)S(1)}, bf16[1,256,256]{2,1,0:T(8,128)(2,1)S(1)}, u32[]{:S(2)}, u32[]{:S(2)}) collective-permute-start(bf16[1,256,256]{2,1,0:T(8,128)(2,1)S(1)} %get-tuple-element.39), channel_id=1, source_target_pairs={{0,24},{4,28},{8,0},{12,4},{16,8},{20,12},{24,16},{28,20},{1,25},{... | collective-permute-start | bytes 393224 | tf_op jit(solution)/shard_map/ppermute | solution.py:45
  122.5 8.1 %collective-permute-start.18 = (bf16[1,256,256]{2,1,0:T(8,128)(2,1)S(1)}, bf16[1,256,256]{2,1,0:T(8,128)(2,1)S(1)}, u32[]{:S(2)}, u32[]{:S(2)}) collective-permute-start(bf16[1,256,256]{2,1,0:T(8,128)(2,1)S(1)} %get-tuple-element.40), channel_id=1, source_target_pairs={{0,20},{4,24},{8,28},{12,0},{16,4},{20,8},{24,12},{28,16},{1,21},{... | collective-permute-start | bytes 393224 | tf_op jit(solution)/shard_map/ppermute | solution.py:45
  122.9 21.4 %collective-permute-start.17 = (bf16[1,256,256]{2,1,0:T(8,128)(2,1)S(1)}, bf16[1,256,256]{2,1,0:T(8,128)(2,1)S(1)}, u32[]{:S(2)}, u32[]{:S(2)}) collective-permute-start(bf16[1,256,256]{2,1,0:T(8,128)(2,1)S(1)} %get-tuple-element.41), channel_id=1, source_target_pairs={{0,16},{4,20},{8,24},{12,28},{16,0},{20,4},{24,8},{28,12},{1,17},{... | collective-permute-start | bytes 393224 | tf_op jit(solution)/shard_map/ppermute | solution.py:45
  126.4 19.3 %collective-permute-start.16 = (bf16[1,256,256]{2,1,0:T(8,128)(2,1)S(1)}, bf16[1,256,256]{2,1,0:T(8,128)(2,1)S(1)}, u32[]{:S(2)}, u32[]{:S(2)}) collective-permute-start(bf16[1,256,256]{2,1,0:T(8,128)(2,1)S(1)} %get-tuple-element.42), channel_id=1, source_target_pairs={{0,12},{4,16},{8,20},{12,24},{16,28},{20,0},{24,4},{28,8},{1,13},{... | collective-permute-start | bytes 393224 | tf_op jit(solution)/shard_map/ppermute | solution.py:45
  126.4 19.3 %collective-permute-start.15 = (bf16[1,256,256]{2,1,0:T(8,128)(2,1)S(1)}, bf16[1,256,256]{2,1,0:T(8,128)(2,1)S(1)}, u32[]{:S(2)}, u32[]{:S(2)}) collective-permute-start(bf16[1,256,256]{2,1,0:T(8,128)(2,1)S(1)} %get-tuple-element.43), channel_id=1, source_target_pairs={{0,8},{4,12},{8,16},{12,20},{16,24},{20,28},{24,0},{28,4},{1,9},{5... | collective-permute-start | bytes 393224 | tf_op jit(solution)/shard_map/ppermute | solution.py:45
  127.7 18.0 %collective-permute-start.14 = (bf16[1,256,256]{2,1,0:T(8,128)(2,1)S(1)}, bf16[1,256,256]{2,1,0:T(8,128)(2,1)S(1)}, u32[]{:S(2)}, u32[]{:S(2)}) collective-permute-start(bf16[1,256,256]{2,1,0:T(8,128)(2,1)S(1)} %get-tuple-element.37), channel_id=1, source_target_pairs={{0,4},{4,8},{8,12},{12,16},{16,20},{20,24},{24,28},{28,0},{1,5},{5... | collective-permute-start | bytes 393224 | tf_op jit(solution)/shard_map/ppermute | solution.py:45

commit v16 on v13

--- a/solution.py
+++ b/solution.py
@@ -34,12 +34,15 @@
     return lax.all_to_all(copies, axis, split_axis=0, concat_axis=0, tiled=True)
 
 
-def exchange(cells, axis, split_axis):
+def exchange(cells, axis, split_axis, far_first=False):
     count = lax.axis_size(axis)
     here = lax.axis_index(axis)
     width = cells.shape[split_axis] // count
+    shifts = list(range(count))
+    if far_first:
+        shifts = [0] + sorted(range(1, count), key=lambda shift: -min(shift, count - shift))
     pieces = []
-    for shift in range(count):
+    for shift in shifts:
         piece = lax.dynamic_slice_in_dim(cells, ((here + shift) % count) * width, width, axis=split_axis)
         if shift:
             piece = lax.ppermute(piece, axis, [(j, (j + shift) % count) for j in range(count)])
@@ -229,7 +232,7 @@
         jnp.float32
     )
     shares = gram_terms.astype(jnp.bfloat16).reshape(lax.axis_size("gx"), row_count, 2 * columns)
-    own_rows = sum(piece.astype(jnp.float32) for piece in exchange(shares, "gx", 0))[0]
+    own_rows = sum(piece.astype(jnp.float32) for piece in exchange(shares, "gx", 0, True))[0]
     row_energy = jnp.sum(own_rows[:, :columns] ** 2, axis=1)
     energy = jnp.sum(gather_small(jnp.sum(selector * row_energy[:, None], axis=0), "gx"), axis=0)
     mean_sq = energy / (2.0 * snap_count * snap_count)

time: 157 us -> 156 us (level)
  blocking collectives: 18.4 us -> 11.7 us
  waiting for transfers between devices: 56.7 us -> 62.1 us
    all_to_all x1, blocking collectives: 18.4 us -> 11.7 us  [gather_small(): return lax.all_to_all(copies, axis, split_axis=0, concat_axis=0, tiled=True)]
    ppermute x19, waiting for transfers between devices: 49.6 us -> 55 us  [exchange(): lax.ppermute(piece, axis, [(j, (j + shift) % count) for j in range(count)])]
  transfers between devices with their start and end apart: 21 -> 21, of which waited for: 13 -> 13; matrix products, arithmetic and copies ran while one was open for 17% -> 17% of each run, Pallas kernels for 4% -> 5%
where the time goes in v16:
time: 156 us; the launch traced here: 155 us
  waiting for transfers between devices  62.1 us (40%)
  starting transfers between devices  32.2 us (21%)
  local copies, waits for them, and re-layouts  26.1 us (17%)
  other arithmetic  14.3 us (9%)
  blocking collectives  11.7 us (8%)
  Pallas kernels  7.02 us (4%)
    ppermute x19, waiting for transfers between devices, exchange(): lax.ppermute(piece, axis, [(j, (j + shift) % count) for j in range(count)])  55 us
    ppermute x19, starting transfers between devices, exchange(): lax.ppermute(piece, axis, [(j, (j + shift) % count) for j in range(count)])  26.1 us
    unnamed x18, local copies, waits for them, and re-layouts  16.7 us
    all_to_all x1, blocking collectives, gather_small(): return lax.all_to_all(copies, axis, split_axis=0, concat_axis=0, tiled=True)  11.7 us
    ppermute x1, waiting for transfers between devices, padded_2(): lax.ppermute(tail, axis, [(i, (i + 1) % count) for i in range(ends)])  7.14 us
    pallas_call x2, Pallas kernels, dft(): pl.pallas_call(functools.partial(dft_kernel, count=count, weighted=weight...  7.02 us
    convert_element_type x1, other arithmetic, local(): image = (-velocity * (forward - behind) * 0.5 + diffusion * (forward + be...  5.9 us
    ppermute x1, starting transfers between devices, padded_2(): lax.ppermute(tail, axis, [(i, (i + 1) % count) for i in range(ends)])  4.76 us
  transfers between devices with their start and end apart: 21, of which 13 were waited for; matrix products, arithmetic and copies ran while one was open for 17% of the time, Pallas kernels for 5%

profile of v16, /device:TPU:0, one launch (start us, length us, event | category | flops | bytes accessed | tf_op | source)
XLA Modules:
  0.0 155.4 jit_solution(13716197143647859182)
XLA Ops:
  0.7 3.1 %constant_dynamic-slice_fusion.10 = (bf16[32,4,16,128]{3,2,1,0:T(8,128)(2,1)}, bf16[32,4,16,128]{3,2,1,0:T(8,128)(2,1)}, bf16[32,4,16,128]{3,2,1,0:T(8,128)(2,1)S(1)}, bf16[32,4,16,128]{3,2,1,0:T(8,128)(2,1)}) fusion(bf16[32,4,64,128]{3,2,1,0:T(8,128)(2,1)} %param.5, s32[]{:T(128)S(6)} %select_n.222, s32[]{:T(128)S(6)} %select_n.218, s32[]{:T(128)S(6)} %select_n.216, ...), kind=kLoop, calls=%fused_computation.107 | loop fusion | bytes 4194320 | tf_op jit(solution)/shard_map/dynamic_slice | solution.py:46
  3.8 2.4 %collective-permute-start.8 = (bf16[32,4,16,128]{3,2,1,0:T(8,128)(2,1)}, bf16[32,4,16,128]{3,2,1,0:T(8,128)(2,1)}, u32[]{:S(2)}, u32[]{:S(2)}) collective-permute-start(bf16[32,4,16,128]{3,2,1,0:T(8,128)(2,1)} %get-tuple-element.19), channel_id=1, source_target_pairs={{0,3},{1,0},{2,1},{3,2},{4,7},{5,4},{6,5},{7,6},{8,11},{9,8},{10,9... | collective-permute-start | bytes 1572872 | tf_op jit(solution)/shard_map/ppermute | solution.py:48
  7.0 1.5 constant_dynamic-slice_fusion.18
  8.5 1.6 %collective-permute-start.2 = (bf16[32,4,16,128]{3,2,1,0:T(8,128)(2,1)}, bf16[32,4,16,128]{3,2,1,0:T(8,128)(2,1)S(1)}, u32[]{:S(2)}, u32[]{:S(2)}) collective-permute-start(bf16[32,4,16,128]{3,2,1,0:T(8,128)(2,1)} %get-tuple-element.31), channel_id=1, source_target_pairs={{0,3},{1,0},{2,1},{3,2},{4,7},{5,4},{6,5},{7,6},{8,11},{9,8},{10,9... | collective-permute-start | bytes 1572872 | tf_op jit(solution)/shard_map/ppermute | solution.py:48
  10.1 1.4 collective-permute-start.1
  13.1 1.2 copy.40
  14.3 1.2 copy.44
  16.2 2.5 %collective-permute-done.8 = bf16[32,4,16,128]{3,2,1,0:T(8,128)(2,1)} collective-permute-done((bf16[32,4,16,128]{3,2,1,0:T(8,128)(2,1)}, bf16[32,4,16,128]{3,2,1,0:T(8,128)(2,1)}, u32[]{:S(2)}, u32[]{:S(2)}) %collective-permute-start.8) | collective-permute-done | bytes 524320 | tf_op jit(solution)/shard_map/ppermute | solution.py:48
  18.7 1.2 collective-permute-start
  20.0 2.2 %copy.37 = bf16[4,8,64,128]{3,1,2,0:T(8,128)(2,1)} copy(bf16[4,8,64,128]{3,2,1,0:T(8,128)(2,1)} %bitcast.47) | data formatting | bytes 1048576
  22.2 8.9 %collective-permute-done.7 = bf16[32,4,16,128]{3,2,1,0:T(8,128)(2,1)} collective-permute-done((bf16[32,4,16,128]{3,2,1,0:T(8,128)(2,1)}, bf16[32,4,16,128]{3,2,1,0:T(8,128)(2,1)}, u32[]{:S(2)}, u32[]{:S(2)}) %collective-permute-start.7) | collective-permute-done | bytes 524320 | tf_op jit(solution)/shard_map/ppermute | solution.py:48
  31.1 2.2 %copy.38 = bf16[4,8,64,128]{3,1,2,0:T(8,128)(2,1)} copy(bf16[4,8,64,128]{3,2,1,0:T(8,128)(2,1)} %bitcast.44) | data formatting | bytes 1048576
  33.3 2.2 %copy.39 = bf16[4,8,64,128]{3,1,2,0:T(8,128)(2,1)} copy(bf16[4,8,64,128]{3,2,1,0:T(8,128)(2,1)} %bitcast.41) | data formatting | bytes 1048576
  35.5 3.4 %shard_map.77 = bf16[128,8192]{1,0:T(8,128)(2,1)} custom-call(bf16[128,256]{1,0:T(8,128)(2,1)} %concatenate.23.refs_0_, bf16[32,8192]{1,0:T(8,128)(2,1)} %bitcast.92, bf16[32,8192]{1,0:T(8,128)(2,1)} %bitcast.98, bf16[32,8192]{1,0:T(8,128)(2,1)} %bitcast.96, bf16[32,8192]{1,0:T(8,128)(2,1)} %bitcast.94), custom_call_target="tpu_custom_call" | custom-call | tf_op jit(solution)/shard_map/pallas_call | solution.py:112
  38.9 2.2 %copy.28 = bf16[16,8,64,128]{3,2,1,0:T(8,128)(2,1)S(1)} copy(bf16[16,8,64,128]{3,1,2,0:T(8,128)(2,1)} %bitcast.86) | data formatting | bytes 4194304
  41.1 1.4 dynamic-slice_bitcast_fusion.4
  42.5 1.4 collective-permute-start.10
  43.9 1.4 collective-permute-start.11
  45.5 1.1 copy.41
  46.7 6.8 %collective-permute-done.1 = bf16[32,4,16,128]{3,2,1,0:T(8,128)(2,1)S(1)} collective-permute-done((bf16[32,4,16,128]{3,2,1,0:T(8,128)(2,1)}, bf16[32,4,16,128]{3,2,1,0:T(8,128)(2,1)S(1)}, u32[]{:S(2)}, u32[]{:S(2)}) %collective-permute-start.1) | collective-permute-done | bytes 524320 | tf_op jit(solution)/shard_map/ppermute | solution.py:48
  53.5 1.2 copy.42
  54.6 1.1 copy.43
  56.4 3.6 %shard_map.76 = bf16[128,8192]{1,0:T(8,128)(2,1)} custom-call(bf16[128,256]{1,0:T(8,128)(2,1)} %concatenate.23.refs_0_, bf16[32,8192]{1,0:T(8,128)(2,1)} %bitcast.91, bf16[32,8192]{1,0:T(8,128)(2,1)} %bitcast.97, bf16[32,8192]{1,0:T(8,128)(2,1)} %bitcast.95, bf16[32,8192]{1,0:T(8,128)(2,1)} %bitcast.93, f32[1,8192]{1,0:T(1,128)} %bitcast.106), custom_call_target="tpu_custom_call" | custom-call | tf_op jit(solution)/shard_map/pallas_call | solution.py:112
  60.0 2.2 %copy.23 = bf16[16,8,64,128]{3,2,1,0:T(8,128)(2,1)S(1)} copy(bf16[16,8,64,128]{3,1,2,0:T(8,128)(2,1)} %bitcast.84) | data formatting | bytes 4194304
  62.7 1.4 collective-permute-start.4
  64.3 1.2 collective-permute-start.5
  65.6 9.3 %collective-permute-done.11 = bf16[32,4,16,128]{3,2,1,0:T(8,128)(2,1)} collective-permute-done((bf16[32,4,16,128]{3,2,1,0:T(8,128)(2,1)S(1)}, bf16[32,4,16,128]{3,2,1,0:T(8,128)(2,1)}, u32[]{:S(2)}, u32[]{:S(2)}) %collective-permute-start.11) | collective-permute-done | bytes 524320 | tf_op jit(solution)/shard_map/ppermute | solution.py:48
  74.8 1.5 pad_maximum_fusion.11
  76.7 0.8 pad_maximum_fusion.12
  77.6 1.3 collective-permute-start.12
  78.9 4.8 %collective-permute-start.13 = (bf16[32,1,64,128]{3,2,1,0:T(8,128)(2,1)S(1)}, bf16[32,1,64,128]{3,2,1,0:T(8,128)(2,1)S(1)}, u32[]{:S(2)}, u32[]{:S(2)}) collective-permute-start(bf16[32,1,64,128]{3,2,1,0:T(8,128)(2,1)S(1)} %get-tuple-element.8), channel_id=1, source_target_pairs={{0,4},{4,8},{8,12},{12,16},{16,20},{20,24},{24,28},{1,5},{5,9},{9,... | collective-permute-start | bytes 1572872 | tf_op jit(solution)/shard_map/ppermute | solution.py:22
  83.7 3.1 %collective-permute-done.3 = bf16[32,4,16,128]{3,2,1,0:T(8,128)(2,1)S(1)} collective-permute-done((bf16[32,4,16,128]{3,2,1,0:T(8,128)(2,1)S(1)}, bf16[32,4,16,128]{3,2,1,0:T(8,128)(2,1)S(1)}, u32[]{:S(2)}, u32[]{:S(2)}) %collective-permute-start.3) | collective-permute-done | bytes 524320 | tf_op jit(solution)/shard_map/ppermute | solution.py:48
  87.2 10.1 %collective-permute-done.5 = bf16[32,4,16,128]{3,2,1,0:T(8,128)(2,1)S(1)} collective-permute-done((bf16[32,4,16,128]{3,2,1,0:T(8,128)(2,1)S(1)}, bf16[32,4,16,128]{3,2,1,0:T(8,128)(2,1)S(1)}, u32[]{:S(2)}, u32[]{:S(2)}) %collective-permute-start.5) | collective-permute-done | bytes 524320 | tf_op jit(solution)/shard_map/ppermute | solution.py:48
  98.3 7.1 %collective-permute-done.13 = bf16[32,1,64,128]{3,2,1,0:T(8,128)(2,1)S(1)} collective-permute-done((bf16[32,1,64,128]{3,2,1,0:T(8,128)(2,1)S(1)}, bf16[32,1,64,128]{3,2,1,0:T(8,128)(2,1)S(1)}, u32[]{:S(2)}, u32[]{:S(2)}) %collective-permute-start.13) | collective-permute-done | bytes 524320 | tf_op jit(solution)/shard_map/ppermute | solution.py:22
  105.4 5.9 %fusion.6 = bf16[32,4,64,128]{3,2,1,0:T(8,128)(2,1)S(1)} fusion(f32[32,4,64,128]{3,2,1,0:T(8,128)S(1)} %get-tuple-element.10, bf16[32,1,64,128]{3,2,1,0:T(8,128)(2,1)S(1)} %collective-permute-done.13, bf16[32,4,16,128]{3,2,1,0:T(8,128)(2,1)S(1)} %get-tuple-element.12, bf16[32,4,16,128]{3,2,1,0:T(8,128)(2,1)S(1)} %get-tuple-element.13, ...), kind=kLoop, calls=%fused_computation.10 | loop fusion | flops 34603008 | bytes 9447424 | tf_op jit(solution)/shard_map/convert_element_type | solution.py:219
  112.1 0.9 fusion.23
  113.0 1.2 fusion.12
  115.0 2.7 %collective-permute-start.14 = (bf16[1,256,256]{2,1,0:T(8,128)(2,1)S(1)}, bf16[1,256,256]{2,1,0:T(8,128)(2,1)S(1)}, u32[]{:S(2)}, u32[]{:S(2)}) collective-permute-start(bf16[1,256,256]{2,1,0:T(8,128)(2,1)S(1)} %get-tuple-element.35), channel_id=1, source_target_pairs={{0,16},{4,20},{8,24},{12,28},{16,0},{20,4},{24,8},{28,12},{1,17},{... | collective-permute-start | bytes 393224 | tf_op jit(solution)/shard_map/ppermute | solution.py:48
  117.6 1.0 collective-permute-start.15
  118.6 2.9 %collective-permute-start.16 = (bf16[1,256,256]{2,1,0:T(8,128)(2,1)S(1)}, bf16[1,256,256]{2,1,0:T(8,128)(2,1)S(1)}, u32[]{:S(2)}, u32[]{:S(2)}) collective-permute-start(bf16[1,256,256]{2,1,0:T(8,128)(2,1)S(1)} %get-tuple-element.40), channel_id=1, source_target_pairs={{0,20},{4,24},{8,28},{12,0},{16,4},{20,8},{24,12},{28,16},{1,21},{... | collective-permute-start | bytes 393224 | tf_op jit(solution)/shard_map/ppermute | solution.py:48
  121.5 1.4 collective-permute-start.17
  122.8 2.5 %collective-permute-start.18 = (bf16[1,256,256]{2,1,0:T(8,128)(2,1)S(1)}, bf16[1,256,256]{2,1,0:T(8,128)(2,1)S(1)}, u32[]{:S(2)}, u32[]{:S(2)}) collective-permute-start(bf16[1,256,256]{2,1,0:T(8,128)(2,1)S(1)} %get-tuple-element.38), channel_id=1, source_target_pairs={{0,24},{4,28},{8,0},{12,4},{16,8},{20,12},{24,16},{28,20},{1,25},{... | collective-permute-start | bytes 393224 | tf_op jit(solution)/shard_map/ppermute | solution.py:48
  125.3 8.3 %collective-permute-done.14 = bf16[1,256,256]{2,1,0:T(8,128)(2,1)S(1)} collective-permute-done((bf16[1,256,256]{2,1,0:T(8,128)(2,1)S(1)}, bf16[1,256,256]{2,1,0:T(8,128)(2,1)S(1)}, u32[]{:S(2)}, u32[]{:S(2)}) %collective-permute-start.14) | collective-permute-done | bytes 131104 | tf_op jit(solution)/shard_map/ppermute | solution.py:48
  133.6 1.9 %collective-permute-done.15 = bf16[1,256,256]{2,1,0:T(8,128)(2,1)S(1)} collective-permute-done((bf16[1,256,256]{2,1,0:T(8,128)(2,1)S(1)}, bf16[1,256,256]{2,1,0:T(8,128)(2,1)S(1)}, u32[]{:S(2)}, u32[]{:S(2)}) %collective-permute-start.15) | collective-permute-done | bytes 131104 | tf_op jit(solution)/shard_map/ppermute | solution.py:48
  135.5 2.9 %collective-permute-start.20 = (bf16[1,256,256]{2,1,0:T(8,128)(2,1)S(1)}, bf16[1,256,256]{2,1,0:T(8,128)(2,1)S(1)}, u32[]{:S(2)}, u32[]{:S(2)}) collective-permute-start(bf16[1,256,256]{2,1,0:T(8,128)(2,1)S(1)} %get-tuple-element.36), channel_id=1, source_target_pairs={{0,28},{4,0},{8,4},{12,8},{16,12},{20,16},{24,20},{28,24},{1,29},{... | collective-permute-start | bytes 393224 | tf_op jit(solution)/shard_map/ppermute | solution.py:48
  138.4 3.1 %collective-permute-done.19 = bf16[1,256,256]{2,1,0:T(8,128)(2,1)S(1)} collective-permute-done((bf16[1,256,256]{2,1,0:T(8,128)(2,1)S(1)}, bf16[1,256,256]{2,1,0:T(8,128)(2,1)S(1)}, u32[]{:S(2)}, u32[]{:S(2)}) %collective-permute-start.19) | collective-permute-done | bytes 131104 | tf_op jit(solution)/shard_map/ppermute | solution.py:48
  142.2 11.7 %all_to_all.6 = f32[8,1,32]{2,1,0:T(1,128)S(1)} all-to-all(f32[8,1,32]{2,1,0:T(1,128)S(1)} %broadcast_in_dim.5), channel_id=1, replica_groups=mesh['gx'=8,'ka'=4] {'gx'}, dimensions={0} | all-to-all | bytes 2048 | tf_op jit(solution)/shard_map/all_to_all | solution.py:34
  154.6 0.8 slice_multiply_fusion
  (61 shorter events, 9.4 us)
Async XLA Ops:
  0.6 6.4 %copy-start = (bf16[32,4,64,128]{3,2,1,0:T(8,128)(2,1)S(1)}, bf16[32,4,64,128]{3,2,1,0:T(8,128)(2,1)}, u32[]{:S(2)}) copy-start(bf16[32,4,64,128]{3,2,1,0:T(8,128)(2,1)} %param.6) | copy-start | bytes 6291460
  3.8 10.5 %copy-start.2 = (f32[4,64]{1,0:T(4,128)S(1)}, f32[4,64]{1,0:T(4,128)}, u32[]{:S(2)}) copy-start(f32[4,64]{1,0:T(4,128)} %param.8) | copy-start | bytes 3076
  3.8 12.4 %copy-start.3 = (f32[4,64]{1,0:T(4,128)S(1)}, f32[4,64]{1,0:T(4,128)}, u32[]{:S(2)}) copy-start(f32[4,64]{1,0:T(4,128)} %param.7) | copy-start | bytes 3076
  3.8 14.9 %collective-permute-start.8 = (bf16[32,4,16,128]{3,2,1,0:T(8,128)(2,1)}, bf16[32,4,16,128]{3,2,1,0:T(8,128)(2,1)}, u32[]{:S(2)}, u32[]{:S(2)}) collective-permute-start(bf16[32,4,16,128]{3,2,1,0:T(8,128)(2,1)} %get-tuple-element.19), channel_id=1, source_target_pairs={{0,3},{1,0},{2,1},{3,2},{4,7},{5,4},{6,5},{7,6},{8,11},{9,8},{10,9... | collective-permute-start | bytes 1572872 | tf_op jit(solution)/shard_map/ppermute | solution.py:48
  6.2 24.9 %collective-permute-start.7 = (bf16[32,4,16,128]{3,2,1,0:T(8,128)(2,1)}, bf16[32,4,16,128]{3,2,1,0:T(8,128)(2,1)}, u32[]{:S(2)}, u32[]{:S(2)}) collective-permute-start(bf16[32,4,16,128]{3,2,1,0:T(8,128)(2,1)} %get-tuple-element.22), channel_id=1, source_target_pairs={{0,2},{1,3},{2,0},{3,1},{4,6},{5,7},{6,4},{7,5},{8,10},{9,11},{10,... | collective-permute-start | bytes 1572872 | tf_op jit(solution)/shard_map/ppermute | solution.py:48
  6.8 26.4 %collective-permute-start.6 = (bf16[32,4,16,128]{3,2,1,0:T(8,128)(2,1)}, bf16[32,4,16,128]{3,2,1,0:T(8,128)(2,1)}, u32[]{:S(2)}, u32[]{:S(2)}) collective-permute-start(bf16[32,4,16,128]{3,2,1,0:T(8,128)(2,1)} %get-tuple-element.20), channel_id=1, source_target_pairs={{0,1},{1,2},{2,3},{3,0},{4,5},{5,6},{6,7},{7,4},{8,9},{9,10},{10,1... | collective-permute-start | bytes 1572872 | tf_op jit(solution)/shard_map/ppermute | solution.py:48
  8.5 35.5 %collective-permute-start.2 = (bf16[32,4,16,128]{3,2,1,0:T(8,128)(2,1)}, bf16[32,4,16,128]{3,2,1,0:T(8,128)(2,1)S(1)}, u32[]{:S(2)}, u32[]{:S(2)}) collective-permute-start(bf16[32,4,16,128]{3,2,1,0:T(8,128)(2,1)} %get-tuple-element.31), channel_id=1, source_target_pairs={{0,3},{1,0},{2,1},{3,2},{4,7},{5,4},{6,5},{7,6},{8,11},{9,8},{10,9... | collective-permute-start | bytes 1572872 | tf_op jit(solution)/shard_map/ppermute | solution.py:48
  10.1 43.4 %collective-permute-start.1 = (bf16[32,4,16,128]{3,2,1,0:T(8,128)(2,1)}, bf16[32,4,16,128]{3,2,1,0:T(8,128)(2,1)S(1)}, u32[]{:S(2)}, u32[]{:S(2)}) collective-permute-start(bf16[32,4,16,128]{3,2,1,0:T(8,128)(2,1)} %get-tuple-element.34), channel_id=1, source_target_pairs={{0,2},{1,3},{2,0},{3,1},{4,6},{5,7},{6,4},{7,5},{8,10},{9,11},{10,... | collective-permute-start | bytes 1572872 | tf_op jit(solution)/shard_map/ppermute | solution.py:48
  18.7 35.9 %collective-permute-start = (bf16[32,4,16,128]{3,2,1,0:T(8,128)(2,1)}, bf16[32,4,16,128]{3,2,1,0:T(8,128)(2,1)S(1)}, u32[]{:S(2)}, u32[]{:S(2)}) collective-permute-start(bf16[32,4,16,128]{3,2,1,0:T(8,128)(2,1)} %get-tuple-element.32), channel_id=1, source_target_pairs={{0,1},{1,2},{2,3},{3,0},{4,5},{5,6},{6,7},{7,4},{8,9},{9,10},{10,1... | collective-permute-start | bytes 1572872 | tf_op jit(solution)/shard_map/ppermute | solution.py:48
  42.5 21.8 %collective-permute-start.9 = (bf16[32,4,16,128]{3,2,1,0:T(8,128)(2,1)}, bf16[32,4,16,128]{3,2,1,0:T(8,128)(2,1)S(1)}, u32[]{:S(2)}, u32[]{:S(2)}) collective-permute-start(bf16[32,4,16,128]{3,2,1,0:T(8,128)(2,1)} %get-tuple-element.18), channel_id=1, source_target_pairs={{0,1},{1,2},{2,3},{3,0},{4,5},{5,6},{6,7},{7,4},{8,9},{9,10},{10,1... | collective-permute-start | bytes 1572872 | tf_op jit(solution)/shard_map/ppermute | solution.py:48
  42.5 23.0 %collective-permute-start.10 = (bf16[32,4,16,128]{3,2,1,0:T(8,128)(2,1)}, bf16[32,4,16,128]{3,2,1,0:T(8,128)(2,1)}, u32[]{:S(2)}, u32[]{:S(2)}) collective-permute-start(bf16[32,4,16,128]{3,2,1,0:T(8,128)(2,1)} %get-tuple-element.17), channel_id=1, source_target_pairs={{0,2},{1,3},{2,0},{3,1},{4,6},{5,7},{6,4},{7,5},{8,10},{9,11},{10,... | collective-permute-start | bytes 1572872 | tf_op jit(solution)/shard_map/ppermute | solution.py:48
  43.9 30.9 %collective-permute-start.11 = (bf16[32,4,16,128]{3,2,1,0:T(8,128)(2,1)S(1)}, bf16[32,4,16,128]{3,2,1,0:T(8,128)(2,1)}, u32[]{:S(2)}, u32[]{:S(2)}) collective-permute-start(bf16[32,4,16,128]{3,2,1,0:T(8,128)(2,1)S(1)} %get-tuple-element.16), channel_id=1, source_target_pairs={{0,3},{1,0},{2,1},{3,2},{4,7},{5,4},{6,5},{7,6},{8,11},{9,8},{10,9... | collective-permute-start | bytes 1572872 | tf_op jit(solution)/shard_map/ppermute | solution.py:48
  62.7 24.1 %collective-permute-start.3 = (bf16[32,4,16,128]{3,2,1,0:T(8,128)(2,1)S(1)}, bf16[32,4,16,128]{3,2,1,0:T(8,128)(2,1)S(1)}, u32[]{:S(2)}, u32[]{:S(2)}) collective-permute-start(bf16[32,4,16,128]{3,2,1,0:T(8,128)(2,1)S(1)} %get-tuple-element.30), channel_id=1, source_target_pairs={{0,1},{1,2},{2,3},{3,0},{4,5},{5,6},{6,7},{7,4},{8,9},{9,10},{10,1... | collective-permute-start | bytes 1572872 | tf_op jit(solution)/shard_map/ppermute | solution.py:48
  62.7 24.4 %collective-permute-start.4 = (bf16[32,4,16,128]{3,2,1,0:T(8,128)(2,1)S(1)}, bf16[32,4,16,128]{3,2,1,0:T(8,128)(2,1)S(1)}, u32[]{:S(2)}, u32[]{:S(2)}) collective-permute-start(bf16[32,4,16,128]{3,2,1,0:T(8,128)(2,1)S(1)} %get-tuple-element.29), channel_id=1, source_target_pairs={{0,2},{1,3},{2,0},{3,1},{4,6},{5,7},{6,4},{7,5},{8,10},{9,11},{10,... | collective-permute-start | bytes 1572872 | tf_op jit(solution)/shard_map/ppermute | solution.py:48
  64.3 32.9 %collective-permute-start.5 = (bf16[32,4,16,128]{3,2,1,0:T(8,128)(2,1)S(1)}, bf16[32,4,16,128]{3,2,1,0:T(8,128)(2,1)S(1)}, u32[]{:S(2)}, u32[]{:S(2)}) collective-permute-start(bf16[32,4,16,128]{3,2,1,0:T(8,128)(2,1)S(1)} %get-tuple-element.28), channel_id=1, source_target_pairs={{0,3},{1,0},{2,1},{3,2},{4,7},{5,4},{6,5},{7,6},{8,11},{9,8},{10,9... | collective-permute-start | bytes 1572872 | tf_op jit(solution)/shard_map/ppermute | solution.py:48
  77.6 20.7 %collective-permute-start.12 = (bf16[32,1,64,128]{3,2,1,0:T(8,128)(2,1)S(1)}, bf16[32,1,64,128]{3,2,1,0:T(8,128)(2,1)S(1)}, u32[]{:S(2)}, u32[]{:S(2)}) collective-permute-start(bf16[32,1,64,128]{3,2,1,0:T(8,128)(2,1)S(1)} %get-tuple-element.7), channel_id=1, source_target_pairs={{4,0},{8,4},{12,8},{16,12},{20,16},{24,20},{28,24},{5,1},{9,5},{13... | collective-permute-start | bytes 1572872 | tf_op jit(solution)/shard_map/ppermute | solution.py:24
  78.9 26.5 %collective-permute-start.13 = (bf16[32,1,64,128]{3,2,1,0:T(8,128)(2,1)S(1)}, bf16[32,1,64,128]{3,2,1,0:T(8,128)(2,1)S(1)}, u32[]{:S(2)}, u32[]{:S(2)}) collective-permute-start(bf16[32,1,64,128]{3,2,1,0:T(8,128)(2,1)S(1)} %get-tuple-element.8), channel_id=1, source_target_pairs={{0,4},{4,8},{8,12},{12,16},{16,20},{20,24},{24,28},{1,5},{5,9},{9,... | collective-permute-start | bytes 1572872 | tf_op jit(solution)/shard_map/ppermute | solution.py:22
  97.5 7.9 %copy-start.1 = (f32[4,64]{1,0:T(4,128)S(1)}, f32[4,64]{1,0:T(4,128)}, u32[]{:S(2)}) copy-start(f32[4,64]{1,0:T(4,128)} %param.9) | copy-start | bytes 3076
  115.0 18.6 %collective-permute-start.14 = (bf16[1,256,256]{2,1,0:T(8,128)(2,1)S(1)}, bf16[1,256,256]{2,1,0:T(8,128)(2,1)S(1)}, u32[]{:S(2)}, u32[]{:S(2)}) collective-permute-start(bf16[1,256,256]{2,1,0:T(8,128)(2,1)S(1)} %get-tuple-element.35), channel_id=1, source_target_pairs={{0,16},{4,20},{8,24},{12,28},{16,0},{20,4},{24,8},{28,12},{1,17},{... | collective-permute-start | bytes 393224 | tf_op jit(solution)/shard_map/ppermute | solution.py:48
  117.6 17.9 %collective-permute-start.15 = (bf16[1,256,256]{2,1,0:T(8,128)(2,1)S(1)}, bf16[1,256,256]{2,1,0:T(8,128)(2,1)S(1)}, u32[]{:S(2)}, u32[]{:S(2)}) collective-permute-start(bf16[1,256,256]{2,1,0:T(8,128)(2,1)S(1)} %get-tuple-element.41), channel_id=1, source_target_pairs={{0,12},{4,16},{8,20},{12,24},{16,28},{20,0},{24,4},{28,8},{1,13},{... | collective-permute-start | bytes 393224 | tf_op jit(solution)/shard_map/ppermute | solution.py:48
  118.6 19.8 %collective-permute-start.16 = (bf16[1,256,256]{2,1,0:T(8,128)(2,1)S(1)}, bf16[1,256,256]{2,1,0:T(8,128)(2,1)S(1)}, u32[]{:S(2)}, u32[]{:S(2)}) collective-permute-start(bf16[1,256,256]{2,1,0:T(8,128)(2,1)S(1)} %get-tuple-element.40), channel_id=1, source_target_pairs={{0,20},{4,24},{8,28},{12,0},{16,4},{20,8},{24,12},{28,16},{1,21},{... | collective-permute-start | bytes 393224 | tf_op jit(solution)/shard_map/ppermute | solution.py:48
  121.5 16.9 %collective-permute-start.17 = (bf16[1,256,256]{2,1,0:T(8,128)(2,1)S(1)}, bf16[1,256,256]{2,1,0:T(8,128)(2,1)S(1)}, u32[]{:S(2)}, u32[]{:S(2)}) collective-permute-start(bf16[1,256,256]{2,1,0:T(8,128)(2,1)S(1)} %get-tuple-element.39), channel_id=1, source_target_pairs={{0,8},{4,12},{8,16},{12,20},{16,24},{20,28},{24,0},{28,4},{1,9},{5... | collective-permute-start | bytes 393224 | tf_op jit(solution)/shard_map/ppermute | solution.py:48
  122.8 15.6 %collective-permute-start.18 = (bf16[1,256,256]{2,1,0:T(8,128)(2,1)S(1)}, bf16[1,256,256]{2,1,0:T(8,128)(2,1)S(1)}, u32[]{:S(2)}, u32[]{:S(2)}) collective-permute-start(bf16[1,256,256]{2,1,0:T(8,128)(2,1)S(1)} %get-tuple-element.38), channel_id=1, source_target_pairs={{0,24},{4,28},{8,0},{12,4},{16,8},{20,12},{24,16},{28,20},{1,25},{... | collective-permute-start | bytes 393224 | tf_op jit(solution)/shard_map/ppermute | solution.py:48
  133.6 7.8 %collective-permute-start.19 = (bf16[1,256,256]{2,1,0:T(8,128)(2,1)S(1)}, bf16[1,256,256]{2,1,0:T(8,128)(2,1)S(1)}, u32[]{:S(2)}, u32[]{:S(2)}) collective-permute-start(bf16[1,256,256]{2,1,0:T(8,128)(2,1)S(1)} %get-tuple-element.37), channel_id=1, source_target_pairs={{0,4},{4,8},{8,12},{12,16},{16,20},{20,24},{24,28},{28,0},{1,5},{5... | collective-permute-start | bytes 393224 | tf_op jit(solution)/shard_map/ppermute | solution.py:48
  135.5 6.4 %collective-permute-start.20 = (bf16[1,256,256]{2,1,0:T(8,128)(2,1)S(1)}, bf16[1,256,256]{2,1,0:T(8,128)(2,1)S(1)}, u32[]{:S(2)}, u32[]{:S(2)}) collective-permute-start(bf16[1,256,256]{2,1,0:T(8,128)(2,1)S(1)} %get-tuple-element.36), channel_id=1, source_target_pairs={{0,28},{4,0},{8,4},{12,8},{16,12},{20,16},{24,20},{28,24},{1,29},{... | collective-permute-start | bytes 393224 | tf_op jit(solution)/shard_map/ppermute | solution.py:48

commit v17 on v16

--- a/solution.py
+++ b/solution.py
@@ -41,12 +41,12 @@
     shifts = list(range(count))
     if far_first:
         shifts = [0] + sorted(range(1, count), key=lambda shift: -min(shift, count - shift))
-    pieces = []
+    pieces = [None] * count
     for shift in shifts:
         piece = lax.dynamic_slice_in_dim(cells, ((here + shift) % count) * width, width, axis=split_axis)
         if shift:
             piece = lax.ppermute(piece, axis, [(j, (j + shift) % count) for j in range(count)])
-        pieces.append(piece)
+        pieces[shift] = piece
     return pieces
 
 
@@ -183,13 +183,13 @@
     lane_weight = jnp.broadcast_to(band_weight[:, :, None], (axial_cells, band, columns)).reshape(1, lanes)
 
     def transform_all(snapshots, weight=None):
-        pieces = [piece.reshape(local_angles, lanes) for piece in exchange(snapshots, "ka", 2)]
+        pieces = [piece.reshape(local_angles, lanes) for piece in exchange(snapshots, "ka", 2, True)]
         modes = dft(table, pieces, weight)
         return modes.reshape(total_angles, axial_cells, band, columns)
 
-    direct_modes = in_source_order(exchange(transform_all(direct_snapshots), "ka", 0), "ka", 2)
+    direct_modes = in_source_order(exchange(transform_all(direct_snapshots), "ka", 0, True), "ka", 2)
     weighted = in_source_order(
-        exchange(transform_all(adjoint_snapshots, lane_weight), "ka", 0), "ka", 2
+        exchange(transform_all(adjoint_snapshots, lane_weight), "ka", 0, True), "ka", 2
     )
     padded = padded_2(direct_modes, (("gx", 1),), 1)
     field_f32 = direct_modes.astype(jnp.float32)

time: 156 us -> 157 us (level)
  blocking collectives: 11.7 us -> 18.4 us
  waiting for transfers between devices: 62.1 us -> 56.7 us
    all_to_all x1, blocking collectives: 11.7 us -> 18.4 us  [gather_small(): return lax.all_to_all(copies, axis, split_axis=0, concat_axis=0, tiled=True)]
    ppermute x19, waiting for transfers between devices: 55 us -> 49.6 us  [exchange(): lax.ppermute(piece, axis, [(j, (j + shift) % count) for j in range(count)])]
  transfers between devices with their start and end apart: 21 -> 21, of which waited for: 13 -> 13; matrix products, arithmetic and copies ran while one was open for 17% -> 17% of each run, Pallas kernels for 5% -> 4%
where the time goes in v17:
time: 157 us; the launch traced here: 156 us
  waiting for transfers between devices  56.7 us (36%)
  starting transfers between devices  31.6 us (20%)
  local copies, waits for them, and re-layouts  26.1 us (17%)
  blocking collectives  18.4 us (12%)
  other arithmetic  14.3 us (9%)
  Pallas kernels  7.02 us (4%)
    ppermute x19, waiting for transfers between devices, exchange(): lax.ppermute(piece, axis, [(j, (j + shift) % count) for j in range(count)])  49.6 us
    ppermute x19, starting transfers between devices, exchange(): lax.ppermute(piece, axis, [(j, (j + shift) % count) for j in range(count)])  25.6 us
    all_to_all x1, blocking collectives, gather_small(): return lax.all_to_all(copies, axis, split_axis=0, concat_axis=0, tiled=True)  18.4 us
    unnamed x18, local copies, waits for them, and re-layouts  16.7 us
    ppermute x1, waiting for transfers between devices, padded_2(): lax.ppermute(tail, axis, [(i, (i + 1) % count) for i in range(ends)])  7.14 us
    pallas_call x2, Pallas kernels, dft(): pl.pallas_call(functools.partial(dft_kernel, count=count, weighted=weight...  7.02 us
    convert_element_type x1, other arithmetic, local(): image = (-velocity * (forward - behind) * 0.5 + diffusion * (forward + be...  5.9 us
    ppermute x1, starting transfers between devices, padded_2(): lax.ppermute(tail, axis, [(i, (i + 1) % count) for i in range(ends)])  4.76 us
  transfers between devices with their start and end apart: 21, of which 13 were waited for; matrix products, arithmetic and copies ran while one was open for 17% of the time, Pallas kernels for 4%

profile of v17, /device:TPU:0, one launch (start us, length us, event | category | flops | bytes accessed | tf_op | source)
XLA Modules:
  0.0 156.2 jit_solution(10622509268149035385)
XLA Ops:
  0.7 3.1 %constant_dynamic-slice_fusion.10 = (bf16[32,4,16,128]{3,2,1,0:T(8,128)(2,1)}, bf16[32,4,16,128]{3,2,1,0:T(8,128)(2,1)}, bf16[32,4,16,128]{3,2,1,0:T(8,128)(2,1)S(1)}, bf16[32,4,16,128]{3,2,1,0:T(8,128)(2,1)}) fusion(bf16[32,4,64,128]{3,2,1,0:T(8,128)(2,1)} %param.5, s32[]{:T(128)S(6)} %select_n.222, s32[]{:T(128)S(6)} %select_n.218, s32[]{:T(128)S(6)} %select_n.216, ...), kind=kLoop, calls=%fused_computation.107 | loop fusion | bytes 4194320 | tf_op jit(solution)/shard_map/dynamic_slice | solution.py:46
  3.8 2.4 %collective-permute-start.8 = (bf16[32,4,16,128]{3,2,1,0:T(8,128)(2,1)}, bf16[32,4,16,128]{3,2,1,0:T(8,128)(2,1)}, u32[]{:S(2)}, u32[]{:S(2)}) collective-permute-start(bf16[32,4,16,128]{3,2,1,0:T(8,128)(2,1)} %get-tuple-element.19), channel_id=1, source_target_pairs={{0,3},{1,0},{2,1},{3,2},{4,7},{5,4},{6,5},{7,6},{8,11},{9,8},{10,9... | collective-permute-start | bytes 1572872 | tf_op jit(solution)/shard_map/ppermute | solution.py:48
  7.0 1.5 constant_dynamic-slice_fusion.18
  8.5 1.6 %collective-permute-start.2 = (bf16[32,4,16,128]{3,2,1,0:T(8,128)(2,1)}, bf16[32,4,16,128]{3,2,1,0:T(8,128)(2,1)S(1)}, u32[]{:S(2)}, u32[]{:S(2)}) collective-permute-start(bf16[32,4,16,128]{3,2,1,0:T(8,128)(2,1)} %get-tuple-element.31), channel_id=1, source_target_pairs={{0,3},{1,0},{2,1},{3,2},{4,7},{5,4},{6,5},{7,6},{8,11},{9,8},{10,9... | collective-permute-start | bytes 1572872 | tf_op jit(solution)/shard_map/ppermute | solution.py:48
  10.1 1.4 collective-permute-start.1
  13.1 1.2 copy.40
  14.3 1.2 copy.44
  16.2 2.5 %collective-permute-done.8 = bf16[32,4,16,128]{3,2,1,0:T(8,128)(2,1)} collective-permute-done((bf16[32,4,16,128]{3,2,1,0:T(8,128)(2,1)}, bf16[32,4,16,128]{3,2,1,0:T(8,128)(2,1)}, u32[]{:S(2)}, u32[]{:S(2)}) %collective-permute-start.8) | collective-permute-done | bytes 524320 | tf_op jit(solution)/shard_map/ppermute | solution.py:48
  18.7 1.2 collective-permute-start
  20.0 2.2 %copy.37 = bf16[4,8,64,128]{3,1,2,0:T(8,128)(2,1)} copy(bf16[4,8,64,128]{3,2,1,0:T(8,128)(2,1)} %bitcast.47) | data formatting | bytes 1048576
  22.2 8.9 %collective-permute-done.7 = bf16[32,4,16,128]{3,2,1,0:T(8,128)(2,1)} collective-permute-done((bf16[32,4,16,128]{3,2,1,0:T(8,128)(2,1)}, bf16[32,4,16,128]{3,2,1,0:T(8,128)(2,1)}, u32[]{:S(2)}, u32[]{:S(2)}) %collective-permute-start.7) | collective-permute-done | bytes 524320 | tf_op jit(solution)/shard_map/ppermute | solution.py:48
  31.1 2.2 %copy.38 = bf16[4,8,64,128]{3,1,2,0:T(8,128)(2,1)} copy(bf16[4,8,64,128]{3,2,1,0:T(8,128)(2,1)} %bitcast.44) | data formatting | bytes 1048576
  33.3 2.2 %copy.39 = bf16[4,8,64,128]{3,1,2,0:T(8,128)(2,1)} copy(bf16[4,8,64,128]{3,2,1,0:T(8,128)(2,1)} %bitcast.41) | data formatting | bytes 1048576
  35.5 3.4 %shard_map.77 = bf16[128,8192]{1,0:T(8,128)(2,1)} custom-call(bf16[128,256]{1,0:T(8,128)(2,1)} %concatenate.23.refs_0_, bf16[32,8192]{1,0:T(8,128)(2,1)} %bitcast.92, bf16[32,8192]{1,0:T(8,128)(2,1)} %bitcast.98, bf16[32,8192]{1,0:T(8,128)(2,1)} %bitcast.96, bf16[32,8192]{1,0:T(8,128)(2,1)} %bitcast.94), custom_call_target="tpu_custom_call" | custom-call | tf_op jit(solution)/shard_map/pallas_call | solution.py:112
  38.9 2.2 %copy.28 = bf16[16,8,64,128]{3,2,1,0:T(8,128)(2,1)S(1)} copy(bf16[16,8,64,128]{3,1,2,0:T(8,128)(2,1)} %bitcast.86) | data formatting | bytes 4194304
  41.1 1.4 dynamic-slice_bitcast_fusion.4
  42.5 1.4 collective-permute-start.10
  43.9 1.4 collective-permute-start.11
  45.5 1.1 copy.41
  46.7 6.8 %collective-permute-done.1 = bf16[32,4,16,128]{3,2,1,0:T(8,128)(2,1)S(1)} collective-permute-done((bf16[32,4,16,128]{3,2,1,0:T(8,128)(2,1)}, bf16[32,4,16,128]{3,2,1,0:T(8,128)(2,1)S(1)}, u32[]{:S(2)}, u32[]{:S(2)}) %collective-permute-start.1) | collective-permute-done | bytes 524320 | tf_op jit(solution)/shard_map/ppermute | solution.py:48
  53.5 1.2 copy.42
  54.6 1.1 copy.43
  56.4 3.6 %shard_map.76 = bf16[128,8192]{1,0:T(8,128)(2,1)} custom-call(bf16[128,256]{1,0:T(8,128)(2,1)} %concatenate.23.refs_0_, bf16[32,8192]{1,0:T(8,128)(2,1)} %bitcast.91, bf16[32,8192]{1,0:T(8,128)(2,1)} %bitcast.97, bf16[32,8192]{1,0:T(8,128)(2,1)} %bitcast.95, bf16[32,8192]{1,0:T(8,128)(2,1)} %bitcast.93, f32[1,8192]{1,0:T(1,128)} %bitcast.106), custom_call_target="tpu_custom_call" | custom-call | tf_op jit(solution)/shard_map/pallas_call | solution.py:112
  60.0 2.2 %copy.23 = bf16[16,8,64,128]{3,2,1,0:T(8,128)(2,1)S(1)} copy(bf16[16,8,64,128]{3,1,2,0:T(8,128)(2,1)} %bitcast.84) | data formatting | bytes 4194304
  62.7 1.4 collective-permute-start.4
  64.3 1.2 collective-permute-start.5
  65.6 9.3 %collective-permute-done.11 = bf16[32,4,16,128]{3,2,1,0:T(8,128)(2,1)} collective-permute-done((bf16[32,4,16,128]{3,2,1,0:T(8,128)(2,1)S(1)}, bf16[32,4,16,128]{3,2,1,0:T(8,128)(2,1)}, u32[]{:S(2)}, u32[]{:S(2)}) %collective-permute-start.11) | collective-permute-done | bytes 524320 | tf_op jit(solution)/shard_map/ppermute | solution.py:48
  74.8 1.5 pad_maximum_fusion.11
  76.7 0.8 pad_maximum_fusion.12
  77.6 1.3 collective-permute-start.12
  78.9 4.8 %collective-permute-start.13 = (bf16[32,1,64,128]{3,2,1,0:T(8,128)(2,1)S(1)}, bf16[32,1,64,128]{3,2,1,0:T(8,128)(2,1)S(1)}, u32[]{:S(2)}, u32[]{:S(2)}) collective-permute-start(bf16[32,1,64,128]{3,2,1,0:T(8,128)(2,1)S(1)} %get-tuple-element.8), channel_id=1, source_target_pairs={{0,4},{4,8},{8,12},{12,16},{16,20},{20,24},{24,28},{1,5},{5,9},{9,... | collective-permute-start | bytes 1572872 | tf_op jit(solution)/shard_map/ppermute | solution.py:22
  83.7 3.1 %collective-permute-done.3 = bf16[32,4,16,128]{3,2,1,0:T(8,128)(2,1)S(1)} collective-permute-done((bf16[32,4,16,128]{3,2,1,0:T(8,128)(2,1)S(1)}, bf16[32,4,16,128]{3,2,1,0:T(8,128)(2,1)S(1)}, u32[]{:S(2)}, u32[]{:S(2)}) %collective-permute-start.3) | collective-permute-done | bytes 524320 | tf_op jit(solution)/shard_map/ppermute | solution.py:48
  87.2 10.1 %collective-permute-done.5 = bf16[32,4,16,128]{3,2,1,0:T(8,128)(2,1)S(1)} collective-permute-done((bf16[32,4,16,128]{3,2,1,0:T(8,128)(2,1)S(1)}, bf16[32,4,16,128]{3,2,1,0:T(8,128)(2,1)S(1)}, u32[]{:S(2)}, u32[]{:S(2)}) %collective-permute-start.5) | collective-permute-done | bytes 524320 | tf_op jit(solution)/shard_map/ppermute | solution.py:48
  98.3 7.1 %collective-permute-done.13 = bf16[32,1,64,128]{3,2,1,0:T(8,128)(2,1)S(1)} collective-permute-done((bf16[32,1,64,128]{3,2,1,0:T(8,128)(2,1)S(1)}, bf16[32,1,64,128]{3,2,1,0:T(8,128)(2,1)S(1)}, u32[]{:S(2)}, u32[]{:S(2)}) %collective-permute-start.13) | collective-permute-done | bytes 524320 | tf_op jit(solution)/shard_map/ppermute | solution.py:22
  105.4 5.9 %fusion.6 = bf16[32,4,64,128]{3,2,1,0:T(8,128)(2,1)S(1)} fusion(f32[32,4,64,128]{3,2,1,0:T(8,128)S(1)} %get-tuple-element.10, bf16[32,1,64,128]{3,2,1,0:T(8,128)(2,1)S(1)} %collective-permute-done.13, bf16[32,4,16,128]{3,2,1,0:T(8,128)(2,1)S(1)} %get-tuple-element.12, bf16[32,4,16,128]{3,2,1,0:T(8,128)(2,1)S(1)} %get-tuple-element.13, ...), kind=kLoop, calls=%fused_computation.10 | loop fusion | flops 34603008 | bytes 9447424 | tf_op jit(solution)/shard_map/convert_element_type | solution.py:219
  112.1 0.9 fusion.23
  113.0 1.2 fusion.12
  115.0 2.5 %collective-permute-start.14 = (bf16[1,256,256]{2,1,0:T(8,128)(2,1)S(1)}, bf16[1,256,256]{2,1,0:T(8,128)(2,1)S(1)}, u32[]{:S(2)}, u32[]{:S(2)}) collective-permute-start(bf16[1,256,256]{2,1,0:T(8,128)(2,1)S(1)} %get-tuple-element.35), channel_id=1, source_target_pairs={{0,4},{4,8},{8,12},{12,16},{16,20},{20,24},{24,28},{28,0},{1,5},{5... | collective-permute-start | bytes 393224 | tf_op jit(solution)/shard_map/ppermute | solution.py:48
  117.5 1.6 %collective-permute-start.15 = (bf16[1,256,256]{2,1,0:T(8,128)(2,1)S(1)}, bf16[1,256,256]{2,1,0:T(8,128)(2,1)S(1)}, u32[]{:S(2)}, u32[]{:S(2)}) collective-permute-start(bf16[1,256,256]{2,1,0:T(8,128)(2,1)S(1)} %get-tuple-element.41), channel_id=1, source_target_pairs={{0,8},{4,12},{8,16},{12,20},{16,24},{20,28},{24,0},{28,4},{1,9},{5... | collective-permute-start | bytes 393224 | tf_op jit(solution)/shard_map/ppermute | solution.py:48
  119.1 1.4 collective-permute-start.16
  120.4 1.4 collective-permute-start.17
  121.9 2.0 %collective-permute-start.18 = (bf16[1,256,256]{2,1,0:T(8,128)(2,1)S(1)}, bf16[1,256,256]{2,1,0:T(8,128)(2,1)S(1)}, u32[]{:S(2)}, u32[]{:S(2)}) collective-permute-start(bf16[1,256,256]{2,1,0:T(8,128)(2,1)S(1)} %get-tuple-element.38), channel_id=1, source_target_pairs={{0,20},{4,24},{8,28},{12,0},{16,4},{20,8},{24,12},{28,16},{1,21},{... | collective-permute-start | bytes 393224 | tf_op jit(solution)/shard_map/ppermute | solution.py:48
  124.2 2.7 %collective-permute-start.19 = (bf16[1,256,256]{2,1,0:T(8,128)(2,1)S(1)}, bf16[1,256,256]{2,1,0:T(8,128)(2,1)S(1)}, u32[]{:S(2)}, u32[]{:S(2)}) collective-permute-start(bf16[1,256,256]{2,1,0:T(8,128)(2,1)S(1)} %get-tuple-element.37), channel_id=1, source_target_pairs={{0,24},{4,28},{8,0},{12,4},{16,8},{20,12},{24,16},{28,20},{1,25},{... | collective-permute-start | bytes 393224 | tf_op jit(solution)/shard_map/ppermute | solution.py:48
  126.9 1.0 collective-permute-start.20
  127.9 6.7 %collective-permute-done.16 = bf16[1,256,256]{2,1,0:T(8,128)(2,1)S(1)} collective-permute-done((bf16[1,256,256]{2,1,0:T(8,128)(2,1)S(1)}, bf16[1,256,256]{2,1,0:T(8,128)(2,1)S(1)}, u32[]{:S(2)}, u32[]{:S(2)}) %collective-permute-start.16) | collective-permute-done | bytes 131104 | tf_op jit(solution)/shard_map/ppermute | solution.py:48
  134.6 1.3 collective-permute-done.17
  136.3 18.4 %all_to_all.6 = f32[8,1,32]{2,1,0:T(1,128)S(1)} all-to-all(f32[8,1,32]{2,1,0:T(1,128)S(1)} %broadcast_in_dim.5), channel_id=1, replica_groups=mesh['gx'=8,'ka'=4] {'gx'}, dimensions={0} | all-to-all | bytes 2048 | tf_op jit(solution)/shard_map/all_to_all | solution.py:34
  155.4 0.8 slice_multiply_fusion
  (61 shorter events, 9.3 us)
Async XLA Ops:
  0.6 6.4 %copy-start = (bf16[32,4,64,128]{3,2,1,0:T(8,128)(2,1)S(1)}, bf16[32,4,64,128]{3,2,1,0:T(8,128)(2,1)}, u32[]{:S(2)}) copy-start(bf16[32,4,64,128]{3,2,1,0:T(8,128)(2,1)} %param.6) | copy-start | bytes 6291460
  3.8 10.5 %copy-start.2 = (f32[4,64]{1,0:T(4,128)S(1)}, f32[4,64]{1,0:T(4,128)}, u32[]{:S(2)}) copy-start(f32[4,64]{1,0:T(4,128)} %param.8) | copy-start | bytes 3076
  3.8 12.4 %copy-start.3 = (f32[4,64]{1,0:T(4,128)S(1)}, f32[4,64]{1,0:T(4,128)}, u32[]{:S(2)}) copy-start(f32[4,64]{1,0:T(4,128)} %param.7) | copy-start | bytes 3076
  3.8 14.9 %collective-permute-start.8 = (bf16[32,4,16,128]{3,2,1,0:T(8,128)(2,1)}, bf16[32,4,16,128]{3,2,1,0:T(8,128)(2,1)}, u32[]{:S(2)}, u32[]{:S(2)}) collective-permute-start(bf16[32,4,16,128]{3,2,1,0:T(8,128)(2,1)} %get-tuple-element.19), channel_id=1, source_target_pairs={{0,3},{1,0},{2,1},{3,2},{4,7},{5,4},{6,5},{7,6},{8,11},{9,8},{10,9... | collective-permute-start | bytes 1572872 | tf_op jit(solution)/shard_map/ppermute | solution.py:48
  6.2 24.9 %collective-permute-start.7 = (bf16[32,4,16,128]{3,2,1,0:T(8,128)(2,1)}, bf16[32,4,16,128]{3,2,1,0:T(8,128)(2,1)}, u32[]{:S(2)}, u32[]{:S(2)}) collective-permute-start(bf16[32,4,16,128]{3,2,1,0:T(8,128)(2,1)} %get-tuple-element.22), channel_id=1, source_target_pairs={{0,2},{1,3},{2,0},{3,1},{4,6},{5,7},{6,4},{7,5},{8,10},{9,11},{10,... | collective-permute-start | bytes 1572872 | tf_op jit(solution)/shard_map/ppermute | solution.py:48
  6.8 26.4 %collective-permute-start.6 = (bf16[32,4,16,128]{3,2,1,0:T(8,128)(2,1)}, bf16[32,4,16,128]{3,2,1,0:T(8,128)(2,1)}, u32[]{:S(2)}, u32[]{:S(2)}) collective-permute-start(bf16[32,4,16,128]{3,2,1,0:T(8,128)(2,1)} %get-tuple-element.20), channel_id=1, source_target_pairs={{0,1},{1,2},{2,3},{3,0},{4,5},{5,6},{6,7},{7,4},{8,9},{9,10},{10,1... | collective-permute-start | bytes 1572872 | tf_op jit(solution)/shard_map/ppermute | solution.py:48
  8.5 35.5 %collective-permute-start.2 = (bf16[32,4,16,128]{3,2,1,0:T(8,128)(2,1)}, bf16[32,4,16,128]{3,2,1,0:T(8,128)(2,1)S(1)}, u32[]{:S(2)}, u32[]{:S(2)}) collective-permute-start(bf16[32,4,16,128]{3,2,1,0:T(8,128)(2,1)} %get-tuple-element.31), channel_id=1, source_target_pairs={{0,3},{1,0},{2,1},{3,2},{4,7},{5,4},{6,5},{7,6},{8,11},{9,8},{10,9... | collective-permute-start | bytes 1572872 | tf_op jit(solution)/shard_map/ppermute | solution.py:48
  10.1 43.4 %collective-permute-start.1 = (bf16[32,4,16,128]{3,2,1,0:T(8,128)(2,1)}, bf16[32,4,16,128]{3,2,1,0:T(8,128)(2,1)S(1)}, u32[]{:S(2)}, u32[]{:S(2)}) collective-permute-start(bf16[32,4,16,128]{3,2,1,0:T(8,128)(2,1)} %get-tuple-element.34), channel_id=1, source_target_pairs={{0,2},{1,3},{2,0},{3,1},{4,6},{5,7},{6,4},{7,5},{8,10},{9,11},{10,... | collective-permute-start | bytes 1572872 | tf_op jit(solution)/shard_map/ppermute | solution.py:48
  18.7 35.9 %collective-permute-start = (bf16[32,4,16,128]{3,2,1,0:T(8,128)(2,1)}, bf16[32,4,16,128]{3,2,1,0:T(8,128)(2,1)S(1)}, u32[]{:S(2)}, u32[]{:S(2)}) collective-permute-start(bf16[32,4,16,128]{3,2,1,0:T(8,128)(2,1)} %get-tuple-element.32), channel_id=1, source_target_pairs={{0,1},{1,2},{2,3},{3,0},{4,5},{5,6},{6,7},{7,4},{8,9},{9,10},{10,1... | collective-permute-start | bytes 1572872 | tf_op jit(solution)/shard_map/ppermute | solution.py:48
  42.5 21.8 %collective-permute-start.9 = (bf16[32,4,16,128]{3,2,1,0:T(8,128)(2,1)}, bf16[32,4,16,128]{3,2,1,0:T(8,128)(2,1)S(1)}, u32[]{:S(2)}, u32[]{:S(2)}) collective-permute-start(bf16[32,4,16,128]{3,2,1,0:T(8,128)(2,1)} %get-tuple-element.18), channel_id=1, source_target_pairs={{0,1},{1,2},{2,3},{3,0},{4,5},{5,6},{6,7},{7,4},{8,9},{9,10},{10,1... | collective-permute-start | bytes 1572872 | tf_op jit(solution)/shard_map/ppermute | solution.py:48
  42.5 23.0 %collective-permute-start.10 = (bf16[32,4,16,128]{3,2,1,0:T(8,128)(2,1)}, bf16[32,4,16,128]{3,2,1,0:T(8,128)(2,1)}, u32[]{:S(2)}, u32[]{:S(2)}) collective-permute-start(bf16[32,4,16,128]{3,2,1,0:T(8,128)(2,1)} %get-tuple-element.17), channel_id=1, source_target_pairs={{0,2},{1,3},{2,0},{3,1},{4,6},{5,7},{6,4},{7,5},{8,10},{9,11},{10,... | collective-permute-start | bytes 1572872 | tf_op jit(solution)/shard_map/ppermute | solution.py:48
  43.9 30.9 %collective-permute-start.11 = (bf16[32,4,16,128]{3,2,1,0:T(8,128)(2,1)S(1)}, bf16[32,4,16,128]{3,2,1,0:T(8,128)(2,1)}, u32[]{:S(2)}, u32[]{:S(2)}) collective-permute-start(bf16[32,4,16,128]{3,2,1,0:T(8,128)(2,1)S(1)} %get-tuple-element.16), channel_id=1, source_target_pairs={{0,3},{1,0},{2,1},{3,2},{4,7},{5,4},{6,5},{7,6},{8,11},{9,8},{10,9... | collective-permute-start | bytes 1572872 | tf_op jit(solution)/shard_map/ppermute | solution.py:48
  62.7 24.1 %collective-permute-start.3 = (bf16[32,4,16,128]{3,2,1,0:T(8,128)(2,1)S(1)}, bf16[32,4,16,128]{3,2,1,0:T(8,128)(2,1)S(1)}, u32[]{:S(2)}, u32[]{:S(2)}) collective-permute-start(bf16[32,4,16,128]{3,2,1,0:T(8,128)(2,1)S(1)} %get-tuple-element.30), channel_id=1, source_target_pairs={{0,1},{1,2},{2,3},{3,0},{4,5},{5,6},{6,7},{7,4},{8,9},{9,10},{10,1... | collective-permute-start | bytes 1572872 | tf_op jit(solution)/shard_map/ppermute | solution.py:48
  62.7 24.4 %collective-permute-start.4 = (bf16[32,4,16,128]{3,2,1,0:T(8,128)(2,1)S(1)}, bf16[32,4,16,128]{3,2,1,0:T(8,128)(2,1)S(1)}, u32[]{:S(2)}, u32[]{:S(2)}) collective-permute-start(bf16[32,4,16,128]{3,2,1,0:T(8,128)(2,1)S(1)} %get-tuple-element.29), channel_id=1, source_target_pairs={{0,2},{1,3},{2,0},{3,1},{4,6},{5,7},{6,4},{7,5},{8,10},{9,11},{10,... | collective-permute-start | bytes 1572872 | tf_op jit(solution)/shard_map/ppermute | solution.py:48
  64.3 32.9 %collective-permute-start.5 = (bf16[32,4,16,128]{3,2,1,0:T(8,128)(2,1)S(1)}, bf16[32,4,16,128]{3,2,1,0:T(8,128)(2,1)S(1)}, u32[]{:S(2)}, u32[]{:S(2)}) collective-permute-start(bf16[32,4,16,128]{3,2,1,0:T(8,128)(2,1)S(1)} %get-tuple-element.28), channel_id=1, source_target_pairs={{0,3},{1,0},{2,1},{3,2},{4,7},{5,4},{6,5},{7,6},{8,11},{9,8},{10,9... | collective-permute-start | bytes 1572872 | tf_op jit(solution)/shard_map/ppermute | solution.py:48
  77.6 20.7 %collective-permute-start.12 = (bf16[32,1,64,128]{3,2,1,0:T(8,128)(2,1)S(1)}, bf16[32,1,64,128]{3,2,1,0:T(8,128)(2,1)S(1)}, u32[]{:S(2)}, u32[]{:S(2)}) collective-permute-start(bf16[32,1,64,128]{3,2,1,0:T(8,128)(2,1)S(1)} %get-tuple-element.7), channel_id=1, source_target_pairs={{4,0},{8,4},{12,8},{16,12},{20,16},{24,20},{28,24},{5,1},{9,5},{13... | collective-permute-start | bytes 1572872 | tf_op jit(solution)/shard_map/ppermute | solution.py:24
  78.9 26.5 %collective-permute-start.13 = (bf16[32,1,64,128]{3,2,1,0:T(8,128)(2,1)S(1)}, bf16[32,1,64,128]{3,2,1,0:T(8,128)(2,1)S(1)}, u32[]{:S(2)}, u32[]{:S(2)}) collective-permute-start(bf16[32,1,64,128]{3,2,1,0:T(8,128)(2,1)S(1)} %get-tuple-element.8), channel_id=1, source_target_pairs={{0,4},{4,8},{8,12},{12,16},{16,20},{20,24},{24,28},{1,5},{5,9},{9,... | collective-permute-start | bytes 1572872 | tf_op jit(solution)/shard_map/ppermute | solution.py:22
  97.5 7.9 %copy-start.1 = (f32[4,64]{1,0:T(4,128)S(1)}, f32[4,64]{1,0:T(4,128)}, u32[]{:S(2)}) copy-start(f32[4,64]{1,0:T(4,128)} %param.9) | copy-start | bytes 3076
  115.0 9.2 %collective-permute-start.14 = (bf16[1,256,256]{2,1,0:T(8,128)(2,1)S(1)}, bf16[1,256,256]{2,1,0:T(8,128)(2,1)S(1)}, u32[]{:S(2)}, u32[]{:S(2)}) collective-permute-start(bf16[1,256,256]{2,1,0:T(8,128)(2,1)S(1)} %get-tuple-element.35), channel_id=1, source_target_pairs={{0,4},{4,8},{8,12},{12,16},{16,20},{20,24},{24,28},{28,0},{1,5},{5... | collective-permute-start | bytes 393224 | tf_op jit(solution)/shard_map/ppermute | solution.py:48
  117.5 9.3 %collective-permute-start.15 = (bf16[1,256,256]{2,1,0:T(8,128)(2,1)S(1)}, bf16[1,256,256]{2,1,0:T(8,128)(2,1)S(1)}, u32[]{:S(2)}, u32[]{:S(2)}) collective-permute-start(bf16[1,256,256]{2,1,0:T(8,128)(2,1)S(1)} %get-tuple-element.41), channel_id=1, source_target_pairs={{0,8},{4,12},{8,16},{12,20},{16,24},{20,28},{24,0},{28,4},{1,9},{5... | collective-permute-start | bytes 393224 | tf_op jit(solution)/shard_map/ppermute | solution.py:48
  119.1 15.5 %collective-permute-start.16 = (bf16[1,256,256]{2,1,0:T(8,128)(2,1)S(1)}, bf16[1,256,256]{2,1,0:T(8,128)(2,1)S(1)}, u32[]{:S(2)}, u32[]{:S(2)}) collective-permute-start(bf16[1,256,256]{2,1,0:T(8,128)(2,1)S(1)} %get-tuple-element.40), channel_id=1, source_target_pairs={{0,12},{4,16},{8,20},{12,24},{16,28},{20,0},{24,4},{28,8},{1,13},{... | collective-permute-start | bytes 393224 | tf_op jit(solution)/shard_map/ppermute | solution.py:48
  120.4 15.4 %collective-permute-start.17 = (bf16[1,256,256]{2,1,0:T(8,128)(2,1)S(1)}, bf16[1,256,256]{2,1,0:T(8,128)(2,1)S(1)}, u32[]{:S(2)}, u32[]{:S(2)}) collective-permute-start(bf16[1,256,256]{2,1,0:T(8,128)(2,1)S(1)} %get-tuple-element.39), channel_id=1, source_target_pairs={{0,16},{4,20},{8,24},{12,28},{16,0},{20,4},{24,8},{28,12},{1,17},{... | collective-permute-start | bytes 393224 | tf_op jit(solution)/shard_map/ppermute | solution.py:48
  121.9 14.0 %collective-permute-start.18 = (bf16[1,256,256]{2,1,0:T(8,128)(2,1)S(1)}, bf16[1,256,256]{2,1,0:T(8,128)(2,1)S(1)}, u32[]{:S(2)}, u32[]{:S(2)}) collective-permute-start(bf16[1,256,256]{2,1,0:T(8,128)(2,1)S(1)} %get-tuple-element.38), channel_id=1, source_target_pairs={{0,20},{4,24},{8,28},{12,0},{16,4},{20,8},{24,12},{28,16},{1,21},{... | collective-permute-start | bytes 393224 | tf_op jit(solution)/shard_map/ppermute | solution.py:48
  124.2 11.7 %collective-permute-start.19 = (bf16[1,256,256]{2,1,0:T(8,128)(2,1)S(1)}, bf16[1,256,256]{2,1,0:T(8,128)(2,1)S(1)}, u32[]{:S(2)}, u32[]{:S(2)}) collective-permute-start(bf16[1,256,256]{2,1,0:T(8,128)(2,1)S(1)} %get-tuple-element.37), channel_id=1, source_target_pairs={{0,24},{4,28},{8,0},{12,4},{16,8},{20,12},{24,16},{28,20},{1,25},{... | collective-permute-start | bytes 393224 | tf_op jit(solution)/shard_map/ppermute | solution.py:48
  126.9 9.1 %collective-permute-start.20 = (bf16[1,256,256]{2,1,0:T(8,128)(2,1)S(1)}, bf16[1,256,256]{2,1,0:T(8,128)(2,1)S(1)}, u32[]{:S(2)}, u32[]{:S(2)}) collective-permute-start(bf16[1,256,256]{2,1,0:T(8,128)(2,1)S(1)} %get-tuple-element.36), channel_id=1, source_target_pairs={{0,28},{4,0},{8,4},{12,8},{16,12},{20,16},{24,20},{28,24},{1,29},{... | collective-permute-start | bytes 393224 | tf_op jit(solution)/shard_map/ppermute | solution.py:48

commit v18 on v16

--- a/solution.py
+++ b/solution.py
@@ -187,9 +187,11 @@
         modes = dft(table, pieces, weight)
         return modes.reshape(total_angles, axial_cells, band, columns)
 
-    direct_modes = in_source_order(exchange(transform_all(direct_snapshots), "ka", 0), "ka", 2)
-    weighted = in_source_order(
-        exchange(transform_all(adjoint_snapshots, lane_weight), "ka", 0), "ka", 2
+    direct_modes = lax.all_to_all(
+        transform_all(direct_snapshots), "ka", split_axis=0, concat_axis=2, tiled=True
+    )
+    weighted = lax.all_to_all(
+        transform_all(adjoint_snapshots, lane_weight), "ka", split_axis=0, concat_axis=2, tiled=True
     )
     padded = padded_2(direct_modes, (("gx", 1),), 1)
     field_f32 = direct_modes.astype(jnp.float32)

time: 156 us -> 188 us (1.21)
  waiting for transfers between devices: 62.1 us -> 91.2 us
  local copies, waits for them, and re-layouts: 26.1 us -> 33 us
  other arithmetic: 14.3 us -> 9.93 us
    ppermute x19 -> x13, waiting for transfers between devices: 55 us -> 72.4 us  [exchange(): lax.ppermute(piece, axis, [(j, (j + shift) % count) for j in range(count)])]
    all_to_all x0 -> x2, waiting for transfers between devices: none -> 16.2 us  [the longest x1 16.2 us: local(): lax.all_to_all(transform_all(adjoint_snapshots, lane_weight), 'ka', split...]
    all_to_all x0 -> x2, starting transfers between devices: none -> 8.06 us  [the longest x1 4.45 us: local(): lax.all_to_all(transform_all(adjoint_snapshots, lane_weight), 'ka', split...]
    ppermute x19 -> x13, starting transfers between devices: 26.1 us -> 19.8 us  [exchange(): lax.ppermute(piece, axis, [(j, (j + shift) % count) for j in range(count)])]
    ppermute x1, waiting for transfers between devices: 7.14 us -> 2.57 us  [padded_2(): lax.ppermute(tail, axis, [(i, (i + 1) % count) for i in range(ends)])]
    all_to_all x0 -> x2, local copies, waits for them, and re-layouts: none -> 4.31 us  [the longest x1 2.15 us: local(): lax.all_to_all(transform_all(adjoint_snapshots, lane_weight), 'ka', split...]
    unnamed x18, local copies, waits for them, and re-layouts: 16.7 us -> 19.6 us
  transfers between devices with their start and end apart: 21 -> 17, of which waited for: 13 -> 9; matrix products, arithmetic and copies ran while one was open for 17% -> 14% of each run, Pallas kernels for 5% -> 2%
where the time goes in v18:
time: 188 us; the launch traced here: 187 us
  waiting for transfers between devices  91.2 us (49%)
  starting transfers between devices  33.9 us (18%)
  local copies, waits for them, and re-layouts  33 us (18%)
  blocking collectives  9.94 us (5%)
  other arithmetic  9.93 us (5%)
  Pallas kernels  7.06 us (4%)
    ppermute x13, waiting for transfers between devices, exchange(): lax.ppermute(piece, axis, [(j, (j + shift) % count) for j in range(count)])  72.4 us
    ppermute x13, starting transfers between devices, exchange(): lax.ppermute(piece, axis, [(j, (j + shift) % count) for j in range(count)])  19.8 us
    unnamed x18, local copies, waits for them, and re-layouts  19.6 us
    all_to_all x1, waiting for transfers between devices, local(): lax.all_to_all(transform_all(adjoint_snapshots, lane_weight), 'ka', split...  16.2 us
    all_to_all x1, blocking collectives, gather_small(): return lax.all_to_all(copies, axis, split_axis=0, concat_axis=0, tiled=True)  9.94 us
    pallas_call x2, Pallas kernels, dft(): pl.pallas_call(functools.partial(dft_kernel, count=count, weighted=weight...  7.06 us
    dynamic_slice x3, local copies, waits for them, and re-layouts, exchange(): lax.dynamic_slice_in_dim(cells, (here + shift) % count * width, width, ax...  6.05 us
    ppermute x1, starting transfers between devices, padded_2(): lax.ppermute(tail, axis, [(i, (i + 1) % count) for i in range(ends)])  4.76 us
  transfers between devices with their start and end apart: 17, of which 9 were waited for; matrix products, arithmetic and copies ran while one was open for 14% of the time, Pallas kernels for 2%

profile of v18, /device:TPU:0, one launch (start us, length us, event | category | flops | bytes accessed | tf_op | source)
XLA Modules:
  0.0 187.1 jit_solution(8528140863105292398)
XLA Ops:
  0.7 3.0 %constant_dynamic-slice_fusion.7 = (bf16[32,4,16,128]{3,2,1,0:T(8,128)(2,1)}, bf16[32,4,16,128]{3,2,1,0:T(8,128)(2,1)S(1)}, bf16[32,4,16,128]{3,2,1,0:T(8,128)(2,1)S(1)}, bf16[32,4,16,128]{3,2,1,0:T(8,128)(2,1)S(1)}) fusion(bf16[32,4,64,128]{3,2,1,0:T(8,128)(2,1)} %param.5, s32[]{:T(128)S(6)} %select_n.157, s32[]{:T(128)S(6)} %select_n.153, ...), kind=kLoop, calls=%fused_computation.87 | loop fusion | bytes 4194320 | tf_op jit(solution)/shard_map/dynamic_slice | solution.py:46
  3.7 2.4 %collective-permute-start.5 = (bf16[32,4,16,128]{3,2,1,0:T(8,128)(2,1)}, bf16[32,4,16,128]{3,2,1,0:T(8,128)(2,1)S(1)}, u32[]{:S(2)}, u32[]{:S(2)}) collective-permute-start(bf16[32,4,16,128]{3,2,1,0:T(8,128)(2,1)} %get-tuple-element.9), channel_id=1, source_target_pairs={{0,3},{1,0},{2,1},{3,2},{4,7},{5,4},{6,5},{7,6},{8,11},{9,8},{10,9... | collective-permute-start | bytes 1572872 | tf_op jit(solution)/shard_map/ppermute | solution.py:48
  6.1 0.6 collective-permute-start.4
  7.8 1.1 copy.52
  9.6 0.8 concatenate.22.refs_0_
  10.4 8.4 %collective-permute-done.5 = bf16[32,4,16,128]{3,2,1,0:T(8,128)(2,1)S(1)} collective-permute-done((bf16[32,4,16,128]{3,2,1,0:T(8,128)(2,1)}, bf16[32,4,16,128]{3,2,1,0:T(8,128)(2,1)S(1)}, u32[]{:S(2)}, u32[]{:S(2)}) %collective-permute-start.5) | collective-permute-done | bytes 524320 | tf_op jit(solution)/shard_map/ppermute | solution.py:48
  18.8 1.1 copy.49
  19.9 10.6 %collective-permute-done.4 = bf16[32,4,16,128]{3,2,1,0:T(8,128)(2,1)S(1)} collective-permute-done((bf16[32,4,16,128]{3,2,1,0:T(8,128)(2,1)S(1)}, bf16[32,4,16,128]{3,2,1,0:T(8,128)(2,1)S(1)}, u32[]{:S(2)}, u32[]{:S(2)}) %collective-permute-start.4) | collective-permute-done | bytes 524320 | tf_op jit(solution)/shard_map/ppermute | solution.py:48
  30.5 1.1 copy.50
  31.7 1.1 copy.51
  32.8 3.4 %shard_map.77 = bf16[128,8192]{1,0:T(8,128)(2,1)} custom-call(bf16[128,256]{1,0:T(8,128)(2,1)} %concatenate.22.refs_0_, bf16[32,8192]{1,0:T(8,128)(2,1)} %bitcast.77, bf16[32,8192]{1,0:T(8,128)(2,1)} %bitcast.85, bf16[32,8192]{1,0:T(8,128)(2,1)} %bitcast.83, bf16[32,8192]{1,0:T(8,128)(2,1)} %bitcast.81), custom_call_target="tpu_custom_call" | custom-call | tf_op jit(solution)/shard_map/pallas_call | solution.py:112
  36.3 3.5 %copy.40 = bf16[16,8,64,128]{3,2,1,0:T(8,128)(2,1)} copy(bf16[16,8,64,128]{3,1,2,0:T(8,128)(2,1)} %bitcast.73) | data formatting | bytes 4194304
  39.8 3.6 %all-to-all-start.1 = ((bf16[128,4,16,128]{3,2,1,0:T(8,128)(2,1)}), bf16[128,4,16,128]{3,2,1,0:T(8,128)(2,1)S(1)}, u32[]{:S(2)}, u32[]{:S(2)}) async-start(bf16[128,4,16,128]{3,2,1,0:T(8,128)(2,1)} %bitcast.70), calls=%async_computation.1 | async-start | bytes 4194304 | tf_op jit(solution)/shard_map/all_to_all | solution.py:190
  43.4 2.9 %constant_dynamic-slice_fusion.12 = (bf16[32,4,16,128]{3,2,1,0:T(8,128)(2,1)}, bf16[32,4,16,128]{3,2,1,0:T(8,128)(2,1)}, bf16[32,4,16,128]{3,2,1,0:T(8,128)(2,1)S(1)}, bf16[32,4,16,128]{3,2,1,0:T(8,128)(2,1)}) fusion(bf16[32,4,64,128]{3,2,1,0:T(8,128)(2,1)} %param.6, s32[]{:T(128)S(6)} %select_n.157, s32[]{:T(128)S(6)} %select_n.153, s32[]{:T(128)S(6)} %select_n.151, ...), kind=kLoop, calls=%fused_computation.92 | loop fusion | bytes 4194320 | tf_op jit(solution)/shard_map/dynamic_slice | solution.py:46
  46.4 1.7 collective-permute-start.2
  48.6 1.1 copy.56
  49.8 28.7 %collective-permute-done.2 = bf16[32,4,16,128]{3,2,1,0:T(8,128)(2,1)} collective-permute-done((bf16[32,4,16,128]{3,2,1,0:T(8,128)(2,1)}, bf16[32,4,16,128]{3,2,1,0:T(8,128)(2,1)}, u32[]{:S(2)}, u32[]{:S(2)}) %collective-permute-start.2) | collective-permute-done | bytes 524320 | tf_op jit(solution)/shard_map/ppermute | solution.py:48
  78.5 2.2 %copy.53 = bf16[4,8,64,128]{3,1,2,0:T(8,128)(2,1)} copy(bf16[4,8,64,128]{3,2,1,0:T(8,128)(2,1)} %bitcast.25) | data formatting | bytes 1048576
  80.7 11.0 %collective-permute-done.1 = bf16[32,4,16,128]{3,2,1,0:T(8,128)(2,1)} collective-permute-done((bf16[32,4,16,128]{3,2,1,0:T(8,128)(2,1)}, bf16[32,4,16,128]{3,2,1,0:T(8,128)(2,1)}, u32[]{:S(2)}, u32[]{:S(2)}) %collective-permute-start.1) | collective-permute-done | bytes 524320 | tf_op jit(solution)/shard_map/ppermute | solution.py:48
  91.7 2.2 %copy.54 = bf16[4,8,64,128]{3,1,2,0:T(8,128)(2,1)} copy(bf16[4,8,64,128]{3,2,1,0:T(8,128)(2,1)} %bitcast.22) | data formatting | bytes 1048576
  93.8 1.1 copy.55
  95.0 0.7 broadcast_in_dim.4
  95.7 3.6 %shard_map.76 = bf16[128,8192]{1,0:T(8,128)(2,1)} custom-call(bf16[128,256]{1,0:T(8,128)(2,1)} %concatenate.22.refs_0_, bf16[32,8192]{1,0:T(8,128)(2,1)} %bitcast.78, bf16[32,8192]{1,0:T(8,128)(2,1)} %bitcast.84, bf16[32,8192]{1,0:T(8,128)(2,1)} %bitcast.82, bf16[32,8192]{1,0:T(8,128)(2,1)} %bitcast.80, f32[1,8192]{1,0:T(1,128)} %bitcast.90), custom_call_target="tpu_custom_call" | custom-call | tf_op jit(solution)/shard_map/pallas_call | solution.py:112
  99.3 3.5 %copy.35 = bf16[16,8,64,128]{3,2,1,0:T(8,128)(2,1)} copy(bf16[16,8,64,128]{3,1,2,0:T(8,128)(2,1)} %bitcast.72) | data formatting | bytes 4194304
  102.8 1.3 copy-done
  104.1 4.5 %all-to-all-start = ((bf16[128,4,16,128]{3,2,1,0:T(8,128)(2,1)}), bf16[128,4,16,128]{3,2,1,0:T(8,128)(2,1)}, u32[]{:S(2)}, u32[]{:S(2)}) async-start(bf16[128,4,16,128]{3,2,1,0:T(8,128)(2,1)} %bitcast.69), calls=%async_computation | async-start | bytes 4194304 | tf_op jit(solution)/shard_map/all_to_all | solution.py:193
  108.8 2.2 %copy.27 = bf16[4,32,4,16,128]{4,3,0,2,1:T(8,128)(2,1)S(1)} copy(bf16[4,32,4,16,128]{4,3,2,1,0:T(8,128)(2,1)} %bitcast.68) | data formatting | bytes 4194304 | tf_op jit(solution)/shard_map/all_to_all | solution.py:190
  110.9 1.1 fusion.26
  112.0 1.3 collective-permute-start.6
  113.3 4.8 %collective-permute-start.7 = (bf16[32,1,64,128]{3,2,1,0:T(8,128)(2,1)}, bf16[32,1,64,128]{3,2,1,0:T(8,128)(2,1)S(1)}, u32[]{:S(2)}, u32[]{:S(2)}) collective-permute-start(bf16[32,1,64,128]{3,2,1,0:T(8,128)(2,1)} %get-tuple-element.8), channel_id=1, source_target_pairs={{0,4},{4,8},{8,12},{12,16},{16,20},{20,24},{24,28},{1,5},{5,9},{9,... | collective-permute-start | bytes 1572872 | tf_op jit(solution)/shard_map/ppermute | solution.py:22
  118.1 16.2 %all-to-all-done = bf16[128,4,16,128]{3,2,1,0:T(8,128)(2,1)} async-done(((bf16[128,4,16,128]{3,2,1,0:T(8,128)(2,1)}), bf16[128,4,16,128]{3,2,1,0:T(8,128)(2,1)}, u32[]{:S(2)}, u32[]{:S(2)}) %all-to-all-start) | async-done | bytes 2097184 | tf_op jit(solution)/shard_map/all_to_all | solution.py:193
  134.3 2.2 %copy.26 = bf16[32,4,4,16,128]{4,3,2,1,0:T(8,128)(2,1)S(1)} copy(bf16[32,4,4,16,128]{4,3,1,0,2:T(8,128)(2,1)} %bitcast.2) | data formatting | bytes 4194304 | tf_op jit(solution)/shard_map/all_to_all | solution.py:193
  136.5 0.6 bitcast_convert_fusion
  137.1 2.6 %collective-permute-done.7 = bf16[32,1,64,128]{3,2,1,0:T(8,128)(2,1)S(1)} collective-permute-done((bf16[32,1,64,128]{3,2,1,0:T(8,128)(2,1)}, bf16[32,1,64,128]{3,2,1,0:T(8,128)(2,1)S(1)}, u32[]{:S(2)}, u32[]{:S(2)}) %collective-permute-start.7) | collective-permute-done | bytes 524320 | tf_op jit(solution)/shard_map/ppermute | solution.py:22
  139.7 4.4 %fusion.6 = bf16[32,4,64,128]{3,2,1,0:T(8,128)(2,1)S(1)} fusion(f32[32,4,64,128]{3,2,1,0:T(8,128)S(1)} %bitcast_convert_fusion, bf16[32,4,64,128]{3,2,1,0:T(8,128)(2,1)S(1)} %bitcast.65, bf16[32,1,64,128]{3,2,1,0:T(8,128)(2,1)S(1)} %collective-permute-done.7, bf16[32,1,64,128]{3,2,1,0:T(8,128)(2,1)S(1)} %collective-permute-done.6, ...), kind=kLoop, calls=%fused_computation.10 | loop fusion | flops 17825792 | bytes 9447424 | tf_op jit(solution)/shard_map/convert_element_type | solution.py:221
  144.1 1.1 fusion.9
  145.2 1.2 fusion.16
  146.4 0.7 pad_maximum_fusion.2
  147.2 4.5 %collective-permute-start.10 = (bf16[1,256,256]{2,1,0:T(8,128)(2,1)S(1)}, bf16[1,256,256]{2,1,0:T(8,128)(2,1)S(1)}, u32[]{:S(2)}, u32[]{:S(2)}) collective-permute-start(bf16[1,256,256]{2,1,0:T(8,128)(2,1)S(1)} %get-tuple-element.22), channel_id=1, source_target_pairs={{0,20},{4,24},{8,28},{12,0},{16,4},{20,8},{24,12},{28,16},{1,21},{... | collective-permute-start | bytes 393224 | tf_op jit(solution)/shard_map/ppermute | solution.py:48
  151.7 3.8 %collective-permute-start.12 = (bf16[1,256,256]{2,1,0:T(8,128)(2,1)S(1)}, bf16[1,256,256]{2,1,0:T(8,128)(2,1)S(1)}, u32[]{:S(2)}, u32[]{:S(2)}) collective-permute-start(bf16[1,256,256]{2,1,0:T(8,128)(2,1)S(1)} %get-tuple-element.20), channel_id=1, source_target_pairs={{0,24},{4,28},{8,0},{12,4},{16,8},{20,12},{24,16},{28,20},{1,25},{... | collective-permute-start | bytes 393224 | tf_op jit(solution)/shard_map/ppermute | solution.py:48
  155.5 0.6 collective-permute-start.13
  156.2 4.1 %collective-permute-start.14 = (bf16[1,256,256]{2,1,0:T(8,128)(2,1)S(1)}, bf16[1,256,256]{2,1,0:T(8,128)(2,1)S(1)}, u32[]{:S(2)}, u32[]{:S(2)}) collective-permute-start(bf16[1,256,256]{2,1,0:T(8,128)(2,1)S(1)} %get-tuple-element.18), channel_id=1, source_target_pairs={{0,28},{4,0},{8,4},{12,8},{16,12},{20,16},{24,20},{28,24},{1,29},{... | collective-permute-start | bytes 393224 | tf_op jit(solution)/shard_map/ppermute | solution.py:48
  160.2 1.3 collective-permute-start.8
  161.6 3.8 %collective-permute-done.13 = bf16[1,256,256]{2,1,0:T(8,128)(2,1)S(1)} collective-permute-done((bf16[1,256,256]{2,1,0:T(8,128)(2,1)S(1)}, bf16[1,256,256]{2,1,0:T(8,128)(2,1)S(1)}, u32[]{:S(2)}, u32[]{:S(2)}) %collective-permute-start.13) | collective-permute-done | bytes 131104 | tf_op jit(solution)/shard_map/ppermute | solution.py:48
  165.4 9.8 %collective-permute-done.8 = bf16[1,256,256]{2,1,0:T(8,128)(2,1)S(1)} collective-permute-done((bf16[1,256,256]{2,1,0:T(8,128)(2,1)S(1)}, bf16[1,256,256]{2,1,0:T(8,128)(2,1)S(1)}, u32[]{:S(2)}, u32[]{:S(2)}) %collective-permute-start.8) | collective-permute-done | bytes 131104 | tf_op jit(solution)/shard_map/ppermute | solution.py:48
  175.7 9.9 %all_to_all.39 = f32[8,1,32]{2,1,0:T(1,128)S(1)} all-to-all(f32[8,1,32]{2,1,0:T(1,128)S(1)} %broadcast_in_dim.5), channel_id=1, replica_groups=mesh['gx'=8,'ka'=4] {'gx'}, dimensions={0} | all-to-all | bytes 2048 | tf_op jit(solution)/shard_map/all_to_all | solution.py:34
  185.7 0.5 multiply_sqrt_fusion
  186.3 0.8 slice_multiply_fusion
  (47 shorter events, 3.2 us)
Async XLA Ops:
  3.7 15.0 %collective-permute-start.5 = (bf16[32,4,16,128]{3,2,1,0:T(8,128)(2,1)}, bf16[32,4,16,128]{3,2,1,0:T(8,128)(2,1)S(1)}, u32[]{:S(2)}, u32[]{:S(2)}) collective-permute-start(bf16[32,4,16,128]{3,2,1,0:T(8,128)(2,1)} %get-tuple-element.9), channel_id=1, source_target_pairs={{0,3},{1,0},{2,1},{3,2},{4,7},{5,4},{6,5},{7,6},{8,11},{9,8},{10,9... | collective-permute-start | bytes 1572872 | tf_op jit(solution)/shard_map/ppermute | solution.py:48
  6.1 24.4 %collective-permute-start.4 = (bf16[32,4,16,128]{3,2,1,0:T(8,128)(2,1)S(1)}, bf16[32,4,16,128]{3,2,1,0:T(8,128)(2,1)S(1)}, u32[]{:S(2)}, u32[]{:S(2)}) collective-permute-start(bf16[32,4,16,128]{3,2,1,0:T(8,128)(2,1)S(1)} %get-tuple-element.12), channel_id=1, source_target_pairs={{0,2},{1,3},{2,0},{3,1},{4,6},{5,7},{6,4},{7,5},{8,10},{9,11},{10,... | collective-permute-start | bytes 1572872 | tf_op jit(solution)/shard_map/ppermute | solution.py:48
  6.7 25.0 %collective-permute-start.3 = (bf16[32,4,16,128]{3,2,1,0:T(8,128)(2,1)S(1)}, bf16[32,4,16,128]{3,2,1,0:T(8,128)(2,1)S(1)}, u32[]{:S(2)}, u32[]{:S(2)}) collective-permute-start(bf16[32,4,16,128]{3,2,1,0:T(8,128)(2,1)S(1)} %get-tuple-element.10), channel_id=1, source_target_pairs={{0,1},{1,2},{2,3},{3,0},{4,5},{5,6},{6,7},{7,4},{8,9},{9,10},{10,1... | collective-permute-start | bytes 1572872 | tf_op jit(solution)/shard_map/ppermute | solution.py:48
  39.8 63.0 %all-to-all-start.1 = ((bf16[128,4,16,128]{3,2,1,0:T(8,128)(2,1)}), bf16[128,4,16,128]{3,2,1,0:T(8,128)(2,1)S(1)}, u32[]{:S(2)}, u32[]{:S(2)}) async-start(bf16[128,4,16,128]{3,2,1,0:T(8,128)(2,1)} %bitcast.70), calls=%async_computation.1 | async-start | bytes 4194304 | tf_op jit(solution)/shard_map/all_to_all | solution.py:190
  43.4 6.3 %copy-start.2 = (f32[4,64]{1,0:T(4,128)S(1)}, f32[4,64]{1,0:T(4,128)}, u32[]{:S(2)}) copy-start(f32[4,64]{1,0:T(4,128)} %param.7) | copy-start | bytes 3076
  46.4 32.1 %collective-permute-start.2 = (bf16[32,4,16,128]{3,2,1,0:T(8,128)(2,1)}, bf16[32,4,16,128]{3,2,1,0:T(8,128)(2,1)}, u32[]{:S(2)}, u32[]{:S(2)}) collective-permute-start(bf16[32,4,16,128]{3,2,1,0:T(8,128)(2,1)} %get-tuple-element.13), channel_id=1, source_target_pairs={{0,3},{1,0},{2,1},{3,2},{4,7},{5,4},{6,5},{7,6},{8,11},{9,8},{10,9... | collective-permute-start | bytes 1572872 | tf_op jit(solution)/shard_map/ppermute | solution.py:48
  48.1 43.6 %collective-permute-start.1 = (bf16[32,4,16,128]{3,2,1,0:T(8,128)(2,1)}, bf16[32,4,16,128]{3,2,1,0:T(8,128)(2,1)}, u32[]{:S(2)}, u32[]{:S(2)}) collective-permute-start(bf16[32,4,16,128]{3,2,1,0:T(8,128)(2,1)} %get-tuple-element.16), channel_id=1, source_target_pairs={{0,2},{1,3},{2,0},{3,1},{4,6},{5,7},{6,4},{7,5},{8,10},{9,11},{10,... | collective-permute-start | bytes 1572872 | tf_op jit(solution)/shard_map/ppermute | solution.py:48
  48.4 45.4 %collective-permute-start = (bf16[32,4,16,128]{3,2,1,0:T(8,128)(2,1)}, bf16[32,4,16,128]{3,2,1,0:T(8,128)(2,1)S(1)}, u32[]{:S(2)}, u32[]{:S(2)}) collective-permute-start(bf16[32,4,16,128]{3,2,1,0:T(8,128)(2,1)} %get-tuple-element.14), channel_id=1, source_target_pairs={{0,1},{1,2},{2,3},{3,0},{4,5},{5,6},{6,7},{7,4},{8,9},{9,10},{10,1... | collective-permute-start | bytes 1572872 | tf_op jit(solution)/shard_map/ppermute | solution.py:48
  102.8 1.3 copy-start
  102.8 5.9 %copy-start.3 = (f32[4,64]{1,0:T(4,128)S(1)}, f32[4,64]{1,0:T(4,128)}, u32[]{:S(2)}) copy-start(f32[4,64]{1,0:T(4,128)} %param.8) | copy-start | bytes 3076
  104.1 30.2 %all-to-all-start = ((bf16[128,4,16,128]{3,2,1,0:T(8,128)(2,1)}), bf16[128,4,16,128]{3,2,1,0:T(8,128)(2,1)}, u32[]{:S(2)}, u32[]{:S(2)}) async-start(bf16[128,4,16,128]{3,2,1,0:T(8,128)(2,1)} %bitcast.69), calls=%async_computation | async-start | bytes 4194304 | tf_op jit(solution)/shard_map/all_to_all | solution.py:193
  112.0 25.1 %collective-permute-start.6 = (bf16[32,1,64,128]{3,2,1,0:T(8,128)(2,1)}, bf16[32,1,64,128]{3,2,1,0:T(8,128)(2,1)S(1)}, u32[]{:S(2)}, u32[]{:S(2)}) collective-permute-start(bf16[32,1,64,128]{3,2,1,0:T(8,128)(2,1)} %get-tuple-element.7), channel_id=1, source_target_pairs={{4,0},{8,4},{12,8},{16,12},{20,16},{24,20},{28,24},{5,1},{9,5},{13... | collective-permute-start | bytes 1572872 | tf_op jit(solution)/shard_map/ppermute | solution.py:24
  113.3 26.4 %collective-permute-start.7 = (bf16[32,1,64,128]{3,2,1,0:T(8,128)(2,1)}, bf16[32,1,64,128]{3,2,1,0:T(8,128)(2,1)S(1)}, u32[]{:S(2)}, u32[]{:S(2)}) collective-permute-start(bf16[32,1,64,128]{3,2,1,0:T(8,128)(2,1)} %get-tuple-element.8), channel_id=1, source_target_pairs={{0,4},{4,8},{8,12},{12,16},{16,20},{20,24},{24,28},{1,5},{5,9},{9,... | collective-permute-start | bytes 1572872 | tf_op jit(solution)/shard_map/ppermute | solution.py:22
  136.5 3.2 %copy-start.1 = (f32[4,64]{1,0:T(4,128)S(1)}, f32[4,64]{1,0:T(4,128)}, u32[]{:S(2)}) copy-start(f32[4,64]{1,0:T(4,128)} %param.9) | copy-start | bytes 3076
  147.2 13.0 %collective-permute-start.10 = (bf16[1,256,256]{2,1,0:T(8,128)(2,1)S(1)}, bf16[1,256,256]{2,1,0:T(8,128)(2,1)S(1)}, u32[]{:S(2)}, u32[]{:S(2)}) collective-permute-start(bf16[1,256,256]{2,1,0:T(8,128)(2,1)S(1)} %get-tuple-element.22), channel_id=1, source_target_pairs={{0,20},{4,24},{8,28},{12,0},{16,4},{20,8},{24,12},{28,16},{1,21},{... | collective-permute-start | bytes 393224 | tf_op jit(solution)/shard_map/ppermute | solution.py:48
  151.7 9.9 %collective-permute-start.11 = (bf16[1,256,256]{2,1,0:T(8,128)(2,1)S(1)}, bf16[1,256,256]{2,1,0:T(8,128)(2,1)S(1)}, u32[]{:S(2)}, u32[]{:S(2)}) collective-permute-start(bf16[1,256,256]{2,1,0:T(8,128)(2,1)S(1)} %get-tuple-element.21), channel_id=1, source_target_pairs={{0,8},{4,12},{8,16},{12,20},{16,24},{20,28},{24,0},{28,4},{1,9},{5... | collective-permute-start | bytes 393224 | tf_op jit(solution)/shard_map/ppermute | solution.py:48
  151.7 9.9 %collective-permute-start.12 = (bf16[1,256,256]{2,1,0:T(8,128)(2,1)S(1)}, bf16[1,256,256]{2,1,0:T(8,128)(2,1)S(1)}, u32[]{:S(2)}, u32[]{:S(2)}) collective-permute-start(bf16[1,256,256]{2,1,0:T(8,128)(2,1)S(1)} %get-tuple-element.20), channel_id=1, source_target_pairs={{0,24},{4,28},{8,0},{12,4},{16,8},{20,12},{24,16},{28,20},{1,25},{... | collective-permute-start | bytes 393224 | tf_op jit(solution)/shard_map/ppermute | solution.py:48
  155.5 9.8 %collective-permute-start.13 = (bf16[1,256,256]{2,1,0:T(8,128)(2,1)S(1)}, bf16[1,256,256]{2,1,0:T(8,128)(2,1)S(1)}, u32[]{:S(2)}, u32[]{:S(2)}) collective-permute-start(bf16[1,256,256]{2,1,0:T(8,128)(2,1)S(1)} %get-tuple-element.19), channel_id=1, source_target_pairs={{0,4},{4,8},{8,12},{12,16},{16,20},{20,24},{24,28},{28,0},{1,5},{5... | collective-permute-start | bytes 393224 | tf_op jit(solution)/shard_map/ppermute | solution.py:48
  156.2 9.2 %collective-permute-start.14 = (bf16[1,256,256]{2,1,0:T(8,128)(2,1)S(1)}, bf16[1,256,256]{2,1,0:T(8,128)(2,1)S(1)}, u32[]{:S(2)}, u32[]{:S(2)}) collective-permute-start(bf16[1,256,256]{2,1,0:T(8,128)(2,1)S(1)} %get-tuple-element.18), channel_id=1, source_target_pairs={{0,28},{4,0},{8,4},{12,8},{16,12},{20,16},{24,20},{28,24},{1,29},{... | collective-permute-start | bytes 393224 | tf_op jit(solution)/shard_map/ppermute | solution.py:48
  160.2 14.9 %collective-permute-start.8 = (bf16[1,256,256]{2,1,0:T(8,128)(2,1)S(1)}, bf16[1,256,256]{2,1,0:T(8,128)(2,1)S(1)}, u32[]{:S(2)}, u32[]{:S(2)}) collective-permute-start(bf16[1,256,256]{2,1,0:T(8,128)(2,1)S(1)} %get-tuple-element.17), channel_id=1, source_target_pairs={{0,16},{4,20},{8,24},{12,28},{16,0},{20,4},{24,8},{28,12},{1,17},{... | collective-permute-start | bytes 393224 | tf_op jit(solution)/shard_map/ppermute | solution.py:48
  161.6 13.8 %collective-permute-start.9 = (bf16[1,256,256]{2,1,0:T(8,128)(2,1)S(1)}, bf16[1,256,256]{2,1,0:T(8,128)(2,1)S(1)}, u32[]{:S(2)}, u32[]{:S(2)}) collective-permute-start(bf16[1,256,256]{2,1,0:T(8,128)(2,1)S(1)} %get-tuple-element.23), channel_id=1, source_target_pairs={{0,12},{4,16},{8,20},{12,24},{16,28},{20,0},{24,4},{28,8},{1,13},{... | collective-permute-start | bytes 393224 | tf_op jit(solution)/shard_map/ppermute | solution.py:48

commit v19 on v16

--- a/solution.py
+++ b/solution.py
@@ -217,12 +217,18 @@
             - azimuthal[:, None, :, None] * field_f32
         )
     ).astype(jnp.bfloat16)
-    right_side = jnp.concatenate([direct_modes, image], axis=-1)
-    product = jnp.einsum(
-        "kpa,kpb->kab",
-        weighted.reshape(local_angles, -1, columns),
-        right_side.reshape(local_angles, -1, 2 * columns),
-        preferred_element_type=jnp.float32,
+    left_side = weighted.reshape(local_angles, -1, columns)
+    product = jnp.concatenate(
+        [
+            jnp.einsum(
+                "kpa,kpb->kab",
+                left_side,
+                right.reshape(local_angles, -1, columns),
+                preferred_element_type=jnp.float32,
+            )
+            for right in (direct_modes, image)
+        ],
+        axis=-1,
     )
     gram_terms = complex_blocks(product, snap_count).reshape(local_angles * snap_count, 2 * columns)
     row_count = gram_terms.shape[0] // lax.axis_size("gx")

time: 156 us -> 176 us (1.13)
  waiting for transfers between devices: 62.1 us -> 84.7 us
  local copies, waits for them, and re-layouts: 26.1 us -> 24 us
    ppermute x19, waiting for transfers between devices: 55 us -> 64.6 us  [exchange(): lax.ppermute(piece, axis, [(j, (j + shift) % count) for j in range(count)])]
    ppermute x1, waiting for transfers between devices: 0.01 us -> 8.69 us  [padded_2(): lax.ppermute(head, axis, [((i + 1) % count, i) for i in range(ends)])]
    ppermute x1, waiting for transfers between devices: 7.14 us -> 11.4 us  [padded_2(): lax.ppermute(tail, axis, [(i, (i + 1) % count) for i in range(ends)])]
    unnamed x18, local copies, waits for them, and re-layouts: 16.7 us -> 14.6 us
  transfers between devices with their start and end apart: 21 -> 21, of which waited for: 13 -> 14; matrix products, arithmetic and copies ran while one was open for 17% -> 14% of each run, Pallas kernels for 5% -> 4%
where the time goes in v19:
time: 176 us
  waiting for transfers between devices  84.7 us (48%)
  starting transfers between devices  32 us (18%)
  local copies, waits for them, and re-layouts  24 us (14%)
  other arithmetic  13.7 us (8%)
  blocking collectives  11.6 us (7%)
  Pallas kernels  7.03 us (4%)
    ppermute x19, waiting for transfers between devices, exchange(): lax.ppermute(piece, axis, [(j, (j + shift) % count) for j in range(count)])  64.6 us
    ppermute x19, starting transfers between devices, exchange(): lax.ppermute(piece, axis, [(j, (j + shift) % count) for j in range(count)])  26 us
    unnamed x18, local copies, waits for them, and re-layouts  14.6 us
    all_to_all x1, blocking collectives, gather_small(): return lax.all_to_all(copies, axis, split_axis=0, concat_axis=0, tiled=True)  11.6 us
    ppermute x1, waiting for transfers between devices, padded_2(): lax.ppermute(tail, axis, [(i, (i + 1) % count) for i in range(ends)])  11.4 us
    ppermute x1, waiting for transfers between devices, padded_2(): lax.ppermute(head, axis, [((i + 1) % count, i) for i in range(ends)])  8.69 us
    pallas_call x2, Pallas kernels, dft(): pl.pallas_call(functools.partial(dft_kernel, count=count, weighted=weight...  7.03 us
    convert_element_type x1, other arithmetic, local(): image = (-velocity * (forward - behind) * 0.5 + diffusion * (forward + be...  5.9 us
  transfers between devices with their start and end apart: 21, of which 14 were waited for; matrix products, arithmetic and copies ran while one was open for 14% of the time, Pallas kernels for 4%

profile of v19, /device:TPU:0, one launch (start us, length us, event | category | flops | bytes accessed | tf_op | source)
XLA Modules:
  0.0 175.7 jit_solution(16038294601260059743)
XLA Ops:
  0.7 3.1 %constant_dynamic-slice_fusion.10 = (bf16[32,4,16,128]{3,2,1,0:T(8,128)(2,1)}, bf16[32,4,16,128]{3,2,1,0:T(8,128)(2,1)}, bf16[32,4,16,128]{3,2,1,0:T(8,128)(2,1)S(1)}, bf16[32,4,16,128]{3,2,1,0:T(8,128)(2,1)}) fusion(bf16[32,4,64,128]{3,2,1,0:T(8,128)(2,1)} %param.5, s32[]{:T(128)S(6)} %select_n.222, s32[]{:T(128)S(6)} %select_n.218, s32[]{:T(128)S(6)} %select_n.216, ...), kind=kLoop, calls=%fused_computation.106 | loop fusion | bytes 4194320 | tf_op jit(solution)/shard_map/dynamic_slice | solution.py:46
  3.8 2.4 %collective-permute-start.8 = (bf16[32,4,16,128]{3,2,1,0:T(8,128)(2,1)}, bf16[32,4,16,128]{3,2,1,0:T(8,128)(2,1)}, u32[]{:S(2)}, u32[]{:S(2)}) collective-permute-start(bf16[32,4,16,128]{3,2,1,0:T(8,128)(2,1)} %get-tuple-element.19), channel_id=1, source_target_pairs={{0,3},{1,0},{2,1},{3,2},{4,7},{5,4},{6,5},{7,6},{8,11},{9,8},{10,9... | collective-permute-start | bytes 1572872 | tf_op jit(solution)/shard_map/ppermute | solution.py:48
  7.0 1.5 constant_dynamic-slice_fusion.18
  8.5 1.5 collective-permute-start.2
  10.0 1.5 collective-permute-start.1
  13.2 1.2 copy.45
  14.3 1.1 copy.49
  16.2 2.5 %collective-permute-done.8 = bf16[32,4,16,128]{3,2,1,0:T(8,128)(2,1)} collective-permute-done((bf16[32,4,16,128]{3,2,1,0:T(8,128)(2,1)}, bf16[32,4,16,128]{3,2,1,0:T(8,128)(2,1)}, u32[]{:S(2)}, u32[]{:S(2)}) %collective-permute-start.8) | collective-permute-done | bytes 524320 | tf_op jit(solution)/shard_map/ppermute | solution.py:48
  18.8 1.1 collective-permute-start
  19.9 2.2 %copy.42 = bf16[4,8,64,128]{3,1,2,0:T(8,128)(2,1)} copy(bf16[4,8,64,128]{3,2,1,0:T(8,128)(2,1)} %bitcast.48) | data formatting | bytes 1048576
  22.1 8.9 %collective-permute-done.7 = bf16[32,4,16,128]{3,2,1,0:T(8,128)(2,1)S(1)} collective-permute-done((bf16[32,4,16,128]{3,2,1,0:T(8,128)(2,1)}, bf16[32,4,16,128]{3,2,1,0:T(8,128)(2,1)S(1)}, u32[]{:S(2)}, u32[]{:S(2)}) %collective-permute-start.7) | collective-permute-done | bytes 524320 | tf_op jit(solution)/shard_map/ppermute | solution.py:48
  31.0 1.1 copy.43
  32.2 1.1 copy.44
  33.3 3.4 %shard_map.77 = bf16[128,8192]{1,0:T(8,128)(2,1)} custom-call(bf16[128,256]{1,0:T(8,128)(2,1)} %concatenate.21.refs_0_, bf16[32,8192]{1,0:T(8,128)(2,1)} %bitcast.97, bf16[32,8192]{1,0:T(8,128)(2,1)} %bitcast.103, bf16[32,8192]{1,0:T(8,128)(2,1)} %bitcast.101, bf16[32,8192]{1,0:T(8,128)(2,1)} %bitcast.99), custom_call_target="tpu_custom_call" | custom-call | tf_op jit(solution)/shard_map/pallas_call | solution.py:112
  36.7 2.2 %copy.33 = bf16[16,8,64,128]{3,2,1,0:T(8,128)(2,1)S(1)} copy(bf16[16,8,64,128]{3,1,2,0:T(8,128)(2,1)} %bitcast.91) | data formatting | bytes 4194304
  38.9 1.5 dynamic-slice_bitcast_fusion.4
  40.5 1.4 collective-permute-start.10
  41.9 1.5 collective-permute-start.11
  43.3 1.1 copy.46
  44.5 9.0 %collective-permute-done.1 = bf16[32,4,16,128]{3,2,1,0:T(8,128)(2,1)S(1)} collective-permute-done((bf16[32,4,16,128]{3,2,1,0:T(8,128)(2,1)}, bf16[32,4,16,128]{3,2,1,0:T(8,128)(2,1)S(1)}, u32[]{:S(2)}, u32[]{:S(2)}) %collective-permute-start.1) | collective-permute-done | bytes 524320 | tf_op jit(solution)/shard_map/ppermute | solution.py:48
  53.5 1.1 copy.47
  54.6 1.1 copy.48
  56.5 3.6 %shard_map.76 = bf16[128,8192]{1,0:T(8,128)(2,1)} custom-call(bf16[128,256]{1,0:T(8,128)(2,1)} %concatenate.21.refs_0_, bf16[32,8192]{1,0:T(8,128)(2,1)} %bitcast.96, bf16[32,8192]{1,0:T(8,128)(2,1)} %bitcast.102, bf16[32,8192]{1,0:T(8,128)(2,1)} %bitcast.100, bf16[32,8192]{1,0:T(8,128)(2,1)} %bitcast.98, f32[1,8192]{1,0:T(1,128)} %bitcast.113), custom_call_target="tpu_custom_call" | custom-call | tf_op jit(solution)/shard_map/pallas_call | solution.py:112
  60.1 2.2 %copy.28 = bf16[16,8,64,128]{3,2,1,0:T(8,128)(2,1)S(1)} copy(bf16[16,8,64,128]{3,1,2,0:T(8,128)(2,1)} %bitcast.89) | data formatting | bytes 4194304
  62.8 1.4 collective-permute-start.4
  64.4 1.2 collective-permute-start.5
  65.7 9.2 %collective-permute-done.11 = bf16[32,4,16,128]{3,2,1,0:T(8,128)(2,1)} collective-permute-done((bf16[32,4,16,128]{3,2,1,0:T(8,128)(2,1)S(1)}, bf16[32,4,16,128]{3,2,1,0:T(8,128)(2,1)}, u32[]{:S(2)}, u32[]{:S(2)}) %collective-permute-start.11) | collective-permute-done | bytes 524320 | tf_op jit(solution)/shard_map/ppermute | solution.py:48
  74.8 1.5 pad_maximum_fusion.10
  76.3 10.5 %collective-permute-done.3 = bf16[32,4,16,128]{3,2,1,0:T(8,128)(2,1)S(1)} collective-permute-done((bf16[32,4,16,128]{3,2,1,0:T(8,128)(2,1)S(1)}, bf16[32,4,16,128]{3,2,1,0:T(8,128)(2,1)S(1)}, u32[]{:S(2)}, u32[]{:S(2)}) %collective-permute-start.3) | collective-permute-done | bytes 524320 | tf_op jit(solution)/shard_map/ppermute | solution.py:48
  87.2 10.1 %collective-permute-done.5 = bf16[32,4,16,128]{3,2,1,0:T(8,128)(2,1)S(1)} collective-permute-done((bf16[32,4,16,128]{3,2,1,0:T(8,128)(2,1)S(1)}, bf16[32,4,16,128]{3,2,1,0:T(8,128)(2,1)S(1)}, u32[]{:S(2)}, u32[]{:S(2)}) %collective-permute-start.5) | collective-permute-done | bytes 524320 | tf_op jit(solution)/shard_map/ppermute | solution.py:48
  98.5 0.8 pad_maximum_fusion.11
  99.3 1.3 collective-permute-start.12
  100.6 4.8 %collective-permute-start.13 = (bf16[32,1,64,128]{3,2,1,0:T(8,128)(2,1)S(1)}, bf16[32,1,64,128]{3,2,1,0:T(8,128)(2,1)S(1)}, u32[]{:S(2)}, u32[]{:S(2)}) collective-permute-start(bf16[32,1,64,128]{3,2,1,0:T(8,128)(2,1)S(1)} %get-tuple-element.8), channel_id=1, source_target_pairs={{0,4},{4,8},{8,12},{12,16},{16,20},{20,24},{24,28},{1,5},{5,9},{9,... | collective-permute-start | bytes 1572872 | tf_op jit(solution)/shard_map/ppermute | solution.py:22
  105.7 0.8 fusion.23
  107.1 8.7 %collective-permute-done.12 = bf16[32,1,64,128]{3,2,1,0:T(8,128)(2,1)S(1)} collective-permute-done((bf16[32,1,64,128]{3,2,1,0:T(8,128)(2,1)S(1)}, bf16[32,1,64,128]{3,2,1,0:T(8,128)(2,1)S(1)}, u32[]{:S(2)}, u32[]{:S(2)}) %collective-permute-start.12) | collective-permute-done | bytes 524320 | tf_op jit(solution)/shard_map/ppermute | solution.py:24
  115.8 11.4 %collective-permute-done.13 = bf16[32,1,64,128]{3,2,1,0:T(8,128)(2,1)S(1)} collective-permute-done((bf16[32,1,64,128]{3,2,1,0:T(8,128)(2,1)S(1)}, bf16[32,1,64,128]{3,2,1,0:T(8,128)(2,1)S(1)}, u32[]{:S(2)}, u32[]{:S(2)}) %collective-permute-start.13) | collective-permute-done | bytes 524320 | tf_op jit(solution)/shard_map/ppermute | solution.py:22
  127.2 5.9 %fusion.6 = bf16[32,4,64,128]{3,2,1,0:T(8,128)(2,1)S(1)} fusion(f32[32,4,64,128]{3,2,1,0:T(8,128)S(1)} %get-tuple-element.10, bf16[32,1,64,128]{3,2,1,0:T(8,128)(2,1)S(1)} %collective-permute-done.13, bf16[32,4,16,128]{3,2,1,0:T(8,128)(2,1)S(1)} %get-tuple-element.12, bf16[32,4,16,128]{3,2,1,0:T(8,128)(2,1)S(1)} %get-tuple-element.13, ...), kind=kLoop, calls=%fused_computation.10 | loop fusion | flops 34603008 | bytes 9447424 | tf_op jit(solution)/shard_map/convert_element_type | solution.py:219
  135.3 2.7 %collective-permute-start.14 = (bf16[1,256,256]{2,1,0:T(8,128)(2,1)S(1)}, bf16[1,256,256]{2,1,0:T(8,128)(2,1)S(1)}, u32[]{:S(2)}, u32[]{:S(2)}) collective-permute-start(bf16[1,256,256]{2,1,0:T(8,128)(2,1)S(1)} %get-tuple-element.35), channel_id=1, source_target_pairs={{0,16},{4,20},{8,24},{12,28},{16,0},{20,4},{24,8},{28,12},{1,17},{... | collective-permute-start | bytes 393224 | tf_op jit(solution)/shard_map/ppermute | solution.py:48
  138.0 0.9 collective-permute-start.15
  138.9 3.0 %collective-permute-start.16 = (bf16[1,256,256]{2,1,0:T(8,128)(2,1)S(1)}, bf16[1,256,256]{2,1,0:T(8,128)(2,1)S(1)}, u32[]{:S(2)}, u32[]{:S(2)}) collective-permute-start(bf16[1,256,256]{2,1,0:T(8,128)(2,1)S(1)} %get-tuple-element.40), channel_id=1, source_target_pairs={{0,20},{4,24},{8,28},{12,0},{16,4},{20,8},{24,12},{28,16},{1,21},{... | collective-permute-start | bytes 393224 | tf_op jit(solution)/shard_map/ppermute | solution.py:48
  141.8 1.6 collective-permute-start.17
  143.4 2.2 %collective-permute-start.18 = (bf16[1,256,256]{2,1,0:T(8,128)(2,1)S(1)}, bf16[1,256,256]{2,1,0:T(8,128)(2,1)S(1)}, u32[]{:S(2)}, u32[]{:S(2)}) collective-permute-start(bf16[1,256,256]{2,1,0:T(8,128)(2,1)S(1)} %get-tuple-element.38), channel_id=1, source_target_pairs={{0,24},{4,28},{8,0},{12,4},{16,8},{20,12},{24,16},{28,20},{1,25},{... | collective-permute-start | bytes 393224 | tf_op jit(solution)/shard_map/ppermute | solution.py:48
  145.7 8.3 %collective-permute-done.14 = bf16[1,256,256]{2,1,0:T(8,128)(2,1)S(1)} collective-permute-done((bf16[1,256,256]{2,1,0:T(8,128)(2,1)S(1)}, bf16[1,256,256]{2,1,0:T(8,128)(2,1)S(1)}, u32[]{:S(2)}, u32[]{:S(2)}) %collective-permute-start.14) | collective-permute-done | bytes 131104 | tf_op jit(solution)/shard_map/ppermute | solution.py:48
  153.9 2.0 %collective-permute-done.15 = bf16[1,256,256]{2,1,0:T(8,128)(2,1)S(1)} collective-permute-done((bf16[1,256,256]{2,1,0:T(8,128)(2,1)S(1)}, bf16[1,256,256]{2,1,0:T(8,128)(2,1)S(1)}, u32[]{:S(2)}, u32[]{:S(2)}) %collective-permute-start.15) | collective-permute-done | bytes 131104 | tf_op jit(solution)/shard_map/ppermute | solution.py:48
  155.9 2.8 %collective-permute-start.20 = (bf16[1,256,256]{2,1,0:T(8,128)(2,1)S(1)}, bf16[1,256,256]{2,1,0:T(8,128)(2,1)S(1)}, u32[]{:S(2)}, u32[]{:S(2)}) collective-permute-start(bf16[1,256,256]{2,1,0:T(8,128)(2,1)S(1)} %get-tuple-element.36), channel_id=1, source_target_pairs={{0,28},{4,0},{8,4},{12,8},{16,12},{20,16},{24,20},{28,24},{1,29},{... | collective-permute-start | bytes 393224 | tf_op jit(solution)/shard_map/ppermute | solution.py:48
  158.7 3.1 %collective-permute-done.19 = bf16[1,256,256]{2,1,0:T(8,128)(2,1)S(1)} collective-permute-done((bf16[1,256,256]{2,1,0:T(8,128)(2,1)S(1)}, bf16[1,256,256]{2,1,0:T(8,128)(2,1)S(1)}, u32[]{:S(2)}, u32[]{:S(2)}) %collective-permute-start.19) | collective-permute-done | bytes 131104 | tf_op jit(solution)/shard_map/ppermute | solution.py:48
  162.6 11.6 %all_to_all.6 = f32[8,1,32]{2,1,0:T(1,128)S(1)} all-to-all(f32[8,1,32]{2,1,0:T(1,128)S(1)} %broadcast_in_dim.5), channel_id=1, replica_groups=mesh['gx'=8,'ka'=4] {'gx'}, dimensions={0} | all-to-all | bytes 2048 | tf_op jit(solution)/shard_map/all_to_all | solution.py:34
  174.9 0.8 slice_multiply_fusion
  (62 shorter events, 10.8 us)
Async XLA Ops:
  0.7 6.3 %copy-start = (bf16[32,4,64,128]{3,2,1,0:T(8,128)(2,1)S(1)}, bf16[32,4,64,128]{3,2,1,0:T(8,128)(2,1)}, u32[]{:S(2)}) copy-start(bf16[32,4,64,128]{3,2,1,0:T(8,128)(2,1)} %param.6) | copy-start | bytes 6291460
  3.8 14.9 %collective-permute-start.8 = (bf16[32,4,16,128]{3,2,1,0:T(8,128)(2,1)}, bf16[32,4,16,128]{3,2,1,0:T(8,128)(2,1)}, u32[]{:S(2)}, u32[]{:S(2)}) collective-permute-start(bf16[32,4,16,128]{3,2,1,0:T(8,128)(2,1)} %get-tuple-element.19), channel_id=1, source_target_pairs={{0,3},{1,0},{2,1},{3,2},{4,7},{5,4},{6,5},{7,6},{8,11},{9,8},{10,9... | collective-permute-start | bytes 1572872 | tf_op jit(solution)/shard_map/ppermute | solution.py:48
  6.2 24.8 %collective-permute-start.7 = (bf16[32,4,16,128]{3,2,1,0:T(8,128)(2,1)}, bf16[32,4,16,128]{3,2,1,0:T(8,128)(2,1)S(1)}, u32[]{:S(2)}, u32[]{:S(2)}) collective-permute-start(bf16[32,4,16,128]{3,2,1,0:T(8,128)(2,1)} %get-tuple-element.22), channel_id=1, source_target_pairs={{0,2},{1,3},{2,0},{3,1},{4,6},{5,7},{6,4},{7,5},{8,10},{9,11},{10,... | collective-permute-start | bytes 1572872 | tf_op jit(solution)/shard_map/ppermute | solution.py:48
  6.8 25.4 %collective-permute-start.6 = (bf16[32,4,16,128]{3,2,1,0:T(8,128)(2,1)}, bf16[32,4,16,128]{3,2,1,0:T(8,128)(2,1)S(1)}, u32[]{:S(2)}, u32[]{:S(2)}) collective-permute-start(bf16[32,4,16,128]{3,2,1,0:T(8,128)(2,1)} %get-tuple-element.20), channel_id=1, source_target_pairs={{0,1},{1,2},{2,3},{3,0},{4,5},{5,6},{6,7},{7,4},{8,9},{9,10},{10,1... | collective-permute-start | bytes 1572872 | tf_op jit(solution)/shard_map/ppermute | solution.py:48
  8.5 7.0 %copy-start.2 = (f32[4,64]{1,0:T(4,128)S(1)}, f32[4,64]{1,0:T(4,128)}, u32[]{:S(2)}) copy-start(f32[4,64]{1,0:T(4,128)} %param.8) | copy-start | bytes 3076
  8.5 33.4 %collective-permute-start.2 = (bf16[32,4,16,128]{3,2,1,0:T(8,128)(2,1)}, bf16[32,4,16,128]{3,2,1,0:T(8,128)(2,1)S(1)}, u32[]{:S(2)}, u32[]{:S(2)}) collective-permute-start(bf16[32,4,16,128]{3,2,1,0:T(8,128)(2,1)} %get-tuple-element.31), channel_id=1, source_target_pairs={{0,3},{1,0},{2,1},{3,2},{4,7},{5,4},{6,5},{7,6},{8,11},{9,8},{10,9... | collective-permute-start | bytes 1572872 | tf_op jit(solution)/shard_map/ppermute | solution.py:48
  10.0 43.5 %collective-permute-start.1 = (bf16[32,4,16,128]{3,2,1,0:T(8,128)(2,1)}, bf16[32,4,16,128]{3,2,1,0:T(8,128)(2,1)S(1)}, u32[]{:S(2)}, u32[]{:S(2)}) collective-permute-start(bf16[32,4,16,128]{3,2,1,0:T(8,128)(2,1)} %get-tuple-element.34), channel_id=1, source_target_pairs={{0,2},{1,3},{2,0},{3,1},{4,6},{5,7},{6,4},{7,5},{8,10},{9,11},{10,... | collective-permute-start | bytes 1572872 | tf_op jit(solution)/shard_map/ppermute | solution.py:48
  18.8 35.9 %collective-permute-start = (bf16[32,4,16,128]{3,2,1,0:T(8,128)(2,1)}, bf16[32,4,16,128]{3,2,1,0:T(8,128)(2,1)S(1)}, u32[]{:S(2)}, u32[]{:S(2)}) collective-permute-start(bf16[32,4,16,128]{3,2,1,0:T(8,128)(2,1)} %get-tuple-element.32), channel_id=1, source_target_pairs={{0,1},{1,2},{2,3},{3,0},{4,5},{5,6},{6,7},{7,4},{8,9},{9,10},{10,1... | collective-permute-start | bytes 1572872 | tf_op jit(solution)/shard_map/ppermute | solution.py:48
  38.9 1.5 copy-start.3
  40.4 24.0 %collective-permute-start.9 = (bf16[32,4,16,128]{3,2,1,0:T(8,128)(2,1)}, bf16[32,4,16,128]{3,2,1,0:T(8,128)(2,1)S(1)}, u32[]{:S(2)}, u32[]{:S(2)}) collective-permute-start(bf16[32,4,16,128]{3,2,1,0:T(8,128)(2,1)} %get-tuple-element.18), channel_id=1, source_target_pairs={{0,1},{1,2},{2,3},{3,0},{4,5},{5,6},{6,7},{7,4},{8,9},{9,10},{10,1... | collective-permute-start | bytes 1572872 | tf_op jit(solution)/shard_map/ppermute | solution.py:48
  40.5 25.2 %collective-permute-start.10 = (bf16[32,4,16,128]{3,2,1,0:T(8,128)(2,1)}, bf16[32,4,16,128]{3,2,1,0:T(8,128)(2,1)}, u32[]{:S(2)}, u32[]{:S(2)}) collective-permute-start(bf16[32,4,16,128]{3,2,1,0:T(8,128)(2,1)} %get-tuple-element.17), channel_id=1, source_target_pairs={{0,2},{1,3},{2,0},{3,1},{4,6},{5,7},{6,4},{7,5},{8,10},{9,11},{10,... | collective-permute-start | bytes 1572872 | tf_op jit(solution)/shard_map/ppermute | solution.py:48
  41.9 33.0 %collective-permute-start.11 = (bf16[32,4,16,128]{3,2,1,0:T(8,128)(2,1)S(1)}, bf16[32,4,16,128]{3,2,1,0:T(8,128)(2,1)}, u32[]{:S(2)}, u32[]{:S(2)}) collective-permute-start(bf16[32,4,16,128]{3,2,1,0:T(8,128)(2,1)S(1)} %get-tuple-element.16), channel_id=1, source_target_pairs={{0,3},{1,0},{2,1},{3,2},{4,7},{5,4},{6,5},{7,6},{8,11},{9,8},{10,9... | collective-permute-start | bytes 1572872 | tf_op jit(solution)/shard_map/ppermute | solution.py:48
  62.7 24.1 %collective-permute-start.3 = (bf16[32,4,16,128]{3,2,1,0:T(8,128)(2,1)S(1)}, bf16[32,4,16,128]{3,2,1,0:T(8,128)(2,1)S(1)}, u32[]{:S(2)}, u32[]{:S(2)}) collective-permute-start(bf16[32,4,16,128]{3,2,1,0:T(8,128)(2,1)S(1)} %get-tuple-element.30), channel_id=1, source_target_pairs={{0,1},{1,2},{2,3},{3,0},{4,5},{5,6},{6,7},{7,4},{8,9},{9,10},{10,1... | collective-permute-start | bytes 1572872 | tf_op jit(solution)/shard_map/ppermute | solution.py:48
  62.8 24.4 %collective-permute-start.4 = (bf16[32,4,16,128]{3,2,1,0:T(8,128)(2,1)S(1)}, bf16[32,4,16,128]{3,2,1,0:T(8,128)(2,1)S(1)}, u32[]{:S(2)}, u32[]{:S(2)}) collective-permute-start(bf16[32,4,16,128]{3,2,1,0:T(8,128)(2,1)S(1)} %get-tuple-element.29), channel_id=1, source_target_pairs={{0,2},{1,3},{2,0},{3,1},{4,6},{5,7},{6,4},{7,5},{8,10},{9,11},{10,... | collective-permute-start | bytes 1572872 | tf_op jit(solution)/shard_map/ppermute | solution.py:48
  64.4 32.9 %collective-permute-start.5 = (bf16[32,4,16,128]{3,2,1,0:T(8,128)(2,1)S(1)}, bf16[32,4,16,128]{3,2,1,0:T(8,128)(2,1)S(1)}, u32[]{:S(2)}, u32[]{:S(2)}) collective-permute-start(bf16[32,4,16,128]{3,2,1,0:T(8,128)(2,1)S(1)} %get-tuple-element.28), channel_id=1, source_target_pairs={{0,3},{1,0},{2,1},{3,2},{4,7},{5,4},{6,5},{7,6},{8,11},{9,8},{10,9... | collective-permute-start | bytes 1572872 | tf_op jit(solution)/shard_map/ppermute | solution.py:48
  99.3 16.5 %collective-permute-start.12 = (bf16[32,1,64,128]{3,2,1,0:T(8,128)(2,1)S(1)}, bf16[32,1,64,128]{3,2,1,0:T(8,128)(2,1)S(1)}, u32[]{:S(2)}, u32[]{:S(2)}) collective-permute-start(bf16[32,1,64,128]{3,2,1,0:T(8,128)(2,1)S(1)} %get-tuple-element.7), channel_id=1, source_target_pairs={{4,0},{8,4},{12,8},{16,12},{20,16},{24,20},{28,24},{5,1},{9,5},{13... | collective-permute-start | bytes 1572872 | tf_op jit(solution)/shard_map/ppermute | solution.py:24
  100.6 26.5 %collective-permute-start.13 = (bf16[32,1,64,128]{3,2,1,0:T(8,128)(2,1)S(1)}, bf16[32,1,64,128]{3,2,1,0:T(8,128)(2,1)S(1)}, u32[]{:S(2)}, u32[]{:S(2)}) collective-permute-start(bf16[32,1,64,128]{3,2,1,0:T(8,128)(2,1)S(1)} %get-tuple-element.8), channel_id=1, source_target_pairs={{0,4},{4,8},{8,12},{12,16},{16,20},{20,24},{24,28},{1,5},{5,9},{9,... | collective-permute-start | bytes 1572872 | tf_op jit(solution)/shard_map/ppermute | solution.py:22
  106.5 20.7 %copy-start.1 = (f32[4,64]{1,0:T(4,128)S(1)}, f32[4,64]{1,0:T(4,128)}, u32[]{:S(2)}) copy-start(f32[4,64]{1,0:T(4,128)} %param.9) | copy-start | bytes 3076
  135.3 18.6 %collective-permute-start.14 = (bf16[1,256,256]{2,1,0:T(8,128)(2,1)S(1)}, bf16[1,256,256]{2,1,0:T(8,128)(2,1)S(1)}, u32[]{:S(2)}, u32[]{:S(2)}) collective-permute-start(bf16[1,256,256]{2,1,0:T(8,128)(2,1)S(1)} %get-tuple-element.35), channel_id=1, source_target_pairs={{0,16},{4,20},{8,24},{12,28},{16,0},{20,4},{24,8},{28,12},{1,17},{... | collective-permute-start | bytes 393224 | tf_op jit(solution)/shard_map/ppermute | solution.py:48
  138.0 17.9 %collective-permute-start.15 = (bf16[1,256,256]{2,1,0:T(8,128)(2,1)S(1)}, bf16[1,256,256]{2,1,0:T(8,128)(2,1)S(1)}, u32[]{:S(2)}, u32[]{:S(2)}) collective-permute-start(bf16[1,256,256]{2,1,0:T(8,128)(2,1)S(1)} %get-tuple-element.41), channel_id=1, source_target_pairs={{0,12},{4,16},{8,20},{12,24},{16,28},{20,0},{24,4},{28,8},{1,13},{... | collective-permute-start | bytes 393224 | tf_op jit(solution)/shard_map/ppermute | solution.py:48
  138.9 19.8 %collective-permute-start.16 = (bf16[1,256,256]{2,1,0:T(8,128)(2,1)S(1)}, bf16[1,256,256]{2,1,0:T(8,128)(2,1)S(1)}, u32[]{:S(2)}, u32[]{:S(2)}) collective-permute-start(bf16[1,256,256]{2,1,0:T(8,128)(2,1)S(1)} %get-tuple-element.40), channel_id=1, source_target_pairs={{0,20},{4,24},{8,28},{12,0},{16,4},{20,8},{24,12},{28,16},{1,21},{... | collective-permute-start | bytes 393224 | tf_op jit(solution)/shard_map/ppermute | solution.py:48
  141.8 16.8 %collective-permute-start.17 = (bf16[1,256,256]{2,1,0:T(8,128)(2,1)S(1)}, bf16[1,256,256]{2,1,0:T(8,128)(2,1)S(1)}, u32[]{:S(2)}, u32[]{:S(2)}) collective-permute-start(bf16[1,256,256]{2,1,0:T(8,128)(2,1)S(1)} %get-tuple-element.39), channel_id=1, source_target_pairs={{0,8},{4,12},{8,16},{12,20},{16,24},{20,28},{24,0},{28,4},{1,9},{5... | collective-permute-start | bytes 393224 | tf_op jit(solution)/shard_map/ppermute | solution.py:48
  143.4 15.3 %collective-permute-start.18 = (bf16[1,256,256]{2,1,0:T(8,128)(2,1)S(1)}, bf16[1,256,256]{2,1,0:T(8,128)(2,1)S(1)}, u32[]{:S(2)}, u32[]{:S(2)}) collective-permute-start(bf16[1,256,256]{2,1,0:T(8,128)(2,1)S(1)} %get-tuple-element.38), channel_id=1, source_target_pairs={{0,24},{4,28},{8,0},{12,4},{16,8},{20,12},{24,16},{28,20},{1,25},{... | collective-permute-start | bytes 393224 | tf_op jit(solution)/shard_map/ppermute | solution.py:48
  153.9 7.8 %collective-permute-start.19 = (bf16[1,256,256]{2,1,0:T(8,128)(2,1)S(1)}, bf16[1,256,256]{2,1,0:T(8,128)(2,1)S(1)}, u32[]{:S(2)}, u32[]{:S(2)}) collective-permute-start(bf16[1,256,256]{2,1,0:T(8,128)(2,1)S(1)} %get-tuple-element.37), channel_id=1, source_target_pairs={{0,4},{4,8},{8,12},{12,16},{16,20},{20,24},{24,28},{28,0},{1,5},{5... | collective-permute-start | bytes 393224 | tf_op jit(solution)/shard_map/ppermute | solution.py:48
  155.9 6.4 %collective-permute-start.20 = (bf16[1,256,256]{2,1,0:T(8,128)(2,1)S(1)}, bf16[1,256,256]{2,1,0:T(8,128)(2,1)S(1)}, u32[]{:S(2)}, u32[]{:S(2)}) collective-permute-start(bf16[1,256,256]{2,1,0:T(8,128)(2,1)S(1)} %get-tuple-element.36), channel_id=1, source_target_pairs={{0,28},{4,0},{8,4},{12,8},{16,12},{20,16},{24,20},{28,24},{1,29},{... | collective-permute-start | bytes 393224 | tf_op jit(solution)/shard_map/ppermute | solution.py:48

commit v20 on v16

--- a/solution.py
+++ b/solution.py
@@ -34,7 +34,7 @@
     return lax.all_to_all(copies, axis, split_axis=0, concat_axis=0, tiled=True)
 
 
-def exchange(cells, axis, split_axis, far_first=False):
+def exchange(cells, axis, split_axis, far_first=False, separate=False):
     count = lax.axis_size(axis)
     here = lax.axis_index(axis)
     width = cells.shape[split_axis] // count
@@ -43,7 +43,10 @@
         shifts = [0] + sorted(range(1, count), key=lambda shift: -min(shift, count - shift))
     pieces = []
     for shift in shifts:
-        piece = lax.dynamic_slice_in_dim(cells, ((here + shift) % count) * width, width, axis=split_axis)
+        source = cells
+        if separate:
+            source, _ = lax.optimization_barrier((cells, jnp.int32(shift)))
+        piece = lax.dynamic_slice_in_dim(source, ((here + shift) % count) * width, width, axis=split_axis)
         if shift:
             piece = lax.ppermute(piece, axis, [(j, (j + shift) % count) for j in range(count)])
         pieces.append(piece)
@@ -183,7 +186,7 @@
     lane_weight = jnp.broadcast_to(band_weight[:, :, None], (axial_cells, band, columns)).reshape(1, lanes)
 
     def transform_all(snapshots, weight=None):
-        pieces = [piece.reshape(local_angles, lanes) for piece in exchange(snapshots, "ka", 2)]
+        pieces = [piece.reshape(local_angles, lanes) for piece in exchange(snapshots, "ka", 2, separate=True)]
         modes = dft(table, pieces, weight)
         return modes.reshape(total_angles, axial_cells, band, columns)
 

time: 156 us -> 153 us (0.981)
  waiting for transfers between devices: 62.1 us -> 52.3 us
  local copies, waits for them, and re-layouts: 26.1 us -> 34.3 us
  starting transfers between devices: 32.2 us -> 30.6 us
    ppermute x19, waiting for transfers between devices: 55 us -> 45.4 us  [exchange(): lax.ppermute(piece, axis, [(j, (j + shift) % count) for j in range(count)])]
    dynamic_slice x3 -> x8, local copies, waits for them, and re-layouts: 4.64 us -> 10.9 us  [exchange(): lax.dynamic_slice_in_dim(source, (here + shift) % count * width, width, a...]
    unnamed x18, local copies, waits for them, and re-layouts: 16.7 us -> 18.8 us
  transfers between devices with their start and end apart: 21 -> 21, of which waited for: 13 -> 13; matrix products, arithmetic and copies ran while one was open for 17% -> 24% of each run, Pallas kernels for 5% -> 5%
where the time goes in v20:
time: 153 us; the launch traced here: 152 us
  waiting for transfers between devices  52.3 us (34%)
  local copies, waits for them, and re-layouts  34.3 us (22%)
  starting transfers between devices  30.6 us (20%)
  other arithmetic  14.2 us (9%)
  blocking collectives  11.7 us (8%)
  Pallas kernels  7.1 us (5%)
    ppermute x19, waiting for transfers between devices, exchange(): lax.ppermute(piece, axis, [(j, (j + shift) % count) for j in range(count)])  45.4 us
    ppermute x19, starting transfers between devices, exchange(): lax.ppermute(piece, axis, [(j, (j + shift) % count) for j in range(count)])  24.5 us
    unnamed x18, local copies, waits for them, and re-layouts  18.8 us
    all_to_all x1, blocking collectives, gather_small(): return lax.all_to_all(copies, axis, split_axis=0, concat_axis=0, tiled=True)  11.7 us
    dynamic_slice x8, local copies, waits for them, and re-layouts, exchange(): lax.dynamic_slice_in_dim(source, (here + shift) % count * width, width, a...  10.9 us
    pallas_call x2, Pallas kernels, dft(): pl.pallas_call(functools.partial(dft_kernel, count=count, weighted=weight...  7.1 us
    ppermute x1, waiting for transfers between devices, padded_2(): lax.ppermute(tail, axis, [(i, (i + 1) % count) for i in range(ends)])  6.89 us
    convert_element_type x1, other arithmetic, local(): image = (-velocity * (forward - behind) * 0.5 + diffusion * (forward + be...  5.9 us
  transfers between devices with their start and end apart: 21, of which 13 were waited for; matrix products, arithmetic and copies ran while one was open for 24% of the time, Pallas kernels for 5%

profile of v20, /device:TPU:0, one launch (start us, length us, event | category | flops | bytes accessed | tf_op | source)
XLA Modules:
  0.0 152.0 jit_solution(4571122543728271244)
XLA Ops:
  0.7 2.1 %constant_dynamic-slice_fusion.10 = bf16[32,4,16,128]{3,2,1,0:T(8,128)(2,1)} fusion(bf16[32,4,64,128]{3,2,1,0:T(8,128)(2,1)} %param.5, s32[]{:T(128)S(6)} %select_n.222), kind=kLoop, calls=%fused_computation.107 | loop fusion | bytes 1048580 | tf_op jit(solution)/shard_map/dynamic_slice | solution.py:49
  2.7 2.4 %collective-permute-start.8 = (bf16[32,4,16,128]{3,2,1,0:T(8,128)(2,1)}, bf16[32,4,16,128]{3,2,1,0:T(8,128)(2,1)}, u32[]{:S(2)}, u32[]{:S(2)}) collective-permute-start(bf16[32,4,16,128]{3,2,1,0:T(8,128)(2,1)} %constant_dynamic-slice_fusion.10), channel_id=1, source_target_pairs={{0,3},{1,0},{2,1},{3,2},{4,7},{5,4},{6,5},{7,6},{8,11},{9,8},{10,9... | collective-permute-start | bytes 1572872 | tf_op jit(solution)/shard_map/ppermute | solution.py:51
  5.1 1.9 %constant_dynamic-slice_fusion.11 = bf16[32,4,16,128]{3,2,1,0:T(8,128)(2,1)} fusion(bf16[32,4,64,128]{3,2,1,0:T(8,128)(2,1)} %param.5, s32[]{:T(128)S(6)} %select_n.220), kind=kLoop, calls=%fused_computation.108 | loop fusion | bytes 1048580 | tf_op jit(solution)/shard_map/dynamic_slice | solution.py:49
  7.6 1.9 %constant_dynamic-slice_fusion.12 = bf16[32,4,16,128]{3,2,1,0:T(8,128)(2,1)} fusion(bf16[32,4,64,128]{3,2,1,0:T(8,128)(2,1)} %param.5, s32[]{:T(128)S(6)} %select_n.218), kind=kLoop, calls=%fused_computation.109 | loop fusion | bytes 1048580 | tf_op jit(solution)/shard_map/dynamic_slice | solution.py:49
  9.7 1.9 %constant_dynamic-slice_fusion.18 = bf16[32,4,16,128]{3,2,1,0:T(8,128)(2,1)} fusion(bf16[32,4,64,128]{3,2,1,0:T(8,128)(2,1)} %param.6, s32[]{:T(128)S(6)} %select_n.222), kind=kLoop, calls=%fused_computation.115 | loop fusion | bytes 1048580 | tf_op jit(solution)/shard_map/dynamic_slice | solution.py:49
  11.6 1.5 collective-permute-start.2
  14.0 1.5 collective-permute-start.1
  17.1 1.3 constant_dynamic-slice_fusion.13
  18.5 1.2 copy.40
  19.7 1.2 copy.44
  22.6 2.2 %copy.37 = bf16[4,8,64,128]{3,1,2,0:T(8,128)(2,1)} copy(bf16[4,8,64,128]{3,2,1,0:T(8,128)(2,1)} %bitcast.47) | data formatting | bytes 1048576
  24.8 3.4 %collective-permute-done.7 = bf16[32,4,16,128]{3,2,1,0:T(8,128)(2,1)} collective-permute-done((bf16[32,4,16,128]{3,2,1,0:T(8,128)(2,1)}, bf16[32,4,16,128]{3,2,1,0:T(8,128)(2,1)}, u32[]{:S(2)}, u32[]{:S(2)}) %collective-permute-start.7) | collective-permute-done | bytes 524320 | tf_op jit(solution)/shard_map/ppermute | solution.py:51
  28.2 2.2 %copy.38 = bf16[4,8,64,128]{3,1,2,0:T(8,128)(2,1)} copy(bf16[4,8,64,128]{3,2,1,0:T(8,128)(2,1)} %bitcast.44) | data formatting | bytes 1048576
  30.4 1.4 collective-permute-done.6
  31.8 2.2 %copy.39 = bf16[4,8,64,128]{3,1,2,0:T(8,128)(2,1)} copy(bf16[4,8,64,128]{3,2,1,0:T(8,128)(2,1)} %bitcast.41) | data formatting | bytes 1048576
  34.0 3.5 %shard_map.77 = bf16[128,8192]{1,0:T(8,128)(2,1)} custom-call(bf16[128,256]{1,0:T(8,128)(2,1)} %concatenate.23.refs_0_, bf16[32,8192]{1,0:T(8,128)(2,1)} %bitcast.92, bf16[32,8192]{1,0:T(8,128)(2,1)} %bitcast.98, bf16[32,8192]{1,0:T(8,128)(2,1)} %bitcast.96, bf16[32,8192]{1,0:T(8,128)(2,1)} %bitcast.94), custom_call_target="tpu_custom_call" | custom-call | tf_op jit(solution)/shard_map/pallas_call | solution.py:115
  37.4 2.2 %copy.28 = bf16[16,8,64,128]{3,2,1,0:T(8,128)(2,1)S(1)} copy(bf16[16,8,64,128]{3,1,2,0:T(8,128)(2,1)} %bitcast.86) | data formatting | bytes 4194304
  39.6 1.2 dynamic-slice_bitcast_fusion.4
  40.9 1.8 %collective-permute-start.10 = (bf16[32,4,16,128]{3,2,1,0:T(8,128)(2,1)S(1)}, bf16[32,4,16,128]{3,2,1,0:T(8,128)(2,1)S(1)}, u32[]{:S(2)}, u32[]{:S(2)}) collective-permute-start(bf16[32,4,16,128]{3,2,1,0:T(8,128)(2,1)S(1)} %get-tuple-element.33), channel_id=1, source_target_pairs={{0,2},{1,3},{2,0},{3,1},{4,6},{5,7},{6,4},{7,5},{8,10},{9,11},{10,... | collective-permute-start | bytes 1572872 | tf_op jit(solution)/shard_map/ppermute | solution.py:51
  42.7 1.4 collective-permute-start.11
  44.2 2.2 %copy.41 = bf16[4,8,64,128]{3,1,2,0:T(8,128)(2,1)} copy(bf16[4,8,64,128]{3,2,1,0:T(8,128)(2,1)} %bitcast.32) | data formatting | bytes 1048576
  46.4 4.3 %collective-permute-done.1 = bf16[32,4,16,128]{3,2,1,0:T(8,128)(2,1)} collective-permute-done((bf16[32,4,16,128]{3,2,1,0:T(8,128)(2,1)}, bf16[32,4,16,128]{3,2,1,0:T(8,128)(2,1)}, u32[]{:S(2)}, u32[]{:S(2)}) %collective-permute-start.1) | collective-permute-done | bytes 524320 | tf_op jit(solution)/shard_map/ppermute | solution.py:51
  50.7 2.2 %copy.42 = bf16[4,8,64,128]{3,1,2,0:T(8,128)(2,1)} copy(bf16[4,8,64,128]{3,2,1,0:T(8,128)(2,1)} %bitcast.29) | data formatting | bytes 1048576
  52.9 1.3 collective-permute-done
  54.2 1.1 copy.43
  56.0 3.6 %shard_map.76 = bf16[128,8192]{1,0:T(8,128)(2,1)} custom-call(bf16[128,256]{1,0:T(8,128)(2,1)} %concatenate.23.refs_0_, bf16[32,8192]{1,0:T(8,128)(2,1)} %bitcast.91, bf16[32,8192]{1,0:T(8,128)(2,1)} %bitcast.97, bf16[32,8192]{1,0:T(8,128)(2,1)} %bitcast.95, bf16[32,8192]{1,0:T(8,128)(2,1)} %bitcast.93, f32[1,8192]{1,0:T(1,128)} %bitcast.105), custom_call_target="tpu_custom_call" | custom-call | tf_op jit(solution)/shard_map/pallas_call | solution.py:115
  59.6 2.2 %copy.23 = bf16[16,8,64,128]{3,2,1,0:T(8,128)(2,1)S(1)} copy(bf16[16,8,64,128]{3,1,2,0:T(8,128)(2,1)} %bitcast.84) | data formatting | bytes 4194304
  62.3 1.8 %collective-permute-start.4 = (bf16[32,4,16,128]{3,2,1,0:T(8,128)(2,1)S(1)}, bf16[32,4,16,128]{3,2,1,0:T(8,128)(2,1)S(1)}, u32[]{:S(2)}, u32[]{:S(2)}) collective-permute-start(bf16[32,4,16,128]{3,2,1,0:T(8,128)(2,1)S(1)} %get-tuple-element.41), channel_id=1, source_target_pairs={{0,2},{1,3},{2,0},{3,1},{4,6},{5,7},{6,4},{7,5},{8,10},{9,11},{10,... | collective-permute-start | bytes 1572872 | tf_op jit(solution)/shard_map/ppermute | solution.py:51
  64.1 1.3 collective-permute-done.9
  65.5 6.2 %collective-permute-done.11 = bf16[32,4,16,128]{3,2,1,0:T(8,128)(2,1)} collective-permute-done((bf16[32,4,16,128]{3,2,1,0:T(8,128)(2,1)S(1)}, bf16[32,4,16,128]{3,2,1,0:T(8,128)(2,1)}, u32[]{:S(2)}, u32[]{:S(2)}) %collective-permute-start.11) | collective-permute-done | bytes 524320 | tf_op jit(solution)/shard_map/ppermute | solution.py:51
  71.8 1.3 pad_maximum_fusion.11
  74.4 1.3 collective-permute-start.12
  75.7 4.8 %collective-permute-start.13 = (bf16[32,1,64,128]{3,2,1,0:T(8,128)(2,1)S(1)}, bf16[32,1,64,128]{3,2,1,0:T(8,128)(2,1)S(1)}, u32[]{:S(2)}, u32[]{:S(2)}) collective-permute-start(bf16[32,1,64,128]{3,2,1,0:T(8,128)(2,1)S(1)} %get-tuple-element.24), channel_id=1, source_target_pairs={{0,4},{4,8},{8,12},{12,16},{16,20},{20,24},{24,28},{1,5},{5,9},{9,... | collective-permute-start | bytes 1572872 | tf_op jit(solution)/shard_map/ppermute | solution.py:22
  80.5 7.4 %collective-permute-done.3 = bf16[32,4,16,128]{3,2,1,0:T(8,128)(2,1)S(1)} collective-permute-done((bf16[32,4,16,128]{3,2,1,0:T(8,128)(2,1)S(1)}, bf16[32,4,16,128]{3,2,1,0:T(8,128)(2,1)S(1)}, u32[]{:S(2)}, u32[]{:S(2)}) %collective-permute-start.3) | collective-permute-done | bytes 524320 | tf_op jit(solution)/shard_map/ppermute | solution.py:51
  87.9 6.4 %collective-permute-done.5 = bf16[32,4,16,128]{3,2,1,0:T(8,128)(2,1)S(1)} collective-permute-done((bf16[32,4,16,128]{3,2,1,0:T(8,128)(2,1)S(1)}, bf16[32,4,16,128]{3,2,1,0:T(8,128)(2,1)S(1)}, u32[]{:S(2)}, u32[]{:S(2)}) %collective-permute-start.5) | collective-permute-done | bytes 524320 | tf_op jit(solution)/shard_map/ppermute | solution.py:51
  95.2 6.9 %collective-permute-done.13 = bf16[32,1,64,128]{3,2,1,0:T(8,128)(2,1)S(1)} collective-permute-done((bf16[32,1,64,128]{3,2,1,0:T(8,128)(2,1)S(1)}, bf16[32,1,64,128]{3,2,1,0:T(8,128)(2,1)S(1)}, u32[]{:S(2)}, u32[]{:S(2)}) %collective-permute-start.13) | collective-permute-done | bytes 524320 | tf_op jit(solution)/shard_map/ppermute | solution.py:22
  102.1 5.9 %fusion.6 = bf16[32,4,64,128]{3,2,1,0:T(8,128)(2,1)S(1)} fusion(f32[32,4,64,128]{3,2,1,0:T(8,128)S(1)} %get-tuple-element.26, bf16[32,1,64,128]{3,2,1,0:T(8,128)(2,1)S(1)} %collective-permute-done.13, bf16[32,4,16,128]{3,2,1,0:T(8,128)(2,1)S(1)} %get-tuple-element.28, bf16[32,4,16,128]{3,2,1,0:T(8,128)(2,1)S(1)} %get-tuple-element.29, ...), kind=kLoop, calls=%fused_computation.10 | loop fusion | flops 34603008 | bytes 9447424 | tf_op jit(solution)/shard_map/convert_element_type | solution.py:222
  108.8 0.9 fusion.23
  109.7 1.2 fusion.12
  111.7 2.7 %collective-permute-start.14 = (bf16[1,256,256]{2,1,0:T(8,128)(2,1)S(1)}, bf16[1,256,256]{2,1,0:T(8,128)(2,1)S(1)}, u32[]{:S(2)}, u32[]{:S(2)}) collective-permute-start(bf16[1,256,256]{2,1,0:T(8,128)(2,1)S(1)} %get-tuple-element.43), channel_id=1, source_target_pairs={{0,16},{4,20},{8,24},{12,28},{16,0},{20,4},{24,8},{28,12},{1,17},{... | collective-permute-start | bytes 393224 | tf_op jit(solution)/shard_map/ppermute | solution.py:51
  114.3 1.0 collective-permute-start.15
  115.3 2.9 %collective-permute-start.16 = (bf16[1,256,256]{2,1,0:T(8,128)(2,1)S(1)}, bf16[1,256,256]{2,1,0:T(8,128)(2,1)S(1)}, u32[]{:S(2)}, u32[]{:S(2)}) collective-permute-start(bf16[1,256,256]{2,1,0:T(8,128)(2,1)S(1)} %get-tuple-element.48), channel_id=1, source_target_pairs={{0,20},{4,24},{8,28},{12,0},{16,4},{20,8},{24,12},{28,16},{1,21},{... | collective-permute-start | bytes 393224 | tf_op jit(solution)/shard_map/ppermute | solution.py:51
  118.2 3.8 %collective-permute-start.18 = (bf16[1,256,256]{2,1,0:T(8,128)(2,1)S(1)}, bf16[1,256,256]{2,1,0:T(8,128)(2,1)S(1)}, u32[]{:S(2)}, u32[]{:S(2)}) collective-permute-start(bf16[1,256,256]{2,1,0:T(8,128)(2,1)S(1)} %get-tuple-element.46), channel_id=1, source_target_pairs={{0,24},{4,28},{8,0},{12,4},{16,8},{20,12},{24,16},{28,20},{1,25},{... | collective-permute-start | bytes 393224 | tf_op jit(solution)/shard_map/ppermute | solution.py:51
  122.0 8.3 %collective-permute-done.14 = bf16[1,256,256]{2,1,0:T(8,128)(2,1)S(1)} collective-permute-done((bf16[1,256,256]{2,1,0:T(8,128)(2,1)S(1)}, bf16[1,256,256]{2,1,0:T(8,128)(2,1)S(1)}, u32[]{:S(2)}, u32[]{:S(2)}) %collective-permute-start.14) | collective-permute-done | bytes 131104 | tf_op jit(solution)/shard_map/ppermute | solution.py:51
  130.3 1.9 %collective-permute-done.15 = bf16[1,256,256]{2,1,0:T(8,128)(2,1)S(1)} collective-permute-done((bf16[1,256,256]{2,1,0:T(8,128)(2,1)S(1)}, bf16[1,256,256]{2,1,0:T(8,128)(2,1)S(1)}, u32[]{:S(2)}, u32[]{:S(2)}) %collective-permute-start.15) | collective-permute-done | bytes 131104 | tf_op jit(solution)/shard_map/ppermute | solution.py:51
  132.2 2.8 %collective-permute-start.20 = (bf16[1,256,256]{2,1,0:T(8,128)(2,1)S(1)}, bf16[1,256,256]{2,1,0:T(8,128)(2,1)S(1)}, u32[]{:S(2)}, u32[]{:S(2)}) collective-permute-start(bf16[1,256,256]{2,1,0:T(8,128)(2,1)S(1)} %get-tuple-element.44), channel_id=1, source_target_pairs={{0,28},{4,0},{8,4},{12,8},{16,12},{20,16},{24,20},{28,24},{1,29},{... | collective-permute-start | bytes 393224 | tf_op jit(solution)/shard_map/ppermute | solution.py:51
  135.1 3.1 %collective-permute-done.19 = bf16[1,256,256]{2,1,0:T(8,128)(2,1)S(1)} collective-permute-done((bf16[1,256,256]{2,1,0:T(8,128)(2,1)S(1)}, bf16[1,256,256]{2,1,0:T(8,128)(2,1)S(1)}, u32[]{:S(2)}, u32[]{:S(2)}) %collective-permute-start.19) | collective-permute-done | bytes 131104 | tf_op jit(solution)/shard_map/ppermute | solution.py:51
  138.9 11.7 %all_to_all.6 = f32[8,1,32]{2,1,0:T(1,128)S(1)} all-to-all(f32[8,1,32]{2,1,0:T(1,128)S(1)} %broadcast_in_dim.5), channel_id=1, replica_groups=mesh['gx'=8,'ka'=4] {'gx'}, dimensions={0} | all-to-all | bytes 2048 | tf_op jit(solution)/shard_map/all_to_all | solution.py:34
  (66 shorter events, 12.5 us)
Async XLA Ops:
  0.6 12.5 %copy-start = (bf16[32,4,64,128]{3,2,1,0:T(8,128)(2,1)S(1)}, bf16[32,4,64,128]{3,2,1,0:T(8,128)(2,1)}, u32[]{:S(2)}) copy-start(bf16[32,4,64,128]{3,2,1,0:T(8,128)(2,1)} %param.6) | copy-start | bytes 6291460
  2.7 19.8 %collective-permute-start.8 = (bf16[32,4,16,128]{3,2,1,0:T(8,128)(2,1)}, bf16[32,4,16,128]{3,2,1,0:T(8,128)(2,1)}, u32[]{:S(2)}, u32[]{:S(2)}) collective-permute-start(bf16[32,4,16,128]{3,2,1,0:T(8,128)(2,1)} %constant_dynamic-slice_fusion.10), channel_id=1, source_target_pairs={{0,3},{1,0},{2,1},{3,2},{4,7},{5,4},{6,5},{7,6},{8,11},{9,8},{10,9... | collective-permute-start | bytes 1572872 | tf_op jit(solution)/shard_map/ppermute | solution.py:51
  5.1 14.6 %copy-start.2 = (f32[4,64]{1,0:T(4,128)S(1)}, f32[4,64]{1,0:T(4,128)}, u32[]{:S(2)}) copy-start(f32[4,64]{1,0:T(4,128)} %param.8) | copy-start | bytes 3076
  7.0 21.2 %collective-permute-start.7 = (bf16[32,4,16,128]{3,2,1,0:T(8,128)(2,1)}, bf16[32,4,16,128]{3,2,1,0:T(8,128)(2,1)}, u32[]{:S(2)}, u32[]{:S(2)}) collective-permute-start(bf16[32,4,16,128]{3,2,1,0:T(8,128)(2,1)} %constant_dynamic-slice_fusion.11), channel_id=1, source_target_pairs={{0,2},{1,3},{2,0},{3,1},{4,6},{5,7},{6,4},{7,5},{8,10},{9,11},{10,... | collective-permute-start | bytes 1572872 | tf_op jit(solution)/shard_map/ppermute | solution.py:51
  9.5 22.3 %collective-permute-start.6 = (bf16[32,4,16,128]{3,2,1,0:T(8,128)(2,1)}, bf16[32,4,16,128]{3,2,1,0:T(8,128)(2,1)}, u32[]{:S(2)}, u32[]{:S(2)}) collective-permute-start(bf16[32,4,16,128]{3,2,1,0:T(8,128)(2,1)} %constant_dynamic-slice_fusion.12), channel_id=1, source_target_pairs={{0,1},{1,2},{2,3},{3,0},{4,5},{5,6},{6,7},{7,4},{8,9},{9,10},{10,1... | collective-permute-start | bytes 1572872 | tf_op jit(solution)/shard_map/ppermute | solution.py:51
  11.6 10.9 %copy-start.3 = (f32[4,64]{1,0:T(4,128)S(1)}, f32[4,64]{1,0:T(4,128)}, u32[]{:S(2)}) copy-start(f32[4,64]{1,0:T(4,128)} %param.7) | copy-start | bytes 3076
  11.6 31.0 %collective-permute-start.2 = (bf16[32,4,16,128]{3,2,1,0:T(8,128)(2,1)}, bf16[32,4,16,128]{3,2,1,0:T(8,128)(2,1)}, u32[]{:S(2)}, u32[]{:S(2)}) collective-permute-start(bf16[32,4,16,128]{3,2,1,0:T(8,128)(2,1)} %constant_dynamic-slice_fusion.18), channel_id=1, source_target_pairs={{0,3},{1,0},{2,1},{3,2},{4,7},{5,4},{6,5},{7,6},{8,11},{9,8},{10,9... | collective-permute-start | bytes 1572872 | tf_op jit(solution)/shard_map/ppermute | solution.py:51
  14.0 36.6 %collective-permute-start.1 = (bf16[32,4,16,128]{3,2,1,0:T(8,128)(2,1)}, bf16[32,4,16,128]{3,2,1,0:T(8,128)(2,1)}, u32[]{:S(2)}, u32[]{:S(2)}) collective-permute-start(bf16[32,4,16,128]{3,2,1,0:T(8,128)(2,1)} %constant_dynamic-slice_fusion.19), channel_id=1, source_target_pairs={{0,2},{1,3},{2,0},{3,1},{4,6},{5,7},{6,4},{7,5},{8,10},{9,11},{10,... | collective-permute-start | bytes 1572872 | tf_op jit(solution)/shard_map/ppermute | solution.py:51
  22.5 31.6 %collective-permute-start = (bf16[32,4,16,128]{3,2,1,0:T(8,128)(2,1)}, bf16[32,4,16,128]{3,2,1,0:T(8,128)(2,1)S(1)}, u32[]{:S(2)}, u32[]{:S(2)}) collective-permute-start(bf16[32,4,16,128]{3,2,1,0:T(8,128)(2,1)} %constant_dynamic-slice_fusion.20), channel_id=1, source_target_pairs={{0,1},{1,2},{2,3},{3,0},{4,5},{5,6},{6,7},{7,4},{8,9},{9,10},{10,1... | collective-permute-start | bytes 1572872 | tf_op jit(solution)/shard_map/ppermute | solution.py:51
  40.9 24.5 %collective-permute-start.9 = (bf16[32,4,16,128]{3,2,1,0:T(8,128)(2,1)}, bf16[32,4,16,128]{3,2,1,0:T(8,128)(2,1)S(1)}, u32[]{:S(2)}, u32[]{:S(2)}) collective-permute-start(bf16[32,4,16,128]{3,2,1,0:T(8,128)(2,1)} %get-tuple-element.34), channel_id=1, source_target_pairs={{0,1},{1,2},{2,3},{3,0},{4,5},{5,6},{6,7},{7,4},{8,9},{9,10},{10,1... | collective-permute-start | bytes 1572872 | tf_op jit(solution)/shard_map/ppermute | solution.py:51
  40.9 24.7 %collective-permute-start.10 = (bf16[32,4,16,128]{3,2,1,0:T(8,128)(2,1)S(1)}, bf16[32,4,16,128]{3,2,1,0:T(8,128)(2,1)S(1)}, u32[]{:S(2)}, u32[]{:S(2)}) collective-permute-start(bf16[32,4,16,128]{3,2,1,0:T(8,128)(2,1)S(1)} %get-tuple-element.33), channel_id=1, source_target_pairs={{0,2},{1,3},{2,0},{3,1},{4,6},{5,7},{6,4},{7,5},{8,10},{9,11},{10,... | collective-permute-start | bytes 1572872 | tf_op jit(solution)/shard_map/ppermute | solution.py:51
  42.7 29.1 %collective-permute-start.11 = (bf16[32,4,16,128]{3,2,1,0:T(8,128)(2,1)S(1)}, bf16[32,4,16,128]{3,2,1,0:T(8,128)(2,1)}, u32[]{:S(2)}, u32[]{:S(2)}) collective-permute-start(bf16[32,4,16,128]{3,2,1,0:T(8,128)(2,1)S(1)} %get-tuple-element.32), channel_id=1, source_target_pairs={{0,3},{1,0},{2,1},{3,2},{4,7},{5,4},{6,5},{7,6},{8,11},{9,8},{10,9... | collective-permute-start | bytes 1572872 | tf_op jit(solution)/shard_map/ppermute | solution.py:51
  62.3 25.6 %collective-permute-start.3 = (bf16[32,4,16,128]{3,2,1,0:T(8,128)(2,1)S(1)}, bf16[32,4,16,128]{3,2,1,0:T(8,128)(2,1)S(1)}, u32[]{:S(2)}, u32[]{:S(2)}) collective-permute-start(bf16[32,4,16,128]{3,2,1,0:T(8,128)(2,1)S(1)} %get-tuple-element.42), channel_id=1, source_target_pairs={{0,1},{1,2},{2,3},{3,0},{4,5},{5,6},{6,7},{7,4},{8,9},{9,10},{10,1... | collective-permute-start | bytes 1572872 | tf_op jit(solution)/shard_map/ppermute | solution.py:51
  62.3 25.6 %collective-permute-start.4 = (bf16[32,4,16,128]{3,2,1,0:T(8,128)(2,1)S(1)}, bf16[32,4,16,128]{3,2,1,0:T(8,128)(2,1)S(1)}, u32[]{:S(2)}, u32[]{:S(2)}) collective-permute-start(bf16[32,4,16,128]{3,2,1,0:T(8,128)(2,1)S(1)} %get-tuple-element.41), channel_id=1, source_target_pairs={{0,2},{1,3},{2,0},{3,1},{4,6},{5,7},{6,4},{7,5},{8,10},{9,11},{10,... | collective-permute-start | bytes 1572872 | tf_op jit(solution)/shard_map/ppermute | solution.py:51
  65.4 28.8 %collective-permute-start.5 = (bf16[32,4,16,128]{3,2,1,0:T(8,128)(2,1)S(1)}, bf16[32,4,16,128]{3,2,1,0:T(8,128)(2,1)S(1)}, u32[]{:S(2)}, u32[]{:S(2)}) collective-permute-start(bf16[32,4,16,128]{3,2,1,0:T(8,128)(2,1)S(1)} %get-tuple-element.40), channel_id=1, source_target_pairs={{0,3},{1,0},{2,1},{3,2},{4,7},{5,4},{6,5},{7,6},{8,11},{9,8},{10,9... | collective-permute-start | bytes 1572872 | tf_op jit(solution)/shard_map/ppermute | solution.py:51
  74.4 20.8 %collective-permute-start.12 = (bf16[32,1,64,128]{3,2,1,0:T(8,128)(2,1)S(1)}, bf16[32,1,64,128]{3,2,1,0:T(8,128)(2,1)S(1)}, u32[]{:S(2)}, u32[]{:S(2)}) collective-permute-start(bf16[32,1,64,128]{3,2,1,0:T(8,128)(2,1)S(1)} %get-tuple-element.23), channel_id=1, source_target_pairs={{4,0},{8,4},{12,8},{16,12},{20,16},{24,20},{28,24},{5,1},{9,5},{13... | collective-permute-start | bytes 1572872 | tf_op jit(solution)/shard_map/ppermute | solution.py:24
  75.7 26.4 %collective-permute-start.13 = (bf16[32,1,64,128]{3,2,1,0:T(8,128)(2,1)S(1)}, bf16[32,1,64,128]{3,2,1,0:T(8,128)(2,1)S(1)}, u32[]{:S(2)}, u32[]{:S(2)}) collective-permute-start(bf16[32,1,64,128]{3,2,1,0:T(8,128)(2,1)S(1)} %get-tuple-element.24), channel_id=1, source_target_pairs={{0,4},{4,8},{8,12},{12,16},{16,20},{20,24},{24,28},{1,5},{5,9},{9,... | collective-permute-start | bytes 1572872 | tf_op jit(solution)/shard_map/ppermute | solution.py:22
  94.5 7.6 %copy-start.1 = (f32[4,64]{1,0:T(4,128)S(1)}, f32[4,64]{1,0:T(4,128)}, u32[]{:S(2)}) copy-start(f32[4,64]{1,0:T(4,128)} %param.9) | copy-start | bytes 3076
  111.7 18.6 %collective-permute-start.14 = (bf16[1,256,256]{2,1,0:T(8,128)(2,1)S(1)}, bf16[1,256,256]{2,1,0:T(8,128)(2,1)S(1)}, u32[]{:S(2)}, u32[]{:S(2)}) collective-permute-start(bf16[1,256,256]{2,1,0:T(8,128)(2,1)S(1)} %get-tuple-element.43), channel_id=1, source_target_pairs={{0,16},{4,20},{8,24},{12,28},{16,0},{20,4},{24,8},{28,12},{1,17},{... | collective-permute-start | bytes 393224 | tf_op jit(solution)/shard_map/ppermute | solution.py:51
  114.3 17.9 %collective-permute-start.15 = (bf16[1,256,256]{2,1,0:T(8,128)(2,1)S(1)}, bf16[1,256,256]{2,1,0:T(8,128)(2,1)S(1)}, u32[]{:S(2)}, u32[]{:S(2)}) collective-permute-start(bf16[1,256,256]{2,1,0:T(8,128)(2,1)S(1)} %get-tuple-element.49), channel_id=1, source_target_pairs={{0,12},{4,16},{8,20},{12,24},{16,28},{20,0},{24,4},{28,8},{1,13},{... | collective-permute-start | bytes 393224 | tf_op jit(solution)/shard_map/ppermute | solution.py:51
  115.3 19.7 %collective-permute-start.16 = (bf16[1,256,256]{2,1,0:T(8,128)(2,1)S(1)}, bf16[1,256,256]{2,1,0:T(8,128)(2,1)S(1)}, u32[]{:S(2)}, u32[]{:S(2)}) collective-permute-start(bf16[1,256,256]{2,1,0:T(8,128)(2,1)S(1)} %get-tuple-element.48), channel_id=1, source_target_pairs={{0,20},{4,24},{8,28},{12,0},{16,4},{20,8},{24,12},{28,16},{1,21},{... | collective-permute-start | bytes 393224 | tf_op jit(solution)/shard_map/ppermute | solution.py:51
  118.2 16.9 %collective-permute-start.17 = (bf16[1,256,256]{2,1,0:T(8,128)(2,1)S(1)}, bf16[1,256,256]{2,1,0:T(8,128)(2,1)S(1)}, u32[]{:S(2)}, u32[]{:S(2)}) collective-permute-start(bf16[1,256,256]{2,1,0:T(8,128)(2,1)S(1)} %get-tuple-element.47), channel_id=1, source_target_pairs={{0,8},{4,12},{8,16},{12,20},{16,24},{20,28},{24,0},{28,4},{1,9},{5... | collective-permute-start | bytes 393224 | tf_op jit(solution)/shard_map/ppermute | solution.py:51
  118.2 16.9 %collective-permute-start.18 = (bf16[1,256,256]{2,1,0:T(8,128)(2,1)S(1)}, bf16[1,256,256]{2,1,0:T(8,128)(2,1)S(1)}, u32[]{:S(2)}, u32[]{:S(2)}) collective-permute-start(bf16[1,256,256]{2,1,0:T(8,128)(2,1)S(1)} %get-tuple-element.46), channel_id=1, source_target_pairs={{0,24},{4,28},{8,0},{12,4},{16,8},{20,12},{24,16},{28,20},{1,25},{... | collective-permute-start | bytes 393224 | tf_op jit(solution)/shard_map/ppermute | solution.py:51
  130.3 7.8 %collective-permute-start.19 = (bf16[1,256,256]{2,1,0:T(8,128)(2,1)S(1)}, bf16[1,256,256]{2,1,0:T(8,128)(2,1)S(1)}, u32[]{:S(2)}, u32[]{:S(2)}) collective-permute-start(bf16[1,256,256]{2,1,0:T(8,128)(2,1)S(1)} %get-tuple-element.45), channel_id=1, source_target_pairs={{0,4},{4,8},{8,12},{12,16},{16,20},{20,24},{24,28},{28,0},{1,5},{5... | collective-permute-start | bytes 393224 | tf_op jit(solution)/shard_map/ppermute | solution.py:51
  132.2 6.4 %collective-permute-start.20 = (bf16[1,256,256]{2,1,0:T(8,128)(2,1)S(1)}, bf16[1,256,256]{2,1,0:T(8,128)(2,1)S(1)}, u32[]{:S(2)}, u32[]{:S(2)}) collective-permute-start(bf16[1,256,256]{2,1,0:T(8,128)(2,1)S(1)} %get-tuple-element.44), channel_id=1, source_target_pairs={{0,28},{4,0},{8,4},{12,8},{16,12},{20,16},{24,20},{28,24},{1,29},{... | collective-permute-start | bytes 393224 | tf_op jit(solution)/shard_map/ppermute | solution.py:51

commit v21 on v20

--- a/solution.py
+++ b/solution.py
@@ -190,9 +190,9 @@
         modes = dft(table, pieces, weight)
         return modes.reshape(total_angles, axial_cells, band, columns)
 
-    direct_modes = in_source_order(exchange(transform_all(direct_snapshots), "ka", 0), "ka", 2)
+    direct_modes = in_source_order(exchange(transform_all(direct_snapshots), "ka", 0, separate=True), "ka", 2)
     weighted = in_source_order(
-        exchange(transform_all(adjoint_snapshots, lane_weight), "ka", 0), "ka", 2
+        exchange(transform_all(adjoint_snapshots, lane_weight), "ka", 0, separate=True), "ka", 2
     )
     padded = padded_2(direct_modes, (("gx", 1),), 1)
     field_f32 = direct_modes.astype(jnp.float32)
@@ -235,7 +235,7 @@
         jnp.float32
     )
     shares = gram_terms.astype(jnp.bfloat16).reshape(lax.axis_size("gx"), row_count, 2 * columns)
-    own_rows = sum(piece.astype(jnp.float32) for piece in exchange(shares, "gx", 0, True))[0]
+    own_rows = sum(piece.astype(jnp.float32) for piece in exchange(shares, "gx", 0, True, True))[0]
     row_energy = jnp.sum(own_rows[:, :columns] ** 2, axis=1)
     energy = jnp.sum(gather_small(jnp.sum(selector * row_energy[:, None], axis=0), "gx"), axis=0)
     mean_sq = energy / (2.0 * snap_count * snap_count)

time: 153 us -> 152 us (level)
  waiting for transfers between devices: 52.3 us -> 49.3 us
    ppermute x19, waiting for transfers between devices: 45.4 us -> 42.1 us  [exchange(): lax.ppermute(piece, axis, [(j, (j + shift) % count) for j in range(count)])]
    unnamed x18 -> x20, local copies, waits for them, and re-layouts: 18.8 us -> 20.6 us
    another operation x2, local copies, waits for them, and re-layouts: 1.68 us -> 0.09 us  [in_source_order(): stacked = jnp.stack(pieces)]
    dynamic_slice x8 -> x20, local copies, waits for them, and re-layouts: 10.9 us -> 11.1 us  [exchange(): lax.dynamic_slice_in_dim(source, (here + shift) % count * width, width, a...]
where the time goes in v21:
time: 152 us; the launch traced here: 151 us
  waiting for transfers between devices  49.3 us (32%)
  local copies, waits for them, and re-layouts  34.7 us (23%)
  starting transfers between devices  31.9 us (21%)
  other arithmetic  14.5 us (10%)
  blocking collectives  11.7 us (8%)
  Pallas kernels  6.99 us (5%)
    ppermute x19, waiting for transfers between devices, exchange(): lax.ppermute(piece, axis, [(j, (j + shift) % count) for j in range(count)])  42.1 us
    ppermute x19, starting transfers between devices, exchange(): lax.ppermute(piece, axis, [(j, (j + shift) % count) for j in range(count)])  25.8 us
    unnamed x20, local copies, waits for them, and re-layouts  20.6 us
    all_to_all x1, blocking collectives, gather_small(): return lax.all_to_all(copies, axis, split_axis=0, concat_axis=0, tiled=True)  11.7 us
    dynamic_slice x20, local copies, waits for them, and re-layouts, exchange(): lax.dynamic_slice_in_dim(source, (here + shift) % count * width, width, a...  11.1 us
    ppermute x1, waiting for transfers between devices, padded_2(): lax.ppermute(tail, axis, [(i, (i + 1) % count) for i in range(ends)])  7.19 us
    pallas_call x2, Pallas kernels, dft(): pl.pallas_call(functools.partial(dft_kernel, count=count, weighted=weight...  6.99 us
    convert_element_type x1, other arithmetic, local(): image = (-velocity * (forward - behind) * 0.5 + diffusion * (forward + be...  5.9 us
  transfers between devices with their start and end apart: 21, of which 13 were waited for; matrix products, arithmetic and copies ran while one was open for 24% of the time, Pallas kernels for 5%

profile of v21, /device:TPU:0, one launch (start us, length us, event | category | flops | bytes accessed | tf_op | source)
XLA Modules:
  0.0 151.1 jit_solution(9284849659581282913)
XLA Ops:
  0.7 1.2 constant_dynamic-slice_fusion.10
  1.9 2.5 %collective-permute-start.8 = (bf16[32,4,16,128]{3,2,1,0:T(8,128)(2,1)S(1)}, bf16[32,4,16,128]{3,2,1,0:T(8,128)(2,1)S(1)}, u32[]{:S(2)}, u32[]{:S(2)}) collective-permute-start(bf16[32,4,16,128]{3,2,1,0:T(8,128)(2,1)S(1)} %constant_dynamic-slice_fusion.10), channel_id=1, source_target_pairs={{0,3},{1,0},{2,1},{3,2},{4,7},{5,4},{6,5},{7,6},{8,11},{9,8},{10,9... | collective-permute-start | bytes 1572872 | tf_op jit(solution)/shard_map/ppermute | solution.py:51
  4.4 1.9 %constant_dynamic-slice_fusion.11 = bf16[32,4,16,128]{3,2,1,0:T(8,128)(2,1)} fusion(bf16[32,4,64,128]{3,2,1,0:T(8,128)(2,1)} %param.5, s32[]{:T(128)S(6)} %select_n.220), kind=kLoop, calls=%fused_computation.108 | loop fusion | bytes 1048580 | tf_op jit(solution)/shard_map/dynamic_slice | solution.py:49
  6.9 1.9 %constant_dynamic-slice_fusion.12 = bf16[32,4,16,128]{3,2,1,0:T(8,128)(2,1)} fusion(bf16[32,4,64,128]{3,2,1,0:T(8,128)(2,1)} %param.5, s32[]{:T(128)S(6)} %select_n.218), kind=kLoop, calls=%fused_computation.109 | loop fusion | bytes 1048580 | tf_op jit(solution)/shard_map/dynamic_slice | solution.py:49
  9.0 1.9 %constant_dynamic-slice_fusion.18 = bf16[32,4,16,128]{3,2,1,0:T(8,128)(2,1)} fusion(bf16[32,4,64,128]{3,2,1,0:T(8,128)(2,1)} %param.6, s32[]{:T(128)S(6)} %select_n.222), kind=kLoop, calls=%fused_computation.115 | loop fusion | bytes 1048580 | tf_op jit(solution)/shard_map/dynamic_slice | solution.py:49
  10.9 1.6 %collective-permute-start.2 = (bf16[32,4,16,128]{3,2,1,0:T(8,128)(2,1)}, bf16[32,4,16,128]{3,2,1,0:T(8,128)(2,1)}, u32[]{:S(2)}, u32[]{:S(2)}) collective-permute-start(bf16[32,4,16,128]{3,2,1,0:T(8,128)(2,1)} %constant_dynamic-slice_fusion.18), channel_id=1, source_target_pairs={{0,3},{1,0},{2,1},{3,2},{4,7},{5,4},{6,5},{7,6},{8,11},{9,8},{10,9... | collective-permute-start | bytes 1572872 | tf_op jit(solution)/shard_map/ppermute | solution.py:51
  12.4 0.9 constant_dynamic-slice_fusion.19
  13.3 1.4 collective-permute-start.1
  16.1 0.9 constant_dynamic-slice_fusion.20
  18.1 1.3 constant_dynamic-slice_fusion.13
  19.6 1.1 copy.40
  20.7 1.2 copy.44
  22.7 2.2 %copy.37 = bf16[4,8,64,128]{3,1,2,0:T(8,128)(2,1)} copy(bf16[4,8,64,128]{3,2,1,0:T(8,128)(2,1)} %bitcast.111) | data formatting | bytes 1048576
  24.9 2.1 %collective-permute-done.7 = bf16[32,4,16,128]{3,2,1,0:T(8,128)(2,1)} collective-permute-done((bf16[32,4,16,128]{3,2,1,0:T(8,128)(2,1)}, bf16[32,4,16,128]{3,2,1,0:T(8,128)(2,1)}, u32[]{:S(2)}, u32[]{:S(2)}) %collective-permute-start.7) | collective-permute-done | bytes 524320 | tf_op jit(solution)/shard_map/ppermute | solution.py:51
  27.1 2.2 %copy.38 = bf16[4,8,64,128]{3,1,2,0:T(8,128)(2,1)} copy(bf16[4,8,64,128]{3,2,1,0:T(8,128)(2,1)} %bitcast.44) | data formatting | bytes 1048576
  29.3 1.8 %collective-permute-done.6 = bf16[32,4,16,128]{3,2,1,0:T(8,128)(2,1)} collective-permute-done((bf16[32,4,16,128]{3,2,1,0:T(8,128)(2,1)}, bf16[32,4,16,128]{3,2,1,0:T(8,128)(2,1)}, u32[]{:S(2)}, u32[]{:S(2)}) %collective-permute-start.6) | collective-permute-done | bytes 524320 | tf_op jit(solution)/shard_map/ppermute | solution.py:51
  31.0 2.2 %copy.39 = bf16[4,8,64,128]{3,1,2,0:T(8,128)(2,1)} copy(bf16[4,8,64,128]{3,2,1,0:T(8,128)(2,1)} %bitcast.41) | data formatting | bytes 1048576
  33.2 3.4 %shard_map.77 = bf16[128,8192]{1,0:T(8,128)(2,1)} custom-call(bf16[128,256]{1,0:T(8,128)(2,1)} %concatenate.23.refs_0_, bf16[32,8192]{1,0:T(8,128)(2,1)} %bitcast.104, bf16[32,8192]{1,0:T(8,128)(2,1)} %bitcast.110, bf16[32,8192]{1,0:T(8,128)(2,1)} %bitcast.108, bf16[32,8192]{1,0:T(8,128)(2,1)} %bitcast.106), custom_call_target="tpu_custom_call" | custom-call | tf_op jit(solution)/shard_map/pallas_call | solution.py:115
  36.6 2.2 %copy.28 = bf16[16,8,64,128]{3,2,1,0:T(8,128)(2,1)S(1)} copy(bf16[16,8,64,128]{3,1,2,0:T(8,128)(2,1)} %bitcast.84) | data formatting | bytes 4194304
  39.7 1.8 %collective-permute-start.10 = (bf16[32,4,16,128]{3,2,1,0:T(8,128)(2,1)S(1)}, bf16[32,4,16,128]{3,2,1,0:T(8,128)(2,1)}, u32[]{:S(2)}, u32[]{:S(2)}) collective-permute-start(bf16[32,4,16,128]{3,2,1,0:T(8,128)(2,1)S(1)} %constant_dynamic-slice_fusion.8), channel_id=1, source_target_pairs={{0,2},{1,3},{2,0},{3,1},{4,6},{5,7},{6,4},{7,5},{8,10},{9,11},{10,... | collective-permute-start | bytes 1572872 | tf_op jit(solution)/shard_map/ppermute | solution.py:51
  41.6 1.5 collective-permute-start.11
  43.1 2.2 %copy.41 = bf16[4,8,64,128]{3,1,2,0:T(8,128)(2,1)} copy(bf16[4,8,64,128]{3,2,1,0:T(8,128)(2,1)} %bitcast.32) | data formatting | bytes 1048576
  45.3 4.3 %collective-permute-done.1 = bf16[32,4,16,128]{3,2,1,0:T(8,128)(2,1)} collective-permute-done((bf16[32,4,16,128]{3,2,1,0:T(8,128)(2,1)}, bf16[32,4,16,128]{3,2,1,0:T(8,128)(2,1)}, u32[]{:S(2)}, u32[]{:S(2)}) %collective-permute-start.1) | collective-permute-done | bytes 524320 | tf_op jit(solution)/shard_map/ppermute | solution.py:51
  49.5 2.2 %copy.42 = bf16[4,8,64,128]{3,1,2,0:T(8,128)(2,1)} copy(bf16[4,8,64,128]{3,2,1,0:T(8,128)(2,1)} %bitcast.29) | data formatting | bytes 1048576
  51.7 1.8 %collective-permute-done = bf16[32,4,16,128]{3,2,1,0:T(8,128)(2,1)} collective-permute-done((bf16[32,4,16,128]{3,2,1,0:T(8,128)(2,1)}, bf16[32,4,16,128]{3,2,1,0:T(8,128)(2,1)}, u32[]{:S(2)}, u32[]{:S(2)}) %collective-permute-start) | collective-permute-done | bytes 524320 | tf_op jit(solution)/shard_map/ppermute | solution.py:51
  53.5 2.2 %copy.43 = bf16[4,8,64,128]{3,1,2,0:T(8,128)(2,1)} copy(bf16[4,8,64,128]{3,2,1,0:T(8,128)(2,1)} %bitcast.26) | data formatting | bytes 1048576
  56.4 3.6 %shard_map.76 = bf16[128,8192]{1,0:T(8,128)(2,1)} custom-call(bf16[128,256]{1,0:T(8,128)(2,1)} %concatenate.23.refs_0_, bf16[32,8192]{1,0:T(8,128)(2,1)} %bitcast.103, bf16[32,8192]{1,0:T(8,128)(2,1)} %bitcast.109, bf16[32,8192]{1,0:T(8,128)(2,1)} %bitcast.107, bf16[32,8192]{1,0:T(8,128)(2,1)} %bitcast.105, f32[1,8192]{1,0:T(1,128)} %bitcast.115), custom_call_target="tpu_custom_call" | custom-call | tf_op jit(solution)/shard_map/pallas_call | solution.py:115
  60.0 2.2 %copy.23 = bf16[16,8,64,128]{3,2,1,0:T(8,128)(2,1)S(1)} copy(bf16[16,8,64,128]{3,1,2,0:T(8,128)(2,1)} %bitcast.83) | data formatting | bytes 4194304
  62.3 1.8 %collective-permute-start.4 = (bf16[32,4,16,128]{3,2,1,0:T(8,128)(2,1)S(1)}, bf16[32,4,16,128]{3,2,1,0:T(8,128)(2,1)S(1)}, u32[]{:S(2)}, u32[]{:S(2)}) collective-permute-start(bf16[32,4,16,128]{3,2,1,0:T(8,128)(2,1)S(1)} %constant_dynamic-slice_fusion.15), channel_id=1, source_target_pairs={{0,2},{1,3},{2,0},{3,1},{4,6},{5,7},{6,4},{7,5},{8,10},{9,11},{10,... | collective-permute-start | bytes 1572872 | tf_op jit(solution)/shard_map/ppermute | solution.py:51
  64.7 1.0 collective-permute-start.5
  65.8 4.8 %collective-permute-done.11 = bf16[32,4,16,128]{3,2,1,0:T(8,128)(2,1)} collective-permute-done((bf16[32,4,16,128]{3,2,1,0:T(8,128)(2,1)S(1)}, bf16[32,4,16,128]{3,2,1,0:T(8,128)(2,1)}, u32[]{:S(2)}, u32[]{:S(2)}) %collective-permute-start.11) | collective-permute-done | bytes 524320 | tf_op jit(solution)/shard_map/ppermute | solution.py:51
  70.6 1.6 %pad_maximum_fusion.11 = bf16[4,32,4,16,128]{4,3,2,1,0:T(8,128)(2,1)S(1)} fusion(bf16[1,32,4,16,128]{4,3,2,1,0:T(8,128)(2,1)} %bitcast.13, bf16[1,32,4,16,128]{4,3,2,1,0:T(8,128)(2,1)} %bitcast.12, bf16[1,32,4,16,128]{4,3,2,1,0:T(8,128)(2,1)} %bitcast.11, bf16[1,32,4,16,128]{4,3,2,1,0:T(8,128)(2,1)S(1)} %dynamic-slice_bitcast_fusion.4), kind=kLoop, calls=%fused_computation.24 | loop fusion | flops 3145728 | bytes 4194304 | tf_op jit(solution)/shard_map/stack | solution.py:59
  73.5 1.3 collective-permute-start.12
  74.8 4.8 %collective-permute-start.13 = (bf16[32,1,64,128]{3,2,1,0:T(8,128)(2,1)S(1)}, bf16[32,1,64,128]{3,2,1,0:T(8,128)(2,1)S(1)}, u32[]{:S(2)}, u32[]{:S(2)}) collective-permute-start(bf16[32,1,64,128]{3,2,1,0:T(8,128)(2,1)S(1)} %get-tuple-element.56), channel_id=1, source_target_pairs={{0,4},{4,8},{8,12},{12,16},{16,20},{20,24},{24,28},{1,5},{5,9},{9,... | collective-permute-start | bytes 1572872 | tf_op jit(solution)/shard_map/ppermute | solution.py:22
  79.6 7.5 %collective-permute-done.3 = bf16[32,4,16,128]{3,2,1,0:T(8,128)(2,1)S(1)} collective-permute-done((bf16[32,4,16,128]{3,2,1,0:T(8,128)(2,1)S(1)}, bf16[32,4,16,128]{3,2,1,0:T(8,128)(2,1)S(1)}, u32[]{:S(2)}, u32[]{:S(2)}) %collective-permute-start.3) | collective-permute-done | bytes 524320 | tf_op jit(solution)/shard_map/ppermute | solution.py:51
  87.1 6.0 %collective-permute-done.5 = bf16[32,4,16,128]{3,2,1,0:T(8,128)(2,1)S(1)} collective-permute-done((bf16[32,4,16,128]{3,2,1,0:T(8,128)(2,1)S(1)}, bf16[32,4,16,128]{3,2,1,0:T(8,128)(2,1)S(1)}, u32[]{:S(2)}, u32[]{:S(2)}) %collective-permute-start.5) | collective-permute-done | bytes 524320 | tf_op jit(solution)/shard_map/ppermute | solution.py:51
  94.1 7.2 %collective-permute-done.13 = bf16[32,1,64,128]{3,2,1,0:T(8,128)(2,1)S(1)} collective-permute-done((bf16[32,1,64,128]{3,2,1,0:T(8,128)(2,1)S(1)}, bf16[32,1,64,128]{3,2,1,0:T(8,128)(2,1)S(1)}, u32[]{:S(2)}, u32[]{:S(2)}) %collective-permute-start.13) | collective-permute-done | bytes 524320 | tf_op jit(solution)/shard_map/ppermute | solution.py:22
  101.3 5.9 %fusion.6 = bf16[32,4,64,128]{3,2,1,0:T(8,128)(2,1)S(1)} fusion(f32[32,4,64,128]{3,2,1,0:T(8,128)S(1)} %get-tuple-element.58, bf16[32,1,64,128]{3,2,1,0:T(8,128)(2,1)S(1)} %collective-permute-done.13, bf16[32,4,16,128]{3,2,1,0:T(8,128)(2,1)S(1)} %get-tuple-element.60, bf16[32,4,16,128]{3,2,1,0:T(8,128)(2,1)S(1)} %get-tuple-element.61, ...), kind=kLoop, calls=%fused_computation.10 | loop fusion | flops 34603008 | bytes 9447424 | tf_op jit(solution)/shard_map/convert_element_type | solution.py:222
  108.8 1.2 fusion.12
  110.7 2.7 %collective-permute-start.14 = (bf16[1,256,256]{2,1,0:T(8,128)(2,1)S(1)}, bf16[1,256,256]{2,1,0:T(8,128)(2,1)S(1)}, u32[]{:S(2)}, u32[]{:S(2)}) collective-permute-start(bf16[1,256,256]{2,1,0:T(8,128)(2,1)S(1)} %constant_dynamic-slice_fusion.6), channel_id=1, source_target_pairs={{0,16},{4,20},{8,24},{12,28},{16,0},{20,4},{24,8},{28,12},{1,17},{... | collective-permute-start | bytes 393224 | tf_op jit(solution)/shard_map/ppermute | solution.py:51
  113.4 1.0 collective-permute-start.15
  114.4 2.9 %collective-permute-start.16 = (bf16[1,256,256]{2,1,0:T(8,128)(2,1)S(1)}, bf16[1,256,256]{2,1,0:T(8,128)(2,1)S(1)}, u32[]{:S(2)}, u32[]{:S(2)}) collective-permute-start(bf16[1,256,256]{2,1,0:T(8,128)(2,1)S(1)} %constant_dynamic-slice_fusion.4), channel_id=1, source_target_pairs={{0,20},{4,24},{8,28},{12,0},{16,4},{20,8},{24,12},{28,16},{1,21},{... | collective-permute-start | bytes 393224 | tf_op jit(solution)/shard_map/ppermute | solution.py:51
  117.4 3.8 %collective-permute-start.18 = (bf16[1,256,256]{2,1,0:T(8,128)(2,1)S(1)}, bf16[1,256,256]{2,1,0:T(8,128)(2,1)S(1)}, u32[]{:S(2)}, u32[]{:S(2)}) collective-permute-start(bf16[1,256,256]{2,1,0:T(8,128)(2,1)S(1)} %constant_dynamic-slice_fusion.2), channel_id=1, source_target_pairs={{0,24},{4,28},{8,0},{12,4},{16,8},{20,12},{24,16},{28,20},{1,25},{... | collective-permute-start | bytes 393224 | tf_op jit(solution)/shard_map/ppermute | solution.py:51
  121.3 8.0 %collective-permute-done.14 = bf16[1,256,256]{2,1,0:T(8,128)(2,1)S(1)} collective-permute-done((bf16[1,256,256]{2,1,0:T(8,128)(2,1)S(1)}, bf16[1,256,256]{2,1,0:T(8,128)(2,1)S(1)}, u32[]{:S(2)}, u32[]{:S(2)}) %collective-permute-start.14) | collective-permute-done | bytes 131104 | tf_op jit(solution)/shard_map/ppermute | solution.py:51
  129.3 1.9 %collective-permute-done.15 = bf16[1,256,256]{2,1,0:T(8,128)(2,1)S(1)} collective-permute-done((bf16[1,256,256]{2,1,0:T(8,128)(2,1)S(1)}, bf16[1,256,256]{2,1,0:T(8,128)(2,1)S(1)}, u32[]{:S(2)}, u32[]{:S(2)}) %collective-permute-start.15) | collective-permute-done | bytes 131104 | tf_op jit(solution)/shard_map/ppermute | solution.py:51
  131.2 2.8 %collective-permute-start.20 = (bf16[1,256,256]{2,1,0:T(8,128)(2,1)S(1)}, bf16[1,256,256]{2,1,0:T(8,128)(2,1)S(1)}, u32[]{:S(2)}, u32[]{:S(2)}) collective-permute-start(bf16[1,256,256]{2,1,0:T(8,128)(2,1)S(1)} %constant_dynamic-slice_fusion), channel_id=1, source_target_pairs={{0,28},{4,0},{8,4},{12,8},{16,12},{20,16},{24,20},{28,24},{1,29},{... | collective-permute-start | bytes 393224 | tf_op jit(solution)/shard_map/ppermute | solution.py:51
  134.1 3.1 %collective-permute-done.19 = bf16[1,256,256]{2,1,0:T(8,128)(2,1)S(1)} collective-permute-done((bf16[1,256,256]{2,1,0:T(8,128)(2,1)S(1)}, bf16[1,256,256]{2,1,0:T(8,128)(2,1)S(1)}, u32[]{:S(2)}, u32[]{:S(2)}) %collective-permute-start.19) | collective-permute-done | bytes 131104 | tf_op jit(solution)/shard_map/ppermute | solution.py:51
  138.0 11.7 %all_to_all.6 = f32[8,1,32]{2,1,0:T(1,128)S(1)} all-to-all(f32[8,1,32]{2,1,0:T(1,128)S(1)} %broadcast_in_dim.5), channel_id=1, replica_groups=mesh['gx'=8,'ka'=4] {'gx'}, dimensions={0} | all-to-all | bytes 2048 | tf_op jit(solution)/shard_map/all_to_all | solution.py:34
  (80 shorter events, 13.4 us)
Async XLA Ops:
  0.6 11.8 %copy-start = (bf16[32,4,64,128]{3,2,1,0:T(8,128)(2,1)S(1)}, bf16[32,4,64,128]{3,2,1,0:T(8,128)(2,1)}, u32[]{:S(2)}) copy-start(bf16[32,4,64,128]{3,2,1,0:T(8,128)(2,1)} %param.6) | copy-start | bytes 6291460
  0.6 15.4 %copy-start.3 = (f32[4,64]{1,0:T(4,128)S(1)}, f32[4,64]{1,0:T(4,128)}, u32[]{:S(2)}) copy-start(f32[4,64]{1,0:T(4,128)} %param.7) | copy-start | bytes 3076
  1.9 15.4 %collective-permute-start.8 = (bf16[32,4,16,128]{3,2,1,0:T(8,128)(2,1)S(1)}, bf16[32,4,16,128]{3,2,1,0:T(8,128)(2,1)S(1)}, u32[]{:S(2)}, u32[]{:S(2)}) collective-permute-start(bf16[32,4,16,128]{3,2,1,0:T(8,128)(2,1)S(1)} %constant_dynamic-slice_fusion.10), channel_id=1, source_target_pairs={{0,3},{1,0},{2,1},{3,2},{4,7},{5,4},{6,5},{7,6},{8,11},{9,8},{10,9... | collective-permute-start | bytes 1572872 | tf_op jit(solution)/shard_map/ppermute | solution.py:51
  6.3 20.8 %collective-permute-start.7 = (bf16[32,4,16,128]{3,2,1,0:T(8,128)(2,1)}, bf16[32,4,16,128]{3,2,1,0:T(8,128)(2,1)}, u32[]{:S(2)}, u32[]{:S(2)}) collective-permute-start(bf16[32,4,16,128]{3,2,1,0:T(8,128)(2,1)} %constant_dynamic-slice_fusion.11), channel_id=1, source_target_pairs={{0,2},{1,3},{2,0},{3,1},{4,6},{5,7},{6,4},{7,5},{8,10},{9,11},{10,... | collective-permute-start | bytes 1572872 | tf_op jit(solution)/shard_map/ppermute | solution.py:51
  6.9 13.9 %copy-start.4 = (f32[4,64]{1,0:T(4,128)S(1)}, f32[4,64]{1,0:T(4,128)}, u32[]{:S(2)}) copy-start(f32[4,64]{1,0:T(4,128)} %param.8) | copy-start | bytes 3076
  8.8 22.2 %collective-permute-start.6 = (bf16[32,4,16,128]{3,2,1,0:T(8,128)(2,1)}, bf16[32,4,16,128]{3,2,1,0:T(8,128)(2,1)}, u32[]{:S(2)}, u32[]{:S(2)}) collective-permute-start(bf16[32,4,16,128]{3,2,1,0:T(8,128)(2,1)} %constant_dynamic-slice_fusion.12), channel_id=1, source_target_pairs={{0,1},{1,2},{2,3},{3,0},{4,5},{5,6},{6,7},{7,4},{8,9},{9,10},{10,1... | collective-permute-start | bytes 1572872 | tf_op jit(solution)/shard_map/ppermute | solution.py:51
  10.9 30.7 %collective-permute-start.2 = (bf16[32,4,16,128]{3,2,1,0:T(8,128)(2,1)}, bf16[32,4,16,128]{3,2,1,0:T(8,128)(2,1)}, u32[]{:S(2)}, u32[]{:S(2)}) collective-permute-start(bf16[32,4,16,128]{3,2,1,0:T(8,128)(2,1)} %constant_dynamic-slice_fusion.18), channel_id=1, source_target_pairs={{0,3},{1,0},{2,1},{3,2},{4,7},{5,4},{6,5},{7,6},{8,11},{9,8},{10,9... | collective-permute-start | bytes 1572872 | tf_op jit(solution)/shard_map/ppermute | solution.py:51
  13.3 36.2 %collective-permute-start.1 = (bf16[32,4,16,128]{3,2,1,0:T(8,128)(2,1)}, bf16[32,4,16,128]{3,2,1,0:T(8,128)(2,1)}, u32[]{:S(2)}, u32[]{:S(2)}) collective-permute-start(bf16[32,4,16,128]{3,2,1,0:T(8,128)(2,1)} %constant_dynamic-slice_fusion.19), channel_id=1, source_target_pairs={{0,2},{1,3},{2,0},{3,1},{4,6},{5,7},{6,4},{7,5},{8,10},{9,11},{10,... | collective-permute-start | bytes 1572872 | tf_op jit(solution)/shard_map/ppermute | solution.py:51
  17.3 0.8 copy-start.1
  18.1 35.4 %collective-permute-start = (bf16[32,4,16,128]{3,2,1,0:T(8,128)(2,1)}, bf16[32,4,16,128]{3,2,1,0:T(8,128)(2,1)}, u32[]{:S(2)}, u32[]{:S(2)}) collective-permute-start(bf16[32,4,16,128]{3,2,1,0:T(8,128)(2,1)} %constant_dynamic-slice_fusion.20), channel_id=1, source_target_pairs={{0,1},{1,2},{2,3},{3,0},{4,5},{5,6},{6,7},{7,4},{8,9},{9,10},{10,1... | collective-permute-start | bytes 1572872 | tf_op jit(solution)/shard_map/ppermute | solution.py:51
  39.7 25.1 %collective-permute-start.9 = (bf16[32,4,16,128]{3,2,1,0:T(8,128)(2,1)}, bf16[32,4,16,128]{3,2,1,0:T(8,128)(2,1)}, u32[]{:S(2)}, u32[]{:S(2)}) collective-permute-start(bf16[32,4,16,128]{3,2,1,0:T(8,128)(2,1)} %constant_dynamic-slice_fusion.9), channel_id=1, source_target_pairs={{0,1},{1,2},{2,3},{3,0},{4,5},{5,6},{6,7},{7,4},{8,9},{9,10},{10,1... | collective-permute-start | bytes 1572872 | tf_op jit(solution)/shard_map/ppermute | solution.py:51
  39.7 26.1 %collective-permute-start.10 = (bf16[32,4,16,128]{3,2,1,0:T(8,128)(2,1)S(1)}, bf16[32,4,16,128]{3,2,1,0:T(8,128)(2,1)}, u32[]{:S(2)}, u32[]{:S(2)}) collective-permute-start(bf16[32,4,16,128]{3,2,1,0:T(8,128)(2,1)S(1)} %constant_dynamic-slice_fusion.8), channel_id=1, source_target_pairs={{0,2},{1,3},{2,0},{3,1},{4,6},{5,7},{6,4},{7,5},{8,10},{9,11},{10,... | collective-permute-start | bytes 1572872 | tf_op jit(solution)/shard_map/ppermute | solution.py:51
  41.6 29.0 %collective-permute-start.11 = (bf16[32,4,16,128]{3,2,1,0:T(8,128)(2,1)S(1)}, bf16[32,4,16,128]{3,2,1,0:T(8,128)(2,1)}, u32[]{:S(2)}, u32[]{:S(2)}) collective-permute-start(bf16[32,4,16,128]{3,2,1,0:T(8,128)(2,1)S(1)} %constant_dynamic-slice_fusion.7), channel_id=1, source_target_pairs={{0,3},{1,0},{2,1},{3,2},{4,7},{5,4},{6,5},{7,6},{8,11},{9,8},{10,9... | collective-permute-start | bytes 1572872 | tf_op jit(solution)/shard_map/ppermute | solution.py:51
  62.2 24.9 %collective-permute-start.3 = (bf16[32,4,16,128]{3,2,1,0:T(8,128)(2,1)S(1)}, bf16[32,4,16,128]{3,2,1,0:T(8,128)(2,1)S(1)}, u32[]{:S(2)}, u32[]{:S(2)}) collective-permute-start(bf16[32,4,16,128]{3,2,1,0:T(8,128)(2,1)S(1)} %constant_dynamic-slice_fusion.16), channel_id=1, source_target_pairs={{0,1},{1,2},{2,3},{3,0},{4,5},{5,6},{6,7},{7,4},{8,9},{9,10},{10,1... | collective-permute-start | bytes 1572872 | tf_op jit(solution)/shard_map/ppermute | solution.py:51
  62.3 24.8 %collective-permute-start.4 = (bf16[32,4,16,128]{3,2,1,0:T(8,128)(2,1)S(1)}, bf16[32,4,16,128]{3,2,1,0:T(8,128)(2,1)S(1)}, u32[]{:S(2)}, u32[]{:S(2)}) collective-permute-start(bf16[32,4,16,128]{3,2,1,0:T(8,128)(2,1)S(1)} %constant_dynamic-slice_fusion.15), channel_id=1, source_target_pairs={{0,2},{1,3},{2,0},{3,1},{4,6},{5,7},{6,4},{7,5},{8,10},{9,11},{10,... | collective-permute-start | bytes 1572872 | tf_op jit(solution)/shard_map/ppermute | solution.py:51
  64.7 28.3 %collective-permute-start.5 = (bf16[32,4,16,128]{3,2,1,0:T(8,128)(2,1)S(1)}, bf16[32,4,16,128]{3,2,1,0:T(8,128)(2,1)S(1)}, u32[]{:S(2)}, u32[]{:S(2)}) collective-permute-start(bf16[32,4,16,128]{3,2,1,0:T(8,128)(2,1)S(1)} %constant_dynamic-slice_fusion.14), channel_id=1, source_target_pairs={{0,3},{1,0},{2,1},{3,2},{4,7},{5,4},{6,5},{7,6},{8,11},{9,8},{10,9... | collective-permute-start | bytes 1572872 | tf_op jit(solution)/shard_map/ppermute | solution.py:51
  73.5 20.5 %collective-permute-start.12 = (bf16[32,1,64,128]{3,2,1,0:T(8,128)(2,1)S(1)}, bf16[32,1,64,128]{3,2,1,0:T(8,128)(2,1)S(1)}, u32[]{:S(2)}, u32[]{:S(2)}) collective-permute-start(bf16[32,1,64,128]{3,2,1,0:T(8,128)(2,1)S(1)} %get-tuple-element.55), channel_id=1, source_target_pairs={{4,0},{8,4},{12,8},{16,12},{20,16},{24,20},{28,24},{5,1},{9,5},{13... | collective-permute-start | bytes 1572872 | tf_op jit(solution)/shard_map/ppermute | solution.py:24
  74.8 26.4 %collective-permute-start.13 = (bf16[32,1,64,128]{3,2,1,0:T(8,128)(2,1)S(1)}, bf16[32,1,64,128]{3,2,1,0:T(8,128)(2,1)S(1)}, u32[]{:S(2)}, u32[]{:S(2)}) collective-permute-start(bf16[32,1,64,128]{3,2,1,0:T(8,128)(2,1)S(1)} %get-tuple-element.56), channel_id=1, source_target_pairs={{0,4},{4,8},{8,12},{12,16},{16,20},{20,24},{24,28},{1,5},{5,9},{9,... | collective-permute-start | bytes 1572872 | tf_op jit(solution)/shard_map/ppermute | solution.py:22
  93.3 7.9 %copy-start.2 = (f32[4,64]{1,0:T(4,128)S(1)}, f32[4,64]{1,0:T(4,128)}, u32[]{:S(2)}) copy-start(f32[4,64]{1,0:T(4,128)} %param.9) | copy-start | bytes 3076
  110.7 18.6 %collective-permute-start.14 = (bf16[1,256,256]{2,1,0:T(8,128)(2,1)S(1)}, bf16[1,256,256]{2,1,0:T(8,128)(2,1)S(1)}, u32[]{:S(2)}, u32[]{:S(2)}) collective-permute-start(bf16[1,256,256]{2,1,0:T(8,128)(2,1)S(1)} %constant_dynamic-slice_fusion.6), channel_id=1, source_target_pairs={{0,16},{4,20},{8,24},{12,28},{16,0},{20,4},{24,8},{28,12},{1,17},{... | collective-permute-start | bytes 393224 | tf_op jit(solution)/shard_map/ppermute | solution.py:51
  113.4 17.9 %collective-permute-start.15 = (bf16[1,256,256]{2,1,0:T(8,128)(2,1)S(1)}, bf16[1,256,256]{2,1,0:T(8,128)(2,1)S(1)}, u32[]{:S(2)}, u32[]{:S(2)}) collective-permute-start(bf16[1,256,256]{2,1,0:T(8,128)(2,1)S(1)} %constant_dynamic-slice_fusion.5), channel_id=1, source_target_pairs={{0,12},{4,16},{8,20},{12,24},{16,28},{20,0},{24,4},{28,8},{1,13},{... | collective-permute-start | bytes 393224 | tf_op jit(solution)/shard_map/ppermute | solution.py:51
  114.4 19.7 %collective-permute-start.16 = (bf16[1,256,256]{2,1,0:T(8,128)(2,1)S(1)}, bf16[1,256,256]{2,1,0:T(8,128)(2,1)S(1)}, u32[]{:S(2)}, u32[]{:S(2)}) collective-permute-start(bf16[1,256,256]{2,1,0:T(8,128)(2,1)S(1)} %constant_dynamic-slice_fusion.4), channel_id=1, source_target_pairs={{0,20},{4,24},{8,28},{12,0},{16,4},{20,8},{24,12},{28,16},{1,21},{... | collective-permute-start | bytes 393224 | tf_op jit(solution)/shard_map/ppermute | solution.py:51
  117.3 16.7 %collective-permute-start.17 = (bf16[1,256,256]{2,1,0:T(8,128)(2,1)S(1)}, bf16[1,256,256]{2,1,0:T(8,128)(2,1)S(1)}, u32[]{:S(2)}, u32[]{:S(2)}) collective-permute-start(bf16[1,256,256]{2,1,0:T(8,128)(2,1)S(1)} %constant_dynamic-slice_fusion.3), channel_id=1, source_target_pairs={{0,8},{4,12},{8,16},{12,20},{16,24},{20,28},{24,0},{28,4},{1,9},{5... | collective-permute-start | bytes 393224 | tf_op jit(solution)/shard_map/ppermute | solution.py:51
  117.4 16.7 %collective-permute-start.18 = (bf16[1,256,256]{2,1,0:T(8,128)(2,1)S(1)}, bf16[1,256,256]{2,1,0:T(8,128)(2,1)S(1)}, u32[]{:S(2)}, u32[]{:S(2)}) collective-permute-start(bf16[1,256,256]{2,1,0:T(8,128)(2,1)S(1)} %constant_dynamic-slice_fusion.2), channel_id=1, source_target_pairs={{0,24},{4,28},{8,0},{12,4},{16,8},{20,12},{24,16},{28,20},{1,25},{... | collective-permute-start | bytes 393224 | tf_op jit(solution)/shard_map/ppermute | solution.py:51
  129.3 7.8 %collective-permute-start.19 = (bf16[1,256,256]{2,1,0:T(8,128)(2,1)S(1)}, bf16[1,256,256]{2,1,0:T(8,128)(2,1)S(1)}, u32[]{:S(2)}, u32[]{:S(2)}) collective-permute-start(bf16[1,256,256]{2,1,0:T(8,128)(2,1)S(1)} %constant_dynamic-slice_fusion.1), channel_id=1, source_target_pairs={{0,4},{4,8},{8,12},{12,16},{16,20},{20,24},{24,28},{28,0},{1,5},{5... | collective-permute-start | bytes 393224 | tf_op jit(solution)/shard_map/ppermute | solution.py:51
  131.2 6.4 %collective-permute-start.20 = (bf16[1,256,256]{2,1,0:T(8,128)(2,1)S(1)}, bf16[1,256,256]{2,1,0:T(8,128)(2,1)S(1)}, u32[]{:S(2)}, u32[]{:S(2)}) collective-permute-start(bf16[1,256,256]{2,1,0:T(8,128)(2,1)S(1)} %constant_dynamic-slice_fusion), channel_id=1, source_target_pairs={{0,28},{4,0},{8,4},{12,8},{16,12},{20,16},{24,20},{28,24},{1,29},{... | collective-permute-start | bytes 393224 | tf_op jit(solution)/shard_map/ppermute | solution.py:51

commit v22 on v21

--- a/solution.py
+++ b/solution.py
@@ -190,11 +190,22 @@
         modes = dft(table, pieces, weight)
         return modes.reshape(total_angles, axial_cells, band, columns)
 
-    direct_modes = in_source_order(exchange(transform_all(direct_snapshots), "ka", 0, separate=True), "ka", 2)
+    direct_pieces = exchange(transform_all(direct_snapshots), "ka", 0, separate=True)
+    direct_modes = in_source_order(direct_pieces, "ka", 2)
+    head = in_source_order([piece[:, :1] for piece in direct_pieces], "ka", 2)
+    tail = in_source_order([piece[:, -1:] for piece in direct_pieces], "ka", 2)
     weighted = in_source_order(
         exchange(transform_all(adjoint_snapshots, lane_weight), "ka", 0, separate=True), "ka", 2
     )
-    padded = padded_2(direct_modes, (("gx", 1),), 1)
+    axial_count = lax.axis_size("gx")
+    padded = jnp.concatenate(
+        [
+            lax.ppermute(tail, "gx", [(i, i + 1) for i in range(axial_count - 1)]),
+            direct_modes,
+            lax.ppermute(head, "gx", [(i + 1, i) for i in range(axial_count - 1)]),
+        ],
+        axis=1,
+    )
     field_f32 = direct_modes.astype(jnp.float32)
     forward = padded[:, 2:].astype(jnp.float32)
     behind = padded[:, :-2].astype(jnp.float32)

time: 152 us -> 164 us (1.079)
  waiting for transfers between devices: 49.3 us -> 67.7 us
  local copies, waits for them, and re-layouts: 34.7 us -> 32 us
  starting transfers between devices: 31.9 us -> 29.4 us
    ppermute x19, waiting for transfers between devices: 42.1 us -> 63.1 us  [exchange(): lax.ppermute(piece, axis, [(j, (j + shift) % count) for j in range(count)])]
    unnamed x20 -> x18, local copies, waits for them, and re-layouts: 20.6 us -> 17.7 us
    ppermute x2, waiting for transfers between devices: 7.19 us -> 4.63 us  [the longest x1 4.63 us: local(): lax.ppermute(tail, 'gx', [(i, i + 1) for i in range(axial_count - 1)])]
    ppermute x19, starting transfers between devices: 25.8 us -> 23.3 us  [exchange(): lax.ppermute(piece, axis, [(j, (j + shift) % count) for j in range(count)])]
  transfers between devices with their start and end apart: 21 -> 21, of which waited for: 13 -> 14; matrix products, arithmetic and copies ran while one was open for 24% -> 18% of each run, Pallas kernels for 5% -> 2%
where the time goes in v22:
time: 164 us; the launch traced here: 163 us
  waiting for transfers between devices  67.7 us (41%)
  local copies, waits for them, and re-layouts  32 us (20%)
  starting transfers between devices  29.4 us (18%)
  other arithmetic  13.5 us (8%)
  blocking collectives  11.7 us (7%)
  Pallas kernels  7.03 us (4%)
    ppermute x19, waiting for transfers between devices, exchange(): lax.ppermute(piece, axis, [(j, (j + shift) % count) for j in range(count)])  63.1 us
    ppermute x19, starting transfers between devices, exchange(): lax.ppermute(piece, axis, [(j, (j + shift) % count) for j in range(count)])  23.3 us
    unnamed x18, local copies, waits for them, and re-layouts  17.7 us
    all_to_all x1, blocking collectives, gather_small(): return lax.all_to_all(copies, axis, split_axis=0, concat_axis=0, tiled=True)  11.7 us
    dynamic_slice x20, local copies, waits for them, and re-layouts, exchange(): lax.dynamic_slice_in_dim(source, (here + shift) % count * width, width, a...  11.1 us
    pallas_call x2, Pallas kernels, dft(): pl.pallas_call(functools.partial(dft_kernel, count=count, weighted=weight...  7.03 us
    convert_element_type x1, other arithmetic, local(): image = (-velocity * (forward - behind) * 0.5 + diffusion * (forward + be...  5.9 us
    ppermute x1, starting transfers between devices, local(): lax.ppermute(tail, 'gx', [(i, i + 1) for i in range(axial_count - 1)])  4.76 us
  transfers between devices with their start and end apart: 21, of which 14 were waited for; matrix products, arithmetic and copies ran while one was open for 18% of the time, Pallas kernels for 2%

profile of v22, /device:TPU:0, one launch (start us, length us, event | category | flops | bytes accessed | tf_op | source)
XLA Modules:
  0.0 163.2 jit_solution(1652956161138973956)
XLA Ops:
  0.7 2.0 %constant_dynamic-slice_fusion.11 = bf16[32,4,16,128]{3,2,1,0:T(8,128)(2,1)} fusion(bf16[32,4,64,128]{3,2,1,0:T(8,128)(2,1)} %param.5, s32[]{:T(128)S(6)} %select_n.247), kind=kLoop, calls=%fused_computation.129 | loop fusion | bytes 1048580 | tf_op jit(solution)/shard_map/dynamic_slice | solution.py:49
  2.7 2.4 %collective-permute-start.8 = (bf16[32,4,16,128]{3,2,1,0:T(8,128)(2,1)}, bf16[32,4,16,128]{3,2,1,0:T(8,128)(2,1)S(1)}, u32[]{:S(2)}, u32[]{:S(2)}) collective-permute-start(bf16[32,4,16,128]{3,2,1,0:T(8,128)(2,1)} %constant_dynamic-slice_fusion.11), channel_id=1, source_target_pairs={{0,3},{1,0},{2,1},{3,2},{4,7},{5,4},{6,5},{7,6},{8,11},{9,8},{10,9... | collective-permute-start | bytes 1572872 | tf_op jit(solution)/shard_map/ppermute | solution.py:51
  5.1 1.9 %constant_dynamic-slice_fusion.12 = bf16[32,4,16,128]{3,2,1,0:T(8,128)(2,1)} fusion(bf16[32,4,64,128]{3,2,1,0:T(8,128)(2,1)} %param.5, s32[]{:T(128)S(6)} %select_n.245), kind=kLoop, calls=%fused_computation.130 | loop fusion | bytes 1048580 | tf_op jit(solution)/shard_map/dynamic_slice | solution.py:49
  7.6 1.9 %constant_dynamic-slice_fusion.13 = bf16[32,4,16,128]{3,2,1,0:T(8,128)(2,1)} fusion(bf16[32,4,64,128]{3,2,1,0:T(8,128)(2,1)} %param.5, s32[]{:T(128)S(6)} %select_n.243), kind=kLoop, calls=%fused_computation.131 | loop fusion | bytes 1048580 | tf_op jit(solution)/shard_map/dynamic_slice | solution.py:49
  9.7 1.9 %constant_dynamic-slice_fusion.19 = bf16[32,4,16,128]{3,2,1,0:T(8,128)(2,1)} fusion(bf16[32,4,64,128]{3,2,1,0:T(8,128)(2,1)} %param.6, s32[]{:T(128)S(6)} %select_n.247), kind=kLoop, calls=%fused_computation.137 | loop fusion | bytes 1048580 | tf_op jit(solution)/shard_map/dynamic_slice | solution.py:49
  11.6 1.5 collective-permute-start.2
  14.0 1.5 collective-permute-start.1
  15.5 1.3 constant_dynamic-slice_fusion.14
  16.8 1.2 copy.93
  19.3 1.2 copy.97
  21.5 0.9 constant_dynamic-slice_fusion.21
  22.5 1.1 copy.90
  23.7 4.5 %collective-permute-done.7 = bf16[32,4,16,128]{3,2,1,0:T(8,128)(2,1)} collective-permute-done((bf16[32,4,16,128]{3,2,1,0:T(8,128)(2,1)}, bf16[32,4,16,128]{3,2,1,0:T(8,128)(2,1)}, u32[]{:S(2)}, u32[]{:S(2)}) %collective-permute-start.7) | collective-permute-done | bytes 524320 | tf_op jit(solution)/shard_map/ppermute | solution.py:51
  28.2 2.2 %copy.91 = bf16[4,8,64,128]{3,1,2,0:T(8,128)(2,1)} copy(bf16[4,8,64,128]{3,2,1,0:T(8,128)(2,1)} %bitcast.62) | data formatting | bytes 1048576
  30.4 1.4 collective-permute-done.6
  31.8 2.2 %copy.92 = bf16[4,8,64,128]{3,1,2,0:T(8,128)(2,1)} copy(bf16[4,8,64,128]{3,2,1,0:T(8,128)(2,1)} %bitcast.59) | data formatting | bytes 1048576
  34.0 3.4 %shard_map.77 = bf16[128,8192]{1,0:T(8,128)(2,1)} custom-call(bf16[128,256]{1,0:T(8,128)(2,1)} %concatenate.29.refs_0_, bf16[32,8192]{1,0:T(8,128)(2,1)} %bitcast.143, bf16[32,8192]{1,0:T(8,128)(2,1)} %bitcast.150, bf16[32,8192]{1,0:T(8,128)(2,1)} %bitcast.148, bf16[32,8192]{1,0:T(8,128)(2,1)} %bitcast.146), custom_call_target="tpu_custom_call" | custom-call | tf_op jit(solution)/shard_map/pallas_call | solution.py:115
  37.4 2.2 %copy.68 = bf16[16,8,64,128]{3,2,1,0:T(8,128)(2,1)S(1)} copy(bf16[16,8,64,128]{3,1,2,0:T(8,128)(2,1)} %bitcast.128) | data formatting | bytes 4194304
  39.6 2.2 %copy.94 = bf16[4,8,64,128]{3,1,2,0:T(8,128)(2,1)} copy(bf16[4,8,64,128]{3,2,1,0:T(8,128)(2,1)} %bitcast.50) | data formatting | bytes 1048576
  41.8 8.9 %collective-permute-done.1 = bf16[32,4,16,128]{3,2,1,0:T(8,128)(2,1)} collective-permute-done((bf16[32,4,16,128]{3,2,1,0:T(8,128)(2,1)}, bf16[32,4,16,128]{3,2,1,0:T(8,128)(2,1)}, u32[]{:S(2)}, u32[]{:S(2)}) %collective-permute-start.1) | collective-permute-done | bytes 524320 | tf_op jit(solution)/shard_map/ppermute | solution.py:51
  50.7 2.2 %copy.95 = bf16[4,8,64,128]{3,1,2,0:T(8,128)(2,1)} copy(bf16[4,8,64,128]{3,2,1,0:T(8,128)(2,1)} %bitcast.47) | data formatting | bytes 1048576
  52.9 1.1 copy.96
  54.7 3.6 %shard_map.76 = bf16[128,8192]{1,0:T(8,128)(2,1)} custom-call(bf16[128,256]{1,0:T(8,128)(2,1)} %concatenate.29.refs_0_, bf16[32,8192]{1,0:T(8,128)(2,1)} %bitcast.144, bf16[32,8192]{1,0:T(8,128)(2,1)} %bitcast.149, bf16[32,8192]{1,0:T(8,128)(2,1)} %bitcast.147, bf16[32,8192]{1,0:T(8,128)(2,1)} %bitcast.145, f32[1,8192]{1,0:T(1,128)} %bitcast.158), custom_call_target="tpu_custom_call" | custom-call | tf_op jit(solution)/shard_map/pallas_call | solution.py:115
  58.3 2.2 %copy.63 = bf16[16,8,64,128]{3,2,1,0:T(8,128)(2,1)S(1)} copy(bf16[16,8,64,128]{3,1,2,0:T(8,128)(2,1)} %bitcast.127) | data formatting | bytes 4194304
  60.7 1.3 collective-permute-start.10
  61.9 1.5 collective-permute-start.11
  63.7 0.9 collective-permute-start.4
  64.7 9.5 %collective-permute-done.9 = bf16[32,4,16,128]{3,2,0,1:T(8,128)(2,1)S(1)} collective-permute-done((bf16[32,4,16,128]{3,2,0,1:T(8,128)(2,1)S(1)}, bf16[32,4,16,128]{3,2,0,1:T(8,128)(2,1)S(1)}, u32[]{:S(2)}, u32[]{:S(2)}) %collective-permute-start.9) | collective-permute-done | bytes 524320 | tf_op jit(solution)/shard_map/ppermute | solution.py:51
  74.2 1.3 collective-permute-done.10
  75.5 9.9 %collective-permute-done.11 = bf16[32,4,16,128]{3,2,0,1:T(8,128)(2,1)S(1)} collective-permute-done((bf16[32,4,16,128]{3,2,0,1:T(8,128)(2,1)S(1)}, bf16[32,4,16,128]{3,2,0,1:T(8,128)(2,1)S(1)}, u32[]{:S(2)}, u32[]{:S(2)}) %collective-permute-start.11) | collective-permute-done | bytes 524320 | tf_op jit(solution)/shard_map/ppermute | solution.py:51
  85.6 1.3 collective-permute-start.12
  87.1 4.8 %collective-permute-start.13 = (bf16[32,1,64,128]{3,2,1,0:T(8,128)(2,1)S(1)}, bf16[32,1,64,128]{3,2,1,0:T(8,128)(2,1)S(1)}, u32[]{:S(2)}, u32[]{:S(2)}) collective-permute-start(bf16[32,1,64,128]{3,2,1,0:T(8,128)(2,1)S(1)} %pad_maximum_fusion.16), channel_id=1, source_target_pairs={{0,4},{4,8},{8,12},{12,16},{16,20},{20,24},{24,28},{1,5},{5,9},{9,... | collective-permute-start | bytes 1572872 | tf_op jit(solution)/shard_map/ppermute | solution.py:203
  93.0 3.6 %collective-permute-done.3 = bf16[32,4,16,128]{3,2,1,0:T(8,128)(2,1)S(1)} collective-permute-done((bf16[32,4,16,128]{3,2,1,0:T(8,128)(2,1)S(1)}, bf16[32,4,16,128]{3,2,1,0:T(8,128)(2,1)S(1)}, u32[]{:S(2)}, u32[]{:S(2)}) %collective-permute-start.3) | collective-permute-done | bytes 524320 | tf_op jit(solution)/shard_map/ppermute | solution.py:51
  96.6 1.3 collective-permute-done.4
  97.9 9.3 %collective-permute-done.5 = bf16[32,4,16,128]{3,2,1,0:T(8,128)(2,1)S(1)} collective-permute-done((bf16[32,4,16,128]{3,2,1,0:T(8,128)(2,1)S(1)}, bf16[32,4,16,128]{3,2,1,0:T(8,128)(2,1)S(1)}, u32[]{:S(2)}, u32[]{:S(2)}) %collective-permute-start.5) | collective-permute-done | bytes 524320 | tf_op jit(solution)/shard_map/ppermute | solution.py:51
  108.8 4.6 %collective-permute-done.13 = bf16[32,1,64,128]{3,2,1,0:T(8,128)(2,1)S(1)} collective-permute-done((bf16[32,1,64,128]{3,2,1,0:T(8,128)(2,1)S(1)}, bf16[32,1,64,128]{3,2,1,0:T(8,128)(2,1)S(1)}, u32[]{:S(2)}, u32[]{:S(2)}) %collective-permute-start.13) | collective-permute-done | bytes 524320 | tf_op jit(solution)/shard_map/ppermute | solution.py:203
  113.5 5.9 %fusion.6 = bf16[32,4,64,128]{3,2,1,0:T(8,128)(2,1)S(1)} fusion(f32[32,4,64,128]{3,2,1,0:T(8,128)S(1)} %maximum_convert_fusion, bf16[32,1,64,128]{3,2,1,0:T(8,128)(2,1)S(1)} %collective-permute-done.13, bf16[32,4,16,128]{3,2,1,0:T(8,128)(2,1)S(1)} %get-tuple-element.58, bf16[32,4,16,128]{3,2,1,0:T(8,128)(2,1)S(1)} %get-tuple-element.59, ...), kind=kLoop, calls=%fused_computation.10 | loop fusion | flops 34603008 | bytes 9447424 | tf_op jit(solution)/shard_map/convert_element_type | solution.py:233
  121.0 1.2 fusion.12
  122.9 2.7 %collective-permute-start.14 = (bf16[1,256,256]{2,1,0:T(8,128)(2,1)S(1)}, bf16[1,256,256]{2,1,0:T(8,128)(2,1)S(1)}, u32[]{:S(2)}, u32[]{:S(2)}) collective-permute-start(bf16[1,256,256]{2,1,0:T(8,128)(2,1)S(1)} %constant_dynamic-slice_fusion.6), channel_id=1, source_target_pairs={{0,16},{4,20},{8,24},{12,28},{16,0},{20,4},{24,8},{28,12},{1,17},{... | collective-permute-start | bytes 393224 | tf_op jit(solution)/shard_map/ppermute | solution.py:51
  125.5 1.0 collective-permute-start.15
  126.5 2.9 %collective-permute-start.16 = (bf16[1,256,256]{2,1,0:T(8,128)(2,1)S(1)}, bf16[1,256,256]{2,1,0:T(8,128)(2,1)S(1)}, u32[]{:S(2)}, u32[]{:S(2)}) collective-permute-start(bf16[1,256,256]{2,1,0:T(8,128)(2,1)S(1)} %constant_dynamic-slice_fusion.4), channel_id=1, source_target_pairs={{0,20},{4,24},{8,28},{12,0},{16,4},{20,8},{24,12},{28,16},{1,21},{... | collective-permute-start | bytes 393224 | tf_op jit(solution)/shard_map/ppermute | solution.py:51
  129.5 1.5 collective-permute-start.17
  131.0 2.4 %collective-permute-start.18 = (bf16[1,256,256]{2,1,0:T(8,128)(2,1)S(1)}, bf16[1,256,256]{2,1,0:T(8,128)(2,1)S(1)}, u32[]{:S(2)}, u32[]{:S(2)}) collective-permute-start(bf16[1,256,256]{2,1,0:T(8,128)(2,1)S(1)} %constant_dynamic-slice_fusion.2), channel_id=1, source_target_pairs={{0,24},{4,28},{8,0},{12,4},{16,8},{20,12},{24,16},{28,20},{1,25},{... | collective-permute-start | bytes 393224 | tf_op jit(solution)/shard_map/ppermute | solution.py:51
  133.5 8.0 %collective-permute-done.14 = bf16[1,256,256]{2,1,0:T(8,128)(2,1)S(1)} collective-permute-done((bf16[1,256,256]{2,1,0:T(8,128)(2,1)S(1)}, bf16[1,256,256]{2,1,0:T(8,128)(2,1)S(1)}, u32[]{:S(2)}, u32[]{:S(2)}) %collective-permute-start.14) | collective-permute-done | bytes 131104 | tf_op jit(solution)/shard_map/ppermute | solution.py:51
  141.5 1.9 %collective-permute-done.15 = bf16[1,256,256]{2,1,0:T(8,128)(2,1)S(1)} collective-permute-done((bf16[1,256,256]{2,1,0:T(8,128)(2,1)S(1)}, bf16[1,256,256]{2,1,0:T(8,128)(2,1)S(1)}, u32[]{:S(2)}, u32[]{:S(2)}) %collective-permute-start.15) | collective-permute-done | bytes 131104 | tf_op jit(solution)/shard_map/ppermute | solution.py:51
  143.4 2.9 %collective-permute-start.20 = (bf16[1,256,256]{2,1,0:T(8,128)(2,1)S(1)}, bf16[1,256,256]{2,1,0:T(8,128)(2,1)S(1)}, u32[]{:S(2)}, u32[]{:S(2)}) collective-permute-start(bf16[1,256,256]{2,1,0:T(8,128)(2,1)S(1)} %constant_dynamic-slice_fusion), channel_id=1, source_target_pairs={{0,28},{4,0},{8,4},{12,8},{16,12},{20,16},{24,20},{28,24},{1,29},{... | collective-permute-start | bytes 393224 | tf_op jit(solution)/shard_map/ppermute | solution.py:51
  146.3 3.1 %collective-permute-done.19 = bf16[1,256,256]{2,1,0:T(8,128)(2,1)S(1)} collective-permute-done((bf16[1,256,256]{2,1,0:T(8,128)(2,1)S(1)}, bf16[1,256,256]{2,1,0:T(8,128)(2,1)S(1)}, u32[]{:S(2)}, u32[]{:S(2)}) %collective-permute-start.19) | collective-permute-done | bytes 131104 | tf_op jit(solution)/shard_map/ppermute | solution.py:51
  150.1 11.7 %all_to_all.6 = f32[8,1,32]{2,1,0:T(1,128)S(1)} all-to-all(f32[8,1,32]{2,1,0:T(1,128)S(1)} %broadcast_in_dim.5), channel_id=1, replica_groups=mesh['gx'=8,'ka'=4] {'gx'}, dimensions={0} | all-to-all | bytes 2048 | tf_op jit(solution)/shard_map/all_to_all | solution.py:34
  (88 shorter events, 13.0 us)
Async XLA Ops:
  0.6 12.5 %copy-start = (bf16[32,4,64,128]{3,2,1,0:T(8,128)(2,1)S(1)}, bf16[32,4,64,128]{3,2,1,0:T(8,128)(2,1)}, u32[]{:S(2)}) copy-start(bf16[32,4,64,128]{3,2,1,0:T(8,128)(2,1)} %param.6) | copy-start | bytes 6291460
  2.7 19.6 %collective-permute-start.8 = (bf16[32,4,16,128]{3,2,1,0:T(8,128)(2,1)}, bf16[32,4,16,128]{3,2,1,0:T(8,128)(2,1)S(1)}, u32[]{:S(2)}, u32[]{:S(2)}) collective-permute-start(bf16[32,4,16,128]{3,2,1,0:T(8,128)(2,1)} %constant_dynamic-slice_fusion.11), channel_id=1, source_target_pairs={{0,3},{1,0},{2,1},{3,2},{4,7},{5,4},{6,5},{7,6},{8,11},{9,8},{10,9... | collective-permute-start | bytes 1572872 | tf_op jit(solution)/shard_map/ppermute | solution.py:51
  5.1 14.1 %copy-start.2 = (f32[4,64]{1,0:T(4,128)S(1)}, f32[4,64]{1,0:T(4,128)}, u32[]{:S(2)}) copy-start(f32[4,64]{1,0:T(4,128)} %param.8) | copy-start | bytes 3076
  7.0 21.2 %collective-permute-start.7 = (bf16[32,4,16,128]{3,2,1,0:T(8,128)(2,1)}, bf16[32,4,16,128]{3,2,1,0:T(8,128)(2,1)}, u32[]{:S(2)}, u32[]{:S(2)}) collective-permute-start(bf16[32,4,16,128]{3,2,1,0:T(8,128)(2,1)} %constant_dynamic-slice_fusion.12), channel_id=1, source_target_pairs={{0,2},{1,3},{2,0},{3,1},{4,6},{5,7},{6,4},{7,5},{8,10},{9,11},{10,... | collective-permute-start | bytes 1572872 | tf_op jit(solution)/shard_map/ppermute | solution.py:51
  9.5 22.3 %collective-permute-start.6 = (bf16[32,4,16,128]{3,2,1,0:T(8,128)(2,1)}, bf16[32,4,16,128]{3,2,1,0:T(8,128)(2,1)}, u32[]{:S(2)}, u32[]{:S(2)}) collective-permute-start(bf16[32,4,16,128]{3,2,1,0:T(8,128)(2,1)} %constant_dynamic-slice_fusion.13), channel_id=1, source_target_pairs={{0,1},{1,2},{2,3},{3,0},{4,5},{5,6},{6,7},{7,4},{8,9},{9,10},{10,1... | collective-permute-start | bytes 1572872 | tf_op jit(solution)/shard_map/ppermute | solution.py:51
  11.6 10.7 %copy-start.3 = (f32[4,64]{1,0:T(4,128)S(1)}, f32[4,64]{1,0:T(4,128)}, u32[]{:S(2)}) copy-start(f32[4,64]{1,0:T(4,128)} %param.7) | copy-start | bytes 3076
  11.6 28.0 %collective-permute-start.2 = (bf16[32,4,16,128]{3,2,1,0:T(8,128)(2,1)}, bf16[32,4,16,128]{3,2,1,0:T(8,128)(2,1)}, u32[]{:S(2)}, u32[]{:S(2)}) collective-permute-start(bf16[32,4,16,128]{3,2,1,0:T(8,128)(2,1)} %constant_dynamic-slice_fusion.19), channel_id=1, source_target_pairs={{0,3},{1,0},{2,1},{3,2},{4,7},{5,4},{6,5},{7,6},{8,11},{9,8},{10,9... | collective-permute-start | bytes 1572872 | tf_op jit(solution)/shard_map/ppermute | solution.py:51
  14.0 36.7 %collective-permute-start.1 = (bf16[32,4,16,128]{3,2,1,0:T(8,128)(2,1)}, bf16[32,4,16,128]{3,2,1,0:T(8,128)(2,1)}, u32[]{:S(2)}, u32[]{:S(2)}) collective-permute-start(bf16[32,4,16,128]{3,2,1,0:T(8,128)(2,1)} %constant_dynamic-slice_fusion.20), channel_id=1, source_target_pairs={{0,2},{1,3},{2,0},{3,1},{4,6},{5,7},{6,4},{7,5},{8,10},{9,11},{10,... | collective-permute-start | bytes 1572872 | tf_op jit(solution)/shard_map/ppermute | solution.py:51
  22.3 30.5 %collective-permute-start = (bf16[32,4,16,128]{3,2,1,0:T(8,128)(2,1)}, bf16[32,4,16,128]{3,2,1,0:T(8,128)(2,1)S(1)}, u32[]{:S(2)}, u32[]{:S(2)}) collective-permute-start(bf16[32,4,16,128]{3,2,1,0:T(8,128)(2,1)} %constant_dynamic-slice_fusion.21), channel_id=1, source_target_pairs={{0,1},{1,2},{2,3},{3,0},{4,5},{5,6},{6,7},{7,4},{8,9},{9,10},{10,1... | collective-permute-start | bytes 1572872 | tf_op jit(solution)/shard_map/ppermute | solution.py:51
  60.5 13.6 %collective-permute-start.9 = (bf16[32,4,16,128]{3,2,0,1:T(8,128)(2,1)S(1)}, bf16[32,4,16,128]{3,2,0,1:T(8,128)(2,1)S(1)}, u32[]{:S(2)}, u32[]{:S(2)}) collective-permute-start(bf16[32,4,16,128]{3,2,0,1:T(8,128)(2,1)S(1)} %constant_dynamic-slice_fusion.9), channel_id=1, source_target_pairs={{0,1},{1,2},{2,3},{3,0},{4,5},{5,6},{6,7},{7,4},{8,9},{9,10},{10,1... | collective-permute-start | bytes 1572872 | tf_op jit(solution)/shard_map/ppermute | solution.py:51
  60.7 14.8 %collective-permute-start.10 = (bf16[32,4,16,128]{3,2,1,0:T(8,128)(2,1)S(1)}, bf16[32,4,16,128]{3,2,1,0:T(8,128)(2,1)S(1)}, u32[]{:S(2)}, u32[]{:S(2)}) collective-permute-start(bf16[32,4,16,128]{3,2,1,0:T(8,128)(2,1)S(1)} %constant_dynamic-slice_fusion.8), channel_id=1, source_target_pairs={{0,2},{1,3},{2,0},{3,1},{4,6},{5,7},{6,4},{7,5},{8,10},{9,11},{10,... | collective-permute-start | bytes 1572872 | tf_op jit(solution)/shard_map/ppermute | solution.py:51
  61.9 23.5 %collective-permute-start.11 = (bf16[32,4,16,128]{3,2,0,1:T(8,128)(2,1)S(1)}, bf16[32,4,16,128]{3,2,0,1:T(8,128)(2,1)S(1)}, u32[]{:S(2)}, u32[]{:S(2)}) collective-permute-start(bf16[32,4,16,128]{3,2,0,1:T(8,128)(2,1)S(1)} %constant_dynamic-slice_fusion.7), channel_id=1, source_target_pairs={{0,3},{1,0},{2,1},{3,2},{4,7},{5,4},{6,5},{7,6},{8,11},{9,8},{10,9... | collective-permute-start | bytes 1572872 | tf_op jit(solution)/shard_map/ppermute | solution.py:51
  63.5 33.1 %collective-permute-start.3 = (bf16[32,4,16,128]{3,2,1,0:T(8,128)(2,1)S(1)}, bf16[32,4,16,128]{3,2,1,0:T(8,128)(2,1)S(1)}, u32[]{:S(2)}, u32[]{:S(2)}) collective-permute-start(bf16[32,4,16,128]{3,2,1,0:T(8,128)(2,1)S(1)} %constant_dynamic-slice_fusion.17), channel_id=1, source_target_pairs={{0,1},{1,2},{2,3},{3,0},{4,5},{5,6},{6,7},{7,4},{8,9},{9,10},{10,1... | collective-permute-start | bytes 1572872 | tf_op jit(solution)/shard_map/ppermute | solution.py:51
  63.7 34.2 %collective-permute-start.4 = (bf16[32,4,16,128]{3,2,1,0:T(8,128)(2,1)S(1)}, bf16[32,4,16,128]{3,2,1,0:T(8,128)(2,1)S(1)}, u32[]{:S(2)}, u32[]{:S(2)}) collective-permute-start(bf16[32,4,16,128]{3,2,1,0:T(8,128)(2,1)S(1)} %constant_dynamic-slice_fusion.16), channel_id=1, source_target_pairs={{0,2},{1,3},{2,0},{3,1},{4,6},{5,7},{6,4},{7,5},{8,10},{9,11},{10,... | collective-permute-start | bytes 1572872 | tf_op jit(solution)/shard_map/ppermute | solution.py:51
  74.1 33.1 %collective-permute-start.5 = (bf16[32,4,16,128]{3,2,1,0:T(8,128)(2,1)S(1)}, bf16[32,4,16,128]{3,2,1,0:T(8,128)(2,1)S(1)}, u32[]{:S(2)}, u32[]{:S(2)}) collective-permute-start(bf16[32,4,16,128]{3,2,1,0:T(8,128)(2,1)S(1)} %constant_dynamic-slice_fusion.15), channel_id=1, source_target_pairs={{0,3},{1,0},{2,1},{3,2},{4,7},{5,4},{6,5},{7,6},{8,11},{9,8},{10,9... | collective-permute-start | bytes 1572872 | tf_op jit(solution)/shard_map/ppermute | solution.py:51
  85.6 23.2 %collective-permute-start.12 = (bf16[32,1,64,128]{3,2,1,0:T(8,128)(2,1)S(1)}, bf16[32,1,64,128]{3,2,1,0:T(8,128)(2,1)S(1)}, u32[]{:S(2)}, u32[]{:S(2)}) collective-permute-start(bf16[32,1,64,128]{3,2,1,0:T(8,128)(2,1)S(1)} %pad_maximum_fusion.14), channel_id=1, source_target_pairs={{4,0},{8,4},{12,8},{16,12},{20,16},{24,20},{28,24},{5,1},{9,5},{13... | collective-permute-start | bytes 1572872 | tf_op jit(solution)/shard_map/ppermute | solution.py:205
  87.1 26.3 %collective-permute-start.13 = (bf16[32,1,64,128]{3,2,1,0:T(8,128)(2,1)S(1)}, bf16[32,1,64,128]{3,2,1,0:T(8,128)(2,1)S(1)}, u32[]{:S(2)}, u32[]{:S(2)}) collective-permute-start(bf16[32,1,64,128]{3,2,1,0:T(8,128)(2,1)S(1)} %pad_maximum_fusion.16), channel_id=1, source_target_pairs={{0,4},{4,8},{8,12},{12,16},{16,20},{20,24},{24,28},{1,5},{5,9},{9,... | collective-permute-start | bytes 1572872 | tf_op jit(solution)/shard_map/ppermute | solution.py:203
  108.2 5.2 %copy-start.1 = (f32[4,64]{1,0:T(4,128)S(1)}, f32[4,64]{1,0:T(4,128)}, u32[]{:S(2)}) copy-start(f32[4,64]{1,0:T(4,128)} %param.9) | copy-start | bytes 3076
  122.9 18.6 %collective-permute-start.14 = (bf16[1,256,256]{2,1,0:T(8,128)(2,1)S(1)}, bf16[1,256,256]{2,1,0:T(8,128)(2,1)S(1)}, u32[]{:S(2)}, u32[]{:S(2)}) collective-permute-start(bf16[1,256,256]{2,1,0:T(8,128)(2,1)S(1)} %constant_dynamic-slice_fusion.6), channel_id=1, source_target_pairs={{0,16},{4,20},{8,24},{12,28},{16,0},{20,4},{24,8},{28,12},{1,17},{... | collective-permute-start | bytes 393224 | tf_op jit(solution)/shard_map/ppermute | solution.py:51
  125.5 17.8 %collective-permute-start.15 = (bf16[1,256,256]{2,1,0:T(8,128)(2,1)S(1)}, bf16[1,256,256]{2,1,0:T(8,128)(2,1)S(1)}, u32[]{:S(2)}, u32[]{:S(2)}) collective-permute-start(bf16[1,256,256]{2,1,0:T(8,128)(2,1)S(1)} %constant_dynamic-slice_fusion.5), channel_id=1, source_target_pairs={{0,12},{4,16},{8,20},{12,24},{16,28},{20,0},{24,4},{28,8},{1,13},{... | collective-permute-start | bytes 393224 | tf_op jit(solution)/shard_map/ppermute | solution.py:51
  126.5 19.7 %collective-permute-start.16 = (bf16[1,256,256]{2,1,0:T(8,128)(2,1)S(1)}, bf16[1,256,256]{2,1,0:T(8,128)(2,1)S(1)}, u32[]{:S(2)}, u32[]{:S(2)}) collective-permute-start(bf16[1,256,256]{2,1,0:T(8,128)(2,1)S(1)} %constant_dynamic-slice_fusion.4), channel_id=1, source_target_pairs={{0,20},{4,24},{8,28},{12,0},{16,4},{20,8},{24,12},{28,16},{1,21},{... | collective-permute-start | bytes 393224 | tf_op jit(solution)/shard_map/ppermute | solution.py:51
  129.5 16.8 %collective-permute-start.17 = (bf16[1,256,256]{2,1,0:T(8,128)(2,1)S(1)}, bf16[1,256,256]{2,1,0:T(8,128)(2,1)S(1)}, u32[]{:S(2)}, u32[]{:S(2)}) collective-permute-start(bf16[1,256,256]{2,1,0:T(8,128)(2,1)S(1)} %constant_dynamic-slice_fusion.3), channel_id=1, source_target_pairs={{0,8},{4,12},{8,16},{12,20},{16,24},{20,28},{24,0},{28,4},{1,9},{5... | collective-permute-start | bytes 393224 | tf_op jit(solution)/shard_map/ppermute | solution.py:51
  131.0 15.3 %collective-permute-start.18 = (bf16[1,256,256]{2,1,0:T(8,128)(2,1)S(1)}, bf16[1,256,256]{2,1,0:T(8,128)(2,1)S(1)}, u32[]{:S(2)}, u32[]{:S(2)}) collective-permute-start(bf16[1,256,256]{2,1,0:T(8,128)(2,1)S(1)} %constant_dynamic-slice_fusion.2), channel_id=1, source_target_pairs={{0,24},{4,28},{8,0},{12,4},{16,8},{20,12},{24,16},{28,20},{1,25},{... | collective-permute-start | bytes 393224 | tf_op jit(solution)/shard_map/ppermute | solution.py:51
  141.5 7.8 %collective-permute-start.19 = (bf16[1,256,256]{2,1,0:T(8,128)(2,1)S(1)}, bf16[1,256,256]{2,1,0:T(8,128)(2,1)S(1)}, u32[]{:S(2)}, u32[]{:S(2)}) collective-permute-start(bf16[1,256,256]{2,1,0:T(8,128)(2,1)S(1)} %constant_dynamic-slice_fusion.1), channel_id=1, source_target_pairs={{0,4},{4,8},{8,12},{12,16},{16,20},{20,24},{24,28},{28,0},{1,5},{5... | collective-permute-start | bytes 393224 | tf_op jit(solution)/shard_map/ppermute | solution.py:51
  143.4 6.4 %collective-permute-start.20 = (bf16[1,256,256]{2,1,0:T(8,128)(2,1)S(1)}, bf16[1,256,256]{2,1,0:T(8,128)(2,1)S(1)}, u32[]{:S(2)}, u32[]{:S(2)}) collective-permute-start(bf16[1,256,256]{2,1,0:T(8,128)(2,1)S(1)} %constant_dynamic-slice_fusion), channel_id=1, source_target_pairs={{0,28},{4,0},{8,4},{12,8},{16,12},{20,16},{24,20},{28,24},{1,29},{... | collective-permute-start | bytes 393224 | tf_op jit(solution)/shard_map/ppermute | solution.py:51

commit v23 on v21

--- a/solution.py
+++ b/solution.py
@@ -41,7 +41,7 @@
     shifts = list(range(count))
     if far_first:
         shifts = [0] + sorted(range(1, count), key=lambda shift: -min(shift, count - shift))
-    pieces = []
+    pieces = [None] * count
     for shift in shifts:
         source = cells
         if separate:
@@ -49,7 +49,7 @@
         piece = lax.dynamic_slice_in_dim(source, ((here + shift) % count) * width, width, axis=split_axis)
         if shift:
             piece = lax.ppermute(piece, axis, [(j, (j + shift) % count) for j in range(count)])
-        pieces.append(piece)
+        pieces[shift] = piece
     return pieces
 
 
@@ -186,7 +186,7 @@
     lane_weight = jnp.broadcast_to(band_weight[:, :, None], (axial_cells, band, columns)).reshape(1, lanes)
 
     def transform_all(snapshots, weight=None):
-        pieces = [piece.reshape(local_angles, lanes) for piece in exchange(snapshots, "ka", 2, separate=True)]
+        pieces = [piece.reshape(local_angles, lanes) for piece in exchange(snapshots, "ka", 2, True, True)]
         modes = dft(table, pieces, weight)
         return modes.reshape(total_angles, axial_cells, band, columns)
 

time: 152 us -> 153 us (level)
  blocking collectives: 11.7 us -> 18.4 us
  waiting for transfers between devices: 49.3 us -> 44 us
    all_to_all x1, blocking collectives: 11.7 us -> 18.4 us  [gather_small(): return lax.all_to_all(copies, axis, split_axis=0, concat_axis=0, tiled=True)]
    ppermute x19, waiting for transfers between devices: 42.1 us -> 36.8 us  [exchange(): lax.ppermute(piece, axis, [(j, (j + shift) % count) for j in range(count)])]
  transfers between devices with their start and end apart: 21 -> 21, of which waited for: 13 -> 12; matrix products, arithmetic and copies ran while one was open for 24% -> 24% of each run, Pallas kernels for 5% -> 5%
where the time goes in v23:
time: 153 us; the launch traced here: 152 us
  waiting for transfers between devices  44 us (29%)
  local copies, waits for them, and re-layouts  34.7 us (23%)
  starting transfers between devices  31.3 us (20%)
  blocking collectives  18.4 us (12%)
  other arithmetic  14.5 us (9%)
  Pallas kernels  6.99 us (5%)
    ppermute x19, waiting for transfers between devices, exchange(): lax.ppermute(piece, axis, [(j, (j + shift) % count) for j in range(count)])  36.8 us
    ppermute x19, starting transfers between devices, exchange(): lax.ppermute(piece, axis, [(j, (j + shift) % count) for j in range(count)])  25.3 us
    unnamed x20, local copies, waits for them, and re-layouts  20.6 us
    all_to_all x1, blocking collectives, gather_small(): return lax.all_to_all(copies, axis, split_axis=0, concat_axis=0, tiled=True)  18.4 us
    dynamic_slice x20, local copies, waits for them, and re-layouts, exchange(): lax.dynamic_slice_in_dim(source, (here + shift) % count * width, width, a...  11.1 us
    ppermute x1, waiting for transfers between devices, padded_2(): lax.ppermute(tail, axis, [(i, (i + 1) % count) for i in range(ends)])  7.19 us
    pallas_call x2, Pallas kernels, dft(): pl.pallas_call(functools.partial(dft_kernel, count=count, weighted=weight...  6.99 us
    convert_element_type x1, other arithmetic, local(): image = (-velocity * (forward - behind) * 0.5 + diffusion * (forward + be...  5.9 us
  transfers between devices with their start and end apart: 21, of which 12 were waited for; matrix products, arithmetic and copies ran while one was open for 24% of the time, Pallas kernels for 5%

profile of v23, /device:TPU:0, one launch (start us, length us, event | category | flops | bytes accessed | tf_op | source)
XLA Modules:
  0.0 152.0 jit_solution(10338970858746144982)
XLA Ops:
  0.7 1.2 constant_dynamic-slice_fusion.10
  1.9 2.5 %collective-permute-start.8 = (bf16[32,4,16,128]{3,2,1,0:T(8,128)(2,1)S(1)}, bf16[32,4,16,128]{3,2,1,0:T(8,128)(2,1)S(1)}, u32[]{:S(2)}, u32[]{:S(2)}) collective-permute-start(bf16[32,4,16,128]{3,2,1,0:T(8,128)(2,1)S(1)} %constant_dynamic-slice_fusion.10), channel_id=1, source_target_pairs={{0,3},{1,0},{2,1},{3,2},{4,7},{5,4},{6,5},{7,6},{8,11},{9,8},{10,9... | collective-permute-start | bytes 1572872 | tf_op jit(solution)/shard_map/ppermute | solution.py:51
  4.4 1.9 %constant_dynamic-slice_fusion.11 = bf16[32,4,16,128]{3,2,1,0:T(8,128)(2,1)} fusion(bf16[32,4,64,128]{3,2,1,0:T(8,128)(2,1)} %param.5, s32[]{:T(128)S(6)} %select_n.220), kind=kLoop, calls=%fused_computation.108 | loop fusion | bytes 1048580 | tf_op jit(solution)/shard_map/dynamic_slice | solution.py:49
  6.9 1.9 %constant_dynamic-slice_fusion.12 = bf16[32,4,16,128]{3,2,1,0:T(8,128)(2,1)} fusion(bf16[32,4,64,128]{3,2,1,0:T(8,128)(2,1)} %param.5, s32[]{:T(128)S(6)} %select_n.218), kind=kLoop, calls=%fused_computation.109 | loop fusion | bytes 1048580 | tf_op jit(solution)/shard_map/dynamic_slice | solution.py:49
  9.0 1.9 %constant_dynamic-slice_fusion.18 = bf16[32,4,16,128]{3,2,1,0:T(8,128)(2,1)} fusion(bf16[32,4,64,128]{3,2,1,0:T(8,128)(2,1)} %param.6, s32[]{:T(128)S(6)} %select_n.222), kind=kLoop, calls=%fused_computation.115 | loop fusion | bytes 1048580 | tf_op jit(solution)/shard_map/dynamic_slice | solution.py:49
  10.9 1.6 %collective-permute-start.2 = (bf16[32,4,16,128]{3,2,1,0:T(8,128)(2,1)}, bf16[32,4,16,128]{3,2,1,0:T(8,128)(2,1)}, u32[]{:S(2)}, u32[]{:S(2)}) collective-permute-start(bf16[32,4,16,128]{3,2,1,0:T(8,128)(2,1)} %constant_dynamic-slice_fusion.18), channel_id=1, source_target_pairs={{0,3},{1,0},{2,1},{3,2},{4,7},{5,4},{6,5},{7,6},{8,11},{9,8},{10,9... | collective-permute-start | bytes 1572872 | tf_op jit(solution)/shard_map/ppermute | solution.py:51
  12.4 0.9 constant_dynamic-slice_fusion.19
  13.3 1.4 collective-permute-start.1
  16.1 0.9 constant_dynamic-slice_fusion.20
  18.1 1.3 constant_dynamic-slice_fusion.13
  19.6 1.1 copy.40
  20.7 1.2 copy.44
  22.7 2.2 %copy.37 = bf16[4,8,64,128]{3,1,2,0:T(8,128)(2,1)} copy(bf16[4,8,64,128]{3,2,1,0:T(8,128)(2,1)} %bitcast.111) | data formatting | bytes 1048576
  24.9 2.1 %collective-permute-done.7 = bf16[32,4,16,128]{3,2,1,0:T(8,128)(2,1)} collective-permute-done((bf16[32,4,16,128]{3,2,1,0:T(8,128)(2,1)}, bf16[32,4,16,128]{3,2,1,0:T(8,128)(2,1)}, u32[]{:S(2)}, u32[]{:S(2)}) %collective-permute-start.7) | collective-permute-done | bytes 524320 | tf_op jit(solution)/shard_map/ppermute | solution.py:51
  27.1 2.2 %copy.38 = bf16[4,8,64,128]{3,1,2,0:T(8,128)(2,1)} copy(bf16[4,8,64,128]{3,2,1,0:T(8,128)(2,1)} %bitcast.44) | data formatting | bytes 1048576
  29.3 1.8 %collective-permute-done.6 = bf16[32,4,16,128]{3,2,1,0:T(8,128)(2,1)} collective-permute-done((bf16[32,4,16,128]{3,2,1,0:T(8,128)(2,1)}, bf16[32,4,16,128]{3,2,1,0:T(8,128)(2,1)}, u32[]{:S(2)}, u32[]{:S(2)}) %collective-permute-start.6) | collective-permute-done | bytes 524320 | tf_op jit(solution)/shard_map/ppermute | solution.py:51
  31.0 2.2 %copy.39 = bf16[4,8,64,128]{3,1,2,0:T(8,128)(2,1)} copy(bf16[4,8,64,128]{3,2,1,0:T(8,128)(2,1)} %bitcast.41) | data formatting | bytes 1048576
  33.2 3.4 %shard_map.77 = bf16[128,8192]{1,0:T(8,128)(2,1)} custom-call(bf16[128,256]{1,0:T(8,128)(2,1)} %concatenate.23.refs_0_, bf16[32,8192]{1,0:T(8,128)(2,1)} %bitcast.104, bf16[32,8192]{1,0:T(8,128)(2,1)} %bitcast.110, bf16[32,8192]{1,0:T(8,128)(2,1)} %bitcast.108, bf16[32,8192]{1,0:T(8,128)(2,1)} %bitcast.106), custom_call_target="tpu_custom_call" | custom-call | tf_op jit(solution)/shard_map/pallas_call | solution.py:115
  36.6 2.2 %copy.28 = bf16[16,8,64,128]{3,2,1,0:T(8,128)(2,1)S(1)} copy(bf16[16,8,64,128]{3,1,2,0:T(8,128)(2,1)} %bitcast.84) | data formatting | bytes 4194304
  39.7 1.8 %collective-permute-start.10 = (bf16[32,4,16,128]{3,2,1,0:T(8,128)(2,1)S(1)}, bf16[32,4,16,128]{3,2,1,0:T(8,128)(2,1)}, u32[]{:S(2)}, u32[]{:S(2)}) collective-permute-start(bf16[32,4,16,128]{3,2,1,0:T(8,128)(2,1)S(1)} %constant_dynamic-slice_fusion.8), channel_id=1, source_target_pairs={{0,2},{1,3},{2,0},{3,1},{4,6},{5,7},{6,4},{7,5},{8,10},{9,11},{10,... | collective-permute-start | bytes 1572872 | tf_op jit(solution)/shard_map/ppermute | solution.py:51
  41.6 1.5 collective-permute-start.11
  43.1 2.2 %copy.41 = bf16[4,8,64,128]{3,1,2,0:T(8,128)(2,1)} copy(bf16[4,8,64,128]{3,2,1,0:T(8,128)(2,1)} %bitcast.32) | data formatting | bytes 1048576
  45.3 4.3 %collective-permute-done.1 = bf16[32,4,16,128]{3,2,1,0:T(8,128)(2,1)} collective-permute-done((bf16[32,4,16,128]{3,2,1,0:T(8,128)(2,1)}, bf16[32,4,16,128]{3,2,1,0:T(8,128)(2,1)}, u32[]{:S(2)}, u32[]{:S(2)}) %collective-permute-start.1) | collective-permute-done | bytes 524320 | tf_op jit(solution)/shard_map/ppermute | solution.py:51
  49.5 2.2 %copy.42 = bf16[4,8,64,128]{3,1,2,0:T(8,128)(2,1)} copy(bf16[4,8,64,128]{3,2,1,0:T(8,128)(2,1)} %bitcast.29) | data formatting | bytes 1048576
  51.7 1.8 %collective-permute-done = bf16[32,4,16,128]{3,2,1,0:T(8,128)(2,1)} collective-permute-done((bf16[32,4,16,128]{3,2,1,0:T(8,128)(2,1)}, bf16[32,4,16,128]{3,2,1,0:T(8,128)(2,1)}, u32[]{:S(2)}, u32[]{:S(2)}) %collective-permute-start) | collective-permute-done | bytes 524320 | tf_op jit(solution)/shard_map/ppermute | solution.py:51
  53.5 2.2 %copy.43 = bf16[4,8,64,128]{3,1,2,0:T(8,128)(2,1)} copy(bf16[4,8,64,128]{3,2,1,0:T(8,128)(2,1)} %bitcast.26) | data formatting | bytes 1048576
  56.4 3.6 %shard_map.76 = bf16[128,8192]{1,0:T(8,128)(2,1)} custom-call(bf16[128,256]{1,0:T(8,128)(2,1)} %concatenate.23.refs_0_, bf16[32,8192]{1,0:T(8,128)(2,1)} %bitcast.103, bf16[32,8192]{1,0:T(8,128)(2,1)} %bitcast.109, bf16[32,8192]{1,0:T(8,128)(2,1)} %bitcast.107, bf16[32,8192]{1,0:T(8,128)(2,1)} %bitcast.105, f32[1,8192]{1,0:T(1,128)} %bitcast.115), custom_call_target="tpu_custom_call" | custom-call | tf_op jit(solution)/shard_map/pallas_call | solution.py:115
  60.0 2.2 %copy.23 = bf16[16,8,64,128]{3,2,1,0:T(8,128)(2,1)S(1)} copy(bf16[16,8,64,128]{3,1,2,0:T(8,128)(2,1)} %bitcast.83) | data formatting | bytes 4194304
  62.3 1.8 %collective-permute-start.4 = (bf16[32,4,16,128]{3,2,1,0:T(8,128)(2,1)S(1)}, bf16[32,4,16,128]{3,2,1,0:T(8,128)(2,1)S(1)}, u32[]{:S(2)}, u32[]{:S(2)}) collective-permute-start(bf16[32,4,16,128]{3,2,1,0:T(8,128)(2,1)S(1)} %constant_dynamic-slice_fusion.15), channel_id=1, source_target_pairs={{0,2},{1,3},{2,0},{3,1},{4,6},{5,7},{6,4},{7,5},{8,10},{9,11},{10,... | collective-permute-start | bytes 1572872 | tf_op jit(solution)/shard_map/ppermute | solution.py:51
  64.7 1.0 collective-permute-start.5
  65.8 4.8 %collective-permute-done.11 = bf16[32,4,16,128]{3,2,1,0:T(8,128)(2,1)} collective-permute-done((bf16[32,4,16,128]{3,2,1,0:T(8,128)(2,1)S(1)}, bf16[32,4,16,128]{3,2,1,0:T(8,128)(2,1)}, u32[]{:S(2)}, u32[]{:S(2)}) %collective-permute-start.11) | collective-permute-done | bytes 524320 | tf_op jit(solution)/shard_map/ppermute | solution.py:51
  70.6 1.6 %pad_maximum_fusion.11 = bf16[4,32,4,16,128]{4,3,2,1,0:T(8,128)(2,1)S(1)} fusion(bf16[1,32,4,16,128]{4,3,2,1,0:T(8,128)(2,1)} %bitcast.13, bf16[1,32,4,16,128]{4,3,2,1,0:T(8,128)(2,1)} %bitcast.12, bf16[1,32,4,16,128]{4,3,2,1,0:T(8,128)(2,1)} %bitcast.11, bf16[1,32,4,16,128]{4,3,2,1,0:T(8,128)(2,1)S(1)} %dynamic-slice_bitcast_fusion.4), kind=kLoop, calls=%fused_computation.24 | loop fusion | flops 3145728 | bytes 4194304 | tf_op jit(solution)/shard_map/stack | solution.py:59
  73.5 1.3 collective-permute-start.12
  74.8 4.8 %collective-permute-start.13 = (bf16[32,1,64,128]{3,2,1,0:T(8,128)(2,1)S(1)}, bf16[32,1,64,128]{3,2,1,0:T(8,128)(2,1)S(1)}, u32[]{:S(2)}, u32[]{:S(2)}) collective-permute-start(bf16[32,1,64,128]{3,2,1,0:T(8,128)(2,1)S(1)} %get-tuple-element.56), channel_id=1, source_target_pairs={{0,4},{4,8},{8,12},{12,16},{16,20},{20,24},{24,28},{1,5},{5,9},{9,... | collective-permute-start | bytes 1572872 | tf_op jit(solution)/shard_map/ppermute | solution.py:22
  79.6 7.5 %collective-permute-done.3 = bf16[32,4,16,128]{3,2,1,0:T(8,128)(2,1)S(1)} collective-permute-done((bf16[32,4,16,128]{3,2,1,0:T(8,128)(2,1)S(1)}, bf16[32,4,16,128]{3,2,1,0:T(8,128)(2,1)S(1)}, u32[]{:S(2)}, u32[]{:S(2)}) %collective-permute-start.3) | collective-permute-done | bytes 524320 | tf_op jit(solution)/shard_map/ppermute | solution.py:51
  87.1 6.0 %collective-permute-done.5 = bf16[32,4,16,128]{3,2,1,0:T(8,128)(2,1)S(1)} collective-permute-done((bf16[32,4,16,128]{3,2,1,0:T(8,128)(2,1)S(1)}, bf16[32,4,16,128]{3,2,1,0:T(8,128)(2,1)S(1)}, u32[]{:S(2)}, u32[]{:S(2)}) %collective-permute-start.5) | collective-permute-done | bytes 524320 | tf_op jit(solution)/shard_map/ppermute | solution.py:51
  94.1 7.2 %collective-permute-done.13 = bf16[32,1,64,128]{3,2,1,0:T(8,128)(2,1)S(1)} collective-permute-done((bf16[32,1,64,128]{3,2,1,0:T(8,128)(2,1)S(1)}, bf16[32,1,64,128]{3,2,1,0:T(8,128)(2,1)S(1)}, u32[]{:S(2)}, u32[]{:S(2)}) %collective-permute-start.13) | collective-permute-done | bytes 524320 | tf_op jit(solution)/shard_map/ppermute | solution.py:22
  101.3 5.9 %fusion.6 = bf16[32,4,64,128]{3,2,1,0:T(8,128)(2,1)S(1)} fusion(f32[32,4,64,128]{3,2,1,0:T(8,128)S(1)} %get-tuple-element.58, bf16[32,1,64,128]{3,2,1,0:T(8,128)(2,1)S(1)} %collective-permute-done.13, bf16[32,4,16,128]{3,2,1,0:T(8,128)(2,1)S(1)} %get-tuple-element.60, bf16[32,4,16,128]{3,2,1,0:T(8,128)(2,1)S(1)} %get-tuple-element.61, ...), kind=kLoop, calls=%fused_computation.10 | loop fusion | flops 34603008 | bytes 9447424 | tf_op jit(solution)/shard_map/convert_element_type | solution.py:222
  108.8 1.2 fusion.12
  110.7 2.5 %collective-permute-start.14 = (bf16[1,256,256]{2,1,0:T(8,128)(2,1)S(1)}, bf16[1,256,256]{2,1,0:T(8,128)(2,1)S(1)}, u32[]{:S(2)}, u32[]{:S(2)}) collective-permute-start(bf16[1,256,256]{2,1,0:T(8,128)(2,1)S(1)} %constant_dynamic-slice_fusion.6), channel_id=1, source_target_pairs={{0,4},{4,8},{8,12},{12,16},{16,20},{20,24},{24,28},{28,0},{1,5},{5... | collective-permute-start | bytes 393224 | tf_op jit(solution)/shard_map/ppermute | solution.py:51
  113.3 1.6 %collective-permute-start.15 = (bf16[1,256,256]{2,1,0:T(8,128)(2,1)S(1)}, bf16[1,256,256]{2,1,0:T(8,128)(2,1)S(1)}, u32[]{:S(2)}, u32[]{:S(2)}) collective-permute-start(bf16[1,256,256]{2,1,0:T(8,128)(2,1)S(1)} %constant_dynamic-slice_fusion.5), channel_id=1, source_target_pairs={{0,8},{4,12},{8,16},{12,20},{16,24},{20,28},{24,0},{28,4},{1,9},{5... | collective-permute-start | bytes 393224 | tf_op jit(solution)/shard_map/ppermute | solution.py:51
  114.9 1.1 collective-permute-start.16
  116.0 1.8 %collective-permute-start.17 = (bf16[1,256,256]{2,1,0:T(8,128)(2,1)S(1)}, bf16[1,256,256]{2,1,0:T(8,128)(2,1)S(1)}, u32[]{:S(2)}, u32[]{:S(2)}) collective-permute-start(bf16[1,256,256]{2,1,0:T(8,128)(2,1)S(1)} %constant_dynamic-slice_fusion.3), channel_id=1, source_target_pairs={{0,16},{4,20},{8,24},{12,28},{16,0},{20,4},{24,8},{28,12},{1,17},{... | collective-permute-start | bytes 393224 | tf_op jit(solution)/shard_map/ppermute | solution.py:51
  117.9 2.1 %collective-permute-start.18 = (bf16[1,256,256]{2,1,0:T(8,128)(2,1)S(1)}, bf16[1,256,256]{2,1,0:T(8,128)(2,1)S(1)}, u32[]{:S(2)}, u32[]{:S(2)}) collective-permute-start(bf16[1,256,256]{2,1,0:T(8,128)(2,1)S(1)} %constant_dynamic-slice_fusion.2), channel_id=1, source_target_pairs={{0,20},{4,24},{8,28},{12,0},{16,4},{20,8},{24,12},{28,16},{1,21},{... | collective-permute-start | bytes 393224 | tf_op jit(solution)/shard_map/ppermute | solution.py:51
  120.0 3.0 %collective-permute-start.19 = (bf16[1,256,256]{2,1,0:T(8,128)(2,1)S(1)}, bf16[1,256,256]{2,1,0:T(8,128)(2,1)S(1)}, u32[]{:S(2)}, u32[]{:S(2)}) collective-permute-start(bf16[1,256,256]{2,1,0:T(8,128)(2,1)S(1)} %constant_dynamic-slice_fusion.1), channel_id=1, source_target_pairs={{0,24},{4,28},{8,0},{12,4},{16,8},{20,12},{24,16},{28,20},{1,25},{... | collective-permute-start | bytes 393224 | tf_op jit(solution)/shard_map/ppermute | solution.py:51
  123.6 6.9 %collective-permute-done.16 = bf16[1,256,256]{2,1,0:T(8,128)(2,1)S(1)} collective-permute-done((bf16[1,256,256]{2,1,0:T(8,128)(2,1)S(1)}, bf16[1,256,256]{2,1,0:T(8,128)(2,1)S(1)}, u32[]{:S(2)}, u32[]{:S(2)}) %collective-permute-start.16) | collective-permute-done | bytes 131104 | tf_op jit(solution)/shard_map/ppermute | solution.py:51
  130.6 1.1 collective-permute-done.17
  132.1 18.4 %all_to_all.6 = f32[8,1,32]{2,1,0:T(1,128)S(1)} all-to-all(f32[8,1,32]{2,1,0:T(1,128)S(1)} %broadcast_in_dim.5), channel_id=1, replica_groups=mesh['gx'=8,'ka'=4] {'gx'}, dimensions={0} | all-to-all | bytes 2048 | tf_op jit(solution)/shard_map/all_to_all | solution.py:34
  (80 shorter events, 13.6 us)
Async XLA Ops:
  0.6 11.8 %copy-start = (bf16[32,4,64,128]{3,2,1,0:T(8,128)(2,1)S(1)}, bf16[32,4,64,128]{3,2,1,0:T(8,128)(2,1)}, u32[]{:S(2)}) copy-start(bf16[32,4,64,128]{3,2,1,0:T(8,128)(2,1)} %param.6) | copy-start | bytes 6291460
  0.6 15.4 %copy-start.3 = (f32[4,64]{1,0:T(4,128)S(1)}, f32[4,64]{1,0:T(4,128)}, u32[]{:S(2)}) copy-start(f32[4,64]{1,0:T(4,128)} %param.7) | copy-start | bytes 3076
  1.9 15.4 %collective-permute-start.8 = (bf16[32,4,16,128]{3,2,1,0:T(8,128)(2,1)S(1)}, bf16[32,4,16,128]{3,2,1,0:T(8,128)(2,1)S(1)}, u32[]{:S(2)}, u32[]{:S(2)}) collective-permute-start(bf16[32,4,16,128]{3,2,1,0:T(8,128)(2,1)S(1)} %constant_dynamic-slice_fusion.10), channel_id=1, source_target_pairs={{0,3},{1,0},{2,1},{3,2},{4,7},{5,4},{6,5},{7,6},{8,11},{9,8},{10,9... | collective-permute-start | bytes 1572872 | tf_op jit(solution)/shard_map/ppermute | solution.py:51
  6.3 20.8 %collective-permute-start.7 = (bf16[32,4,16,128]{3,2,1,0:T(8,128)(2,1)}, bf16[32,4,16,128]{3,2,1,0:T(8,128)(2,1)}, u32[]{:S(2)}, u32[]{:S(2)}) collective-permute-start(bf16[32,4,16,128]{3,2,1,0:T(8,128)(2,1)} %constant_dynamic-slice_fusion.11), channel_id=1, source_target_pairs={{0,2},{1,3},{2,0},{3,1},{4,6},{5,7},{6,4},{7,5},{8,10},{9,11},{10,... | collective-permute-start | bytes 1572872 | tf_op jit(solution)/shard_map/ppermute | solution.py:51
  6.9 13.9 %copy-start.4 = (f32[4,64]{1,0:T(4,128)S(1)}, f32[4,64]{1,0:T(4,128)}, u32[]{:S(2)}) copy-start(f32[4,64]{1,0:T(4,128)} %param.8) | copy-start | bytes 3076
  8.8 22.2 %collective-permute-start.6 = (bf16[32,4,16,128]{3,2,1,0:T(8,128)(2,1)}, bf16[32,4,16,128]{3,2,1,0:T(8,128)(2,1)}, u32[]{:S(2)}, u32[]{:S(2)}) collective-permute-start(bf16[32,4,16,128]{3,2,1,0:T(8,128)(2,1)} %constant_dynamic-slice_fusion.12), channel_id=1, source_target_pairs={{0,1},{1,2},{2,3},{3,0},{4,5},{5,6},{6,7},{7,4},{8,9},{9,10},{10,1... | collective-permute-start | bytes 1572872 | tf_op jit(solution)/shard_map/ppermute | solution.py:51
  10.9 30.7 %collective-permute-start.2 = (bf16[32,4,16,128]{3,2,1,0:T(8,128)(2,1)}, bf16[32,4,16,128]{3,2,1,0:T(8,128)(2,1)}, u32[]{:S(2)}, u32[]{:S(2)}) collective-permute-start(bf16[32,4,16,128]{3,2,1,0:T(8,128)(2,1)} %constant_dynamic-slice_fusion.18), channel_id=1, source_target_pairs={{0,3},{1,0},{2,1},{3,2},{4,7},{5,4},{6,5},{7,6},{8,11},{9,8},{10,9... | collective-permute-start | bytes 1572872 | tf_op jit(solution)/shard_map/ppermute | solution.py:51
  13.3 36.2 %collective-permute-start.1 = (bf16[32,4,16,128]{3,2,1,0:T(8,128)(2,1)}, bf16[32,4,16,128]{3,2,1,0:T(8,128)(2,1)}, u32[]{:S(2)}, u32[]{:S(2)}) collective-permute-start(bf16[32,4,16,128]{3,2,1,0:T(8,128)(2,1)} %constant_dynamic-slice_fusion.19), channel_id=1, source_target_pairs={{0,2},{1,3},{2,0},{3,1},{4,6},{5,7},{6,4},{7,5},{8,10},{9,11},{10,... | collective-permute-start | bytes 1572872 | tf_op jit(solution)/shard_map/ppermute | solution.py:51
  17.3 0.8 copy-start.1
  18.1 35.4 %collective-permute-start = (bf16[32,4,16,128]{3,2,1,0:T(8,128)(2,1)}, bf16[32,4,16,128]{3,2,1,0:T(8,128)(2,1)}, u32[]{:S(2)}, u32[]{:S(2)}) collective-permute-start(bf16[32,4,16,128]{3,2,1,0:T(8,128)(2,1)} %constant_dynamic-slice_fusion.20), channel_id=1, source_target_pairs={{0,1},{1,2},{2,3},{3,0},{4,5},{5,6},{6,7},{7,4},{8,9},{9,10},{10,1... | collective-permute-start | bytes 1572872 | tf_op jit(solution)/shard_map/ppermute | solution.py:51
  39.7 25.1 %collective-permute-start.9 = (bf16[32,4,16,128]{3,2,1,0:T(8,128)(2,1)}, bf16[32,4,16,128]{3,2,1,0:T(8,128)(2,1)}, u32[]{:S(2)}, u32[]{:S(2)}) collective-permute-start(bf16[32,4,16,128]{3,2,1,0:T(8,128)(2,1)} %constant_dynamic-slice_fusion.9), channel_id=1, source_target_pairs={{0,1},{1,2},{2,3},{3,0},{4,5},{5,6},{6,7},{7,4},{8,9},{9,10},{10,1... | collective-permute-start | bytes 1572872 | tf_op jit(solution)/shard_map/ppermute | solution.py:51
  39.7 26.1 %collective-permute-start.10 = (bf16[32,4,16,128]{3,2,1,0:T(8,128)(2,1)S(1)}, bf16[32,4,16,128]{3,2,1,0:T(8,128)(2,1)}, u32[]{:S(2)}, u32[]{:S(2)}) collective-permute-start(bf16[32,4,16,128]{3,2,1,0:T(8,128)(2,1)S(1)} %constant_dynamic-slice_fusion.8), channel_id=1, source_target_pairs={{0,2},{1,3},{2,0},{3,1},{4,6},{5,7},{6,4},{7,5},{8,10},{9,11},{10,... | collective-permute-start | bytes 1572872 | tf_op jit(solution)/shard_map/ppermute | solution.py:51
  41.6 29.0 %collective-permute-start.11 = (bf16[32,4,16,128]{3,2,1,0:T(8,128)(2,1)S(1)}, bf16[32,4,16,128]{3,2,1,0:T(8,128)(2,1)}, u32[]{:S(2)}, u32[]{:S(2)}) collective-permute-start(bf16[32,4,16,128]{3,2,1,0:T(8,128)(2,1)S(1)} %constant_dynamic-slice_fusion.7), channel_id=1, source_target_pairs={{0,3},{1,0},{2,1},{3,2},{4,7},{5,4},{6,5},{7,6},{8,11},{9,8},{10,9... | collective-permute-start | bytes 1572872 | tf_op jit(solution)/shard_map/ppermute | solution.py:51
  62.2 24.9 %collective-permute-start.3 = (bf16[32,4,16,128]{3,2,1,0:T(8,128)(2,1)S(1)}, bf16[32,4,16,128]{3,2,1,0:T(8,128)(2,1)S(1)}, u32[]{:S(2)}, u32[]{:S(2)}) collective-permute-start(bf16[32,4,16,128]{3,2,1,0:T(8,128)(2,1)S(1)} %constant_dynamic-slice_fusion.16), channel_id=1, source_target_pairs={{0,1},{1,2},{2,3},{3,0},{4,5},{5,6},{6,7},{7,4},{8,9},{9,10},{10,1... | collective-permute-start | bytes 1572872 | tf_op jit(solution)/shard_map/ppermute | solution.py:51
  62.3 24.8 %collective-permute-start.4 = (bf16[32,4,16,128]{3,2,1,0:T(8,128)(2,1)S(1)}, bf16[32,4,16,128]{3,2,1,0:T(8,128)(2,1)S(1)}, u32[]{:S(2)}, u32[]{:S(2)}) collective-permute-start(bf16[32,4,16,128]{3,2,1,0:T(8,128)(2,1)S(1)} %constant_dynamic-slice_fusion.15), channel_id=1, source_target_pairs={{0,2},{1,3},{2,0},{3,1},{4,6},{5,7},{6,4},{7,5},{8,10},{9,11},{10,... | collective-permute-start | bytes 1572872 | tf_op jit(solution)/shard_map/ppermute | solution.py:51
  64.7 28.3 %collective-permute-start.5 = (bf16[32,4,16,128]{3,2,1,0:T(8,128)(2,1)S(1)}, bf16[32,4,16,128]{3,2,1,0:T(8,128)(2,1)S(1)}, u32[]{:S(2)}, u32[]{:S(2)}) collective-permute-start(bf16[32,4,16,128]{3,2,1,0:T(8,128)(2,1)S(1)} %constant_dynamic-slice_fusion.14), channel_id=1, source_target_pairs={{0,3},{1,0},{2,1},{3,2},{4,7},{5,4},{6,5},{7,6},{8,11},{9,8},{10,9... | collective-permute-start | bytes 1572872 | tf_op jit(solution)/shard_map/ppermute | solution.py:51
  73.5 20.5 %collective-permute-start.12 = (bf16[32,1,64,128]{3,2,1,0:T(8,128)(2,1)S(1)}, bf16[32,1,64,128]{3,2,1,0:T(8,128)(2,1)S(1)}, u32[]{:S(2)}, u32[]{:S(2)}) collective-permute-start(bf16[32,1,64,128]{3,2,1,0:T(8,128)(2,1)S(1)} %get-tuple-element.55), channel_id=1, source_target_pairs={{4,0},{8,4},{12,8},{16,12},{20,16},{24,20},{28,24},{5,1},{9,5},{13... | collective-permute-start | bytes 1572872 | tf_op jit(solution)/shard_map/ppermute | solution.py:24
  74.8 26.4 %collective-permute-start.13 = (bf16[32,1,64,128]{3,2,1,0:T(8,128)(2,1)S(1)}, bf16[32,1,64,128]{3,2,1,0:T(8,128)(2,1)S(1)}, u32[]{:S(2)}, u32[]{:S(2)}) collective-permute-start(bf16[32,1,64,128]{3,2,1,0:T(8,128)(2,1)S(1)} %get-tuple-element.56), channel_id=1, source_target_pairs={{0,4},{4,8},{8,12},{12,16},{16,20},{20,24},{24,28},{1,5},{5,9},{9,... | collective-permute-start | bytes 1572872 | tf_op jit(solution)/shard_map/ppermute | solution.py:22
  93.3 7.9 %copy-start.2 = (f32[4,64]{1,0:T(4,128)S(1)}, f32[4,64]{1,0:T(4,128)}, u32[]{:S(2)}) copy-start(f32[4,64]{1,0:T(4,128)} %param.9) | copy-start | bytes 3076
  110.7 9.3 %collective-permute-start.14 = (bf16[1,256,256]{2,1,0:T(8,128)(2,1)S(1)}, bf16[1,256,256]{2,1,0:T(8,128)(2,1)S(1)}, u32[]{:S(2)}, u32[]{:S(2)}) collective-permute-start(bf16[1,256,256]{2,1,0:T(8,128)(2,1)S(1)} %constant_dynamic-slice_fusion.6), channel_id=1, source_target_pairs={{0,4},{4,8},{8,12},{12,16},{16,20},{20,24},{24,28},{28,0},{1,5},{5... | collective-permute-start | bytes 393224 | tf_op jit(solution)/shard_map/ppermute | solution.py:51
  113.3 9.7 %collective-permute-start.15 = (bf16[1,256,256]{2,1,0:T(8,128)(2,1)S(1)}, bf16[1,256,256]{2,1,0:T(8,128)(2,1)S(1)}, u32[]{:S(2)}, u32[]{:S(2)}) collective-permute-start(bf16[1,256,256]{2,1,0:T(8,128)(2,1)S(1)} %constant_dynamic-slice_fusion.5), channel_id=1, source_target_pairs={{0,8},{4,12},{8,16},{12,20},{16,24},{20,28},{24,0},{28,4},{1,9},{5... | collective-permute-start | bytes 393224 | tf_op jit(solution)/shard_map/ppermute | solution.py:51
  114.9 15.6 %collective-permute-start.16 = (bf16[1,256,256]{2,1,0:T(8,128)(2,1)S(1)}, bf16[1,256,256]{2,1,0:T(8,128)(2,1)S(1)}, u32[]{:S(2)}, u32[]{:S(2)}) collective-permute-start(bf16[1,256,256]{2,1,0:T(8,128)(2,1)S(1)} %constant_dynamic-slice_fusion.4), channel_id=1, source_target_pairs={{0,12},{4,16},{8,20},{12,24},{16,28},{20,0},{24,4},{28,8},{1,13},{... | collective-permute-start | bytes 393224 | tf_op jit(solution)/shard_map/ppermute | solution.py:51
  116.0 15.7 %collective-permute-start.17 = (bf16[1,256,256]{2,1,0:T(8,128)(2,1)S(1)}, bf16[1,256,256]{2,1,0:T(8,128)(2,1)S(1)}, u32[]{:S(2)}, u32[]{:S(2)}) collective-permute-start(bf16[1,256,256]{2,1,0:T(8,128)(2,1)S(1)} %constant_dynamic-slice_fusion.3), channel_id=1, source_target_pairs={{0,16},{4,20},{8,24},{12,28},{16,0},{20,4},{24,8},{28,12},{1,17},{... | collective-permute-start | bytes 393224 | tf_op jit(solution)/shard_map/ppermute | solution.py:51
  117.9 13.8 %collective-permute-start.18 = (bf16[1,256,256]{2,1,0:T(8,128)(2,1)S(1)}, bf16[1,256,256]{2,1,0:T(8,128)(2,1)S(1)}, u32[]{:S(2)}, u32[]{:S(2)}) collective-permute-start(bf16[1,256,256]{2,1,0:T(8,128)(2,1)S(1)} %constant_dynamic-slice_fusion.2), channel_id=1, source_target_pairs={{0,20},{4,24},{8,28},{12,0},{16,4},{20,8},{24,12},{28,16},{1,21},{... | collective-permute-start | bytes 393224 | tf_op jit(solution)/shard_map/ppermute | solution.py:51
  120.0 11.7 %collective-permute-start.19 = (bf16[1,256,256]{2,1,0:T(8,128)(2,1)S(1)}, bf16[1,256,256]{2,1,0:T(8,128)(2,1)S(1)}, u32[]{:S(2)}, u32[]{:S(2)}) collective-permute-start(bf16[1,256,256]{2,1,0:T(8,128)(2,1)S(1)} %constant_dynamic-slice_fusion.1), channel_id=1, source_target_pairs={{0,24},{4,28},{8,0},{12,4},{16,8},{20,12},{24,16},{28,20},{1,25},{... | collective-permute-start | bytes 393224 | tf_op jit(solution)/shard_map/ppermute | solution.py:51
  123.0 8.8 %collective-permute-start.20 = (bf16[1,256,256]{2,1,0:T(8,128)(2,1)S(1)}, bf16[1,256,256]{2,1,0:T(8,128)(2,1)S(1)}, u32[]{:S(2)}, u32[]{:S(2)}) collective-permute-start(bf16[1,256,256]{2,1,0:T(8,128)(2,1)S(1)} %constant_dynamic-slice_fusion), channel_id=1, source_target_pairs={{0,28},{4,0},{8,4},{12,8},{16,12},{20,16},{24,20},{28,24},{1,29},{... | collective-permute-start | bytes 393224 | tf_op jit(solution)/shard_map/ppermute | solution.py:51

commit v24 on v21

--- a/solution.py
+++ b/solution.py
@@ -237,9 +237,11 @@
     shares = gram_terms.astype(jnp.bfloat16).reshape(lax.axis_size("gx"), row_count, 2 * columns)
     own_rows = sum(piece.astype(jnp.float32) for piece in exchange(shares, "gx", 0, True, True))[0]
     row_energy = jnp.sum(own_rows[:, :columns] ** 2, axis=1)
-    energy = jnp.sum(gather_small(jnp.sum(selector * row_energy[:, None], axis=0), "gx"), axis=0)
+    partial_energy = jnp.sum(selector * row_energy[:, None], axis=0)
+    energy = jnp.sum(gather_small(partial_energy, "gx"), axis=0)
     mean_sq = energy / (2.0 * snap_count * snap_count)
-    row_scale = jnp.sum(selector * lax.rsqrt(mean_sq + epsilon)[None, :], axis=1)
+    own_sq = partial_energy / (2.0 * snap_count * snap_count) if row_count % snap_count == 0 else mean_sq
+    row_scale = jnp.sum(selector * lax.rsqrt(own_sq + epsilon)[None, :], axis=1)
     hankel_gram = own_rows[:, :columns] * row_scale[:, None]
     reduced_operator = own_rows[:, columns:] * row_scale[:, None]
     hankel_norm = jnp.sqrt(mean_sq)

time: 152 us -> 152 us (level)
  blocking collectives: 11.7 us -> 0 us
  waiting for transfers between devices: 49.3 us -> 54.7 us
  starting transfers between devices: 31.9 us -> 37.3 us
    all_to_all x1 -> x0, blocking collectives: 11.7 us -> none  [gather_small(): return lax.all_to_all(copies, axis, split_axis=0, concat_axis=0, tiled=True)]
    all_to_all x0 -> x1, waiting for transfers between devices: none -> 5.66 us  [gather_small(): return lax.all_to_all(copies, axis, split_axis=0, concat_axis=0, tiled=True)]
    all_to_all x0 -> x1, starting transfers between devices: none -> 5.39 us  [gather_small(): return lax.all_to_all(copies, axis, split_axis=0, concat_axis=0, tiled=True)]
  transfers between devices with their start and end apart: 21 -> 22, of which waited for: 13 -> 14; matrix products, arithmetic and copies ran while one was open for 24% -> 25% of each run, Pallas kernels for 5% -> 5%
where the time goes in v24:
time: 152 us; the launch traced here: 151 us
  waiting for transfers between devices  54.7 us (36%)
  starting transfers between devices  37.3 us (25%)
  local copies, waits for them, and re-layouts  35.3 us (23%)
  other arithmetic  14.5 us (10%)
  Pallas kernels  7.2 us (5%)
    ppermute x19, waiting for transfers between devices, exchange(): lax.ppermute(piece, axis, [(j, (j + shift) % count) for j in range(count)])  41.8 us
    ppermute x19, starting transfers between devices, exchange(): lax.ppermute(piece, axis, [(j, (j + shift) % count) for j in range(count)])  25.9 us
    unnamed x20, local copies, waits for them, and re-layouts  20.6 us
    dynamic_slice x20, local copies, waits for them, and re-layouts, exchange(): lax.dynamic_slice_in_dim(source, (here + shift) % count * width, width, a...  11.1 us
    pallas_call x2, Pallas kernels, dft(): pl.pallas_call(functools.partial(dft_kernel, count=count, weighted=weight...  7.2 us
    ppermute x1, waiting for transfers between devices, padded_2(): lax.ppermute(tail, axis, [(i, (i + 1) % count) for i in range(ends)])  7.19 us
    convert_element_type x1, other arithmetic, local(): image = (-velocity * (forward - behind) * 0.5 + diffusion * (forward + be...  5.9 us
    all_to_all x1, waiting for transfers between devices, gather_small(): return lax.all_to_all(copies, axis, split_axis=0, concat_axis=0, tiled=True)  5.66 us
  transfers between devices with their start and end apart: 22, of which 14 were waited for; matrix products, arithmetic and copies ran while one was open for 25% of the time, Pallas kernels for 5%

profile of v24, /device:TPU:0, one launch (start us, length us, event | category | flops | bytes accessed | tf_op | source)
XLA Modules:
  0.0 151.1 jit_solution(15486747828134164324)
XLA Ops:
  0.7 1.2 constant_dynamic-slice_fusion.10
  1.9 2.5 %collective-permute-start.8 = (bf16[32,4,16,128]{3,2,1,0:T(8,128)(2,1)S(1)}, bf16[32,4,16,128]{3,2,1,0:T(8,128)(2,1)S(1)}, u32[]{:S(2)}, u32[]{:S(2)}) collective-permute-start(bf16[32,4,16,128]{3,2,1,0:T(8,128)(2,1)S(1)} %constant_dynamic-slice_fusion.10), channel_id=1, source_target_pairs={{0,3},{1,0},{2,1},{3,2},{4,7},{5,4},{6,5},{7,6},{8,11},{9,8},{10,9... | collective-permute-start | bytes 1572872 | tf_op jit(solution)/shard_map/ppermute | solution.py:51
  4.4 1.9 %constant_dynamic-slice_fusion.11 = bf16[32,4,16,128]{3,2,1,0:T(8,128)(2,1)} fusion(bf16[32,4,64,128]{3,2,1,0:T(8,128)(2,1)} %param.5, s32[]{:T(128)S(6)} %select_n.220), kind=kLoop, calls=%fused_computation.108 | loop fusion | bytes 1048580 | tf_op jit(solution)/shard_map/dynamic_slice | solution.py:49
  6.9 1.9 %constant_dynamic-slice_fusion.12 = bf16[32,4,16,128]{3,2,1,0:T(8,128)(2,1)} fusion(bf16[32,4,64,128]{3,2,1,0:T(8,128)(2,1)} %param.5, s32[]{:T(128)S(6)} %select_n.218), kind=kLoop, calls=%fused_computation.109 | loop fusion | bytes 1048580 | tf_op jit(solution)/shard_map/dynamic_slice | solution.py:49
  9.0 1.9 %constant_dynamic-slice_fusion.18 = bf16[32,4,16,128]{3,2,1,0:T(8,128)(2,1)} fusion(bf16[32,4,64,128]{3,2,1,0:T(8,128)(2,1)} %param.6, s32[]{:T(128)S(6)} %select_n.222), kind=kLoop, calls=%fused_computation.115 | loop fusion | bytes 1048580 | tf_op jit(solution)/shard_map/dynamic_slice | solution.py:49
  10.9 1.6 %collective-permute-start.2 = (bf16[32,4,16,128]{3,2,1,0:T(8,128)(2,1)}, bf16[32,4,16,128]{3,2,1,0:T(8,128)(2,1)}, u32[]{:S(2)}, u32[]{:S(2)}) collective-permute-start(bf16[32,4,16,128]{3,2,1,0:T(8,128)(2,1)} %constant_dynamic-slice_fusion.18), channel_id=1, source_target_pairs={{0,3},{1,0},{2,1},{3,2},{4,7},{5,4},{6,5},{7,6},{8,11},{9,8},{10,9... | collective-permute-start | bytes 1572872 | tf_op jit(solution)/shard_map/ppermute | solution.py:51
  12.4 0.9 constant_dynamic-slice_fusion.19
  13.3 1.4 collective-permute-start.1
  18.1 1.3 constant_dynamic-slice_fusion.13
  19.6 1.2 copy.40
  20.7 1.2 copy.44
  22.7 2.2 %copy.37 = bf16[4,8,64,128]{3,1,2,0:T(8,128)(2,1)} copy(bf16[4,8,64,128]{3,2,1,0:T(8,128)(2,1)} %bitcast.111) | data formatting | bytes 1048576
  24.9 2.1 %collective-permute-done.7 = bf16[32,4,16,128]{3,2,1,0:T(8,128)(2,1)} collective-permute-done((bf16[32,4,16,128]{3,2,1,0:T(8,128)(2,1)}, bf16[32,4,16,128]{3,2,1,0:T(8,128)(2,1)}, u32[]{:S(2)}, u32[]{:S(2)}) %collective-permute-start.7) | collective-permute-done | bytes 524320 | tf_op jit(solution)/shard_map/ppermute | solution.py:51
  27.1 2.2 %copy.38 = bf16[4,8,64,128]{3,1,2,0:T(8,128)(2,1)} copy(bf16[4,8,64,128]{3,2,1,0:T(8,128)(2,1)} %bitcast.44) | data formatting | bytes 1048576
  29.2 1.8 %collective-permute-done.6 = bf16[32,4,16,128]{3,2,1,0:T(8,128)(2,1)} collective-permute-done((bf16[32,4,16,128]{3,2,1,0:T(8,128)(2,1)}, bf16[32,4,16,128]{3,2,1,0:T(8,128)(2,1)}, u32[]{:S(2)}, u32[]{:S(2)}) %collective-permute-start.6) | collective-permute-done | bytes 524320 | tf_op jit(solution)/shard_map/ppermute | solution.py:51
  31.0 2.2 %copy.39 = bf16[4,8,64,128]{3,1,2,0:T(8,128)(2,1)} copy(bf16[4,8,64,128]{3,2,1,0:T(8,128)(2,1)} %bitcast.41) | data formatting | bytes 1048576
  33.2 3.5 %shard_map.77 = bf16[128,8192]{1,0:T(8,128)(2,1)} custom-call(bf16[128,256]{1,0:T(8,128)(2,1)} %concatenate.23.refs_0_, bf16[32,8192]{1,0:T(8,128)(2,1)} %bitcast.104, bf16[32,8192]{1,0:T(8,128)(2,1)} %bitcast.110, bf16[32,8192]{1,0:T(8,128)(2,1)} %bitcast.108, bf16[32,8192]{1,0:T(8,128)(2,1)} %bitcast.106), custom_call_target="tpu_custom_call" | custom-call | tf_op jit(solution)/shard_map/pallas_call | solution.py:115
  36.7 2.2 %copy.28 = bf16[16,8,64,128]{3,2,1,0:T(8,128)(2,1)S(1)} copy(bf16[16,8,64,128]{3,1,2,0:T(8,128)(2,1)} %bitcast.84) | data formatting | bytes 4194304
  39.8 1.8 %collective-permute-start.10 = (bf16[32,4,16,128]{3,2,1,0:T(8,128)(2,1)S(1)}, bf16[32,4,16,128]{3,2,1,0:T(8,128)(2,1)}, u32[]{:S(2)}, u32[]{:S(2)}) collective-permute-start(bf16[32,4,16,128]{3,2,1,0:T(8,128)(2,1)S(1)} %constant_dynamic-slice_fusion.8), channel_id=1, source_target_pairs={{0,2},{1,3},{2,0},{3,1},{4,6},{5,7},{6,4},{7,5},{8,10},{9,11},{10,... | collective-permute-start | bytes 1572872 | tf_op jit(solution)/shard_map/ppermute | solution.py:51
  41.7 1.5 %collective-permute-start.11 = (bf16[32,4,16,128]{3,2,1,0:T(8,128)(2,1)S(1)}, bf16[32,4,16,128]{3,2,1,0:T(8,128)(2,1)}, u32[]{:S(2)}, u32[]{:S(2)}) collective-permute-start(bf16[32,4,16,128]{3,2,1,0:T(8,128)(2,1)S(1)} %constant_dynamic-slice_fusion.7), channel_id=1, source_target_pairs={{0,3},{1,0},{2,1},{3,2},{4,7},{5,4},{6,5},{7,6},{8,11},{9,8},{10,9... | collective-permute-start | bytes 1572872 | tf_op jit(solution)/shard_map/ppermute | solution.py:51
  43.2 2.2 %copy.41 = bf16[4,8,64,128]{3,1,2,0:T(8,128)(2,1)} copy(bf16[4,8,64,128]{3,2,1,0:T(8,128)(2,1)} %bitcast.32) | data formatting | bytes 1048576
  45.4 4.1 %collective-permute-done.1 = bf16[32,4,16,128]{3,2,1,0:T(8,128)(2,1)} collective-permute-done((bf16[32,4,16,128]{3,2,1,0:T(8,128)(2,1)}, bf16[32,4,16,128]{3,2,1,0:T(8,128)(2,1)}, u32[]{:S(2)}, u32[]{:S(2)}) %collective-permute-start.1) | collective-permute-done | bytes 524320 | tf_op jit(solution)/shard_map/ppermute | solution.py:51
  49.5 2.2 %copy.42 = bf16[4,8,64,128]{3,1,2,0:T(8,128)(2,1)} copy(bf16[4,8,64,128]{3,2,1,0:T(8,128)(2,1)} %bitcast.29) | data formatting | bytes 1048576
  51.7 1.8 %collective-permute-done = bf16[32,4,16,128]{3,2,1,0:T(8,128)(2,1)} collective-permute-done((bf16[32,4,16,128]{3,2,1,0:T(8,128)(2,1)}, bf16[32,4,16,128]{3,2,1,0:T(8,128)(2,1)}, u32[]{:S(2)}, u32[]{:S(2)}) %collective-permute-start) | collective-permute-done | bytes 524320 | tf_op jit(solution)/shard_map/ppermute | solution.py:51
  53.5 2.2 %copy.43 = bf16[4,8,64,128]{3,1,2,0:T(8,128)(2,1)} copy(bf16[4,8,64,128]{3,2,1,0:T(8,128)(2,1)} %bitcast.26) | data formatting | bytes 1048576
  56.4 3.7 %shard_map.76 = bf16[128,8192]{1,0:T(8,128)(2,1)} custom-call(bf16[128,256]{1,0:T(8,128)(2,1)} %concatenate.23.refs_0_, bf16[32,8192]{1,0:T(8,128)(2,1)} %bitcast.103, bf16[32,8192]{1,0:T(8,128)(2,1)} %bitcast.109, bf16[32,8192]{1,0:T(8,128)(2,1)} %bitcast.107, bf16[32,8192]{1,0:T(8,128)(2,1)} %bitcast.105, f32[1,8192]{1,0:T(1,128)} %bitcast.115), custom_call_target="tpu_custom_call" | custom-call | tf_op jit(solution)/shard_map/pallas_call | solution.py:115
  60.1 2.2 %copy.23 = bf16[16,8,64,128]{3,2,1,0:T(8,128)(2,1)S(1)} copy(bf16[16,8,64,128]{3,1,2,0:T(8,128)(2,1)} %bitcast.83) | data formatting | bytes 4194304
  62.4 1.8 %collective-permute-start.4 = (bf16[32,4,16,128]{3,2,1,0:T(8,128)(2,1)S(1)}, bf16[32,4,16,128]{3,2,1,0:T(8,128)(2,1)S(1)}, u32[]{:S(2)}, u32[]{:S(2)}) collective-permute-start(bf16[32,4,16,128]{3,2,1,0:T(8,128)(2,1)S(1)} %constant_dynamic-slice_fusion.15), channel_id=1, source_target_pairs={{0,2},{1,3},{2,0},{3,1},{4,6},{5,7},{6,4},{7,5},{8,10},{9,11},{10,... | collective-permute-start | bytes 1572872 | tf_op jit(solution)/shard_map/ppermute | solution.py:51
  64.7 1.1 collective-permute-start.5
  65.9 4.7 %collective-permute-done.11 = bf16[32,4,16,128]{3,2,1,0:T(8,128)(2,1)} collective-permute-done((bf16[32,4,16,128]{3,2,1,0:T(8,128)(2,1)S(1)}, bf16[32,4,16,128]{3,2,1,0:T(8,128)(2,1)}, u32[]{:S(2)}, u32[]{:S(2)}) %collective-permute-start.11) | collective-permute-done | bytes 524320 | tf_op jit(solution)/shard_map/ppermute | solution.py:51
  70.6 1.6 %pad_maximum_fusion.11 = bf16[4,32,4,16,128]{4,3,2,1,0:T(8,128)(2,1)S(1)} fusion(bf16[1,32,4,16,128]{4,3,2,1,0:T(8,128)(2,1)} %bitcast.13, bf16[1,32,4,16,128]{4,3,2,1,0:T(8,128)(2,1)} %bitcast.12, bf16[1,32,4,16,128]{4,3,2,1,0:T(8,128)(2,1)} %bitcast.11, bf16[1,32,4,16,128]{4,3,2,1,0:T(8,128)(2,1)S(1)} %dynamic-slice_bitcast_fusion.4), kind=kLoop, calls=%fused_computation.24 | loop fusion | flops 3145728 | bytes 4194304 | tf_op jit(solution)/shard_map/stack | solution.py:59
  73.5 1.3 collective-permute-start.12
  74.8 4.8 %collective-permute-start.13 = (bf16[32,1,64,128]{3,2,1,0:T(8,128)(2,1)S(1)}, bf16[32,1,64,128]{3,2,1,0:T(8,128)(2,1)S(1)}, u32[]{:S(2)}, u32[]{:S(2)}) collective-permute-start(bf16[32,1,64,128]{3,2,1,0:T(8,128)(2,1)S(1)} %get-tuple-element.56), channel_id=1, source_target_pairs={{0,4},{4,8},{8,12},{12,16},{16,20},{20,24},{24,28},{1,5},{5,9},{9,... | collective-permute-start | bytes 1572872 | tf_op jit(solution)/shard_map/ppermute | solution.py:22
  79.6 7.5 %collective-permute-done.3 = bf16[32,4,16,128]{3,2,1,0:T(8,128)(2,1)S(1)} collective-permute-done((bf16[32,4,16,128]{3,2,1,0:T(8,128)(2,1)S(1)}, bf16[32,4,16,128]{3,2,1,0:T(8,128)(2,1)S(1)}, u32[]{:S(2)}, u32[]{:S(2)}) %collective-permute-start.3) | collective-permute-done | bytes 524320 | tf_op jit(solution)/shard_map/ppermute | solution.py:51
  87.1 6.0 %collective-permute-done.5 = bf16[32,4,16,128]{3,2,1,0:T(8,128)(2,1)S(1)} collective-permute-done((bf16[32,4,16,128]{3,2,1,0:T(8,128)(2,1)S(1)}, bf16[32,4,16,128]{3,2,1,0:T(8,128)(2,1)S(1)}, u32[]{:S(2)}, u32[]{:S(2)}) %collective-permute-start.5) | collective-permute-done | bytes 524320 | tf_op jit(solution)/shard_map/ppermute | solution.py:51
  94.1 7.2 %collective-permute-done.13 = bf16[32,1,64,128]{3,2,1,0:T(8,128)(2,1)S(1)} collective-permute-done((bf16[32,1,64,128]{3,2,1,0:T(8,128)(2,1)S(1)}, bf16[32,1,64,128]{3,2,1,0:T(8,128)(2,1)S(1)}, u32[]{:S(2)}, u32[]{:S(2)}) %collective-permute-start.13) | collective-permute-done | bytes 524320 | tf_op jit(solution)/shard_map/ppermute | solution.py:22
  101.3 5.9 %fusion.6 = bf16[32,4,64,128]{3,2,1,0:T(8,128)(2,1)S(1)} fusion(f32[32,4,64,128]{3,2,1,0:T(8,128)S(1)} %get-tuple-element.58, bf16[32,1,64,128]{3,2,1,0:T(8,128)(2,1)S(1)} %collective-permute-done.13, bf16[32,4,16,128]{3,2,1,0:T(8,128)(2,1)S(1)} %get-tuple-element.60, bf16[32,4,16,128]{3,2,1,0:T(8,128)(2,1)S(1)} %get-tuple-element.61, ...), kind=kLoop, calls=%fused_computation.10 | loop fusion | flops 34603008 | bytes 9447424 | tf_op jit(solution)/shard_map/convert_element_type | solution.py:222
  108.8 1.2 fusion.12
  110.7 2.7 %collective-permute-start.14 = (bf16[1,256,256]{2,1,0:T(8,128)(2,1)S(1)}, bf16[1,256,256]{2,1,0:T(8,128)(2,1)S(1)}, u32[]{:S(2)}, u32[]{:S(2)}) collective-permute-start(bf16[1,256,256]{2,1,0:T(8,128)(2,1)S(1)} %constant_dynamic-slice_fusion.6), channel_id=1, source_target_pairs={{0,16},{4,20},{8,24},{12,28},{16,0},{20,4},{24,8},{28,12},{1,17},{... | collective-permute-start | bytes 393224 | tf_op jit(solution)/shard_map/ppermute | solution.py:51
  113.4 1.0 collective-permute-start.15
  114.4 2.9 %collective-permute-start.16 = (bf16[1,256,256]{2,1,0:T(8,128)(2,1)S(1)}, bf16[1,256,256]{2,1,0:T(8,128)(2,1)S(1)}, u32[]{:S(2)}, u32[]{:S(2)}) collective-permute-start(bf16[1,256,256]{2,1,0:T(8,128)(2,1)S(1)} %constant_dynamic-slice_fusion.4), channel_id=1, source_target_pairs={{0,20},{4,24},{8,28},{12,0},{16,4},{20,8},{24,12},{28,16},{1,21},{... | collective-permute-start | bytes 393224 | tf_op jit(solution)/shard_map/ppermute | solution.py:51
  117.4 3.8 %collective-permute-start.18 = (bf16[1,256,256]{2,1,0:T(8,128)(2,1)S(1)}, bf16[1,256,256]{2,1,0:T(8,128)(2,1)S(1)}, u32[]{:S(2)}, u32[]{:S(2)}) collective-permute-start(bf16[1,256,256]{2,1,0:T(8,128)(2,1)S(1)} %constant_dynamic-slice_fusion.2), channel_id=1, source_target_pairs={{0,24},{4,28},{8,0},{12,4},{16,8},{20,12},{24,16},{28,20},{1,25},{... | collective-permute-start | bytes 393224 | tf_op jit(solution)/shard_map/ppermute | solution.py:51
  121.3 8.0 %collective-permute-done.14 = bf16[1,256,256]{2,1,0:T(8,128)(2,1)S(1)} collective-permute-done((bf16[1,256,256]{2,1,0:T(8,128)(2,1)S(1)}, bf16[1,256,256]{2,1,0:T(8,128)(2,1)S(1)}, u32[]{:S(2)}, u32[]{:S(2)}) %collective-permute-start.14) | collective-permute-done | bytes 131104 | tf_op jit(solution)/shard_map/ppermute | solution.py:51
  129.3 1.9 %collective-permute-done.15 = bf16[1,256,256]{2,1,0:T(8,128)(2,1)S(1)} collective-permute-done((bf16[1,256,256]{2,1,0:T(8,128)(2,1)S(1)}, bf16[1,256,256]{2,1,0:T(8,128)(2,1)S(1)}, u32[]{:S(2)}, u32[]{:S(2)}) %collective-permute-start.15) | collective-permute-done | bytes 131104 | tf_op jit(solution)/shard_map/ppermute | solution.py:51
  131.2 2.8 %collective-permute-start.20 = (bf16[1,256,256]{2,1,0:T(8,128)(2,1)S(1)}, bf16[1,256,256]{2,1,0:T(8,128)(2,1)S(1)}, u32[]{:S(2)}, u32[]{:S(2)}) collective-permute-start(bf16[1,256,256]{2,1,0:T(8,128)(2,1)S(1)} %constant_dynamic-slice_fusion), channel_id=1, source_target_pairs={{0,28},{4,0},{8,4},{12,8},{16,12},{20,16},{24,20},{28,24},{1,29},{... | collective-permute-start | bytes 393224 | tf_op jit(solution)/shard_map/ppermute | solution.py:51
  134.1 3.1 %collective-permute-done.19 = bf16[1,256,256]{2,1,0:T(8,128)(2,1)S(1)} collective-permute-done((bf16[1,256,256]{2,1,0:T(8,128)(2,1)S(1)}, bf16[1,256,256]{2,1,0:T(8,128)(2,1)S(1)}, u32[]{:S(2)}, u32[]{:S(2)}) %collective-permute-start.19) | collective-permute-done | bytes 131104 | tf_op jit(solution)/shard_map/ppermute | solution.py:51
  138.7 5.4 %all-to-all-start = ((f32[8,1,32]{2,1,0:T(1,128)}), f32[8,1,32]{2,1,0:T(1,128)S(1)}, u32[]{:S(2)}, u32[]{:S(2)}) async-start(f32[8,1,32]{2,1,0:T(1,128)} %broadcast_in_dim.5), calls=%async_computation | async-start | bytes 8192 | tf_op jit(solution)/shard_map/all_to_all | solution.py:34
  144.9 5.7 %all-to-all-done = f32[8,1,32]{2,1,0:T(1,128)S(1)} async-done(((f32[8,1,32]{2,1,0:T(1,128)}), f32[8,1,32]{2,1,0:T(1,128)S(1)}, u32[]{:S(2)}, u32[]{:S(2)}) %all-to-all-start) | async-done | bytes 1056 | tf_op jit(solution)/shard_map/all_to_all | solution.py:34
  (82 shorter events, 14.8 us)
Async XLA Ops:
  0.6 11.8 %copy-start = (bf16[32,4,64,128]{3,2,1,0:T(8,128)(2,1)S(1)}, bf16[32,4,64,128]{3,2,1,0:T(8,128)(2,1)}, u32[]{:S(2)}) copy-start(bf16[32,4,64,128]{3,2,1,0:T(8,128)(2,1)} %param.6) | copy-start | bytes 6291460
  0.6 15.4 %copy-start.3 = (f32[4,64]{1,0:T(4,128)S(1)}, f32[4,64]{1,0:T(4,128)}, u32[]{:S(2)}) copy-start(f32[4,64]{1,0:T(4,128)} %param.7) | copy-start | bytes 3076
  1.9 15.4 %collective-permute-start.8 = (bf16[32,4,16,128]{3,2,1,0:T(8,128)(2,1)S(1)}, bf16[32,4,16,128]{3,2,1,0:T(8,128)(2,1)S(1)}, u32[]{:S(2)}, u32[]{:S(2)}) collective-permute-start(bf16[32,4,16,128]{3,2,1,0:T(8,128)(2,1)S(1)} %constant_dynamic-slice_fusion.10), channel_id=1, source_target_pairs={{0,3},{1,0},{2,1},{3,2},{4,7},{5,4},{6,5},{7,6},{8,11},{9,8},{10,9... | collective-permute-start | bytes 1572872 | tf_op jit(solution)/shard_map/ppermute | solution.py:51
  6.3 20.8 %collective-permute-start.7 = (bf16[32,4,16,128]{3,2,1,0:T(8,128)(2,1)}, bf16[32,4,16,128]{3,2,1,0:T(8,128)(2,1)}, u32[]{:S(2)}, u32[]{:S(2)}) collective-permute-start(bf16[32,4,16,128]{3,2,1,0:T(8,128)(2,1)} %constant_dynamic-slice_fusion.11), channel_id=1, source_target_pairs={{0,2},{1,3},{2,0},{3,1},{4,6},{5,7},{6,4},{7,5},{8,10},{9,11},{10,... | collective-permute-start | bytes 1572872 | tf_op jit(solution)/shard_map/ppermute | solution.py:51
  6.9 13.9 %copy-start.4 = (f32[4,64]{1,0:T(4,128)S(1)}, f32[4,64]{1,0:T(4,128)}, u32[]{:S(2)}) copy-start(f32[4,64]{1,0:T(4,128)} %param.8) | copy-start | bytes 3076
  8.8 22.3 %collective-permute-start.6 = (bf16[32,4,16,128]{3,2,1,0:T(8,128)(2,1)}, bf16[32,4,16,128]{3,2,1,0:T(8,128)(2,1)}, u32[]{:S(2)}, u32[]{:S(2)}) collective-permute-start(bf16[32,4,16,128]{3,2,1,0:T(8,128)(2,1)} %constant_dynamic-slice_fusion.12), channel_id=1, source_target_pairs={{0,1},{1,2},{2,3},{3,0},{4,5},{5,6},{6,7},{7,4},{8,9},{9,10},{10,1... | collective-permute-start | bytes 1572872 | tf_op jit(solution)/shard_map/ppermute | solution.py:51
  10.9 30.8 %collective-permute-start.2 = (bf16[32,4,16,128]{3,2,1,0:T(8,128)(2,1)}, bf16[32,4,16,128]{3,2,1,0:T(8,128)(2,1)}, u32[]{:S(2)}, u32[]{:S(2)}) collective-permute-start(bf16[32,4,16,128]{3,2,1,0:T(8,128)(2,1)} %constant_dynamic-slice_fusion.18), channel_id=1, source_target_pairs={{0,3},{1,0},{2,1},{3,2},{4,7},{5,4},{6,5},{7,6},{8,11},{9,8},{10,9... | collective-permute-start | bytes 1572872 | tf_op jit(solution)/shard_map/ppermute | solution.py:51
  13.3 36.2 %collective-permute-start.1 = (bf16[32,4,16,128]{3,2,1,0:T(8,128)(2,1)}, bf16[32,4,16,128]{3,2,1,0:T(8,128)(2,1)}, u32[]{:S(2)}, u32[]{:S(2)}) collective-permute-start(bf16[32,4,16,128]{3,2,1,0:T(8,128)(2,1)} %constant_dynamic-slice_fusion.19), channel_id=1, source_target_pairs={{0,2},{1,3},{2,0},{3,1},{4,6},{5,7},{6,4},{7,5},{8,10},{9,11},{10,... | collective-permute-start | bytes 1572872 | tf_op jit(solution)/shard_map/ppermute | solution.py:51
  17.3 0.8 copy-start.1
  18.1 35.4 %collective-permute-start = (bf16[32,4,16,128]{3,2,1,0:T(8,128)(2,1)}, bf16[32,4,16,128]{3,2,1,0:T(8,128)(2,1)}, u32[]{:S(2)}, u32[]{:S(2)}) collective-permute-start(bf16[32,4,16,128]{3,2,1,0:T(8,128)(2,1)} %constant_dynamic-slice_fusion.20), channel_id=1, source_target_pairs={{0,1},{1,2},{2,3},{3,0},{4,5},{5,6},{6,7},{7,4},{8,9},{9,10},{10,1... | collective-permute-start | bytes 1572872 | tf_op jit(solution)/shard_map/ppermute | solution.py:51
  39.8 24.9 %collective-permute-start.9 = (bf16[32,4,16,128]{3,2,1,0:T(8,128)(2,1)}, bf16[32,4,16,128]{3,2,1,0:T(8,128)(2,1)}, u32[]{:S(2)}, u32[]{:S(2)}) collective-permute-start(bf16[32,4,16,128]{3,2,1,0:T(8,128)(2,1)} %constant_dynamic-slice_fusion.9), channel_id=1, source_target_pairs={{0,1},{1,2},{2,3},{3,0},{4,5},{5,6},{6,7},{7,4},{8,9},{9,10},{10,1... | collective-permute-start | bytes 1572872 | tf_op jit(solution)/shard_map/ppermute | solution.py:51
  39.8 26.0 %collective-permute-start.10 = (bf16[32,4,16,128]{3,2,1,0:T(8,128)(2,1)S(1)}, bf16[32,4,16,128]{3,2,1,0:T(8,128)(2,1)}, u32[]{:S(2)}, u32[]{:S(2)}) collective-permute-start(bf16[32,4,16,128]{3,2,1,0:T(8,128)(2,1)S(1)} %constant_dynamic-slice_fusion.8), channel_id=1, source_target_pairs={{0,2},{1,3},{2,0},{3,1},{4,6},{5,7},{6,4},{7,5},{8,10},{9,11},{10,... | collective-permute-start | bytes 1572872 | tf_op jit(solution)/shard_map/ppermute | solution.py:51
  41.7 28.9 %collective-permute-start.11 = (bf16[32,4,16,128]{3,2,1,0:T(8,128)(2,1)S(1)}, bf16[32,4,16,128]{3,2,1,0:T(8,128)(2,1)}, u32[]{:S(2)}, u32[]{:S(2)}) collective-permute-start(bf16[32,4,16,128]{3,2,1,0:T(8,128)(2,1)S(1)} %constant_dynamic-slice_fusion.7), channel_id=1, source_target_pairs={{0,3},{1,0},{2,1},{3,2},{4,7},{5,4},{6,5},{7,6},{8,11},{9,8},{10,9... | collective-permute-start | bytes 1572872 | tf_op jit(solution)/shard_map/ppermute | solution.py:51
  62.3 24.8 %collective-permute-start.3 = (bf16[32,4,16,128]{3,2,1,0:T(8,128)(2,1)S(1)}, bf16[32,4,16,128]{3,2,1,0:T(8,128)(2,1)S(1)}, u32[]{:S(2)}, u32[]{:S(2)}) collective-permute-start(bf16[32,4,16,128]{3,2,1,0:T(8,128)(2,1)S(1)} %constant_dynamic-slice_fusion.16), channel_id=1, source_target_pairs={{0,1},{1,2},{2,3},{3,0},{4,5},{5,6},{6,7},{7,4},{8,9},{9,10},{10,1... | collective-permute-start | bytes 1572872 | tf_op jit(solution)/shard_map/ppermute | solution.py:51
  62.4 24.7 %collective-permute-start.4 = (bf16[32,4,16,128]{3,2,1,0:T(8,128)(2,1)S(1)}, bf16[32,4,16,128]{3,2,1,0:T(8,128)(2,1)S(1)}, u32[]{:S(2)}, u32[]{:S(2)}) collective-permute-start(bf16[32,4,16,128]{3,2,1,0:T(8,128)(2,1)S(1)} %constant_dynamic-slice_fusion.15), channel_id=1, source_target_pairs={{0,2},{1,3},{2,0},{3,1},{4,6},{5,7},{6,4},{7,5},{8,10},{9,11},{10,... | collective-permute-start | bytes 1572872 | tf_op jit(solution)/shard_map/ppermute | solution.py:51
  64.7 28.3 %collective-permute-start.5 = (bf16[32,4,16,128]{3,2,1,0:T(8,128)(2,1)S(1)}, bf16[32,4,16,128]{3,2,1,0:T(8,128)(2,1)S(1)}, u32[]{:S(2)}, u32[]{:S(2)}) collective-permute-start(bf16[32,4,16,128]{3,2,1,0:T(8,128)(2,1)S(1)} %constant_dynamic-slice_fusion.14), channel_id=1, source_target_pairs={{0,3},{1,0},{2,1},{3,2},{4,7},{5,4},{6,5},{7,6},{8,11},{9,8},{10,9... | collective-permute-start | bytes 1572872 | tf_op jit(solution)/shard_map/ppermute | solution.py:51
  73.5 20.5 %collective-permute-start.12 = (bf16[32,1,64,128]{3,2,1,0:T(8,128)(2,1)S(1)}, bf16[32,1,64,128]{3,2,1,0:T(8,128)(2,1)S(1)}, u32[]{:S(2)}, u32[]{:S(2)}) collective-permute-start(bf16[32,1,64,128]{3,2,1,0:T(8,128)(2,1)S(1)} %get-tuple-element.55), channel_id=1, source_target_pairs={{4,0},{8,4},{12,8},{16,12},{20,16},{24,20},{28,24},{5,1},{9,5},{13... | collective-permute-start | bytes 1572872 | tf_op jit(solution)/shard_map/ppermute | solution.py:24
  74.8 26.4 %collective-permute-start.13 = (bf16[32,1,64,128]{3,2,1,0:T(8,128)(2,1)S(1)}, bf16[32,1,64,128]{3,2,1,0:T(8,128)(2,1)S(1)}, u32[]{:S(2)}, u32[]{:S(2)}) collective-permute-start(bf16[32,1,64,128]{3,2,1,0:T(8,128)(2,1)S(1)} %get-tuple-element.56), channel_id=1, source_target_pairs={{0,4},{4,8},{8,12},{12,16},{16,20},{20,24},{24,28},{1,5},{5,9},{9,... | collective-permute-start | bytes 1572872 | tf_op jit(solution)/shard_map/ppermute | solution.py:22
  93.3 7.9 %copy-start.2 = (f32[4,64]{1,0:T(4,128)S(1)}, f32[4,64]{1,0:T(4,128)}, u32[]{:S(2)}) copy-start(f32[4,64]{1,0:T(4,128)} %param.9) | copy-start | bytes 3076
  110.7 18.6 %collective-permute-start.14 = (bf16[1,256,256]{2,1,0:T(8,128)(2,1)S(1)}, bf16[1,256,256]{2,1,0:T(8,128)(2,1)S(1)}, u32[]{:S(2)}, u32[]{:S(2)}) collective-permute-start(bf16[1,256,256]{2,1,0:T(8,128)(2,1)S(1)} %constant_dynamic-slice_fusion.6), channel_id=1, source_target_pairs={{0,16},{4,20},{8,24},{12,28},{16,0},{20,4},{24,8},{28,12},{1,17},{... | collective-permute-start | bytes 393224 | tf_op jit(solution)/shard_map/ppermute | solution.py:51
  113.4 17.9 %collective-permute-start.15 = (bf16[1,256,256]{2,1,0:T(8,128)(2,1)S(1)}, bf16[1,256,256]{2,1,0:T(8,128)(2,1)S(1)}, u32[]{:S(2)}, u32[]{:S(2)}) collective-permute-start(bf16[1,256,256]{2,1,0:T(8,128)(2,1)S(1)} %constant_dynamic-slice_fusion.5), channel_id=1, source_target_pairs={{0,12},{4,16},{8,20},{12,24},{16,28},{20,0},{24,4},{28,8},{1,13},{... | collective-permute-start | bytes 393224 | tf_op jit(solution)/shard_map/ppermute | solution.py:51
  114.4 19.7 %collective-permute-start.16 = (bf16[1,256,256]{2,1,0:T(8,128)(2,1)S(1)}, bf16[1,256,256]{2,1,0:T(8,128)(2,1)S(1)}, u32[]{:S(2)}, u32[]{:S(2)}) collective-permute-start(bf16[1,256,256]{2,1,0:T(8,128)(2,1)S(1)} %constant_dynamic-slice_fusion.4), channel_id=1, source_target_pairs={{0,20},{4,24},{8,28},{12,0},{16,4},{20,8},{24,12},{28,16},{1,21},{... | collective-permute-start | bytes 393224 | tf_op jit(solution)/shard_map/ppermute | solution.py:51
  117.3 16.7 %collective-permute-start.17 = (bf16[1,256,256]{2,1,0:T(8,128)(2,1)S(1)}, bf16[1,256,256]{2,1,0:T(8,128)(2,1)S(1)}, u32[]{:S(2)}, u32[]{:S(2)}) collective-permute-start(bf16[1,256,256]{2,1,0:T(8,128)(2,1)S(1)} %constant_dynamic-slice_fusion.3), channel_id=1, source_target_pairs={{0,8},{4,12},{8,16},{12,20},{16,24},{20,28},{24,0},{28,4},{1,9},{5... | collective-permute-start | bytes 393224 | tf_op jit(solution)/shard_map/ppermute | solution.py:51
  117.4 16.7 %collective-permute-start.18 = (bf16[1,256,256]{2,1,0:T(8,128)(2,1)S(1)}, bf16[1,256,256]{2,1,0:T(8,128)(2,1)S(1)}, u32[]{:S(2)}, u32[]{:S(2)}) collective-permute-start(bf16[1,256,256]{2,1,0:T(8,128)(2,1)S(1)} %constant_dynamic-slice_fusion.2), channel_id=1, source_target_pairs={{0,24},{4,28},{8,0},{12,4},{16,8},{20,12},{24,16},{28,20},{1,25},{... | collective-permute-start | bytes 393224 | tf_op jit(solution)/shard_map/ppermute | solution.py:51
  129.3 7.8 %collective-permute-start.19 = (bf16[1,256,256]{2,1,0:T(8,128)(2,1)S(1)}, bf16[1,256,256]{2,1,0:T(8,128)(2,1)S(1)}, u32[]{:S(2)}, u32[]{:S(2)}) collective-permute-start(bf16[1,256,256]{2,1,0:T(8,128)(2,1)S(1)} %constant_dynamic-slice_fusion.1), channel_id=1, source_target_pairs={{0,4},{4,8},{8,12},{12,16},{16,20},{20,24},{24,28},{28,0},{1,5},{5... | collective-permute-start | bytes 393224 | tf_op jit(solution)/shard_map/ppermute | solution.py:51
  131.2 6.4 %collective-permute-start.20 = (bf16[1,256,256]{2,1,0:T(8,128)(2,1)S(1)}, bf16[1,256,256]{2,1,0:T(8,128)(2,1)S(1)}, u32[]{:S(2)}, u32[]{:S(2)}) collective-permute-start(bf16[1,256,256]{2,1,0:T(8,128)(2,1)S(1)} %constant_dynamic-slice_fusion), channel_id=1, source_target_pairs={{0,28},{4,0},{8,4},{12,8},{16,12},{20,16},{24,20},{28,24},{1,29},{... | collective-permute-start | bytes 393224 | tf_op jit(solution)/shard_map/ppermute | solution.py:51
  138.7 11.9 %all-to-all-start = ((f32[8,1,32]{2,1,0:T(1,128)}), f32[8,1,32]{2,1,0:T(1,128)S(1)}, u32[]{:S(2)}, u32[]{:S(2)}) async-start(f32[8,1,32]{2,1,0:T(1,128)} %broadcast_in_dim.5), calls=%async_computation | async-start | bytes 8192 | tf_op jit(solution)/shard_map/all_to_all | solution.py:34

commit v25 on v21

--- a/solution.py
+++ b/solution.py
@@ -118,6 +118,11 @@
         in_specs=in_specs,
         out_specs=pl.BlockSpec((waves, block), lambda j: (0, j)),
         out_shape=jax.ShapeDtypeStruct((waves, total), jnp.bfloat16),
+        cost_estimate=pl.CostEstimate(
+            flops=2 * waves * table.shape[1] * total,
+            transcendentals=0,
+            bytes_accessed=2 * (count * angles * total + waves * total + table.size),
+        ),
     )(*args)
 
 

time: 152 us -> 153 us (level)
  waiting for transfers between devices: 49.3 us -> 52.9 us
    ppermute x19, waiting for transfers between devices: 42.1 us -> 45.6 us  [exchange(): lax.ppermute(piece, axis, [(j, (j + shift) % count) for j in range(count)])]
    unnamed x20 -> x18, local copies, waits for them, and re-layouts: 20.6 us -> 17.8 us
    dynamic_slice x20, local copies, waits for them, and re-layouts: 11.1 us -> 12.8 us  [exchange(): lax.dynamic_slice_in_dim(source, (here + shift) % count * width, width, a...]
  transfers between devices with their start and end apart: 21 -> 21, of which waited for: 13 -> 13; matrix products, arithmetic and copies ran while one was open for 24% -> 23% of each run, Pallas kernels for 5% -> 5%
where the time goes in v25:
time: 153 us; the launch traced here: 152 us
  waiting for transfers between devices  52.9 us (35%)
  local copies, waits for them, and re-layouts  33.5 us (22%)
  starting transfers between devices  30.7 us (20%)
  other arithmetic  14.5 us (9%)
  blocking collectives  11.7 us (8%)
  Pallas kernels  7.13 us (5%)
    ppermute x19, waiting for transfers between devices, exchange(): lax.ppermute(piece, axis, [(j, (j + shift) % count) for j in range(count)])  45.6 us
    ppermute x19, starting transfers between devices, exchange(): lax.ppermute(piece, axis, [(j, (j + shift) % count) for j in range(count)])  24.7 us
    unnamed x18, local copies, waits for them, and re-layouts  17.8 us
    dynamic_slice x20, local copies, waits for them, and re-layouts, exchange(): lax.dynamic_slice_in_dim(source, (here + shift) % count * width, width, a...  12.8 us
    all_to_all x1, blocking collectives, gather_small(): return lax.all_to_all(copies, axis, split_axis=0, concat_axis=0, tiled=True)  11.7 us
    ppermute x1, waiting for transfers between devices, padded_2(): lax.ppermute(tail, axis, [(i, (i + 1) % count) for i in range(ends)])  7.3 us
    pallas_call x2, Pallas kernels, dft(): pl.pallas_call(functools.partial(dft_kernel, count=count, weighted=weight...  7.13 us
    convert_element_type x1, other arithmetic, local(): image = (-velocity * (forward - behind) * 0.5 + diffusion * (forward + be...  5.9 us
  transfers between devices with their start and end apart: 21, of which 13 were waited for; matrix products, arithmetic and copies ran while one was open for 23% of the time, Pallas kernels for 5%

profile of v25, /device:TPU:0, one launch (start us, length us, event | category | flops | bytes accessed | tf_op | source)
XLA Modules:
  0.0 152.4 jit_solution(8507130601901921501)
XLA Ops:
  0.7 2.1 %constant_dynamic-slice_fusion.10 = bf16[32,4,16,128]{3,2,1,0:T(8,128)(2,1)} fusion(bf16[32,4,64,128]{3,2,1,0:T(8,128)(2,1)} %param.5, s32[]{:T(128)S(6)} %select_n.222), kind=kLoop, calls=%fused_computation.107 | loop fusion | bytes 1048580 | tf_op jit(solution)/shard_map/dynamic_slice | solution.py:49
  2.7 2.4 %collective-permute-start.8 = (bf16[32,4,16,128]{3,2,1,0:T(8,128)(2,1)}, bf16[32,4,16,128]{3,2,1,0:T(8,128)(2,1)S(1)}, u32[]{:S(2)}, u32[]{:S(2)}) collective-permute-start(bf16[32,4,16,128]{3,2,1,0:T(8,128)(2,1)} %constant_dynamic-slice_fusion.10), channel_id=1, source_target_pairs={{0,3},{1,0},{2,1},{3,2},{4,7},{5,4},{6,5},{7,6},{8,11},{9,8},{10,9... | collective-permute-start | bytes 1572872 | tf_op jit(solution)/shard_map/ppermute | solution.py:51
  5.1 1.9 %constant_dynamic-slice_fusion.11 = bf16[32,4,16,128]{3,2,1,0:T(8,128)(2,1)} fusion(bf16[32,4,64,128]{3,2,1,0:T(8,128)(2,1)} %param.5, s32[]{:T(128)S(6)} %select_n.220), kind=kLoop, calls=%fused_computation.108 | loop fusion | bytes 1048580 | tf_op jit(solution)/shard_map/dynamic_slice | solution.py:49
  7.6 1.9 %constant_dynamic-slice_fusion.12 = bf16[32,4,16,128]{3,2,1,0:T(8,128)(2,1)} fusion(bf16[32,4,64,128]{3,2,1,0:T(8,128)(2,1)} %param.5, s32[]{:T(128)S(6)} %select_n.218), kind=kLoop, calls=%fused_computation.109 | loop fusion | bytes 1048580 | tf_op jit(solution)/shard_map/dynamic_slice | solution.py:49
  9.7 1.9 %constant_dynamic-slice_fusion.18 = bf16[32,4,16,128]{3,2,1,0:T(8,128)(2,1)} fusion(bf16[32,4,64,128]{3,2,1,0:T(8,128)(2,1)} %param.6, s32[]{:T(128)S(6)} %select_n.222), kind=kLoop, calls=%fused_computation.115 | loop fusion | bytes 1048580 | tf_op jit(solution)/shard_map/dynamic_slice | solution.py:49
  11.6 1.5 collective-permute-start.2
  14.0 1.5 collective-permute-start.1
  15.6 1.3 constant_dynamic-slice_fusion.13
  16.9 1.2 copy.40
  19.6 0.9 constant_dynamic-slice_fusion.20
  20.5 1.2 copy.44
  22.6 1.2 copy.37
  23.8 4.5 %collective-permute-done.7 = bf16[32,4,16,128]{3,2,1,0:T(8,128)(2,1)} collective-permute-done((bf16[32,4,16,128]{3,2,1,0:T(8,128)(2,1)}, bf16[32,4,16,128]{3,2,1,0:T(8,128)(2,1)}, u32[]{:S(2)}, u32[]{:S(2)}) %collective-permute-start.7) | collective-permute-done | bytes 524320 | tf_op jit(solution)/shard_map/ppermute | solution.py:51
  28.2 2.2 %copy.38 = bf16[4,8,64,128]{3,1,2,0:T(8,128)(2,1)} copy(bf16[4,8,64,128]{3,2,1,0:T(8,128)(2,1)} %bitcast.44) | data formatting | bytes 1048576
  30.4 1.4 collective-permute-done.6
  31.8 2.2 %copy.39 = bf16[4,8,64,128]{3,1,2,0:T(8,128)(2,1)} copy(bf16[4,8,64,128]{3,2,1,0:T(8,128)(2,1)} %bitcast.41) | data formatting | bytes 1048576
  34.0 3.5 %shard_map.77 = bf16[128,8192]{1,0:T(8,128)(2,1)} custom-call(bf16[128,256]{1,0:T(8,128)(2,1)} %concatenate.23.refs_0_, bf16[32,8192]{1,0:T(8,128)(2,1)} %bitcast.103, bf16[32,8192]{1,0:T(8,128)(2,1)} %bitcast.110, bf16[32,8192]{1,0:T(8,128)(2,1)} %bitcast.108, bf16[32,8192]{1,0:T(8,128)(2,1)} %bitcast.106), custom_call_target="tpu_custom_call" | custom-call | flops 536870912 | bytes 4259840 | tf_op jit(solution)/shard_map/pallas_call | solution.py:115
  37.5 2.2 %copy.28 = bf16[16,8,64,128]{3,2,1,0:T(8,128)(2,1)S(1)} copy(bf16[16,8,64,128]{3,1,2,0:T(8,128)(2,1)} %bitcast.84) | data formatting | bytes 4194304
  39.6 0.9 constant_dynamic-slice_fusion.9
  40.5 1.8 %collective-permute-start.10 = (bf16[32,4,16,128]{3,2,1,0:T(8,128)(2,1)S(1)}, bf16[32,4,16,128]{3,2,1,0:T(8,128)(2,1)}, u32[]{:S(2)}, u32[]{:S(2)}) collective-permute-start(bf16[32,4,16,128]{3,2,1,0:T(8,128)(2,1)S(1)} %constant_dynamic-slice_fusion.8), channel_id=1, source_target_pairs={{0,2},{1,3},{2,0},{3,1},{4,6},{5,7},{6,4},{7,5},{8,10},{9,11},{10,... | collective-permute-start | bytes 1572872 | tf_op jit(solution)/shard_map/ppermute | solution.py:51
  43.2 1.4 collective-permute-start.11
  44.7 2.2 %copy.41 = bf16[4,8,64,128]{3,1,2,0:T(8,128)(2,1)} copy(bf16[4,8,64,128]{3,2,1,0:T(8,128)(2,1)} %bitcast.32) | data formatting | bytes 1048576
  46.9 3.8 %collective-permute-done.1 = bf16[32,4,16,128]{3,2,1,0:T(8,128)(2,1)} collective-permute-done((bf16[32,4,16,128]{3,2,1,0:T(8,128)(2,1)}, bf16[32,4,16,128]{3,2,1,0:T(8,128)(2,1)}, u32[]{:S(2)}, u32[]{:S(2)}) %collective-permute-start.1) | collective-permute-done | bytes 524320 | tf_op jit(solution)/shard_map/ppermute | solution.py:51
  50.7 2.2 %copy.42 = bf16[4,8,64,128]{3,1,2,0:T(8,128)(2,1)} copy(bf16[4,8,64,128]{3,2,1,0:T(8,128)(2,1)} %bitcast.29) | data formatting | bytes 1048576
  52.9 1.3 collective-permute-done
  54.2 1.2 copy.43
  56.0 3.7 %shard_map.76 = bf16[128,8192]{1,0:T(8,128)(2,1)} custom-call(bf16[128,256]{1,0:T(8,128)(2,1)} %concatenate.23.refs_0_, bf16[32,8192]{1,0:T(8,128)(2,1)} %bitcast.104, bf16[32,8192]{1,0:T(8,128)(2,1)} %bitcast.109, bf16[32,8192]{1,0:T(8,128)(2,1)} %bitcast.107, bf16[32,8192]{1,0:T(8,128)(2,1)} %bitcast.105, f32[1,8192]{1,0:T(1,128)} %bitcast.116), custom_call_target="tpu_custom_call" | custom-call | flops 536870912 | bytes 4259840 | tf_op jit(solution)/shard_map/pallas_call | solution.py:115
  59.7 2.2 %copy.23 = bf16[16,8,64,128]{3,2,1,0:T(8,128)(2,1)S(1)} copy(bf16[16,8,64,128]{3,1,2,0:T(8,128)(2,1)} %bitcast.83) | data formatting | bytes 4194304
  62.0 1.8 %collective-permute-start.4 = (bf16[32,4,16,128]{3,2,1,0:T(8,128)(2,1)S(1)}, bf16[32,4,16,128]{3,2,1,0:T(8,128)(2,1)S(1)}, u32[]{:S(2)}, u32[]{:S(2)}) collective-permute-start(bf16[32,4,16,128]{3,2,1,0:T(8,128)(2,1)S(1)} %constant_dynamic-slice_fusion.15), channel_id=1, source_target_pairs={{0,2},{1,3},{2,0},{3,1},{4,6},{5,7},{6,4},{7,5},{8,10},{9,11},{10,... | collective-permute-start | bytes 1572872 | tf_op jit(solution)/shard_map/ppermute | solution.py:51
  64.0 1.5 collective-permute-done.9
  65.5 6.4 %collective-permute-done.11 = bf16[32,4,16,128]{3,2,1,0:T(8,128)(2,1)} collective-permute-done((bf16[32,4,16,128]{3,2,1,0:T(8,128)(2,1)}, bf16[32,4,16,128]{3,2,1,0:T(8,128)(2,1)}, u32[]{:S(2)}, u32[]{:S(2)}) %collective-permute-start.11) | collective-permute-done | bytes 524320 | tf_op jit(solution)/shard_map/ppermute | solution.py:51
  71.9 1.6 %pad_maximum_fusion.11 = bf16[4,32,4,16,128]{4,3,2,1,0:T(8,128)(2,1)S(1)} fusion(bf16[1,32,4,16,128]{4,3,2,1,0:T(8,128)(2,1)} %bitcast.13, bf16[1,32,4,16,128]{4,3,2,1,0:T(8,128)(2,1)} %bitcast.12, bf16[1,32,4,16,128]{4,3,2,1,0:T(8,128)(2,1)} %bitcast.11, bf16[1,32,4,16,128]{4,3,2,1,0:T(8,128)(2,1)S(1)} %dynamic-slice_bitcast_fusion.4), kind=kLoop, calls=%fused_computation.24 | loop fusion | flops 3145728 | bytes 4194304 | tf_op jit(solution)/shard_map/stack | solution.py:59
  74.8 1.3 collective-permute-start.12
  76.1 4.8 %collective-permute-start.13 = (bf16[32,1,64,128]{3,2,1,0:T(8,128)(2,1)S(1)}, bf16[32,1,64,128]{3,2,1,0:T(8,128)(2,1)S(1)}, u32[]{:S(2)}, u32[]{:S(2)}) collective-permute-start(bf16[32,1,64,128]{3,2,1,0:T(8,128)(2,1)S(1)} %get-tuple-element.56), channel_id=1, source_target_pairs={{0,4},{4,8},{8,12},{12,16},{16,20},{20,24},{24,28},{1,5},{5,9},{9,... | collective-permute-start | bytes 1572872 | tf_op jit(solution)/shard_map/ppermute | solution.py:22
  80.9 7.0 %collective-permute-done.3 = bf16[32,4,16,128]{3,2,1,0:T(8,128)(2,1)S(1)} collective-permute-done((bf16[32,4,16,128]{3,2,1,0:T(8,128)(2,1)S(1)}, bf16[32,4,16,128]{3,2,1,0:T(8,128)(2,1)S(1)}, u32[]{:S(2)}, u32[]{:S(2)}) %collective-permute-start.3) | collective-permute-done | bytes 524320 | tf_op jit(solution)/shard_map/ppermute | solution.py:51
  87.9 6.4 %collective-permute-done.5 = bf16[32,4,16,128]{3,2,1,0:T(8,128)(2,1)S(1)} collective-permute-done((bf16[32,4,16,128]{3,2,1,0:T(8,128)(2,1)S(1)}, bf16[32,4,16,128]{3,2,1,0:T(8,128)(2,1)S(1)}, u32[]{:S(2)}, u32[]{:S(2)}) %collective-permute-start.5) | collective-permute-done | bytes 524320 | tf_op jit(solution)/shard_map/ppermute | solution.py:51
  95.3 7.3 %collective-permute-done.13 = bf16[32,1,64,128]{3,2,1,0:T(8,128)(2,1)S(1)} collective-permute-done((bf16[32,1,64,128]{3,2,1,0:T(8,128)(2,1)S(1)}, bf16[32,1,64,128]{3,2,1,0:T(8,128)(2,1)S(1)}, u32[]{:S(2)}, u32[]{:S(2)}) %collective-permute-start.13) | collective-permute-done | bytes 524320 | tf_op jit(solution)/shard_map/ppermute | solution.py:22
  102.6 5.9 %fusion.6 = bf16[32,4,64,128]{3,2,1,0:T(8,128)(2,1)S(1)} fusion(f32[32,4,64,128]{3,2,1,0:T(8,128)S(1)} %get-tuple-element.58, bf16[32,1,64,128]{3,2,1,0:T(8,128)(2,1)S(1)} %collective-permute-done.13, bf16[32,4,16,128]{3,2,1,0:T(8,128)(2,1)S(1)} %get-tuple-element.60, bf16[32,4,16,128]{3,2,1,0:T(8,128)(2,1)S(1)} %get-tuple-element.61, ...), kind=kLoop, calls=%fused_computation.10 | loop fusion | flops 34603008 | bytes 9447424 | tf_op jit(solution)/shard_map/convert_element_type | solution.py:227
  110.1 1.2 fusion.12
  112.0 2.7 %collective-permute-start.14 = (bf16[1,256,256]{2,1,0:T(8,128)(2,1)S(1)}, bf16[1,256,256]{2,1,0:T(8,128)(2,1)S(1)}, u32[]{:S(2)}, u32[]{:S(2)}) collective-permute-start(bf16[1,256,256]{2,1,0:T(8,128)(2,1)S(1)} %constant_dynamic-slice_fusion.6), channel_id=1, source_target_pairs={{0,16},{4,20},{8,24},{12,28},{16,0},{20,4},{24,8},{28,12},{1,17},{... | collective-permute-start | bytes 393224 | tf_op jit(solution)/shard_map/ppermute | solution.py:51
  114.7 1.0 collective-permute-start.15
  115.7 2.9 %collective-permute-start.16 = (bf16[1,256,256]{2,1,0:T(8,128)(2,1)S(1)}, bf16[1,256,256]{2,1,0:T(8,128)(2,1)S(1)}, u32[]{:S(2)}, u32[]{:S(2)}) collective-permute-start(bf16[1,256,256]{2,1,0:T(8,128)(2,1)S(1)} %constant_dynamic-slice_fusion.4), channel_id=1, source_target_pairs={{0,20},{4,24},{8,28},{12,0},{16,4},{20,8},{24,12},{28,16},{1,21},{... | collective-permute-start | bytes 393224 | tf_op jit(solution)/shard_map/ppermute | solution.py:51
  118.7 3.8 %collective-permute-start.18 = (bf16[1,256,256]{2,1,0:T(8,128)(2,1)S(1)}, bf16[1,256,256]{2,1,0:T(8,128)(2,1)S(1)}, u32[]{:S(2)}, u32[]{:S(2)}) collective-permute-start(bf16[1,256,256]{2,1,0:T(8,128)(2,1)S(1)} %constant_dynamic-slice_fusion.2), channel_id=1, source_target_pairs={{0,24},{4,28},{8,0},{12,4},{16,8},{20,12},{24,16},{28,20},{1,25},{... | collective-permute-start | bytes 393224 | tf_op jit(solution)/shard_map/ppermute | solution.py:51
  122.6 8.0 %collective-permute-done.14 = bf16[1,256,256]{2,1,0:T(8,128)(2,1)S(1)} collective-permute-done((bf16[1,256,256]{2,1,0:T(8,128)(2,1)S(1)}, bf16[1,256,256]{2,1,0:T(8,128)(2,1)S(1)}, u32[]{:S(2)}, u32[]{:S(2)}) %collective-permute-start.14) | collective-permute-done | bytes 131104 | tf_op jit(solution)/shard_map/ppermute | solution.py:51
  130.6 1.9 %collective-permute-done.15 = bf16[1,256,256]{2,1,0:T(8,128)(2,1)S(1)} collective-permute-done((bf16[1,256,256]{2,1,0:T(8,128)(2,1)S(1)}, bf16[1,256,256]{2,1,0:T(8,128)(2,1)S(1)}, u32[]{:S(2)}, u32[]{:S(2)}) %collective-permute-start.15) | collective-permute-done | bytes 131104 | tf_op jit(solution)/shard_map/ppermute | solution.py:51
  132.5 2.8 %collective-permute-start.20 = (bf16[1,256,256]{2,1,0:T(8,128)(2,1)S(1)}, bf16[1,256,256]{2,1,0:T(8,128)(2,1)S(1)}, u32[]{:S(2)}, u32[]{:S(2)}) collective-permute-start(bf16[1,256,256]{2,1,0:T(8,128)(2,1)S(1)} %constant_dynamic-slice_fusion), channel_id=1, source_target_pairs={{0,28},{4,0},{8,4},{12,8},{16,12},{20,16},{24,20},{28,24},{1,29},{... | collective-permute-start | bytes 393224 | tf_op jit(solution)/shard_map/ppermute | solution.py:51
  135.4 3.1 %collective-permute-done.19 = bf16[1,256,256]{2,1,0:T(8,128)(2,1)S(1)} collective-permute-done((bf16[1,256,256]{2,1,0:T(8,128)(2,1)S(1)}, bf16[1,256,256]{2,1,0:T(8,128)(2,1)S(1)}, u32[]{:S(2)}, u32[]{:S(2)}) %collective-permute-start.19) | collective-permute-done | bytes 131104 | tf_op jit(solution)/shard_map/ppermute | solution.py:51
  139.3 11.7 %all_to_all.6 = f32[8,1,32]{2,1,0:T(1,128)S(1)} all-to-all(f32[8,1,32]{2,1,0:T(1,128)S(1)} %broadcast_in_dim.5), channel_id=1, replica_groups=mesh['gx'=8,'ka'=4] {'gx'}, dimensions={0} | all-to-all | bytes 2048 | tf_op jit(solution)/shard_map/all_to_all | solution.py:34
  (78 shorter events, 13.0 us)
Async XLA Ops:
  0.6 12.5 %copy-start = (bf16[32,4,64,128]{3,2,1,0:T(8,128)(2,1)S(1)}, bf16[32,4,64,128]{3,2,1,0:T(8,128)(2,1)}, u32[]{:S(2)}) copy-start(bf16[32,4,64,128]{3,2,1,0:T(8,128)(2,1)} %param.6) | copy-start | bytes 6291460
  2.7 19.8 %collective-permute-start.8 = (bf16[32,4,16,128]{3,2,1,0:T(8,128)(2,1)}, bf16[32,4,16,128]{3,2,1,0:T(8,128)(2,1)S(1)}, u32[]{:S(2)}, u32[]{:S(2)}) collective-permute-start(bf16[32,4,16,128]{3,2,1,0:T(8,128)(2,1)} %constant_dynamic-slice_fusion.10), channel_id=1, source_target_pairs={{0,3},{1,0},{2,1},{3,2},{4,7},{5,4},{6,5},{7,6},{8,11},{9,8},{10,9... | collective-permute-start | bytes 1572872 | tf_op jit(solution)/shard_map/ppermute | solution.py:51
  5.1 14.5 %copy-start.2 = (f32[4,64]{1,0:T(4,128)S(1)}, f32[4,64]{1,0:T(4,128)}, u32[]{:S(2)}) copy-start(f32[4,64]{1,0:T(4,128)} %param.8) | copy-start | bytes 3076
  7.0 21.2 %collective-permute-start.7 = (bf16[32,4,16,128]{3,2,1,0:T(8,128)(2,1)}, bf16[32,4,16,128]{3,2,1,0:T(8,128)(2,1)}, u32[]{:S(2)}, u32[]{:S(2)}) collective-permute-start(bf16[32,4,16,128]{3,2,1,0:T(8,128)(2,1)} %constant_dynamic-slice_fusion.11), channel_id=1, source_target_pairs={{0,2},{1,3},{2,0},{3,1},{4,6},{5,7},{6,4},{7,5},{8,10},{9,11},{10,... | collective-permute-start | bytes 1572872 | tf_op jit(solution)/shard_map/ppermute | solution.py:51
  9.5 22.3 %collective-permute-start.6 = (bf16[32,4,16,128]{3,2,1,0:T(8,128)(2,1)}, bf16[32,4,16,128]{3,2,1,0:T(8,128)(2,1)}, u32[]{:S(2)}, u32[]{:S(2)}) collective-permute-start(bf16[32,4,16,128]{3,2,1,0:T(8,128)(2,1)} %constant_dynamic-slice_fusion.12), channel_id=1, source_target_pairs={{0,1},{1,2},{2,3},{3,0},{4,5},{5,6},{6,7},{7,4},{8,9},{9,10},{10,1... | collective-permute-start | bytes 1572872 | tf_op jit(solution)/shard_map/ppermute | solution.py:51
  11.6 10.8 %copy-start.3 = (f32[4,64]{1,0:T(4,128)S(1)}, f32[4,64]{1,0:T(4,128)}, u32[]{:S(2)}) copy-start(f32[4,64]{1,0:T(4,128)} %param.7) | copy-start | bytes 3076
  11.6 31.6 %collective-permute-start.2 = (bf16[32,4,16,128]{3,2,1,0:T(8,128)(2,1)}, bf16[32,4,16,128]{3,2,1,0:T(8,128)(2,1)}, u32[]{:S(2)}, u32[]{:S(2)}) collective-permute-start(bf16[32,4,16,128]{3,2,1,0:T(8,128)(2,1)} %constant_dynamic-slice_fusion.18), channel_id=1, source_target_pairs={{0,3},{1,0},{2,1},{3,2},{4,7},{5,4},{6,5},{7,6},{8,11},{9,8},{10,9... | collective-permute-start | bytes 1572872 | tf_op jit(solution)/shard_map/ppermute | solution.py:51
  14.0 36.7 %collective-permute-start.1 = (bf16[32,4,16,128]{3,2,1,0:T(8,128)(2,1)}, bf16[32,4,16,128]{3,2,1,0:T(8,128)(2,1)}, u32[]{:S(2)}, u32[]{:S(2)}) collective-permute-start(bf16[32,4,16,128]{3,2,1,0:T(8,128)(2,1)} %constant_dynamic-slice_fusion.19), channel_id=1, source_target_pairs={{0,2},{1,3},{2,0},{3,1},{4,6},{5,7},{6,4},{7,5},{8,10},{9,11},{10,... | collective-permute-start | bytes 1572872 | tf_op jit(solution)/shard_map/ppermute | solution.py:51
  22.5 31.6 %collective-permute-start = (bf16[32,4,16,128]{3,2,1,0:T(8,128)(2,1)}, bf16[32,4,16,128]{3,2,1,0:T(8,128)(2,1)S(1)}, u32[]{:S(2)}, u32[]{:S(2)}) collective-permute-start(bf16[32,4,16,128]{3,2,1,0:T(8,128)(2,1)} %constant_dynamic-slice_fusion.20), channel_id=1, source_target_pairs={{0,1},{1,2},{2,3},{3,0},{4,5},{5,6},{6,7},{7,4},{8,9},{9,10},{10,1... | collective-permute-start | bytes 1572872 | tf_op jit(solution)/shard_map/ppermute | solution.py:51
  40.5 25.0 %collective-permute-start.9 = (bf16[32,4,16,128]{3,2,1,0:T(8,128)(2,1)}, bf16[32,4,16,128]{3,2,1,0:T(8,128)(2,1)}, u32[]{:S(2)}, u32[]{:S(2)}) collective-permute-start(bf16[32,4,16,128]{3,2,1,0:T(8,128)(2,1)} %constant_dynamic-slice_fusion.9), channel_id=1, source_target_pairs={{0,1},{1,2},{2,3},{3,0},{4,5},{5,6},{6,7},{7,4},{8,9},{9,10},{10,1... | collective-permute-start | bytes 1572872 | tf_op jit(solution)/shard_map/ppermute | solution.py:51
  40.5 25.0 %collective-permute-start.10 = (bf16[32,4,16,128]{3,2,1,0:T(8,128)(2,1)S(1)}, bf16[32,4,16,128]{3,2,1,0:T(8,128)(2,1)}, u32[]{:S(2)}, u32[]{:S(2)}) collective-permute-start(bf16[32,4,16,128]{3,2,1,0:T(8,128)(2,1)S(1)} %constant_dynamic-slice_fusion.8), channel_id=1, source_target_pairs={{0,2},{1,3},{2,0},{3,1},{4,6},{5,7},{6,4},{7,5},{8,10},{9,11},{10,... | collective-permute-start | bytes 1572872 | tf_op jit(solution)/shard_map/ppermute | solution.py:51
  43.2 28.6 %collective-permute-start.11 = (bf16[32,4,16,128]{3,2,1,0:T(8,128)(2,1)}, bf16[32,4,16,128]{3,2,1,0:T(8,128)(2,1)}, u32[]{:S(2)}, u32[]{:S(2)}) collective-permute-start(bf16[32,4,16,128]{3,2,1,0:T(8,128)(2,1)} %constant_dynamic-slice_fusion.7), channel_id=1, source_target_pairs={{0,3},{1,0},{2,1},{3,2},{4,7},{5,4},{6,5},{7,6},{8,11},{9,8},{10,9... | collective-permute-start | bytes 1572872 | tf_op jit(solution)/shard_map/ppermute | solution.py:51
  61.9 26.0 %collective-permute-start.3 = (bf16[32,4,16,128]{3,2,1,0:T(8,128)(2,1)S(1)}, bf16[32,4,16,128]{3,2,1,0:T(8,128)(2,1)S(1)}, u32[]{:S(2)}, u32[]{:S(2)}) collective-permute-start(bf16[32,4,16,128]{3,2,1,0:T(8,128)(2,1)S(1)} %constant_dynamic-slice_fusion.16), channel_id=1, source_target_pairs={{0,1},{1,2},{2,3},{3,0},{4,5},{5,6},{6,7},{7,4},{8,9},{9,10},{10,1... | collective-permute-start | bytes 1572872 | tf_op jit(solution)/shard_map/ppermute | solution.py:51
  62.0 25.9 %collective-permute-start.4 = (bf16[32,4,16,128]{3,2,1,0:T(8,128)(2,1)S(1)}, bf16[32,4,16,128]{3,2,1,0:T(8,128)(2,1)S(1)}, u32[]{:S(2)}, u32[]{:S(2)}) collective-permute-start(bf16[32,4,16,128]{3,2,1,0:T(8,128)(2,1)S(1)} %constant_dynamic-slice_fusion.15), channel_id=1, source_target_pairs={{0,2},{1,3},{2,0},{3,1},{4,6},{5,7},{6,4},{7,5},{8,10},{9,11},{10,... | collective-permute-start | bytes 1572872 | tf_op jit(solution)/shard_map/ppermute | solution.py:51
  65.5 28.7 %collective-permute-start.5 = (bf16[32,4,16,128]{3,2,1,0:T(8,128)(2,1)S(1)}, bf16[32,4,16,128]{3,2,1,0:T(8,128)(2,1)S(1)}, u32[]{:S(2)}, u32[]{:S(2)}) collective-permute-start(bf16[32,4,16,128]{3,2,1,0:T(8,128)(2,1)S(1)} %constant_dynamic-slice_fusion.14), channel_id=1, source_target_pairs={{0,3},{1,0},{2,1},{3,2},{4,7},{5,4},{6,5},{7,6},{8,11},{9,8},{10,9... | collective-permute-start | bytes 1572872 | tf_op jit(solution)/shard_map/ppermute | solution.py:51
  74.8 20.4 %collective-permute-start.12 = (bf16[32,1,64,128]{3,2,1,0:T(8,128)(2,1)S(1)}, bf16[32,1,64,128]{3,2,1,0:T(8,128)(2,1)S(1)}, u32[]{:S(2)}, u32[]{:S(2)}) collective-permute-start(bf16[32,1,64,128]{3,2,1,0:T(8,128)(2,1)S(1)} %get-tuple-element.55), channel_id=1, source_target_pairs={{4,0},{8,4},{12,8},{16,12},{20,16},{24,20},{28,24},{5,1},{9,5},{13... | collective-permute-start | bytes 1572872 | tf_op jit(solution)/shard_map/ppermute | solution.py:24
  76.1 26.4 %collective-permute-start.13 = (bf16[32,1,64,128]{3,2,1,0:T(8,128)(2,1)S(1)}, bf16[32,1,64,128]{3,2,1,0:T(8,128)(2,1)S(1)}, u32[]{:S(2)}, u32[]{:S(2)}) collective-permute-start(bf16[32,1,64,128]{3,2,1,0:T(8,128)(2,1)S(1)} %get-tuple-element.56), channel_id=1, source_target_pairs={{0,4},{4,8},{8,12},{12,16},{16,20},{20,24},{24,28},{1,5},{5,9},{9,... | collective-permute-start | bytes 1572872 | tf_op jit(solution)/shard_map/ppermute | solution.py:22
  94.5 8.1 %copy-start.1 = (f32[4,64]{1,0:T(4,128)S(1)}, f32[4,64]{1,0:T(4,128)}, u32[]{:S(2)}) copy-start(f32[4,64]{1,0:T(4,128)} %param.9) | copy-start | bytes 3076
  112.0 18.6 %collective-permute-start.14 = (bf16[1,256,256]{2,1,0:T(8,128)(2,1)S(1)}, bf16[1,256,256]{2,1,0:T(8,128)(2,1)S(1)}, u32[]{:S(2)}, u32[]{:S(2)}) collective-permute-start(bf16[1,256,256]{2,1,0:T(8,128)(2,1)S(1)} %constant_dynamic-slice_fusion.6), channel_id=1, source_target_pairs={{0,16},{4,20},{8,24},{12,28},{16,0},{20,4},{24,8},{28,12},{1,17},{... | collective-permute-start | bytes 393224 | tf_op jit(solution)/shard_map/ppermute | solution.py:51
  114.7 17.9 %collective-permute-start.15 = (bf16[1,256,256]{2,1,0:T(8,128)(2,1)S(1)}, bf16[1,256,256]{2,1,0:T(8,128)(2,1)S(1)}, u32[]{:S(2)}, u32[]{:S(2)}) collective-permute-start(bf16[1,256,256]{2,1,0:T(8,128)(2,1)S(1)} %constant_dynamic-slice_fusion.5), channel_id=1, source_target_pairs={{0,12},{4,16},{8,20},{12,24},{16,28},{20,0},{24,4},{28,8},{1,13},{... | collective-permute-start | bytes 393224 | tf_op jit(solution)/shard_map/ppermute | solution.py:51
  115.7 19.7 %collective-permute-start.16 = (bf16[1,256,256]{2,1,0:T(8,128)(2,1)S(1)}, bf16[1,256,256]{2,1,0:T(8,128)(2,1)S(1)}, u32[]{:S(2)}, u32[]{:S(2)}) collective-permute-start(bf16[1,256,256]{2,1,0:T(8,128)(2,1)S(1)} %constant_dynamic-slice_fusion.4), channel_id=1, source_target_pairs={{0,20},{4,24},{8,28},{12,0},{16,4},{20,8},{24,12},{28,16},{1,21},{... | collective-permute-start | bytes 393224 | tf_op jit(solution)/shard_map/ppermute | solution.py:51
  118.6 16.7 %collective-permute-start.17 = (bf16[1,256,256]{2,1,0:T(8,128)(2,1)S(1)}, bf16[1,256,256]{2,1,0:T(8,128)(2,1)S(1)}, u32[]{:S(2)}, u32[]{:S(2)}) collective-permute-start(bf16[1,256,256]{2,1,0:T(8,128)(2,1)S(1)} %constant_dynamic-slice_fusion.3), channel_id=1, source_target_pairs={{0,8},{4,12},{8,16},{12,20},{16,24},{20,28},{24,0},{28,4},{1,9},{5... | collective-permute-start | bytes 393224 | tf_op jit(solution)/shard_map/ppermute | solution.py:51
  118.7 16.7 %collective-permute-start.18 = (bf16[1,256,256]{2,1,0:T(8,128)(2,1)S(1)}, bf16[1,256,256]{2,1,0:T(8,128)(2,1)S(1)}, u32[]{:S(2)}, u32[]{:S(2)}) collective-permute-start(bf16[1,256,256]{2,1,0:T(8,128)(2,1)S(1)} %constant_dynamic-slice_fusion.2), channel_id=1, source_target_pairs={{0,24},{4,28},{8,0},{12,4},{16,8},{20,12},{24,16},{28,20},{1,25},{... | collective-permute-start | bytes 393224 | tf_op jit(solution)/shard_map/ppermute | solution.py:51
  130.6 7.8 %collective-permute-start.19 = (bf16[1,256,256]{2,1,0:T(8,128)(2,1)S(1)}, bf16[1,256,256]{2,1,0:T(8,128)(2,1)S(1)}, u32[]{:S(2)}, u32[]{:S(2)}) collective-permute-start(bf16[1,256,256]{2,1,0:T(8,128)(2,1)S(1)} %constant_dynamic-slice_fusion.1), channel_id=1, source_target_pairs={{0,4},{4,8},{8,12},{12,16},{16,20},{20,24},{24,28},{28,0},{1,5},{5... | collective-permute-start | bytes 393224 | tf_op jit(solution)/shard_map/ppermute | solution.py:51
  132.5 6.4 %collective-permute-start.20 = (bf16[1,256,256]{2,1,0:T(8,128)(2,1)S(1)}, bf16[1,256,256]{2,1,0:T(8,128)(2,1)S(1)}, u32[]{:S(2)}, u32[]{:S(2)}) collective-permute-start(bf16[1,256,256]{2,1,0:T(8,128)(2,1)S(1)} %constant_dynamic-slice_fusion), channel_id=1, source_target_pairs={{0,28},{4,0},{8,4},{12,8},{16,12},{20,16},{24,20},{28,24},{1,29},{... | collective-permute-start | bytes 393224 | tf_op jit(solution)/shard_map/ppermute | solution.py:51

commit v26 on v21

--- a/solution.py
+++ b/solution.py
@@ -198,7 +198,7 @@
     field_f32 = direct_modes.astype(jnp.float32)
     forward = padded[:, 2:].astype(jnp.float32)
     behind = padded[:, :-2].astype(jnp.float32)
-    radial_pad = jnp.pad(field_f32, ((0, 0), (0, 0), (1, 1), (0, 0)))
+    radial_pad = jnp.pad(direct_modes, ((0, 0), (0, 0), (1, 1), (0, 0))).astype(jnp.float32)
     outward = radial_pad[:, :, 2:]
     inward = radial_pad[:, :, :-2]
     radius = 0.25 + (jnp.arange(radial_cells, dtype=jnp.float32) + 0.5) / radial_cells

time: 152 us -> 151 us (level)
    ppermute x1, waiting for transfers between devices: 7.19 us -> 5.66 us  [padded_2(): lax.ppermute(tail, axis, [(i, (i + 1) % count) for i in range(ends)])]
  transfers between devices with their start and end apart: 21 -> 21, of which waited for: 13 -> 13; matrix products, arithmetic and copies ran while one was open for 24% -> 25% of each run, Pallas kernels for 5% -> 5%
where the time goes in v26:
time: 151 us; the launch traced here: 150 us
  waiting for transfers between devices  47.9 us (32%)
  local copies, waits for them, and re-layouts  34.9 us (23%)
  starting transfers between devices  31.9 us (21%)
  other arithmetic  14.7 us (10%)
  blocking collectives  11.7 us (8%)
  Pallas kernels  7.13 us (5%)
    ppermute x19, waiting for transfers between devices, exchange(): lax.ppermute(piece, axis, [(j, (j + shift) % count) for j in range(count)])  42.3 us
    ppermute x19, starting transfers between devices, exchange(): lax.ppermute(piece, axis, [(j, (j + shift) % count) for j in range(count)])  25.9 us
    unnamed x20, local copies, waits for them, and re-layouts  20.7 us
    all_to_all x1, blocking collectives, gather_small(): return lax.all_to_all(copies, axis, split_axis=0, concat_axis=0, tiled=True)  11.7 us
    dynamic_slice x20, local copies, waits for them, and re-layouts, exchange(): lax.dynamic_slice_in_dim(source, (here + shift) % count * width, width, a...  11.2 us
    pallas_call x2, Pallas kernels, dft(): pl.pallas_call(functools.partial(dft_kernel, count=count, weighted=weight...  7.13 us
    ppermute x1, waiting for transfers between devices, padded_2(): lax.ppermute(tail, axis, [(i, (i + 1) % count) for i in range(ends)])  5.66 us
    convert_element_type x1, other arithmetic, local(): image = (-velocity * (forward - behind) * 0.5 + diffusion * (forward + be...  5.55 us
  transfers between devices with their start and end apart: 21, of which 13 were waited for; matrix products, arithmetic and copies ran while one was open for 25% of the time, Pallas kernels for 5%

profile of v26, /device:TPU:0, one launch (start us, length us, event | category | flops | bytes accessed | tf_op | source)
XLA Modules:
  0.0 150.3 jit_solution(822581659107773189)
XLA Ops:
  0.7 1.2 constant_dynamic-slice_fusion.10
  1.9 2.5 %collective-permute-start.8 = (bf16[32,4,16,128]{3,2,1,0:T(8,128)(2,1)S(1)}, bf16[32,4,16,128]{3,2,1,0:T(8,128)(2,1)S(1)}, u32[]{:S(2)}, u32[]{:S(2)}) collective-permute-start(bf16[32,4,16,128]{3,2,1,0:T(8,128)(2,1)S(1)} %constant_dynamic-slice_fusion.10), channel_id=1, source_target_pairs={{0,3},{1,0},{2,1},{3,2},{4,7},{5,4},{6,5},{7,6},{8,11},{9,8},{10,9... | collective-permute-start | bytes 1572872 | tf_op jit(solution)/shard_map/ppermute | solution.py:51
  4.4 1.9 %constant_dynamic-slice_fusion.11 = bf16[32,4,16,128]{3,2,1,0:T(8,128)(2,1)} fusion(bf16[32,4,64,128]{3,2,1,0:T(8,128)(2,1)} %param.5, s32[]{:T(128)S(6)} %select_n.220), kind=kLoop, calls=%fused_computation.109 | loop fusion | bytes 1048580 | tf_op jit(solution)/shard_map/dynamic_slice | solution.py:49
  6.9 1.9 %constant_dynamic-slice_fusion.12 = bf16[32,4,16,128]{3,2,1,0:T(8,128)(2,1)} fusion(bf16[32,4,64,128]{3,2,1,0:T(8,128)(2,1)} %param.5, s32[]{:T(128)S(6)} %select_n.218), kind=kLoop, calls=%fused_computation.110 | loop fusion | bytes 1048580 | tf_op jit(solution)/shard_map/dynamic_slice | solution.py:49
  9.0 1.9 %constant_dynamic-slice_fusion.18 = bf16[32,4,16,128]{3,2,1,0:T(8,128)(2,1)} fusion(bf16[32,4,64,128]{3,2,1,0:T(8,128)(2,1)} %param.6, s32[]{:T(128)S(6)} %select_n.222), kind=kLoop, calls=%fused_computation.116 | loop fusion | bytes 1048580 | tf_op jit(solution)/shard_map/dynamic_slice | solution.py:49
  10.9 1.6 %collective-permute-start.2 = (bf16[32,4,16,128]{3,2,1,0:T(8,128)(2,1)}, bf16[32,4,16,128]{3,2,1,0:T(8,128)(2,1)}, u32[]{:S(2)}, u32[]{:S(2)}) collective-permute-start(bf16[32,4,16,128]{3,2,1,0:T(8,128)(2,1)} %constant_dynamic-slice_fusion.18), channel_id=1, source_target_pairs={{0,3},{1,0},{2,1},{3,2},{4,7},{5,4},{6,5},{7,6},{8,11},{9,8},{10,9... | collective-permute-start | bytes 1572872 | tf_op jit(solution)/shard_map/ppermute | solution.py:51
  12.4 0.9 constant_dynamic-slice_fusion.19
  13.3 1.4 collective-permute-start.1
  18.2 1.3 constant_dynamic-slice_fusion.13
  19.6 1.2 copy.40
  20.8 1.2 copy.44
  22.8 2.2 %copy.37 = bf16[4,8,64,128]{3,1,2,0:T(8,128)(2,1)} copy(bf16[4,8,64,128]{3,2,1,0:T(8,128)(2,1)} %bitcast.111) | data formatting | bytes 1048576
  25.0 2.1 %collective-permute-done.7 = bf16[32,4,16,128]{3,2,1,0:T(8,128)(2,1)} collective-permute-done((bf16[32,4,16,128]{3,2,1,0:T(8,128)(2,1)}, bf16[32,4,16,128]{3,2,1,0:T(8,128)(2,1)}, u32[]{:S(2)}, u32[]{:S(2)}) %collective-permute-start.7) | collective-permute-done | bytes 524320 | tf_op jit(solution)/shard_map/ppermute | solution.py:51
  27.1 2.2 %copy.38 = bf16[4,8,64,128]{3,1,2,0:T(8,128)(2,1)} copy(bf16[4,8,64,128]{3,2,1,0:T(8,128)(2,1)} %bitcast.44) | data formatting | bytes 1048576
  29.3 1.8 %collective-permute-done.6 = bf16[32,4,16,128]{3,2,1,0:T(8,128)(2,1)} collective-permute-done((bf16[32,4,16,128]{3,2,1,0:T(8,128)(2,1)}, bf16[32,4,16,128]{3,2,1,0:T(8,128)(2,1)}, u32[]{:S(2)}, u32[]{:S(2)}) %collective-permute-start.6) | collective-permute-done | bytes 524320 | tf_op jit(solution)/shard_map/ppermute | solution.py:51
  31.0 2.2 %copy.39 = bf16[4,8,64,128]{3,1,2,0:T(8,128)(2,1)} copy(bf16[4,8,64,128]{3,2,1,0:T(8,128)(2,1)} %bitcast.41) | data formatting | bytes 1048576
  33.2 3.5 %shard_map.77 = bf16[128,8192]{1,0:T(8,128)(2,1)} custom-call(bf16[128,256]{1,0:T(8,128)(2,1)} %concatenate.23.refs_0_, bf16[32,8192]{1,0:T(8,128)(2,1)} %bitcast.104, bf16[32,8192]{1,0:T(8,128)(2,1)} %bitcast.110, bf16[32,8192]{1,0:T(8,128)(2,1)} %bitcast.108, bf16[32,8192]{1,0:T(8,128)(2,1)} %bitcast.106), custom_call_target="tpu_custom_call" | custom-call | tf_op jit(solution)/shard_map/pallas_call | solution.py:115
  36.7 2.2 %copy.28 = bf16[16,8,64,128]{3,2,1,0:T(8,128)(2,1)S(1)} copy(bf16[16,8,64,128]{3,1,2,0:T(8,128)(2,1)} %bitcast.84) | data formatting | bytes 4194304
  39.8 1.8 %collective-permute-start.10 = (bf16[32,4,16,128]{3,2,1,0:T(8,128)(2,1)S(1)}, bf16[32,4,16,128]{3,2,1,0:T(8,128)(2,1)}, u32[]{:S(2)}, u32[]{:S(2)}) collective-permute-start(bf16[32,4,16,128]{3,2,1,0:T(8,128)(2,1)S(1)} %constant_dynamic-slice_fusion.8), channel_id=1, source_target_pairs={{0,2},{1,3},{2,0},{3,1},{4,6},{5,7},{6,4},{7,5},{8,10},{9,11},{10,... | collective-permute-start | bytes 1572872 | tf_op jit(solution)/shard_map/ppermute | solution.py:51
  41.7 1.5 collective-permute-start.11
  43.2 2.2 %copy.41 = bf16[4,8,64,128]{3,1,2,0:T(8,128)(2,1)} copy(bf16[4,8,64,128]{3,2,1,0:T(8,128)(2,1)} %bitcast.32) | data formatting | bytes 1048576
  45.4 4.2 %collective-permute-done.1 = bf16[32,4,16,128]{3,2,1,0:T(8,128)(2,1)} collective-permute-done((bf16[32,4,16,128]{3,2,1,0:T(8,128)(2,1)}, bf16[32,4,16,128]{3,2,1,0:T(8,128)(2,1)}, u32[]{:S(2)}, u32[]{:S(2)}) %collective-permute-start.1) | collective-permute-done | bytes 524320 | tf_op jit(solution)/shard_map/ppermute | solution.py:51
  49.6 2.2 %copy.42 = bf16[4,8,64,128]{3,1,2,0:T(8,128)(2,1)} copy(bf16[4,8,64,128]{3,2,1,0:T(8,128)(2,1)} %bitcast.29) | data formatting | bytes 1048576
  51.8 1.7 %collective-permute-done = bf16[32,4,16,128]{3,2,1,0:T(8,128)(2,1)} collective-permute-done((bf16[32,4,16,128]{3,2,1,0:T(8,128)(2,1)}, bf16[32,4,16,128]{3,2,1,0:T(8,128)(2,1)}, u32[]{:S(2)}, u32[]{:S(2)}) %collective-permute-start) | collective-permute-done | bytes 524320 | tf_op jit(solution)/shard_map/ppermute | solution.py:51
  53.5 2.2 %copy.43 = bf16[4,8,64,128]{3,1,2,0:T(8,128)(2,1)} copy(bf16[4,8,64,128]{3,2,1,0:T(8,128)(2,1)} %bitcast.26) | data formatting | bytes 1048576
  56.4 3.7 %shard_map.76 = bf16[128,8192]{1,0:T(8,128)(2,1)} custom-call(bf16[128,256]{1,0:T(8,128)(2,1)} %concatenate.23.refs_0_, bf16[32,8192]{1,0:T(8,128)(2,1)} %bitcast.103, bf16[32,8192]{1,0:T(8,128)(2,1)} %bitcast.109, bf16[32,8192]{1,0:T(8,128)(2,1)} %bitcast.107, bf16[32,8192]{1,0:T(8,128)(2,1)} %bitcast.105, f32[1,8192]{1,0:T(1,128)} %bitcast.115), custom_call_target="tpu_custom_call" | custom-call | tf_op jit(solution)/shard_map/pallas_call | solution.py:115
  60.0 2.2 %copy.23 = bf16[16,8,64,128]{3,2,1,0:T(8,128)(2,1)S(1)} copy(bf16[16,8,64,128]{3,1,2,0:T(8,128)(2,1)} %bitcast.83) | data formatting | bytes 4194304
  62.4 1.8 %collective-permute-start.4 = (bf16[32,4,16,128]{3,2,1,0:T(8,128)(2,1)S(1)}, bf16[32,4,16,128]{3,2,1,0:T(8,128)(2,1)S(1)}, u32[]{:S(2)}, u32[]{:S(2)}) collective-permute-start(bf16[32,4,16,128]{3,2,1,0:T(8,128)(2,1)S(1)} %constant_dynamic-slice_fusion.15), channel_id=1, source_target_pairs={{0,2},{1,3},{2,0},{3,1},{4,6},{5,7},{6,4},{7,5},{8,10},{9,11},{10,... | collective-permute-start | bytes 1572872 | tf_op jit(solution)/shard_map/ppermute | solution.py:51
  64.7 1.1 collective-permute-start.5
  65.8 4.8 %collective-permute-done.11 = bf16[32,4,16,128]{3,2,1,0:T(8,128)(2,1)} collective-permute-done((bf16[32,4,16,128]{3,2,1,0:T(8,128)(2,1)S(1)}, bf16[32,4,16,128]{3,2,1,0:T(8,128)(2,1)}, u32[]{:S(2)}, u32[]{:S(2)}) %collective-permute-start.11) | collective-permute-done | bytes 524320 | tf_op jit(solution)/shard_map/ppermute | solution.py:51
  70.6 1.6 %pad_maximum_fusion.11 = bf16[4,32,4,16,128]{4,3,2,1,0:T(8,128)(2,1)S(1)} fusion(bf16[1,32,4,16,128]{4,3,2,1,0:T(8,128)(2,1)} %bitcast.13, bf16[1,32,4,16,128]{4,3,2,1,0:T(8,128)(2,1)} %bitcast.12, bf16[1,32,4,16,128]{4,3,2,1,0:T(8,128)(2,1)} %bitcast.11, bf16[1,32,4,16,128]{4,3,2,1,0:T(8,128)(2,1)S(1)} %dynamic-slice_bitcast_fusion.4), kind=kLoop, calls=%fused_computation.25 | loop fusion | flops 3145728 | bytes 4194304 | tf_op jit(solution)/shard_map/stack | solution.py:59
  73.1 1.3 collective-permute-start.12
  74.4 4.8 %collective-permute-start.13 = (bf16[32,1,64,128]{3,2,1,0:T(8,128)(2,1)S(1)}, bf16[32,1,64,128]{3,2,1,0:T(8,128)(2,1)S(1)}, u32[]{:S(2)}, u32[]{:S(2)}) collective-permute-start(bf16[32,1,64,128]{3,2,1,0:T(8,128)(2,1)S(1)} %get-tuple-element.56), channel_id=1, source_target_pairs={{0,4},{4,8},{8,12},{12,16},{16,20},{20,24},{24,28},{1,5},{5,9},{9,... | collective-permute-start | bytes 1572872 | tf_op jit(solution)/shard_map/ppermute | solution.py:22
  79.2 7.9 %collective-permute-done.3 = bf16[32,4,16,128]{3,2,1,0:T(8,128)(2,1)S(1)} collective-permute-done((bf16[32,4,16,128]{3,2,1,0:T(8,128)(2,1)S(1)}, bf16[32,4,16,128]{3,2,1,0:T(8,128)(2,1)S(1)}, u32[]{:S(2)}, u32[]{:S(2)}) %collective-permute-start.3) | collective-permute-done | bytes 524320 | tf_op jit(solution)/shard_map/ppermute | solution.py:51
  87.1 6.0 %collective-permute-done.5 = bf16[32,4,16,128]{3,2,1,0:T(8,128)(2,1)S(1)} collective-permute-done((bf16[32,4,16,128]{3,2,1,0:T(8,128)(2,1)S(1)}, bf16[32,4,16,128]{3,2,1,0:T(8,128)(2,1)S(1)}, u32[]{:S(2)}, u32[]{:S(2)}) %collective-permute-start.5) | collective-permute-done | bytes 524320 | tf_op jit(solution)/shard_map/ppermute | solution.py:51
  94.1 1.0 pad_convert_fusion
  95.2 5.7 %collective-permute-done.13 = bf16[32,1,64,128]{3,2,1,0:T(8,128)(2,1)S(1)} collective-permute-done((bf16[32,1,64,128]{3,2,1,0:T(8,128)(2,1)S(1)}, bf16[32,1,64,128]{3,2,1,0:T(8,128)(2,1)S(1)}, u32[]{:S(2)}, u32[]{:S(2)}) %collective-permute-start.13) | collective-permute-done | bytes 524320 | tf_op jit(solution)/shard_map/ppermute | solution.py:22
  100.8 5.5 %fusion.3 = bf16[32,4,64,128]{3,2,1,0:T(8,128)(2,1)S(1)} fusion(f32[32,4,66,128]{3,2,1,0:T(8,128)S(1)} %pad_convert_fusion, bf16[32,1,64,128]{3,2,1,0:T(8,128)(2,1)S(1)} %collective-permute-done.13, bf16[32,4,16,128]{3,2,1,0:T(8,128)(2,1)S(1)} %get-tuple-element.58, bf16[32,4,16,128]{3,2,1,0:T(8,128)(2,1)S(1)} %get-tuple-element.59, ...), kind=kLoop, calls=%fused_computation.7 | loop fusion | flops 42991616 | bytes 13641728 | tf_op jit(solution)/shard_map/convert_element_type | solution.py:222
  108.0 1.2 fusion.12
  109.9 2.7 %collective-permute-start.14 = (bf16[1,256,256]{2,1,0:T(8,128)(2,1)S(1)}, bf16[1,256,256]{2,1,0:T(8,128)(2,1)S(1)}, u32[]{:S(2)}, u32[]{:S(2)}) collective-permute-start(bf16[1,256,256]{2,1,0:T(8,128)(2,1)S(1)} %constant_dynamic-slice_fusion.6), channel_id=1, source_target_pairs={{0,16},{4,20},{8,24},{12,28},{16,0},{20,4},{24,8},{28,12},{1,17},{... | collective-permute-start | bytes 393224 | tf_op jit(solution)/shard_map/ppermute | solution.py:51
  112.6 1.0 collective-permute-start.15
  113.6 2.9 %collective-permute-start.16 = (bf16[1,256,256]{2,1,0:T(8,128)(2,1)S(1)}, bf16[1,256,256]{2,1,0:T(8,128)(2,1)S(1)}, u32[]{:S(2)}, u32[]{:S(2)}) collective-permute-start(bf16[1,256,256]{2,1,0:T(8,128)(2,1)S(1)} %constant_dynamic-slice_fusion.4), channel_id=1, source_target_pairs={{0,20},{4,24},{8,28},{12,0},{16,4},{20,8},{24,12},{28,16},{1,21},{... | collective-permute-start | bytes 393224 | tf_op jit(solution)/shard_map/ppermute | solution.py:51
  116.6 3.8 %collective-permute-start.18 = (bf16[1,256,256]{2,1,0:T(8,128)(2,1)S(1)}, bf16[1,256,256]{2,1,0:T(8,128)(2,1)S(1)}, u32[]{:S(2)}, u32[]{:S(2)}) collective-permute-start(bf16[1,256,256]{2,1,0:T(8,128)(2,1)S(1)} %constant_dynamic-slice_fusion.2), channel_id=1, source_target_pairs={{0,24},{4,28},{8,0},{12,4},{16,8},{20,12},{24,16},{28,20},{1,25},{... | collective-permute-start | bytes 393224 | tf_op jit(solution)/shard_map/ppermute | solution.py:51
  120.5 8.0 %collective-permute-done.14 = bf16[1,256,256]{2,1,0:T(8,128)(2,1)S(1)} collective-permute-done((bf16[1,256,256]{2,1,0:T(8,128)(2,1)S(1)}, bf16[1,256,256]{2,1,0:T(8,128)(2,1)S(1)}, u32[]{:S(2)}, u32[]{:S(2)}) %collective-permute-start.14) | collective-permute-done | bytes 131104 | tf_op jit(solution)/shard_map/ppermute | solution.py:51
  128.5 1.9 %collective-permute-done.15 = bf16[1,256,256]{2,1,0:T(8,128)(2,1)S(1)} collective-permute-done((bf16[1,256,256]{2,1,0:T(8,128)(2,1)S(1)}, bf16[1,256,256]{2,1,0:T(8,128)(2,1)S(1)}, u32[]{:S(2)}, u32[]{:S(2)}) %collective-permute-start.15) | collective-permute-done | bytes 131104 | tf_op jit(solution)/shard_map/ppermute | solution.py:51
  130.4 2.8 %collective-permute-start.20 = (bf16[1,256,256]{2,1,0:T(8,128)(2,1)S(1)}, bf16[1,256,256]{2,1,0:T(8,128)(2,1)S(1)}, u32[]{:S(2)}, u32[]{:S(2)}) collective-permute-start(bf16[1,256,256]{2,1,0:T(8,128)(2,1)S(1)} %constant_dynamic-slice_fusion), channel_id=1, source_target_pairs={{0,28},{4,0},{8,4},{12,8},{16,12},{20,16},{24,20},{28,24},{1,29},{... | collective-permute-start | bytes 393224 | tf_op jit(solution)/shard_map/ppermute | solution.py:51
  133.3 3.1 %collective-permute-done.19 = bf16[1,256,256]{2,1,0:T(8,128)(2,1)S(1)} collective-permute-done((bf16[1,256,256]{2,1,0:T(8,128)(2,1)S(1)}, bf16[1,256,256]{2,1,0:T(8,128)(2,1)S(1)}, u32[]{:S(2)}, u32[]{:S(2)}) %collective-permute-start.19) | collective-permute-done | bytes 131104 | tf_op jit(solution)/shard_map/ppermute | solution.py:51
  137.2 11.7 %all_to_all.6 = f32[8,1,32]{2,1,0:T(1,128)S(1)} all-to-all(f32[8,1,32]{2,1,0:T(1,128)S(1)} %broadcast_in_dim.5), channel_id=1, replica_groups=mesh['gx'=8,'ka'=4] {'gx'}, dimensions={0} | all-to-all | bytes 2048 | tf_op jit(solution)/shard_map/all_to_all | solution.py:34
  (81 shorter events, 13.8 us)
Async XLA Ops:
  0.6 11.8 %copy-start = (bf16[32,4,64,128]{3,2,1,0:T(8,128)(2,1)S(1)}, bf16[32,4,64,128]{3,2,1,0:T(8,128)(2,1)}, u32[]{:S(2)}) copy-start(bf16[32,4,64,128]{3,2,1,0:T(8,128)(2,1)} %param.6) | copy-start | bytes 6291460
  0.6 15.5 %copy-start.3 = (f32[4,64]{1,0:T(4,128)S(1)}, f32[4,64]{1,0:T(4,128)}, u32[]{:S(2)}) copy-start(f32[4,64]{1,0:T(4,128)} %param.7) | copy-start | bytes 3076
  1.9 15.4 %collective-permute-start.8 = (bf16[32,4,16,128]{3,2,1,0:T(8,128)(2,1)S(1)}, bf16[32,4,16,128]{3,2,1,0:T(8,128)(2,1)S(1)}, u32[]{:S(2)}, u32[]{:S(2)}) collective-permute-start(bf16[32,4,16,128]{3,2,1,0:T(8,128)(2,1)S(1)} %constant_dynamic-slice_fusion.10), channel_id=1, source_target_pairs={{0,3},{1,0},{2,1},{3,2},{4,7},{5,4},{6,5},{7,6},{8,11},{9,8},{10,9... | collective-permute-start | bytes 1572872 | tf_op jit(solution)/shard_map/ppermute | solution.py:51
  6.3 20.8 %collective-permute-start.7 = (bf16[32,4,16,128]{3,2,1,0:T(8,128)(2,1)}, bf16[32,4,16,128]{3,2,1,0:T(8,128)(2,1)}, u32[]{:S(2)}, u32[]{:S(2)}) collective-permute-start(bf16[32,4,16,128]{3,2,1,0:T(8,128)(2,1)} %constant_dynamic-slice_fusion.11), channel_id=1, source_target_pairs={{0,2},{1,3},{2,0},{3,1},{4,6},{5,7},{6,4},{7,5},{8,10},{9,11},{10,... | collective-permute-start | bytes 1572872 | tf_op jit(solution)/shard_map/ppermute | solution.py:51
  6.9 13.9 %copy-start.4 = (f32[4,64]{1,0:T(4,128)S(1)}, f32[4,64]{1,0:T(4,128)}, u32[]{:S(2)}) copy-start(f32[4,64]{1,0:T(4,128)} %param.8) | copy-start | bytes 3076
  8.8 22.2 %collective-permute-start.6 = (bf16[32,4,16,128]{3,2,1,0:T(8,128)(2,1)}, bf16[32,4,16,128]{3,2,1,0:T(8,128)(2,1)}, u32[]{:S(2)}, u32[]{:S(2)}) collective-permute-start(bf16[32,4,16,128]{3,2,1,0:T(8,128)(2,1)} %constant_dynamic-slice_fusion.12), channel_id=1, source_target_pairs={{0,1},{1,2},{2,3},{3,0},{4,5},{5,6},{6,7},{7,4},{8,9},{9,10},{10,1... | collective-permute-start | bytes 1572872 | tf_op jit(solution)/shard_map/ppermute | solution.py:51
  10.9 30.8 %collective-permute-start.2 = (bf16[32,4,16,128]{3,2,1,0:T(8,128)(2,1)}, bf16[32,4,16,128]{3,2,1,0:T(8,128)(2,1)}, u32[]{:S(2)}, u32[]{:S(2)}) collective-permute-start(bf16[32,4,16,128]{3,2,1,0:T(8,128)(2,1)} %constant_dynamic-slice_fusion.18), channel_id=1, source_target_pairs={{0,3},{1,0},{2,1},{3,2},{4,7},{5,4},{6,5},{7,6},{8,11},{9,8},{10,9... | collective-permute-start | bytes 1572872 | tf_op jit(solution)/shard_map/ppermute | solution.py:51
  13.3 36.2 %collective-permute-start.1 = (bf16[32,4,16,128]{3,2,1,0:T(8,128)(2,1)}, bf16[32,4,16,128]{3,2,1,0:T(8,128)(2,1)}, u32[]{:S(2)}, u32[]{:S(2)}) collective-permute-start(bf16[32,4,16,128]{3,2,1,0:T(8,128)(2,1)} %constant_dynamic-slice_fusion.19), channel_id=1, source_target_pairs={{0,2},{1,3},{2,0},{3,1},{4,6},{5,7},{6,4},{7,5},{8,10},{9,11},{10,... | collective-permute-start | bytes 1572872 | tf_op jit(solution)/shard_map/ppermute | solution.py:51
  17.4 0.8 copy-start.1
  18.2 35.3 %collective-permute-start = (bf16[32,4,16,128]{3,2,1,0:T(8,128)(2,1)}, bf16[32,4,16,128]{3,2,1,0:T(8,128)(2,1)}, u32[]{:S(2)}, u32[]{:S(2)}) collective-permute-start(bf16[32,4,16,128]{3,2,1,0:T(8,128)(2,1)} %constant_dynamic-slice_fusion.20), channel_id=1, source_target_pairs={{0,1},{1,2},{2,3},{3,0},{4,5},{5,6},{6,7},{7,4},{8,9},{9,10},{10,1... | collective-permute-start | bytes 1572872 | tf_op jit(solution)/shard_map/ppermute | solution.py:51
  39.8 25.0 %collective-permute-start.9 = (bf16[32,4,16,128]{3,2,1,0:T(8,128)(2,1)}, bf16[32,4,16,128]{3,2,1,0:T(8,128)(2,1)}, u32[]{:S(2)}, u32[]{:S(2)}) collective-permute-start(bf16[32,4,16,128]{3,2,1,0:T(8,128)(2,1)} %constant_dynamic-slice_fusion.9), channel_id=1, source_target_pairs={{0,1},{1,2},{2,3},{3,0},{4,5},{5,6},{6,7},{7,4},{8,9},{9,10},{10,1... | collective-permute-start | bytes 1572872 | tf_op jit(solution)/shard_map/ppermute | solution.py:51
  39.8 26.0 %collective-permute-start.10 = (bf16[32,4,16,128]{3,2,1,0:T(8,128)(2,1)S(1)}, bf16[32,4,16,128]{3,2,1,0:T(8,128)(2,1)}, u32[]{:S(2)}, u32[]{:S(2)}) collective-permute-start(bf16[32,4,16,128]{3,2,1,0:T(8,128)(2,1)S(1)} %constant_dynamic-slice_fusion.8), channel_id=1, source_target_pairs={{0,2},{1,3},{2,0},{3,1},{4,6},{5,7},{6,4},{7,5},{8,10},{9,11},{10,... | collective-permute-start | bytes 1572872 | tf_op jit(solution)/shard_map/ppermute | solution.py:51
  41.7 28.9 %collective-permute-start.11 = (bf16[32,4,16,128]{3,2,1,0:T(8,128)(2,1)S(1)}, bf16[32,4,16,128]{3,2,1,0:T(8,128)(2,1)}, u32[]{:S(2)}, u32[]{:S(2)}) collective-permute-start(bf16[32,4,16,128]{3,2,1,0:T(8,128)(2,1)S(1)} %constant_dynamic-slice_fusion.7), channel_id=1, source_target_pairs={{0,3},{1,0},{2,1},{3,2},{4,7},{5,4},{6,5},{7,6},{8,11},{9,8},{10,9... | collective-permute-start | bytes 1572872 | tf_op jit(solution)/shard_map/ppermute | solution.py:51
  62.3 24.8 %collective-permute-start.3 = (bf16[32,4,16,128]{3,2,1,0:T(8,128)(2,1)S(1)}, bf16[32,4,16,128]{3,2,1,0:T(8,128)(2,1)S(1)}, u32[]{:S(2)}, u32[]{:S(2)}) collective-permute-start(bf16[32,4,16,128]{3,2,1,0:T(8,128)(2,1)S(1)} %constant_dynamic-slice_fusion.16), channel_id=1, source_target_pairs={{0,1},{1,2},{2,3},{3,0},{4,5},{5,6},{6,7},{7,4},{8,9},{9,10},{10,1... | collective-permute-start | bytes 1572872 | tf_op jit(solution)/shard_map/ppermute | solution.py:51
  62.4 24.7 %collective-permute-start.4 = (bf16[32,4,16,128]{3,2,1,0:T(8,128)(2,1)S(1)}, bf16[32,4,16,128]{3,2,1,0:T(8,128)(2,1)S(1)}, u32[]{:S(2)}, u32[]{:S(2)}) collective-permute-start(bf16[32,4,16,128]{3,2,1,0:T(8,128)(2,1)S(1)} %constant_dynamic-slice_fusion.15), channel_id=1, source_target_pairs={{0,2},{1,3},{2,0},{3,1},{4,6},{5,7},{6,4},{7,5},{8,10},{9,11},{10,... | collective-permute-start | bytes 1572872 | tf_op jit(solution)/shard_map/ppermute | solution.py:51
  64.7 28.3 %collective-permute-start.5 = (bf16[32,4,16,128]{3,2,1,0:T(8,128)(2,1)S(1)}, bf16[32,4,16,128]{3,2,1,0:T(8,128)(2,1)S(1)}, u32[]{:S(2)}, u32[]{:S(2)}) collective-permute-start(bf16[32,4,16,128]{3,2,1,0:T(8,128)(2,1)S(1)} %constant_dynamic-slice_fusion.14), channel_id=1, source_target_pairs={{0,3},{1,0},{2,1},{3,2},{4,7},{5,4},{6,5},{7,6},{8,11},{9,8},{10,9... | collective-permute-start | bytes 1572872 | tf_op jit(solution)/shard_map/ppermute | solution.py:51
  73.1 22.1 %collective-permute-start.12 = (bf16[32,1,64,128]{3,2,1,0:T(8,128)(2,1)S(1)}, bf16[32,1,64,128]{3,2,1,0:T(8,128)(2,1)S(1)}, u32[]{:S(2)}, u32[]{:S(2)}) collective-permute-start(bf16[32,1,64,128]{3,2,1,0:T(8,128)(2,1)S(1)} %get-tuple-element.55), channel_id=1, source_target_pairs={{4,0},{8,4},{12,8},{16,12},{20,16},{24,20},{28,24},{5,1},{9,5},{13... | collective-permute-start | bytes 1572872 | tf_op jit(solution)/shard_map/ppermute | solution.py:24
  74.4 26.4 %collective-permute-start.13 = (bf16[32,1,64,128]{3,2,1,0:T(8,128)(2,1)S(1)}, bf16[32,1,64,128]{3,2,1,0:T(8,128)(2,1)S(1)}, u32[]{:S(2)}, u32[]{:S(2)}) collective-permute-start(bf16[32,1,64,128]{3,2,1,0:T(8,128)(2,1)S(1)} %get-tuple-element.56), channel_id=1, source_target_pairs={{0,4},{4,8},{8,12},{12,16},{16,20},{20,24},{24,28},{1,5},{5,9},{9,... | collective-permute-start | bytes 1572872 | tf_op jit(solution)/shard_map/ppermute | solution.py:22
  94.1 6.7 %copy-start.2 = (f32[4,64]{1,0:T(4,128)S(1)}, f32[4,64]{1,0:T(4,128)}, u32[]{:S(2)}) copy-start(f32[4,64]{1,0:T(4,128)} %param.9) | copy-start | bytes 3076
  109.9 18.6 %collective-permute-start.14 = (bf16[1,256,256]{2,1,0:T(8,128)(2,1)S(1)}, bf16[1,256,256]{2,1,0:T(8,128)(2,1)S(1)}, u32[]{:S(2)}, u32[]{:S(2)}) collective-permute-start(bf16[1,256,256]{2,1,0:T(8,128)(2,1)S(1)} %constant_dynamic-slice_fusion.6), channel_id=1, source_target_pairs={{0,16},{4,20},{8,24},{12,28},{16,0},{20,4},{24,8},{28,12},{1,17},{... | collective-permute-start | bytes 393224 | tf_op jit(solution)/shard_map/ppermute | solution.py:51
  112.6 17.9 %collective-permute-start.15 = (bf16[1,256,256]{2,1,0:T(8,128)(2,1)S(1)}, bf16[1,256,256]{2,1,0:T(8,128)(2,1)S(1)}, u32[]{:S(2)}, u32[]{:S(2)}) collective-permute-start(bf16[1,256,256]{2,1,0:T(8,128)(2,1)S(1)} %constant_dynamic-slice_fusion.5), channel_id=1, source_target_pairs={{0,12},{4,16},{8,20},{12,24},{16,28},{20,0},{24,4},{28,8},{1,13},{... | collective-permute-start | bytes 393224 | tf_op jit(solution)/shard_map/ppermute | solution.py:51
  113.6 19.7 %collective-permute-start.16 = (bf16[1,256,256]{2,1,0:T(8,128)(2,1)S(1)}, bf16[1,256,256]{2,1,0:T(8,128)(2,1)S(1)}, u32[]{:S(2)}, u32[]{:S(2)}) collective-permute-start(bf16[1,256,256]{2,1,0:T(8,128)(2,1)S(1)} %constant_dynamic-slice_fusion.4), channel_id=1, source_target_pairs={{0,20},{4,24},{8,28},{12,0},{16,4},{20,8},{24,12},{28,16},{1,21},{... | collective-permute-start | bytes 393224 | tf_op jit(solution)/shard_map/ppermute | solution.py:51
  116.5 16.7 %collective-permute-start.17 = (bf16[1,256,256]{2,1,0:T(8,128)(2,1)S(1)}, bf16[1,256,256]{2,1,0:T(8,128)(2,1)S(1)}, u32[]{:S(2)}, u32[]{:S(2)}) collective-permute-start(bf16[1,256,256]{2,1,0:T(8,128)(2,1)S(1)} %constant_dynamic-slice_fusion.3), channel_id=1, source_target_pairs={{0,8},{4,12},{8,16},{12,20},{16,24},{20,28},{24,0},{28,4},{1,9},{5... | collective-permute-start | bytes 393224 | tf_op jit(solution)/shard_map/ppermute | solution.py:51
  116.6 16.7 %collective-permute-start.18 = (bf16[1,256,256]{2,1,0:T(8,128)(2,1)S(1)}, bf16[1,256,256]{2,1,0:T(8,128)(2,1)S(1)}, u32[]{:S(2)}, u32[]{:S(2)}) collective-permute-start(bf16[1,256,256]{2,1,0:T(8,128)(2,1)S(1)} %constant_dynamic-slice_fusion.2), channel_id=1, source_target_pairs={{0,24},{4,28},{8,0},{12,4},{16,8},{20,12},{24,16},{28,20},{1,25},{... | collective-permute-start | bytes 393224 | tf_op jit(solution)/shard_map/ppermute | solution.py:51
  128.5 7.8 %collective-permute-start.19 = (bf16[1,256,256]{2,1,0:T(8,128)(2,1)S(1)}, bf16[1,256,256]{2,1,0:T(8,128)(2,1)S(1)}, u32[]{:S(2)}, u32[]{:S(2)}) collective-permute-start(bf16[1,256,256]{2,1,0:T(8,128)(2,1)S(1)} %constant_dynamic-slice_fusion.1), channel_id=1, source_target_pairs={{0,4},{4,8},{8,12},{12,16},{16,20},{20,24},{24,28},{28,0},{1,5},{5... | collective-permute-start | bytes 393224 | tf_op jit(solution)/shard_map/ppermute | solution.py:51
  130.4 6.4 %collective-permute-start.20 = (bf16[1,256,256]{2,1,0:T(8,128)(2,1)S(1)}, bf16[1,256,256]{2,1,0:T(8,128)(2,1)S(1)}, u32[]{:S(2)}, u32[]{:S(2)}) collective-permute-start(bf16[1,256,256]{2,1,0:T(8,128)(2,1)S(1)} %constant_dynamic-slice_fusion), channel_id=1, source_target_pairs={{0,28},{4,0},{8,4},{12,8},{16,12},{20,16},{24,20},{28,24},{1,29},{... | collective-permute-start | bytes 393224 | tf_op jit(solution)/shard_map/ppermute | solution.py:51

commit v27 on v26

--- a/solution.py
+++ b/solution.py
@@ -34,7 +34,7 @@
     return lax.all_to_all(copies, axis, split_axis=0, concat_axis=0, tiled=True)
 
 
-def exchange(cells, axis, split_axis, far_first=False, separate=False):
+def exchange(cells, axis, split_axis, far_first=False, separate=False, dtype=None):
     count = lax.axis_size(axis)
     here = lax.axis_index(axis)
     width = cells.shape[split_axis] // count
@@ -47,6 +47,8 @@
         if separate:
             source, _ = lax.optimization_barrier((cells, jnp.int32(shift)))
         piece = lax.dynamic_slice_in_dim(source, ((here + shift) % count) * width, width, axis=split_axis)
+        if dtype is not None:
+            piece = piece.astype(dtype)
         if shift:
             piece = lax.ppermute(piece, axis, [(j, (j + shift) % count) for j in range(count)])
         pieces.append(piece)
@@ -234,8 +236,8 @@
     selector = (owner[:, None] == jnp.arange(local_angles, dtype=jnp.int32)[None, :]).astype(
         jnp.float32
     )
-    shares = gram_terms.astype(jnp.bfloat16).reshape(lax.axis_size("gx"), row_count, 2 * columns)
-    own_rows = sum(piece.astype(jnp.float32) for piece in exchange(shares, "gx", 0, True, True))[0]
+    shares = gram_terms.reshape(lax.axis_size("gx"), row_count, 2 * columns)
+    own_rows = sum(piece.astype(jnp.float32) for piece in exchange(shares, "gx", 0, True, True, jnp.bfloat16))[0]
     row_energy = jnp.sum(own_rows[:, :columns] ** 2, axis=1)
     energy = jnp.sum(gather_small(jnp.sum(selector * row_energy[:, None], axis=0), "gx"), axis=0)
     mean_sq = energy / (2.0 * snap_count * snap_count)

time: 151 us -> 151 us (level)
    dynamic_slice x20 -> x13, local copies, waits for them, and re-layouts: 11.2 us -> 11.1 us  [exchange(): lax.dynamic_slice_in_dim(source, (here + shift) % count * width, width, a...]
where the time goes in v27:
time: 151 us; the launch traced here: 150 us
  waiting for transfers between devices  47.9 us (32%)
  local copies, waits for them, and re-layouts  34.9 us (23%)
  starting transfers between devices  31.9 us (21%)
  other arithmetic  14.7 us (10%)
  blocking collectives  11.7 us (8%)
  Pallas kernels  7.13 us (5%)
    ppermute x19, waiting for transfers between devices, exchange(): lax.ppermute(piece, axis, [(j, (j + shift) % count) for j in range(count)])  42.3 us
    ppermute x19, starting transfers between devices, exchange(): lax.ppermute(piece, axis, [(j, (j + shift) % count) for j in range(count)])  25.9 us
    unnamed x20, local copies, waits for them, and re-layouts  20.7 us
    all_to_all x1, blocking collectives, gather_small(): return lax.all_to_all(copies, axis, split_axis=0, concat_axis=0, tiled=True)  11.7 us
    dynamic_slice x13, local copies, waits for them, and re-layouts, exchange(): lax.dynamic_slice_in_dim(source, (here + shift) % count * width, width, a...  11.1 us
    pallas_call x2, Pallas kernels, dft(): pl.pallas_call(functools.partial(dft_kernel, count=count, weighted=weight...  7.13 us
    ppermute x1, waiting for transfers between devices, padded_2(): lax.ppermute(tail, axis, [(i, (i + 1) % count) for i in range(ends)])  5.66 us
    convert_element_type x1, other arithmetic, local(): image = (-velocity * (forward - behind) * 0.5 + diffusion * (forward + be...  5.55 us
  transfers between devices with their start and end apart: 21, of which 13 were waited for; matrix products, arithmetic and copies ran while one was open for 25% of the time, Pallas kernels for 5%

profile of v27, /device:TPU:0, one launch (start us, length us, event | category | flops | bytes accessed | tf_op | source)
XLA Modules:
  0.0 150.3 jit_solution(822581659107773189)
XLA Ops:
  0.7 1.2 constant_dynamic-slice_fusion.3
  1.9 2.5 %collective-permute-start.8 = (bf16[32,4,16,128]{3,2,1,0:T(8,128)(2,1)S(1)}, bf16[32,4,16,128]{3,2,1,0:T(8,128)(2,1)S(1)}, u32[]{:S(2)}, u32[]{:S(2)}) collective-permute-start(bf16[32,4,16,128]{3,2,1,0:T(8,128)(2,1)S(1)} %constant_dynamic-slice_fusion.3), channel_id=1, source_target_pairs={{0,3},{1,0},{2,1},{3,2},{4,7},{5,4},{6,5},{7,6},{8,11},{9,8},{10,9... | collective-permute-start | bytes 1572872 | tf_op jit(solution)/shard_map/ppermute | solution.py:53
  4.4 1.9 %constant_dynamic-slice_fusion.4 = bf16[32,4,16,128]{3,2,1,0:T(8,128)(2,1)} fusion(bf16[32,4,64,128]{3,2,1,0:T(8,128)(2,1)} %param.5, s32[]{:T(128)S(6)} %select_n.220), kind=kLoop, calls=%fused_computation.106 | loop fusion | bytes 1048580 | tf_op jit(solution)/shard_map/dynamic_slice | solution.py:49
  6.9 1.9 %constant_dynamic-slice_fusion.5 = bf16[32,4,16,128]{3,2,1,0:T(8,128)(2,1)} fusion(bf16[32,4,64,128]{3,2,1,0:T(8,128)(2,1)} %param.5, s32[]{:T(128)S(6)} %select_n.218), kind=kLoop, calls=%fused_computation.107 | loop fusion | bytes 1048580 | tf_op jit(solution)/shard_map/dynamic_slice | solution.py:49
  9.0 1.9 %constant_dynamic-slice_fusion.11 = bf16[32,4,16,128]{3,2,1,0:T(8,128)(2,1)} fusion(bf16[32,4,64,128]{3,2,1,0:T(8,128)(2,1)} %param.6, s32[]{:T(128)S(6)} %select_n.222), kind=kLoop, calls=%fused_computation.113 | loop fusion | bytes 1048580 | tf_op jit(solution)/shard_map/dynamic_slice | solution.py:49
  10.9 1.6 %collective-permute-start.2 = (bf16[32,4,16,128]{3,2,1,0:T(8,128)(2,1)}, bf16[32,4,16,128]{3,2,1,0:T(8,128)(2,1)}, u32[]{:S(2)}, u32[]{:S(2)}) collective-permute-start(bf16[32,4,16,128]{3,2,1,0:T(8,128)(2,1)} %constant_dynamic-slice_fusion.11), channel_id=1, source_target_pairs={{0,3},{1,0},{2,1},{3,2},{4,7},{5,4},{6,5},{7,6},{8,11},{9,8},{10,9... | collective-permute-start | bytes 1572872 | tf_op jit(solution)/shard_map/ppermute | solution.py:53
  12.4 0.9 constant_dynamic-slice_fusion.12
  13.3 1.4 collective-permute-start.1
  18.2 1.3 constant_dynamic-slice_fusion.6
  19.6 1.2 copy.40
  20.8 1.2 copy.44
  22.8 2.2 %copy.37 = bf16[4,8,64,128]{3,1,2,0:T(8,128)(2,1)} copy(bf16[4,8,64,128]{3,2,1,0:T(8,128)(2,1)} %bitcast.111) | data formatting | bytes 1048576
  25.0 2.1 %collective-permute-done.7 = bf16[32,4,16,128]{3,2,1,0:T(8,128)(2,1)} collective-permute-done((bf16[32,4,16,128]{3,2,1,0:T(8,128)(2,1)}, bf16[32,4,16,128]{3,2,1,0:T(8,128)(2,1)}, u32[]{:S(2)}, u32[]{:S(2)}) %collective-permute-start.7) | collective-permute-done | bytes 524320 | tf_op jit(solution)/shard_map/ppermute | solution.py:53
  27.1 2.2 %copy.38 = bf16[4,8,64,128]{3,1,2,0:T(8,128)(2,1)} copy(bf16[4,8,64,128]{3,2,1,0:T(8,128)(2,1)} %bitcast.44) | data formatting | bytes 1048576
  29.3 1.8 %collective-permute-done.6 = bf16[32,4,16,128]{3,2,1,0:T(8,128)(2,1)} collective-permute-done((bf16[32,4,16,128]{3,2,1,0:T(8,128)(2,1)}, bf16[32,4,16,128]{3,2,1,0:T(8,128)(2,1)}, u32[]{:S(2)}, u32[]{:S(2)}) %collective-permute-start.6) | collective-permute-done | bytes 524320 | tf_op jit(solution)/shard_map/ppermute | solution.py:53
  31.0 2.2 %copy.39 = bf16[4,8,64,128]{3,1,2,0:T(8,128)(2,1)} copy(bf16[4,8,64,128]{3,2,1,0:T(8,128)(2,1)} %bitcast.41) | data formatting | bytes 1048576
  33.2 3.5 %shard_map.77 = bf16[128,8192]{1,0:T(8,128)(2,1)} custom-call(bf16[128,256]{1,0:T(8,128)(2,1)} %concatenate.22.refs_0_, bf16[32,8192]{1,0:T(8,128)(2,1)} %bitcast.104, bf16[32,8192]{1,0:T(8,128)(2,1)} %bitcast.110, bf16[32,8192]{1,0:T(8,128)(2,1)} %bitcast.108, bf16[32,8192]{1,0:T(8,128)(2,1)} %bitcast.106), custom_call_target="tpu_custom_call" | custom-call | tf_op jit(solution)/shard_map/pallas_call | solution.py:117
  36.7 2.2 %copy.28 = bf16[16,8,64,128]{3,2,1,0:T(8,128)(2,1)S(1)} copy(bf16[16,8,64,128]{3,1,2,0:T(8,128)(2,1)} %bitcast.84) | data formatting | bytes 4194304
  39.8 1.8 %collective-permute-start.10 = (bf16[32,4,16,128]{3,2,1,0:T(8,128)(2,1)S(1)}, bf16[32,4,16,128]{3,2,1,0:T(8,128)(2,1)}, u32[]{:S(2)}, u32[]{:S(2)}) collective-permute-start(bf16[32,4,16,128]{3,2,1,0:T(8,128)(2,1)S(1)} %constant_dynamic-slice_fusion.1), channel_id=1, source_target_pairs={{0,2},{1,3},{2,0},{3,1},{4,6},{5,7},{6,4},{7,5},{8,10},{9,11},{10,... | collective-permute-start | bytes 1572872 | tf_op jit(solution)/shard_map/ppermute | solution.py:53
  41.7 1.5 collective-permute-start.11
  43.2 2.2 %copy.41 = bf16[4,8,64,128]{3,1,2,0:T(8,128)(2,1)} copy(bf16[4,8,64,128]{3,2,1,0:T(8,128)(2,1)} %bitcast.32) | data formatting | bytes 1048576
  45.4 4.2 %collective-permute-done.1 = bf16[32,4,16,128]{3,2,1,0:T(8,128)(2,1)} collective-permute-done((bf16[32,4,16,128]{3,2,1,0:T(8,128)(2,1)}, bf16[32,4,16,128]{3,2,1,0:T(8,128)(2,1)}, u32[]{:S(2)}, u32[]{:S(2)}) %collective-permute-start.1) | collective-permute-done | bytes 524320 | tf_op jit(solution)/shard_map/ppermute | solution.py:53
  49.6 2.2 %copy.42 = bf16[4,8,64,128]{3,1,2,0:T(8,128)(2,1)} copy(bf16[4,8,64,128]{3,2,1,0:T(8,128)(2,1)} %bitcast.29) | data formatting | bytes 1048576
  51.8 1.7 %collective-permute-done = bf16[32,4,16,128]{3,2,1,0:T(8,128)(2,1)} collective-permute-done((bf16[32,4,16,128]{3,2,1,0:T(8,128)(2,1)}, bf16[32,4,16,128]{3,2,1,0:T(8,128)(2,1)}, u32[]{:S(2)}, u32[]{:S(2)}) %collective-permute-start) | collective-permute-done | bytes 524320 | tf_op jit(solution)/shard_map/ppermute | solution.py:53
  53.5 2.2 %copy.43 = bf16[4,8,64,128]{3,1,2,0:T(8,128)(2,1)} copy(bf16[4,8,64,128]{3,2,1,0:T(8,128)(2,1)} %bitcast.26) | data formatting | bytes 1048576
  56.4 3.7 %shard_map.76 = bf16[128,8192]{1,0:T(8,128)(2,1)} custom-call(bf16[128,256]{1,0:T(8,128)(2,1)} %concatenate.22.refs_0_, bf16[32,8192]{1,0:T(8,128)(2,1)} %bitcast.103, bf16[32,8192]{1,0:T(8,128)(2,1)} %bitcast.109, bf16[32,8192]{1,0:T(8,128)(2,1)} %bitcast.107, bf16[32,8192]{1,0:T(8,128)(2,1)} %bitcast.105, f32[1,8192]{1,0:T(1,128)} %bitcast.115), custom_call_target="tpu_custom_call" | custom-call | tf_op jit(solution)/shard_map/pallas_call | solution.py:117
  60.0 2.2 %copy.23 = bf16[16,8,64,128]{3,2,1,0:T(8,128)(2,1)S(1)} copy(bf16[16,8,64,128]{3,1,2,0:T(8,128)(2,1)} %bitcast.83) | data formatting | bytes 4194304
  62.4 1.8 %collective-permute-start.4 = (bf16[32,4,16,128]{3,2,1,0:T(8,128)(2,1)S(1)}, bf16[32,4,16,128]{3,2,1,0:T(8,128)(2,1)S(1)}, u32[]{:S(2)}, u32[]{:S(2)}) collective-permute-start(bf16[32,4,16,128]{3,2,1,0:T(8,128)(2,1)S(1)} %constant_dynamic-slice_fusion.8), channel_id=1, source_target_pairs={{0,2},{1,3},{2,0},{3,1},{4,6},{5,7},{6,4},{7,5},{8,10},{9,11},{10,... | collective-permute-start | bytes 1572872 | tf_op jit(solution)/shard_map/ppermute | solution.py:53
  64.7 1.1 collective-permute-start.5
  65.8 4.8 %collective-permute-done.11 = bf16[32,4,16,128]{3,2,1,0:T(8,128)(2,1)} collective-permute-done((bf16[32,4,16,128]{3,2,1,0:T(8,128)(2,1)S(1)}, bf16[32,4,16,128]{3,2,1,0:T(8,128)(2,1)}, u32[]{:S(2)}, u32[]{:S(2)}) %collective-permute-start.11) | collective-permute-done | bytes 524320 | tf_op jit(solution)/shard_map/ppermute | solution.py:53
  70.6 1.6 %pad_maximum_fusion.11 = bf16[4,32,4,16,128]{4,3,2,1,0:T(8,128)(2,1)S(1)} fusion(bf16[1,32,4,16,128]{4,3,2,1,0:T(8,128)(2,1)} %bitcast.13, bf16[1,32,4,16,128]{4,3,2,1,0:T(8,128)(2,1)} %bitcast.12, bf16[1,32,4,16,128]{4,3,2,1,0:T(8,128)(2,1)} %bitcast.11, bf16[1,32,4,16,128]{4,3,2,1,0:T(8,128)(2,1)S(1)} %dynamic-slice_bitcast_fusion.4), kind=kLoop, calls=%fused_computation.25 | loop fusion | flops 3145728 | bytes 4194304 | tf_op jit(solution)/shard_map/stack | solution.py:61
  73.1 1.3 collective-permute-start.12
  74.4 4.8 %collective-permute-start.13 = (bf16[32,1,64,128]{3,2,1,0:T(8,128)(2,1)S(1)}, bf16[32,1,64,128]{3,2,1,0:T(8,128)(2,1)S(1)}, u32[]{:S(2)}, u32[]{:S(2)}) collective-permute-start(bf16[32,1,64,128]{3,2,1,0:T(8,128)(2,1)S(1)} %get-tuple-element.56), channel_id=1, source_target_pairs={{0,4},{4,8},{8,12},{12,16},{16,20},{20,24},{24,28},{1,5},{5,9},{9,... | collective-permute-start | bytes 1572872 | tf_op jit(solution)/shard_map/ppermute | solution.py:22
  79.2 7.9 %collective-permute-done.3 = bf16[32,4,16,128]{3,2,1,0:T(8,128)(2,1)S(1)} collective-permute-done((bf16[32,4,16,128]{3,2,1,0:T(8,128)(2,1)S(1)}, bf16[32,4,16,128]{3,2,1,0:T(8,128)(2,1)S(1)}, u32[]{:S(2)}, u32[]{:S(2)}) %collective-permute-start.3) | collective-permute-done | bytes 524320 | tf_op jit(solution)/shard_map/ppermute | solution.py:53
  87.1 6.0 %collective-permute-done.5 = bf16[32,4,16,128]{3,2,1,0:T(8,128)(2,1)S(1)} collective-permute-done((bf16[32,4,16,128]{3,2,1,0:T(8,128)(2,1)S(1)}, bf16[32,4,16,128]{3,2,1,0:T(8,128)(2,1)S(1)}, u32[]{:S(2)}, u32[]{:S(2)}) %collective-permute-start.5) | collective-permute-done | bytes 524320 | tf_op jit(solution)/shard_map/ppermute | solution.py:53
  94.1 1.0 pad_convert_fusion
  95.2 5.7 %collective-permute-done.13 = bf16[32,1,64,128]{3,2,1,0:T(8,128)(2,1)S(1)} collective-permute-done((bf16[32,1,64,128]{3,2,1,0:T(8,128)(2,1)S(1)}, bf16[32,1,64,128]{3,2,1,0:T(8,128)(2,1)S(1)}, u32[]{:S(2)}, u32[]{:S(2)}) %collective-permute-start.13) | collective-permute-done | bytes 524320 | tf_op jit(solution)/shard_map/ppermute | solution.py:22
  100.8 5.5 %fusion.3 = bf16[32,4,64,128]{3,2,1,0:T(8,128)(2,1)S(1)} fusion(f32[32,4,66,128]{3,2,1,0:T(8,128)S(1)} %pad_convert_fusion, bf16[32,1,64,128]{3,2,1,0:T(8,128)(2,1)S(1)} %collective-permute-done.13, bf16[32,4,16,128]{3,2,1,0:T(8,128)(2,1)S(1)} %get-tuple-element.58, bf16[32,4,16,128]{3,2,1,0:T(8,128)(2,1)S(1)} %get-tuple-element.59, ...), kind=kLoop, calls=%fused_computation.7 | loop fusion | flops 42991616 | bytes 13641728 | tf_op jit(solution)/shard_map/convert_element_type | solution.py:224
  108.0 1.2 slice_add_fusion.1
  109.9 2.7 %collective-permute-start.14 = (bf16[1,256,256]{2,1,0:T(8,128)(2,1)S(1)}, bf16[1,256,256]{2,1,0:T(8,128)(2,1)S(1)}, u32[]{:S(2)}, u32[]{:S(2)}) collective-permute-start(bf16[1,256,256]{2,1,0:T(8,128)(2,1)S(1)} %dynamic-slice_convert_fusion.6), channel_id=1, source_target_pairs={{0,16},{4,20},{8,24},{12,28},{16,0},{20,4},{24,8},{28,12},{1,17},{... | collective-permute-start | bytes 393224 | tf_op jit(solution)/shard_map/ppermute | solution.py:53
  112.6 1.0 collective-permute-start.15
  113.6 2.9 %collective-permute-start.16 = (bf16[1,256,256]{2,1,0:T(8,128)(2,1)S(1)}, bf16[1,256,256]{2,1,0:T(8,128)(2,1)S(1)}, u32[]{:S(2)}, u32[]{:S(2)}) collective-permute-start(bf16[1,256,256]{2,1,0:T(8,128)(2,1)S(1)} %dynamic-slice_convert_fusion.4), channel_id=1, source_target_pairs={{0,20},{4,24},{8,28},{12,0},{16,4},{20,8},{24,12},{28,16},{1,21},{... | collective-permute-start | bytes 393224 | tf_op jit(solution)/shard_map/ppermute | solution.py:53
  116.6 3.8 %collective-permute-start.18 = (bf16[1,256,256]{2,1,0:T(8,128)(2,1)S(1)}, bf16[1,256,256]{2,1,0:T(8,128)(2,1)S(1)}, u32[]{:S(2)}, u32[]{:S(2)}) collective-permute-start(bf16[1,256,256]{2,1,0:T(8,128)(2,1)S(1)} %dynamic-slice_convert_fusion.2), channel_id=1, source_target_pairs={{0,24},{4,28},{8,0},{12,4},{16,8},{20,12},{24,16},{28,20},{1,25},{... | collective-permute-start | bytes 393224 | tf_op jit(solution)/shard_map/ppermute | solution.py:53
  120.5 8.0 %collective-permute-done.14 = bf16[1,256,256]{2,1,0:T(8,128)(2,1)S(1)} collective-permute-done((bf16[1,256,256]{2,1,0:T(8,128)(2,1)S(1)}, bf16[1,256,256]{2,1,0:T(8,128)(2,1)S(1)}, u32[]{:S(2)}, u32[]{:S(2)}) %collective-permute-start.14) | collective-permute-done | bytes 131104 | tf_op jit(solution)/shard_map/ppermute | solution.py:53
  128.5 1.9 %collective-permute-done.15 = bf16[1,256,256]{2,1,0:T(8,128)(2,1)S(1)} collective-permute-done((bf16[1,256,256]{2,1,0:T(8,128)(2,1)S(1)}, bf16[1,256,256]{2,1,0:T(8,128)(2,1)S(1)}, u32[]{:S(2)}, u32[]{:S(2)}) %collective-permute-start.15) | collective-permute-done | bytes 131104 | tf_op jit(solution)/shard_map/ppermute | solution.py:53
  130.4 2.8 %collective-permute-start.20 = (bf16[1,256,256]{2,1,0:T(8,128)(2,1)S(1)}, bf16[1,256,256]{2,1,0:T(8,128)(2,1)S(1)}, u32[]{:S(2)}, u32[]{:S(2)}) collective-permute-start(bf16[1,256,256]{2,1,0:T(8,128)(2,1)S(1)} %dynamic-slice_convert_fusion), channel_id=1, source_target_pairs={{0,28},{4,0},{8,4},{12,8},{16,12},{20,16},{24,20},{28,24},{1,29},{... | collective-permute-start | bytes 393224 | tf_op jit(solution)/shard_map/ppermute | solution.py:53
  133.3 3.1 %collective-permute-done.19 = bf16[1,256,256]{2,1,0:T(8,128)(2,1)S(1)} collective-permute-done((bf16[1,256,256]{2,1,0:T(8,128)(2,1)S(1)}, bf16[1,256,256]{2,1,0:T(8,128)(2,1)S(1)}, u32[]{:S(2)}, u32[]{:S(2)}) %collective-permute-start.19) | collective-permute-done | bytes 131104 | tf_op jit(solution)/shard_map/ppermute | solution.py:53
  137.2 11.7 %all_to_all.6 = f32[8,1,32]{2,1,0:T(1,128)S(1)} all-to-all(f32[8,1,32]{2,1,0:T(1,128)S(1)} %broadcast_in_dim.5), channel_id=1, replica_groups=mesh['gx'=8,'ka'=4] {'gx'}, dimensions={0} | all-to-all | bytes 2048 | tf_op jit(solution)/shard_map/all_to_all | solution.py:34
  (81 shorter events, 13.8 us)
Async XLA Ops:
  0.6 11.8 %copy-start = (bf16[32,4,64,128]{3,2,1,0:T(8,128)(2,1)S(1)}, bf16[32,4,64,128]{3,2,1,0:T(8,128)(2,1)}, u32[]{:S(2)}) copy-start(bf16[32,4,64,128]{3,2,1,0:T(8,128)(2,1)} %param.6) | copy-start | bytes 6291460
  0.6 15.5 %copy-start.3 = (f32[4,64]{1,0:T(4,128)S(1)}, f32[4,64]{1,0:T(4,128)}, u32[]{:S(2)}) copy-start(f32[4,64]{1,0:T(4,128)} %param.7) | copy-start | bytes 3076
  1.9 15.4 %collective-permute-start.8 = (bf16[32,4,16,128]{3,2,1,0:T(8,128)(2,1)S(1)}, bf16[32,4,16,128]{3,2,1,0:T(8,128)(2,1)S(1)}, u32[]{:S(2)}, u32[]{:S(2)}) collective-permute-start(bf16[32,4,16,128]{3,2,1,0:T(8,128)(2,1)S(1)} %constant_dynamic-slice_fusion.3), channel_id=1, source_target_pairs={{0,3},{1,0},{2,1},{3,2},{4,7},{5,4},{6,5},{7,6},{8,11},{9,8},{10,9... | collective-permute-start | bytes 1572872 | tf_op jit(solution)/shard_map/ppermute | solution.py:53
  6.3 20.8 %collective-permute-start.7 = (bf16[32,4,16,128]{3,2,1,0:T(8,128)(2,1)}, bf16[32,4,16,128]{3,2,1,0:T(8,128)(2,1)}, u32[]{:S(2)}, u32[]{:S(2)}) collective-permute-start(bf16[32,4,16,128]{3,2,1,0:T(8,128)(2,1)} %constant_dynamic-slice_fusion.4), channel_id=1, source_target_pairs={{0,2},{1,3},{2,0},{3,1},{4,6},{5,7},{6,4},{7,5},{8,10},{9,11},{10,... | collective-permute-start | bytes 1572872 | tf_op jit(solution)/shard_map/ppermute | solution.py:53
  6.9 13.9 %copy-start.4 = (f32[4,64]{1,0:T(4,128)S(1)}, f32[4,64]{1,0:T(4,128)}, u32[]{:S(2)}) copy-start(f32[4,64]{1,0:T(4,128)} %param.8) | copy-start | bytes 3076
  8.8 22.2 %collective-permute-start.6 = (bf16[32,4,16,128]{3,2,1,0:T(8,128)(2,1)}, bf16[32,4,16,128]{3,2,1,0:T(8,128)(2,1)}, u32[]{:S(2)}, u32[]{:S(2)}) collective-permute-start(bf16[32,4,16,128]{3,2,1,0:T(8,128)(2,1)} %constant_dynamic-slice_fusion.5), channel_id=1, source_target_pairs={{0,1},{1,2},{2,3},{3,0},{4,5},{5,6},{6,7},{7,4},{8,9},{9,10},{10,1... | collective-permute-start | bytes 1572872 | tf_op jit(solution)/shard_map/ppermute | solution.py:53
  10.9 30.8 %collective-permute-start.2 = (bf16[32,4,16,128]{3,2,1,0:T(8,128)(2,1)}, bf16[32,4,16,128]{3,2,1,0:T(8,128)(2,1)}, u32[]{:S(2)}, u32[]{:S(2)}) collective-permute-start(bf16[32,4,16,128]{3,2,1,0:T(8,128)(2,1)} %constant_dynamic-slice_fusion.11), channel_id=1, source_target_pairs={{0,3},{1,0},{2,1},{3,2},{4,7},{5,4},{6,5},{7,6},{8,11},{9,8},{10,9... | collective-permute-start | bytes 1572872 | tf_op jit(solution)/shard_map/ppermute | solution.py:53
  13.3 36.2 %collective-permute-start.1 = (bf16[32,4,16,128]{3,2,1,0:T(8,128)(2,1)}, bf16[32,4,16,128]{3,2,1,0:T(8,128)(2,1)}, u32[]{:S(2)}, u32[]{:S(2)}) collective-permute-start(bf16[32,4,16,128]{3,2,1,0:T(8,128)(2,1)} %constant_dynamic-slice_fusion.12), channel_id=1, source_target_pairs={{0,2},{1,3},{2,0},{3,1},{4,6},{5,7},{6,4},{7,5},{8,10},{9,11},{10,... | collective-permute-start | bytes 1572872 | tf_op jit(solution)/shard_map/ppermute | solution.py:53
  17.4 0.8 copy-start.1
  18.2 35.3 %collective-permute-start = (bf16[32,4,16,128]{3,2,1,0:T(8,128)(2,1)}, bf16[32,4,16,128]{3,2,1,0:T(8,128)(2,1)}, u32[]{:S(2)}, u32[]{:S(2)}) collective-permute-start(bf16[32,4,16,128]{3,2,1,0:T(8,128)(2,1)} %constant_dynamic-slice_fusion.13), channel_id=1, source_target_pairs={{0,1},{1,2},{2,3},{3,0},{4,5},{5,6},{6,7},{7,4},{8,9},{9,10},{10,1... | collective-permute-start | bytes 1572872 | tf_op jit(solution)/shard_map/ppermute | solution.py:53
  39.8 25.0 %collective-permute-start.9 = (bf16[32,4,16,128]{3,2,1,0:T(8,128)(2,1)}, bf16[32,4,16,128]{3,2,1,0:T(8,128)(2,1)}, u32[]{:S(2)}, u32[]{:S(2)}) collective-permute-start(bf16[32,4,16,128]{3,2,1,0:T(8,128)(2,1)} %constant_dynamic-slice_fusion.2), channel_id=1, source_target_pairs={{0,1},{1,2},{2,3},{3,0},{4,5},{5,6},{6,7},{7,4},{8,9},{9,10},{10,1... | collective-permute-start | bytes 1572872 | tf_op jit(solution)/shard_map/ppermute | solution.py:53
  39.8 26.0 %collective-permute-start.10 = (bf16[32,4,16,128]{3,2,1,0:T(8,128)(2,1)S(1)}, bf16[32,4,16,128]{3,2,1,0:T(8,128)(2,1)}, u32[]{:S(2)}, u32[]{:S(2)}) collective-permute-start(bf16[32,4,16,128]{3,2,1,0:T(8,128)(2,1)S(1)} %constant_dynamic-slice_fusion.1), channel_id=1, source_target_pairs={{0,2},{1,3},{2,0},{3,1},{4,6},{5,7},{6,4},{7,5},{8,10},{9,11},{10,... | collective-permute-start | bytes 1572872 | tf_op jit(solution)/shard_map/ppermute | solution.py:53
  41.7 28.9 %collective-permute-start.11 = (bf16[32,4,16,128]{3,2,1,0:T(8,128)(2,1)S(1)}, bf16[32,4,16,128]{3,2,1,0:T(8,128)(2,1)}, u32[]{:S(2)}, u32[]{:S(2)}) collective-permute-start(bf16[32,4,16,128]{3,2,1,0:T(8,128)(2,1)S(1)} %constant_dynamic-slice_fusion), channel_id=1, source_target_pairs={{0,3},{1,0},{2,1},{3,2},{4,7},{5,4},{6,5},{7,6},{8,11},{9,8},{10,9... | collective-permute-start | bytes 1572872 | tf_op jit(solution)/shard_map/ppermute | solution.py:53
  62.3 24.8 %collective-permute-start.3 = (bf16[32,4,16,128]{3,2,1,0:T(8,128)(2,1)S(1)}, bf16[32,4,16,128]{3,2,1,0:T(8,128)(2,1)S(1)}, u32[]{:S(2)}, u32[]{:S(2)}) collective-permute-start(bf16[32,4,16,128]{3,2,1,0:T(8,128)(2,1)S(1)} %constant_dynamic-slice_fusion.9), channel_id=1, source_target_pairs={{0,1},{1,2},{2,3},{3,0},{4,5},{5,6},{6,7},{7,4},{8,9},{9,10},{10,1... | collective-permute-start | bytes 1572872 | tf_op jit(solution)/shard_map/ppermute | solution.py:53
  62.4 24.7 %collective-permute-start.4 = (bf16[32,4,16,128]{3,2,1,0:T(8,128)(2,1)S(1)}, bf16[32,4,16,128]{3,2,1,0:T(8,128)(2,1)S(1)}, u32[]{:S(2)}, u32[]{:S(2)}) collective-permute-start(bf16[32,4,16,128]{3,2,1,0:T(8,128)(2,1)S(1)} %constant_dynamic-slice_fusion.8), channel_id=1, source_target_pairs={{0,2},{1,3},{2,0},{3,1},{4,6},{5,7},{6,4},{7,5},{8,10},{9,11},{10,... | collective-permute-start | bytes 1572872 | tf_op jit(solution)/shard_map/ppermute | solution.py:53
  64.7 28.3 %collective-permute-start.5 = (bf16[32,4,16,128]{3,2,1,0:T(8,128)(2,1)S(1)}, bf16[32,4,16,128]{3,2,1,0:T(8,128)(2,1)S(1)}, u32[]{:S(2)}, u32[]{:S(2)}) collective-permute-start(bf16[32,4,16,128]{3,2,1,0:T(8,128)(2,1)S(1)} %constant_dynamic-slice_fusion.7), channel_id=1, source_target_pairs={{0,3},{1,0},{2,1},{3,2},{4,7},{5,4},{6,5},{7,6},{8,11},{9,8},{10,9... | collective-permute-start | bytes 1572872 | tf_op jit(solution)/shard_map/ppermute | solution.py:53
  73.1 22.1 %collective-permute-start.12 = (bf16[32,1,64,128]{3,2,1,0:T(8,128)(2,1)S(1)}, bf16[32,1,64,128]{3,2,1,0:T(8,128)(2,1)S(1)}, u32[]{:S(2)}, u32[]{:S(2)}) collective-permute-start(bf16[32,1,64,128]{3,2,1,0:T(8,128)(2,1)S(1)} %get-tuple-element.55), channel_id=1, source_target_pairs={{4,0},{8,4},{12,8},{16,12},{20,16},{24,20},{28,24},{5,1},{9,5},{13... | collective-permute-start | bytes 1572872 | tf_op jit(solution)/shard_map/ppermute | solution.py:24
  74.4 26.4 %collective-permute-start.13 = (bf16[32,1,64,128]{3,2,1,0:T(8,128)(2,1)S(1)}, bf16[32,1,64,128]{3,2,1,0:T(8,128)(2,1)S(1)}, u32[]{:S(2)}, u32[]{:S(2)}) collective-permute-start(bf16[32,1,64,128]{3,2,1,0:T(8,128)(2,1)S(1)} %get-tuple-element.56), channel_id=1, source_target_pairs={{0,4},{4,8},{8,12},{12,16},{16,20},{20,24},{24,28},{1,5},{5,9},{9,... | collective-permute-start | bytes 1572872 | tf_op jit(solution)/shard_map/ppermute | solution.py:22
  94.1 6.7 %copy-start.2 = (f32[4,64]{1,0:T(4,128)S(1)}, f32[4,64]{1,0:T(4,128)}, u32[]{:S(2)}) copy-start(f32[4,64]{1,0:T(4,128)} %param.9) | copy-start | bytes 3076
  109.9 18.6 %collective-permute-start.14 = (bf16[1,256,256]{2,1,0:T(8,128)(2,1)S(1)}, bf16[1,256,256]{2,1,0:T(8,128)(2,1)S(1)}, u32[]{:S(2)}, u32[]{:S(2)}) collective-permute-start(bf16[1,256,256]{2,1,0:T(8,128)(2,1)S(1)} %dynamic-slice_convert_fusion.6), channel_id=1, source_target_pairs={{0,16},{4,20},{8,24},{12,28},{16,0},{20,4},{24,8},{28,12},{1,17},{... | collective-permute-start | bytes 393224 | tf_op jit(solution)/shard_map/ppermute | solution.py:53
  112.6 17.9 %collective-permute-start.15 = (bf16[1,256,256]{2,1,0:T(8,128)(2,1)S(1)}, bf16[1,256,256]{2,1,0:T(8,128)(2,1)S(1)}, u32[]{:S(2)}, u32[]{:S(2)}) collective-permute-start(bf16[1,256,256]{2,1,0:T(8,128)(2,1)S(1)} %dynamic-slice_convert_fusion.5), channel_id=1, source_target_pairs={{0,12},{4,16},{8,20},{12,24},{16,28},{20,0},{24,4},{28,8},{1,13},{... | collective-permute-start | bytes 393224 | tf_op jit(solution)/shard_map/ppermute | solution.py:53
  113.6 19.7 %collective-permute-start.16 = (bf16[1,256,256]{2,1,0:T(8,128)(2,1)S(1)}, bf16[1,256,256]{2,1,0:T(8,128)(2,1)S(1)}, u32[]{:S(2)}, u32[]{:S(2)}) collective-permute-start(bf16[1,256,256]{2,1,0:T(8,128)(2,1)S(1)} %dynamic-slice_convert_fusion.4), channel_id=1, source_target_pairs={{0,20},{4,24},{8,28},{12,0},{16,4},{20,8},{24,12},{28,16},{1,21},{... | collective-permute-start | bytes 393224 | tf_op jit(solution)/shard_map/ppermute | solution.py:53
  116.5 16.7 %collective-permute-start.17 = (bf16[1,256,256]{2,1,0:T(8,128)(2,1)S(1)}, bf16[1,256,256]{2,1,0:T(8,128)(2,1)S(1)}, u32[]{:S(2)}, u32[]{:S(2)}) collective-permute-start(bf16[1,256,256]{2,1,0:T(8,128)(2,1)S(1)} %dynamic-slice_convert_fusion.3), channel_id=1, source_target_pairs={{0,8},{4,12},{8,16},{12,20},{16,24},{20,28},{24,0},{28,4},{1,9},{5... | collective-permute-start | bytes 393224 | tf_op jit(solution)/shard_map/ppermute | solution.py:53
  116.6 16.7 %collective-permute-start.18 = (bf16[1,256,256]{2,1,0:T(8,128)(2,1)S(1)}, bf16[1,256,256]{2,1,0:T(8,128)(2,1)S(1)}, u32[]{:S(2)}, u32[]{:S(2)}) collective-permute-start(bf16[1,256,256]{2,1,0:T(8,128)(2,1)S(1)} %dynamic-slice_convert_fusion.2), channel_id=1, source_target_pairs={{0,24},{4,28},{8,0},{12,4},{16,8},{20,12},{24,16},{28,20},{1,25},{... | collective-permute-start | bytes 393224 | tf_op jit(solution)/shard_map/ppermute | solution.py:53
  128.5 7.8 %collective-permute-start.19 = (bf16[1,256,256]{2,1,0:T(8,128)(2,1)S(1)}, bf16[1,256,256]{2,1,0:T(8,128)(2,1)S(1)}, u32[]{:S(2)}, u32[]{:S(2)}) collective-permute-start(bf16[1,256,256]{2,1,0:T(8,128)(2,1)S(1)} %dynamic-slice_convert_fusion.1), channel_id=1, source_target_pairs={{0,4},{4,8},{8,12},{12,16},{16,20},{20,24},{24,28},{28,0},{1,5},{5... | collective-permute-start | bytes 393224 | tf_op jit(solution)/shard_map/ppermute | solution.py:53
  130.4 6.4 %collective-permute-start.20 = (bf16[1,256,256]{2,1,0:T(8,128)(2,1)S(1)}, bf16[1,256,256]{2,1,0:T(8,128)(2,1)S(1)}, u32[]{:S(2)}, u32[]{:S(2)}) collective-permute-start(bf16[1,256,256]{2,1,0:T(8,128)(2,1)S(1)} %dynamic-slice_convert_fusion), channel_id=1, source_target_pairs={{0,28},{4,0},{8,4},{12,8},{16,12},{20,16},{24,20},{28,24},{1,29},{... | collective-permute-start | bytes 393224 | tf_op jit(solution)/shard_map/ppermute | solution.py:53
